TPU v7x, 32 devices: a whole 2x2x4 slice. The times are simulated.
32 devices in a mesh: groups: 2 (over x), wide: 16 (over z, y, core).
Axes of the slice: x: 2, y: 2, z: 4, core: 2. Of those that a mesh axis runs over, the one named last changes fastest.
Arguments:
- retarded_tiles: bfloat16 [32, 16, 2, 128, 128], P(('groups', 'wide')), parts along dimension 0, may hold values from -0.0625 to 0.0625
- tile_lags: int32 [32, 16, 2], P(('groups', 'wide')), parts along dimension 0, may hold values from 1 to 4, as said below
- block_owner: int32 [32], P('groups'), parts along dimension 0, may hold values from 0 to 15, each once
- later_current: bfloat16 [4, 4096, 128], P(None, ('groups', 'wide')), parts along dimension 1, may hold values from -6 to 6
- excitation: float32 [3, 4096, 128], P(None, ('groups', 'wide')), parts along dimension 1, may hold values from -6 to 6
- inverse_blocks: float32 [32, 128, 128], P(('groups', 'wide')), parts along dimension 0, may hold values from -0.5 to 0.5
Outputs:
- adjoint_current: float32 [3, 4096, 128], P(None, ('groups', 'wide')), parts along dimension 1
There are 2 independent parts, one for each index of `groups`. A program takes and returns all parts, laid end to end along the dimension named above; each array names one. Nothing has to cross between parts.
Inputs may be any that keep to these rules, and one draw needn't show every extreme that they name: `tile_lags`: the two slots of every tile name different lags. `block_owner`: each edge block is named once.
All inputs are finite; a program needn't handle non-finite values.
Results may differ from a plain program's by a relative error of at most 0.003.
Values may be sent and summed in bfloat16 or wider, within the bound.
No kernel may reach another device: no remote copies, remote signals or barrier semaphores. Data moves between devices by JAX's collectives and lax.ppermute only.
A program may use at most 128 MiB of HBM per device.

v0:
```python
import jax
import jax.numpy as jnp
from jax import lax
from jax.sharding import PartitionSpec as P


def per_device(retarded_tiles, tile_lags, block_owner, later_current, excitation, inverse_blocks):
    tile_size = retarded_tiles.shape[-1]
    pulses = later_current.shape[-1]
    lag_count = later_current.shape[0]
    step_count = excitation.shape[0]
    column_order = jnp.argsort(block_owner)
    local_tiles = jnp.take(retarded_tiles[0], column_order, axis=0)
    local_lags = jnp.take(tile_lags[0], column_order, axis=0)
    inverse = inverse_blocks[0]
    results = [None] * step_count
    later = lax.all_gather(later_current, "wide", axis=1, tiled=True)
    history = {}
    for offset in range(lag_count):
        history[step_count + offset] = later[offset].reshape(-1, tile_size, pulses)
    for moment in range(step_count - 1, -1, -1):
        chosen = jnp.zeros(local_lags.shape + (tile_size, pulses), jnp.bfloat16)
        for delay in range(1, lag_count + 1):
            chosen = jnp.where(
                (local_lags == delay)[:, :, None, None], history[moment + delay][:, None], chosen
            )
        retarded = jnp.einsum(
            "jspq,jspr->qr", local_tiles, chosen, preferred_element_type=jnp.float32
        )
        source = excitation[moment] - retarded
        current = jnp.dot(
            inverse.T, source, precision=lax.Precision.HIGHEST, preferred_element_type=jnp.float32
        )
        results[moment] = current
        if moment > 0:
            rounded = current.astype(jnp.bfloat16)[None]
            history[moment] = lax.all_gather(rounded, "wide", axis=0, tiled=True)
    return jnp.stack(results)


def solution(mesh):
    in_specs = (
        P(("groups", "wide"), None, None, None, None),
        P(("groups", "wide"), None, None),
        P("groups"),
        P(None, ("groups", "wide"), None),
        P(None, ("groups", "wide"), None),
        P(("groups", "wide"), None, None),
    )
    out_specs = P(None, ("groups", "wide"), None)
    return jax.shard_map(
        per_device, mesh=mesh, in_specs=in_specs, out_specs=out_specs, check_vma=False
    )
```

profile of v0, /device:TPU:0, one launch (start us, length us, event | category | flops | bytes accessed | tf_op | source)
XLA Modules:
  0.0 111.3 jit_solution(3623664762194302780)
XLA Ops:
  6.5 0.0 copy-start
  6.5 0.0 all-gather.4.cloned.1.call-start
  6.5 0.7 all-gather.4.cloned.1.call-update
  7.3 0.8 copy.7
  8.0 1.9 %sort.17 = (s32[16]{0:T(128)}, s32[16]{0:T(128)S(1)}) sort(s32[16]{0:T(128)} %param.8, s32[16]{0:T(128)S(1)} %iota.4), dimensions={0}, to_apply=%region_0.0 | sort | flops 64 | bytes 256 | tf_op jit(solution)/shard_map/jit(argsort)/sort | solution.py:12
  9.9 0.6 gather_fusion.1
  10.5 0.0 copy-done
  10.5 0.7 gather_fusion
  11.3 0.1 select_compare_fusion.3
  11.4 42.4 %all-gather.4.cloned.1.call-done = bf16[4,2048,128]{2,1,0:T(8,128)(2,1)} async-done(((bf16[4,128,128]{2,1,0:T(8,128)(2,1)}), bf16[4,2048,128]{2,1,0:T(8,128)(2,1)}) %all-gather.4.cloned.1.call-update) | async-done | bytes 2097168 | tf_op jit(solution)/shard_map/all_gather | solution.py:17
  53.7 1.7 %fusion.50 = (bf16[1,2048,128]{2,1,0:T(8,128)(2,1)S(1)}, bf16[1,2048,128]{2,1,0:T(8,128)(2,1)S(1)}, bf16[1,2048,128]{2,1,0:T(8,128)(2,1)S(1)}, bf16[1,2048,128]{2,1,0:T(8,128)(2,1)S(1)}) fusion(bf16[4,2048,128]{2,1,0:T(8,128)(2,1)} %all-gather.4.cloned.1.call-done), kind=kLoop, calls=%fused_computation.67 | loop fusion | bytes 4194304 | tf_op jit(solution)/shard_map/slice | solution.py:20
  55.4 0.0 copy-start.2
  55.4 0.0 copy-start.3
  55.4 0.0 copy-start.4
  55.4 0.0 copy-start.1
  55.4 1.9 %fusion = f32[128,128]{1,0:T(8,128)S(1)} fusion(pred[16,2]{1,0:T(8,128)(4,1)S(1)} %get-tuple-element.14, pred[16,2]{1,0:T(8,128)(4,1)S(1)} %get-tuple-element.13, pred[16,2]{1,0:T(8,128)(4,1)S(1)} %get-tuple-element.12, pred[16,2]{1,0:T(8,128)(4,1)S(1)} %get-tuple-element.11, bf16[16,128,128]{2,1,0:T(8,128)(2,1)S(1)} %bitcast.68, ...), kind=kOutput, calls=%fused_computation.6 | convolution fusion | flops 136855552 | bytes 3276944 | tf_op jit(solution)/shard_map/jspq,jspr->qr/dot_general | solution.py:27
  57.3 0.0 copy-done.2
  57.3 0.0 copy-done.3
  57.4 0.0 copy-done.4
  57.4 0.0 copy-done.1
  57.4 0.3 bitcast_convert_fusion.1
  57.7 20.6 %all-gather = bf16[2048,128]{0,1:T(8,128)(2,1)S(1)} all-gather(bf16[128,128]{0,1:T(8,128)(2,1)S(1)} %get-tuple-element.15), channel_id=2, replica_groups=mesh['groups'=2,'wide'=16] {'wide'}, dimensions={0}, use_global_device_ids=true | all-gather | bytes 557056 | tf_op jit(solution)/shard_map/all_gather | solution.py:37
  78.3 0.3 copy.14
  78.6 2.3 %fusion.1 = f32[128,128]{1,0:T(8,128)S(1)} fusion(pred[16,2]{1,0:T(8,128)(4,1)S(1)} %get-tuple-element.14, pred[16,2]{1,0:T(8,128)(4,1)S(1)} %get-tuple-element.13, pred[16,2]{1,0:T(8,128)(4,1)S(1)} %get-tuple-element.12, pred[16,2]{1,0:T(8,128)(4,1)S(1)} %get-tuple-element.11, bf16[16,128,128]{2,1,0:T(8,128)(2,1)S(1)} %bitcast.59, ...), kind=kOutput, calls=%fused_computation.7 | convolution fusion | flops 136855552 | bytes 3276944 | tf_op jit(solution)/shard_map/jspq,jspr->qr/dot_general | solution.py:27
  80.8 0.3 bitcast_convert_fusion
  81.1 18.9 %all-gather.1 = bf16[2048,128]{0,1:T(8,128)(2,1)S(1)} all-gather(bf16[128,128]{0,1:T(8,128)(2,1)S(1)} %get-tuple-element.17), channel_id=3, replica_groups=mesh['groups'=2,'wide'=16] {'wide'}, dimensions={0}, use_global_device_ids=true | all-gather | bytes 557056 | tf_op jit(solution)/shard_map/all_gather | solution.py:37
  100.0 1.0 copy.15
  101.0 2.3 %fusion.2 = f32[128,128]{1,0:T(8,128)S(1)} fusion(pred[16,2]{1,0:T(8,128)(4,1)S(1)} %get-tuple-element.14, pred[16,2]{1,0:T(8,128)(4,1)S(1)} %get-tuple-element.13, pred[16,2]{1,0:T(8,128)(4,1)S(1)} %get-tuple-element.12, pred[16,2]{1,0:T(8,128)(4,1)S(1)} %get-tuple-element.11, bf16[16,128,128]{2,1,0:T(8,128)(2,1)} %bitcast.61, ...), kind=kOutput, calls=%fused_computation.8 | convolution fusion | flops 136855552 | bytes 3276944 | tf_op jit(solution)/shard_map/jspq,jspr->qr/dot_general | solution.py:27
  103.3 0.3 convolution_bitcast_fusion
  103.6 0.8 copy.10
  (5 shorter events, 0.0 us)
Async XLA Ops:
  6.5 4.0 %copy-start = (bf16[1,16,2,128,128]{4,3,2,1,0:T(8,128)(2,1)S(1)}, bf16[1,16,2,128,128]{4,3,2,1,0:T(8,128)(2,1)}, u32[]{:S(2)}) copy-start(bf16[1,16,2,128,128]{4,3,2,1,0:T(8,128)(2,1)} %param.6) | copy-start | bytes 3145732
  6.5 47.2 %all-gather.4.cloned.1.call-start = ((), (), s32[]{:S(2)}) async-start(), calls=%async_computation | async-start | bytes 2228224 | tf_op jit(solution)/shard_map/all_gather | solution.py:17
  55.4 2.0 %copy-start.2 = (bf16[1,2048,128]{2,1,0:T(8,128)(2,1)}, bf16[1,2048,128]{2,1,0:T(8,128)(2,1)S(1)}, u32[]{:S(2)}) copy-start(bf16[1,2048,128]{2,1,0:T(8,128)(2,1)S(1)} %get-tuple-element.7) | copy-start | bytes 1572868
  55.4 2.0 %copy-start.3 = (bf16[1,2048,128]{2,1,0:T(8,128)(2,1)}, bf16[1,2048,128]{2,1,0:T(8,128)(2,1)S(1)}, u32[]{:S(2)}) copy-start(bf16[1,2048,128]{2,1,0:T(8,128)(2,1)S(1)} %get-tuple-element.10) | copy-start | bytes 1572868
  55.4 2.0 %copy-start.4 = (bf16[1,2048,128]{2,1,0:T(8,128)(2,1)}, bf16[1,2048,128]{2,1,0:T(8,128)(2,1)S(1)}, u32[]{:S(2)}) copy-start(bf16[1,2048,128]{2,1,0:T(8,128)(2,1)S(1)} %get-tuple-element.8) | copy-start | bytes 1572868
  55.4 2.0 %copy-start.1 = (f32[1,128,128]{2,1,0:T(8,128)S(1)}, f32[1,128,128]{2,1,0:T(8,128)}, u32[]{:S(2)}) copy-start(f32[1,128,128]{2,1,0:T(8,128)} %param.11) | copy-start | bytes 196612
Sparse Core Ops, SparseCore 0:
  9.5 44.1 all-gather.3
where the time goes:
time: 112 us; the launch traced here: 111 us
  waiting for transfers between devices  43.1 us (38%)
  blocking collectives  39.5 us (35%)
  between operations  13.5 us (12%)
  matrix products  7.31 us (7%)
  local copies, waits for them, and re-layouts  5.84 us (5%)
  other arithmetic  2.01 us (2%)
    all_gather x1, waiting for transfers between devices, per_device(): later = lax.all_gather(later_current, 'wide', axis=1, tiled=True)  42.4 us
    all_gather x2, blocking collectives, per_device(): history[moment] = lax.all_gather(rounded, 'wide', axis=0, tiled=True)  39.5 us
    dot_general x3, matrix products, per_device(): jnp.einsum('jspq,jspr->qr', local_tiles, chosen, preferred_element_type=j...  6.46 us
  transfers between devices with their start and end apart: 1, of which 1 were waited for; matrix products, arithmetic and copies ran while one was open for 4% of the time, Pallas kernels for 0%

commit v1 on v0

v1 whole, which is shorter than its diff:
```python
import functools

import jax
import jax.numpy as jnp
from jax import lax
from jax.sharding import PartitionSpec as P


def inner_size(wide):
    for size in (4, 2):
        if wide % size == 0:
            return size
    return 1


def gather_lines_first(x, wide, inner):
    lines = wide // inner
    line_groups = [[z * inner + k for z in range(lines)] for k in range(inner)]
    along = lax.all_gather(x, "wide", axis=0, tiled=False, axis_index_groups=line_groups)
    parts = [along]
    for m in range(1, inner):
        parts.append(lax.ppermute(along, "wide", [(d, d ^ m) for d in range(wide)]))
    return jnp.stack(parts).reshape((wide,) + x.shape)


def rowwise(tiles, currents):
    spec = "slpq,slpr->qr" if tiles.ndim == 4 else "spq,spr->qr"
    return jnp.einsum(spec, tiles, currents, preferred_element_type=jnp.float32)


def per_device(wide, retarded_tiles, tile_lags, block_owner, later_current, excitation, inverse_blocks):
    inner = inner_size(wide)
    lines = wide // inner
    lag_count = later_current.shape[0]
    step_count = excitation.shape[0]
    me = lax.axis_index("wide")
    own = me % inner

    slot = jnp.arange(wide, dtype=jnp.int32)
    slot_block = (slot % lines) * inner + jnp.bitwise_xor(own, slot // lines)
    block = jnp.arange(wide, dtype=jnp.int32)
    block_slot = jnp.bitwise_xor(block % inner, own) * lines + block // inner

    column_of_block = jnp.argsort(block_owner)
    column_of_slot = jnp.take(column_of_block, slot_block, axis=0)
    tiles = jnp.take(retarded_tiles[0], column_of_slot, axis=0)
    lags = jnp.take(tile_lags[0], column_of_slot, axis=0)

    zero = jnp.zeros_like(tiles[:, 0])
    by_lag = jnp.stack(
        [
            jnp.where(
                (lags[:, 0] == lag)[:, None, None],
                tiles[:, 0],
                jnp.where((lags[:, 1] == lag)[:, None, None], tiles[:, 1], zero),
            )
            for lag in range(1, lag_count + 1)
        ],
        axis=1,
    )

    later = gather_lines_first(later_current, wide, inner)
    inverse_t = inverse_blocks[0].T

    def advance(moment, retarded):
        source = excitation[moment] - retarded
        return jnp.dot(
            inverse_t, source, precision=lax.Precision.HIGHEST, preferred_element_type=jnp.float32
        )

    by_block = jnp.take(by_lag[:, :2], block_slot, axis=0)

    results = [None] * step_count
    newer = {}
    for moment in range(step_count - 1, -1, -1):
        known = [
            delay for delay in range(1, lag_count + 1) if moment + delay >= step_count
        ]
        first = known[0]
        retarded = rowwise(
            by_lag[:, first - 1 :],
            later[:, moment + first - step_count : moment + lag_count + 1 - step_count],
        )
        for delay in range(1, first):
            retarded = retarded + rowwise(by_block[:, delay - 1], newer[moment + delay])
        current = advance(moment, retarded)
        results[moment] = current
        if moment > 0:
            newer[moment] = lax.all_gather(
                current.astype(jnp.bfloat16), "wide", axis=0, tiled=False
            )
    return jnp.stack(results)


def solution(mesh):
    in_specs = (
        P(("groups", "wide"), None, None, None, None),
        P(("groups", "wide"), None, None),
        P("groups"),
        P(None, ("groups", "wide"), None),
        P(None, ("groups", "wide"), None),
        P(("groups", "wide"), None, None),
    )
    out_specs = P(None, ("groups", "wide"), None)
    return jax.shard_map(
        functools.partial(per_device, mesh.shape["wide"]), mesh=mesh, in_specs=in_specs, out_specs=out_specs, check_vma=False
    )
```

time: 112 us -> 97.1 us (0.87)
  waiting for transfers between devices: 43.1 us -> 11.2 us
  blocking collectives: 39.5 us -> 58.4 us
  between operations: 13.5 us -> 0.23 us
  other arithmetic: 2.01 us -> 7.08 us
  local copies, waits for them, and re-layouts: 5.84 us -> 10.6 us
  starting transfers between devices: 0.01 us -> 1.86 us
    all_gather x1 -> x0, waiting for transfers between devices: 42.4 us -> none  [per_device(): later = lax.all_gather(later_current, 'wide', axis=1, tiled=True)]
    all_gather x2 -> x3, blocking collectives: 39.5 us -> 58.4 us  [the longest x2 40.7 us: per_device(): lax.all_gather(current.astype(jnp.bfloat16), 'wide', axis=0, tiled=False)]
    ppermute x0 -> x3, waiting for transfers between devices: none -> 11.2 us  [gather_lines_first(): parts.append(lax.ppermute(along, 'wide', [(d, d ^ m) for d in range(wide)]))]
    gather x2 -> x6, local copies, waits for them, and re-layouts: 1.31 us -> 6.27 us  [the longest x2 3.3 us: per_device(): tiles = jnp.take(retarded_tiles[0], column_of_slot, axis=0)]
    select_n x1 -> x7, other arithmetic: 0.01 us -> 3.13 us  [the longest x2 1.39 us: per_device(): by_block = jnp.take(by_lag[:, :2], block_slot, axis=0)]
    unnamed x10 -> x20, local copies, waits for them, and re-layouts: 0.02 us -> 2 us
    ppermute x0 -> x3, starting transfers between devices: none -> 1.86 us  [gather_lines_first(): parts.append(lax.ppermute(along, 'wide', [(d, d ^ m) for d in range(wide)]))]
    another operation x0 -> x2, other arithmetic: none -> 1.71 us  [the longest x1 1.62 us: gather_lines_first(): return jnp.stack(parts).reshape((wide,) + x.shape)]
  transfers between devices with their start and end apart: 1 -> 3, of which waited for: 1 -> 1; matrix products, arithmetic and copies ran while one was open for 4% -> 12% of each run, Pallas kernels for 0% -> 0%
where the time goes in v1:
time: 97.1 us; the launch traced here: 96.8 us
  blocking collectives  58.4 us (60%)
  waiting for transfers between devices  11.2 us (12%)
  local copies, waits for them, and re-layouts  10.6 us (11%)
  matrix products  7.38 us (8%)
  other arithmetic  7.08 us (7%)
  starting transfers between devices  1.86 us (2%)
    all_gather x2, blocking collectives, per_device(): lax.all_gather(current.astype(jnp.bfloat16), 'wide', axis=0, tiled=False)  40.7 us
    all_gather x1, blocking collectives, gather_lines_first(): lax.all_gather(x, 'wide', axis=0, tiled=False, axis_index_groups=line_gro...  17.7 us
    ppermute x3, waiting for transfers between devices, gather_lines_first(): parts.append(lax.ppermute(along, 'wide', [(d, d ^ m) for d in range(wide)]))  11.2 us
    dot_general x6, matrix products, rowwise(): return jnp.einsum(spec, tiles, currents, preferred_element_type=jnp.float32)  6.53 us
    gather x2, local copies, waits for them, and re-layouts, per_device(): tiles = jnp.take(retarded_tiles[0], column_of_slot, axis=0)  3.3 us
    unnamed x20, local copies, waits for them, and re-layouts  2 us
  transfers between devices with their start and end apart: 3, of which 1 were waited for; matrix products, arithmetic and copies ran while one was open for 12% of the time, Pallas kernels for 0%

profile of v1, /device:TPU:0, one launch (start us, length us, event | category | flops | bytes accessed | tf_op | source)
XLA Modules:
  0.0 96.8 jit_solution(7875907550957481972)
XLA Ops:
  0.0 17.7 %all-gather = bf16[16,128,128]{2,1,0:T(8,128)(2,1)S(1)} all-gather(bf16[4,128,128]{2,1,0:T(8,128)(2,1)} %param.11), channel_id=2, replica_groups={{0,4,8,12},{1,5,9,13},{2,6,10,14},{3,7,11,15},{16,20,24,28},{17,21,25,2..., dimensions={0}, use_global_device_ids=true | all-gather | bytes 655360 | tf_op jit(solution)/shard_map/all_gather | solution.py:19
  17.7 0.9 copy.26
  18.6 0.0 collective-permute-start.2
  18.6 1.6 %collective-permute-start.1 = (bf16[4,4,128,128]{3,2,0,1:T(8,128)(2,1)}, bf16[4,4,128,128]{3,2,0,1:T(8,128)(2,1)}, u32[]{:S(2)}, u32[]{:S(2)}) collective-permute-start(bf16[4,4,128,128]{3,2,0,1:T(8,128)(2,1)} %copy.26), channel_id=1, source_target_pairs={{0,2},{1,3},{2,0},{3,1},{4,6},{5,7},{6,4},{7,5},{8,10},{9,11},{10,... | collective-permute-start | bytes 1572872 | tf_op jit(solution)/shard_map/ppermute | solution.py:22
  20.1 0.3 collective-permute-start
  20.4 0.1 fusion.57
  20.6 1.9 %sort.17 = (s32[16]{0:T(128)}, s32[16]{0:T(128)S(1)}) sort(s32[16]{0:T(128)} %param.10, s32[16]{0:T(128)S(1)} %iota.22), dimensions={0}, to_apply=%region_0.1 | sort | flops 64 | bytes 256 | tf_op jit(solution)/shard_map/jit(argsort)/sort | solution.py:44
  22.5 0.7 gather_fusion
  23.2 0.1 copy.23
  23.3 0.1 fusion.52
  23.4 0.1 copy.24
  23.5 0.6 gather_fusion.1
  24.0 0.1 broadcast_select_fusion.2
  24.1 0.3 compare_reduce_fusion.3
  24.4 1.7 %gather_fusion.2 = bf16[16,2,128,128]{3,2,1,0:T(8,128)(2,1)} fusion(bf16[16,2,128,128]{3,2,1,0:T(8,128)(2,1)S(1)} %bitcast.84, s32[1024]{0:T(1024)S(1)} %pad_clamp_fusion.1), kind=kCustom, calls=%fused_computation.clone | custom fusion | bytes 2097216 | tf_op jit(solution)/shard_map/jit(_take)/gather | solution.py:46
  26.1 1.6 %copy.25 = bf16[16,2,128,128]{2,3,0,1:T(8,128)(2,1)S(1)} copy(bf16[16,2,128,128]{3,2,1,0:T(8,128)(2,1)} %gather_fusion.2) | data formatting | bytes 2097152 | tf_op jit(solution)/shard_map/jit(_take)/gather | solution.py:46
  27.7 0.2 broadcast_select_fusion.1
  27.9 1.3 %select_select_fusion.1 = (bf16[16,1,128,128]{2,3,0,1:T(8,128)(2,1)S(1)}, bf16[16,1,128,128]{2,3,0,1:T(8,128)(2,1)S(1)}, bf16[16,1,128,128]{2,3,0,1:T(8,128)(2,1)}, bf16[16,1,128,128]{2,3,0,1:T(8,128)(2,1)}) fusion(pred[16]{0:T(512)(128)(4,1)S(1)} %get-tuple-element.12, pred[16]{0:T(512)(128)(4,1)S(1)} %get-tuple-element.8, ...), kind=kLoop, calls=%fused_computation.43 | loop fusion | flops 2097152 | bytes 3145856 | tf_op jit(solution)/shard_map/jit(_where)/select_n | solution.py:52
  29.1 0.8 copy-done.4
  29.9 0.1 pad_maximum_fusion.1
  30.0 1.7 %gather_fusion.3 = bf16[16,2,128,128]{2,3,1,0:T(8,128)(2,1)} fusion(bf16[16,2,128,128]{2,3,0,1:T(8,128)(2,1)S(1)} %pad_maximum_fusion.1, s32[1024]{0:T(1024)S(1)} %pad_clamp_fusion), kind=kCustom, calls=%fused_computation.1.clone | custom fusion | bytes 2097216 | tf_op jit(solution)/shard_map/jit(_take)/gather | solution.py:71
  31.7 1.4 %broadcast_select_fusion = bf16[16,2,128,128]{2,3,1,0:T(8,128)(2,1)S(1)} fusion(bf16[16,2,128,128]{2,3,1,0:T(8,128)(2,1)} %gather_fusion.3, pred[16]{0:T(512)(128)(4,1)S(1)} %compare_and_fusion), kind=kLoop, calls=%fused_computation.38 | loop fusion | flops 524288 | bytes 2097168 | tf_op jit(solution)/shard_map/jit(_take)/select_n | solution.py:71
  33.1 0.0 collective-permute-done.2
  33.1 11.2 %collective-permute-done.1 = bf16[4,4,128,128]{3,2,0,1:T(8,128)(2,1)} collective-permute-done((bf16[4,4,128,128]{3,2,0,1:T(8,128)(2,1)}, bf16[4,4,128,128]{3,2,0,1:T(8,128)(2,1)}, u32[]{:S(2)}, u32[]{:S(2)}) %collective-permute-start.1) | collective-permute-done | bytes 524320 | tf_op jit(solution)/shard_map/ppermute | solution.py:22
  44.3 0.0 collective-permute-done
  44.3 1.6 %pad_maximum_fusion = bf16[4,4,4,128,128]{4,3,1,0,2:T(8,128)(2,1)S(1)} fusion(bf16[1,4,4,128,128]{4,3,1,0,2:T(8,128)(2,1)} %bitcast.8, bf16[1,4,4,128,128]{4,3,1,0,2:T(8,128)(2,1)} %bitcast.7, bf16[1,4,4,128,128]{4,3,1,0,2:T(8,128)(2,1)} %bitcast.6, bf16[1,4,4,128,128]{4,3,2,1,0:T(8,128)(2,1)S(1)} %bitcast.88), kind=kLoop, calls=%fused_computation.4 | loop fusion | flops 8388608 | bytes 4194304 | tf_op jit(solution)/shard_map/stack | solution.py:23
  46.0 0.0 copy-start.1
  46.0 0.0 copy-done.3
  46.0 0.0 copy-done.5
  46.0 0.0 copy-done.7
  46.0 0.2 copy-done.8
  46.2 1.7 %fusion.33 = f32[128,128]{1,0:T(8,128)S(1)} fusion(bf16[16,4,128,128]{3,2,0,1:T(8,128)(2,1)S(1)} %bitcast.89, bf16[16,1,128,128]{2,3,0,1:T(8,128)(2,1)S(1)} %copy-done.8, bf16[16,1,128,128]{2,3,0,1:T(8,128)(2,1)S(1)} %copy-done.7, bf16[16,1,128,128]{2,3,0,1:T(8,128)(2,1)S(1)} %get-tuple-element.19, bf16[16,1,128,128]{2,3,0,1:T(8,128)(2,1)S(1)} %copy-done.5, ...), kind=kOutput, calls=%fused_computation.29 | convolution fusion | flops 271597568 | bytes 4325376 | tf_op jit(solution)/shard_map/slpq,slpr->qr/dot_general | solution.py:28
  47.9 0.0 copy-done.1
  47.9 0.0 copy-done.6
  47.9 0.3 bitcast_convert_fusion.1
  48.2 21.9 %all-gather.1 = bf16[2048,128]{0,1:T(8,128)(2,1)S(1)} all-gather(bf16[128,128]{0,1:T(8,128)(2,1)S(1)} %get-tuple-element.22), channel_id=3, replica_groups=mesh['groups'=2,'wide'=16] {'wide'}, dimensions={0}, use_global_device_ids=true | all-gather | bytes 557056 | tf_op jit(solution)/shard_map/all_gather | solution.py:89
  70.0 0.3 copy.38
  70.3 0.3 convolution_bitcast_fusion.1
  70.6 0.3 convolution_bitcast_fusion.3
  70.9 1.0 %copy-done.2 = bf16[4,4,4,128,128]{4,3,1,0,2:T(8,128)(2,1)S(1)} copy-done((bf16[4,4,4,128,128]{4,3,1,0,2:T(8,128)(2,1)S(1)}, bf16[4,4,4,128,128]{4,3,1,0,2:T(8,128)(2,1)}, u32[]{:S(2)}) %copy-start.2) | copy-done | bytes 2097176
  71.9 2.0 %fusion.28 = f32[128,128]{1,0:T(8,128)S(1)} fusion(f32[128,128]{1,0:T(8,128)S(1)} %convolution_bitcast_fusion.3, bf16[16,4,128,128]{3,2,0,1:T(8,128)(2,1)S(1)} %bitcast.91, bf16[16,1,128,128]{2,3,0,1:T(8,128)(2,1)} %get-tuple-element.21, bf16[16,1,128,128]{2,3,0,1:T(8,128)(2,1)} %get-tuple-element.20, bf16[16,1,128,128]{2,3,0,1:T(8,128)(2,1)} %copy-done.3, ...), kind=kOutput, calls=%fused_computation.28 | convolution fusion | flops 202932224 | bytes 3342336 | tf_op jit(solution)/shard_map/slpq,slpr->qr/dot_general | solution.py:28
  73.9 0.3 bitcast_convert_fusion
  74.2 18.9 %all-gather.2 = bf16[2048,128]{0,1:T(8,128)(2,1)S(1)} all-gather(bf16[128,128]{0,1:T(8,128)(2,1)S(1)} %get-tuple-element.24), channel_id=4, replica_groups=mesh['groups'=2,'wide'=16] {'wide'}, dimensions={0}, use_global_device_ids=true | all-gather | bytes 557056 | tf_op jit(solution)/shard_map/all_gather | solution.py:89
  93.1 0.3 copy.37
  93.3 0.3 convolution_bitcast_fusion.2
  93.6 2.0 %fusion.38 = f32[128,128]{1,0:T(8,128)S(1)} fusion(f32[128,128]{1,0:T(8,128)S(1)} %convolution_bitcast_fusion.1, f32[128,128]{1,0:T(8,128)S(1)} %convolution_bitcast_fusion.2, bf16[16,4,128,128]{3,2,0,1:T(8,128)(2,1)} %bitcast.90, bf16[16,1,128,128]{2,3,0,1:T(8,128)(2,1)} %get-tuple-element.21, bf16[16,1,128,128]{2,3,0,1:T(8,128)(2,1)} %get-tuple-element.20, ...), kind=kOutput, calls=%fused_computation.32 | convolution fusion | flops 134791168 | bytes 2359296 | tf_op jit(solution)/shard_map/slpq,slpr->qr/dot_general | solution.py:28
  95.6 0.3 convolution_bitcast_fusion
  96.0 0.8 copy.33
  (20 shorter events, 0.1 us)
Async XLA Ops:
  0.0 24.4 %copy-start = (bf16[1,16,2,128,128]{4,3,2,1,0:T(8,128)(2,1)S(1)}, bf16[1,16,2,128,128]{4,3,2,1,0:T(8,128)(2,1)}, u32[]{:S(2)}) copy-start(bf16[1,16,2,128,128]{4,3,2,1,0:T(8,128)(2,1)} %param.8) | copy-start | bytes 3145732
  0.0 23.4 %copy-start.9 = (s32[1,16,2]{1,2,0:T(2,128)S(1)}, s32[1,16,2]{1,2,0:T(2,128)}, u32[]{:S(2)}) copy-start(s32[1,16,2]{1,2,0:T(2,128)} %param.9) | copy-start | bytes 388
  18.6 14.5 %collective-permute-start.2 = (bf16[4,4,128,128]{3,2,0,1:T(8,128)(2,1)}, bf16[4,4,128,128]{3,2,0,1:T(8,128)(2,1)}, u32[]{:S(2)}, u32[]{:S(2)}) collective-permute-start(bf16[4,4,128,128]{3,2,0,1:T(8,128)(2,1)} %copy.26), channel_id=1, source_target_pairs={{0,3},{1,2},{2,1},{3,0},{4,7},{5,6},{6,5},{7,4},{8,11},{9,10},{10,... | collective-permute-start | bytes 1572872 | tf_op jit(solution)/shard_map/ppermute | solution.py:22
  18.6 25.8 %collective-permute-start.1 = (bf16[4,4,128,128]{3,2,0,1:T(8,128)(2,1)}, bf16[4,4,128,128]{3,2,0,1:T(8,128)(2,1)}, u32[]{:S(2)}, u32[]{:S(2)}) collective-permute-start(bf16[4,4,128,128]{3,2,0,1:T(8,128)(2,1)} %copy.26), channel_id=1, source_target_pairs={{0,2},{1,3},{2,0},{3,1},{4,6},{5,7},{6,4},{7,5},{8,10},{9,11},{10,... | collective-permute-start | bytes 1572872 | tf_op jit(solution)/shard_map/ppermute | solution.py:22
  20.1 24.2 %collective-permute-start = (bf16[4,4,128,128]{3,2,0,1:T(8,128)(2,1)}, bf16[4,4,128,128]{3,2,0,1:T(8,128)(2,1)}, u32[]{:S(2)}, u32[]{:S(2)}) collective-permute-start(bf16[4,4,128,128]{3,2,0,1:T(8,128)(2,1)} %copy.26), channel_id=1, source_target_pairs={{0,1},{1,0},{2,3},{3,2},{4,5},{5,4},{6,7},{7,6},{8,9},{9,8},{10,11... | collective-permute-start | bytes 1572872 | tf_op jit(solution)/shard_map/ppermute | solution.py:22
  29.1 0.8 copy-start.4
  29.1 16.8 %copy-start.3 = (bf16[16,1,128,128]{2,3,0,1:T(8,128)(2,1)}, bf16[16,1,128,128]{2,3,0,1:T(8,128)(2,1)S(1)}, u32[]{:S(2)}) copy-start(bf16[16,1,128,128]{2,3,0,1:T(8,128)(2,1)S(1)} %get-tuple-element.19) | copy-start | bytes 1572868
  44.3 1.7 %copy-start.5 = (bf16[16,1,128,128]{2,3,0,1:T(8,128)(2,1)S(1)}, bf16[16,1,128,128]{2,3,0,1:T(8,128)(2,1)}, u32[]{:S(2)}) copy-start(bf16[16,1,128,128]{2,3,0,1:T(8,128)(2,1)} %copy-done.4) | copy-start | bytes 1572868
  44.3 1.7 %copy-start.7 = (bf16[16,1,128,128]{2,3,0,1:T(8,128)(2,1)S(1)}, bf16[16,1,128,128]{2,3,0,1:T(8,128)(2,1)}, u32[]{:S(2)}) copy-start(bf16[16,1,128,128]{2,3,0,1:T(8,128)(2,1)} %get-tuple-element.20) | copy-start | bytes 1572868
  44.3 1.8 %copy-start.8 = (bf16[16,1,128,128]{2,3,0,1:T(8,128)(2,1)S(1)}, bf16[16,1,128,128]{2,3,0,1:T(8,128)(2,1)}, u32[]{:S(2)}) copy-start(bf16[16,1,128,128]{2,3,0,1:T(8,128)(2,1)} %get-tuple-element.21) | copy-start | bytes 1572868
  46.0 1.9 %copy-start.1 = (bf16[4,4,4,128,128]{4,3,1,0,2:T(8,128)(2,1)}, bf16[4,4,4,128,128]{4,3,1,0,2:T(8,128)(2,1)S(1)}, u32[]{:S(2)}) copy-start(bf16[4,4,4,128,128]{4,3,1,0,2:T(8,128)(2,1)S(1)} %pad_maximum_fusion) | copy-start | bytes 6291460
  46.2 1.7 %copy-start.6 = (f32[1,128,128]{2,1,0:T(8,128)S(1)}, f32[1,128,128]{2,1,0:T(8,128)}, u32[]{:S(2)}) copy-start(f32[1,128,128]{2,1,0:T(8,128)} %param.13) | copy-start | bytes 196612
  70.3 1.6 %copy-start.2 = (bf16[4,4,4,128,128]{4,3,1,0,2:T(8,128)(2,1)S(1)}, bf16[4,4,4,128,128]{4,3,1,0,2:T(8,128)(2,1)}, u32[]{:S(2)}) copy-start(bf16[4,4,4,128,128]{4,3,1,0,2:T(8,128)(2,1)} %copy-done.1) | copy-start | bytes 6291460

commit v2 on v1

v2 whole, which is shorter than its diff:
```python
import functools

import jax
import jax.numpy as jnp
import numpy as np
from jax import lax
from jax.sharding import PartitionSpec as P


def inner_size(wide):
    for size in (4, 2):
        if wide % size == 0:
            return size
    return 1


def line_stage(x, wide, inner):
    lines = wide // inner
    if lines <= 4:
        parts = [x]
        for shift in range(1, lines):
            pairs = [
                (d, ((d // inner + shift) % lines) * inner + d % inner) for d in range(wide)
            ]
            parts.append(lax.ppermute(x, "wide", pairs))
        return jnp.stack(parts), True
    groups = [[z * inner + k for z in range(lines)] for k in range(inner)]
    return lax.all_gather(x, "wide", axis=0, tiled=False, axis_index_groups=groups), False


def slab_stage(stack, wide, inner, doubling):
    if doubling:
        masks = np.zeros((1,), np.int32)
        bit = inner // 2
        while bit >= 1:
            other = lax.ppermute(stack, "wide", [(d, d ^ bit) for d in range(wide)])
            stack = jnp.stack([stack, other])
            masks = np.concatenate([masks, masks ^ bit])
            bit //= 2
        return stack, masks
    parts = [stack]
    for m in range(1, inner):
        parts.append(lax.ppermute(stack, "wide", [(d, d ^ m) for d in range(wide)]))
    return jnp.stack(parts), np.arange(inner, dtype=np.int32)


def gather_blocks(x, wide, doubling):
    inner = inner_size(wide)
    lines = wide // inner
    stack, shifted = line_stage(x, wide, inner)
    stack, masks = slab_stage(stack, wide, inner, doubling)
    me = lax.axis_index("wide")
    line = np.arange(lines, dtype=np.int32)
    source_line = (me // inner - line) % lines if shifted else jnp.asarray(line)
    blocks = (
        source_line[None, :] * inner
        + jnp.bitwise_xor(me % inner, jnp.asarray(masks))[:, None]
    )
    return stack.reshape((wide,) + x.shape), blocks.reshape(wide)


def tiles_by_lag(retarded_tiles, tile_lags, column_of_block, block_of_slot, lags_wanted):
    columns = jnp.take(column_of_block, block_of_slot, axis=0)
    tiles = jnp.take(retarded_tiles[0], columns, axis=0)
    lags = jnp.take(tile_lags[0], columns, axis=0)
    zero = jnp.zeros_like(tiles[:, 0])
    return jnp.stack(
        [
            jnp.where(
                (lags[:, 0] == lag)[:, None, None],
                tiles[:, 0],
                jnp.where((lags[:, 1] == lag)[:, None, None], tiles[:, 1], zero),
            )
            for lag in lags_wanted
        ],
        axis=1,
    )


def rowwise(tiles, currents):
    spec = "slpq,slpr->qr" if tiles.ndim == 4 else "spq,spr->qr"
    return jnp.einsum(spec, tiles, currents, preferred_element_type=jnp.float32)


def per_device(wide, retarded_tiles, tile_lags, block_owner, later_current, excitation, inverse_blocks):
    lag_count = later_current.shape[0]
    step_count = excitation.shape[0]
    column_of_block = jnp.argsort(block_owner)

    later, later_blocks = gather_blocks(later_current, wide, True)
    by_lag = tiles_by_lag(
        retarded_tiles, tile_lags, column_of_block, later_blocks, range(1, lag_count + 1)
    )
    inverse_t = inverse_blocks[0].T

    def advance(moment, retarded):
        source = excitation[moment] - retarded
        return jnp.dot(
            inverse_t, source, precision=lax.Precision.HIGHEST, preferred_element_type=jnp.float32
        )

    results = [None] * step_count
    newer = {}
    recent = None
    for moment in range(step_count - 1, -1, -1):
        first = max(1, step_count - moment)
        retarded = rowwise(
            by_lag[:, first - 1 :],
            later[:, moment + first - step_count : moment + lag_count + 1 - step_count],
        )
        for delay in range(1, first):
            retarded = retarded + rowwise(recent[:, delay - 1], newer[moment + delay])
        current = advance(moment, retarded)
        results[moment] = current
        if moment > 0:
            newer[moment], new_blocks = gather_blocks(current.astype(jnp.bfloat16), wide, False)
            if recent is None:
                recent = tiles_by_lag(
                    retarded_tiles,
                    tile_lags,
                    column_of_block,
                    new_blocks,
                    range(1, min(lag_count, step_count - 1) + 1),
                )
    return jnp.stack(results)


def solution(mesh):
    in_specs = (
        P(("groups", "wide"), None, None, None, None),
        P(("groups", "wide"), None, None),
        P("groups"),
        P(None, ("groups", "wide"), None),
        P(None, ("groups", "wide"), None),
        P(("groups", "wide"), None, None),
    )
    out_specs = P(None, ("groups", "wide"), None)
    return jax.shard_map(
        functools.partial(per_device, mesh.shape["wide"]),
        mesh=mesh,
        in_specs=in_specs,
        out_specs=out_specs,
        check_vma=False,
    )
```

time: 97.1 us -> 72.3 us (0.74)
  blocking collectives: 58.4 us -> 0 us
  waiting for transfers between devices: 11.2 us -> 35.3 us
  starting transfers between devices: 1.86 us -> 18.2 us
  local copies, waits for them, and re-layouts: 10.6 us -> 6.49 us
  matrix products: 7.38 us -> 3.86 us
    all_gather x3 -> x0, blocking collectives: 58.4 us -> none  [the longest x2 40.7 us: per_device(): lax.all_gather(current.astype(jnp.bfloat16), 'wide', axis=0, tiled=False)]
    ppermute x3 -> x17, waiting for transfers between devices: 11.2 us -> 35.3 us  [the longest x9 13.8 us: line_stage(): parts.append(lax.ppermute(x, 'wide', pairs))]
    ppermute x3 -> x17, starting transfers between devices: 1.86 us -> 18.2 us  [the longest x9 12.7 us: line_stage(): parts.append(lax.ppermute(x, 'wide', pairs))]
    dot_general x6, matrix products: 6.53 us -> 3.01 us  [rowwise(): return jnp.einsum(spec, tiles, currents, preferred_element_type=jnp.float32)]
    gather x6, local copies, waits for them, and re-layouts: 6.27 us -> 3.93 us  [the longest x2 1.5 us: tiles_by_lag(): tiles = jnp.take(retarded_tiles[0], columns, axis=0)]
    select_n x7 -> x8, other arithmetic: 3.13 us -> 0.93 us  [the longest x2 0.45 us: tiles_by_lag(): jnp.where((lags[:, 0] == lag)[:, None, None], tiles[:, 0], jnp.where((lag...]
    another operation x2 -> x7, other arithmetic: 1.71 us -> 3.7 us  [the longest x3 3.51 us: slab_stage(): stack = jnp.stack([stack, other])]
    all_gather x3 -> x0, local copies, waits for them, and re-layouts: 1.4 us -> none  [the longest x1 0.87 us: gather_lines_first(): lax.all_gather(x, 'wide', axis=0, tiled=False, axis_index_groups=line_gro...]
  transfers between devices with their start and end apart: 3 -> 17, of which waited for: 1 -> 12; matrix products, arithmetic and copies ran while one was open for 12% -> 14% of each run, Pallas kernels for 0% -> 0%
where the time goes in v2:
time: 72.3 us; the launch traced here: 71.9 us
  waiting for transfers between devices  35.3 us (49%)
  starting transfers between devices  18.2 us (25%)
  other arithmetic  7.83 us (11%)
  local copies, waits for them, and re-layouts  6.49 us (9%)
  matrix products  3.86 us (5%)
    ppermute x9, waiting for transfers between devices, line_stage(): parts.append(lax.ppermute(x, 'wide', pairs))  13.8 us
    ppermute x9, starting transfers between devices, line_stage(): parts.append(lax.ppermute(x, 'wide', pairs))  12.7 us
    ppermute x2, waiting for transfers between devices, slab_stage(): other = lax.ppermute(stack, 'wide', [(d, d ^ bit) for d in range(wide)])  10.9 us
    ppermute x6, waiting for transfers between devices, slab_stage(): parts.append(lax.ppermute(stack, 'wide', [(d, d ^ m) for d in range(wide)]))  10.6 us
    ppermute x6, starting transfers between devices, slab_stage(): parts.append(lax.ppermute(stack, 'wide', [(d, d ^ m) for d in range(wide)]))  3.83 us
    another operation x3, other arithmetic, slab_stage(): stack = jnp.stack([stack, other])  3.51 us
    dot_general x6, matrix products, rowwise(): return jnp.einsum(spec, tiles, currents, preferred_element_type=jnp.float32)  3.01 us
    sort x1, other arithmetic, per_device(): column_of_block = jnp.argsort(block_owner)  1.9 us
  transfers between devices with their start and end apart: 17, of which 12 were waited for; matrix products, arithmetic and copies ran while one was open for 14% of the time, Pallas kernels for 0%

profile of v2, /device:TPU:0, one launch (start us, length us, event | category | flops | bytes accessed | tf_op | source)
XLA Modules:
  0.0 71.9 jit_solution(7678563131325612580)
XLA Ops:
  0.0 5.0 %collective-permute-start.2 = (bf16[4,128,128]{2,1,0:T(8,128)(2,1)}, bf16[4,128,128]{2,1,0:T(8,128)(2,1)S(1)}, u32[]{:S(2)}, u32[]{:S(2)}) collective-permute-start(bf16[4,128,128]{2,1,0:T(8,128)(2,1)} %param.19), channel_id=1, source_target_pairs={{0,12},{1,13},{2,14},{3,15},{4,0},{5,1},{6,2},{7,3},{8,4},{9,5},{1... | collective-permute-start | bytes 393224 | tf_op jit(solution)/shard_map/ppermute | solution.py:25
  5.1 1.0 %collective-permute-start = (bf16[4,128,128]{2,1,0:T(8,128)(2,1)}, bf16[4,128,128]{2,1,0:T(8,128)(2,1)S(1)}, u32[]{:S(2)}, u32[]{:S(2)}) collective-permute-start(bf16[4,128,128]{2,1,0:T(8,128)(2,1)} %param.19), channel_id=1, source_target_pairs={{0,4},{1,5},{2,6},{3,7},{4,8},{5,9},{6,10},{7,11},{8,12},{9,13},{1... | collective-permute-start | bytes 393224 | tf_op jit(solution)/shard_map/ppermute | solution.py:25
  6.1 0.8 %copy.15 = s32[16,2]{1,0:T(8,128)S(1)} copy(s32[16,2]{0,1:T(2,128)} %bitcast.145) | data formatting | bytes 256 | tf_op jit(solution)/shard_map/squeeze | solution.py:65
  6.8 0.7 iota_xor_fusion
  7.7 1.9 %sort.17 = (s32[16]{0:T(128)}, s32[16]{0:T(128)S(1)}) sort(s32[16]{0:T(128)} %param.18, s32[16]{0:T(128)S(1)} %iota.5), dimensions={0}, to_apply=%region_0.0 | sort | flops 64 | bytes 256 | tf_op jit(solution)/shard_map/jit(argsort)/sort | solution.py:88
  9.6 0.7 gather_fusion
  10.4 0.7 gather_fusion.3
  11.1 5.4 %collective-permute-done.1 = bf16[4,128,128]{2,1,0:T(8,128)(2,1)S(1)} collective-permute-done((bf16[4,128,128]{2,1,0:T(8,128)(2,1)}, bf16[4,128,128]{2,1,0:T(8,128)(2,1)S(1)}, u32[]{:S(2)}, u32[]{:S(2)}) %collective-permute-start.1) | collective-permute-done | bytes 131104 | tf_op jit(solution)/shard_map/ppermute | solution.py:25
  16.5 2.0 %fusion.52 = (bf16[1,4,4,128,128]{4,3,2,1,0:T(8,128)(2,1)}, bf16[4,4,128,128]{3,2,1,0:T(8,128)(2,1)}) fusion(bf16[1,4,128,128]{3,2,1,0:T(8,128)(2,1)S(1)} %bitcast.128, bf16[1,4,128,128]{3,2,1,0:T(8,128)(2,1)S(1)} %bitcast.129, bf16[1,4,128,128]{3,2,1,0:T(8,128)(2,1)S(1)} %bitcast.130, bf16[1,4,128,128]{3,2,1,0:T(8,128)(2,1)} %bitcast.127), kind=kLoop, calls=%fused_computation.99 | loop fusion | flops 786432 | bytes 1572864 | tf_op jit(solution)/shard_map/stack | solution.py:37
  18.5 1.5 %collective-permute-start.3 = (bf16[4,4,128,128]{3,2,1,0:T(8,128)(2,1)}, bf16[4,4,128,128]{3,2,1,0:T(8,128)(2,1)}, u32[]{:S(2)}, u32[]{:S(2)}) collective-permute-start(bf16[4,4,128,128]{3,2,1,0:T(8,128)(2,1)} %get-tuple-element.33), channel_id=1, source_target_pairs={{0,2},{1,3},{2,0},{3,1},{4,6},{5,7},{6,4},{7,5},{8,10},{9,11},{10,... | collective-permute-start | bytes 1572872 | tf_op jit(solution)/shard_map/ppermute | solution.py:36
  20.0 0.6 gather_fusion.1
  20.6 0.7 %gather_fusion.2 = bf16[16,2,128,128]{3,2,1,0:T(8,128)(2,1)S(1)} fusion(bf16[16,2,128,128]{3,2,1,0:T(8,128)(2,1)S(1)} %bitcast.116, s32[1024]{0:T(1024)S(1)} %pad_clamp_fusion.2), kind=kCustom, calls=%fused_computation.2.clone | custom fusion | bytes 2097216 | tf_op jit(solution)/shard_map/jit(_take)/gather | solution.py:64
  21.3 0.6 gather_fusion.4
  21.9 0.7 %gather_fusion.5 = bf16[16,2,128,128]{3,2,1,0:T(8,128)(2,1)S(1)} fusion(bf16[16,2,128,128]{3,2,1,0:T(8,128)(2,1)S(1)} %bitcast.117, s32[1024]{0:T(1024)S(1)} %pad_clamp_fusion), kind=kCustom, calls=%fused_computation.5.clone | custom fusion | bytes 2097216 | tf_op jit(solution)/shard_map/jit(_take)/gather | solution.py:64
  22.7 0.3 compare_reduce_fusion.3
  23.0 9.0 %collective-permute-done.3 = bf16[4,4,128,128]{3,2,1,0:T(8,128)(2,1)} collective-permute-done((bf16[4,4,128,128]{3,2,1,0:T(8,128)(2,1)}, bf16[4,4,128,128]{3,2,1,0:T(8,128)(2,1)}, u32[]{:S(2)}, u32[]{:S(2)}) %collective-permute-start.3) | collective-permute-done | bytes 524320 | tf_op jit(solution)/shard_map/ppermute | solution.py:36
  32.0 1.3 %fusion.51 = (bf16[1,2,4,4,128,128]{5,4,3,2,1,0:T(8,128)(2,1)S(1)}, bf16[2,4,4,128,128]{4,3,2,1,0:T(8,128)(2,1)S(1)}) fusion(bf16[1,4,4,128,128]{4,3,2,1,0:T(8,128)(2,1)} %bitcast.8, bf16[1,4,4,128,128]{4,3,2,1,0:T(8,128)(2,1)} %get-tuple-element.32), kind=kLoop, calls=%fused_computation.98 | loop fusion | flops 524288 | bytes 3145728 | tf_op jit(solution)/shard_map/stack | solution.py:37
  33.8 0.3 select_select_fusion
  34.1 1.9 %collective-permute-done.4 = bf16[2,4,4,128,128]{4,3,2,1,0:T(8,128)(2,1)S(1)} collective-permute-done((bf16[2,4,4,128,128]{4,3,2,1,0:T(8,128)(2,1)S(1)}, bf16[2,4,4,128,128]{4,3,2,1,0:T(8,128)(2,1)S(1)}, u32[]{:S(2)}, u32[]{:S(2)}) %collective-permute-start.4) | collective-permute-done | bytes 1048608 | tf_op jit(solution)/shard_map/ppermute | solution.py:36
  36.2 0.7 %copy-done.2 = f32[3,128,128]{2,1,0:T(8,128)S(1)} copy-done((f32[3,128,128]{2,1,0:T(8,128)S(1)}, f32[3,128,128]{2,1,0:T(8,128)}, u32[]{:S(2)}) %copy-start.2) | copy-done | bytes 196632
  37.0 0.7 %fusion.16 = f32[128,128]{1,0:T(8,128)S(1)} fusion(bf16[16,4,128,128]{3,2,1,0:T(8,128)(2,1)S(1)} %bitcast.118, f32[3,128,128]{2,1,0:T(8,128)S(1)} %copy-done.2, bf16[16,1,128,128]{3,2,1,0:T(8,128)(2,1)S(1)} %get-tuple-element.29, bf16[16,1,128,128]{3,2,1,0:T(8,128)(2,1)S(1)} %get-tuple-element.28, bf16[16,1,128,128]{3,2,1,0:T(8,128)(2,1)S(1)} %get-tuple-element.27, ...), kind=kOutput, calls=%fused_computation.22 | convolution fusion | flops 271597568 | bytes 4325376 | tf_op jit(solution)/shard_map/slpq,slpr->qr/dot_general | solution.py:82
  37.8 0.3 bitcast_convert_fusion.1
  38.1 0.7 collective-permute-start.7
  38.7 2.0 %collective-permute-start.6 = (bf16[128,128]{0,1:T(8,128)(2,1)S(1)}, bf16[128,128]{0,1:T(8,128)(2,1)S(1)}, u32[]{:S(2)}, u32[]{:S(2)}) collective-permute-start(bf16[128,128]{0,1:T(8,128)(2,1)S(1)} %get-tuple-element.40), channel_id=1, source_target_pairs={{0,8},{1,9},{2,10},{3,11},{4,12},{5,13},{6,14},{7,15},{8,0},{9,1},... | collective-permute-start | bytes 98312 | tf_op jit(solution)/shard_map/ppermute | solution.py:25
  40.7 1.9 %collective-permute-start.5 = (bf16[128,128]{0,1:T(8,128)(2,1)S(1)}, bf16[128,128]{0,1:T(8,128)(2,1)S(1)}, u32[]{:S(2)}, u32[]{:S(2)}) collective-permute-start(bf16[128,128]{0,1:T(8,128)(2,1)S(1)} %get-tuple-element.40), channel_id=1, source_target_pairs={{0,4},{1,5},{2,6},{3,7},{4,8},{5,9},{6,10},{7,11},{8,12},{9,13},{1... | collective-permute-start | bytes 98312 | tf_op jit(solution)/shard_map/ppermute | solution.py:25
  42.9 1.0 %collective-permute-done.6 = bf16[128,128]{0,1:T(8,128)(2,1)S(1)} collective-permute-done((bf16[128,128]{0,1:T(8,128)(2,1)S(1)}, bf16[128,128]{0,1:T(8,128)(2,1)S(1)}, u32[]{:S(2)}, u32[]{:S(2)}) %collective-permute-start.6) | collective-permute-done | bytes 32800 | tf_op jit(solution)/shard_map/ppermute | solution.py:25
  43.9 2.6 %collective-permute-done.5 = bf16[128,128]{0,1:T(8,128)(2,1)S(1)} collective-permute-done((bf16[128,128]{0,1:T(8,128)(2,1)S(1)}, bf16[128,128]{0,1:T(8,128)(2,1)S(1)}, u32[]{:S(2)}, u32[]{:S(2)}) %collective-permute-start.5) | collective-permute-done | bytes 32800 | tf_op jit(solution)/shard_map/ppermute | solution.py:25
  46.5 1.6 %collective-permute-start.9 = (bf16[4,128,128]{1,2,0:T(8,128)(2,1)S(1)}, bf16[4,128,128]{1,2,0:T(8,128)(2,1)S(1)}, u32[]{:S(2)}, u32[]{:S(2)}) collective-permute-start(bf16[4,128,128]{1,2,0:T(8,128)(2,1)S(1)} %get-tuple-element.37), channel_id=1, source_target_pairs={{0,2},{1,3},{2,0},{3,1},{4,6},{5,7},{6,4},{7,5},{8,10},{9,11},{10,... | collective-permute-start | bytes 393224 | tf_op jit(solution)/shard_map/ppermute | solution.py:43
  48.1 0.3 collective-permute-start.8
  48.6 3.7 %collective-permute-done.10 = bf16[4,128,128]{1,2,0:T(8,128)(2,1)S(1)} collective-permute-done((bf16[4,128,128]{1,2,0:T(8,128)(2,1)S(1)}, bf16[4,128,128]{1,2,0:T(8,128)(2,1)S(1)}, u32[]{:S(2)}, u32[]{:S(2)}) %collective-permute-start.10) | collective-permute-done | bytes 131104 | tf_op jit(solution)/shard_map/ppermute | solution.py:43
  52.2 2.9 %collective-permute-done.9 = bf16[4,128,128]{1,2,0:T(8,128)(2,1)S(1)} collective-permute-done((bf16[4,128,128]{1,2,0:T(8,128)(2,1)S(1)}, bf16[4,128,128]{1,2,0:T(8,128)(2,1)S(1)}, u32[]{:S(2)}, u32[]{:S(2)}) %collective-permute-start.9) | collective-permute-done | bytes 131104 | tf_op jit(solution)/shard_map/ppermute | solution.py:43
  55.2 0.3 convolution_bitcast_fusion.3
  55.5 0.6 fusion.26
  56.2 0.3 bitcast_convert_fusion
  56.5 0.6 collective-permute-start.13
  57.1 1.0 %collective-permute-start.12 = (bf16[128,128]{0,1:T(8,128)(2,1)S(1)}, bf16[128,128]{0,1:T(8,128)(2,1)S(1)}, u32[]{:S(2)}, u32[]{:S(2)}) collective-permute-start(bf16[128,128]{0,1:T(8,128)(2,1)S(1)} %get-tuple-element.42), channel_id=1, source_target_pairs={{0,8},{1,9},{2,10},{3,11},{4,12},{5,13},{6,14},{7,15},{8,0},{9,1},... | collective-permute-start | bytes 98312 | tf_op jit(solution)/shard_map/ppermute | solution.py:25
  58.1 0.4 collective-permute-start.11
  58.6 0.5 convolution_bitcast_fusion.4
  59.0 1.4 %collective-permute-done.13 = bf16[128,128]{0,1:T(8,128)(2,1)S(1)} collective-permute-done((bf16[128,128]{0,1:T(8,128)(2,1)S(1)}, bf16[128,128]{0,1:T(8,128)(2,1)S(1)}, u32[]{:S(2)}, u32[]{:S(2)}) %collective-permute-start.13) | collective-permute-done | bytes 32800 | tf_op jit(solution)/shard_map/ppermute | solution.py:25
  60.4 1.5 %collective-permute-done.12 = bf16[128,128]{0,1:T(8,128)(2,1)S(1)} collective-permute-done((bf16[128,128]{0,1:T(8,128)(2,1)S(1)}, bf16[128,128]{0,1:T(8,128)(2,1)S(1)}, u32[]{:S(2)}, u32[]{:S(2)}) %collective-permute-start.12) | collective-permute-done | bytes 32800 | tf_op jit(solution)/shard_map/ppermute | solution.py:25
  61.9 1.9 %collective-permute-done.11 = bf16[128,128]{0,1:T(8,128)(2,1)S(1)} collective-permute-done((bf16[128,128]{0,1:T(8,128)(2,1)S(1)}, bf16[128,128]{0,1:T(8,128)(2,1)S(1)}, u32[]{:S(2)}, u32[]{:S(2)}) %collective-permute-start.11) | collective-permute-done | bytes 32800 | tf_op jit(solution)/shard_map/ppermute | solution.py:25
  64.0 1.8 %collective-permute-start.14 = (bf16[4,128,128]{1,2,0:T(8,128)(2,1)S(1)}, bf16[4,128,128]{1,2,0:T(8,128)(2,1)S(1)}, u32[]{:S(2)}, u32[]{:S(2)}) collective-permute-start(bf16[4,128,128]{1,2,0:T(8,128)(2,1)S(1)} %get-tuple-element.35), channel_id=1, source_target_pairs={{0,1},{1,0},{2,3},{3,2},{4,5},{5,4},{6,7},{7,6},{8,9},{9,8},{10,11... | collective-permute-start | bytes 393224 | tf_op jit(solution)/shard_map/ppermute | solution.py:43
  65.8 0.5 convolution_bitcast_fusion.1
  66.3 2.8 %collective-permute-done.16 = bf16[4,128,128]{1,2,0:T(8,128)(2,1)S(1)} collective-permute-done((bf16[4,128,128]{1,2,0:T(8,128)(2,1)S(1)}, bf16[4,128,128]{1,2,0:T(8,128)(2,1)S(1)}, u32[]{:S(2)}, u32[]{:S(2)}) %collective-permute-start.16) | collective-permute-done | bytes 131104 | tf_op jit(solution)/shard_map/ppermute | solution.py:43
  69.1 1.2 %collective-permute-done.15 = bf16[4,128,128]{1,2,0:T(8,128)(2,1)S(1)} collective-permute-done((bf16[4,128,128]{1,2,0:T(8,128)(2,1)S(1)}, bf16[4,128,128]{1,2,0:T(8,128)(2,1)S(1)}, u32[]{:S(2)}, u32[]{:S(2)}) %collective-permute-start.15) | collective-permute-done | bytes 131104 | tf_op jit(solution)/shard_map/ppermute | solution.py:43
  70.4 0.3 fusion.33
  70.8 0.3 convolution_bitcast_fusion
  71.1 0.8 %copy.18 = f32[3,128,128]{2,1,0:T(8,128)} copy(f32[3,128,128]{1,2,0:T(8,128)S(1)} %pad_maximum_fusion.8) | data formatting | bytes 393216 | tf_op jit(solution)/shard_map/stack | solution.py:125
  (40 shorter events, 2.0 us)
Async XLA Ops:
  0.0 20.5 %copy-start = (bf16[1,16,2,128,128]{4,3,2,1,0:T(8,128)(2,1)S(1)}, bf16[1,16,2,128,128]{4,3,2,1,0:T(8,128)(2,1)}, u32[]{:S(2)}) copy-start(bf16[1,16,2,128,128]{4,3,2,1,0:T(8,128)(2,1)} %param.16) | copy-start | bytes 3145732
  0.0 11.0 %collective-permute-start.2 = (bf16[4,128,128]{2,1,0:T(8,128)(2,1)}, bf16[4,128,128]{2,1,0:T(8,128)(2,1)S(1)}, u32[]{:S(2)}, u32[]{:S(2)}) collective-permute-start(bf16[4,128,128]{2,1,0:T(8,128)(2,1)} %param.19), channel_id=1, source_target_pairs={{0,12},{1,13},{2,14},{3,15},{4,0},{5,1},{6,2},{7,3},{8,4},{9,5},{1... | collective-permute-start | bytes 393224 | tf_op jit(solution)/shard_map/ppermute | solution.py:25
  5.1 11.4 %collective-permute-start.1 = (bf16[4,128,128]{2,1,0:T(8,128)(2,1)}, bf16[4,128,128]{2,1,0:T(8,128)(2,1)S(1)}, u32[]{:S(2)}, u32[]{:S(2)}) collective-permute-start(bf16[4,128,128]{2,1,0:T(8,128)(2,1)} %param.19), channel_id=1, source_target_pairs={{0,8},{1,9},{2,10},{3,11},{4,12},{5,13},{6,14},{7,15},{8,0},{9,1},... | collective-permute-start | bytes 393224 | tf_op jit(solution)/shard_map/ppermute | solution.py:25
  5.1 11.4 %collective-permute-start = (bf16[4,128,128]{2,1,0:T(8,128)(2,1)}, bf16[4,128,128]{2,1,0:T(8,128)(2,1)S(1)}, u32[]{:S(2)}, u32[]{:S(2)}) collective-permute-start(bf16[4,128,128]{2,1,0:T(8,128)(2,1)} %param.19), channel_id=1, source_target_pairs={{0,4},{1,5},{2,6},{3,7},{4,8},{5,9},{6,10},{7,11},{8,12},{9,13},{1... | collective-permute-start | bytes 393224 | tf_op jit(solution)/shard_map/ppermute | solution.py:25
  18.5 13.5 %collective-permute-start.3 = (bf16[4,4,128,128]{3,2,1,0:T(8,128)(2,1)}, bf16[4,4,128,128]{3,2,1,0:T(8,128)(2,1)}, u32[]{:S(2)}, u32[]{:S(2)}) collective-permute-start(bf16[4,4,128,128]{3,2,1,0:T(8,128)(2,1)} %get-tuple-element.33), channel_id=1, source_target_pairs={{0,2},{1,3},{2,0},{3,1},{4,6},{5,7},{6,4},{7,5},{8,10},{9,11},{10,... | collective-permute-start | bytes 1572872 | tf_op jit(solution)/shard_map/ppermute | solution.py:36
  33.3 2.7 %collective-permute-start.4 = (bf16[2,4,4,128,128]{4,3,2,1,0:T(8,128)(2,1)S(1)}, bf16[2,4,4,128,128]{4,3,2,1,0:T(8,128)(2,1)S(1)}, u32[]{:S(2)}, u32[]{:S(2)}) collective-permute-start(bf16[2,4,4,128,128]{4,3,2,1,0:T(8,128)(2,1)S(1)} %get-tuple-element.31), channel_id=1, source_target_pairs={{0,1},{1,0},{2,3},{3,2},{4,5},{5,4},{6,7},{7,6},{8,9},{9,8},{10,11... | collective-permute-start | bytes 3145736 | tf_op jit(solution)/shard_map/ppermute | solution.py:36
  36.0 0.9 %copy-start.2 = (f32[3,128,128]{2,1,0:T(8,128)S(1)}, f32[3,128,128]{2,1,0:T(8,128)}, u32[]{:S(2)}) copy-start(f32[3,128,128]{2,1,0:T(8,128)} %param.20) | copy-start | bytes 589828
  36.9 0.8 %copy-start.1 = (f32[1,128,128]{2,1,0:T(8,128)S(1)}, f32[1,128,128]{2,1,0:T(8,128)}, u32[]{:S(2)}) copy-start(f32[1,128,128]{2,1,0:T(8,128)} %param.21) | copy-start | bytes 196612
  38.1 4.8 %collective-permute-start.7 = (bf16[128,128]{0,1:T(8,128)(2,1)S(1)}, bf16[128,128]{0,1:T(8,128)(2,1)S(1)}, u32[]{:S(2)}, u32[]{:S(2)}) collective-permute-start(bf16[128,128]{0,1:T(8,128)(2,1)S(1)} %get-tuple-element.40), channel_id=1, source_target_pairs={{0,12},{1,13},{2,14},{3,15},{4,0},{5,1},{6,2},{7,3},{8,4},{9,5},{1... | collective-permute-start | bytes 98312 | tf_op jit(solution)/shard_map/ppermute | solution.py:25
  38.7 5.1 %collective-permute-start.6 = (bf16[128,128]{0,1:T(8,128)(2,1)S(1)}, bf16[128,128]{0,1:T(8,128)(2,1)S(1)}, u32[]{:S(2)}, u32[]{:S(2)}) collective-permute-start(bf16[128,128]{0,1:T(8,128)(2,1)S(1)} %get-tuple-element.40), channel_id=1, source_target_pairs={{0,8},{1,9},{2,10},{3,11},{4,12},{5,13},{6,14},{7,15},{8,0},{9,1},... | collective-permute-start | bytes 98312 | tf_op jit(solution)/shard_map/ppermute | solution.py:25
  40.7 5.7 %collective-permute-start.5 = (bf16[128,128]{0,1:T(8,128)(2,1)S(1)}, bf16[128,128]{0,1:T(8,128)(2,1)S(1)}, u32[]{:S(2)}, u32[]{:S(2)}) collective-permute-start(bf16[128,128]{0,1:T(8,128)(2,1)S(1)} %get-tuple-element.40), channel_id=1, source_target_pairs={{0,4},{1,5},{2,6},{3,7},{4,8},{5,9},{6,10},{7,11},{8,12},{9,13},{1... | collective-permute-start | bytes 98312 | tf_op jit(solution)/shard_map/ppermute | solution.py:25
  46.5 5.8 %collective-permute-start.10 = (bf16[4,128,128]{1,2,0:T(8,128)(2,1)S(1)}, bf16[4,128,128]{1,2,0:T(8,128)(2,1)S(1)}, u32[]{:S(2)}, u32[]{:S(2)}) collective-permute-start(bf16[4,128,128]{1,2,0:T(8,128)(2,1)S(1)} %get-tuple-element.37), channel_id=1, source_target_pairs={{0,3},{1,2},{2,1},{3,0},{4,7},{5,6},{6,5},{7,4},{8,11},{9,10},{10,... | collective-permute-start | bytes 393224 | tf_op jit(solution)/shard_map/ppermute | solution.py:43
  46.5 8.6 %collective-permute-start.9 = (bf16[4,128,128]{1,2,0:T(8,128)(2,1)S(1)}, bf16[4,128,128]{1,2,0:T(8,128)(2,1)S(1)}, u32[]{:S(2)}, u32[]{:S(2)}) collective-permute-start(bf16[4,128,128]{1,2,0:T(8,128)(2,1)S(1)} %get-tuple-element.37), channel_id=1, source_target_pairs={{0,2},{1,3},{2,0},{3,1},{4,6},{5,7},{6,4},{7,5},{8,10},{9,11},{10,... | collective-permute-start | bytes 393224 | tf_op jit(solution)/shard_map/ppermute | solution.py:43
  48.1 7.0 %collective-permute-start.8 = (bf16[4,128,128]{1,2,0:T(8,128)(2,1)S(1)}, bf16[4,128,128]{1,2,0:T(8,128)(2,1)S(1)}, u32[]{:S(2)}, u32[]{:S(2)}) collective-permute-start(bf16[4,128,128]{1,2,0:T(8,128)(2,1)S(1)} %get-tuple-element.37), channel_id=1, source_target_pairs={{0,1},{1,0},{2,3},{3,2},{4,5},{5,4},{6,7},{7,6},{8,9},{9,8},{10,11... | collective-permute-start | bytes 393224 | tf_op jit(solution)/shard_map/ppermute | solution.py:43
  56.5 4.0 %collective-permute-start.13 = (bf16[128,128]{0,1:T(8,128)(2,1)S(1)}, bf16[128,128]{0,1:T(8,128)(2,1)S(1)}, u32[]{:S(2)}, u32[]{:S(2)}) collective-permute-start(bf16[128,128]{0,1:T(8,128)(2,1)S(1)} %get-tuple-element.42), channel_id=1, source_target_pairs={{0,12},{1,13},{2,14},{3,15},{4,0},{5,1},{6,2},{7,3},{8,4},{9,5},{1... | collective-permute-start | bytes 98312 | tf_op jit(solution)/shard_map/ppermute | solution.py:25
  57.1 4.8 %collective-permute-start.12 = (bf16[128,128]{0,1:T(8,128)(2,1)S(1)}, bf16[128,128]{0,1:T(8,128)(2,1)S(1)}, u32[]{:S(2)}, u32[]{:S(2)}) collective-permute-start(bf16[128,128]{0,1:T(8,128)(2,1)S(1)} %get-tuple-element.42), channel_id=1, source_target_pairs={{0,8},{1,9},{2,10},{3,11},{4,12},{5,13},{6,14},{7,15},{8,0},{9,1},... | collective-permute-start | bytes 98312 | tf_op jit(solution)/shard_map/ppermute | solution.py:25
  58.1 5.7 %collective-permute-start.11 = (bf16[128,128]{0,1:T(8,128)(2,1)S(1)}, bf16[128,128]{0,1:T(8,128)(2,1)S(1)}, u32[]{:S(2)}, u32[]{:S(2)}) collective-permute-start(bf16[128,128]{0,1:T(8,128)(2,1)S(1)} %get-tuple-element.42), channel_id=1, source_target_pairs={{0,4},{1,5},{2,6},{3,7},{4,8},{5,9},{6,10},{7,11},{8,12},{9,13},{1... | collective-permute-start | bytes 98312 | tf_op jit(solution)/shard_map/ppermute | solution.py:25
  63.9 5.3 %collective-permute-start.16 = (bf16[4,128,128]{1,2,0:T(8,128)(2,1)S(1)}, bf16[4,128,128]{1,2,0:T(8,128)(2,1)S(1)}, u32[]{:S(2)}, u32[]{:S(2)}) collective-permute-start(bf16[4,128,128]{1,2,0:T(8,128)(2,1)S(1)} %get-tuple-element.35), channel_id=1, source_target_pairs={{0,3},{1,2},{2,1},{3,0},{4,7},{5,6},{6,5},{7,4},{8,11},{9,10},{10,... | collective-permute-start | bytes 393224 | tf_op jit(solution)/shard_map/ppermute | solution.py:43
  63.9 6.4 %collective-permute-start.15 = (bf16[4,128,128]{1,2,0:T(8,128)(2,1)S(1)}, bf16[4,128,128]{1,2,0:T(8,128)(2,1)S(1)}, u32[]{:S(2)}, u32[]{:S(2)}) collective-permute-start(bf16[4,128,128]{1,2,0:T(8,128)(2,1)S(1)} %get-tuple-element.35), channel_id=1, source_target_pairs={{0,2},{1,3},{2,0},{3,1},{4,6},{5,7},{6,4},{7,5},{8,10},{9,11},{10,... | collective-permute-start | bytes 393224 | tf_op jit(solution)/shard_map/ppermute | solution.py:43
  64.0 6.3 %collective-permute-start.14 = (bf16[4,128,128]{1,2,0:T(8,128)(2,1)S(1)}, bf16[4,128,128]{1,2,0:T(8,128)(2,1)S(1)}, u32[]{:S(2)}, u32[]{:S(2)}) collective-permute-start(bf16[4,128,128]{1,2,0:T(8,128)(2,1)S(1)} %get-tuple-element.35), channel_id=1, source_target_pairs={{0,1},{1,0},{2,3},{3,2},{4,5},{5,4},{6,7},{7,6},{8,9},{9,8},{10,11... | collective-permute-start | bytes 393224 | tf_op jit(solution)/shard_map/ppermute | solution.py:43

commit v3 on v2

--- a/solution.py
+++ b/solution.py
@@ -87,7 +87,12 @@
     step_count = excitation.shape[0]
     column_of_block = jnp.argsort(block_owner)
 
-    later, later_blocks = gather_blocks(later_current, wide, True)
+    split = (lag_count + 1) // 2
+    bounds = [(0, split), (split, lag_count)] if lag_count > 1 else [(0, lag_count)]
+    later = []
+    for low, high in bounds:
+        gathered, later_blocks = gather_blocks(later_current[low:high], wide, True)
+        later.append((low, high, gathered))
     by_lag = tiles_by_lag(
         retarded_tiles, tile_lags, column_of_block, later_blocks, range(1, lag_count + 1)
     )
@@ -104,10 +109,17 @@
     recent = None
     for moment in range(step_count - 1, -1, -1):
         first = max(1, step_count - moment)
-        retarded = rowwise(
-            by_lag[:, first - 1 :],
-            later[:, moment + first - step_count : moment + lag_count + 1 - step_count],
-        )
+        retarded = None
+        for low, high, gathered in later:
+            start = max(low, moment + first - step_count)
+            stop = min(high, moment + lag_count + 1 - step_count)
+            if start >= stop:
+                continue
+            term = rowwise(
+                by_lag[:, start + step_count - moment - 1 : stop + step_count - moment - 1],
+                gathered[:, start - low : stop - low],
+            )
+            retarded = term if retarded is None else retarded + term
         for delay in range(1, first):
             retarded = retarded + rowwise(recent[:, delay - 1], newer[moment + delay])
         current = advance(moment, retarded)

time: 72.3 us -> 75.5 us (1.044)
  waiting for transfers between devices: 35.3 us -> 22.5 us
  starting transfers between devices: 18.2 us -> 26.7 us
  local copies, waits for them, and re-layouts: 6.49 us -> 13.9 us
    ppermute x9 -> x12, waiting for transfers between devices: 13.8 us -> 4.7 us  [line_stage(): parts.append(lax.ppermute(x, 'wide', pairs))]
    ppermute x9 -> x12, starting transfers between devices: 12.7 us -> 20.3 us  [line_stage(): parts.append(lax.ppermute(x, 'wide', pairs))]
    unnamed x6 -> x26, local copies, waits for them, and re-layouts: 0.82 us -> 6.07 us
    ppermute x2 -> x4, waiting for transfers between devices: 10.9 us -> 6 us  [slab_stage(): other = lax.ppermute(stack, 'wide', [(d, d ^ bit) for d in range(wide)])]
    another operation x3 -> x6, other arithmetic: 3.51 us -> 1.3 us  [slab_stage(): stack = jnp.stack([stack, other])]
    another operation x0 -> x1, local copies, waits for them, and re-layouts: none -> 1.64 us  [line_stage(): return (jnp.stack(parts), True)]
    ppermute x6, waiting for transfers between devices: 10.6 us -> 11.8 us  [slab_stage(): parts.append(lax.ppermute(stack, 'wide', [(d, d ^ m) for d in range(wide)]))]
    gather x2, local copies, waits for them, and re-layouts: 1.12 us -> 2.3 us  [tiles_by_lag(): lags = jnp.take(tile_lags[0], columns, axis=0)]
  transfers between devices with their start and end apart: 17 -> 22, of which waited for: 12 -> 11; matrix products, arithmetic and copies ran while one was open for 14% -> 19% of each run, Pallas kernels for 0% -> 0%
where the time goes in v3:
time: 75.5 us; the launch traced here: 75.1 us
  starting transfers between devices  26.7 us (35%)
  waiting for transfers between devices  22.5 us (30%)
  local copies, waits for them, and re-layouts  13.9 us (18%)
  other arithmetic  7.1 us (9%)
  matrix products  4.61 us (6%)
    ppermute x12, starting transfers between devices, line_stage(): parts.append(lax.ppermute(x, 'wide', pairs))  20.3 us
    ppermute x6, waiting for transfers between devices, slab_stage(): parts.append(lax.ppermute(stack, 'wide', [(d, d ^ m) for d in range(wide)]))  11.8 us
    unnamed x26, local copies, waits for them, and re-layouts  6.07 us
    ppermute x4, waiting for transfers between devices, slab_stage(): other = lax.ppermute(stack, 'wide', [(d, d ^ bit) for d in range(wide)])  6 us
    ppermute x12, waiting for transfers between devices, line_stage(): parts.append(lax.ppermute(x, 'wide', pairs))  4.7 us
    ppermute x6, starting transfers between devices, slab_stage(): parts.append(lax.ppermute(stack, 'wide', [(d, d ^ m) for d in range(wide)]))  3.87 us
    dot_general x8, matrix products, rowwise(): return jnp.einsum(spec, tiles, currents, preferred_element_type=jnp.float32)  3.76 us
    ppermute x4, starting transfers between devices, slab_stage(): other = lax.ppermute(stack, 'wide', [(d, d ^ bit) for d in range(wide)])  2.5 us
  transfers between devices with their start and end apart: 22, of which 11 were waited for; matrix products, arithmetic and copies ran while one was open for 19% of the time, Pallas kernels for 0%

profile of v3, /device:TPU:0, one launch (start us, length us, event | category | flops | bytes accessed | tf_op | source)
XLA Modules:
  0.0 75.1 jit_solution(14288824097106837919)
XLA Ops:
  0.0 1.6 %slice_bitcast_fusion.7 = (bf16[1,2,128,128]{3,2,1,0:T(8,128)(2,1)S(1)}, bf16[1,2,128,128]{3,2,1,0:T(8,128)(2,1)S(1)}, bf16[2,128,128]{2,1,0:T(8,128)(2,1)}, bf16[2,128,128]{2,1,0:T(8,128)(2,1)}) fusion(bf16[4,128,128]{2,1,0:T(8,128)(2,1)} %param.19), kind=kLoop, calls=%fused_computation.106 | loop fusion | bytes 393216 | tf_op jit(solution)/shard_map/stack | solution.py:26
  1.6 3.0 %collective-permute-start.5 = (bf16[2,128,128]{2,1,0:T(8,128)(2,1)}, bf16[2,128,128]{2,1,0:T(8,128)(2,1)S(1)}, u32[]{:S(2)}, u32[]{:S(2)}) collective-permute-start(bf16[2,128,128]{2,1,0:T(8,128)(2,1)} %get-tuple-element.47), channel_id=1, source_target_pairs={{0,4},{1,5},{2,6},{3,7},{4,8},{5,9},{6,10},{7,11},{8,12},{9,13},{1... | collective-permute-start | bytes 196616 | tf_op jit(solution)/shard_map/ppermute | solution.py:25
  4.7 2.6 %collective-permute-start.6 = (bf16[2,128,128]{2,1,0:T(8,128)(2,1)}, bf16[2,128,128]{2,1,0:T(8,128)(2,1)S(1)}, u32[]{:S(2)}, u32[]{:S(2)}) collective-permute-start(bf16[2,128,128]{2,1,0:T(8,128)(2,1)} %get-tuple-element.47), channel_id=1, source_target_pairs={{0,8},{1,9},{2,10},{3,11},{4,12},{5,13},{6,14},{7,15},{8,0},{9,1},... | collective-permute-start | bytes 196616 | tf_op jit(solution)/shard_map/ppermute | solution.py:25
  7.3 1.3 %collective-permute-start.7 = (bf16[2,128,128]{2,1,0:T(8,128)(2,1)}, bf16[2,128,128]{2,1,0:T(8,128)(2,1)S(1)}, u32[]{:S(2)}, u32[]{:S(2)}) collective-permute-start(bf16[2,128,128]{2,1,0:T(8,128)(2,1)} %get-tuple-element.47), channel_id=1, source_target_pairs={{0,12},{1,13},{2,14},{3,15},{4,0},{5,1},{6,2},{7,3},{8,4},{9,5},{1... | collective-permute-start | bytes 196616 | tf_op jit(solution)/shard_map/ppermute | solution.py:25
  8.6 0.7 collective-permute-start
  9.6 0.6 copy-done.10
  10.5 0.6 copy-done.12
  11.1 1.3 %sort.17 = (s32[16]{0:T(128)}, s32[16]{0:T(128)S(1)}) sort(s32[16]{0:T(128)S(1)} %copy-done.12, s32[16]{0:T(128)S(1)} %iota.5), dimensions={0}, to_apply=%region_0.0 | sort | flops 64 | bytes 256 | tf_op jit(solution)/shard_map/jit(argsort)/sort | solution.py:88
  12.4 0.7 gather_fusion
  13.1 0.6 compare_and_fusion.1
  13.7 0.7 copy-done.9
  14.5 0.7 gather_fusion.2
  15.2 1.1 %gather_fusion.1 = s32[16,2]{1,0:T(8,128)} fusion(s32[16,2]{1,0:T(8,128)S(1)} %copy.15, s32[1024]{0:T(1024)S(1)} %pad_clamp_fusion.2), kind=kCustom, calls=%fused_computation.1.clone | custom fusion | bytes 320 | tf_op jit(solution)/shard_map/jit(_take)/gather | solution.py:65
  16.4 0.7 copy-done.8
  17.2 0.5 copy-done.7
  18.1 0.7 gather_fusion.3
  18.8 1.4 %select_select_fusion = (bf16[16,1,128,128]{3,2,1,0:T(8,128)(2,1)}, bf16[16,1,128,128]{3,2,1,0:T(8,128)(2,1)}, bf16[16,1,128,128]{3,2,1,0:T(8,128)(2,1)}, bf16[16,1,128,128]{3,2,1,0:T(8,128)(2,1)S(1)}) fusion(pred[16]{0:T(512)(128)(4,1)S(1)} %get-tuple-element.19, pred[16]{0:T(512)(128)(4,1)S(1)} %get-tuple-element.14, ...), kind=kLoop, calls=%fused_computation.48 | loop fusion | flops 2097152 | bytes 3145856 | tf_op jit(solution)/shard_map/jit(_where)/select_n | solution.py:69
  20.3 0.7 gather_fusion.5
  21.0 2.9 %collective-permute-start.2 = (bf16[2,128,128]{2,1,0:T(8,128)(2,1)}, bf16[2,128,128]{2,1,0:T(8,128)(2,1)}, u32[]{:S(2)}, u32[]{:S(2)}) collective-permute-start(bf16[2,128,128]{2,1,0:T(8,128)(2,1)} %get-tuple-element.48), channel_id=1, source_target_pairs={{0,12},{1,13},{2,14},{3,15},{4,0},{5,1},{6,2},{7,3},{8,4},{9,5},{1... | collective-permute-start | bytes 196616 | tf_op jit(solution)/shard_map/ppermute | solution.py:25
  24.0 1.6 %collective-permute-start.8 = (bf16[4,2,128,128]{3,2,1,0:T(8,128)(2,1)S(1)}, bf16[4,2,128,128]{3,2,1,0:T(8,128)(2,1)S(1)}, u32[]{:S(2)}, u32[]{:S(2)}) collective-permute-start(bf16[4,2,128,128]{3,2,1,0:T(8,128)(2,1)S(1)} %get-tuple-element.40), channel_id=1, source_target_pairs={{0,2},{1,3},{2,0},{3,1},{4,6},{5,7},{6,4},{7,5},{8,10},{9,11},{10,... | collective-permute-start | bytes 786440 | tf_op jit(solution)/shard_map/ppermute | solution.py:36
  25.5 1.1 %broadcast_select_fusion = bf16[16,2,128,128]{3,2,1,0:T(8,128)(2,1)} fusion(bf16[16,2,128,128]{3,2,1,0:T(8,128)(2,1)S(1)} %gather_fusion.5, pred[16]{0:T(512)(128)(4,1)S(1)} %get-tuple-element.22), kind=kLoop, calls=%fused_computation.31 | loop fusion | flops 524288 | bytes 2097168 | tf_op jit(solution)/shard_map/jit(_take)/select_n | solution.py:64
  26.7 1.1 %gather_fusion.4 = s32[16,2]{1,0:T(8,128)} fusion(s32[16,2]{1,0:T(8,128)S(1)} %copy.15, s32[1024]{0:T(1024)S(1)} %pad_clamp_fusion), kind=kCustom, calls=%fused_computation.4.clone | custom fusion | bytes 320 | tf_op jit(solution)/shard_map/jit(_take)/gather | solution.py:65
  27.8 0.9 %fusion.35 = (bf16[1,4,2,128,128]{4,3,2,1,0:T(8,128)(2,1)S(1)}, bf16[4,2,128,128]{3,2,1,0:T(8,128)(2,1)S(1)}) fusion(bf16[1,2,128,128]{3,2,1,0:T(8,128)(2,1)} %bitcast.6, bf16[1,2,128,128]{3,2,1,0:T(8,128)(2,1)} %bitcast.5, bf16[1,2,128,128]{3,2,1,0:T(8,128)(2,1)S(1)} %bitcast.171, bf16[1,2,128,128]{3,2,1,0:T(8,128)(2,1)S(1)} %get-tuple-element.45), kind=kLoop, calls=%fused_computation.112 | loop fusion | flops 393216 | bytes 786432 | tf_op jit(solution)/shard_map/stack | solution.py:37
  28.8 0.8 %collective-permute-start.3 = (bf16[4,2,128,128]{3,2,1,0:T(8,128)(2,1)S(1)}, bf16[4,2,128,128]{3,2,1,0:T(8,128)(2,1)S(1)}, u32[]{:S(2)}, u32[]{:S(2)}) collective-permute-start(bf16[4,2,128,128]{3,2,1,0:T(8,128)(2,1)S(1)} %get-tuple-element.38), channel_id=1, source_target_pairs={{0,2},{1,3},{2,0},{3,1},{4,6},{5,7},{6,4},{7,5},{8,10},{9,11},{10,... | collective-permute-start | bytes 786440 | tf_op jit(solution)/shard_map/ppermute | solution.py:36
  29.5 2.3 %collective-permute-done.8 = bf16[4,2,128,128]{3,2,1,0:T(8,128)(2,1)S(1)} collective-permute-done((bf16[4,2,128,128]{3,2,1,0:T(8,128)(2,1)S(1)}, bf16[4,2,128,128]{3,2,1,0:T(8,128)(2,1)S(1)}, u32[]{:S(2)}, u32[]{:S(2)}) %collective-permute-start.8) | collective-permute-done | bytes 262176 | tf_op jit(solution)/shard_map/ppermute | solution.py:36
  32.0 0.5 copy-done.6
  32.6 3.7 %collective-permute-done.3 = bf16[4,2,128,128]{3,2,1,0:T(8,128)(2,1)S(1)} collective-permute-done((bf16[4,2,128,128]{3,2,1,0:T(8,128)(2,1)S(1)}, bf16[4,2,128,128]{3,2,1,0:T(8,128)(2,1)S(1)}, u32[]{:S(2)}, u32[]{:S(2)}) %collective-permute-start.3) | collective-permute-done | bytes 262176 | tf_op jit(solution)/shard_map/ppermute | solution.py:36
  36.5 0.9 %copy-done.1 = bf16[16,1,128,128]{3,2,1,0:T(8,128)(2,1)S(1)} copy-done((bf16[16,1,128,128]{3,2,1,0:T(8,128)(2,1)S(1)}, bf16[16,1,128,128]{3,2,1,0:T(8,128)(2,1)}, u32[]{:S(2)}) %copy-start.1) | copy-done | bytes 524312
  38.2 0.5 convolution_bitcast_fusion.4
  38.8 0.8 %copy-done.11 = f32[3,128,128]{2,1,0:T(8,128)S(1)} copy-done((f32[3,128,128]{2,1,0:T(8,128)S(1)}, f32[3,128,128]{2,1,0:T(8,128)}, u32[]{:S(2)}) %copy-start.11) | copy-done | bytes 196632
  40.8 0.6 collective-permute-start.10
  41.4 1.3 %collective-permute-start.11 = (bf16[128,128]{0,1:T(8,128)(2,1)S(1)}, bf16[128,128]{0,1:T(8,128)(2,1)S(1)}, u32[]{:S(2)}, u32[]{:S(2)}) collective-permute-start(bf16[128,128]{0,1:T(8,128)(2,1)S(1)} %get-tuple-element.51), channel_id=1, source_target_pairs={{0,8},{1,9},{2,10},{3,11},{4,12},{5,13},{6,14},{7,15},{8,0},{9,1},... | collective-permute-start | bytes 98312 | tf_op jit(solution)/shard_map/ppermute | solution.py:25
  42.7 2.8 %collective-permute-start.12 = (bf16[128,128]{0,1:T(8,128)(2,1)S(1)}, bf16[128,128]{0,1:T(8,128)(2,1)S(1)}, u32[]{:S(2)}, u32[]{:S(2)}) collective-permute-start(bf16[128,128]{0,1:T(8,128)(2,1)S(1)} %get-tuple-element.51), channel_id=1, source_target_pairs={{0,12},{1,13},{2,14},{3,15},{4,0},{5,1},{6,2},{7,3},{8,4},{9,5},{1... | collective-permute-start | bytes 98312 | tf_op jit(solution)/shard_map/ppermute | solution.py:25
  45.8 0.8 %collective-permute-done.10 = bf16[128,128]{0,1:T(8,128)(2,1)S(1)} collective-permute-done((bf16[128,128]{0,1:T(8,128)(2,1)S(1)}, bf16[128,128]{0,1:T(8,128)(2,1)S(1)}, u32[]{:S(2)}, u32[]{:S(2)}) %collective-permute-start.10) | collective-permute-done | bytes 32800 | tf_op jit(solution)/shard_map/ppermute | solution.py:25
  47.2 1.6 %collective-permute-start.14 = (bf16[4,128,128]{1,2,0:T(8,128)(2,1)S(1)}, bf16[4,128,128]{1,2,0:T(8,128)(2,1)S(1)}, u32[]{:S(2)}, u32[]{:S(2)}) collective-permute-start(bf16[4,128,128]{1,2,0:T(8,128)(2,1)S(1)} %get-tuple-element.44), channel_id=1, source_target_pairs={{0,2},{1,3},{2,0},{3,1},{4,6},{5,7},{6,4},{7,5},{8,10},{9,11},{10,... | collective-permute-start | bytes 393224 | tf_op jit(solution)/shard_map/ppermute | solution.py:43
  49.6 4.0 %collective-permute-done.14 = bf16[4,128,128]{1,2,0:T(8,128)(2,1)S(1)} collective-permute-done((bf16[4,128,128]{1,2,0:T(8,128)(2,1)S(1)}, bf16[4,128,128]{1,2,0:T(8,128)(2,1)S(1)}, u32[]{:S(2)}, u32[]{:S(2)}) %collective-permute-start.14) | collective-permute-done | bytes 131104 | tf_op jit(solution)/shard_map/ppermute | solution.py:43
  53.6 1.9 %collective-permute-done.15 = bf16[4,128,128]{1,2,0:T(8,128)(2,1)S(1)} collective-permute-done((bf16[4,128,128]{1,2,0:T(8,128)(2,1)S(1)}, bf16[4,128,128]{1,2,0:T(8,128)(2,1)S(1)}, u32[]{:S(2)}, u32[]{:S(2)}) %collective-permute-start.15) | collective-permute-done | bytes 131104 | tf_op jit(solution)/shard_map/ppermute | solution.py:43
  55.6 0.5 fusion.4
  56.4 2.1 %collective-permute-start.16 = (bf16[128,128]{0,1:T(8,128)(2,1)S(1)}, bf16[128,128]{0,1:T(8,128)(2,1)S(1)}, u32[]{:S(2)}, u32[]{:S(2)}) collective-permute-start(bf16[128,128]{0,1:T(8,128)(2,1)S(1)} %get-tuple-element.53), channel_id=1, source_target_pairs={{0,4},{1,5},{2,6},{3,7},{4,8},{5,9},{6,10},{7,11},{8,12},{9,13},{1... | collective-permute-start | bytes 98312 | tf_op jit(solution)/shard_map/ppermute | solution.py:25
  58.4 2.6 %collective-permute-start.17 = (bf16[128,128]{0,1:T(8,128)(2,1)S(1)}, bf16[128,128]{0,1:T(8,128)(2,1)S(1)}, u32[]{:S(2)}, u32[]{:S(2)}) collective-permute-start(bf16[128,128]{0,1:T(8,128)(2,1)S(1)} %get-tuple-element.53), channel_id=1, source_target_pairs={{0,8},{1,9},{2,10},{3,11},{4,12},{5,13},{6,14},{7,15},{8,0},{9,1},... | collective-permute-start | bytes 98312 | tf_op jit(solution)/shard_map/ppermute | solution.py:25
  61.6 1.2 %collective-permute-done.16 = bf16[128,128]{0,1:T(8,128)(2,1)S(1)} collective-permute-done((bf16[128,128]{0,1:T(8,128)(2,1)S(1)}, bf16[128,128]{0,1:T(8,128)(2,1)S(1)}, u32[]{:S(2)}, u32[]{:S(2)}) %collective-permute-start.16) | collective-permute-done | bytes 32800 | tf_op jit(solution)/shard_map/ppermute | solution.py:25
  62.8 1.1 %collective-permute-done.17 = bf16[128,128]{0,1:T(8,128)(2,1)S(1)} collective-permute-done((bf16[128,128]{0,1:T(8,128)(2,1)S(1)}, bf16[128,128]{0,1:T(8,128)(2,1)S(1)}, u32[]{:S(2)}, u32[]{:S(2)}) %collective-permute-start.17) | collective-permute-done | bytes 32800 | tf_op jit(solution)/shard_map/ppermute | solution.py:25
  63.8 1.2 %collective-permute-done.18 = bf16[128,128]{0,1:T(8,128)(2,1)S(1)} collective-permute-done((bf16[128,128]{0,1:T(8,128)(2,1)S(1)}, bf16[128,128]{0,1:T(8,128)(2,1)S(1)}, u32[]{:S(2)}, u32[]{:S(2)}) %collective-permute-start.18) | collective-permute-done | bytes 32800 | tf_op jit(solution)/shard_map/ppermute | solution.py:25
  65.1 1.6 %collective-permute-start.20 = (bf16[4,128,128]{1,2,0:T(8,128)(2,1)S(1)}, bf16[4,128,128]{1,2,0:T(8,128)(2,1)S(1)}, u32[]{:S(2)}, u32[]{:S(2)}) collective-permute-start(bf16[4,128,128]{1,2,0:T(8,128)(2,1)S(1)} %get-tuple-element.42), channel_id=1, source_target_pairs={{0,2},{1,3},{2,0},{3,1},{4,6},{5,7},{6,4},{7,5},{8,10},{9,11},{10,... | collective-permute-start | bytes 393224 | tf_op jit(solution)/shard_map/ppermute | solution.py:43
  67.5 4.0 %collective-permute-done.20 = bf16[4,128,128]{1,2,0:T(8,128)(2,1)S(1)} collective-permute-done((bf16[4,128,128]{1,2,0:T(8,128)(2,1)S(1)}, bf16[4,128,128]{1,2,0:T(8,128)(2,1)S(1)}, u32[]{:S(2)}, u32[]{:S(2)}) %collective-permute-start.20) | collective-permute-done | bytes 131104 | tf_op jit(solution)/shard_map/ppermute | solution.py:43
  71.5 1.9 %collective-permute-done.21 = bf16[4,128,128]{1,2,0:T(8,128)(2,1)S(1)} collective-permute-done((bf16[4,128,128]{1,2,0:T(8,128)(2,1)S(1)}, bf16[4,128,128]{1,2,0:T(8,128)(2,1)S(1)}, u32[]{:S(2)}, u32[]{:S(2)}) %collective-permute-start.21) | collective-permute-done | bytes 131104 | tf_op jit(solution)/shard_map/ppermute | solution.py:43
  73.4 0.5 fusion.7
  74.3 0.8 %copy.18 = f32[3,128,128]{2,1,0:T(8,128)} copy(f32[3,128,128]{1,2,0:T(8,128)S(1)} %pad_maximum_fusion.11) | data formatting | bytes 393216 | tf_op jit(solution)/shard_map/stack | solution.py:137
  (76 shorter events, 7.5 us)
Async XLA Ops:
  0.0 14.5 %copy-start = (bf16[1,16,2,128,128]{4,3,2,1,0:T(8,128)(2,1)S(1)}, bf16[1,16,2,128,128]{4,3,2,1,0:T(8,128)(2,1)}, u32[]{:S(2)}) copy-start(bf16[1,16,2,128,128]{4,3,2,1,0:T(8,128)(2,1)} %param.16) | copy-start | bytes 3145732
  1.6 19.4 %collective-permute-start.5 = (bf16[2,128,128]{2,1,0:T(8,128)(2,1)}, bf16[2,128,128]{2,1,0:T(8,128)(2,1)S(1)}, u32[]{:S(2)}, u32[]{:S(2)}) collective-permute-start(bf16[2,128,128]{2,1,0:T(8,128)(2,1)} %get-tuple-element.47), channel_id=1, source_target_pairs={{0,4},{1,5},{2,6},{3,7},{4,8},{5,9},{6,10},{7,11},{8,12},{9,13},{1... | collective-permute-start | bytes 196616 | tf_op jit(solution)/shard_map/ppermute | solution.py:25
  4.7 19.2 %collective-permute-start.6 = (bf16[2,128,128]{2,1,0:T(8,128)(2,1)}, bf16[2,128,128]{2,1,0:T(8,128)(2,1)S(1)}, u32[]{:S(2)}, u32[]{:S(2)}) collective-permute-start(bf16[2,128,128]{2,1,0:T(8,128)(2,1)} %get-tuple-element.47), channel_id=1, source_target_pairs={{0,8},{1,9},{2,10},{3,11},{4,12},{5,13},{6,14},{7,15},{8,0},{9,1},... | collective-permute-start | bytes 196616 | tf_op jit(solution)/shard_map/ppermute | solution.py:25
  7.3 16.6 %collective-permute-start.7 = (bf16[2,128,128]{2,1,0:T(8,128)(2,1)}, bf16[2,128,128]{2,1,0:T(8,128)(2,1)S(1)}, u32[]{:S(2)}, u32[]{:S(2)}) collective-permute-start(bf16[2,128,128]{2,1,0:T(8,128)(2,1)} %get-tuple-element.47), channel_id=1, source_target_pairs={{0,12},{1,13},{2,14},{3,15},{4,0},{5,1},{6,2},{7,3},{8,4},{9,5},{1... | collective-permute-start | bytes 196616 | tf_op jit(solution)/shard_map/ppermute | solution.py:25
  8.6 19.2 %collective-permute-start = (bf16[2,128,128]{2,1,0:T(8,128)(2,1)}, bf16[2,128,128]{2,1,0:T(8,128)(2,1)S(1)}, u32[]{:S(2)}, u32[]{:S(2)}) collective-permute-start(bf16[2,128,128]{2,1,0:T(8,128)(2,1)} %get-tuple-element.48), channel_id=1, source_target_pairs={{0,4},{1,5},{2,6},{3,7},{4,8},{5,9},{6,10},{7,11},{8,12},{9,13},{1... | collective-permute-start | bytes 196616 | tf_op jit(solution)/shard_map/ppermute | solution.py:25
  9.3 18.5 %collective-permute-start.1 = (bf16[2,128,128]{2,1,0:T(8,128)(2,1)}, bf16[2,128,128]{2,1,0:T(8,128)(2,1)}, u32[]{:S(2)}, u32[]{:S(2)}) collective-permute-start(bf16[2,128,128]{2,1,0:T(8,128)(2,1)} %get-tuple-element.48), channel_id=1, source_target_pairs={{0,8},{1,9},{2,10},{3,11},{4,12},{5,13},{6,14},{7,15},{8,0},{9,1},... | collective-permute-start | bytes 196616 | tf_op jit(solution)/shard_map/ppermute | solution.py:25
  9.6 0.7 copy-start.10
  10.5 0.7 copy-start.12
  13.7 0.7 copy-start.9
  16.4 0.7 copy-start.8
  17.0 0.7 copy-start.7
  21.0 6.8 %collective-permute-start.2 = (bf16[2,128,128]{2,1,0:T(8,128)(2,1)}, bf16[2,128,128]{2,1,0:T(8,128)(2,1)}, u32[]{:S(2)}, u32[]{:S(2)}) collective-permute-start(bf16[2,128,128]{2,1,0:T(8,128)(2,1)} %get-tuple-element.48), channel_id=1, source_target_pairs={{0,12},{1,13},{2,14},{3,15},{4,0},{5,1},{6,2},{7,3},{8,4},{9,5},{1... | collective-permute-start | bytes 196616 | tf_op jit(solution)/shard_map/ppermute | solution.py:25
  24.0 7.9 %collective-permute-start.8 = (bf16[4,2,128,128]{3,2,1,0:T(8,128)(2,1)S(1)}, bf16[4,2,128,128]{3,2,1,0:T(8,128)(2,1)S(1)}, u32[]{:S(2)}, u32[]{:S(2)}) collective-permute-start(bf16[4,2,128,128]{3,2,1,0:T(8,128)(2,1)S(1)} %get-tuple-element.40), channel_id=1, source_target_pairs={{0,2},{1,3},{2,0},{3,1},{4,6},{5,7},{6,4},{7,5},{8,10},{9,11},{10,... | collective-permute-start | bytes 786440 | tf_op jit(solution)/shard_map/ppermute | solution.py:36
  28.8 7.5 %collective-permute-start.3 = (bf16[4,2,128,128]{3,2,1,0:T(8,128)(2,1)S(1)}, bf16[4,2,128,128]{3,2,1,0:T(8,128)(2,1)S(1)}, u32[]{:S(2)}, u32[]{:S(2)}) collective-permute-start(bf16[4,2,128,128]{3,2,1,0:T(8,128)(2,1)S(1)} %get-tuple-element.38), channel_id=1, source_target_pairs={{0,2},{1,3},{2,0},{3,1},{4,6},{5,7},{6,4},{7,5},{8,10},{9,11},{10,... | collective-permute-start | bytes 786440 | tf_op jit(solution)/shard_map/ppermute | solution.py:36
  31.8 0.7 copy-start.6
  31.9 6.2 %collective-permute-start.9 = (bf16[2,4,2,128,128]{4,3,2,1,0:T(8,128)(2,1)S(1)}, bf16[2,4,2,128,128]{4,3,2,1,0:T(8,128)(2,1)S(1)}, u32[]{:S(2)}, u32[]{:S(2)}) collective-permute-start(bf16[2,4,2,128,128]{4,3,2,1,0:T(8,128)(2,1)S(1)} %get-tuple-element.36), channel_id=1, source_target_pairs={{0,1},{1,0},{2,3},{3,2},{4,5},{5,4},{6,7},{7,6},{8,9},{9,8},{10,11... | collective-permute-start | bytes 1572872 | tf_op jit(solution)/shard_map/ppermute | solution.py:36
  36.3 1.0 %copy-start.1 = (bf16[16,1,128,128]{3,2,1,0:T(8,128)(2,1)S(1)}, bf16[16,1,128,128]{3,2,1,0:T(8,128)(2,1)}, u32[]{:S(2)}) copy-start(bf16[16,1,128,128]{3,2,1,0:T(8,128)(2,1)} %get-tuple-element.26) | copy-start | bytes 1572868
  36.3 1.2 %copy-start.2 = (bf16[16,1,128,128]{3,2,1,0:T(8,128)(2,1)S(1)}, bf16[16,1,128,128]{3,2,1,0:T(8,128)(2,1)}, u32[]{:S(2)}) copy-start(bf16[16,1,128,128]{3,2,1,0:T(8,128)(2,1)} %get-tuple-element.27) | copy-start | bytes 1572868
  36.3 1.4 %copy-start.3 = (bf16[16,1,128,128]{3,2,1,0:T(8,128)(2,1)S(1)}, bf16[16,1,128,128]{3,2,1,0:T(8,128)(2,1)}, u32[]{:S(2)}) copy-start(bf16[16,1,128,128]{3,2,1,0:T(8,128)(2,1)} %get-tuple-element.28) | copy-start | bytes 1572868
  36.4 2.3 %collective-permute-start.4 = (bf16[2,4,2,128,128]{4,3,2,1,0:T(8,128)(2,1)S(1)}, bf16[2,4,2,128,128]{4,3,2,1,0:T(8,128)(2,1)S(1)}, u32[]{:S(2)}, u32[]{:S(2)}) collective-permute-start(bf16[2,4,2,128,128]{4,3,2,1,0:T(8,128)(2,1)S(1)} %get-tuple-element.34), channel_id=1, source_target_pairs={{0,1},{1,0},{2,3},{3,2},{4,5},{5,4},{6,7},{7,6},{8,9},{9,8},{10,11... | collective-permute-start | bytes 1572872 | tf_op jit(solution)/shard_map/ppermute | solution.py:36
  38.7 0.9 %copy-start.11 = (f32[3,128,128]{2,1,0:T(8,128)S(1)}, f32[3,128,128]{2,1,0:T(8,128)}, u32[]{:S(2)}) copy-start(f32[3,128,128]{2,1,0:T(8,128)} %param.20) | copy-start | bytes 589828
  39.6 0.8 %copy-start.5 = (f32[1,128,128]{2,1,0:T(8,128)S(1)}, f32[1,128,128]{2,1,0:T(8,128)}, u32[]{:S(2)}) copy-start(f32[1,128,128]{2,1,0:T(8,128)} %param.21) | copy-start | bytes 196612
  40.8 5.9 %collective-permute-start.10 = (bf16[128,128]{0,1:T(8,128)(2,1)S(1)}, bf16[128,128]{0,1:T(8,128)(2,1)S(1)}, u32[]{:S(2)}, u32[]{:S(2)}) collective-permute-start(bf16[128,128]{0,1:T(8,128)(2,1)S(1)} %get-tuple-element.51), channel_id=1, source_target_pairs={{0,4},{1,5},{2,6},{3,7},{4,8},{5,9},{6,10},{7,11},{8,12},{9,13},{1... | collective-permute-start | bytes 98312 | tf_op jit(solution)/shard_map/ppermute | solution.py:25
  41.4 5.2 %collective-permute-start.11 = (bf16[128,128]{0,1:T(8,128)(2,1)S(1)}, bf16[128,128]{0,1:T(8,128)(2,1)S(1)}, u32[]{:S(2)}, u32[]{:S(2)}) collective-permute-start(bf16[128,128]{0,1:T(8,128)(2,1)S(1)} %get-tuple-element.51), channel_id=1, source_target_pairs={{0,8},{1,9},{2,10},{3,11},{4,12},{5,13},{6,14},{7,15},{8,0},{9,1},... | collective-permute-start | bytes 98312 | tf_op jit(solution)/shard_map/ppermute | solution.py:25
  42.7 4.4 %collective-permute-start.12 = (bf16[128,128]{0,1:T(8,128)(2,1)S(1)}, bf16[128,128]{0,1:T(8,128)(2,1)S(1)}, u32[]{:S(2)}, u32[]{:S(2)}) collective-permute-start(bf16[128,128]{0,1:T(8,128)(2,1)S(1)} %get-tuple-element.51), channel_id=1, source_target_pairs={{0,12},{1,13},{2,14},{3,15},{4,0},{5,1},{6,2},{7,3},{8,4},{9,5},{1... | collective-permute-start | bytes 98312 | tf_op jit(solution)/shard_map/ppermute | solution.py:25
  47.1 2.4 %collective-permute-start.13 = (bf16[4,128,128]{1,2,0:T(8,128)(2,1)S(1)}, bf16[4,128,128]{1,2,0:T(8,128)(2,1)S(1)}, u32[]{:S(2)}, u32[]{:S(2)}) collective-permute-start(bf16[4,128,128]{1,2,0:T(8,128)(2,1)S(1)} %get-tuple-element.44), channel_id=1, source_target_pairs={{0,1},{1,0},{2,3},{3,2},{4,5},{5,4},{6,7},{7,6},{8,9},{9,8},{10,11... | collective-permute-start | bytes 393224 | tf_op jit(solution)/shard_map/ppermute | solution.py:43
  47.2 6.4 %collective-permute-start.14 = (bf16[4,128,128]{1,2,0:T(8,128)(2,1)S(1)}, bf16[4,128,128]{1,2,0:T(8,128)(2,1)S(1)}, u32[]{:S(2)}, u32[]{:S(2)}) collective-permute-start(bf16[4,128,128]{1,2,0:T(8,128)(2,1)S(1)} %get-tuple-element.44), channel_id=1, source_target_pairs={{0,2},{1,3},{2,0},{3,1},{4,6},{5,7},{6,4},{7,5},{8,10},{9,11},{10,... | collective-permute-start | bytes 393224 | tf_op jit(solution)/shard_map/ppermute | solution.py:43
  48.8 6.7 %collective-permute-start.15 = (bf16[4,128,128]{1,2,0:T(8,128)(2,1)S(1)}, bf16[4,128,128]{1,2,0:T(8,128)(2,1)S(1)}, u32[]{:S(2)}, u32[]{:S(2)}) collective-permute-start(bf16[4,128,128]{1,2,0:T(8,128)(2,1)S(1)} %get-tuple-element.44), channel_id=1, source_target_pairs={{0,3},{1,2},{2,1},{3,0},{4,7},{5,6},{6,5},{7,4},{8,11},{9,10},{10,... | collective-permute-start | bytes 393224 | tf_op jit(solution)/shard_map/ppermute | solution.py:43
  49.6 6.0 %copy-start.4 = (bf16[16,2,128,128]{3,2,1,0:T(8,128)(2,1)S(1)}, bf16[16,2,128,128]{3,2,1,0:T(8,128)(2,1)}, u32[]{:S(2)}) copy-start(bf16[16,2,128,128]{3,2,1,0:T(8,128)(2,1)} %broadcast_select_fusion) | copy-start | bytes 3145732
  56.4 6.4 %collective-permute-start.16 = (bf16[128,128]{0,1:T(8,128)(2,1)S(1)}, bf16[128,128]{0,1:T(8,128)(2,1)S(1)}, u32[]{:S(2)}, u32[]{:S(2)}) collective-permute-start(bf16[128,128]{0,1:T(8,128)(2,1)S(1)} %get-tuple-element.53), channel_id=1, source_target_pairs={{0,4},{1,5},{2,6},{3,7},{4,8},{5,9},{6,10},{7,11},{8,12},{9,13},{1... | collective-permute-start | bytes 98312 | tf_op jit(solution)/shard_map/ppermute | solution.py:25
  58.4 5.4 %collective-permute-start.17 = (bf16[128,128]{0,1:T(8,128)(2,1)S(1)}, bf16[128,128]{0,1:T(8,128)(2,1)S(1)}, u32[]{:S(2)}, u32[]{:S(2)}) collective-permute-start(bf16[128,128]{0,1:T(8,128)(2,1)S(1)} %get-tuple-element.53), channel_id=1, source_target_pairs={{0,8},{1,9},{2,10},{3,11},{4,12},{5,13},{6,14},{7,15},{8,0},{9,1},... | collective-permute-start | bytes 98312 | tf_op jit(solution)/shard_map/ppermute | solution.py:25
  61.1 3.9 %collective-permute-start.18 = (bf16[128,128]{0,1:T(8,128)(2,1)S(1)}, bf16[128,128]{0,1:T(8,128)(2,1)S(1)}, u32[]{:S(2)}, u32[]{:S(2)}) collective-permute-start(bf16[128,128]{0,1:T(8,128)(2,1)S(1)} %get-tuple-element.53), channel_id=1, source_target_pairs={{0,12},{1,13},{2,14},{3,15},{4,0},{5,1},{6,2},{7,3},{8,4},{9,5},{1... | collective-permute-start | bytes 98312 | tf_op jit(solution)/shard_map/ppermute | solution.py:25
  65.0 2.4 %collective-permute-start.19 = (bf16[4,128,128]{1,2,0:T(8,128)(2,1)S(1)}, bf16[4,128,128]{1,2,0:T(8,128)(2,1)S(1)}, u32[]{:S(2)}, u32[]{:S(2)}) collective-permute-start(bf16[4,128,128]{1,2,0:T(8,128)(2,1)S(1)} %get-tuple-element.42), channel_id=1, source_target_pairs={{0,1},{1,0},{2,3},{3,2},{4,5},{5,4},{6,7},{7,6},{8,9},{9,8},{10,11... | collective-permute-start | bytes 393224 | tf_op jit(solution)/shard_map/ppermute | solution.py:43
  65.1 6.4 %collective-permute-start.20 = (bf16[4,128,128]{1,2,0:T(8,128)(2,1)S(1)}, bf16[4,128,128]{1,2,0:T(8,128)(2,1)S(1)}, u32[]{:S(2)}, u32[]{:S(2)}) collective-permute-start(bf16[4,128,128]{1,2,0:T(8,128)(2,1)S(1)} %get-tuple-element.42), channel_id=1, source_target_pairs={{0,2},{1,3},{2,0},{3,1},{4,6},{5,7},{6,4},{7,5},{8,10},{9,11},{10,... | collective-permute-start | bytes 393224 | tf_op jit(solution)/shard_map/ppermute | solution.py:43
  66.7 6.7 %collective-permute-start.21 = (bf16[4,128,128]{1,2,0:T(8,128)(2,1)S(1)}, bf16[4,128,128]{1,2,0:T(8,128)(2,1)S(1)}, u32[]{:S(2)}, u32[]{:S(2)}) collective-permute-start(bf16[4,128,128]{1,2,0:T(8,128)(2,1)S(1)} %get-tuple-element.42), channel_id=1, source_target_pairs={{0,3},{1,2},{2,1},{3,0},{4,7},{5,6},{6,5},{7,4},{8,11},{9,10},{10,... | collective-permute-start | bytes 393224 | tf_op jit(solution)/shard_map/ppermute | solution.py:43

commit v4 on v2

--- a/solution.py
+++ b/solution.py
@@ -29,15 +29,11 @@
 
 
 def slab_stage(stack, wide, inner, doubling):
-    if doubling:
-        masks = np.zeros((1,), np.int32)
-        bit = inner // 2
-        while bit >= 1:
-            other = lax.ppermute(stack, "wide", [(d, d ^ bit) for d in range(wide)])
-            stack = jnp.stack([stack, other])
-            masks = np.concatenate([masks, masks ^ bit])
-            bit //= 2
-        return stack, masks
+    if doubling and inner == 4:
+        across = lax.ppermute(stack, "wide", [(d, d ^ 2) for d in range(wide)])
+        beside = lax.ppermute(stack, "wide", [(d, d ^ 1) for d in range(wide)])
+        diagonal = lax.ppermute(across, "wide", [(d, d ^ 1) for d in range(wide)])
+        return jnp.stack([stack, beside, across, diagonal]), np.array([0, 1, 2, 3], np.int32)
     parts = [stack]
     for m in range(1, inner):
         parts.append(lax.ppermute(stack, "wide", [(d, d ^ m) for d in range(wide)]))

time: 72.3 us -> 69.7 us (0.964)
  local copies, waits for them, and re-layouts: 6.49 us -> 2.98 us
  waiting for transfers between devices: 35.3 us -> 38.4 us
  other arithmetic: 7.83 us -> 5.5 us
    ppermute x9, waiting for transfers between devices: 13.8 us -> 16.2 us  [line_stage(): parts.append(lax.ppermute(x, 'wide', pairs))]
    another operation x3 -> x2, other arithmetic: 3.51 us -> 2.33 us  [slab_stage(): jnp.stack([stack, beside, across, diagonal])]
    unnamed x6 -> x8, local copies, waits for them, and re-layouts: 0.82 us -> 0.03 us
    gather x2 -> x1, local copies, waits for them, and re-layouts: 1.5 us -> 0.75 us  [tiles_by_lag(): tiles = jnp.take(retarded_tiles[0], columns, axis=0)]
    ppermute x2 -> x3, waiting for transfers between devices: 10.9 us -> 11.6 us  [the longest x1 9.91 us: slab_stage(): across = lax.ppermute(stack, 'wide', [(d, d ^ 2) for d in range(wide)])]
    ppermute x2 -> x3, starting transfers between devices: 1.59 us -> 1.65 us  [the longest x1 1.58 us: slab_stage(): across = lax.ppermute(stack, 'wide', [(d, d ^ 2) for d in range(wide)])]
  transfers between devices with their start and end apart: 17 -> 18, of which waited for: 12 -> 13; matrix products, arithmetic and copies ran while one was open for 14% -> 9% of each run, Pallas kernels for 0% -> 0%
where the time goes in v4:
time: 69.7 us; the launch traced here: 69.3 us
  waiting for transfers between devices  38.4 us (55%)
  starting transfers between devices  18.2 us (26%)
  other arithmetic  5.5 us (8%)
  matrix products  3.98 us (6%)
  local copies, waits for them, and re-layouts  2.98 us (4%)
    ppermute x9, waiting for transfers between devices, line_stage(): parts.append(lax.ppermute(x, 'wide', pairs))  16.2 us
    ppermute x9, starting transfers between devices, line_stage(): parts.append(lax.ppermute(x, 'wide', pairs))  12.7 us
    ppermute x6, waiting for transfers between devices, slab_stage(): parts.append(lax.ppermute(stack, 'wide', [(d, d ^ m) for d in range(wide)]))  10.6 us
    ppermute x1, waiting for transfers between devices, slab_stage(): across = lax.ppermute(stack, 'wide', [(d, d ^ 2) for d in range(wide)])  9.91 us
    ppermute x6, starting transfers between devices, slab_stage(): parts.append(lax.ppermute(stack, 'wide', [(d, d ^ m) for d in range(wide)]))  3.83 us
    dot_general x6, matrix products, rowwise(): return jnp.einsum(spec, tiles, currents, preferred_element_type=jnp.float32)  3.13 us
    another operation x2, other arithmetic, slab_stage(): jnp.stack([stack, beside, across, diagonal])  2.33 us
    sort x1, other arithmetic, per_device(): column_of_block = jnp.argsort(block_owner)  1.9 us
  transfers between devices with their start and end apart: 18, of which 13 were waited for; matrix products, arithmetic and copies ran while one was open for 9% of the time, Pallas kernels for 0%

profile of v4, /device:TPU:0, one launch (start us, length us, event | category | flops | bytes accessed | tf_op | source)
XLA Modules:
  0.0 69.3 jit_solution(17355746796307697457)
XLA Ops:
  0.0 5.0 %collective-permute-start.2 = (bf16[4,128,128]{2,1,0:T(8,128)(2,1)}, bf16[4,128,128]{2,1,0:T(8,128)(2,1)S(1)}, u32[]{:S(2)}, u32[]{:S(2)}) collective-permute-start(bf16[4,128,128]{2,1,0:T(8,128)(2,1)} %param.19), channel_id=1, source_target_pairs={{0,12},{1,13},{2,14},{3,15},{4,0},{5,1},{6,2},{7,3},{8,4},{9,5},{1... | collective-permute-start | bytes 393224 | tf_op jit(solution)/shard_map/ppermute | solution.py:25
  5.1 1.0 %collective-permute-start = (bf16[4,128,128]{2,1,0:T(8,128)(2,1)}, bf16[4,128,128]{2,1,0:T(8,128)(2,1)S(1)}, u32[]{:S(2)}, u32[]{:S(2)}) collective-permute-start(bf16[4,128,128]{2,1,0:T(8,128)(2,1)} %param.19), channel_id=1, source_target_pairs={{0,4},{1,5},{2,6},{3,7},{4,8},{5,9},{6,10},{7,11},{8,12},{9,13},{1... | collective-permute-start | bytes 393224 | tf_op jit(solution)/shard_map/ppermute | solution.py:25
  6.1 0.1 broadcast_add_fusion
  6.2 0.1 add.73
  6.2 1.9 %sort.17 = (s32[16]{0:T(128)}, s32[16]{0:T(128)S(1)}) sort(s32[16]{0:T(128)} %param.18, s32[16]{0:T(128)S(1)} %iota.5), dimensions={0}, to_apply=%region_0.0 | sort | flops 64 | bytes 256 | tf_op jit(solution)/shard_map/jit(argsort)/sort | solution.py:84
  8.2 0.7 gather_fusion
  8.8 0.5 collective-permute-done.2
  9.3 7.2 %collective-permute-done.1 = bf16[4,128,128]{2,1,0:T(8,128)(2,1)S(1)} collective-permute-done((bf16[4,128,128]{2,1,0:T(8,128)(2,1)}, bf16[4,128,128]{2,1,0:T(8,128)(2,1)S(1)}, u32[]{:S(2)}, u32[]{:S(2)}) %collective-permute-start.1) | collective-permute-done | bytes 131104 | tf_op jit(solution)/shard_map/ppermute | solution.py:25
  16.5 1.0 %fusion.66 = (bf16[1,4,4,128,128]{4,3,2,1,0:T(8,128)(2,1)S(1)}, bf16[4,4,128,128]{3,2,1,0:T(8,128)(2,1)S(1)}) fusion(bf16[1,4,128,128]{3,2,1,0:T(8,128)(2,1)S(1)} %bitcast.145, bf16[1,4,128,128]{3,2,1,0:T(8,128)(2,1)S(1)} %bitcast.146, bf16[1,4,128,128]{3,2,1,0:T(8,128)(2,1)S(1)} %bitcast.147, bf16[1,4,128,128]{3,2,1,0:T(8,128)(2,1)} %bitcast.144), kind=kLoop, calls=%fused_computation.97 | loop fusion | flops 786432 | bytes 1572864 | tf_op jit(solution)/shard_map/stack | solution.py:36
  17.5 1.6 %collective-permute-start.4 = (bf16[4,4,128,128]{3,2,1,0:T(8,128)(2,1)S(1)}, bf16[4,4,128,128]{3,2,1,0:T(8,128)(2,1)}, u32[]{:S(2)}, u32[]{:S(2)}) collective-permute-start(bf16[4,4,128,128]{3,2,1,0:T(8,128)(2,1)S(1)} %get-tuple-element.25), channel_id=1, source_target_pairs={{0,2},{1,3},{2,0},{3,1},{4,6},{5,7},{6,4},{7,5},{8,10},{9,11},{10,... | collective-permute-start | bytes 1572872 | tf_op jit(solution)/shard_map/ppermute | solution.py:33
  19.1 0.1 copy.18
  19.2 0.6 gather_fusion.1
  19.7 0.7 %gather_fusion.2 = bf16[16,2,128,128]{3,2,1,0:T(8,128)(2,1)S(1)} fusion(bf16[16,2,128,128]{3,2,1,0:T(8,128)(2,1)S(1)} %bitcast.133, s32[1024]{0:T(1024)S(1)} %pad_clamp_fusion), kind=kCustom, calls=%fused_computation.2.clone | custom fusion | bytes 2097216 | tf_op jit(solution)/shard_map/jit(_take)/gather | solution.py:60
  20.6 0.3 compare_reduce_fusion.3
  20.9 9.9 %collective-permute-done.4 = bf16[4,4,128,128]{3,2,1,0:T(8,128)(2,1)} collective-permute-done((bf16[4,4,128,128]{3,2,1,0:T(8,128)(2,1)S(1)}, bf16[4,4,128,128]{3,2,1,0:T(8,128)(2,1)}, u32[]{:S(2)}, u32[]{:S(2)}) %collective-permute-start.4) | collective-permute-done | bytes 524320 | tf_op jit(solution)/shard_map/ppermute | solution.py:33
  30.8 0.2 broadcast_select_fusion
  31.0 0.3 bitcast_select_fusion.3
  31.3 1.6 %collective-permute-done.5 = bf16[4,4,128,128]{3,2,1,0:T(8,128)(2,1)S(1)} collective-permute-done((bf16[4,4,128,128]{3,2,1,0:T(8,128)(2,1)}, bf16[4,4,128,128]{3,2,1,0:T(8,128)(2,1)S(1)}, u32[]{:S(2)}, u32[]{:S(2)}) %collective-permute-start.5) | collective-permute-done | bytes 524320 | tf_op jit(solution)/shard_map/ppermute | solution.py:35
  32.9 1.3 %pad_maximum_fusion = bf16[4,4,4,128,128]{4,3,2,1,0:T(8,128)(2,1)S(1)} fusion(bf16[1,4,4,128,128]{4,3,2,1,0:T(8,128)(2,1)S(1)} %bitcast.141, bf16[1,4,4,128,128]{4,3,2,1,0:T(8,128)(2,1)} %bitcast.11, bf16[1,4,4,128,128]{4,3,2,1,0:T(8,128)(2,1)S(1)} %bitcast.140, bf16[1,4,4,128,128]{4,3,2,1,0:T(8,128)(2,1)S(1)} %get-tuple-element.24), kind=kLoop, calls=%fused_computation.3 | loop fusion | flops 3145728 | bytes 4194304 | tf_op jit(solution)/shard_map/stack | solution.py:36
  34.3 0.8 %fusion.36 = f32[128,128]{1,0:T(8,128)S(1)} fusion(bf16[16,4,128,128]{3,2,1,0:T(8,128)(2,1)S(1)} %bitcast.134, bf16[16,1,128,128]{3,2,0,1:T(8,128)(2,1)S(1)} %get-tuple-element.22, bf16[16,1,128,128]{3,2,0,1:T(8,128)(2,1)S(1)} %get-tuple-element.23, bf16[16,1,128,128]{3,2,0,1:T(8,128)(2,1)S(1)} %get-tuple-element.21, ...), kind=kOutput, calls=%fused_computation.29 | convolution fusion | flops 271597568 | bytes 4325376 | tf_op jit(solution)/shard_map/slpq,slpr->qr/dot_general | solution.py:78
  35.1 0.3 bitcast_convert_fusion.1
  35.4 0.7 collective-permute-start.8
  36.1 2.0 %collective-permute-start.7 = (bf16[128,128]{0,1:T(8,128)(2,1)S(1)}, bf16[128,128]{0,1:T(8,128)(2,1)S(1)}, u32[]{:S(2)}, u32[]{:S(2)}) collective-permute-start(bf16[128,128]{0,1:T(8,128)(2,1)S(1)} %get-tuple-element.30), channel_id=1, source_target_pairs={{0,8},{1,9},{2,10},{3,11},{4,12},{5,13},{6,14},{7,15},{8,0},{9,1},... | collective-permute-start | bytes 98312 | tf_op jit(solution)/shard_map/ppermute | solution.py:25
  38.1 1.9 %collective-permute-start.6 = (bf16[128,128]{0,1:T(8,128)(2,1)S(1)}, bf16[128,128]{0,1:T(8,128)(2,1)S(1)}, u32[]{:S(2)}, u32[]{:S(2)}) collective-permute-start(bf16[128,128]{0,1:T(8,128)(2,1)S(1)} %get-tuple-element.30), channel_id=1, source_target_pairs={{0,4},{1,5},{2,6},{3,7},{4,8},{5,9},{6,10},{7,11},{8,12},{9,13},{1... | collective-permute-start | bytes 98312 | tf_op jit(solution)/shard_map/ppermute | solution.py:25
  40.0 1.2 %collective-permute-done.7 = bf16[128,128]{0,1:T(8,128)(2,1)S(1)} collective-permute-done((bf16[128,128]{0,1:T(8,128)(2,1)S(1)}, bf16[128,128]{0,1:T(8,128)(2,1)S(1)}, u32[]{:S(2)}, u32[]{:S(2)}) %collective-permute-start.7) | collective-permute-done | bytes 32800 | tf_op jit(solution)/shard_map/ppermute | solution.py:25
  41.2 2.6 %collective-permute-done.6 = bf16[128,128]{0,1:T(8,128)(2,1)S(1)} collective-permute-done((bf16[128,128]{0,1:T(8,128)(2,1)S(1)}, bf16[128,128]{0,1:T(8,128)(2,1)S(1)}, u32[]{:S(2)}, u32[]{:S(2)}) %collective-permute-start.6) | collective-permute-done | bytes 32800 | tf_op jit(solution)/shard_map/ppermute | solution.py:25
  43.9 1.6 %collective-permute-start.10 = (bf16[4,128,128]{1,2,0:T(8,128)(2,1)S(1)}, bf16[4,128,128]{1,2,0:T(8,128)(2,1)S(1)}, u32[]{:S(2)}, u32[]{:S(2)}) collective-permute-start(bf16[4,128,128]{1,2,0:T(8,128)(2,1)S(1)} %get-tuple-element.29), channel_id=1, source_target_pairs={{0,2},{1,3},{2,0},{3,1},{4,6},{5,7},{6,4},{7,5},{8,10},{9,11},{10,... | collective-permute-start | bytes 393224 | tf_op jit(solution)/shard_map/ppermute | solution.py:39
  45.5 0.3 collective-permute-start.9
  45.7 0.2 bitcast_select_fusion.1
  45.9 3.7 %collective-permute-done.11 = bf16[4,128,128]{1,2,0:T(8,128)(2,1)S(1)} collective-permute-done((bf16[4,128,128]{1,2,0:T(8,128)(2,1)S(1)}, bf16[4,128,128]{1,2,0:T(8,128)(2,1)S(1)}, u32[]{:S(2)}, u32[]{:S(2)}) %collective-permute-start.11) | collective-permute-done | bytes 131104 | tf_op jit(solution)/shard_map/ppermute | solution.py:39
  49.6 2.9 %collective-permute-done.10 = bf16[4,128,128]{1,2,0:T(8,128)(2,1)S(1)} collective-permute-done((bf16[4,128,128]{1,2,0:T(8,128)(2,1)S(1)}, bf16[4,128,128]{1,2,0:T(8,128)(2,1)S(1)}, u32[]{:S(2)}, u32[]{:S(2)}) %collective-permute-start.10) | collective-permute-done | bytes 131104 | tf_op jit(solution)/shard_map/ppermute | solution.py:39
  52.6 0.3 convolution_bitcast_fusion.3
  52.9 0.7 fusion.31
  53.6 0.3 bitcast_convert_fusion
  53.9 0.6 collective-permute-start.14
  54.5 1.0 %collective-permute-start.13 = (bf16[128,128]{0,1:T(8,128)(2,1)S(1)}, bf16[128,128]{0,1:T(8,128)(2,1)S(1)}, u32[]{:S(2)}, u32[]{:S(2)}) collective-permute-start(bf16[128,128]{0,1:T(8,128)(2,1)S(1)} %get-tuple-element.32), channel_id=1, source_target_pairs={{0,8},{1,9},{2,10},{3,11},{4,12},{5,13},{6,14},{7,15},{8,0},{9,1},... | collective-permute-start | bytes 98312 | tf_op jit(solution)/shard_map/ppermute | solution.py:25
  55.5 0.4 collective-permute-start.12
  56.0 0.5 convolution_bitcast_fusion.4
  56.5 1.4 %collective-permute-done.14 = bf16[128,128]{0,1:T(8,128)(2,1)S(1)} collective-permute-done((bf16[128,128]{0,1:T(8,128)(2,1)S(1)}, bf16[128,128]{0,1:T(8,128)(2,1)S(1)}, u32[]{:S(2)}, u32[]{:S(2)}) %collective-permute-start.14) | collective-permute-done | bytes 32800 | tf_op jit(solution)/shard_map/ppermute | solution.py:25
  57.8 1.5 %collective-permute-done.13 = bf16[128,128]{0,1:T(8,128)(2,1)S(1)} collective-permute-done((bf16[128,128]{0,1:T(8,128)(2,1)S(1)}, bf16[128,128]{0,1:T(8,128)(2,1)S(1)}, u32[]{:S(2)}, u32[]{:S(2)}) %collective-permute-start.13) | collective-permute-done | bytes 32800 | tf_op jit(solution)/shard_map/ppermute | solution.py:25
  59.3 1.9 %collective-permute-done.12 = bf16[128,128]{0,1:T(8,128)(2,1)S(1)} collective-permute-done((bf16[128,128]{0,1:T(8,128)(2,1)S(1)}, bf16[128,128]{0,1:T(8,128)(2,1)S(1)}, u32[]{:S(2)}, u32[]{:S(2)}) %collective-permute-start.12) | collective-permute-done | bytes 32800 | tf_op jit(solution)/shard_map/ppermute | solution.py:25
  61.4 1.8 %collective-permute-start.15 = (bf16[4,128,128]{1,2,0:T(8,128)(2,1)S(1)}, bf16[4,128,128]{1,2,0:T(8,128)(2,1)S(1)}, u32[]{:S(2)}, u32[]{:S(2)}) collective-permute-start(bf16[4,128,128]{1,2,0:T(8,128)(2,1)S(1)} %get-tuple-element.27), channel_id=1, source_target_pairs={{0,1},{1,0},{2,3},{3,2},{4,5},{5,4},{6,7},{7,6},{8,9},{9,8},{10,11... | collective-permute-start | bytes 393224 | tf_op jit(solution)/shard_map/ppermute | solution.py:39
  63.2 0.5 convolution_bitcast_fusion.1
  63.7 2.8 %collective-permute-done.17 = bf16[4,128,128]{1,2,0:T(8,128)(2,1)S(1)} collective-permute-done((bf16[4,128,128]{1,2,0:T(8,128)(2,1)S(1)}, bf16[4,128,128]{1,2,0:T(8,128)(2,1)S(1)}, u32[]{:S(2)}, u32[]{:S(2)}) %collective-permute-start.17) | collective-permute-done | bytes 131104 | tf_op jit(solution)/shard_map/ppermute | solution.py:39
  66.5 1.2 %collective-permute-done.16 = bf16[4,128,128]{1,2,0:T(8,128)(2,1)S(1)} collective-permute-done((bf16[4,128,128]{1,2,0:T(8,128)(2,1)S(1)}, bf16[4,128,128]{1,2,0:T(8,128)(2,1)S(1)}, u32[]{:S(2)}, u32[]{:S(2)}) %collective-permute-start.16) | collective-permute-done | bytes 131104 | tf_op jit(solution)/shard_map/ppermute | solution.py:39
  67.8 0.3 fusion.43
  68.2 0.3 convolution_bitcast_fusion
  68.5 0.8 %copy.24 = f32[3,128,128]{2,1,0:T(8,128)} copy(f32[3,128,128]{1,2,0:T(8,128)S(1)} %pad_maximum_fusion.4) | data formatting | bytes 393216 | tf_op jit(solution)/shard_map/stack | solution.py:121
  (31 shorter events, 0.6 us)
Async XLA Ops:
  0.0 19.7 %copy-start = (bf16[1,16,2,128,128]{4,3,2,1,0:T(8,128)(2,1)S(1)}, bf16[1,16,2,128,128]{4,3,2,1,0:T(8,128)(2,1)}, u32[]{:S(2)}) copy-start(bf16[1,16,2,128,128]{4,3,2,1,0:T(8,128)(2,1)} %param.16) | copy-start | bytes 3145732
  0.0 19.1 %copy-start.3 = (s32[1,16,2]{1,2,0:T(2,128)S(1)}, s32[1,16,2]{1,2,0:T(2,128)}, u32[]{:S(2)}) copy-start(s32[1,16,2]{1,2,0:T(2,128)} %param.17) | copy-start | bytes 388
  0.0 9.3 %collective-permute-start.2 = (bf16[4,128,128]{2,1,0:T(8,128)(2,1)}, bf16[4,128,128]{2,1,0:T(8,128)(2,1)S(1)}, u32[]{:S(2)}, u32[]{:S(2)}) collective-permute-start(bf16[4,128,128]{2,1,0:T(8,128)(2,1)} %param.19), channel_id=1, source_target_pairs={{0,12},{1,13},{2,14},{3,15},{4,0},{5,1},{6,2},{7,3},{8,4},{9,5},{1... | collective-permute-start | bytes 393224 | tf_op jit(solution)/shard_map/ppermute | solution.py:25
  5.1 11.4 %collective-permute-start.1 = (bf16[4,128,128]{2,1,0:T(8,128)(2,1)}, bf16[4,128,128]{2,1,0:T(8,128)(2,1)S(1)}, u32[]{:S(2)}, u32[]{:S(2)}) collective-permute-start(bf16[4,128,128]{2,1,0:T(8,128)(2,1)} %param.19), channel_id=1, source_target_pairs={{0,8},{1,9},{2,10},{3,11},{4,12},{5,13},{6,14},{7,15},{8,0},{9,1},... | collective-permute-start | bytes 393224 | tf_op jit(solution)/shard_map/ppermute | solution.py:25
  5.1 11.4 %collective-permute-start = (bf16[4,128,128]{2,1,0:T(8,128)(2,1)}, bf16[4,128,128]{2,1,0:T(8,128)(2,1)S(1)}, u32[]{:S(2)}, u32[]{:S(2)}) collective-permute-start(bf16[4,128,128]{2,1,0:T(8,128)(2,1)} %param.19), channel_id=1, source_target_pairs={{0,4},{1,5},{2,6},{3,7},{4,8},{5,9},{6,10},{7,11},{8,12},{9,13},{1... | collective-permute-start | bytes 393224 | tf_op jit(solution)/shard_map/ppermute | solution.py:25
  17.5 13.4 %collective-permute-start.4 = (bf16[4,4,128,128]{3,2,1,0:T(8,128)(2,1)S(1)}, bf16[4,4,128,128]{3,2,1,0:T(8,128)(2,1)}, u32[]{:S(2)}, u32[]{:S(2)}) collective-permute-start(bf16[4,4,128,128]{3,2,1,0:T(8,128)(2,1)S(1)} %get-tuple-element.25), channel_id=1, source_target_pairs={{0,2},{1,3},{2,0},{3,1},{4,6},{5,7},{6,4},{7,5},{8,10},{9,11},{10,... | collective-permute-start | bytes 1572872 | tf_op jit(solution)/shard_map/ppermute | solution.py:33
  20.8 10.5 %collective-permute-start.3 = (bf16[4,4,128,128]{3,2,1,0:T(8,128)(2,1)S(1)}, bf16[4,4,128,128]{3,2,1,0:T(8,128)(2,1)S(1)}, u32[]{:S(2)}, u32[]{:S(2)}) collective-permute-start(bf16[4,4,128,128]{3,2,1,0:T(8,128)(2,1)S(1)} %get-tuple-element.25), channel_id=1, source_target_pairs={{0,1},{1,0},{2,3},{3,2},{4,5},{5,4},{6,7},{7,6},{8,9},{9,8},{10,11... | collective-permute-start | bytes 1572872 | tf_op jit(solution)/shard_map/ppermute | solution.py:34
  30.8 2.1 %collective-permute-start.5 = (bf16[4,4,128,128]{3,2,1,0:T(8,128)(2,1)}, bf16[4,4,128,128]{3,2,1,0:T(8,128)(2,1)S(1)}, u32[]{:S(2)}, u32[]{:S(2)}) collective-permute-start(bf16[4,4,128,128]{3,2,1,0:T(8,128)(2,1)} %collective-permute-done.4), channel_id=1, source_target_pairs={{0,1},{1,0},{2,3},{3,2},{4,5},{5,4},{6,7},{7,6},{8,9},{9,8},{10,11... | collective-permute-start | bytes 1572872 | tf_op jit(solution)/shard_map/ppermute | solution.py:35
  32.9 1.4 %copy-start.2 = (f32[3,128,128]{2,1,0:T(8,128)S(1)}, f32[3,128,128]{2,1,0:T(8,128)}, u32[]{:S(2)}) copy-start(f32[3,128,128]{2,1,0:T(8,128)} %param.20) | copy-start | bytes 589828
  34.3 0.8 %copy-start.1 = (f32[1,128,128]{2,1,0:T(8,128)S(1)}, f32[1,128,128]{2,1,0:T(8,128)}, u32[]{:S(2)}) copy-start(f32[1,128,128]{2,1,0:T(8,128)} %param.21) | copy-start | bytes 196612
  35.4 4.6 %collective-permute-start.8 = (bf16[128,128]{0,1:T(8,128)(2,1)S(1)}, bf16[128,128]{0,1:T(8,128)(2,1)S(1)}, u32[]{:S(2)}, u32[]{:S(2)}) collective-permute-start(bf16[128,128]{0,1:T(8,128)(2,1)S(1)} %get-tuple-element.30), channel_id=1, source_target_pairs={{0,12},{1,13},{2,14},{3,15},{4,0},{5,1},{6,2},{7,3},{8,4},{9,5},{1... | collective-permute-start | bytes 98312 | tf_op jit(solution)/shard_map/ppermute | solution.py:25
  36.1 5.1 %collective-permute-start.7 = (bf16[128,128]{0,1:T(8,128)(2,1)S(1)}, bf16[128,128]{0,1:T(8,128)(2,1)S(1)}, u32[]{:S(2)}, u32[]{:S(2)}) collective-permute-start(bf16[128,128]{0,1:T(8,128)(2,1)S(1)} %get-tuple-element.30), channel_id=1, source_target_pairs={{0,8},{1,9},{2,10},{3,11},{4,12},{5,13},{6,14},{7,15},{8,0},{9,1},... | collective-permute-start | bytes 98312 | tf_op jit(solution)/shard_map/ppermute | solution.py:25
  38.1 5.7 %collective-permute-start.6 = (bf16[128,128]{0,1:T(8,128)(2,1)S(1)}, bf16[128,128]{0,1:T(8,128)(2,1)S(1)}, u32[]{:S(2)}, u32[]{:S(2)}) collective-permute-start(bf16[128,128]{0,1:T(8,128)(2,1)S(1)} %get-tuple-element.30), channel_id=1, source_target_pairs={{0,4},{1,5},{2,6},{3,7},{4,8},{5,9},{6,10},{7,11},{8,12},{9,13},{1... | collective-permute-start | bytes 98312 | tf_op jit(solution)/shard_map/ppermute | solution.py:25
  43.8 5.8 %collective-permute-start.11 = (bf16[4,128,128]{1,2,0:T(8,128)(2,1)S(1)}, bf16[4,128,128]{1,2,0:T(8,128)(2,1)S(1)}, u32[]{:S(2)}, u32[]{:S(2)}) collective-permute-start(bf16[4,128,128]{1,2,0:T(8,128)(2,1)S(1)} %get-tuple-element.29), channel_id=1, source_target_pairs={{0,3},{1,2},{2,1},{3,0},{4,7},{5,6},{6,5},{7,4},{8,11},{9,10},{10,... | collective-permute-start | bytes 393224 | tf_op jit(solution)/shard_map/ppermute | solution.py:39
  43.9 8.6 %collective-permute-start.10 = (bf16[4,128,128]{1,2,0:T(8,128)(2,1)S(1)}, bf16[4,128,128]{1,2,0:T(8,128)(2,1)S(1)}, u32[]{:S(2)}, u32[]{:S(2)}) collective-permute-start(bf16[4,128,128]{1,2,0:T(8,128)(2,1)S(1)} %get-tuple-element.29), channel_id=1, source_target_pairs={{0,2},{1,3},{2,0},{3,1},{4,6},{5,7},{6,4},{7,5},{8,10},{9,11},{10,... | collective-permute-start | bytes 393224 | tf_op jit(solution)/shard_map/ppermute | solution.py:39
  45.5 7.0 %collective-permute-start.9 = (bf16[4,128,128]{1,2,0:T(8,128)(2,1)S(1)}, bf16[4,128,128]{1,2,0:T(8,128)(2,1)S(1)}, u32[]{:S(2)}, u32[]{:S(2)}) collective-permute-start(bf16[4,128,128]{1,2,0:T(8,128)(2,1)S(1)} %get-tuple-element.29), channel_id=1, source_target_pairs={{0,1},{1,0},{2,3},{3,2},{4,5},{5,4},{6,7},{7,6},{8,9},{9,8},{10,11... | collective-permute-start | bytes 393224 | tf_op jit(solution)/shard_map/ppermute | solution.py:39
  53.9 4.0 %collective-permute-start.14 = (bf16[128,128]{0,1:T(8,128)(2,1)S(1)}, bf16[128,128]{0,1:T(8,128)(2,1)S(1)}, u32[]{:S(2)}, u32[]{:S(2)}) collective-permute-start(bf16[128,128]{0,1:T(8,128)(2,1)S(1)} %get-tuple-element.32), channel_id=1, source_target_pairs={{0,12},{1,13},{2,14},{3,15},{4,0},{5,1},{6,2},{7,3},{8,4},{9,5},{1... | collective-permute-start | bytes 98312 | tf_op jit(solution)/shard_map/ppermute | solution.py:25
  54.5 4.8 %collective-permute-start.13 = (bf16[128,128]{0,1:T(8,128)(2,1)S(1)}, bf16[128,128]{0,1:T(8,128)(2,1)S(1)}, u32[]{:S(2)}, u32[]{:S(2)}) collective-permute-start(bf16[128,128]{0,1:T(8,128)(2,1)S(1)} %get-tuple-element.32), channel_id=1, source_target_pairs={{0,8},{1,9},{2,10},{3,11},{4,12},{5,13},{6,14},{7,15},{8,0},{9,1},... | collective-permute-start | bytes 98312 | tf_op jit(solution)/shard_map/ppermute | solution.py:25
  55.5 5.7 %collective-permute-start.12 = (bf16[128,128]{0,1:T(8,128)(2,1)S(1)}, bf16[128,128]{0,1:T(8,128)(2,1)S(1)}, u32[]{:S(2)}, u32[]{:S(2)}) collective-permute-start(bf16[128,128]{0,1:T(8,128)(2,1)S(1)} %get-tuple-element.32), channel_id=1, source_target_pairs={{0,4},{1,5},{2,6},{3,7},{4,8},{5,9},{6,10},{7,11},{8,12},{9,13},{1... | collective-permute-start | bytes 98312 | tf_op jit(solution)/shard_map/ppermute | solution.py:25
  61.3 5.3 %collective-permute-start.17 = (bf16[4,128,128]{1,2,0:T(8,128)(2,1)S(1)}, bf16[4,128,128]{1,2,0:T(8,128)(2,1)S(1)}, u32[]{:S(2)}, u32[]{:S(2)}) collective-permute-start(bf16[4,128,128]{1,2,0:T(8,128)(2,1)S(1)} %get-tuple-element.27), channel_id=1, source_target_pairs={{0,3},{1,2},{2,1},{3,0},{4,7},{5,6},{6,5},{7,4},{8,11},{9,10},{10,... | collective-permute-start | bytes 393224 | tf_op jit(solution)/shard_map/ppermute | solution.py:39
  61.3 6.4 %collective-permute-start.16 = (bf16[4,128,128]{1,2,0:T(8,128)(2,1)S(1)}, bf16[4,128,128]{1,2,0:T(8,128)(2,1)S(1)}, u32[]{:S(2)}, u32[]{:S(2)}) collective-permute-start(bf16[4,128,128]{1,2,0:T(8,128)(2,1)S(1)} %get-tuple-element.27), channel_id=1, source_target_pairs={{0,2},{1,3},{2,0},{3,1},{4,6},{5,7},{6,4},{7,5},{8,10},{9,11},{10,... | collective-permute-start | bytes 393224 | tf_op jit(solution)/shard_map/ppermute | solution.py:39
  61.4 6.3 %collective-permute-start.15 = (bf16[4,128,128]{1,2,0:T(8,128)(2,1)S(1)}, bf16[4,128,128]{1,2,0:T(8,128)(2,1)S(1)}, u32[]{:S(2)}, u32[]{:S(2)}) collective-permute-start(bf16[4,128,128]{1,2,0:T(8,128)(2,1)S(1)} %get-tuple-element.27), channel_id=1, source_target_pairs={{0,1},{1,0},{2,3},{3,2},{4,5},{5,4},{6,7},{7,6},{8,9},{9,8},{10,11... | collective-permute-start | bytes 393224 | tf_op jit(solution)/shard_map/ppermute | solution.py:39

commit v5 on v4

--- a/solution.py
+++ b/solution.py
@@ -33,26 +33,27 @@
         across = lax.ppermute(stack, "wide", [(d, d ^ 2) for d in range(wide)])
         beside = lax.ppermute(stack, "wide", [(d, d ^ 1) for d in range(wide)])
         diagonal = lax.ppermute(across, "wide", [(d, d ^ 1) for d in range(wide)])
-        return jnp.stack([stack, beside, across, diagonal]), np.array([0, 1, 2, 3], np.int32)
+        return [stack, beside, across, diagonal]
     parts = [stack]
     for m in range(1, inner):
         parts.append(lax.ppermute(stack, "wide", [(d, d ^ m) for d in range(wide)]))
-    return jnp.stack(parts), np.arange(inner, dtype=np.int32)
+    return parts
 
 
 def gather_blocks(x, wide, doubling):
     inner = inner_size(wide)
     lines = wide // inner
     stack, shifted = line_stage(x, wide, inner)
-    stack, masks = slab_stage(stack, wide, inner, doubling)
+    pieces = slab_stage(stack, wide, inner, doubling)
     me = lax.axis_index("wide")
     line = np.arange(lines, dtype=np.int32)
     source_line = (me // inner - line) % lines if shifted else jnp.asarray(line)
+    masks = np.arange(inner, dtype=np.int32)
     blocks = (
         source_line[None, :] * inner
         + jnp.bitwise_xor(me % inner, jnp.asarray(masks))[:, None]
     )
-    return stack.reshape((wide,) + x.shape), blocks.reshape(wide)
+    return pieces, blocks.reshape(wide)
 
 
 def tiles_by_lag(retarded_tiles, tile_lags, column_of_block, block_of_slot, lags_wanted):
@@ -84,6 +85,7 @@
     column_of_block = jnp.argsort(block_owner)
 
     later, later_blocks = gather_blocks(later_current, wide, True)
+    lines = later[0].shape[0]
     by_lag = tiles_by_lag(
         retarded_tiles, tile_lags, column_of_block, later_blocks, range(1, lag_count + 1)
     )
@@ -100,16 +102,20 @@
     recent = None
     for moment in range(step_count - 1, -1, -1):
         first = max(1, step_count - moment)
-        retarded = rowwise(
-            by_lag[:, first - 1 :],
-            later[:, moment + first - step_count : moment + lag_count + 1 - step_count],
-        )
+        retarded = None
+        for m, piece in enumerate(later):
+            term = rowwise(
+                by_lag[m * lines : (m + 1) * lines, first - 1 :],
+                piece[:, moment + first - step_count : moment + lag_count + 1 - step_count],
+            )
+            retarded = term if retarded is None else retarded + term
         for delay in range(1, first):
             retarded = retarded + rowwise(recent[:, delay - 1], newer[moment + delay])
         current = advance(moment, retarded)
         results[moment] = current
         if moment > 0:
-            newer[moment], new_blocks = gather_blocks(current.astype(jnp.bfloat16), wide, False)
+            pieces, new_blocks = gather_blocks(current.astype(jnp.bfloat16), wide, False)
+            newer[moment] = jnp.concatenate(pieces)
             if recent is None:
                 recent = tiles_by_lag(
                     retarded_tiles,

time: 69.7 us -> 67.3 us (0.966)
  waiting for transfers between devices: 38.4 us -> 30.7 us
  starting transfers between devices: 18.2 us -> 23 us
  other arithmetic: 5.5 us -> 3.07 us
  matrix products: 3.98 us -> 5.8 us
  local copies, waits for them, and re-layouts: 2.98 us -> 4.34 us
    ppermute x9, waiting for transfers between devices: 16.2 us -> 6.62 us  [line_stage(): parts.append(lax.ppermute(x, 'wide', pairs))]
    ppermute x9, starting transfers between devices: 12.7 us -> 17.5 us  [line_stage(): parts.append(lax.ppermute(x, 'wide', pairs))]
    another operation x6 -> x3, other arithmetic: 2.52 us -> 0.11 us  [line_stage(): return (jnp.stack(parts), True)]
    ppermute x6, waiting for transfers between devices: 10.6 us -> 12.6 us  [slab_stage(): parts.append(lax.ppermute(stack, 'wide', [(d, d ^ m) for d in range(wide)]))]
    dot_general x6 -> x15, matrix products: 3.13 us -> 4.95 us  [rowwise(): return jnp.einsum(spec, tiles, currents, preferred_element_type=jnp.float32)]
    ppermute x1, waiting for transfers between devices: 1.65 us -> 0.01 us  [slab_stage(): diagonal = lax.ppermute(across, 'wide', [(d, d ^ 1) for d in range(wide)])]
    ppermute x1, waiting for transfers between devices: 9.91 us -> 11.4 us  [slab_stage(): across = lax.ppermute(stack, 'wide', [(d, d ^ 2) for d in range(wide)])]
  transfers between devices with their start and end apart: 18 -> 18, of which waited for: 13 -> 10; matrix products, arithmetic and copies ran while one was open for 9% -> 14% of each run, Pallas kernels for 0% -> 0%
where the time goes in v5:
time: 67.3 us; the launch traced here: 67.2 us
  waiting for transfers between devices  30.7 us (46%)
  starting transfers between devices  23 us (34%)
  matrix products  5.8 us (9%)
  local copies, waits for them, and re-layouts  4.34 us (6%)
  other arithmetic  3.07 us (5%)
    ppermute x9, starting transfers between devices, line_stage(): parts.append(lax.ppermute(x, 'wide', pairs))  17.5 us
    ppermute x6, waiting for transfers between devices, slab_stage(): parts.append(lax.ppermute(stack, 'wide', [(d, d ^ m) for d in range(wide)]))  12.6 us
    ppermute x1, waiting for transfers between devices, slab_stage(): across = lax.ppermute(stack, 'wide', [(d, d ^ 2) for d in range(wide)])  11.4 us
    ppermute x9, waiting for transfers between devices, line_stage(): parts.append(lax.ppermute(x, 'wide', pairs))  6.62 us
    dot_general x15, matrix products, rowwise(): return jnp.einsum(spec, tiles, currents, preferred_element_type=jnp.float32)  4.95 us
    ppermute x6, starting transfers between devices, slab_stage(): parts.append(lax.ppermute(stack, 'wide', [(d, d ^ m) for d in range(wide)]))  3.87 us
    sort x1, other arithmetic, per_device(): column_of_block = jnp.argsort(block_owner)  1.9 us
    ppermute x1, starting transfers between devices, slab_stage(): across = lax.ppermute(stack, 'wide', [(d, d ^ 2) for d in range(wide)])  1.58 us
  transfers between devices with their start and end apart: 18, of which 10 were waited for; matrix products, arithmetic and copies ran while one was open for 14% of the time, Pallas kernels for 0%

profile of v5, /device:TPU:0, one launch (start us, length us, event | category | flops | bytes accessed | tf_op | source)
XLA Modules:
  0.0 67.2 jit_solution(7103541702538329861)
XLA Ops:
  0.0 3.0 %collective-permute-start = (bf16[4,128,128]{2,1,0:T(8,128)(2,1)}, bf16[4,128,128]{2,1,0:T(8,128)(2,1)S(1)}, u32[]{:S(2)}, u32[]{:S(2)}) collective-permute-start(bf16[4,128,128]{2,1,0:T(8,128)(2,1)} %param.19), channel_id=1, source_target_pairs={{0,4},{1,5},{2,6},{3,7},{4,8},{5,9},{6,10},{7,11},{8,12},{9,13},{1... | collective-permute-start | bytes 393224 | tf_op jit(solution)/shard_map/ppermute | solution.py:25
  3.0 2.6 %collective-permute-start.1 = (bf16[4,128,128]{2,1,0:T(8,128)(2,1)}, bf16[4,128,128]{2,1,0:T(8,128)(2,1)S(1)}, u32[]{:S(2)}, u32[]{:S(2)}) collective-permute-start(bf16[4,128,128]{2,1,0:T(8,128)(2,1)} %param.19), channel_id=1, source_target_pairs={{0,8},{1,9},{2,10},{3,11},{4,12},{5,13},{6,14},{7,15},{8,0},{9,1},... | collective-permute-start | bytes 393224 | tf_op jit(solution)/shard_map/ppermute | solution.py:25
  5.6 1.3 %collective-permute-start.2 = (bf16[4,128,128]{2,1,0:T(8,128)(2,1)}, bf16[4,128,128]{2,1,0:T(8,128)(2,1)S(1)}, u32[]{:S(2)}, u32[]{:S(2)}) collective-permute-start(bf16[4,128,128]{2,1,0:T(8,128)(2,1)} %param.19), channel_id=1, source_target_pairs={{0,12},{1,13},{2,14},{3,15},{4,0},{5,1},{6,2},{7,3},{8,4},{9,5},{1... | collective-permute-start | bytes 393224 | tf_op jit(solution)/shard_map/ppermute | solution.py:25
  7.2 1.9 %sort.17 = (s32[16]{0:T(128)}, s32[16]{0:T(128)S(1)}) sort(s32[16]{0:T(128)} %param.18, s32[16]{0:T(128)S(1)} %iota.5), dimensions={0}, to_apply=%region_0.0 | sort | flops 64 | bytes 256 | tf_op jit(solution)/shard_map/jit(argsort)/sort | solution.py:85
  9.1 0.7 gather_fusion
  9.7 0.8 %copy.18 = s32[16,2]{1,0:T(8,128)S(1)} copy(s32[16,2]{0,1:T(2,128)} %bitcast.198) | data formatting | bytes 256 | tf_op jit(solution)/shard_map/squeeze | solution.py:62
  10.5 0.7 %gather_fusion.2 = bf16[16,2,128,128]{3,2,1,0:T(8,128)(2,1)S(1)} fusion(bf16[16,2,128,128]{3,2,1,0:T(8,128)(2,1)S(1)} %bitcast.179, s32[1024]{0:T(1024)S(1)} %pad_clamp_fusion), kind=kCustom, calls=%fused_computation.2.clone | custom fusion | bytes 2097216 | tf_op jit(solution)/shard_map/jit(_take)/gather | solution.py:61
  11.3 0.6 gather_fusion.1
  12.3 0.3 bitcast_select_fusion.3
  12.6 1.8 %collective-permute-done.1 = bf16[4,128,128]{2,1,0:T(8,128)(2,1)S(1)} collective-permute-done((bf16[4,128,128]{2,1,0:T(8,128)(2,1)}, bf16[4,128,128]{2,1,0:T(8,128)(2,1)S(1)}, u32[]{:S(2)}, u32[]{:S(2)}) %collective-permute-start.1) | collective-permute-done | bytes 131104 | tf_op jit(solution)/shard_map/ppermute | solution.py:25
  14.5 1.6 %collective-permute-start.4 = (bf16[4,4,128,128]{3,2,1,0:T(8,128)(2,1)S(1)}, bf16[4,4,128,128]{3,2,1,0:T(8,128)(2,1)S(1)}, u32[]{:S(2)}, u32[]{:S(2)}) collective-permute-start(bf16[4,4,128,128]{3,2,1,0:T(8,128)(2,1)S(1)} %pad_maximum_fusion.3), channel_id=1, source_target_pairs={{0,2},{1,3},{2,0},{3,1},{4,6},{5,7},{6,4},{7,5},{8,10},{9,11},{10,... | collective-permute-start | bytes 1572872 | tf_op jit(solution)/shard_map/ppermute | solution.py:33
  16.4 0.3 convolution_bitcast_fusion.7
  17.0 11.4 %collective-permute-done.4 = bf16[4,4,128,128]{3,2,1,0:T(8,128)(2,1)S(1)} collective-permute-done((bf16[4,4,128,128]{3,2,1,0:T(8,128)(2,1)S(1)}, bf16[4,4,128,128]{3,2,1,0:T(8,128)(2,1)S(1)}, u32[]{:S(2)}, u32[]{:S(2)}) %collective-permute-start.4) | collective-permute-done | bytes 524320 | tf_op jit(solution)/shard_map/ppermute | solution.py:33
  28.4 0.3 convolution_bitcast_fusion.5
  28.7 0.4 convolution_bitcast_fusion.1
  29.1 0.3 convolution_bitcast_fusion.2
  29.4 0.3 convolution_bitcast_fusion.9
  29.7 0.3 fusion.7
  30.0 0.4 fusion.12
  30.4 0.5 copy-done.3
  31.0 0.3 fusion.14
  31.3 0.3 constant_dynamic-update-slice_fusion.6
  31.6 3.4 %collective-permute-start.6 = (bf16[128,128]{0,1:T(8,128)(2,1)S(1)}, bf16[128,128]{0,1:T(8,128)(2,1)S(1)}, u32[]{:S(2)}, u32[]{:S(2)}) collective-permute-start(bf16[128,128]{0,1:T(8,128)(2,1)S(1)} %get-tuple-element.21), channel_id=1, source_target_pairs={{0,4},{1,5},{2,6},{3,7},{4,8},{5,9},{6,10},{7,11},{8,12},{9,13},{1... | collective-permute-start | bytes 98312 | tf_op jit(solution)/shard_map/ppermute | solution.py:25
  35.0 0.6 collective-permute-start.7
  35.6 1.9 %collective-permute-start.8 = (bf16[128,128]{0,1:T(8,128)(2,1)S(1)}, bf16[128,128]{0,1:T(8,128)(2,1)S(1)}, u32[]{:S(2)}, u32[]{:S(2)}) collective-permute-start(bf16[128,128]{0,1:T(8,128)(2,1)S(1)} %get-tuple-element.21), channel_id=1, source_target_pairs={{0,12},{1,13},{2,14},{3,15},{4,0},{5,1},{6,2},{7,3},{8,4},{9,5},{1... | collective-permute-start | bytes 98312 | tf_op jit(solution)/shard_map/ppermute | solution.py:25
  37.8 2.4 %collective-permute-done.7 = bf16[128,128]{0,1:T(8,128)(2,1)S(1)} collective-permute-done((bf16[128,128]{0,1:T(8,128)(2,1)S(1)}, bf16[128,128]{0,1:T(8,128)(2,1)S(1)}, u32[]{:S(2)}, u32[]{:S(2)}) %collective-permute-start.7) | collective-permute-done | bytes 32800 | tf_op jit(solution)/shard_map/ppermute | solution.py:25
  40.3 1.6 %collective-permute-start.10 = (bf16[4,128,128]{1,2,0:T(8,128)(2,1)S(1)}, bf16[4,128,128]{1,2,0:T(8,128)(2,1)S(1)}, u32[]{:S(2)}, u32[]{:S(2)}) collective-permute-start(bf16[4,128,128]{1,2,0:T(8,128)(2,1)S(1)} %pad_maximum_fusion.5), channel_id=1, source_target_pairs={{0,2},{1,3},{2,0},{3,1},{4,6},{5,7},{6,4},{7,5},{8,10},{9,11},{10,... | collective-permute-start | bytes 393224 | tf_op jit(solution)/shard_map/ppermute | solution.py:39
  41.9 0.3 collective-permute-start.11
  42.2 4.4 %collective-permute-done.10 = bf16[4,128,128]{1,2,0:T(8,128)(2,1)S(1)} collective-permute-done((bf16[4,128,128]{1,2,0:T(8,128)(2,1)S(1)}, bf16[4,128,128]{1,2,0:T(8,128)(2,1)S(1)}, u32[]{:S(2)}, u32[]{:S(2)}) %collective-permute-start.10) | collective-permute-done | bytes 131104 | tf_op jit(solution)/shard_map/ppermute | solution.py:39
  46.7 1.9 %collective-permute-done.11 = bf16[4,128,128]{1,2,0:T(8,128)(2,1)S(1)} collective-permute-done((bf16[4,128,128]{1,2,0:T(8,128)(2,1)S(1)}, bf16[4,128,128]{1,2,0:T(8,128)(2,1)S(1)}, u32[]{:S(2)}, u32[]{:S(2)}) %collective-permute-start.11) | collective-permute-done | bytes 131104 | tf_op jit(solution)/shard_map/ppermute | solution.py:39
  48.6 0.3 convolution_bitcast_fusion.15
  48.9 0.3 fusion.10
  49.2 0.3 constant_dynamic-update-slice_fusion.13
  49.5 1.1 %collective-permute-start.12 = (bf16[128,128]{0,1:T(8,128)(2,1)S(1)}, bf16[128,128]{0,1:T(8,128)(2,1)S(1)}, u32[]{:S(2)}, u32[]{:S(2)}) collective-permute-start(bf16[128,128]{0,1:T(8,128)(2,1)S(1)} %get-tuple-element.19), channel_id=1, source_target_pairs={{0,4},{1,5},{2,6},{3,7},{4,8},{5,9},{6,10},{7,11},{8,12},{9,13},{1... | collective-permute-start | bytes 98312 | tf_op jit(solution)/shard_map/ppermute | solution.py:25
  50.6 2.5 %collective-permute-start.13 = (bf16[128,128]{0,1:T(8,128)(2,1)S(1)}, bf16[128,128]{0,1:T(8,128)(2,1)S(1)}, u32[]{:S(2)}, u32[]{:S(2)}) collective-permute-start(bf16[128,128]{0,1:T(8,128)(2,1)S(1)} %get-tuple-element.19), channel_id=1, source_target_pairs={{0,8},{1,9},{2,10},{3,11},{4,12},{5,13},{6,14},{7,15},{8,0},{9,1},... | collective-permute-start | bytes 98312 | tf_op jit(solution)/shard_map/ppermute | solution.py:25
  53.1 1.1 %collective-permute-start.14 = (bf16[128,128]{0,1:T(8,128)(2,1)S(1)}, bf16[128,128]{0,1:T(8,128)(2,1)S(1)}, u32[]{:S(2)}, u32[]{:S(2)}) collective-permute-start(bf16[128,128]{0,1:T(8,128)(2,1)S(1)} %get-tuple-element.19), channel_id=1, source_target_pairs={{0,12},{1,13},{2,14},{3,15},{4,0},{5,1},{6,2},{7,3},{8,4},{9,5},{1... | collective-permute-start | bytes 98312 | tf_op jit(solution)/shard_map/ppermute | solution.py:25
  54.2 0.5 convolution_bitcast_fusion.13
  54.7 1.0 %collective-permute-done.12 = bf16[128,128]{0,1:T(8,128)(2,1)S(1)} collective-permute-done((bf16[128,128]{0,1:T(8,128)(2,1)S(1)}, bf16[128,128]{0,1:T(8,128)(2,1)S(1)}, u32[]{:S(2)}, u32[]{:S(2)}) %collective-permute-start.12) | collective-permute-done | bytes 32800 | tf_op jit(solution)/shard_map/ppermute | solution.py:25
  55.7 0.7 collective-permute-done.13
  56.3 0.7 %collective-permute-done.14 = bf16[128,128]{0,1:T(8,128)(2,1)S(1)} collective-permute-done((bf16[128,128]{0,1:T(8,128)(2,1)S(1)}, bf16[128,128]{0,1:T(8,128)(2,1)S(1)}, u32[]{:S(2)}, u32[]{:S(2)}) %collective-permute-start.14) | collective-permute-done | bytes 32800 | tf_op jit(solution)/shard_map/ppermute | solution.py:25
  57.1 1.6 %collective-permute-start.16 = (bf16[4,128,128]{1,2,0:T(8,128)(2,1)S(1)}, bf16[4,128,128]{1,2,0:T(8,128)(2,1)S(1)}, u32[]{:S(2)}, u32[]{:S(2)}) collective-permute-start(bf16[4,128,128]{1,2,0:T(8,128)(2,1)S(1)} %pad_maximum_fusion.6), channel_id=1, source_target_pairs={{0,2},{1,3},{2,0},{3,1},{4,6},{5,7},{6,4},{7,5},{8,10},{9,11},{10,... | collective-permute-start | bytes 393224 | tf_op jit(solution)/shard_map/ppermute | solution.py:39
  58.7 0.3 collective-permute-start.17
  59.1 4.4 %collective-permute-done.16 = bf16[4,128,128]{1,2,0:T(8,128)(2,1)S(1)} collective-permute-done((bf16[4,128,128]{1,2,0:T(8,128)(2,1)S(1)}, bf16[4,128,128]{1,2,0:T(8,128)(2,1)S(1)}, u32[]{:S(2)}, u32[]{:S(2)}) %collective-permute-start.16) | collective-permute-done | bytes 131104 | tf_op jit(solution)/shard_map/ppermute | solution.py:39
  63.5 1.9 %collective-permute-done.17 = bf16[4,128,128]{1,2,0:T(8,128)(2,1)S(1)} collective-permute-done((bf16[4,128,128]{1,2,0:T(8,128)(2,1)S(1)}, bf16[4,128,128]{1,2,0:T(8,128)(2,1)S(1)}, u32[]{:S(2)}, u32[]{:S(2)}) %collective-permute-start.17) | collective-permute-done | bytes 131104 | tf_op jit(solution)/shard_map/ppermute | solution.py:39
  65.4 0.3 convolution_bitcast_fusion.14
  65.8 0.3 fusion.5
  66.1 0.3 convolution_bitcast_fusion.12
  66.4 0.8 %copy.24 = f32[3,128,128]{2,1,0:T(8,128)} copy(f32[3,128,128]{1,2,0:T(8,128)S(1)} %pad_maximum_fusion.4) | data formatting | bytes 393216 | tf_op jit(solution)/shard_map/stack | solution.py:127
  (49 shorter events, 1.9 us)
Async XLA Ops:
  0.0 10.5 %copy-start = (bf16[1,16,2,128,128]{4,3,2,1,0:T(8,128)(2,1)S(1)}, bf16[1,16,2,128,128]{4,3,2,1,0:T(8,128)(2,1)}, u32[]{:S(2)}) copy-start(bf16[1,16,2,128,128]{4,3,2,1,0:T(8,128)(2,1)} %param.16) | copy-start | bytes 3145732
  0.0 12.6 %collective-permute-start = (bf16[4,128,128]{2,1,0:T(8,128)(2,1)}, bf16[4,128,128]{2,1,0:T(8,128)(2,1)S(1)}, u32[]{:S(2)}, u32[]{:S(2)}) collective-permute-start(bf16[4,128,128]{2,1,0:T(8,128)(2,1)} %param.19), channel_id=1, source_target_pairs={{0,4},{1,5},{2,6},{3,7},{4,8},{5,9},{6,10},{7,11},{8,12},{9,13},{1... | collective-permute-start | bytes 393224 | tf_op jit(solution)/shard_map/ppermute | solution.py:25
  3.0 11.4 %collective-permute-start.1 = (bf16[4,128,128]{2,1,0:T(8,128)(2,1)}, bf16[4,128,128]{2,1,0:T(8,128)(2,1)S(1)}, u32[]{:S(2)}, u32[]{:S(2)}) collective-permute-start(bf16[4,128,128]{2,1,0:T(8,128)(2,1)} %param.19), channel_id=1, source_target_pairs={{0,8},{1,9},{2,10},{3,11},{4,12},{5,13},{6,14},{7,15},{8,0},{9,1},... | collective-permute-start | bytes 393224 | tf_op jit(solution)/shard_map/ppermute | solution.py:25
  5.6 8.9 %collective-permute-start.2 = (bf16[4,128,128]{2,1,0:T(8,128)(2,1)}, bf16[4,128,128]{2,1,0:T(8,128)(2,1)S(1)}, u32[]{:S(2)}, u32[]{:S(2)}) collective-permute-start(bf16[4,128,128]{2,1,0:T(8,128)(2,1)} %param.19), channel_id=1, source_target_pairs={{0,12},{1,13},{2,14},{3,15},{4,0},{5,1},{6,2},{7,3},{8,4},{9,5},{1... | collective-permute-start | bytes 393224 | tf_op jit(solution)/shard_map/ppermute | solution.py:25
  12.3 2.1 %copy-start.2 = (bf16[4,128,128]{2,1,0:T(8,128)(2,1)S(1)}, bf16[4,128,128]{2,1,0:T(8,128)(2,1)}, u32[]{:S(2)}) copy-start(bf16[4,128,128]{2,1,0:T(8,128)(2,1)} %param.19) | copy-start | bytes 393220
  14.5 13.8 %collective-permute-start.4 = (bf16[4,4,128,128]{3,2,1,0:T(8,128)(2,1)S(1)}, bf16[4,4,128,128]{3,2,1,0:T(8,128)(2,1)S(1)}, u32[]{:S(2)}, u32[]{:S(2)}) collective-permute-start(bf16[4,4,128,128]{3,2,1,0:T(8,128)(2,1)S(1)} %pad_maximum_fusion.3), channel_id=1, source_target_pairs={{0,2},{1,3},{2,0},{3,1},{4,6},{5,7},{6,4},{7,5},{8,10},{9,11},{10,... | collective-permute-start | bytes 1572872 | tf_op jit(solution)/shard_map/ppermute | solution.py:33
  16.3 12.8 %collective-permute-start.3 = (bf16[4,4,128,128]{3,2,1,0:T(8,128)(2,1)S(1)}, bf16[4,4,128,128]{3,2,1,0:T(8,128)(2,1)S(1)}, u32[]{:S(2)}, u32[]{:S(2)}) collective-permute-start(bf16[4,4,128,128]{3,2,1,0:T(8,128)(2,1)S(1)} %pad_maximum_fusion.3), channel_id=1, source_target_pairs={{0,1},{1,0},{2,3},{3,2},{4,5},{5,4},{6,7},{7,6},{8,9},{9,8},{10,11... | collective-permute-start | bytes 1572872 | tf_op jit(solution)/shard_map/ppermute | solution.py:34
  28.4 2.0 %collective-permute-start.5 = (bf16[4,4,128,128]{3,2,1,0:T(8,128)(2,1)S(1)}, bf16[4,4,128,128]{3,2,1,0:T(8,128)(2,1)S(1)}, u32[]{:S(2)}, u32[]{:S(2)}) collective-permute-start(bf16[4,4,128,128]{3,2,1,0:T(8,128)(2,1)S(1)} %collective-permute-done.4), channel_id=1, source_target_pairs={{0,1},{1,0},{2,3},{3,2},{4,5},{5,4},{6,7},{7,6},{8,9},{9,8},{10,11... | collective-permute-start | bytes 1572872 | tf_op jit(solution)/shard_map/ppermute | solution.py:35
  30.0 0.9 %copy-start.3 = (f32[3,128,128]{2,1,0:T(8,128)S(1)}, f32[3,128,128]{2,1,0:T(8,128)}, u32[]{:S(2)}) copy-start(f32[3,128,128]{2,1,0:T(8,128)} %param.20) | copy-start | bytes 589828
  30.4 0.9 %copy-start.1 = (f32[1,128,128]{2,1,0:T(8,128)S(1)}, f32[1,128,128]{2,1,0:T(8,128)}, u32[]{:S(2)}) copy-start(f32[1,128,128]{2,1,0:T(8,128)} %param.21) | copy-start | bytes 196612
  31.6 6.1 %collective-permute-start.6 = (bf16[128,128]{0,1:T(8,128)(2,1)S(1)}, bf16[128,128]{0,1:T(8,128)(2,1)S(1)}, u32[]{:S(2)}, u32[]{:S(2)}) collective-permute-start(bf16[128,128]{0,1:T(8,128)(2,1)S(1)} %get-tuple-element.21), channel_id=1, source_target_pairs={{0,4},{1,5},{2,6},{3,7},{4,8},{5,9},{6,10},{7,11},{8,12},{9,13},{1... | collective-permute-start | bytes 98312 | tf_op jit(solution)/shard_map/ppermute | solution.py:25
  35.0 5.2 %collective-permute-start.7 = (bf16[128,128]{0,1:T(8,128)(2,1)S(1)}, bf16[128,128]{0,1:T(8,128)(2,1)S(1)}, u32[]{:S(2)}, u32[]{:S(2)}) collective-permute-start(bf16[128,128]{0,1:T(8,128)(2,1)S(1)} %get-tuple-element.21), channel_id=1, source_target_pairs={{0,8},{1,9},{2,10},{3,11},{4,12},{5,13},{6,14},{7,15},{8,0},{9,1},... | collective-permute-start | bytes 98312 | tf_op jit(solution)/shard_map/ppermute | solution.py:25
  35.6 4.6 %collective-permute-start.8 = (bf16[128,128]{0,1:T(8,128)(2,1)S(1)}, bf16[128,128]{0,1:T(8,128)(2,1)S(1)}, u32[]{:S(2)}, u32[]{:S(2)}) collective-permute-start(bf16[128,128]{0,1:T(8,128)(2,1)S(1)} %get-tuple-element.21), channel_id=1, source_target_pairs={{0,12},{1,13},{2,14},{3,15},{4,0},{5,1},{6,2},{7,3},{8,4},{9,5},{1... | collective-permute-start | bytes 98312 | tf_op jit(solution)/shard_map/ppermute | solution.py:25
  40.2 2.0 %collective-permute-start.9 = (bf16[4,128,128]{1,2,0:T(8,128)(2,1)S(1)}, bf16[4,128,128]{1,2,0:T(8,128)(2,1)S(1)}, u32[]{:S(2)}, u32[]{:S(2)}) collective-permute-start(bf16[4,128,128]{1,2,0:T(8,128)(2,1)S(1)} %pad_maximum_fusion.5), channel_id=1, source_target_pairs={{0,1},{1,0},{2,3},{3,2},{4,5},{5,4},{6,7},{7,6},{8,9},{9,8},{10,11... | collective-permute-start | bytes 393224 | tf_op jit(solution)/shard_map/ppermute | solution.py:39
  40.3 6.4 %collective-permute-start.10 = (bf16[4,128,128]{1,2,0:T(8,128)(2,1)S(1)}, bf16[4,128,128]{1,2,0:T(8,128)(2,1)S(1)}, u32[]{:S(2)}, u32[]{:S(2)}) collective-permute-start(bf16[4,128,128]{1,2,0:T(8,128)(2,1)S(1)} %pad_maximum_fusion.5), channel_id=1, source_target_pairs={{0,2},{1,3},{2,0},{3,1},{4,6},{5,7},{6,4},{7,5},{8,10},{9,11},{10,... | collective-permute-start | bytes 393224 | tf_op jit(solution)/shard_map/ppermute | solution.py:39
  41.9 6.7 %collective-permute-start.11 = (bf16[4,128,128]{1,2,0:T(8,128)(2,1)S(1)}, bf16[4,128,128]{1,2,0:T(8,128)(2,1)S(1)}, u32[]{:S(2)}, u32[]{:S(2)}) collective-permute-start(bf16[4,128,128]{1,2,0:T(8,128)(2,1)S(1)} %pad_maximum_fusion.5), channel_id=1, source_target_pairs={{0,3},{1,2},{2,1},{3,0},{4,7},{5,6},{6,5},{7,4},{8,11},{9,10},{10,... | collective-permute-start | bytes 393224 | tf_op jit(solution)/shard_map/ppermute | solution.py:39
  49.5 6.1 %collective-permute-start.12 = (bf16[128,128]{0,1:T(8,128)(2,1)S(1)}, bf16[128,128]{0,1:T(8,128)(2,1)S(1)}, u32[]{:S(2)}, u32[]{:S(2)}) collective-permute-start(bf16[128,128]{0,1:T(8,128)(2,1)S(1)} %get-tuple-element.19), channel_id=1, source_target_pairs={{0,4},{1,5},{2,6},{3,7},{4,8},{5,9},{6,10},{7,11},{8,12},{9,13},{1... | collective-permute-start | bytes 98312 | tf_op jit(solution)/shard_map/ppermute | solution.py:25
  50.6 5.7 %collective-permute-start.13 = (bf16[128,128]{0,1:T(8,128)(2,1)S(1)}, bf16[128,128]{0,1:T(8,128)(2,1)S(1)}, u32[]{:S(2)}, u32[]{:S(2)}) collective-permute-start(bf16[128,128]{0,1:T(8,128)(2,1)S(1)} %get-tuple-element.19), channel_id=1, source_target_pairs={{0,8},{1,9},{2,10},{3,11},{4,12},{5,13},{6,14},{7,15},{8,0},{9,1},... | collective-permute-start | bytes 98312 | tf_op jit(solution)/shard_map/ppermute | solution.py:25
  53.1 3.9 %collective-permute-start.14 = (bf16[128,128]{0,1:T(8,128)(2,1)S(1)}, bf16[128,128]{0,1:T(8,128)(2,1)S(1)}, u32[]{:S(2)}, u32[]{:S(2)}) collective-permute-start(bf16[128,128]{0,1:T(8,128)(2,1)S(1)} %get-tuple-element.19), channel_id=1, source_target_pairs={{0,12},{1,13},{2,14},{3,15},{4,0},{5,1},{6,2},{7,3},{8,4},{9,5},{1... | collective-permute-start | bytes 98312 | tf_op jit(solution)/shard_map/ppermute | solution.py:25
  57.1 2.0 %collective-permute-start.15 = (bf16[4,128,128]{1,2,0:T(8,128)(2,1)S(1)}, bf16[4,128,128]{1,2,0:T(8,128)(2,1)S(1)}, u32[]{:S(2)}, u32[]{:S(2)}) collective-permute-start(bf16[4,128,128]{1,2,0:T(8,128)(2,1)S(1)} %pad_maximum_fusion.6), channel_id=1, source_target_pairs={{0,1},{1,0},{2,3},{3,2},{4,5},{5,4},{6,7},{7,6},{8,9},{9,8},{10,11... | collective-permute-start | bytes 393224 | tf_op jit(solution)/shard_map/ppermute | solution.py:39
  57.1 6.4 %collective-permute-start.16 = (bf16[4,128,128]{1,2,0:T(8,128)(2,1)S(1)}, bf16[4,128,128]{1,2,0:T(8,128)(2,1)S(1)}, u32[]{:S(2)}, u32[]{:S(2)}) collective-permute-start(bf16[4,128,128]{1,2,0:T(8,128)(2,1)S(1)} %pad_maximum_fusion.6), channel_id=1, source_target_pairs={{0,2},{1,3},{2,0},{3,1},{4,6},{5,7},{6,4},{7,5},{8,10},{9,11},{10,... | collective-permute-start | bytes 393224 | tf_op jit(solution)/shard_map/ppermute | solution.py:39
  58.7 6.7 %collective-permute-start.17 = (bf16[4,128,128]{1,2,0:T(8,128)(2,1)S(1)}, bf16[4,128,128]{1,2,0:T(8,128)(2,1)S(1)}, u32[]{:S(2)}, u32[]{:S(2)}) collective-permute-start(bf16[4,128,128]{1,2,0:T(8,128)(2,1)S(1)} %pad_maximum_fusion.6), channel_id=1, source_target_pairs={{0,3},{1,2},{2,1},{3,0},{4,7},{5,6},{6,5},{7,4},{8,11},{9,10},{10,... | collective-permute-start | bytes 393224 | tf_op jit(solution)/shard_map/ppermute | solution.py:39

commit v6 on v5

--- a/solution.py
+++ b/solution.py
@@ -17,43 +17,48 @@
 def line_stage(x, wide, inner):
     lines = wide // inner
     if lines <= 4:
-        parts = [x]
+        parts = [x[None]]
         for shift in range(1, lines):
             pairs = [
                 (d, ((d // inner + shift) % lines) * inner + d % inner) for d in range(wide)
             ]
-            parts.append(lax.ppermute(x, "wide", pairs))
-        return jnp.stack(parts), True
+            parts.append(lax.ppermute(x, "wide", pairs)[None])
+        return parts, True
     groups = [[z * inner + k for z in range(lines)] for k in range(inner)]
-    return lax.all_gather(x, "wide", axis=0, tiled=False, axis_index_groups=groups), False
+    return [lax.all_gather(x, "wide", axis=0, tiled=False, axis_index_groups=groups)], False
 
 
-def slab_stage(stack, wide, inner, doubling):
-    if doubling and inner == 4:
-        across = lax.ppermute(stack, "wide", [(d, d ^ 2) for d in range(wide)])
-        beside = lax.ppermute(stack, "wide", [(d, d ^ 1) for d in range(wide)])
-        diagonal = lax.ppermute(across, "wide", [(d, d ^ 1) for d in range(wide)])
-        return [stack, beside, across, diagonal]
-    parts = [stack]
-    for m in range(1, inner):
-        parts.append(lax.ppermute(stack, "wide", [(d, d ^ m) for d in range(wide)]))
-    return parts
+def swap(x, wide, mask):
+    return lax.ppermute(x, "wide", [(d, d ^ mask) for d in range(wide)])
 
 
-def gather_blocks(x, wide, doubling):
+def gather_blocks(x, wide, early):
     inner = inner_size(wide)
     lines = wide // inner
-    stack, shifted = line_stage(x, wide, inner)
-    pieces = slab_stage(stack, wide, inner, doubling)
+    parts, shifted = line_stage(x, wide, inner)
+    own = parts[0] if len(parts) == 1 else jnp.concatenate(parts)
+    every = list(range(lines))
+    pieces = [(own, 0, every)]
+    if early and inner == 4 and len(parts) > 1:
+        rest = jnp.concatenate(parts[1:])
+        across_own = swap(parts[0], wide, 2)
+        across_rest = swap(rest, wide, 2)
+        pieces += [
+            (swap(own, wide, 1), 1, every),
+            (across_own, 2, every[:1]),
+            (across_rest, 2, every[1:]),
+            (swap(across_own, wide, 1), 3, every[:1]),
+            (swap(across_rest, wide, 1), 3, every[1:]),
+        ]
+    else:
+        pieces += [(swap(own, wide, m), m, every) for m in range(1, inner)]
     me = lax.axis_index("wide")
     line = np.arange(lines, dtype=np.int32)
     source_line = (me // inner - line) % lines if shifted else jnp.asarray(line)
-    masks = np.arange(inner, dtype=np.int32)
-    blocks = (
-        source_line[None, :] * inner
-        + jnp.bitwise_xor(me % inner, jnp.asarray(masks))[:, None]
+    blocks = jnp.concatenate(
+        [source_line[np.array(held)] * inner + jnp.bitwise_xor(me % inner, m) for _, m, held in pieces]
     )
-    return pieces, blocks.reshape(wide)
+    return [piece for piece, _, _ in pieces], blocks
 
 
 def tiles_by_lag(retarded_tiles, tile_lags, column_of_block, block_of_slot, lags_wanted):
@@ -85,7 +90,7 @@
     column_of_block = jnp.argsort(block_owner)
 
     later, later_blocks = gather_blocks(later_current, wide, True)
-    lines = later[0].shape[0]
+    offsets = np.cumsum([0] + [piece.shape[0] for piece in later])
     by_lag = tiles_by_lag(
         retarded_tiles, tile_lags, column_of_block, later_blocks, range(1, lag_count + 1)
     )
@@ -105,7 +110,7 @@
         retarded = None
         for m, piece in enumerate(later):
             term = rowwise(
-                by_lag[m * lines : (m + 1) * lines, first - 1 :],
+                by_lag[offsets[m] : offsets[m + 1], first - 1 :],
                 piece[:, moment + first - step_count : moment + lag_count + 1 - step_count],
             )
             retarded = term if retarded is None else retarded + term

time: 67.3 us -> 78.1 us (1.16)
  other arithmetic: 3.07 us -> 11.5 us
  local copies, waits for them, and re-layouts: 4.34 us -> 12.3 us
  waiting for transfers between devices: 30.7 us -> 25.2 us
  starting transfers between devices: 23 us -> 21.4 us
  matrix products: 5.8 us -> 6.84 us
    ppermute x18 -> x20, waiting for transfers between devices: 30.7 us -> 25.2 us  [the longest x11 20 us: swap(): return lax.ppermute(x, 'wide', [(d, d ^ mask) for d in range(wide)])]
    another operation x3 -> x4, other arithmetic: 0.11 us -> 3.21 us  [tiles_by_lag(): jnp.stack([jnp.where((lags[:, 0] == lag)[:, None, None], tiles[:, 0], jnp...]
    concatenate x0 -> x4, other arithmetic: none -> 1.96 us  [the longest x3 1.01 us: gather_blocks(): own = parts[0] if len(parts) == 1 else jnp.concatenate(parts)]
    gather x1 -> x2, local copies, waits for them, and re-layouts: 0.75 us -> 2.4 us  [tiles_by_lag(): tiles = jnp.take(retarded_tiles[0], columns, axis=0)]
    ppermute x18 -> x20, starting transfers between devices: 23 us -> 21.4 us  [the longest x9 14.8 us: line_stage(): parts.append(lax.ppermute(x, 'wide', pairs)[None])]
    unnamed x18 -> x44, local copies, waits for them, and re-layouts: 0.68 us -> 2.06 us
    gather x0 -> x2, local copies, waits for them, and re-layouts: none -> 1.28 us  [gather_blocks(): source_line[np.array(held)] * inner + jnp.bitwise_xor(me % inner, m)]
    slice x0 -> x2, local copies, waits for them, and re-layouts: none -> 1.24 us  [per_device(): by_lag[offsets[m]:offsets[m + 1], first - 1:]]
  transfers between devices with their start and end apart: 18 -> 20, of which waited for: 10 -> 10; matrix products, arithmetic and copies ran while one was open for 14% -> 33% of each run, Pallas kernels for 0% -> 0%
where the time goes in v6:
time: 78.1 us; the launch traced here: 77.8 us
  waiting for transfers between devices  25.2 us (32%)
  starting transfers between devices  21.4 us (27%)
  local copies, waits for them, and re-layouts  12.3 us (16%)
  other arithmetic  11.5 us (15%)
  matrix products  6.84 us (9%)
    ppermute x11, waiting for transfers between devices, swap(): return lax.ppermute(x, 'wide', [(d, d ^ mask) for d in range(wide)])  20 us
    ppermute x9, starting transfers between devices, line_stage(): parts.append(lax.ppermute(x, 'wide', pairs)[None])  14.8 us
    ppermute x11, starting transfers between devices, swap(): return lax.ppermute(x, 'wide', [(d, d ^ mask) for d in range(wide)])  6.53 us
    dot_general x21, matrix products, rowwise(): return jnp.einsum(spec, tiles, currents, preferred_element_type=jnp.float32)  5.99 us
    ppermute x9, waiting for transfers between devices, line_stage(): parts.append(lax.ppermute(x, 'wide', pairs)[None])  5.18 us
    another operation x4, other arithmetic, tiles_by_lag(): jnp.stack([jnp.where((lags[:, 0] == lag)[:, None, None], tiles[:, 0], jnp...  3.21 us
    gather x2, local copies, waits for them, and re-layouts, tiles_by_lag(): tiles = jnp.take(retarded_tiles[0], columns, axis=0)  2.4 us
    unnamed x44, local copies, waits for them, and re-layouts  2.06 us
  transfers between devices with their start and end apart: 20, of which 10 were waited for; matrix products, arithmetic and copies ran while one was open for 33% of the time, Pallas kernels for 0%

profile of v6, /device:TPU:0, one launch (start us, length us, event | category | flops | bytes accessed | tf_op | source)
XLA Modules:
  0.0 77.8 jit_solution(8789209725782095931)
XLA Ops:
  0.0 3.0 %collective-permute-start = (bf16[4,128,128]{2,1,0:T(8,128)(2,1)}, bf16[4,128,128]{2,1,0:T(8,128)(2,1)S(1)}, u32[]{:S(2)}, u32[]{:S(2)}) collective-permute-start(bf16[4,128,128]{2,1,0:T(8,128)(2,1)} %param.37), channel_id=1, source_target_pairs={{0,4},{1,5},{2,6},{3,7},{4,8},{5,9},{6,10},{7,11},{8,12},{9,13},{1... | collective-permute-start | bytes 393224 | tf_op jit(solution)/shard_map/ppermute | solution.py:25
  3.0 2.6 %collective-permute-start.1 = (bf16[4,128,128]{2,1,0:T(8,128)(2,1)}, bf16[4,128,128]{2,1,0:T(8,128)(2,1)S(1)}, u32[]{:S(2)}, u32[]{:S(2)}) collective-permute-start(bf16[4,128,128]{2,1,0:T(8,128)(2,1)} %param.37), channel_id=1, source_target_pairs={{0,8},{1,9},{2,10},{3,11},{4,12},{5,13},{6,14},{7,15},{8,0},{9,1},... | collective-permute-start | bytes 393224 | tf_op jit(solution)/shard_map/ppermute | solution.py:25
  5.6 1.3 %collective-permute-start.2 = (bf16[4,128,128]{2,1,0:T(8,128)(2,1)}, bf16[4,128,128]{2,1,0:T(8,128)(2,1)}, u32[]{:S(2)}, u32[]{:S(2)}) collective-permute-start(bf16[4,128,128]{2,1,0:T(8,128)(2,1)} %param.37), channel_id=1, source_target_pairs={{0,12},{1,13},{2,14},{3,15},{4,0},{5,1},{6,2},{7,3},{8,4},{9,5},{1... | collective-permute-start | bytes 393224 | tf_op jit(solution)/shard_map/ppermute | solution.py:25
  7.0 1.5 %collective-permute-start.4 = (bf16[1,4,128,128]{3,2,1,0:T(8,128)(2,1)}, bf16[1,4,128,128]{3,2,1,0:T(8,128)(2,1)S(1)}, u32[]{:S(2)}, u32[]{:S(2)}) collective-permute-start(bf16[1,4,128,128]{3,2,1,0:T(8,128)(2,1)} %bitcast.239), channel_id=1, source_target_pairs={{0,2},{1,3},{2,0},{3,1},{4,6},{5,7},{6,4},{7,5},{8,10},{9,11},{10,... | collective-permute-start | bytes 393224 | tf_op jit(solution)/shard_map/ppermute | solution.py:32
  8.5 0.7 pad_clamp_fusion.4
  9.2 0.6 gather_fusion
  9.8 0.6 gather_fusion.1
  10.5 0.6 broadcast_add_fusion.1
  11.2 1.9 %sort.17 = (s32[16]{0:T(128)}, s32[16]{0:T(128)S(1)}) sort(s32[16]{0:T(128)} %param.36, s32[16]{0:T(128)S(1)} %iota.5), dimensions={0}, to_apply=%region_0.0 | sort | flops 64 | bytes 256 | tf_op jit(solution)/shard_map/jit(argsort)/sort | solution.py:90
  13.1 0.7 gather_fusion.2
  13.8 0.8 copy.33
  14.6 0.7 gather_fusion.4
  15.3 0.6 gather_fusion.3
  16.7 0.8 %fusion.48 = (bf16[3,2,128,128]{3,2,1,0:T(8,128)(2,1)}, bf16[3,2,128,128]{3,2,1,0:T(8,128)(2,1)}) fusion(bf16[16,1,128,128]{3,2,1,0:T(8,128)(2,1)S(1)} %get-tuple-element.55, bf16[16,1,128,128]{3,2,1,0:T(8,128)(2,1)S(1)} %get-tuple-element.56), kind=kLoop, calls=%fused_computation.105 | loop fusion | flops 196608 | bytes 1441792 | tf_op jit(solution)/shard_map/stack | solution.py:69
  17.5 0.9 %fusion.42 = (bf16[4,2,128,128]{3,2,1,0:T(8,128)(2,1)}, bf16[4,2,128,128]{3,2,1,0:T(8,128)(2,1)}) fusion(bf16[16,1,128,128]{3,2,1,0:T(8,128)(2,1)S(1)} %get-tuple-element.55, bf16[16,1,128,128]{3,2,1,0:T(8,128)(2,1)S(1)} %get-tuple-element.56), kind=kLoop, calls=%fused_computation.99 | loop fusion | flops 262144 | bytes 1572864 | tf_op jit(solution)/shard_map/stack | solution.py:69
  18.3 1.3 %pad_maximum_fusion.1 = bf16[16,3,128,128]{3,2,1,0:T(8,128)(2,1)} fusion(bf16[16,1,128,128]{3,2,1,0:T(8,128)(2,1)S(1)} %get-tuple-element.56, bf16[16,1,128,128]{3,2,1,0:T(8,128)(2,1)S(1)} %get-tuple-element.55, bf16[16,1,128,128]{3,2,1,0:T(8,128)(2,1)S(1)} %get-tuple-element.54), kind=kLoop, calls=%fused_computation.19 | loop fusion | flops 1572864 | bytes 3145728 | tf_op jit(solution)/shard_map/stack | solution.py:69
  19.6 0.9 %pad_maximum_fusion.7 = (bf16[3,3,128,128]{3,2,1,0:T(8,128)(2,1)}, bf16[3,3,128,128]{3,2,1,0:T(8,128)(2,1)}) fusion(bf16[16,1,128,128]{3,2,1,0:T(8,128)(2,1)S(1)} %get-tuple-element.56, bf16[16,1,128,128]{3,2,1,0:T(8,128)(2,1)S(1)} %get-tuple-element.55, bf16[16,1,128,128]{3,2,1,0:T(8,128)(2,1)S(1)} %get-tuple-element.54), kind=kLoop, calls=%fused_computation.93 | loop fusion | flops 589824 | bytes 2162688 | tf_op jit(solution)/shard_map/slice | solution.py:113
  20.6 0.5 copy-done.14
  21.1 1.2 %gather_fusion.5 = s32[16]{0:T(128)} fusion(s32[16]{0:T(128)S(1)} %get-tuple-element.8, s32[1024]{0:T(1024)S(1)} %pad_clamp_fusion.1), kind=kCustom, calls=%fused_computation.3.clone | custom fusion | bytes 192 | tf_op jit(solution)/shard_map/jit(_take)/gather | solution.py:65
  22.3 0.7 compare_and_fusion
  23.0 1.6 %gather_fusion.7 = bf16[16,2,128,128]{3,2,1,0:T(8,128)(2,1)} fusion(bf16[16,2,128,128]{3,2,1,0:T(8,128)(2,1)S(1)} %bitcast.225, s32[1024]{0:T(1024)S(1)} %pad_clamp_fusion), kind=kCustom, calls=%fused_computation.5.clone | custom fusion | bytes 2097216 | tf_op jit(solution)/shard_map/jit(_take)/gather | solution.py:66
  24.7 1.1 %gather_fusion.6 = s32[16,2]{1,0:T(8,128)} fusion(s32[16,2]{1,0:T(8,128)S(1)} %copy.33, s32[1024]{0:T(1024)S(1)} %pad_clamp_fusion), kind=kCustom, calls=%fused_computation.4.clone | custom fusion | bytes 320 | tf_op jit(solution)/shard_map/jit(_take)/gather | solution.py:67
  25.8 1.2 %fusion.95 = (bf16[4,3,128,128]{3,2,1,0:T(8,128)(2,1)S(1)}, bf16[4,3,128,128]{3,2,1,0:T(8,128)(2,1)S(1)}) fusion(bf16[16,3,128,128]{3,2,1,0:T(8,128)(2,1)} %pad_maximum_fusion.1), kind=kLoop, calls=%fused_computation.216 | loop fusion | bytes 1572864 | tf_op jit(solution)/shard_map/slice | solution.py:113
  27.4 1.1 %copy-done.1 = bf16[16,2,128,128]{3,2,1,0:T(8,128)(2,1)S(1)} copy-done((bf16[16,2,128,128]{3,2,1,0:T(8,128)(2,1)S(1)}, bf16[16,2,128,128]{3,2,1,0:T(8,128)(2,1)}, u32[]{:S(2)}) %copy-start.1) | copy-done | bytes 1048600
  29.3 0.9 %pad_maximum_fusion.5 = bf16[3,4,128,128]{3,2,1,0:T(8,128)(2,1)S(1)} fusion(bf16[1,4,128,128]{3,2,1,0:T(8,128)(2,1)} %bitcast.8, bf16[1,4,128,128]{3,2,1,0:T(8,128)(2,1)S(1)} %bitcast.229, bf16[1,4,128,128]{3,2,1,0:T(8,128)(2,1)S(1)} %bitcast.227), kind=kLoop, calls=%fused_computation.83 | loop fusion | flops 393216 | bytes 786432 | tf_op jit(solution)/shard_map/concatenate | solution.py:43
  30.2 1.0 %pad_maximum_fusion.2 = bf16[4,4,128,128]{3,2,1,0:T(8,128)(2,1)S(1)} fusion(bf16[1,4,128,128]{3,2,1,0:T(8,128)(2,1)} %bitcast.8, bf16[1,4,128,128]{3,2,1,0:T(8,128)(2,1)S(1)} %bitcast.230, bf16[1,4,128,128]{3,2,1,0:T(8,128)(2,1)S(1)} %bitcast.228, bf16[1,4,128,128]{3,2,1,0:T(8,128)(2,1)S(1)} %bitcast.240), kind=kLoop, calls=%fused_computation.67 | loop fusion | flops 786432 | bytes 1048576 | tf_op jit(solution)/shard_map/concatenate | solution.py:39
  31.2 0.6 collective-permute-start.5
  32.3 0.6 collective-permute-start.6
  33.6 7.4 %collective-permute-done.5 = bf16[3,4,128,128]{3,2,1,0:T(8,128)(2,1)S(1)} collective-permute-done((bf16[3,4,128,128]{3,2,1,0:T(8,128)(2,1)S(1)}, bf16[3,4,128,128]{3,2,1,0:T(8,128)(2,1)S(1)}, u32[]{:S(2)}, u32[]{:S(2)}) %collective-permute-start.5) | collective-permute-done | bytes 393248 | tf_op jit(solution)/shard_map/ppermute | solution.py:32
  44.4 0.7 collective-permute-start.8
  45.5 2.8 %collective-permute-start.10 = (bf16[128,128]{0,1:T(8,128)(2,1)S(1)}, bf16[128,128]{0,1:T(8,128)(2,1)S(1)}, u32[]{:S(2)}, u32[]{:S(2)}) collective-permute-start(bf16[128,128]{0,1:T(8,128)(2,1)S(1)} %get-tuple-element.36), channel_id=1, source_target_pairs={{0,12},{1,13},{2,14},{3,15},{4,0},{5,1},{6,2},{7,3},{8,4},{9,5},{1... | collective-permute-start | bytes 98312 | tf_op jit(solution)/shard_map/ppermute | solution.py:25
  48.8 1.6 %collective-permute-done.8 = bf16[128,128]{0,1:T(8,128)(2,1)S(1)} collective-permute-done((bf16[128,128]{0,1:T(8,128)(2,1)S(1)}, bf16[128,128]{0,1:T(8,128)(2,1)S(1)}, u32[]{:S(2)}, u32[]{:S(2)}) %collective-permute-start.8) | collective-permute-done | bytes 32800 | tf_op jit(solution)/shard_map/ppermute | solution.py:25
  50.5 0.7 collective-permute-done.9
  51.3 0.6 collective-permute-start.12
  51.9 1.3 %collective-permute-start.13 = (bf16[4,128,128]{1,2,0:T(8,128)(2,1)S(1)}, bf16[4,128,128]{1,2,0:T(8,128)(2,1)S(1)}, u32[]{:S(2)}, u32[]{:S(2)}) collective-permute-start(bf16[4,128,128]{1,2,0:T(8,128)(2,1)S(1)} %pad_maximum_fusion.10), channel_id=1, source_target_pairs={{0,3},{1,2},{2,1},{3,0},{4,7},{5,6},{6,5},{7,4},{8,11},{9,10},{10,... | collective-permute-start | bytes 393224 | tf_op jit(solution)/shard_map/ppermute | solution.py:32
  53.3 4.4 %collective-permute-done.12 = bf16[4,128,128]{1,2,0:T(8,128)(2,1)S(1)} collective-permute-done((bf16[4,128,128]{1,2,0:T(8,128)(2,1)S(1)}, bf16[4,128,128]{1,2,0:T(8,128)(2,1)S(1)}, u32[]{:S(2)}, u32[]{:S(2)}) %collective-permute-start.12) | collective-permute-done | bytes 131104 | tf_op jit(solution)/shard_map/ppermute | solution.py:32
  57.7 1.9 %collective-permute-done.13 = bf16[4,128,128]{1,2,0:T(8,128)(2,1)S(1)} collective-permute-done((bf16[4,128,128]{1,2,0:T(8,128)(2,1)S(1)}, bf16[4,128,128]{1,2,0:T(8,128)(2,1)S(1)}, u32[]{:S(2)}, u32[]{:S(2)}) %collective-permute-start.13) | collective-permute-done | bytes 131104 | tf_op jit(solution)/shard_map/ppermute | solution.py:32
  60.5 1.6 %collective-permute-start.14 = (bf16[128,128]{0,1:T(8,128)(2,1)S(1)}, bf16[128,128]{0,1:T(8,128)(2,1)S(1)}, u32[]{:S(2)}, u32[]{:S(2)}) collective-permute-start(bf16[128,128]{0,1:T(8,128)(2,1)S(1)} %get-tuple-element.34), channel_id=1, source_target_pairs={{0,4},{1,5},{2,6},{3,7},{4,8},{5,9},{6,10},{7,11},{8,12},{9,13},{1... | collective-permute-start | bytes 98312 | tf_op jit(solution)/shard_map/ppermute | solution.py:25
  62.0 1.8 %collective-permute-start.15 = (bf16[128,128]{0,1:T(8,128)(2,1)S(1)}, bf16[128,128]{0,1:T(8,128)(2,1)S(1)}, u32[]{:S(2)}, u32[]{:S(2)}) collective-permute-start(bf16[128,128]{0,1:T(8,128)(2,1)S(1)} %get-tuple-element.34), channel_id=1, source_target_pairs={{0,8},{1,9},{2,10},{3,11},{4,12},{5,13},{6,14},{7,15},{8,0},{9,1},... | collective-permute-start | bytes 98312 | tf_op jit(solution)/shard_map/ppermute | solution.py:25
  63.8 0.6 collective-permute-start.16
  64.5 0.5 convolution_bitcast_fusion.1
  65.0 1.4 %collective-permute-done.14 = bf16[128,128]{0,1:T(8,128)(2,1)S(1)} collective-permute-done((bf16[128,128]{0,1:T(8,128)(2,1)S(1)}, bf16[128,128]{0,1:T(8,128)(2,1)S(1)}, u32[]{:S(2)}, u32[]{:S(2)}) %collective-permute-start.14) | collective-permute-done | bytes 32800 | tf_op jit(solution)/shard_map/ppermute | solution.py:25
  66.3 1.0 %collective-permute-done.15 = bf16[128,128]{0,1:T(8,128)(2,1)S(1)} collective-permute-done((bf16[128,128]{0,1:T(8,128)(2,1)S(1)}, bf16[128,128]{0,1:T(8,128)(2,1)S(1)}, u32[]{:S(2)}, u32[]{:S(2)}) %collective-permute-start.15) | collective-permute-done | bytes 32800 | tf_op jit(solution)/shard_map/ppermute | solution.py:25
  67.9 0.6 collective-permute-start.18
  68.4 1.3 %collective-permute-start.19 = (bf16[4,128,128]{1,2,0:T(8,128)(2,1)S(1)}, bf16[4,128,128]{1,2,0:T(8,128)(2,1)S(1)}, u32[]{:S(2)}, u32[]{:S(2)}) collective-permute-start(bf16[4,128,128]{1,2,0:T(8,128)(2,1)S(1)} %pad_maximum_fusion.11), channel_id=1, source_target_pairs={{0,3},{1,2},{2,1},{3,0},{4,7},{5,6},{6,5},{7,4},{8,11},{9,10},{10,... | collective-permute-start | bytes 393224 | tf_op jit(solution)/shard_map/ppermute | solution.py:32
  69.8 4.4 %collective-permute-done.18 = bf16[4,128,128]{1,2,0:T(8,128)(2,1)S(1)} collective-permute-done((bf16[4,128,128]{1,2,0:T(8,128)(2,1)S(1)}, bf16[4,128,128]{1,2,0:T(8,128)(2,1)S(1)}, u32[]{:S(2)}, u32[]{:S(2)}) %collective-permute-start.18) | collective-permute-done | bytes 131104 | tf_op jit(solution)/shard_map/ppermute | solution.py:32
  74.2 1.9 %collective-permute-done.19 = bf16[4,128,128]{1,2,0:T(8,128)(2,1)S(1)} collective-permute-done((bf16[4,128,128]{1,2,0:T(8,128)(2,1)S(1)}, bf16[4,128,128]{1,2,0:T(8,128)(2,1)S(1)}, u32[]{:S(2)}, u32[]{:S(2)}) %collective-permute-start.19) | collective-permute-done | bytes 131104 | tf_op jit(solution)/shard_map/ppermute | solution.py:32
  77.0 0.8 %copy.36 = f32[3,128,128]{2,1,0:T(8,128)} copy(f32[3,128,128]{1,2,0:T(8,128)S(1)} %pad_maximum_fusion.9) | data formatting | bytes 393216 | tf_op jit(solution)/shard_map/stack | solution.py:132
  (109 shorter events, 9.8 us)
Async XLA Ops:
  0.0 14.6 %copy-start = (bf16[1,16,2,128,128]{4,3,2,1,0:T(8,128)(2,1)S(1)}, bf16[1,16,2,128,128]{4,3,2,1,0:T(8,128)(2,1)}, u32[]{:S(2)}) copy-start(bf16[1,16,2,128,128]{4,3,2,1,0:T(8,128)(2,1)} %param.34) | copy-start | bytes 3145732
  0.0 29.2 %collective-permute-start = (bf16[4,128,128]{2,1,0:T(8,128)(2,1)}, bf16[4,128,128]{2,1,0:T(8,128)(2,1)S(1)}, u32[]{:S(2)}, u32[]{:S(2)}) collective-permute-start(bf16[4,128,128]{2,1,0:T(8,128)(2,1)} %param.37), channel_id=1, source_target_pairs={{0,4},{1,5},{2,6},{3,7},{4,8},{5,9},{6,10},{7,11},{8,12},{9,13},{1... | collective-permute-start | bytes 393224 | tf_op jit(solution)/shard_map/ppermute | solution.py:25
  3.0 26.2 %collective-permute-start.1 = (bf16[4,128,128]{2,1,0:T(8,128)(2,1)}, bf16[4,128,128]{2,1,0:T(8,128)(2,1)S(1)}, u32[]{:S(2)}, u32[]{:S(2)}) collective-permute-start(bf16[4,128,128]{2,1,0:T(8,128)(2,1)} %param.37), channel_id=1, source_target_pairs={{0,8},{1,9},{2,10},{3,11},{4,12},{5,13},{6,14},{7,15},{8,0},{9,1},... | collective-permute-start | bytes 393224 | tf_op jit(solution)/shard_map/ppermute | solution.py:25
  5.6 23.7 %collective-permute-start.2 = (bf16[4,128,128]{2,1,0:T(8,128)(2,1)}, bf16[4,128,128]{2,1,0:T(8,128)(2,1)}, u32[]{:S(2)}, u32[]{:S(2)}) collective-permute-start(bf16[4,128,128]{2,1,0:T(8,128)(2,1)} %param.37), channel_id=1, source_target_pairs={{0,12},{1,13},{2,14},{3,15},{4,0},{5,1},{6,2},{7,3},{8,4},{9,5},{1... | collective-permute-start | bytes 393224 | tf_op jit(solution)/shard_map/ppermute | solution.py:25
  7.0 25.1 %collective-permute-start.4 = (bf16[1,4,128,128]{3,2,1,0:T(8,128)(2,1)}, bf16[1,4,128,128]{3,2,1,0:T(8,128)(2,1)S(1)}, u32[]{:S(2)}, u32[]{:S(2)}) collective-permute-start(bf16[1,4,128,128]{3,2,1,0:T(8,128)(2,1)} %bitcast.239), channel_id=1, source_target_pairs={{0,2},{1,3},{2,0},{3,1},{4,6},{5,7},{6,4},{7,5},{8,10},{9,11},{10,... | collective-permute-start | bytes 393224 | tf_op jit(solution)/shard_map/ppermute | solution.py:32
  11.1 3.5 %copy-start.12 = (s32[4]{0:T(128)}, s32[4]{0:T(128)S(1)}, u32[]{:S(2)}) copy-start(s32[4]{0:T(128)S(1)} %get-tuple-element.60) | copy-start | bytes 52
  18.3 2.2 %copy-start.13 = (s32[4]{0:T(128)S(1)}, s32[4]{0:T(128)}, u32[]{:S(2)}) copy-start(s32[4]{0:T(128)} %copy-done.12) | copy-start | bytes 52
  18.3 2.2 %copy-start.15 = (s32[4]{0:T(128)S(1)}, s32[4]{0:T(128)}, u32[]{:S(2)}) copy-start(s32[4]{0:T(128)} %get-tuple-element.57) | copy-start | bytes 52
  18.3 2.2 %copy-start.16 = (s32[4]{0:T(128)S(1)}, s32[4]{0:T(128)}, u32[]{:S(2)}) copy-start(s32[4]{0:T(128)} %get-tuple-element.59) | copy-start | bytes 52
  20.6 0.5 copy-start.14
  27.3 1.2 %copy-start.1 = (bf16[16,2,128,128]{3,2,1,0:T(8,128)(2,1)S(1)}, bf16[16,2,128,128]{3,2,1,0:T(8,128)(2,1)}, u32[]{:S(2)}) copy-start(bf16[16,2,128,128]{3,2,1,0:T(8,128)(2,1)} %gather_fusion.7) | copy-start | bytes 3145732
  27.3 1.4 %copy-start.11 = (s32[16,2]{1,0:T(8,128)S(1)}, s32[16,2]{1,0:T(8,128)}, u32[]{:S(2)}) copy-start(s32[16,2]{1,0:T(8,128)} %gather_fusion.6) | copy-start | bytes 388
  29.1 1.1 %copy-start.10 = (bf16[4,128,128]{2,1,0:T(8,128)(2,1)S(1)}, bf16[4,128,128]{2,1,0:T(8,128)(2,1)}, u32[]{:S(2)}) copy-start(bf16[4,128,128]{2,1,0:T(8,128)(2,1)} %param.37) | copy-start | bytes 393220
  29.1 2.7 %copy-start.6 = (bf16[4,2,128,128]{3,2,1,0:T(8,128)(2,1)S(1)}, bf16[4,2,128,128]{3,2,1,0:T(8,128)(2,1)}, u32[]{:S(2)}) copy-start(bf16[4,2,128,128]{3,2,1,0:T(8,128)(2,1)} %get-tuple-element.50) | copy-start | bytes 786436
  31.2 9.8 %collective-permute-start.5 = (bf16[3,4,128,128]{3,2,1,0:T(8,128)(2,1)S(1)}, bf16[3,4,128,128]{3,2,1,0:T(8,128)(2,1)S(1)}, u32[]{:S(2)}, u32[]{:S(2)}) collective-permute-start(bf16[3,4,128,128]{3,2,1,0:T(8,128)(2,1)S(1)} %pad_maximum_fusion.5), channel_id=1, source_target_pairs={{0,2},{1,3},{2,0},{3,1},{4,6},{5,7},{6,4},{7,5},{8,10},{9,11},{10,... | collective-permute-start | bytes 1179656 | tf_op jit(solution)/shard_map/ppermute | solution.py:32
  31.8 10.1 %collective-permute-start.3 = (bf16[4,4,128,128]{3,2,1,0:T(8,128)(2,1)S(1)}, bf16[4,4,128,128]{3,2,1,0:T(8,128)(2,1)S(1)}, u32[]{:S(2)}, u32[]{:S(2)}) collective-permute-start(bf16[4,4,128,128]{3,2,1,0:T(8,128)(2,1)S(1)} %pad_maximum_fusion.2), channel_id=1, source_target_pairs={{0,1},{1,0},{2,3},{3,2},{4,5},{5,4},{6,7},{7,6},{8,9},{9,8},{10,11... | collective-permute-start | bytes 1572872 | tf_op jit(solution)/shard_map/ppermute | solution.py:32
  32.3 8.7 %copy-start.9 = (bf16[3,2,128,128]{3,2,1,0:T(8,128)(2,1)S(1)}, bf16[3,2,128,128]{3,2,1,0:T(8,128)(2,1)}, u32[]{:S(2)}) copy-start(bf16[3,2,128,128]{3,2,1,0:T(8,128)(2,1)} %get-tuple-element.51) | copy-start | bytes 589828
  32.3 9.0 %copy-start.4 = (bf16[3,3,128,128]{3,2,1,0:T(8,128)(2,1)S(1)}, bf16[3,3,128,128]{3,2,1,0:T(8,128)(2,1)}, u32[]{:S(2)}) copy-start(bf16[3,3,128,128]{3,2,1,0:T(8,128)(2,1)} %get-tuple-element.47) | copy-start | bytes 884740
  32.3 11.2 %collective-permute-start.6 = (bf16[1,4,128,128]{3,2,1,0:T(8,128)(2,1)S(1)}, bf16[1,4,128,128]{3,2,1,0:T(8,128)(2,1)S(1)}, u32[]{:S(2)}, u32[]{:S(2)}) collective-permute-start(bf16[1,4,128,128]{3,2,1,0:T(8,128)(2,1)S(1)} %collective-permute-done.4), channel_id=1, source_target_pairs={{0,1},{1,0},{2,3},{3,2},{4,5},{5,4},{6,7},{7,6},{8,9},{9,8},{10,11... | collective-permute-start | bytes 393224 | tf_op jit(solution)/shard_map/ppermute | solution.py:32
  33.4 8.5 %copy-start.5 = (bf16[4,2,128,128]{3,2,1,0:T(8,128)(2,1)S(1)}, bf16[4,2,128,128]{3,2,1,0:T(8,128)(2,1)}, u32[]{:S(2)}) copy-start(bf16[4,2,128,128]{3,2,1,0:T(8,128)(2,1)} %get-tuple-element.49) | copy-start | bytes 786436
  41.0 2.2 %collective-permute-start.7 = (bf16[3,4,128,128]{3,2,1,0:T(8,128)(2,1)S(1)}, bf16[3,4,128,128]{3,2,1,0:T(8,128)(2,1)S(1)}, u32[]{:S(2)}, u32[]{:S(2)}) collective-permute-start(bf16[3,4,128,128]{3,2,1,0:T(8,128)(2,1)S(1)} %collective-permute-done.5), channel_id=1, source_target_pairs={{0,1},{1,0},{2,3},{3,2},{4,5},{5,4},{6,7},{7,6},{8,9},{9,8},{10,11... | collective-permute-start | bytes 1179656 | tf_op jit(solution)/shard_map/ppermute | solution.py:32
  42.5 1.1 %copy-start.7 = (f32[3,128,128]{2,1,0:T(8,128)S(1)}, f32[3,128,128]{2,1,0:T(8,128)}, u32[]{:S(2)}) copy-start(f32[3,128,128]{2,1,0:T(8,128)} %param.38) | copy-start | bytes 589828
  43.2 0.9 %copy-start.2 = (f32[1,128,128]{2,1,0:T(8,128)S(1)}, f32[1,128,128]{2,1,0:T(8,128)}, u32[]{:S(2)}) copy-start(f32[1,128,128]{2,1,0:T(8,128)} %param.39) | copy-start | bytes 196612
  43.2 5.0 %copy-start.3 = (bf16[3,3,128,128]{3,2,1,0:T(8,128)(2,1)S(1)}, bf16[3,3,128,128]{3,2,1,0:T(8,128)(2,1)}, u32[]{:S(2)}) copy-start(bf16[3,3,128,128]{3,2,1,0:T(8,128)(2,1)} %get-tuple-element.48) | copy-start | bytes 884740
  43.3 5.3 %copy-start.8 = (bf16[3,2,128,128]{3,2,1,0:T(8,128)(2,1)S(1)}, bf16[3,2,128,128]{3,2,1,0:T(8,128)(2,1)}, u32[]{:S(2)}) copy-start(bf16[3,2,128,128]{3,2,1,0:T(8,128)(2,1)} %get-tuple-element.52) | copy-start | bytes 589828
  44.4 6.1 %collective-permute-start.8 = (bf16[128,128]{0,1:T(8,128)(2,1)S(1)}, bf16[128,128]{0,1:T(8,128)(2,1)S(1)}, u32[]{:S(2)}, u32[]{:S(2)}) collective-permute-start(bf16[128,128]{0,1:T(8,128)(2,1)S(1)} %get-tuple-element.36), channel_id=1, source_target_pairs={{0,4},{1,5},{2,6},{3,7},{4,8},{5,9},{6,10},{7,11},{8,12},{9,13},{1... | collective-permute-start | bytes 98312 | tf_op jit(solution)/shard_map/ppermute | solution.py:25
  45.1 6.1 %collective-permute-start.9 = (bf16[128,128]{0,1:T(8,128)(2,1)S(1)}, bf16[128,128]{0,1:T(8,128)(2,1)S(1)}, u32[]{:S(2)}, u32[]{:S(2)}) collective-permute-start(bf16[128,128]{0,1:T(8,128)(2,1)S(1)} %get-tuple-element.36), channel_id=1, source_target_pairs={{0,8},{1,9},{2,10},{3,11},{4,12},{5,13},{6,14},{7,15},{8,0},{9,1},... | collective-permute-start | bytes 98312 | tf_op jit(solution)/shard_map/ppermute | solution.py:25
  45.5 5.8 %collective-permute-start.10 = (bf16[128,128]{0,1:T(8,128)(2,1)S(1)}, bf16[128,128]{0,1:T(8,128)(2,1)S(1)}, u32[]{:S(2)}, u32[]{:S(2)}) collective-permute-start(bf16[128,128]{0,1:T(8,128)(2,1)S(1)} %get-tuple-element.36), channel_id=1, source_target_pairs={{0,12},{1,13},{2,14},{3,15},{4,0},{5,1},{6,2},{7,3},{8,4},{9,5},{1... | collective-permute-start | bytes 98312 | tf_op jit(solution)/shard_map/ppermute | solution.py:25
  51.3 2.0 %collective-permute-start.11 = (bf16[4,128,128]{1,2,0:T(8,128)(2,1)S(1)}, bf16[4,128,128]{1,2,0:T(8,128)(2,1)S(1)}, u32[]{:S(2)}, u32[]{:S(2)}) collective-permute-start(bf16[4,128,128]{1,2,0:T(8,128)(2,1)S(1)} %pad_maximum_fusion.10), channel_id=1, source_target_pairs={{0,1},{1,0},{2,3},{3,2},{4,5},{5,4},{6,7},{7,6},{8,9},{9,8},{10,11... | collective-permute-start | bytes 393224 | tf_op jit(solution)/shard_map/ppermute | solution.py:32
  51.3 6.4 %collective-permute-start.12 = (bf16[4,128,128]{1,2,0:T(8,128)(2,1)S(1)}, bf16[4,128,128]{1,2,0:T(8,128)(2,1)S(1)}, u32[]{:S(2)}, u32[]{:S(2)}) collective-permute-start(bf16[4,128,128]{1,2,0:T(8,128)(2,1)S(1)} %pad_maximum_fusion.10), channel_id=1, source_target_pairs={{0,2},{1,3},{2,0},{3,1},{4,6},{5,7},{6,4},{7,5},{8,10},{9,11},{10,... | collective-permute-start | bytes 393224 | tf_op jit(solution)/shard_map/ppermute | solution.py:32
  51.9 7.7 %collective-permute-start.13 = (bf16[4,128,128]{1,2,0:T(8,128)(2,1)S(1)}, bf16[4,128,128]{1,2,0:T(8,128)(2,1)S(1)}, u32[]{:S(2)}, u32[]{:S(2)}) collective-permute-start(bf16[4,128,128]{1,2,0:T(8,128)(2,1)S(1)} %pad_maximum_fusion.10), channel_id=1, source_target_pairs={{0,3},{1,2},{2,1},{3,0},{4,7},{5,6},{6,5},{7,4},{8,11},{9,10},{10,... | collective-permute-start | bytes 393224 | tf_op jit(solution)/shard_map/ppermute | solution.py:32
  60.5 5.9 %collective-permute-start.14 = (bf16[128,128]{0,1:T(8,128)(2,1)S(1)}, bf16[128,128]{0,1:T(8,128)(2,1)S(1)}, u32[]{:S(2)}, u32[]{:S(2)}) collective-permute-start(bf16[128,128]{0,1:T(8,128)(2,1)S(1)} %get-tuple-element.34), channel_id=1, source_target_pairs={{0,4},{1,5},{2,6},{3,7},{4,8},{5,9},{6,10},{7,11},{8,12},{9,13},{1... | collective-permute-start | bytes 98312 | tf_op jit(solution)/shard_map/ppermute | solution.py:25
  62.0 5.3 %collective-permute-start.15 = (bf16[128,128]{0,1:T(8,128)(2,1)S(1)}, bf16[128,128]{0,1:T(8,128)(2,1)S(1)}, u32[]{:S(2)}, u32[]{:S(2)}) collective-permute-start(bf16[128,128]{0,1:T(8,128)(2,1)S(1)} %get-tuple-element.34), channel_id=1, source_target_pairs={{0,8},{1,9},{2,10},{3,11},{4,12},{5,13},{6,14},{7,15},{8,0},{9,1},... | collective-permute-start | bytes 98312 | tf_op jit(solution)/shard_map/ppermute | solution.py:25
  63.8 3.9 %collective-permute-start.16 = (bf16[128,128]{0,1:T(8,128)(2,1)S(1)}, bf16[128,128]{0,1:T(8,128)(2,1)S(1)}, u32[]{:S(2)}, u32[]{:S(2)}) collective-permute-start(bf16[128,128]{0,1:T(8,128)(2,1)S(1)} %get-tuple-element.34), channel_id=1, source_target_pairs={{0,12},{1,13},{2,14},{3,15},{4,0},{5,1},{6,2},{7,3},{8,4},{9,5},{1... | collective-permute-start | bytes 98312 | tf_op jit(solution)/shard_map/ppermute | solution.py:25
  67.8 2.0 %collective-permute-start.17 = (bf16[4,128,128]{1,2,0:T(8,128)(2,1)S(1)}, bf16[4,128,128]{1,2,0:T(8,128)(2,1)S(1)}, u32[]{:S(2)}, u32[]{:S(2)}) collective-permute-start(bf16[4,128,128]{1,2,0:T(8,128)(2,1)S(1)} %pad_maximum_fusion.11), channel_id=1, source_target_pairs={{0,1},{1,0},{2,3},{3,2},{4,5},{5,4},{6,7},{7,6},{8,9},{9,8},{10,11... | collective-permute-start | bytes 393224 | tf_op jit(solution)/shard_map/ppermute | solution.py:32
  67.9 6.4 %collective-permute-start.18 = (bf16[4,128,128]{1,2,0:T(8,128)(2,1)S(1)}, bf16[4,128,128]{1,2,0:T(8,128)(2,1)S(1)}, u32[]{:S(2)}, u32[]{:S(2)}) collective-permute-start(bf16[4,128,128]{1,2,0:T(8,128)(2,1)S(1)} %pad_maximum_fusion.11), channel_id=1, source_target_pairs={{0,2},{1,3},{2,0},{3,1},{4,6},{5,7},{6,4},{7,5},{8,10},{9,11},{10,... | collective-permute-start | bytes 393224 | tf_op jit(solution)/shard_map/ppermute | solution.py:32
  68.4 7.7 %collective-permute-start.19 = (bf16[4,128,128]{1,2,0:T(8,128)(2,1)S(1)}, bf16[4,128,128]{1,2,0:T(8,128)(2,1)S(1)}, u32[]{:S(2)}, u32[]{:S(2)}) collective-permute-start(bf16[4,128,128]{1,2,0:T(8,128)(2,1)S(1)} %pad_maximum_fusion.11), channel_id=1, source_target_pairs={{0,3},{1,2},{2,1},{3,0},{4,7},{5,6},{6,5},{7,4},{8,11},{9,10},{10,... | collective-permute-start | bytes 393224 | tf_op jit(solution)/shard_map/ppermute | solution.py:32

commit v7 on v5

--- a/solution.py
+++ b/solution.py
@@ -34,6 +34,10 @@
         beside = lax.ppermute(stack, "wide", [(d, d ^ 1) for d in range(wide)])
         diagonal = lax.ppermute(across, "wide", [(d, d ^ 1) for d in range(wide)])
         return [stack, beside, across, diagonal]
+    if inner == 4:
+        slabs = [[z * inner + k for k in range(inner)] for z in range(wide // inner)]
+        gathered = lax.all_gather(stack, "wide", axis=0, tiled=False, axis_index_groups=slabs)
+        return [gathered[k] for k in range(inner)]
     parts = [stack]
     for m in range(1, inner):
         parts.append(lax.ppermute(stack, "wide", [(d, d ^ m) for d in range(wide)]))
@@ -49,10 +53,8 @@
     line = np.arange(lines, dtype=np.int32)
     source_line = (me // inner - line) % lines if shifted else jnp.asarray(line)
     masks = np.arange(inner, dtype=np.int32)
-    blocks = (
-        source_line[None, :] * inner
-        + jnp.bitwise_xor(me % inner, jnp.asarray(masks))[:, None]
-    )
+    position = jnp.asarray(masks) if not doubling and inner == 4 else jnp.bitwise_xor(me % inner, jnp.asarray(masks))
+    blocks = source_line[None, :] * inner + position[:, None]
     return pieces, blocks.reshape(wide)
 
 

time: 67.3 us -> 72.9 us (1.083)
  waiting for transfers between devices: 30.7 us -> 16.2 us
  blocking collectives: 0 us -> 14 us
  starting transfers between devices: 23 us -> 16.5 us
  matrix products: 5.8 us -> 10.7 us
  other arithmetic: 3.07 us -> 7.61 us
  local copies, waits for them, and re-layouts: 4.34 us -> 6.96 us
    all_gather x0 -> x2, blocking collectives: none -> 14 us  [slab_stage(): lax.all_gather(stack, 'wide', axis=0, tiled=False, axis_index_groups=slabs)]
    ppermute x6 -> x0, waiting for transfers between devices: 12.6 us -> none  [slab_stage(): parts.append(lax.ppermute(stack, 'wide', [(d, d ^ m) for d in range(wide)]))]
    dot_general x15, matrix products: 4.95 us -> 9.2 us  [rowwise(): return jnp.einsum(spec, tiles, currents, preferred_element_type=jnp.float32)]
    ppermute x6 -> x0, starting transfers between devices: 3.87 us -> none  [slab_stage(): parts.append(lax.ppermute(stack, 'wide', [(d, d ^ m) for d in range(wide)]))]
    ppermute x9, starting transfers between devices: 17.5 us -> 14.8 us  [line_stage(): parts.append(lax.ppermute(x, 'wide', pairs))]
    gather x1 -> x3, local copies, waits for them, and re-layouts: 0.75 us -> 3.11 us  [tiles_by_lag(): tiles = jnp.take(retarded_tiles[0], columns, axis=0)]
    select_n x2, other arithmetic: 0.43 us -> 2.44 us  [tiles_by_lag(): jnp.where((lags[:, 0] == lag)[:, None, None], tiles[:, 0], jnp.where((lag...]
    ppermute x9, waiting for transfers between devices: 6.62 us -> 4.88 us  [line_stage(): parts.append(lax.ppermute(x, 'wide', pairs))]
  transfers between devices with their start and end apart: 18 -> 12, of which waited for: 10 -> 6; matrix products, arithmetic and copies ran while one was open for 14% -> 23% of each run, Pallas kernels for 0% -> 0%
where the time goes in v7:
time: 72.9 us; the launch traced here: 72.5 us
  starting transfers between devices  16.5 us (23%)
  waiting for transfers between devices  16.2 us (22%)
  blocking collectives  14 us (19%)
  matrix products  10.7 us (15%)
  other arithmetic  7.61 us (10%)
  local copies, waits for them, and re-layouts  6.96 us (10%)
    ppermute x9, starting transfers between devices, line_stage(): parts.append(lax.ppermute(x, 'wide', pairs))  14.8 us
    all_gather x2, blocking collectives, slab_stage(): lax.all_gather(stack, 'wide', axis=0, tiled=False, axis_index_groups=slabs)  14 us
    ppermute x1, waiting for transfers between devices, slab_stage(): across = lax.ppermute(stack, 'wide', [(d, d ^ 2) for d in range(wide)])  11.3 us
    dot_general x15, matrix products, rowwise(): return jnp.einsum(spec, tiles, currents, preferred_element_type=jnp.float32)  9.2 us
    ppermute x9, waiting for transfers between devices, line_stage(): parts.append(lax.ppermute(x, 'wide', pairs))  4.88 us
    gather x3, local copies, waits for them, and re-layouts, tiles_by_lag(): tiles = jnp.take(retarded_tiles[0], columns, axis=0)  3.11 us
    select_n x2, other arithmetic, tiles_by_lag(): jnp.where((lags[:, 0] == lag)[:, None, None], tiles[:, 0], jnp.where((lag...  2.44 us
    sort x1, other arithmetic, per_device(): column_of_block = jnp.argsort(block_owner)  1.9 us
  transfers between devices with their start and end apart: 12, of which 6 were waited for; matrix products, arithmetic and copies ran while one was open for 23% of the time, Pallas kernels for 0%

profile of v7, /device:TPU:0, one launch (start us, length us, event | category | flops | bytes accessed | tf_op | source)
XLA Modules:
  0.0 72.5 jit_solution(3317019083182218668)
XLA Ops:
  0.0 3.0 %collective-permute-start = (bf16[4,128,128]{2,1,0:T(8,128)(2,1)}, bf16[4,128,128]{2,1,0:T(8,128)(2,1)S(1)}, u32[]{:S(2)}, u32[]{:S(2)}) collective-permute-start(bf16[4,128,128]{2,1,0:T(8,128)(2,1)} %param.19), channel_id=1, source_target_pairs={{0,4},{1,5},{2,6},{3,7},{4,8},{5,9},{6,10},{7,11},{8,12},{9,13},{1... | collective-permute-start | bytes 393224 | tf_op jit(solution)/shard_map/ppermute | solution.py:25
  3.0 2.6 %collective-permute-start.1 = (bf16[4,128,128]{2,1,0:T(8,128)(2,1)}, bf16[4,128,128]{2,1,0:T(8,128)(2,1)}, u32[]{:S(2)}, u32[]{:S(2)}) collective-permute-start(bf16[4,128,128]{2,1,0:T(8,128)(2,1)} %param.19), channel_id=1, source_target_pairs={{0,8},{1,9},{2,10},{3,11},{4,12},{5,13},{6,14},{7,15},{8,0},{9,1},... | collective-permute-start | bytes 393224 | tf_op jit(solution)/shard_map/ppermute | solution.py:25
  5.6 1.3 %collective-permute-start.2 = (bf16[4,128,128]{2,1,0:T(8,128)(2,1)}, bf16[4,128,128]{2,1,0:T(8,128)(2,1)}, u32[]{:S(2)}, u32[]{:S(2)}) collective-permute-start(bf16[4,128,128]{2,1,0:T(8,128)(2,1)} %param.19), channel_id=1, source_target_pairs={{0,12},{1,13},{2,14},{3,15},{4,0},{5,1},{6,2},{7,3},{8,4},{9,5},{1... | collective-permute-start | bytes 393224 | tf_op jit(solution)/shard_map/ppermute | solution.py:25
  7.2 1.9 %sort.17 = (s32[16]{0:T(128)}, s32[16]{0:T(128)S(1)}) sort(s32[16]{0:T(128)} %param.18, s32[16]{0:T(128)S(1)} %iota.5), dimensions={0}, to_apply=%region_0.0 | sort | flops 64 | bytes 256 | tf_op jit(solution)/shard_map/jit(argsort)/sort | solution.py:87
  9.1 0.7 gather_fusion
  9.8 0.7 %gather_fusion.2 = bf16[16,2,128,128]{3,2,1,0:T(8,128)(2,1)S(1)} fusion(bf16[16,2,128,128]{3,2,1,0:T(8,128)(2,1)S(1)} %bitcast.154, s32[1024]{0:T(1024)S(1)} %pad_clamp_fusion.2), kind=kCustom, calls=%fused_computation.2.clone | custom fusion | bytes 2097216 | tf_op jit(solution)/shard_map/jit(_take)/gather | solution.py:63
  10.5 0.7 copy.29
  11.3 0.6 gather_fusion.1
  11.9 1.2 %broadcast_select_fusion.1 = bf16[16,2,128,128]{2,3,0,1:T(8,128)(2,1)} fusion(bf16[16,2,128,128]{2,3,0,1:T(8,128)(2,1)S(1)} %copy.29, pred[16]{0:T(512)(128)(4,1)S(1)} %get-tuple-element.24), kind=kLoop, calls=%fused_computation.41 | loop fusion | flops 524288 | bytes 2097168 | tf_op jit(solution)/shard_map/jit(_take)/select_n | solution.py:63
  13.1 0.3 compare_reduce_fusion.3
  13.5 0.7 gather_fusion.3
  14.2 0.6 gather_fusion.4
  14.7 1.5 %select_select_fusion = (bf16[16,1,128,128]{2,3,0,1:T(8,128)(2,1)S(1)}, bf16[16,1,128,128]{2,3,0,1:T(8,128)(2,1)S(1)}, bf16[16,1,128,128]{2,3,0,1:T(8,128)(2,1)S(1)}, bf16[16,1,128,128]{2,3,0,1:T(8,128)(2,1)S(1)}) fusion(pred[16]{0:T(512)(128)(4,1)S(1)} %get-tuple-element.19, pred[16]{0:T(512)(128)(4,1)S(1)} %get-tuple-element.14, ...), kind=kLoop, calls=%fused_computation.47 | loop fusion | flops 2097152 | bytes 3145856 | tf_op jit(solution)/shard_map/jit(_where)/select_n | solution.py:68
  16.3 1.7 %gather_fusion.5 = bf16[16,2,128,128]{3,2,1,0:T(8,128)(2,1)} fusion(bf16[16,2,128,128]{3,2,1,0:T(8,128)(2,1)S(1)} %bitcast.155, s32[1024]{0:T(1024)S(1)} %pad_clamp_fusion), kind=kCustom, calls=%fused_computation.5.clone | custom fusion | bytes 2097216 | tf_op jit(solution)/shard_map/jit(_take)/gather | solution.py:63
  18.2 1.1 %pad_maximum_fusion.3 = bf16[4,4,128,128]{3,2,0,1:T(8,128)(2,1)S(1)} fusion(bf16[1,4,128,128]{3,2,0,1:T(8,128)(2,1)} %bitcast.6, bf16[1,4,128,128]{3,2,0,1:T(8,128)(2,1)} %bitcast.5, bf16[1,4,128,128]{3,2,0,1:T(8,128)(2,1)S(1)} %bitcast.162, bf16[1,4,128,128]{3,2,0,1:T(8,128)(2,1)S(1)} %bitcast.160), kind=kLoop, calls=%fused_computation.44 | loop fusion | flops 786432 | bytes 1048576 | tf_op jit(solution)/shard_map/stack | solution.py:26
  19.7 1.6 %collective-permute-start.4 = (bf16[4,4,128,128]{3,2,0,1:T(8,128)(2,1)S(1)}, bf16[4,4,128,128]{3,2,0,1:T(8,128)(2,1)S(1)}, u32[]{:S(2)}, u32[]{:S(2)}) collective-permute-start(bf16[4,4,128,128]{3,2,0,1:T(8,128)(2,1)S(1)} %pad_maximum_fusion.3), channel_id=1, source_target_pairs={{0,2},{1,3},{2,0},{3,1},{4,6},{5,7},{6,4},{7,5},{8,10},{9,11},{10,... | collective-permute-start | bytes 1572872 | tf_op jit(solution)/shard_map/ppermute | solution.py:33
  21.2 1.0 %select_select_fusion.2 = bf16[16,128,128]{2,1,0:T(8,128)(2,1)} fusion(pred[16]{0:T(512)(128)(4,1)S(1)} %get-tuple-element.12, pred[16]{0:T(512)(128)(4,1)S(1)} %get-tuple-element.13, bf16[16,2,128,128]{3,2,1,0:T(8,128)(2,1)S(1)} %broadcast_select_fusion), kind=kLoop, calls=%fused_computation.49 | loop fusion | flops 524288 | bytes 1572896 | tf_op jit(solution)/shard_map/jit(_where)/select_n | solution.py:68
  22.2 0.2 convolution_bitcast_fusion.10
  22.4 0.3 convolution_bitcast_fusion.6
  22.7 11.3 %collective-permute-done.4 = bf16[4,4,128,128]{3,2,0,1:T(8,128)(2,1)S(1)} collective-permute-done((bf16[4,4,128,128]{3,2,0,1:T(8,128)(2,1)S(1)}, bf16[4,4,128,128]{3,2,0,1:T(8,128)(2,1)S(1)}, u32[]{:S(2)}, u32[]{:S(2)}) %collective-permute-start.4) | collective-permute-done | bytes 524320 | tf_op jit(solution)/shard_map/ppermute | solution.py:33
  34.0 0.2 convolution_bitcast_fusion.5
  34.3 0.3 convolution_bitcast_fusion.2
  34.6 0.3 convolution_bitcast_fusion.1
  35.2 0.9 %fusion.7 = f32[128,128]{1,0:T(8,128)} fusion(f32[128,128]{1,0:T(8,128)S(1)} %convolution_bitcast_fusion.5, f32[128,128]{1,0:T(8,128)S(1)} %convolution_bitcast_fusion.6, bf16[4,4,128,128]{3,2,0,1:T(8,128)(2,1)S(1)} %pad_maximum_fusion.3, bf16[16,1,128,128]{2,3,0,1:T(8,128)(2,1)S(1)} %get-tuple-element.29, ...), kind=kOutput, calls=%fused_computation.31 | convolution fusion | flops 55083008 | bytes 2162688 | tf_op jit(solution)/shard_map/slpq,slpr->qr/dot_general | solution.py:81
  36.1 1.3 %fusion.12 = f32[128,128]{1,0:T(8,128)S(1)} fusion(f32[128,128]{1,0:T(8,128)S(1)} %convolution_bitcast_fusion.1, f32[128,128]{1,0:T(8,128)S(1)} %convolution_bitcast_fusion.2, bf16[1,4,128,128]{3,2,0,1:T(8,128)(2,1)} %bitcast.6, bf16[1,4,128,128]{3,2,0,1:T(8,128)(2,1)} %bitcast.5, bf16[1,4,128,128]{3,2,0,1:T(8,128)(2,1)S(1)} %bitcast.163, ...), kind=kOutput, calls=%fused_computation.36 | convolution fusion | flops 77627392 | bytes 2818048 | tf_op jit(solution)/shard_map/slpq,slpr->qr/dot_general | solution.py:81
  37.4 1.2 %fusion.14 = f32[128,128]{1,0:T(8,128)S(1)} fusion(f32[128,128]{1,0:T(8,128)S(1)} %fusion.12, bf16[4,4,128,128]{3,2,0,1:T(8,128)(2,1)S(1)} %collective-permute-done.5, f32[3,128,128]{2,1,0:T(8,128)} %param.20, bf16[16,1,128,128]{2,3,0,1:T(8,128)(2,1)S(1)} %get-tuple-element.29, bf16[16,1,128,128]{2,3,0,1:T(8,128)(2,1)S(1)} %get-tuple-element.28, ...), kind=kOutput, calls=%fused_computation.38 | convolution fusion | flops 75530240 | bytes 2818048 | tf_op jit(solution)/shard_map/slpq,slpr->qr/dot_general | solution.py:81
  38.6 0.9 %bitcast_convert_fusion.1 = (bf16[128,128]{0,1:T(8,128)(2,1)S(1)}, f32[128,128]{1,0:T(8,128)}) fusion(f32[128,128]{1,0:T(8,128)S(1)} %fusion.14, f32[1,128,128]{2,1,0:T(8,128)S(1)} %copy-done.8), kind=kOutput, calls=%fused_computation.67 | convolution fusion | flops 25182208 | bytes 229376 | tf_op jit(solution)/shard_map/dot_general | solution.py:98
  39.5 0.7 collective-permute-start.6
  40.2 0.5 collective-permute-start.7
  40.7 2.7 %collective-permute-start.8 = (bf16[128,128]{0,1:T(8,128)(2,1)S(1)}, bf16[128,128]{0,1:T(8,128)(2,1)S(1)}, u32[]{:S(2)}, u32[]{:S(2)}) collective-permute-start(bf16[128,128]{0,1:T(8,128)(2,1)S(1)} %get-tuple-element.32), channel_id=1, source_target_pairs={{0,12},{1,13},{2,14},{3,15},{4,0},{5,1},{6,2},{7,3},{8,4},{9,5},{1... | collective-permute-start | bytes 98312 | tf_op jit(solution)/shard_map/ppermute | solution.py:25
  43.6 2.0 %collective-permute-done.6 = bf16[128,128]{0,1:T(8,128)(2,1)S(1)} collective-permute-done((bf16[128,128]{0,1:T(8,128)(2,1)S(1)}, bf16[128,128]{0,1:T(8,128)(2,1)S(1)}, u32[]{:S(2)}, u32[]{:S(2)}) %collective-permute-start.6) | collective-permute-done | bytes 32800 | tf_op jit(solution)/shard_map/ppermute | solution.py:25
  45.6 0.7 %collective-permute-done.7 = bf16[128,128]{0,1:T(8,128)(2,1)S(1)} collective-permute-done((bf16[128,128]{0,1:T(8,128)(2,1)S(1)}, bf16[128,128]{0,1:T(8,128)(2,1)S(1)}, u32[]{:S(2)}, u32[]{:S(2)}) %collective-permute-start.7) | collective-permute-done | bytes 32800 | tf_op jit(solution)/shard_map/ppermute | solution.py:25
  46.5 7.3 %all-gather = bf16[16,128,128]{2,1,0:T(8,128)(2,1)S(1)} all-gather(bf16[4,128,128]{2,1,0:T(8,128)(2,1)S(1)} %copy.32), channel_id=2, replica_groups={{0,1,2,3},{4,5,6,7},{8,9,10,11},{12,13,14,15},{16,17,18,19},{20,21,22,2..., dimensions={0}, use_global_device_ids=true | all-gather | bytes 655360 | tf_op jit(solution)/shard_map/all_gather | solution.py:39
  53.8 0.3 convolution_bitcast_fusion.15
  54.2 1.2 %fusion.10 = f32[128,128]{1,0:T(8,128)S(1)} fusion(f32[128,128]{1,0:T(8,128)S(1)} %convolution_bitcast_fusion.15, f32[128,128]{1,0:T(8,128)S(1)} %copy-done.15, bf16[4,4,128,128]{3,2,0,1:T(8,128)(2,1)S(1)} %copy-done.6, f32[3,128,128]{2,1,0:T(8,128)} %param.20, bf16[16,1,128,128]{2,3,0,1:T(8,128)(2,1)S(1)} %get-tuple-element.29, ...), kind=kOutput, calls=%fused_computation.34 | convolution fusion | flops 55099392 | bytes 2228224 | tf_op jit(solution)/shard_map/slpq,slpr->qr/dot_general | solution.py:81
  55.4 0.3 bitcast_convert_fusion
  55.7 1.6 %collective-permute-start.9 = (bf16[128,128]{0,1:T(8,128)(2,1)S(1)}, bf16[128,128]{0,1:T(8,128)(2,1)S(1)}, u32[]{:S(2)}, u32[]{:S(2)}) collective-permute-start(bf16[128,128]{0,1:T(8,128)(2,1)S(1)} %get-tuple-element.34), channel_id=1, source_target_pairs={{0,4},{1,5},{2,6},{3,7},{4,8},{5,9},{6,10},{7,11},{8,12},{9,13},{1... | collective-permute-start | bytes 98312 | tf_op jit(solution)/shard_map/ppermute | solution.py:25
  57.3 1.8 %collective-permute-start.10 = (bf16[128,128]{0,1:T(8,128)(2,1)S(1)}, bf16[128,128]{0,1:T(8,128)(2,1)S(1)}, u32[]{:S(2)}, u32[]{:S(2)}) collective-permute-start(bf16[128,128]{0,1:T(8,128)(2,1)S(1)} %get-tuple-element.34), channel_id=1, source_target_pairs={{0,8},{1,9},{2,10},{3,11},{4,12},{5,13},{6,14},{7,15},{8,0},{9,1},... | collective-permute-start | bytes 98312 | tf_op jit(solution)/shard_map/ppermute | solution.py:25
  59.1 0.6 collective-permute-start.11
  59.7 1.1 %convolution_bitcast_fusion.13 = f32[128,128]{1,0:T(8,128)} fusion(bf16[16,128,128]{2,1,0:T(8,128)(2,1)S(1)} %all-gather, pred[16]{0:T(512)(128)(4,1)S(1)} %get-tuple-element.11, pred[16]{0:T(512)(128)(4,1)S(1)} %get-tuple-element.10, bf16[16,2,128,128]{3,2,1,0:T(8,128)(2,1)S(1)} %copy-done.4), kind=kOutput, calls=%fused_computation.21 | convolution fusion | flops 67633152 | bytes 1638432 | tf_op jit(solution)/shard_map/spq,spr->qr/dot_general | solution.py:81
  60.9 0.8 %collective-permute-done.9 = bf16[128,128]{0,1:T(8,128)(2,1)S(1)} collective-permute-done((bf16[128,128]{0,1:T(8,128)(2,1)S(1)}, bf16[128,128]{0,1:T(8,128)(2,1)S(1)}, u32[]{:S(2)}, u32[]{:S(2)}) %collective-permute-start.9) | collective-permute-done | bytes 32800 | tf_op jit(solution)/shard_map/ppermute | solution.py:25
  61.6 1.1 %collective-permute-done.10 = bf16[128,128]{0,1:T(8,128)(2,1)S(1)} collective-permute-done((bf16[128,128]{0,1:T(8,128)(2,1)S(1)}, bf16[128,128]{0,1:T(8,128)(2,1)S(1)}, u32[]{:S(2)}, u32[]{:S(2)}) %collective-permute-start.10) | collective-permute-done | bytes 32800 | tf_op jit(solution)/shard_map/ppermute | solution.py:25
  62.7 0.3 collective-permute-done.11
  63.2 6.7 %all-gather.1 = bf16[16,128,128]{2,1,0:T(8,128)(2,1)S(1)} all-gather(bf16[4,128,128]{2,1,0:T(8,128)(2,1)S(1)} %copy.34), channel_id=3, replica_groups={{0,1,2,3},{4,5,6,7},{8,9,10,11},{12,13,14,15},{16,17,18,19},{20,21,22,2..., dimensions={0}, use_global_device_ids=true | all-gather | bytes 655360 | tf_op jit(solution)/shard_map/all_gather | solution.py:39
  69.9 0.3 convolution_bitcast_fusion.14
  70.3 1.1 %fusion.5 = f32[128,128]{1,0:T(8,128)S(1)} fusion(f32[128,128]{1,0:T(8,128)S(1)} %copy-done.13, f32[128,128]{1,0:T(8,128)S(1)} %convolution_bitcast_fusion.14, f32[128,128]{1,0:T(8,128)S(1)} %fusion.1, bf16[4,4,128,128]{3,2,0,1:T(8,128)(2,1)S(1)} %copy-done.7, f32[3,128,128]{2,1,0:T(8,128)} %param.20, bf16[16,1,128,128]{2,3,0,1:T(8,128)(2,1)S(1)} %get-tuple-element.29, ...), kind=kOutput, calls=%fused_computation.29 | convolution fusion | flops 35717120 | bytes 1638400 | tf_op jit(solution)/shard_map/slpq,slpr->qr/dot_general | solution.py:81
  71.4 0.3 convolution_bitcast_fusion.12
  71.7 0.8 %copy.37 = f32[3,128,128]{2,1,0:T(8,128)} copy(f32[3,128,128]{1,2,0:T(8,128)S(1)} %pad_maximum_fusion.4) | data formatting | bytes 393216 | tf_op jit(solution)/shard_map/stack | solution.py:129
  (65 shorter events, 1.9 us)
Async XLA Ops:
  0.0 9.8 %copy-start = (bf16[1,16,2,128,128]{4,3,2,1,0:T(8,128)(2,1)S(1)}, bf16[1,16,2,128,128]{4,3,2,1,0:T(8,128)(2,1)}, u32[]{:S(2)}) copy-start(bf16[1,16,2,128,128]{4,3,2,1,0:T(8,128)(2,1)} %param.16) | copy-start | bytes 3145732
  0.0 18.2 %collective-permute-start = (bf16[4,128,128]{2,1,0:T(8,128)(2,1)}, bf16[4,128,128]{2,1,0:T(8,128)(2,1)S(1)}, u32[]{:S(2)}, u32[]{:S(2)}) collective-permute-start(bf16[4,128,128]{2,1,0:T(8,128)(2,1)} %param.19), channel_id=1, source_target_pairs={{0,4},{1,5},{2,6},{3,7},{4,8},{5,9},{6,10},{7,11},{8,12},{9,13},{1... | collective-permute-start | bytes 393224 | tf_op jit(solution)/shard_map/ppermute | solution.py:25
  3.0 15.2 %collective-permute-start.1 = (bf16[4,128,128]{2,1,0:T(8,128)(2,1)}, bf16[4,128,128]{2,1,0:T(8,128)(2,1)}, u32[]{:S(2)}, u32[]{:S(2)}) collective-permute-start(bf16[4,128,128]{2,1,0:T(8,128)(2,1)} %param.19), channel_id=1, source_target_pairs={{0,8},{1,9},{2,10},{3,11},{4,12},{5,13},{6,14},{7,15},{8,0},{9,1},... | collective-permute-start | bytes 393224 | tf_op jit(solution)/shard_map/ppermute | solution.py:25
  5.6 12.6 %collective-permute-start.2 = (bf16[4,128,128]{2,1,0:T(8,128)(2,1)}, bf16[4,128,128]{2,1,0:T(8,128)(2,1)}, u32[]{:S(2)}, u32[]{:S(2)}) collective-permute-start(bf16[4,128,128]{2,1,0:T(8,128)(2,1)} %param.19), channel_id=1, source_target_pairs={{0,12},{1,13},{2,14},{3,15},{4,0},{5,1},{6,2},{7,3},{8,4},{9,5},{1... | collective-permute-start | bytes 393224 | tf_op jit(solution)/shard_map/ppermute | solution.py:25
  10.5 0.7 copy-start.14
  16.3 1.9 %copy-start.10 = (bf16[4,128,128]{2,1,0:T(8,128)(2,1)S(1)}, bf16[4,128,128]{2,1,0:T(8,128)(2,1)}, u32[]{:S(2)}) copy-start(bf16[4,128,128]{2,1,0:T(8,128)(2,1)} %param.19) | copy-start | bytes 393220
  18.0 1.5 %copy-start.2 = (bf16[16,2,128,128]{3,2,1,0:T(8,128)(2,1)S(1)}, bf16[16,2,128,128]{3,2,1,0:T(8,128)(2,1)}, u32[]{:S(2)}) copy-start(bf16[16,2,128,128]{3,2,1,0:T(8,128)(2,1)} %gather_fusion.5) | copy-start | bytes 3145732
  18.2 1.4 %copy-start.11 = (bf16[4,128,128]{2,1,0:T(8,128)(2,1)}, bf16[4,128,128]{2,1,0:T(8,128)(2,1)S(1)}, u32[]{:S(2)}) copy-start(bf16[4,128,128]{2,1,0:T(8,128)(2,1)S(1)} %collective-permute-done) | copy-start | bytes 393220
  19.4 2.8 %collective-permute-start.3 = (bf16[4,4,128,128]{3,2,0,1:T(8,128)(2,1)S(1)}, bf16[4,4,128,128]{3,2,0,1:T(8,128)(2,1)S(1)}, u32[]{:S(2)}, u32[]{:S(2)}) collective-permute-start(bf16[4,4,128,128]{3,2,0,1:T(8,128)(2,1)S(1)} %pad_maximum_fusion.3), channel_id=1, source_target_pairs={{0,1},{1,0},{2,3},{3,2},{4,5},{5,4},{6,7},{7,6},{8,9},{9,8},{10,11... | collective-permute-start | bytes 1572872 | tf_op jit(solution)/shard_map/ppermute | solution.py:34
  19.6 2.8 %copy-start.3 = (bf16[16,2,128,128]{3,2,1,0:T(8,128)(2,1)}, bf16[16,2,128,128]{3,2,1,0:T(8,128)(2,1)S(1)}, u32[]{:S(2)}) copy-start(bf16[16,2,128,128]{3,2,1,0:T(8,128)(2,1)S(1)} %broadcast_select_fusion) | copy-start | bytes 3145732
  19.7 14.4 %collective-permute-start.4 = (bf16[4,4,128,128]{3,2,0,1:T(8,128)(2,1)S(1)}, bf16[4,4,128,128]{3,2,0,1:T(8,128)(2,1)S(1)}, u32[]{:S(2)}, u32[]{:S(2)}) collective-permute-start(bf16[4,4,128,128]{3,2,0,1:T(8,128)(2,1)S(1)} %pad_maximum_fusion.3), channel_id=1, source_target_pairs={{0,2},{1,3},{2,0},{3,1},{4,6},{5,7},{6,4},{7,5},{8,10},{9,11},{10,... | collective-permute-start | bytes 1572872 | tf_op jit(solution)/shard_map/ppermute | solution.py:33
  34.9 2.5 %collective-permute-start.5 = (bf16[4,4,128,128]{3,2,0,1:T(8,128)(2,1)S(1)}, bf16[4,4,128,128]{3,2,0,1:T(8,128)(2,1)S(1)}, u32[]{:S(2)}, u32[]{:S(2)}) collective-permute-start(bf16[4,4,128,128]{3,2,0,1:T(8,128)(2,1)S(1)} %collective-permute-done.4), channel_id=1, source_target_pairs={{0,1},{1,0},{2,3},{3,2},{4,5},{5,4},{6,7},{7,6},{8,9},{9,8},{10,11... | collective-permute-start | bytes 1572872 | tf_op jit(solution)/shard_map/ppermute | solution.py:35
  35.2 0.9 %copy-start.12 = (bf16[4,128,128]{2,1,0:T(8,128)(2,1)S(1)}, bf16[4,128,128]{2,1,0:T(8,128)(2,1)}, u32[]{:S(2)}) copy-start(bf16[4,128,128]{2,1,0:T(8,128)(2,1)} %copy-done.11) | copy-start | bytes 393220
  37.4 1.3 %copy-start.8 = (f32[1,128,128]{2,1,0:T(8,128)S(1)}, f32[1,128,128]{2,1,0:T(8,128)}, u32[]{:S(2)}) copy-start(f32[1,128,128]{2,1,0:T(8,128)} %param.21) | copy-start | bytes 196612
  37.4 1.2 %copy-start.5 = (bf16[4,4,128,128]{3,2,0,1:T(8,128)(2,1)}, bf16[4,4,128,128]{3,2,0,1:T(8,128)(2,1)S(1)}, u32[]{:S(2)}) copy-start(bf16[4,4,128,128]{3,2,0,1:T(8,128)(2,1)S(1)} %collective-permute-done.5) | copy-start | bytes 1572868
  39.5 14.3 %copy-start.1 = (bf16[16,128,128]{2,1,0:T(8,128)(2,1)S(1)}, bf16[16,128,128]{2,1,0:T(8,128)(2,1)}, u32[]{:S(2)}) copy-start(bf16[16,128,128]{2,1,0:T(8,128)(2,1)} %select_select_fusion.2) | copy-start | bytes 1572868
  39.5 6.0 %collective-permute-start.6 = (bf16[128,128]{0,1:T(8,128)(2,1)S(1)}, bf16[128,128]{0,1:T(8,128)(2,1)S(1)}, u32[]{:S(2)}, u32[]{:S(2)}) collective-permute-start(bf16[128,128]{0,1:T(8,128)(2,1)S(1)} %get-tuple-element.32), channel_id=1, source_target_pairs={{0,4},{1,5},{2,6},{3,7},{4,8},{5,9},{6,10},{7,11},{8,12},{9,13},{1... | collective-permute-start | bytes 98312 | tf_op jit(solution)/shard_map/ppermute | solution.py:25
  40.2 6.1 %collective-permute-start.7 = (bf16[128,128]{0,1:T(8,128)(2,1)S(1)}, bf16[128,128]{0,1:T(8,128)(2,1)S(1)}, u32[]{:S(2)}, u32[]{:S(2)}) collective-permute-start(bf16[128,128]{0,1:T(8,128)(2,1)S(1)} %get-tuple-element.32), channel_id=1, source_target_pairs={{0,8},{1,9},{2,10},{3,11},{4,12},{5,13},{6,14},{7,15},{8,0},{9,1},... | collective-permute-start | bytes 98312 | tf_op jit(solution)/shard_map/ppermute | solution.py:25
  40.7 5.6 %collective-permute-start.8 = (bf16[128,128]{0,1:T(8,128)(2,1)S(1)}, bf16[128,128]{0,1:T(8,128)(2,1)S(1)}, u32[]{:S(2)}, u32[]{:S(2)}) collective-permute-start(bf16[128,128]{0,1:T(8,128)(2,1)S(1)} %get-tuple-element.32), channel_id=1, source_target_pairs={{0,12},{1,13},{2,14},{3,15},{4,0},{5,1},{6,2},{7,3},{8,4},{9,5},{1... | collective-permute-start | bytes 98312 | tf_op jit(solution)/shard_map/ppermute | solution.py:25
  46.5 7.7 %copy-start.6 = (bf16[4,4,128,128]{3,2,0,1:T(8,128)(2,1)S(1)}, bf16[4,4,128,128]{3,2,0,1:T(8,128)(2,1)}, u32[]{:S(2)}) copy-start(bf16[4,4,128,128]{3,2,0,1:T(8,128)(2,1)} %copy-done.5) | copy-start | bytes 1572868
  46.5 7.7 %copy-start.15 = (f32[128,128]{1,0:T(8,128)S(1)}, f32[128,128]{1,0:T(8,128)}, u32[]{:S(2)}) copy-start(f32[128,128]{1,0:T(8,128)} %fusion.7) | copy-start | bytes 196612
  54.2 5.5 %copy-start.4 = (bf16[16,2,128,128]{3,2,1,0:T(8,128)(2,1)S(1)}, bf16[16,2,128,128]{3,2,1,0:T(8,128)(2,1)}, u32[]{:S(2)}) copy-start(bf16[16,2,128,128]{3,2,1,0:T(8,128)(2,1)} %copy-done.3) | copy-start | bytes 3145732
  55.7 5.9 %collective-permute-start.9 = (bf16[128,128]{0,1:T(8,128)(2,1)S(1)}, bf16[128,128]{0,1:T(8,128)(2,1)S(1)}, u32[]{:S(2)}, u32[]{:S(2)}) collective-permute-start(bf16[128,128]{0,1:T(8,128)(2,1)S(1)} %get-tuple-element.34), channel_id=1, source_target_pairs={{0,4},{1,5},{2,6},{3,7},{4,8},{5,9},{6,10},{7,11},{8,12},{9,13},{1... | collective-permute-start | bytes 98312 | tf_op jit(solution)/shard_map/ppermute | solution.py:25
  57.3 5.4 %collective-permute-start.10 = (bf16[128,128]{0,1:T(8,128)(2,1)S(1)}, bf16[128,128]{0,1:T(8,128)(2,1)S(1)}, u32[]{:S(2)}, u32[]{:S(2)}) collective-permute-start(bf16[128,128]{0,1:T(8,128)(2,1)S(1)} %get-tuple-element.34), channel_id=1, source_target_pairs={{0,8},{1,9},{2,10},{3,11},{4,12},{5,13},{6,14},{7,15},{8,0},{9,1},... | collective-permute-start | bytes 98312 | tf_op jit(solution)/shard_map/ppermute | solution.py:25
  59.1 3.9 %collective-permute-start.11 = (bf16[128,128]{0,1:T(8,128)(2,1)S(1)}, bf16[128,128]{0,1:T(8,128)(2,1)S(1)}, u32[]{:S(2)}, u32[]{:S(2)}) collective-permute-start(bf16[128,128]{0,1:T(8,128)(2,1)S(1)} %get-tuple-element.34), channel_id=1, source_target_pairs={{0,12},{1,13},{2,14},{3,15},{4,0},{5,1},{6,2},{7,3},{8,4},{9,5},{1... | collective-permute-start | bytes 98312 | tf_op jit(solution)/shard_map/ppermute | solution.py:25
  63.2 7.0 %copy-start.7 = (bf16[4,4,128,128]{3,2,0,1:T(8,128)(2,1)S(1)}, bf16[4,4,128,128]{3,2,0,1:T(8,128)(2,1)}, u32[]{:S(2)}) copy-start(bf16[4,4,128,128]{3,2,0,1:T(8,128)(2,1)} %copy-done.5) | copy-start | bytes 1572868
  63.2 7.0 %copy-start.13 = (f32[128,128]{1,0:T(8,128)S(1)}, f32[128,128]{1,0:T(8,128)}, u32[]{:S(2)}) copy-start(f32[128,128]{1,0:T(8,128)} %convolution_bitcast_fusion.13) | copy-start | bytes 196612
  70.2 1.4 %copy-start.9 = (f32[128,128]{1,0:T(8,128)S(1)}, f32[128,128]{1,0:T(8,128)}, u32[]{:S(2)}) copy-start(f32[128,128]{1,0:T(8,128)} %get-tuple-element.33) | copy-start | bytes 196612

commit v8 on v5

--- a/solution.py
+++ b/solution.py
@@ -114,7 +114,7 @@
         current = advance(moment, retarded)
         results[moment] = current
         if moment > 0:
-            pieces, new_blocks = gather_blocks(current.astype(jnp.bfloat16), wide, False)
+            pieces, new_blocks = gather_blocks(current.astype(jnp.bfloat16), wide, True)
             newer[moment] = jnp.concatenate(pieces)
             if recent is None:
                 recent = tiles_by_lag(

time: 67.3 us -> 65.4 us (0.972)
  waiting for transfers between devices: 30.7 us -> 29.2 us
    ppermute x6 -> x0, waiting for transfers between devices: 12.6 us -> none  [slab_stage(): parts.append(lax.ppermute(stack, 'wide', [(d, d ^ m) for d in range(wide)]))]
    ppermute x1 -> x3, waiting for transfers between devices: 11.4 us -> 20 us  [slab_stage(): across = lax.ppermute(stack, 'wide', [(d, d ^ 2) for d in range(wide)])]
    ppermute x6 -> x0, starting transfers between devices: 3.87 us -> none  [slab_stage(): parts.append(lax.ppermute(stack, 'wide', [(d, d ^ m) for d in range(wide)]))]
    ppermute x1 -> x3, starting transfers between devices: 1.58 us -> 4.74 us  [slab_stage(): across = lax.ppermute(stack, 'wide', [(d, d ^ 2) for d in range(wide)])]
    ppermute x1 -> x3, waiting for transfers between devices: 0.01 us -> 2.59 us  [slab_stage(): diagonal = lax.ppermute(across, 'wide', [(d, d ^ 1) for d in range(wide)])]
where the time goes in v8:
time: 65.4 us; the launch traced here: 65.2 us
  waiting for transfers between devices  29.2 us (45%)
  starting transfers between devices  22.4 us (34%)
  matrix products  5.8 us (9%)
  local copies, waits for them, and re-layouts  4.34 us (7%)
  other arithmetic  3.07 us (5%)
    ppermute x3, waiting for transfers between devices, slab_stage(): across = lax.ppermute(stack, 'wide', [(d, d ^ 2) for d in range(wide)])  20 us
    ppermute x9, starting transfers between devices, line_stage(): parts.append(lax.ppermute(x, 'wide', pairs))  17.5 us
    ppermute x9, waiting for transfers between devices, line_stage(): parts.append(lax.ppermute(x, 'wide', pairs))  6.64 us
    dot_general x15, matrix products, rowwise(): return jnp.einsum(spec, tiles, currents, preferred_element_type=jnp.float32)  4.94 us
    ppermute x3, starting transfers between devices, slab_stage(): across = lax.ppermute(stack, 'wide', [(d, d ^ 2) for d in range(wide)])  4.74 us
    ppermute x3, waiting for transfers between devices, slab_stage(): diagonal = lax.ppermute(across, 'wide', [(d, d ^ 1) for d in range(wide)])  2.59 us
    sort x1, other arithmetic, per_device(): column_of_block = jnp.argsort(block_owner)  1.9 us
  transfers between devices with their start and end apart: 18, of which 10 were waited for; matrix products, arithmetic and copies ran while one was open for 14% of the time, Pallas kernels for 0%

profile of v8, /device:TPU:0, one launch (start us, length us, event | category | flops | bytes accessed | tf_op | source)
XLA Modules:
  0.0 65.2 jit_solution(16241818880055242410)
XLA Ops:
  0.0 3.0 %collective-permute-start = (bf16[4,128,128]{2,1,0:T(8,128)(2,1)}, bf16[4,128,128]{2,1,0:T(8,128)(2,1)S(1)}, u32[]{:S(2)}, u32[]{:S(2)}) collective-permute-start(bf16[4,128,128]{2,1,0:T(8,128)(2,1)} %param.19), channel_id=1, source_target_pairs={{0,4},{1,5},{2,6},{3,7},{4,8},{5,9},{6,10},{7,11},{8,12},{9,13},{1... | collective-permute-start | bytes 393224 | tf_op jit(solution)/shard_map/ppermute | solution.py:25
  3.0 2.6 %collective-permute-start.1 = (bf16[4,128,128]{2,1,0:T(8,128)(2,1)}, bf16[4,128,128]{2,1,0:T(8,128)(2,1)S(1)}, u32[]{:S(2)}, u32[]{:S(2)}) collective-permute-start(bf16[4,128,128]{2,1,0:T(8,128)(2,1)} %param.19), channel_id=1, source_target_pairs={{0,8},{1,9},{2,10},{3,11},{4,12},{5,13},{6,14},{7,15},{8,0},{9,1},... | collective-permute-start | bytes 393224 | tf_op jit(solution)/shard_map/ppermute | solution.py:25
  5.6 1.3 %collective-permute-start.2 = (bf16[4,128,128]{2,1,0:T(8,128)(2,1)}, bf16[4,128,128]{2,1,0:T(8,128)(2,1)S(1)}, u32[]{:S(2)}, u32[]{:S(2)}) collective-permute-start(bf16[4,128,128]{2,1,0:T(8,128)(2,1)} %param.19), channel_id=1, source_target_pairs={{0,12},{1,13},{2,14},{3,15},{4,0},{5,1},{6,2},{7,3},{8,4},{9,5},{1... | collective-permute-start | bytes 393224 | tf_op jit(solution)/shard_map/ppermute | solution.py:25
  7.2 1.9 %sort.17 = (s32[16]{0:T(128)}, s32[16]{0:T(128)S(1)}) sort(s32[16]{0:T(128)} %param.18, s32[16]{0:T(128)S(1)} %iota.5), dimensions={0}, to_apply=%region_0.0 | sort | flops 64 | bytes 256 | tf_op jit(solution)/shard_map/jit(argsort)/sort | solution.py:85
  9.1 0.7 %gather_fusion = s32[16]{0:T(128)S(1)} fusion(s32[16]{0:T(128)S(1)} %get-tuple-element.8, s32[1024]{0:T(1024)S(1)} %pad_clamp_fusion.1), kind=kCustom, calls=%fused_computation.clone | custom fusion | bytes 192 | tf_op jit(solution)/shard_map/jit(_take)/gather | solution.py:60
  9.7 0.8 %copy.18 = s32[16,2]{1,0:T(8,128)S(1)} copy(s32[16,2]{0,1:T(2,128)} %bitcast.198) | data formatting | bytes 256 | tf_op jit(solution)/shard_map/squeeze | solution.py:62
  10.5 0.7 %gather_fusion.2 = bf16[16,2,128,128]{3,2,1,0:T(8,128)(2,1)S(1)} fusion(bf16[16,2,128,128]{3,2,1,0:T(8,128)(2,1)S(1)} %bitcast.179, s32[1024]{0:T(1024)S(1)} %pad_clamp_fusion), kind=kCustom, calls=%fused_computation.2.clone | custom fusion | bytes 2097216 | tf_op jit(solution)/shard_map/jit(_take)/gather | solution.py:61
  11.3 0.6 gather_fusion.1
  12.3 0.3 bitcast_select_fusion.3
  12.6 1.8 %collective-permute-done.1 = bf16[4,128,128]{2,1,0:T(8,128)(2,1)S(1)} collective-permute-done((bf16[4,128,128]{2,1,0:T(8,128)(2,1)}, bf16[4,128,128]{2,1,0:T(8,128)(2,1)S(1)}, u32[]{:S(2)}, u32[]{:S(2)}) %collective-permute-start.1) | collective-permute-done | bytes 131104 | tf_op jit(solution)/shard_map/ppermute | solution.py:25
  14.5 1.6 %collective-permute-start.4 = (bf16[4,4,128,128]{3,2,1,0:T(8,128)(2,1)S(1)}, bf16[4,4,128,128]{3,2,1,0:T(8,128)(2,1)S(1)}, u32[]{:S(2)}, u32[]{:S(2)}) collective-permute-start(bf16[4,4,128,128]{3,2,1,0:T(8,128)(2,1)S(1)} %pad_maximum_fusion.3), channel_id=1, source_target_pairs={{0,2},{1,3},{2,0},{3,1},{4,6},{5,7},{6,4},{7,5},{8,10},{9,11},{10,... | collective-permute-start | bytes 1572872 | tf_op jit(solution)/shard_map/ppermute | solution.py:33
  16.4 0.3 convolution_bitcast_fusion.7
  16.7 0.3 convolution_bitcast_fusion.11
  17.0 11.4 %collective-permute-done.4 = bf16[4,4,128,128]{3,2,1,0:T(8,128)(2,1)S(1)} collective-permute-done((bf16[4,4,128,128]{3,2,1,0:T(8,128)(2,1)S(1)}, bf16[4,4,128,128]{3,2,1,0:T(8,128)(2,1)S(1)}, u32[]{:S(2)}, u32[]{:S(2)}) %collective-permute-start.4) | collective-permute-done | bytes 524320 | tf_op jit(solution)/shard_map/ppermute | solution.py:33
  28.4 0.3 convolution_bitcast_fusion.5
  28.7 0.4 convolution_bitcast_fusion.1
  29.1 0.3 convolution_bitcast_fusion.2
  29.4 0.3 convolution_bitcast_fusion.9
  29.7 0.3 fusion.7
  30.0 0.4 fusion.12
  30.4 0.5 copy-done.3
  31.0 0.3 fusion.14
  31.3 0.3 constant_dynamic-update-slice_fusion.6
  31.6 3.4 %collective-permute-start.6 = (bf16[128,128]{0,1:T(8,128)(2,1)S(1)}, bf16[128,128]{0,1:T(8,128)(2,1)S(1)}, u32[]{:S(2)}, u32[]{:S(2)}) collective-permute-start(bf16[128,128]{0,1:T(8,128)(2,1)S(1)} %get-tuple-element.21), channel_id=1, source_target_pairs={{0,4},{1,5},{2,6},{3,7},{4,8},{5,9},{6,10},{7,11},{8,12},{9,13},{1... | collective-permute-start | bytes 98312 | tf_op jit(solution)/shard_map/ppermute | solution.py:25
  35.0 0.6 collective-permute-start.7
  35.6 1.9 %collective-permute-start.8 = (bf16[128,128]{0,1:T(8,128)(2,1)S(1)}, bf16[128,128]{0,1:T(8,128)(2,1)S(1)}, u32[]{:S(2)}, u32[]{:S(2)}) collective-permute-start(bf16[128,128]{0,1:T(8,128)(2,1)S(1)} %get-tuple-element.21), channel_id=1, source_target_pairs={{0,12},{1,13},{2,14},{3,15},{4,0},{5,1},{6,2},{7,3},{8,4},{9,5},{1... | collective-permute-start | bytes 98312 | tf_op jit(solution)/shard_map/ppermute | solution.py:25
  37.5 0.3 fusion.1
  37.8 2.4 %collective-permute-done.7 = bf16[128,128]{0,1:T(8,128)(2,1)S(1)} collective-permute-done((bf16[128,128]{0,1:T(8,128)(2,1)S(1)}, bf16[128,128]{0,1:T(8,128)(2,1)S(1)}, u32[]{:S(2)}, u32[]{:S(2)}) %collective-permute-start.7) | collective-permute-done | bytes 32800 | tf_op jit(solution)/shard_map/ppermute | solution.py:25
  40.3 1.6 %collective-permute-start.10 = (bf16[4,128,128]{1,2,0:T(8,128)(2,1)S(1)}, bf16[4,128,128]{1,2,0:T(8,128)(2,1)S(1)}, u32[]{:S(2)}, u32[]{:S(2)}) collective-permute-start(bf16[4,128,128]{1,2,0:T(8,128)(2,1)S(1)} %pad_maximum_fusion.5), channel_id=1, source_target_pairs={{0,2},{1,3},{2,0},{3,1},{4,6},{5,7},{6,4},{7,5},{8,10},{9,11},{10,... | collective-permute-start | bytes 393224 | tf_op jit(solution)/shard_map/ppermute | solution.py:33
  41.9 4.3 %collective-permute-done.10 = bf16[4,128,128]{1,2,0:T(8,128)(2,1)S(1)} collective-permute-done((bf16[4,128,128]{1,2,0:T(8,128)(2,1)S(1)}, bf16[4,128,128]{1,2,0:T(8,128)(2,1)S(1)}, u32[]{:S(2)}, u32[]{:S(2)}) %collective-permute-start.10) | collective-permute-done | bytes 131104 | tf_op jit(solution)/shard_map/ppermute | solution.py:33
  46.3 1.3 %collective-permute-done.11 = bf16[4,128,128]{1,2,0:T(8,128)(2,1)S(1)} collective-permute-done((bf16[4,128,128]{1,2,0:T(8,128)(2,1)S(1)}, bf16[4,128,128]{1,2,0:T(8,128)(2,1)S(1)}, u32[]{:S(2)}, u32[]{:S(2)}) %collective-permute-start.11) | collective-permute-done | bytes 131104 | tf_op jit(solution)/shard_map/ppermute | solution.py:35
  47.6 0.3 convolution_bitcast_fusion.15
  47.9 0.3 fusion.10
  48.2 0.3 constant_dynamic-update-slice_fusion.13
  48.5 1.1 %collective-permute-start.12 = (bf16[128,128]{0,1:T(8,128)(2,1)S(1)}, bf16[128,128]{0,1:T(8,128)(2,1)S(1)}, u32[]{:S(2)}, u32[]{:S(2)}) collective-permute-start(bf16[128,128]{0,1:T(8,128)(2,1)S(1)} %get-tuple-element.19), channel_id=1, source_target_pairs={{0,4},{1,5},{2,6},{3,7},{4,8},{5,9},{6,10},{7,11},{8,12},{9,13},{1... | collective-permute-start | bytes 98312 | tf_op jit(solution)/shard_map/ppermute | solution.py:25
  49.6 2.6 %collective-permute-start.13 = (bf16[128,128]{0,1:T(8,128)(2,1)S(1)}, bf16[128,128]{0,1:T(8,128)(2,1)S(1)}, u32[]{:S(2)}, u32[]{:S(2)}) collective-permute-start(bf16[128,128]{0,1:T(8,128)(2,1)S(1)} %get-tuple-element.19), channel_id=1, source_target_pairs={{0,8},{1,9},{2,10},{3,11},{4,12},{5,13},{6,14},{7,15},{8,0},{9,1},... | collective-permute-start | bytes 98312 | tf_op jit(solution)/shard_map/ppermute | solution.py:25
  52.1 1.0 %collective-permute-start.14 = (bf16[128,128]{0,1:T(8,128)(2,1)S(1)}, bf16[128,128]{0,1:T(8,128)(2,1)S(1)}, u32[]{:S(2)}, u32[]{:S(2)}) collective-permute-start(bf16[128,128]{0,1:T(8,128)(2,1)S(1)} %get-tuple-element.19), channel_id=1, source_target_pairs={{0,12},{1,13},{2,14},{3,15},{4,0},{5,1},{6,2},{7,3},{8,4},{9,5},{1... | collective-permute-start | bytes 98312 | tf_op jit(solution)/shard_map/ppermute | solution.py:25
  53.2 0.5 convolution_bitcast_fusion.13
  53.7 0.8 %collective-permute-done.12 = bf16[128,128]{0,1:T(8,128)(2,1)S(1)} collective-permute-done((bf16[128,128]{0,1:T(8,128)(2,1)S(1)}, bf16[128,128]{0,1:T(8,128)(2,1)S(1)}, u32[]{:S(2)}, u32[]{:S(2)}) %collective-permute-start.12) | collective-permute-done | bytes 32800 | tf_op jit(solution)/shard_map/ppermute | solution.py:25
  54.5 0.7 %collective-permute-done.13 = bf16[128,128]{0,1:T(8,128)(2,1)S(1)} collective-permute-done((bf16[128,128]{0,1:T(8,128)(2,1)S(1)}, bf16[128,128]{0,1:T(8,128)(2,1)S(1)}, u32[]{:S(2)}, u32[]{:S(2)}) %collective-permute-start.13) | collective-permute-done | bytes 32800 | tf_op jit(solution)/shard_map/ppermute | solution.py:25
  55.2 0.9 %collective-permute-done.14 = bf16[128,128]{0,1:T(8,128)(2,1)S(1)} collective-permute-done((bf16[128,128]{0,1:T(8,128)(2,1)S(1)}, bf16[128,128]{0,1:T(8,128)(2,1)S(1)}, u32[]{:S(2)}, u32[]{:S(2)}) %collective-permute-start.14) | collective-permute-done | bytes 32800 | tf_op jit(solution)/shard_map/ppermute | solution.py:25
  56.2 1.6 %collective-permute-start.16 = (bf16[4,128,128]{1,2,0:T(8,128)(2,1)S(1)}, bf16[4,128,128]{1,2,0:T(8,128)(2,1)S(1)}, u32[]{:S(2)}, u32[]{:S(2)}) collective-permute-start(bf16[4,128,128]{1,2,0:T(8,128)(2,1)S(1)} %pad_maximum_fusion.6), channel_id=1, source_target_pairs={{0,2},{1,3},{2,0},{3,1},{4,6},{5,7},{6,4},{7,5},{8,10},{9,11},{10,... | collective-permute-start | bytes 393224 | tf_op jit(solution)/shard_map/ppermute | solution.py:33
  57.8 4.3 %collective-permute-done.16 = bf16[4,128,128]{1,2,0:T(8,128)(2,1)S(1)} collective-permute-done((bf16[4,128,128]{1,2,0:T(8,128)(2,1)S(1)}, bf16[4,128,128]{1,2,0:T(8,128)(2,1)S(1)}, u32[]{:S(2)}, u32[]{:S(2)}) %collective-permute-start.16) | collective-permute-done | bytes 131104 | tf_op jit(solution)/shard_map/ppermute | solution.py:33
  62.1 1.3 %collective-permute-done.17 = bf16[4,128,128]{1,2,0:T(8,128)(2,1)S(1)} collective-permute-done((bf16[4,128,128]{1,2,0:T(8,128)(2,1)S(1)}, bf16[4,128,128]{1,2,0:T(8,128)(2,1)S(1)}, u32[]{:S(2)}, u32[]{:S(2)}) %collective-permute-start.17) | collective-permute-done | bytes 131104 | tf_op jit(solution)/shard_map/ppermute | solution.py:35
  63.4 0.3 convolution_bitcast_fusion.14
  63.8 0.3 fusion.5
  64.1 0.3 convolution_bitcast_fusion.12
  64.4 0.8 %copy.24 = f32[3,128,128]{2,1,0:T(8,128)} copy(f32[3,128,128]{1,2,0:T(8,128)S(1)} %pad_maximum_fusion.4) | data formatting | bytes 393216 | tf_op jit(solution)/shard_map/stack | solution.py:127
  (49 shorter events, 1.4 us)
Async XLA Ops:
  0.0 10.5 %copy-start = (bf16[1,16,2,128,128]{4,3,2,1,0:T(8,128)(2,1)S(1)}, bf16[1,16,2,128,128]{4,3,2,1,0:T(8,128)(2,1)}, u32[]{:S(2)}) copy-start(bf16[1,16,2,128,128]{4,3,2,1,0:T(8,128)(2,1)} %param.16) | copy-start | bytes 3145732
  0.0 12.6 %collective-permute-start = (bf16[4,128,128]{2,1,0:T(8,128)(2,1)}, bf16[4,128,128]{2,1,0:T(8,128)(2,1)S(1)}, u32[]{:S(2)}, u32[]{:S(2)}) collective-permute-start(bf16[4,128,128]{2,1,0:T(8,128)(2,1)} %param.19), channel_id=1, source_target_pairs={{0,4},{1,5},{2,6},{3,7},{4,8},{5,9},{6,10},{7,11},{8,12},{9,13},{1... | collective-permute-start | bytes 393224 | tf_op jit(solution)/shard_map/ppermute | solution.py:25
  3.0 11.4 %collective-permute-start.1 = (bf16[4,128,128]{2,1,0:T(8,128)(2,1)}, bf16[4,128,128]{2,1,0:T(8,128)(2,1)S(1)}, u32[]{:S(2)}, u32[]{:S(2)}) collective-permute-start(bf16[4,128,128]{2,1,0:T(8,128)(2,1)} %param.19), channel_id=1, source_target_pairs={{0,8},{1,9},{2,10},{3,11},{4,12},{5,13},{6,14},{7,15},{8,0},{9,1},... | collective-permute-start | bytes 393224 | tf_op jit(solution)/shard_map/ppermute | solution.py:25
  5.6 8.9 %collective-permute-start.2 = (bf16[4,128,128]{2,1,0:T(8,128)(2,1)}, bf16[4,128,128]{2,1,0:T(8,128)(2,1)S(1)}, u32[]{:S(2)}, u32[]{:S(2)}) collective-permute-start(bf16[4,128,128]{2,1,0:T(8,128)(2,1)} %param.19), channel_id=1, source_target_pairs={{0,12},{1,13},{2,14},{3,15},{4,0},{5,1},{6,2},{7,3},{8,4},{9,5},{1... | collective-permute-start | bytes 393224 | tf_op jit(solution)/shard_map/ppermute | solution.py:25
  12.3 2.1 %copy-start.2 = (bf16[4,128,128]{2,1,0:T(8,128)(2,1)S(1)}, bf16[4,128,128]{2,1,0:T(8,128)(2,1)}, u32[]{:S(2)}) copy-start(bf16[4,128,128]{2,1,0:T(8,128)(2,1)} %param.19) | copy-start | bytes 393220
  14.5 13.8 %collective-permute-start.4 = (bf16[4,4,128,128]{3,2,1,0:T(8,128)(2,1)S(1)}, bf16[4,4,128,128]{3,2,1,0:T(8,128)(2,1)S(1)}, u32[]{:S(2)}, u32[]{:S(2)}) collective-permute-start(bf16[4,4,128,128]{3,2,1,0:T(8,128)(2,1)S(1)} %pad_maximum_fusion.3), channel_id=1, source_target_pairs={{0,2},{1,3},{2,0},{3,1},{4,6},{5,7},{6,4},{7,5},{8,10},{9,11},{10,... | collective-permute-start | bytes 1572872 | tf_op jit(solution)/shard_map/ppermute | solution.py:33
  16.3 12.8 %collective-permute-start.3 = (bf16[4,4,128,128]{3,2,1,0:T(8,128)(2,1)S(1)}, bf16[4,4,128,128]{3,2,1,0:T(8,128)(2,1)S(1)}, u32[]{:S(2)}, u32[]{:S(2)}) collective-permute-start(bf16[4,4,128,128]{3,2,1,0:T(8,128)(2,1)S(1)} %pad_maximum_fusion.3), channel_id=1, source_target_pairs={{0,1},{1,0},{2,3},{3,2},{4,5},{5,4},{6,7},{7,6},{8,9},{9,8},{10,11... | collective-permute-start | bytes 1572872 | tf_op jit(solution)/shard_map/ppermute | solution.py:34
  28.4 2.0 %collective-permute-start.5 = (bf16[4,4,128,128]{3,2,1,0:T(8,128)(2,1)S(1)}, bf16[4,4,128,128]{3,2,1,0:T(8,128)(2,1)S(1)}, u32[]{:S(2)}, u32[]{:S(2)}) collective-permute-start(bf16[4,4,128,128]{3,2,1,0:T(8,128)(2,1)S(1)} %collective-permute-done.4), channel_id=1, source_target_pairs={{0,1},{1,0},{2,3},{3,2},{4,5},{5,4},{6,7},{7,6},{8,9},{9,8},{10,11... | collective-permute-start | bytes 1572872 | tf_op jit(solution)/shard_map/ppermute | solution.py:35
  30.0 0.9 %copy-start.3 = (f32[3,128,128]{2,1,0:T(8,128)S(1)}, f32[3,128,128]{2,1,0:T(8,128)}, u32[]{:S(2)}) copy-start(f32[3,128,128]{2,1,0:T(8,128)} %param.20) | copy-start | bytes 589828
  30.4 0.9 %copy-start.1 = (f32[1,128,128]{2,1,0:T(8,128)S(1)}, f32[1,128,128]{2,1,0:T(8,128)}, u32[]{:S(2)}) copy-start(f32[1,128,128]{2,1,0:T(8,128)} %param.21) | copy-start | bytes 196612
  31.6 6.1 %collective-permute-start.6 = (bf16[128,128]{0,1:T(8,128)(2,1)S(1)}, bf16[128,128]{0,1:T(8,128)(2,1)S(1)}, u32[]{:S(2)}, u32[]{:S(2)}) collective-permute-start(bf16[128,128]{0,1:T(8,128)(2,1)S(1)} %get-tuple-element.21), channel_id=1, source_target_pairs={{0,4},{1,5},{2,6},{3,7},{4,8},{5,9},{6,10},{7,11},{8,12},{9,13},{1... | collective-permute-start | bytes 98312 | tf_op jit(solution)/shard_map/ppermute | solution.py:25
  35.0 5.2 %collective-permute-start.7 = (bf16[128,128]{0,1:T(8,128)(2,1)S(1)}, bf16[128,128]{0,1:T(8,128)(2,1)S(1)}, u32[]{:S(2)}, u32[]{:S(2)}) collective-permute-start(bf16[128,128]{0,1:T(8,128)(2,1)S(1)} %get-tuple-element.21), channel_id=1, source_target_pairs={{0,8},{1,9},{2,10},{3,11},{4,12},{5,13},{6,14},{7,15},{8,0},{9,1},... | collective-permute-start | bytes 98312 | tf_op jit(solution)/shard_map/ppermute | solution.py:25
  35.6 4.6 %collective-permute-start.8 = (bf16[128,128]{0,1:T(8,128)(2,1)S(1)}, bf16[128,128]{0,1:T(8,128)(2,1)S(1)}, u32[]{:S(2)}, u32[]{:S(2)}) collective-permute-start(bf16[128,128]{0,1:T(8,128)(2,1)S(1)} %get-tuple-element.21), channel_id=1, source_target_pairs={{0,12},{1,13},{2,14},{3,15},{4,0},{5,1},{6,2},{7,3},{8,4},{9,5},{1... | collective-permute-start | bytes 98312 | tf_op jit(solution)/shard_map/ppermute | solution.py:25
  40.2 6.0 %collective-permute-start.9 = (bf16[4,128,128]{1,2,0:T(8,128)(2,1)S(1)}, bf16[4,128,128]{1,2,0:T(8,128)(2,1)S(1)}, u32[]{:S(2)}, u32[]{:S(2)}) collective-permute-start(bf16[4,128,128]{1,2,0:T(8,128)(2,1)S(1)} %pad_maximum_fusion.5), channel_id=1, source_target_pairs={{0,1},{1,0},{2,3},{3,2},{4,5},{5,4},{6,7},{7,6},{8,9},{9,8},{10,11... | collective-permute-start | bytes 393224 | tf_op jit(solution)/shard_map/ppermute | solution.py:34
  40.3 5.9 %collective-permute-start.10 = (bf16[4,128,128]{1,2,0:T(8,128)(2,1)S(1)}, bf16[4,128,128]{1,2,0:T(8,128)(2,1)S(1)}, u32[]{:S(2)}, u32[]{:S(2)}) collective-permute-start(bf16[4,128,128]{1,2,0:T(8,128)(2,1)S(1)} %pad_maximum_fusion.5), channel_id=1, source_target_pairs={{0,2},{1,3},{2,0},{3,1},{4,6},{5,7},{6,4},{7,5},{8,10},{9,11},{10,... | collective-permute-start | bytes 393224 | tf_op jit(solution)/shard_map/ppermute | solution.py:33
  46.2 1.3 %collective-permute-start.11 = (bf16[4,128,128]{1,2,0:T(8,128)(2,1)S(1)}, bf16[4,128,128]{1,2,0:T(8,128)(2,1)S(1)}, u32[]{:S(2)}, u32[]{:S(2)}) collective-permute-start(bf16[4,128,128]{1,2,0:T(8,128)(2,1)S(1)} %collective-permute-done.10), channel_id=1, source_target_pairs={{0,1},{1,0},{2,3},{3,2},{4,5},{5,4},{6,7},{7,6},{8,9},{9,8},{10,11... | collective-permute-start | bytes 393224 | tf_op jit(solution)/shard_map/ppermute | solution.py:35
  48.5 6.0 %collective-permute-start.12 = (bf16[128,128]{0,1:T(8,128)(2,1)S(1)}, bf16[128,128]{0,1:T(8,128)(2,1)S(1)}, u32[]{:S(2)}, u32[]{:S(2)}) collective-permute-start(bf16[128,128]{0,1:T(8,128)(2,1)S(1)} %get-tuple-element.19), channel_id=1, source_target_pairs={{0,4},{1,5},{2,6},{3,7},{4,8},{5,9},{6,10},{7,11},{8,12},{9,13},{1... | collective-permute-start | bytes 98312 | tf_op jit(solution)/shard_map/ppermute | solution.py:25
  49.6 5.6 %collective-permute-start.13 = (bf16[128,128]{0,1:T(8,128)(2,1)S(1)}, bf16[128,128]{0,1:T(8,128)(2,1)S(1)}, u32[]{:S(2)}, u32[]{:S(2)}) collective-permute-start(bf16[128,128]{0,1:T(8,128)(2,1)S(1)} %get-tuple-element.19), channel_id=1, source_target_pairs={{0,8},{1,9},{2,10},{3,11},{4,12},{5,13},{6,14},{7,15},{8,0},{9,1},... | collective-permute-start | bytes 98312 | tf_op jit(solution)/shard_map/ppermute | solution.py:25
  52.1 3.9 %collective-permute-start.14 = (bf16[128,128]{0,1:T(8,128)(2,1)S(1)}, bf16[128,128]{0,1:T(8,128)(2,1)S(1)}, u32[]{:S(2)}, u32[]{:S(2)}) collective-permute-start(bf16[128,128]{0,1:T(8,128)(2,1)S(1)} %get-tuple-element.19), channel_id=1, source_target_pairs={{0,12},{1,13},{2,14},{3,15},{4,0},{5,1},{6,2},{7,3},{8,4},{9,5},{1... | collective-permute-start | bytes 98312 | tf_op jit(solution)/shard_map/ppermute | solution.py:25
  56.1 6.0 %collective-permute-start.15 = (bf16[4,128,128]{1,2,0:T(8,128)(2,1)S(1)}, bf16[4,128,128]{1,2,0:T(8,128)(2,1)S(1)}, u32[]{:S(2)}, u32[]{:S(2)}) collective-permute-start(bf16[4,128,128]{1,2,0:T(8,128)(2,1)S(1)} %pad_maximum_fusion.6), channel_id=1, source_target_pairs={{0,1},{1,0},{2,3},{3,2},{4,5},{5,4},{6,7},{7,6},{8,9},{9,8},{10,11... | collective-permute-start | bytes 393224 | tf_op jit(solution)/shard_map/ppermute | solution.py:34
  56.2 5.9 %collective-permute-start.16 = (bf16[4,128,128]{1,2,0:T(8,128)(2,1)S(1)}, bf16[4,128,128]{1,2,0:T(8,128)(2,1)S(1)}, u32[]{:S(2)}, u32[]{:S(2)}) collective-permute-start(bf16[4,128,128]{1,2,0:T(8,128)(2,1)S(1)} %pad_maximum_fusion.6), channel_id=1, source_target_pairs={{0,2},{1,3},{2,0},{3,1},{4,6},{5,7},{6,4},{7,5},{8,10},{9,11},{10,... | collective-permute-start | bytes 393224 | tf_op jit(solution)/shard_map/ppermute | solution.py:33
  62.1 1.3 %collective-permute-start.17 = (bf16[4,128,128]{1,2,0:T(8,128)(2,1)S(1)}, bf16[4,128,128]{1,2,0:T(8,128)(2,1)S(1)}, u32[]{:S(2)}, u32[]{:S(2)}) collective-permute-start(bf16[4,128,128]{1,2,0:T(8,128)(2,1)S(1)} %collective-permute-done.16), channel_id=1, source_target_pairs={{0,1},{1,0},{2,3},{3,2},{4,5},{5,4},{6,7},{7,6},{8,9},{9,8},{10,11... | collective-permute-start | bytes 393224 | tf_op jit(solution)/shard_map/ppermute | solution.py:35

commit v9 on v6

--- a/solution.py
+++ b/solution.py
@@ -32,33 +32,40 @@
     return lax.ppermute(x, "wide", [(d, d ^ mask) for d in range(wide)])
 
 
+def slab_stage(parts, wide, inner, early):
+    stack = parts[0] if len(parts) == 1 else jnp.concatenate(parts)
+    if inner != 4:
+        return [stack] + [swap(stack, wide, m) for m in range(1, inner)]
+    if early and len(parts) > 1:
+        rest = jnp.concatenate(parts[1:])
+        across_own = swap(parts[0], wide, 2)
+        across_rest = swap(rest, wide, 2)
+        return [
+            stack,
+            swap(stack, wide, 1),
+            across_own,
+            across_rest,
+            swap(across_own, wide, 1),
+            swap(across_rest, wide, 1),
+        ]
+    across = swap(stack, wide, 2)
+    return [stack, swap(stack, wide, 1), across, swap(across, wide, 1)]
+
+
 def gather_blocks(x, wide, early):
     inner = inner_size(wide)
     lines = wide // inner
     parts, shifted = line_stage(x, wide, inner)
-    own = parts[0] if len(parts) == 1 else jnp.concatenate(parts)
-    every = list(range(lines))
-    pieces = [(own, 0, every)]
-    if early and inner == 4 and len(parts) > 1:
-        rest = jnp.concatenate(parts[1:])
-        across_own = swap(parts[0], wide, 2)
-        across_rest = swap(rest, wide, 2)
-        pieces += [
-            (swap(own, wide, 1), 1, every),
-            (across_own, 2, every[:1]),
-            (across_rest, 2, every[1:]),
-            (swap(across_own, wide, 1), 3, every[:1]),
-            (swap(across_rest, wide, 1), 3, every[1:]),
-        ]
-    else:
-        pieces += [(swap(own, wide, m), m, every) for m in range(1, inner)]
+    pieces = slab_stage(parts, wide, inner, early)
     me = lax.axis_index("wide")
     line = np.arange(lines, dtype=np.int32)
     source_line = (me // inner - line) % lines if shifted else jnp.asarray(line)
-    blocks = jnp.concatenate(
-        [source_line[np.array(held)] * inner + jnp.bitwise_xor(me % inner, m) for _, m, held in pieces]
+    masks = np.arange(inner, dtype=np.int32)
+    blocks = (
+        source_line[None, :] * inner
+        + jnp.bitwise_xor(me % inner, jnp.asarray(masks))[:, None]
     )
-    return [piece for piece, _, _ in pieces], blocks
+    return pieces, blocks.reshape(wide)
 
 
 def tiles_by_lag(retarded_tiles, tile_lags, column_of_block, block_of_slot, lags_wanted):

time: 78.1 us -> 63.5 us (0.81)
  other arithmetic: 11.5 us -> 3.12 us
  local copies, waits for them, and re-layouts: 12.3 us -> 4.41 us
  starting transfers between devices: 21.4 us -> 24.5 us
  waiting for transfers between devices: 25.2 us -> 24 us
    another operation x4 -> x0, other arithmetic: 3.21 us -> none  [tiles_by_lag(): jnp.stack([jnp.where((lags[:, 0] == lag)[:, None, None], tiles[:, 0], jnp...]
    ppermute x9, starting transfers between devices: 14.8 us -> 17.5 us  [line_stage(): parts.append(lax.ppermute(x, 'wide', pairs)[None])]
    concatenate x4, other arithmetic: 1.96 us -> 0.15 us  [the longest x3 0.11 us: slab_stage(): stack = parts[0] if len(parts) == 1 else jnp.concatenate(parts)]
    gather x2 -> x1, local copies, waits for them, and re-layouts: 2.4 us -> 0.75 us  [tiles_by_lag(): tiles = jnp.take(retarded_tiles[0], columns, axis=0)]
    unnamed x44 -> x18, local copies, waits for them, and re-layouts: 2.06 us -> 0.76 us
    gather x2 -> x0, local copies, waits for them, and re-layouts: 1.28 us -> none  [gather_blocks(): source_line[np.array(held)] * inner + jnp.bitwise_xor(me % inner, m)]
    slice x2 -> x0, local copies, waits for them, and re-layouts: 1.24 us -> none  [per_device(): by_lag[offsets[m]:offsets[m + 1], first - 1:]]
    gather x2 -> x1, local copies, waits for them, and re-layouts: 1.89 us -> 0.66 us  [tiles_by_lag(): columns = jnp.take(column_of_block, block_of_slot, axis=0)]
  transfers between devices with their start and end apart: 20 -> 20, of which waited for: 10 -> 10; matrix products, arithmetic and copies ran while one was open for 33% -> 17% of each run, Pallas kernels for 0% -> 0%
where the time goes in v9:
time: 63.5 us; the launch traced here: 63.3 us
  starting transfers between devices  24.5 us (39%)
  waiting for transfers between devices  24 us (38%)
  matrix products  6.95 us (11%)
  local copies, waits for them, and re-layouts  4.41 us (7%)
  other arithmetic  3.12 us (5%)
    ppermute x11, waiting for transfers between devices, swap(): return lax.ppermute(x, 'wide', [(d, d ^ mask) for d in range(wide)])  19.3 us
    ppermute x9, starting transfers between devices, line_stage(): parts.append(lax.ppermute(x, 'wide', pairs)[None])  17.5 us
    ppermute x11, starting transfers between devices, swap(): return lax.ppermute(x, 'wide', [(d, d ^ mask) for d in range(wide)])  7.05 us
    dot_general x21, matrix products, rowwise(): return jnp.einsum(spec, tiles, currents, preferred_element_type=jnp.float32)  6.09 us
    ppermute x9, waiting for transfers between devices, line_stage(): parts.append(lax.ppermute(x, 'wide', pairs)[None])  4.67 us
    sort x1, other arithmetic, per_device(): column_of_block = jnp.argsort(block_owner)  1.9 us
  transfers between devices with their start and end apart: 20, of which 10 were waited for; matrix products, arithmetic and copies ran while one was open for 17% of the time, Pallas kernels for 0%

profile of v9, /device:TPU:0, one launch (start us, length us, event | category | flops | bytes accessed | tf_op | source)
XLA Modules:
  0.0 63.3 jit_solution(6213240440445635578)
XLA Ops:
  0.0 3.0 %collective-permute-start = (bf16[4,128,128]{2,1,0:T(8,128)(2,1)}, bf16[4,128,128]{2,1,0:T(8,128)(2,1)S(1)}, u32[]{:S(2)}, u32[]{:S(2)}) collective-permute-start(bf16[4,128,128]{2,1,0:T(8,128)(2,1)} %param.19), channel_id=1, source_target_pairs={{0,4},{1,5},{2,6},{3,7},{4,8},{5,9},{6,10},{7,11},{8,12},{9,13},{1... | collective-permute-start | bytes 393224 | tf_op jit(solution)/shard_map/ppermute | solution.py:25
  3.0 2.6 %collective-permute-start.1 = (bf16[4,128,128]{2,1,0:T(8,128)(2,1)}, bf16[4,128,128]{2,1,0:T(8,128)(2,1)S(1)}, u32[]{:S(2)}, u32[]{:S(2)}) collective-permute-start(bf16[4,128,128]{2,1,0:T(8,128)(2,1)} %param.19), channel_id=1, source_target_pairs={{0,8},{1,9},{2,10},{3,11},{4,12},{5,13},{6,14},{7,15},{8,0},{9,1},... | collective-permute-start | bytes 393224 | tf_op jit(solution)/shard_map/ppermute | solution.py:25
  5.6 1.3 %collective-permute-start.2 = (bf16[4,128,128]{2,1,0:T(8,128)(2,1)}, bf16[4,128,128]{2,1,0:T(8,128)(2,1)S(1)}, u32[]{:S(2)}, u32[]{:S(2)}) collective-permute-start(bf16[4,128,128]{2,1,0:T(8,128)(2,1)} %param.19), channel_id=1, source_target_pairs={{0,12},{1,13},{2,14},{3,15},{4,0},{5,1},{6,2},{7,3},{8,4},{9,5},{1... | collective-permute-start | bytes 393224 | tf_op jit(solution)/shard_map/ppermute | solution.py:25
  7.0 1.5 %collective-permute-start.4 = (bf16[1,4,128,128]{3,2,1,0:T(8,128)(2,1)}, bf16[1,4,128,128]{3,2,1,0:T(8,128)(2,1)S(1)}, u32[]{:S(2)}, u32[]{:S(2)}) collective-permute-start(bf16[1,4,128,128]{3,2,1,0:T(8,128)(2,1)} %bitcast.257), channel_id=1, source_target_pairs={{0,2},{1,3},{2,0},{3,1},{4,6},{5,7},{6,4},{7,5},{8,10},{9,11},{10,... | collective-permute-start | bytes 393224 | tf_op jit(solution)/shard_map/ppermute | solution.py:32
  8.7 1.9 %sort.17 = (s32[16]{0:T(128)}, s32[16]{0:T(128)S(1)}) sort(s32[16]{0:T(128)} %param.18, s32[16]{0:T(128)S(1)} %iota.5), dimensions={0}, to_apply=%region_0.0 | sort | flops 64 | bytes 256 | tf_op jit(solution)/shard_map/jit(argsort)/sort | solution.py:97
  10.6 0.7 %gather_fusion = s32[16]{0:T(128)S(1)} fusion(s32[16]{0:T(128)S(1)} %get-tuple-element.8, s32[1024]{0:T(1024)S(1)} %pad_clamp_fusion.1), kind=kCustom, calls=%fused_computation.clone | custom fusion | bytes 192 | tf_op jit(solution)/shard_map/jit(_take)/gather | solution.py:72
  11.3 0.8 %copy.18 = s32[16,2]{1,0:T(8,128)S(1)} copy(s32[16,2]{0,1:T(2,128)} %bitcast.262) | data formatting | bytes 256 | tf_op jit(solution)/shard_map/squeeze | solution.py:74
  12.0 0.7 %gather_fusion.2 = bf16[16,2,128,128]{3,2,1,0:T(8,128)(2,1)S(1)} fusion(bf16[16,2,128,128]{3,2,1,0:T(8,128)(2,1)S(1)} %bitcast.239, s32[1024]{0:T(1024)S(1)} %pad_clamp_fusion), kind=kCustom, calls=%fused_computation.2.clone | custom fusion | bytes 2097216 | tf_op jit(solution)/shard_map/jit(_take)/gather | solution.py:73
  12.8 0.6 gather_fusion.1
  13.6 0.3 compare_reduce_fusion.3
  13.9 0.3 bitcast_select_fusion.3
  14.5 1.6 %collective-permute-start.5 = (bf16[3,4,128,128]{3,2,1,0:T(8,128)(2,1)S(1)}, bf16[3,4,128,128]{3,2,1,0:T(8,128)(2,1)S(1)}, u32[]{:S(2)}, u32[]{:S(2)}) collective-permute-start(bf16[3,4,128,128]{3,2,1,0:T(8,128)(2,1)S(1)} %pad_maximum_fusion.4), channel_id=1, source_target_pairs={{0,2},{1,3},{2,0},{3,1},{4,6},{5,7},{6,4},{7,5},{8,10},{9,11},{10,... | collective-permute-start | bytes 1179656 | tf_op jit(solution)/shard_map/ppermute | solution.py:32
  16.3 0.3 convolution_bitcast_fusion.7
  16.6 0.3 convolution_bitcast_fusion.9
  16.9 0.6 collective-permute-start.6
  17.4 8.1 %collective-permute-done.5 = bf16[3,4,128,128]{3,2,1,0:T(8,128)(2,1)S(1)} collective-permute-done((bf16[3,4,128,128]{3,2,1,0:T(8,128)(2,1)S(1)}, bf16[3,4,128,128]{3,2,1,0:T(8,128)(2,1)S(1)}, u32[]{:S(2)}, u32[]{:S(2)}) %collective-permute-start.5) | collective-permute-done | bytes 393248 | tf_op jit(solution)/shard_map/ppermute | solution.py:32
  25.8 0.3 convolution_bitcast_fusion.5
  26.1 0.3 convolution_bitcast_fusion.3
  26.4 0.3 convolution_bitcast_fusion
  26.8 0.4 fusion.20
  27.1 0.3 fusion.18
  27.4 0.3 fusion.19
  28.4 0.3 convolution_bitcast_fusion.2
  28.8 0.6 copy-done.2
  29.6 0.3 constant_dynamic-update-slice_fusion.6
  29.9 3.4 %collective-permute-start.8 = (bf16[128,128]{0,1:T(8,128)(2,1)S(1)}, bf16[128,128]{0,1:T(8,128)(2,1)S(1)}, u32[]{:S(2)}, u32[]{:S(2)}) collective-permute-start(bf16[128,128]{0,1:T(8,128)(2,1)S(1)} %get-tuple-element.21), channel_id=1, source_target_pairs={{0,4},{1,5},{2,6},{3,7},{4,8},{5,9},{6,10},{7,11},{8,12},{9,13},{1... | collective-permute-start | bytes 98312 | tf_op jit(solution)/shard_map/ppermute | solution.py:25
  33.3 0.6 collective-permute-start.9
  33.9 1.8 %collective-permute-start.10 = (bf16[128,128]{0,1:T(8,128)(2,1)S(1)}, bf16[128,128]{0,1:T(8,128)(2,1)S(1)}, u32[]{:S(2)}, u32[]{:S(2)}) collective-permute-start(bf16[128,128]{0,1:T(8,128)(2,1)S(1)} %get-tuple-element.21), channel_id=1, source_target_pairs={{0,12},{1,13},{2,14},{3,15},{4,0},{5,1},{6,2},{7,3},{8,4},{9,5},{1... | collective-permute-start | bytes 98312 | tf_op jit(solution)/shard_map/ppermute | solution.py:25
  35.8 0.3 convolution_bitcast_fusion.4
  36.3 2.2 %collective-permute-done.9 = bf16[128,128]{0,1:T(8,128)(2,1)S(1)} collective-permute-done((bf16[128,128]{0,1:T(8,128)(2,1)S(1)}, bf16[128,128]{0,1:T(8,128)(2,1)S(1)}, u32[]{:S(2)}, u32[]{:S(2)}) %collective-permute-start.9) | collective-permute-done | bytes 32800 | tf_op jit(solution)/shard_map/ppermute | solution.py:25
  38.6 1.6 %collective-permute-start.12 = (bf16[4,128,128]{1,2,0:T(8,128)(2,1)S(1)}, bf16[4,128,128]{1,2,0:T(8,128)(2,1)S(1)}, u32[]{:S(2)}, u32[]{:S(2)}) collective-permute-start(bf16[4,128,128]{1,2,0:T(8,128)(2,1)S(1)} %pad_maximum_fusion.6), channel_id=1, source_target_pairs={{0,2},{1,3},{2,0},{3,1},{4,6},{5,7},{6,4},{7,5},{8,10},{9,11},{10,... | collective-permute-start | bytes 393224 | tf_op jit(solution)/shard_map/ppermute | solution.py:32
  40.2 4.3 %collective-permute-done.12 = bf16[4,128,128]{1,2,0:T(8,128)(2,1)S(1)} collective-permute-done((bf16[4,128,128]{1,2,0:T(8,128)(2,1)S(1)}, bf16[4,128,128]{1,2,0:T(8,128)(2,1)S(1)}, u32[]{:S(2)}, u32[]{:S(2)}) %collective-permute-start.12) | collective-permute-done | bytes 131104 | tf_op jit(solution)/shard_map/ppermute | solution.py:32
  44.6 1.3 %collective-permute-done.13 = bf16[4,128,128]{1,2,0:T(8,128)(2,1)S(1)} collective-permute-done((bf16[4,128,128]{1,2,0:T(8,128)(2,1)S(1)}, bf16[4,128,128]{1,2,0:T(8,128)(2,1)S(1)}, u32[]{:S(2)}, u32[]{:S(2)}) %collective-permute-start.13) | collective-permute-done | bytes 131104 | tf_op jit(solution)/shard_map/ppermute | solution.py:32
  45.9 0.3 convolution_bitcast_fusion.13
  46.4 0.3 constant_dynamic-update-slice_fusion.13
  46.7 1.1 %collective-permute-start.14 = (bf16[128,128]{0,1:T(8,128)(2,1)S(1)}, bf16[128,128]{0,1:T(8,128)(2,1)S(1)}, u32[]{:S(2)}, u32[]{:S(2)}) collective-permute-start(bf16[128,128]{0,1:T(8,128)(2,1)S(1)} %get-tuple-element.19), channel_id=1, source_target_pairs={{0,4},{1,5},{2,6},{3,7},{4,8},{5,9},{6,10},{7,11},{8,12},{9,13},{1... | collective-permute-start | bytes 98312 | tf_op jit(solution)/shard_map/ppermute | solution.py:25
  47.8 2.5 %collective-permute-start.15 = (bf16[128,128]{0,1:T(8,128)(2,1)S(1)}, bf16[128,128]{0,1:T(8,128)(2,1)S(1)}, u32[]{:S(2)}, u32[]{:S(2)}) collective-permute-start(bf16[128,128]{0,1:T(8,128)(2,1)S(1)} %get-tuple-element.19), channel_id=1, source_target_pairs={{0,8},{1,9},{2,10},{3,11},{4,12},{5,13},{6,14},{7,15},{8,0},{9,1},... | collective-permute-start | bytes 98312 | tf_op jit(solution)/shard_map/ppermute | solution.py:25
  50.3 1.0 %collective-permute-start.16 = (bf16[128,128]{0,1:T(8,128)(2,1)S(1)}, bf16[128,128]{0,1:T(8,128)(2,1)S(1)}, u32[]{:S(2)}, u32[]{:S(2)}) collective-permute-start(bf16[128,128]{0,1:T(8,128)(2,1)S(1)} %get-tuple-element.19), channel_id=1, source_target_pairs={{0,12},{1,13},{2,14},{3,15},{4,0},{5,1},{6,2},{7,3},{8,4},{9,5},{1... | collective-permute-start | bytes 98312 | tf_op jit(solution)/shard_map/ppermute | solution.py:25
  51.4 0.5 convolution_bitcast_fusion.11
  51.9 0.8 %collective-permute-done.14 = bf16[128,128]{0,1:T(8,128)(2,1)S(1)} collective-permute-done((bf16[128,128]{0,1:T(8,128)(2,1)S(1)}, bf16[128,128]{0,1:T(8,128)(2,1)S(1)}, u32[]{:S(2)}, u32[]{:S(2)}) %collective-permute-start.14) | collective-permute-done | bytes 32800 | tf_op jit(solution)/shard_map/ppermute | solution.py:25
  52.7 0.7 %collective-permute-done.15 = bf16[128,128]{0,1:T(8,128)(2,1)S(1)} collective-permute-done((bf16[128,128]{0,1:T(8,128)(2,1)S(1)}, bf16[128,128]{0,1:T(8,128)(2,1)S(1)}, u32[]{:S(2)}, u32[]{:S(2)}) %collective-permute-start.15) | collective-permute-done | bytes 32800 | tf_op jit(solution)/shard_map/ppermute | solution.py:25
  53.4 0.9 %collective-permute-done.16 = bf16[128,128]{0,1:T(8,128)(2,1)S(1)} collective-permute-done((bf16[128,128]{0,1:T(8,128)(2,1)S(1)}, bf16[128,128]{0,1:T(8,128)(2,1)S(1)}, u32[]{:S(2)}, u32[]{:S(2)}) %collective-permute-start.16) | collective-permute-done | bytes 32800 | tf_op jit(solution)/shard_map/ppermute | solution.py:25
  54.4 1.6 %collective-permute-start.18 = (bf16[4,128,128]{1,2,0:T(8,128)(2,1)S(1)}, bf16[4,128,128]{1,2,0:T(8,128)(2,1)S(1)}, u32[]{:S(2)}, u32[]{:S(2)}) collective-permute-start(bf16[4,128,128]{1,2,0:T(8,128)(2,1)S(1)} %pad_maximum_fusion.7), channel_id=1, source_target_pairs={{0,2},{1,3},{2,0},{3,1},{4,6},{5,7},{6,4},{7,5},{8,10},{9,11},{10,... | collective-permute-start | bytes 393224 | tf_op jit(solution)/shard_map/ppermute | solution.py:32
  56.0 4.3 %collective-permute-done.18 = bf16[4,128,128]{1,2,0:T(8,128)(2,1)S(1)} collective-permute-done((bf16[4,128,128]{1,2,0:T(8,128)(2,1)S(1)}, bf16[4,128,128]{1,2,0:T(8,128)(2,1)S(1)}, u32[]{:S(2)}, u32[]{:S(2)}) %collective-permute-start.18) | collective-permute-done | bytes 131104 | tf_op jit(solution)/shard_map/ppermute | solution.py:32
  60.3 1.3 %collective-permute-done.19 = bf16[4,128,128]{1,2,0:T(8,128)(2,1)S(1)} collective-permute-done((bf16[4,128,128]{1,2,0:T(8,128)(2,1)S(1)}, bf16[4,128,128]{1,2,0:T(8,128)(2,1)S(1)}, u32[]{:S(2)}, u32[]{:S(2)}) %collective-permute-start.19) | collective-permute-done | bytes 131104 | tf_op jit(solution)/shard_map/ppermute | solution.py:32
  61.6 0.3 convolution_bitcast_fusion.12
  62.2 0.3 convolution_bitcast_fusion.10
  62.5 0.8 %copy.24 = f32[3,128,128]{2,1,0:T(8,128)} copy(f32[3,128,128]{1,2,0:T(8,128)S(1)} %pad_maximum_fusion.5) | data formatting | bytes 393216 | tf_op jit(solution)/shard_map/stack | solution.py:139
  (60 shorter events, 3.2 us)
Async XLA Ops:
  0.0 12.0 %copy-start = (bf16[1,16,2,128,128]{4,3,2,1,0:T(8,128)(2,1)S(1)}, bf16[1,16,2,128,128]{4,3,2,1,0:T(8,128)(2,1)}, u32[]{:S(2)}) copy-start(bf16[1,16,2,128,128]{4,3,2,1,0:T(8,128)(2,1)} %param.16) | copy-start | bytes 3145732
  0.0 14.3 %collective-permute-start = (bf16[4,128,128]{2,1,0:T(8,128)(2,1)}, bf16[4,128,128]{2,1,0:T(8,128)(2,1)S(1)}, u32[]{:S(2)}, u32[]{:S(2)}) collective-permute-start(bf16[4,128,128]{2,1,0:T(8,128)(2,1)} %param.19), channel_id=1, source_target_pairs={{0,4},{1,5},{2,6},{3,7},{4,8},{5,9},{6,10},{7,11},{8,12},{9,13},{1... | collective-permute-start | bytes 393224 | tf_op jit(solution)/shard_map/ppermute | solution.py:25
  3.0 11.4 %collective-permute-start.1 = (bf16[4,128,128]{2,1,0:T(8,128)(2,1)}, bf16[4,128,128]{2,1,0:T(8,128)(2,1)S(1)}, u32[]{:S(2)}, u32[]{:S(2)}) collective-permute-start(bf16[4,128,128]{2,1,0:T(8,128)(2,1)} %param.19), channel_id=1, source_target_pairs={{0,8},{1,9},{2,10},{3,11},{4,12},{5,13},{6,14},{7,15},{8,0},{9,1},... | collective-permute-start | bytes 393224 | tf_op jit(solution)/shard_map/ppermute | solution.py:25
  5.6 8.9 %collective-permute-start.2 = (bf16[4,128,128]{2,1,0:T(8,128)(2,1)}, bf16[4,128,128]{2,1,0:T(8,128)(2,1)S(1)}, u32[]{:S(2)}, u32[]{:S(2)}) collective-permute-start(bf16[4,128,128]{2,1,0:T(8,128)(2,1)} %param.19), channel_id=1, source_target_pairs={{0,12},{1,13},{2,14},{3,15},{4,0},{5,1},{6,2},{7,3},{8,4},{9,5},{1... | collective-permute-start | bytes 393224 | tf_op jit(solution)/shard_map/ppermute | solution.py:25
  7.0 9.9 %collective-permute-start.4 = (bf16[1,4,128,128]{3,2,1,0:T(8,128)(2,1)}, bf16[1,4,128,128]{3,2,1,0:T(8,128)(2,1)S(1)}, u32[]{:S(2)}, u32[]{:S(2)}) collective-permute-start(bf16[1,4,128,128]{3,2,1,0:T(8,128)(2,1)} %bitcast.257), channel_id=1, source_target_pairs={{0,2},{1,3},{2,0},{3,1},{4,6},{5,7},{6,4},{7,5},{8,10},{9,11},{10,... | collective-permute-start | bytes 393224 | tf_op jit(solution)/shard_map/ppermute | solution.py:32
  14.1 2.0 %copy-start.3 = (bf16[4,128,128]{2,1,0:T(8,128)(2,1)S(1)}, bf16[4,128,128]{2,1,0:T(8,128)(2,1)}, u32[]{:S(2)}) copy-start(bf16[4,128,128]{2,1,0:T(8,128)(2,1)} %param.19) | copy-start | bytes 393220
  14.5 11.0 %collective-permute-start.5 = (bf16[3,4,128,128]{3,2,1,0:T(8,128)(2,1)S(1)}, bf16[3,4,128,128]{3,2,1,0:T(8,128)(2,1)S(1)}, u32[]{:S(2)}, u32[]{:S(2)}) collective-permute-start(bf16[3,4,128,128]{3,2,1,0:T(8,128)(2,1)S(1)} %pad_maximum_fusion.4), channel_id=1, source_target_pairs={{0,2},{1,3},{2,0},{3,1},{4,6},{5,7},{6,4},{7,5},{8,10},{9,11},{10,... | collective-permute-start | bytes 1179656 | tf_op jit(solution)/shard_map/ppermute | solution.py:32
  16.2 10.2 %collective-permute-start.3 = (bf16[4,4,128,128]{3,2,1,0:T(8,128)(2,1)S(1)}, bf16[4,4,128,128]{3,2,1,0:T(8,128)(2,1)S(1)}, u32[]{:S(2)}, u32[]{:S(2)}) collective-permute-start(bf16[4,4,128,128]{3,2,1,0:T(8,128)(2,1)S(1)} %pad_maximum_fusion.3), channel_id=1, source_target_pairs={{0,1},{1,0},{2,3},{3,2},{4,5},{5,4},{6,7},{7,6},{8,9},{9,8},{10,11... | collective-permute-start | bytes 1572872 | tf_op jit(solution)/shard_map/ppermute | solution.py:32
  16.9 11.9 %collective-permute-start.6 = (bf16[1,4,128,128]{3,2,1,0:T(8,128)(2,1)S(1)}, bf16[1,4,128,128]{3,2,1,0:T(8,128)(2,1)S(1)}, u32[]{:S(2)}, u32[]{:S(2)}) collective-permute-start(bf16[1,4,128,128]{3,2,1,0:T(8,128)(2,1)S(1)} %collective-permute-done.4), channel_id=1, source_target_pairs={{0,1},{1,0},{2,3},{3,2},{4,5},{5,4},{6,7},{7,6},{8,9},{9,8},{10,11... | collective-permute-start | bytes 393224 | tf_op jit(solution)/shard_map/ppermute | solution.py:32
  25.5 2.9 %collective-permute-start.7 = (bf16[3,4,128,128]{3,2,1,0:T(8,128)(2,1)S(1)}, bf16[3,4,128,128]{3,2,1,0:T(8,128)(2,1)S(1)}, u32[]{:S(2)}, u32[]{:S(2)}) collective-permute-start(bf16[3,4,128,128]{3,2,1,0:T(8,128)(2,1)S(1)} %collective-permute-done.5), channel_id=1, source_target_pairs={{0,1},{1,0},{2,3},{3,2},{4,5},{5,4},{6,7},{7,6},{8,9},{9,8},{10,11... | collective-permute-start | bytes 1179656 | tf_op jit(solution)/shard_map/ppermute | solution.py:32
  28.4 0.9 %copy-start.2 = (f32[3,128,128]{2,1,0:T(8,128)S(1)}, f32[3,128,128]{2,1,0:T(8,128)}, u32[]{:S(2)}) copy-start(f32[3,128,128]{2,1,0:T(8,128)} %param.20) | copy-start | bytes 589828
  28.8 0.9 %copy-start.1 = (f32[1,128,128]{2,1,0:T(8,128)S(1)}, f32[1,128,128]{2,1,0:T(8,128)}, u32[]{:S(2)}) copy-start(f32[1,128,128]{2,1,0:T(8,128)} %param.21) | copy-start | bytes 196612
  29.9 6.4 %collective-permute-start.8 = (bf16[128,128]{0,1:T(8,128)(2,1)S(1)}, bf16[128,128]{0,1:T(8,128)(2,1)S(1)}, u32[]{:S(2)}, u32[]{:S(2)}) collective-permute-start(bf16[128,128]{0,1:T(8,128)(2,1)S(1)} %get-tuple-element.21), channel_id=1, source_target_pairs={{0,4},{1,5},{2,6},{3,7},{4,8},{5,9},{6,10},{7,11},{8,12},{9,13},{1... | collective-permute-start | bytes 98312 | tf_op jit(solution)/shard_map/ppermute | solution.py:25
  33.3 5.2 %collective-permute-start.9 = (bf16[128,128]{0,1:T(8,128)(2,1)S(1)}, bf16[128,128]{0,1:T(8,128)(2,1)S(1)}, u32[]{:S(2)}, u32[]{:S(2)}) collective-permute-start(bf16[128,128]{0,1:T(8,128)(2,1)S(1)} %get-tuple-element.21), channel_id=1, source_target_pairs={{0,8},{1,9},{2,10},{3,11},{4,12},{5,13},{6,14},{7,15},{8,0},{9,1},... | collective-permute-start | bytes 98312 | tf_op jit(solution)/shard_map/ppermute | solution.py:25
  33.9 4.6 %collective-permute-start.10 = (bf16[128,128]{0,1:T(8,128)(2,1)S(1)}, bf16[128,128]{0,1:T(8,128)(2,1)S(1)}, u32[]{:S(2)}, u32[]{:S(2)}) collective-permute-start(bf16[128,128]{0,1:T(8,128)(2,1)S(1)} %get-tuple-element.21), channel_id=1, source_target_pairs={{0,12},{1,13},{2,14},{3,15},{4,0},{5,1},{6,2},{7,3},{8,4},{9,5},{1... | collective-permute-start | bytes 98312 | tf_op jit(solution)/shard_map/ppermute | solution.py:25
  38.5 6.0 %collective-permute-start.11 = (bf16[4,128,128]{1,2,0:T(8,128)(2,1)S(1)}, bf16[4,128,128]{1,2,0:T(8,128)(2,1)S(1)}, u32[]{:S(2)}, u32[]{:S(2)}) collective-permute-start(bf16[4,128,128]{1,2,0:T(8,128)(2,1)S(1)} %pad_maximum_fusion.6), channel_id=1, source_target_pairs={{0,1},{1,0},{2,3},{3,2},{4,5},{5,4},{6,7},{7,6},{8,9},{9,8},{10,11... | collective-permute-start | bytes 393224 | tf_op jit(solution)/shard_map/ppermute | solution.py:32
  38.6 5.9 %collective-permute-start.12 = (bf16[4,128,128]{1,2,0:T(8,128)(2,1)S(1)}, bf16[4,128,128]{1,2,0:T(8,128)(2,1)S(1)}, u32[]{:S(2)}, u32[]{:S(2)}) collective-permute-start(bf16[4,128,128]{1,2,0:T(8,128)(2,1)S(1)} %pad_maximum_fusion.6), channel_id=1, source_target_pairs={{0,2},{1,3},{2,0},{3,1},{4,6},{5,7},{6,4},{7,5},{8,10},{9,11},{10,... | collective-permute-start | bytes 393224 | tf_op jit(solution)/shard_map/ppermute | solution.py:32
  44.5 1.3 %collective-permute-start.13 = (bf16[4,128,128]{1,2,0:T(8,128)(2,1)S(1)}, bf16[4,128,128]{1,2,0:T(8,128)(2,1)S(1)}, u32[]{:S(2)}, u32[]{:S(2)}) collective-permute-start(bf16[4,128,128]{1,2,0:T(8,128)(2,1)S(1)} %collective-permute-done.12), channel_id=1, source_target_pairs={{0,1},{1,0},{2,3},{3,2},{4,5},{5,4},{6,7},{7,6},{8,9},{9,8},{10,11... | collective-permute-start | bytes 393224 | tf_op jit(solution)/shard_map/ppermute | solution.py:32
  46.7 6.0 %collective-permute-start.14 = (bf16[128,128]{0,1:T(8,128)(2,1)S(1)}, bf16[128,128]{0,1:T(8,128)(2,1)S(1)}, u32[]{:S(2)}, u32[]{:S(2)}) collective-permute-start(bf16[128,128]{0,1:T(8,128)(2,1)S(1)} %get-tuple-element.19), channel_id=1, source_target_pairs={{0,4},{1,5},{2,6},{3,7},{4,8},{5,9},{6,10},{7,11},{8,12},{9,13},{1... | collective-permute-start | bytes 98312 | tf_op jit(solution)/shard_map/ppermute | solution.py:25
  47.8 5.6 %collective-permute-start.15 = (bf16[128,128]{0,1:T(8,128)(2,1)S(1)}, bf16[128,128]{0,1:T(8,128)(2,1)S(1)}, u32[]{:S(2)}, u32[]{:S(2)}) collective-permute-start(bf16[128,128]{0,1:T(8,128)(2,1)S(1)} %get-tuple-element.19), channel_id=1, source_target_pairs={{0,8},{1,9},{2,10},{3,11},{4,12},{5,13},{6,14},{7,15},{8,0},{9,1},... | collective-permute-start | bytes 98312 | tf_op jit(solution)/shard_map/ppermute | solution.py:25
  50.3 3.9 %collective-permute-start.16 = (bf16[128,128]{0,1:T(8,128)(2,1)S(1)}, bf16[128,128]{0,1:T(8,128)(2,1)S(1)}, u32[]{:S(2)}, u32[]{:S(2)}) collective-permute-start(bf16[128,128]{0,1:T(8,128)(2,1)S(1)} %get-tuple-element.19), channel_id=1, source_target_pairs={{0,12},{1,13},{2,14},{3,15},{4,0},{5,1},{6,2},{7,3},{8,4},{9,5},{1... | collective-permute-start | bytes 98312 | tf_op jit(solution)/shard_map/ppermute | solution.py:25
  54.3 6.0 %collective-permute-start.17 = (bf16[4,128,128]{1,2,0:T(8,128)(2,1)S(1)}, bf16[4,128,128]{1,2,0:T(8,128)(2,1)S(1)}, u32[]{:S(2)}, u32[]{:S(2)}) collective-permute-start(bf16[4,128,128]{1,2,0:T(8,128)(2,1)S(1)} %pad_maximum_fusion.7), channel_id=1, source_target_pairs={{0,1},{1,0},{2,3},{3,2},{4,5},{5,4},{6,7},{7,6},{8,9},{9,8},{10,11... | collective-permute-start | bytes 393224 | tf_op jit(solution)/shard_map/ppermute | solution.py:32
  54.4 5.9 %collective-permute-start.18 = (bf16[4,128,128]{1,2,0:T(8,128)(2,1)S(1)}, bf16[4,128,128]{1,2,0:T(8,128)(2,1)S(1)}, u32[]{:S(2)}, u32[]{:S(2)}) collective-permute-start(bf16[4,128,128]{1,2,0:T(8,128)(2,1)S(1)} %pad_maximum_fusion.7), channel_id=1, source_target_pairs={{0,2},{1,3},{2,0},{3,1},{4,6},{5,7},{6,4},{7,5},{8,10},{9,11},{10,... | collective-permute-start | bytes 393224 | tf_op jit(solution)/shard_map/ppermute | solution.py:32
  60.3 1.3 %collective-permute-start.19 = (bf16[4,128,128]{1,2,0:T(8,128)(2,1)S(1)}, bf16[4,128,128]{1,2,0:T(8,128)(2,1)S(1)}, u32[]{:S(2)}, u32[]{:S(2)}) collective-permute-start(bf16[4,128,128]{1,2,0:T(8,128)(2,1)S(1)} %collective-permute-done.18), channel_id=1, source_target_pairs={{0,1},{1,0},{2,3},{3,2},{4,5},{5,4},{6,7},{7,6},{8,9},{9,8},{10,11... | collective-permute-start | bytes 393224 | tf_op jit(solution)/shard_map/ppermute | solution.py:32

commit v10 on v9

--- a/solution.py
+++ b/solution.py
@@ -126,7 +126,7 @@
         current = advance(moment, retarded)
         results[moment] = current
         if moment > 0:
-            pieces, new_blocks = gather_blocks(current.astype(jnp.bfloat16), wide, False)
+            pieces, new_blocks = gather_blocks(current.astype(jnp.bfloat16), wide, True)
             newer[moment] = jnp.concatenate(pieces)
             if recent is None:
                 recent = tiles_by_lag(

time: 63.5 us -> 60.8 us (0.957)
  waiting for transfers between devices: 24 us -> 17.1 us
  starting transfers between devices: 24.5 us -> 28.6 us
    ppermute x11 -> x15, starting transfers between devices: 7.05 us -> 11.1 us  [swap(): return lax.ppermute(x, 'wide', [(d, d ^ mask) for d in range(wide)])]
    ppermute x11 -> x15, waiting for transfers between devices: 19.3 us -> 15.5 us  [swap(): return lax.ppermute(x, 'wide', [(d, d ^ mask) for d in range(wide)])]
    ppermute x9, waiting for transfers between devices: 4.67 us -> 1.57 us  [line_stage(): parts.append(lax.ppermute(x, 'wide', pairs)[None])]
  transfers between devices with their start and end apart: 20 -> 24, of which waited for: 10 -> 8; matrix products, arithmetic and copies ran while one was open for 17% -> 18% of each run, Pallas kernels for 0% -> 0%
where the time goes in v10:
time: 60.8 us; the launch traced here: 60.6 us
  starting transfers between devices  28.6 us (47%)
  waiting for transfers between devices  17.1 us (28%)
  matrix products  6.94 us (11%)
  local copies, waits for them, and re-layouts  4.44 us (7%)
  other arithmetic  3.15 us (5%)
    ppermute x9, starting transfers between devices, line_stage(): parts.append(lax.ppermute(x, 'wide', pairs)[None])  17.5 us
    ppermute x15, waiting for transfers between devices, swap(): return lax.ppermute(x, 'wide', [(d, d ^ mask) for d in range(wide)])  15.5 us
    ppermute x15, starting transfers between devices, swap(): return lax.ppermute(x, 'wide', [(d, d ^ mask) for d in range(wide)])  11.1 us
    dot_general x21, matrix products, rowwise(): return jnp.einsum(spec, tiles, currents, preferred_element_type=jnp.float32)  6.09 us
    sort x1, other arithmetic, per_device(): column_of_block = jnp.argsort(block_owner)  1.9 us
    ppermute x9, waiting for transfers between devices, line_stage(): parts.append(lax.ppermute(x, 'wide', pairs)[None])  1.57 us
  transfers between devices with their start and end apart: 24, of which 8 were waited for; matrix products, arithmetic and copies ran while one was open for 18% of the time, Pallas kernels for 0%

profile of v10, /device:TPU:0, one launch (start us, length us, event | category | flops | bytes accessed | tf_op | source)
XLA Modules:
  0.0 60.6 jit_solution(9929819440045427920)
XLA Ops:
  0.0 3.0 %collective-permute-start = (bf16[4,128,128]{2,1,0:T(8,128)(2,1)}, bf16[4,128,128]{2,1,0:T(8,128)(2,1)S(1)}, u32[]{:S(2)}, u32[]{:S(2)}) collective-permute-start(bf16[4,128,128]{2,1,0:T(8,128)(2,1)} %param.19), channel_id=1, source_target_pairs={{0,4},{1,5},{2,6},{3,7},{4,8},{5,9},{6,10},{7,11},{8,12},{9,13},{1... | collective-permute-start | bytes 393224 | tf_op jit(solution)/shard_map/ppermute | solution.py:25
  3.0 2.6 %collective-permute-start.1 = (bf16[4,128,128]{2,1,0:T(8,128)(2,1)}, bf16[4,128,128]{2,1,0:T(8,128)(2,1)S(1)}, u32[]{:S(2)}, u32[]{:S(2)}) collective-permute-start(bf16[4,128,128]{2,1,0:T(8,128)(2,1)} %param.19), channel_id=1, source_target_pairs={{0,8},{1,9},{2,10},{3,11},{4,12},{5,13},{6,14},{7,15},{8,0},{9,1},... | collective-permute-start | bytes 393224 | tf_op jit(solution)/shard_map/ppermute | solution.py:25
  5.6 1.3 %collective-permute-start.2 = (bf16[4,128,128]{2,1,0:T(8,128)(2,1)}, bf16[4,128,128]{2,1,0:T(8,128)(2,1)S(1)}, u32[]{:S(2)}, u32[]{:S(2)}) collective-permute-start(bf16[4,128,128]{2,1,0:T(8,128)(2,1)} %param.19), channel_id=1, source_target_pairs={{0,12},{1,13},{2,14},{3,15},{4,0},{5,1},{6,2},{7,3},{8,4},{9,5},{1... | collective-permute-start | bytes 393224 | tf_op jit(solution)/shard_map/ppermute | solution.py:25
  7.0 1.5 %collective-permute-start.4 = (bf16[1,4,128,128]{3,2,1,0:T(8,128)(2,1)}, bf16[1,4,128,128]{3,2,1,0:T(8,128)(2,1)S(1)}, u32[]{:S(2)}, u32[]{:S(2)}) collective-permute-start(bf16[1,4,128,128]{3,2,1,0:T(8,128)(2,1)} %bitcast.263), channel_id=1, source_target_pairs={{0,2},{1,3},{2,0},{3,1},{4,6},{5,7},{6,4},{7,5},{8,10},{9,11},{10,... | collective-permute-start | bytes 393224 | tf_op jit(solution)/shard_map/ppermute | solution.py:32
  8.7 1.9 %sort.17 = (s32[16]{0:T(128)}, s32[16]{0:T(128)S(1)}) sort(s32[16]{0:T(128)} %param.18, s32[16]{0:T(128)S(1)} %iota.5), dimensions={0}, to_apply=%region_0.0 | sort | flops 64 | bytes 256 | tf_op jit(solution)/shard_map/jit(argsort)/sort | solution.py:97
  10.6 0.7 %gather_fusion = s32[16]{0:T(128)S(1)} fusion(s32[16]{0:T(128)S(1)} %get-tuple-element.8, s32[1024]{0:T(1024)S(1)} %pad_clamp_fusion.1), kind=kCustom, calls=%fused_computation.clone | custom fusion | bytes 192 | tf_op jit(solution)/shard_map/jit(_take)/gather | solution.py:72
  11.3 0.8 %copy.18 = s32[16,2]{1,0:T(8,128)S(1)} copy(s32[16,2]{0,1:T(2,128)} %bitcast.270) | data formatting | bytes 256 | tf_op jit(solution)/shard_map/squeeze | solution.py:74
  12.0 0.7 %gather_fusion.2 = bf16[16,2,128,128]{3,2,1,0:T(8,128)(2,1)S(1)} fusion(bf16[16,2,128,128]{3,2,1,0:T(8,128)(2,1)S(1)} %bitcast.239, s32[1024]{0:T(1024)S(1)} %pad_clamp_fusion), kind=kCustom, calls=%fused_computation.2.clone | custom fusion | bytes 2097216 | tf_op jit(solution)/shard_map/jit(_take)/gather | solution.py:73
  12.8 0.6 gather_fusion.1
  13.9 0.3 bitcast_select_fusion.3
  14.5 1.6 %collective-permute-start.5 = (bf16[3,4,128,128]{3,2,1,0:T(8,128)(2,1)S(1)}, bf16[3,4,128,128]{3,2,1,0:T(8,128)(2,1)S(1)}, u32[]{:S(2)}, u32[]{:S(2)}) collective-permute-start(bf16[3,4,128,128]{3,2,1,0:T(8,128)(2,1)S(1)} %pad_maximum_fusion.4), channel_id=1, source_target_pairs={{0,2},{1,3},{2,0},{3,1},{4,6},{5,7},{6,4},{7,5},{8,10},{9,11},{10,... | collective-permute-start | bytes 1179656 | tf_op jit(solution)/shard_map/ppermute | solution.py:32
  16.3 0.3 convolution_bitcast_fusion.7
  16.6 0.3 convolution_bitcast_fusion.9
  16.9 0.6 collective-permute-start.6
  17.4 8.1 %collective-permute-done.5 = bf16[3,4,128,128]{3,2,1,0:T(8,128)(2,1)S(1)} collective-permute-done((bf16[3,4,128,128]{3,2,1,0:T(8,128)(2,1)S(1)}, bf16[3,4,128,128]{3,2,1,0:T(8,128)(2,1)S(1)}, u32[]{:S(2)}, u32[]{:S(2)}) %collective-permute-start.5) | collective-permute-done | bytes 393248 | tf_op jit(solution)/shard_map/ppermute | solution.py:32
  25.8 0.3 convolution_bitcast_fusion.5
  26.1 0.3 convolution_bitcast_fusion.3
  26.4 0.3 convolution_bitcast_fusion
  26.8 0.4 fusion.20
  27.4 0.3 fusion.19
  28.4 0.3 convolution_bitcast_fusion.2
  28.8 0.6 copy-done.2
  29.6 0.3 constant_dynamic-update-slice_fusion.8
  29.9 3.4 %collective-permute-start.8 = (bf16[128,128]{0,1:T(8,128)(2,1)S(1)}, bf16[128,128]{0,1:T(8,128)(2,1)S(1)}, u32[]{:S(2)}, u32[]{:S(2)}) collective-permute-start(bf16[128,128]{0,1:T(8,128)(2,1)S(1)} %get-tuple-element.21), channel_id=1, source_target_pairs={{0,4},{1,5},{2,6},{3,7},{4,8},{5,9},{6,10},{7,11},{8,12},{9,13},{1... | collective-permute-start | bytes 98312 | tf_op jit(solution)/shard_map/ppermute | solution.py:25
  33.3 0.6 collective-permute-start.9
  33.9 1.8 %collective-permute-start.10 = (bf16[128,128]{0,1:T(8,128)(2,1)S(1)}, bf16[128,128]{0,1:T(8,128)(2,1)S(1)}, u32[]{:S(2)}, u32[]{:S(2)}) collective-permute-start(bf16[128,128]{0,1:T(8,128)(2,1)S(1)} %get-tuple-element.21), channel_id=1, source_target_pairs={{0,12},{1,13},{2,14},{3,15},{4,0},{5,1},{6,2},{7,3},{8,4},{9,5},{1... | collective-permute-start | bytes 98312 | tf_op jit(solution)/shard_map/ppermute | solution.py:25
  35.8 1.5 %collective-permute-start.12 = (bf16[1,128,128]{1,2,0:T(8,128)(2,1)S(1)}, bf16[1,128,128]{1,2,0:T(8,128)(2,1)S(1)}, u32[]{:S(2)}, u32[]{:S(2)}) collective-permute-start(bf16[1,128,128]{1,2,0:T(8,128)(2,1)S(1)} %bitcast.268), channel_id=1, source_target_pairs={{0,2},{1,3},{2,0},{3,1},{4,6},{5,7},{6,4},{7,5},{8,10},{9,11},{10,... | collective-permute-start | bytes 98312 | tf_op jit(solution)/shard_map/ppermute | solution.py:32
  37.3 0.3 convolution_bitcast_fusion.4
  37.9 0.6 %collective-permute-done.9 = bf16[128,128]{0,1:T(8,128)(2,1)S(1)} collective-permute-done((bf16[128,128]{0,1:T(8,128)(2,1)S(1)}, bf16[128,128]{0,1:T(8,128)(2,1)S(1)}, u32[]{:S(2)}, u32[]{:S(2)}) %collective-permute-start.9) | collective-permute-done | bytes 32800 | tf_op jit(solution)/shard_map/ppermute | solution.py:25
  38.5 1.6 %collective-permute-start.13 = (bf16[3,128,128]{1,2,0:T(8,128)(2,1)S(1)}, bf16[3,128,128]{1,2,0:T(8,128)(2,1)S(1)}, u32[]{:S(2)}, u32[]{:S(2)}) collective-permute-start(bf16[3,128,128]{1,2,0:T(8,128)(2,1)S(1)} %pad_maximum_fusion.8), channel_id=1, source_target_pairs={{0,2},{1,3},{2,0},{3,1},{4,6},{5,7},{6,4},{7,5},{8,10},{9,11},{10,... | collective-permute-start | bytes 294920 | tf_op jit(solution)/shard_map/ppermute | solution.py:32
  40.2 0.6 collective-permute-start.14
  40.7 2.5 %collective-permute-done.13 = bf16[3,128,128]{1,2,0:T(8,128)(2,1)S(1)} collective-permute-done((bf16[3,128,128]{1,2,0:T(8,128)(2,1)S(1)}, bf16[3,128,128]{1,2,0:T(8,128)(2,1)S(1)}, u32[]{:S(2)}, u32[]{:S(2)}) %collective-permute-start.13) | collective-permute-done | bytes 98336 | tf_op jit(solution)/shard_map/ppermute | solution.py:32
  43.3 1.2 %collective-permute-done.15 = bf16[3,128,128]{1,2,0:T(8,128)(2,1)S(1)} collective-permute-done((bf16[3,128,128]{1,2,0:T(8,128)(2,1)S(1)}, bf16[3,128,128]{1,2,0:T(8,128)(2,1)S(1)}, u32[]{:S(2)}, u32[]{:S(2)}) %collective-permute-start.15) | collective-permute-done | bytes 98336 | tf_op jit(solution)/shard_map/ppermute | solution.py:32
  44.5 0.3 convolution_bitcast_fusion.13
  45.1 0.3 constant_dynamic-update-slice_fusion.17
  45.4 1.1 %collective-permute-start.16 = (bf16[128,128]{0,1:T(8,128)(2,1)S(1)}, bf16[128,128]{0,1:T(8,128)(2,1)S(1)}, u32[]{:S(2)}, u32[]{:S(2)}) collective-permute-start(bf16[128,128]{0,1:T(8,128)(2,1)S(1)} %get-tuple-element.19), channel_id=1, source_target_pairs={{0,4},{1,5},{2,6},{3,7},{4,8},{5,9},{6,10},{7,11},{8,12},{9,13},{1... | collective-permute-start | bytes 98312 | tf_op jit(solution)/shard_map/ppermute | solution.py:25
  46.5 2.5 %collective-permute-start.17 = (bf16[128,128]{0,1:T(8,128)(2,1)S(1)}, bf16[128,128]{0,1:T(8,128)(2,1)S(1)}, u32[]{:S(2)}, u32[]{:S(2)}) collective-permute-start(bf16[128,128]{0,1:T(8,128)(2,1)S(1)} %get-tuple-element.19), channel_id=1, source_target_pairs={{0,8},{1,9},{2,10},{3,11},{4,12},{5,13},{6,14},{7,15},{8,0},{9,1},... | collective-permute-start | bytes 98312 | tf_op jit(solution)/shard_map/ppermute | solution.py:25
  49.0 1.0 %collective-permute-start.18 = (bf16[128,128]{0,1:T(8,128)(2,1)S(1)}, bf16[128,128]{0,1:T(8,128)(2,1)S(1)}, u32[]{:S(2)}, u32[]{:S(2)}) collective-permute-start(bf16[128,128]{0,1:T(8,128)(2,1)S(1)} %get-tuple-element.19), channel_id=1, source_target_pairs={{0,12},{1,13},{2,14},{3,15},{4,0},{5,1},{6,2},{7,3},{8,4},{9,5},{1... | collective-permute-start | bytes 98312 | tf_op jit(solution)/shard_map/ppermute | solution.py:25
  50.1 0.5 convolution_bitcast_fusion.11
  50.5 1.6 %collective-permute-start.20 = (bf16[1,128,128]{1,2,0:T(8,128)(2,1)S(1)}, bf16[1,128,128]{1,2,0:T(8,128)(2,1)S(1)}, u32[]{:S(2)}, u32[]{:S(2)}) collective-permute-start(bf16[1,128,128]{1,2,0:T(8,128)(2,1)S(1)} %bitcast.266), channel_id=1, source_target_pairs={{0,2},{1,3},{2,0},{3,1},{4,6},{5,7},{6,4},{7,5},{8,10},{9,11},{10,... | collective-permute-start | bytes 98312 | tf_op jit(solution)/shard_map/ppermute | solution.py:32
  52.1 0.8 %collective-permute-done.18 = bf16[128,128]{0,1:T(8,128)(2,1)S(1)} collective-permute-done((bf16[128,128]{0,1:T(8,128)(2,1)S(1)}, bf16[128,128]{0,1:T(8,128)(2,1)S(1)}, u32[]{:S(2)}, u32[]{:S(2)}) %collective-permute-start.18) | collective-permute-done | bytes 32800 | tf_op jit(solution)/shard_map/ppermute | solution.py:25
  53.0 1.6 %collective-permute-start.21 = (bf16[3,128,128]{1,2,0:T(8,128)(2,1)S(1)}, bf16[3,128,128]{1,2,0:T(8,128)(2,1)S(1)}, u32[]{:S(2)}, u32[]{:S(2)}) collective-permute-start(bf16[3,128,128]{1,2,0:T(8,128)(2,1)S(1)} %pad_maximum_fusion.9), channel_id=1, source_target_pairs={{0,2},{1,3},{2,0},{3,1},{4,6},{5,7},{6,4},{7,5},{8,10},{9,11},{10,... | collective-permute-start | bytes 294920 | tf_op jit(solution)/shard_map/ppermute | solution.py:32
  54.6 0.6 collective-permute-start.22
  55.2 2.5 %collective-permute-done.21 = bf16[3,128,128]{1,2,0:T(8,128)(2,1)S(1)} collective-permute-done((bf16[3,128,128]{1,2,0:T(8,128)(2,1)S(1)}, bf16[3,128,128]{1,2,0:T(8,128)(2,1)S(1)}, u32[]{:S(2)}, u32[]{:S(2)}) %collective-permute-start.21) | collective-permute-done | bytes 98336 | tf_op jit(solution)/shard_map/ppermute | solution.py:32
  57.7 1.2 %collective-permute-done.23 = bf16[3,128,128]{1,2,0:T(8,128)(2,1)S(1)} collective-permute-done((bf16[3,128,128]{1,2,0:T(8,128)(2,1)S(1)}, bf16[3,128,128]{1,2,0:T(8,128)(2,1)S(1)}, u32[]{:S(2)}, u32[]{:S(2)}) %collective-permute-start.23) | collective-permute-done | bytes 98336 | tf_op jit(solution)/shard_map/ppermute | solution.py:32
  59.0 0.3 convolution_bitcast_fusion.12
  59.5 0.3 convolution_bitcast_fusion.10
  59.8 0.8 %copy.24 = f32[3,128,128]{2,1,0:T(8,128)} copy(f32[3,128,128]{1,2,0:T(8,128)S(1)} %pad_maximum_fusion.5) | data formatting | bytes 393216 | tf_op jit(solution)/shard_map/stack | solution.py:139
  (74 shorter events, 3.7 us)
Async XLA Ops:
  0.0 12.0 %copy-start = (bf16[1,16,2,128,128]{4,3,2,1,0:T(8,128)(2,1)S(1)}, bf16[1,16,2,128,128]{4,3,2,1,0:T(8,128)(2,1)}, u32[]{:S(2)}) copy-start(bf16[1,16,2,128,128]{4,3,2,1,0:T(8,128)(2,1)} %param.16) | copy-start | bytes 3145732
  0.0 14.3 %collective-permute-start = (bf16[4,128,128]{2,1,0:T(8,128)(2,1)}, bf16[4,128,128]{2,1,0:T(8,128)(2,1)S(1)}, u32[]{:S(2)}, u32[]{:S(2)}) collective-permute-start(bf16[4,128,128]{2,1,0:T(8,128)(2,1)} %param.19), channel_id=1, source_target_pairs={{0,4},{1,5},{2,6},{3,7},{4,8},{5,9},{6,10},{7,11},{8,12},{9,13},{1... | collective-permute-start | bytes 393224 | tf_op jit(solution)/shard_map/ppermute | solution.py:25
  3.0 11.4 %collective-permute-start.1 = (bf16[4,128,128]{2,1,0:T(8,128)(2,1)}, bf16[4,128,128]{2,1,0:T(8,128)(2,1)S(1)}, u32[]{:S(2)}, u32[]{:S(2)}) collective-permute-start(bf16[4,128,128]{2,1,0:T(8,128)(2,1)} %param.19), channel_id=1, source_target_pairs={{0,8},{1,9},{2,10},{3,11},{4,12},{5,13},{6,14},{7,15},{8,0},{9,1},... | collective-permute-start | bytes 393224 | tf_op jit(solution)/shard_map/ppermute | solution.py:25
  5.6 8.9 %collective-permute-start.2 = (bf16[4,128,128]{2,1,0:T(8,128)(2,1)}, bf16[4,128,128]{2,1,0:T(8,128)(2,1)S(1)}, u32[]{:S(2)}, u32[]{:S(2)}) collective-permute-start(bf16[4,128,128]{2,1,0:T(8,128)(2,1)} %param.19), channel_id=1, source_target_pairs={{0,12},{1,13},{2,14},{3,15},{4,0},{5,1},{6,2},{7,3},{8,4},{9,5},{1... | collective-permute-start | bytes 393224 | tf_op jit(solution)/shard_map/ppermute | solution.py:25
  7.0 9.9 %collective-permute-start.4 = (bf16[1,4,128,128]{3,2,1,0:T(8,128)(2,1)}, bf16[1,4,128,128]{3,2,1,0:T(8,128)(2,1)S(1)}, u32[]{:S(2)}, u32[]{:S(2)}) collective-permute-start(bf16[1,4,128,128]{3,2,1,0:T(8,128)(2,1)} %bitcast.263), channel_id=1, source_target_pairs={{0,2},{1,3},{2,0},{3,1},{4,6},{5,7},{6,4},{7,5},{8,10},{9,11},{10,... | collective-permute-start | bytes 393224 | tf_op jit(solution)/shard_map/ppermute | solution.py:32
  14.1 2.0 %copy-start.3 = (bf16[4,128,128]{2,1,0:T(8,128)(2,1)S(1)}, bf16[4,128,128]{2,1,0:T(8,128)(2,1)}, u32[]{:S(2)}) copy-start(bf16[4,128,128]{2,1,0:T(8,128)(2,1)} %param.19) | copy-start | bytes 393220
  14.5 11.0 %collective-permute-start.5 = (bf16[3,4,128,128]{3,2,1,0:T(8,128)(2,1)S(1)}, bf16[3,4,128,128]{3,2,1,0:T(8,128)(2,1)S(1)}, u32[]{:S(2)}, u32[]{:S(2)}) collective-permute-start(bf16[3,4,128,128]{3,2,1,0:T(8,128)(2,1)S(1)} %pad_maximum_fusion.4), channel_id=1, source_target_pairs={{0,2},{1,3},{2,0},{3,1},{4,6},{5,7},{6,4},{7,5},{8,10},{9,11},{10,... | collective-permute-start | bytes 1179656 | tf_op jit(solution)/shard_map/ppermute | solution.py:32
  16.2 10.2 %collective-permute-start.3 = (bf16[4,4,128,128]{3,2,1,0:T(8,128)(2,1)S(1)}, bf16[4,4,128,128]{3,2,1,0:T(8,128)(2,1)S(1)}, u32[]{:S(2)}, u32[]{:S(2)}) collective-permute-start(bf16[4,4,128,128]{3,2,1,0:T(8,128)(2,1)S(1)} %pad_maximum_fusion.3), channel_id=1, source_target_pairs={{0,1},{1,0},{2,3},{3,2},{4,5},{5,4},{6,7},{7,6},{8,9},{9,8},{10,11... | collective-permute-start | bytes 1572872 | tf_op jit(solution)/shard_map/ppermute | solution.py:32
  16.9 11.9 %collective-permute-start.6 = (bf16[1,4,128,128]{3,2,1,0:T(8,128)(2,1)S(1)}, bf16[1,4,128,128]{3,2,1,0:T(8,128)(2,1)S(1)}, u32[]{:S(2)}, u32[]{:S(2)}) collective-permute-start(bf16[1,4,128,128]{3,2,1,0:T(8,128)(2,1)S(1)} %collective-permute-done.4), channel_id=1, source_target_pairs={{0,1},{1,0},{2,3},{3,2},{4,5},{5,4},{6,7},{7,6},{8,9},{9,8},{10,11... | collective-permute-start | bytes 393224 | tf_op jit(solution)/shard_map/ppermute | solution.py:32
  25.5 2.9 %collective-permute-start.7 = (bf16[3,4,128,128]{3,2,1,0:T(8,128)(2,1)S(1)}, bf16[3,4,128,128]{3,2,1,0:T(8,128)(2,1)S(1)}, u32[]{:S(2)}, u32[]{:S(2)}) collective-permute-start(bf16[3,4,128,128]{3,2,1,0:T(8,128)(2,1)S(1)} %collective-permute-done.5), channel_id=1, source_target_pairs={{0,1},{1,0},{2,3},{3,2},{4,5},{5,4},{6,7},{7,6},{8,9},{9,8},{10,11... | collective-permute-start | bytes 1179656 | tf_op jit(solution)/shard_map/ppermute | solution.py:32
  28.4 0.9 %copy-start.2 = (f32[3,128,128]{2,1,0:T(8,128)S(1)}, f32[3,128,128]{2,1,0:T(8,128)}, u32[]{:S(2)}) copy-start(f32[3,128,128]{2,1,0:T(8,128)} %param.20) | copy-start | bytes 589828
  28.8 0.9 %copy-start.1 = (f32[1,128,128]{2,1,0:T(8,128)S(1)}, f32[1,128,128]{2,1,0:T(8,128)}, u32[]{:S(2)}) copy-start(f32[1,128,128]{2,1,0:T(8,128)} %param.21) | copy-start | bytes 196612
  29.9 7.9 %collective-permute-start.8 = (bf16[128,128]{0,1:T(8,128)(2,1)S(1)}, bf16[128,128]{0,1:T(8,128)(2,1)S(1)}, u32[]{:S(2)}, u32[]{:S(2)}) collective-permute-start(bf16[128,128]{0,1:T(8,128)(2,1)S(1)} %get-tuple-element.21), channel_id=1, source_target_pairs={{0,4},{1,5},{2,6},{3,7},{4,8},{5,9},{6,10},{7,11},{8,12},{9,13},{1... | collective-permute-start | bytes 98312 | tf_op jit(solution)/shard_map/ppermute | solution.py:25
  33.3 5.2 %collective-permute-start.9 = (bf16[128,128]{0,1:T(8,128)(2,1)S(1)}, bf16[128,128]{0,1:T(8,128)(2,1)S(1)}, u32[]{:S(2)}, u32[]{:S(2)}) collective-permute-start(bf16[128,128]{0,1:T(8,128)(2,1)S(1)} %get-tuple-element.21), channel_id=1, source_target_pairs={{0,8},{1,9},{2,10},{3,11},{4,12},{5,13},{6,14},{7,15},{8,0},{9,1},... | collective-permute-start | bytes 98312 | tf_op jit(solution)/shard_map/ppermute | solution.py:25
  33.9 4.6 %collective-permute-start.10 = (bf16[128,128]{0,1:T(8,128)(2,1)S(1)}, bf16[128,128]{0,1:T(8,128)(2,1)S(1)}, u32[]{:S(2)}, u32[]{:S(2)}) collective-permute-start(bf16[128,128]{0,1:T(8,128)(2,1)S(1)} %get-tuple-element.21), channel_id=1, source_target_pairs={{0,12},{1,13},{2,14},{3,15},{4,0},{5,1},{6,2},{7,3},{8,4},{9,5},{1... | collective-permute-start | bytes 98312 | tf_op jit(solution)/shard_map/ppermute | solution.py:25
  35.8 4.4 %collective-permute-start.12 = (bf16[1,128,128]{1,2,0:T(8,128)(2,1)S(1)}, bf16[1,128,128]{1,2,0:T(8,128)(2,1)S(1)}, u32[]{:S(2)}, u32[]{:S(2)}) collective-permute-start(bf16[1,128,128]{1,2,0:T(8,128)(2,1)S(1)} %bitcast.268), channel_id=1, source_target_pairs={{0,2},{1,3},{2,0},{3,1},{4,6},{5,7},{6,4},{7,5},{8,10},{9,11},{10,... | collective-permute-start | bytes 98312 | tf_op jit(solution)/shard_map/ppermute | solution.py:32
  38.5 4.7 %collective-permute-start.13 = (bf16[3,128,128]{1,2,0:T(8,128)(2,1)S(1)}, bf16[3,128,128]{1,2,0:T(8,128)(2,1)S(1)}, u32[]{:S(2)}, u32[]{:S(2)}) collective-permute-start(bf16[3,128,128]{1,2,0:T(8,128)(2,1)S(1)} %pad_maximum_fusion.8), channel_id=1, source_target_pairs={{0,2},{1,3},{2,0},{3,1},{4,6},{5,7},{6,4},{7,5},{8,10},{9,11},{10,... | collective-permute-start | bytes 294920 | tf_op jit(solution)/shard_map/ppermute | solution.py:32
  40.1 3.1 %collective-permute-start.11 = (bf16[4,128,128]{1,2,0:T(8,128)(2,1)S(1)}, bf16[4,128,128]{1,2,0:T(8,128)(2,1)S(1)}, u32[]{:S(2)}, u32[]{:S(2)}) collective-permute-start(bf16[4,128,128]{1,2,0:T(8,128)(2,1)S(1)} %pad_maximum_fusion.6), channel_id=1, source_target_pairs={{0,1},{1,0},{2,3},{3,2},{4,5},{5,4},{6,7},{7,6},{8,9},{9,8},{10,11... | collective-permute-start | bytes 393224 | tf_op jit(solution)/shard_map/ppermute | solution.py:32
  40.2 3.1 %collective-permute-start.14 = (bf16[1,128,128]{1,2,0:T(8,128)(2,1)S(1)}, bf16[1,128,128]{1,2,0:T(8,128)(2,1)S(1)}, u32[]{:S(2)}, u32[]{:S(2)}) collective-permute-start(bf16[1,128,128]{1,2,0:T(8,128)(2,1)S(1)} %collective-permute-done.12), channel_id=1, source_target_pairs={{0,1},{1,0},{2,3},{3,2},{4,5},{5,4},{6,7},{7,6},{8,9},{9,8},{10,11... | collective-permute-start | bytes 98312 | tf_op jit(solution)/shard_map/ppermute | solution.py:32
  43.2 1.3 %collective-permute-start.15 = (bf16[3,128,128]{1,2,0:T(8,128)(2,1)S(1)}, bf16[3,128,128]{1,2,0:T(8,128)(2,1)S(1)}, u32[]{:S(2)}, u32[]{:S(2)}) collective-permute-start(bf16[3,128,128]{1,2,0:T(8,128)(2,1)S(1)} %collective-permute-done.13), channel_id=1, source_target_pairs={{0,1},{1,0},{2,3},{3,2},{4,5},{5,4},{6,7},{7,6},{8,9},{9,8},{10,11... | collective-permute-start | bytes 294920 | tf_op jit(solution)/shard_map/ppermute | solution.py:32
  45.4 6.7 %collective-permute-start.16 = (bf16[128,128]{0,1:T(8,128)(2,1)S(1)}, bf16[128,128]{0,1:T(8,128)(2,1)S(1)}, u32[]{:S(2)}, u32[]{:S(2)}) collective-permute-start(bf16[128,128]{0,1:T(8,128)(2,1)S(1)} %get-tuple-element.19), channel_id=1, source_target_pairs={{0,4},{1,5},{2,6},{3,7},{4,8},{5,9},{6,10},{7,11},{8,12},{9,13},{1... | collective-permute-start | bytes 98312 | tf_op jit(solution)/shard_map/ppermute | solution.py:25
  46.5 5.7 %collective-permute-start.17 = (bf16[128,128]{0,1:T(8,128)(2,1)S(1)}, bf16[128,128]{0,1:T(8,128)(2,1)S(1)}, u32[]{:S(2)}, u32[]{:S(2)}) collective-permute-start(bf16[128,128]{0,1:T(8,128)(2,1)S(1)} %get-tuple-element.19), channel_id=1, source_target_pairs={{0,8},{1,9},{2,10},{3,11},{4,12},{5,13},{6,14},{7,15},{8,0},{9,1},... | collective-permute-start | bytes 98312 | tf_op jit(solution)/shard_map/ppermute | solution.py:25
  49.0 3.9 %collective-permute-start.18 = (bf16[128,128]{0,1:T(8,128)(2,1)S(1)}, bf16[128,128]{0,1:T(8,128)(2,1)S(1)}, u32[]{:S(2)}, u32[]{:S(2)}) collective-permute-start(bf16[128,128]{0,1:T(8,128)(2,1)S(1)} %get-tuple-element.19), channel_id=1, source_target_pairs={{0,12},{1,13},{2,14},{3,15},{4,0},{5,1},{6,2},{7,3},{8,4},{9,5},{1... | collective-permute-start | bytes 98312 | tf_op jit(solution)/shard_map/ppermute | solution.py:25
  50.5 4.0 %collective-permute-start.20 = (bf16[1,128,128]{1,2,0:T(8,128)(2,1)S(1)}, bf16[1,128,128]{1,2,0:T(8,128)(2,1)S(1)}, u32[]{:S(2)}, u32[]{:S(2)}) collective-permute-start(bf16[1,128,128]{1,2,0:T(8,128)(2,1)S(1)} %bitcast.266), channel_id=1, source_target_pairs={{0,2},{1,3},{2,0},{3,1},{4,6},{5,7},{6,4},{7,5},{8,10},{9,11},{10,... | collective-permute-start | bytes 98312 | tf_op jit(solution)/shard_map/ppermute | solution.py:32
  53.0 4.7 %collective-permute-start.21 = (bf16[3,128,128]{1,2,0:T(8,128)(2,1)S(1)}, bf16[3,128,128]{1,2,0:T(8,128)(2,1)S(1)}, u32[]{:S(2)}, u32[]{:S(2)}) collective-permute-start(bf16[3,128,128]{1,2,0:T(8,128)(2,1)S(1)} %pad_maximum_fusion.9), channel_id=1, source_target_pairs={{0,2},{1,3},{2,0},{3,1},{4,6},{5,7},{6,4},{7,5},{8,10},{9,11},{10,... | collective-permute-start | bytes 294920 | tf_op jit(solution)/shard_map/ppermute | solution.py:32
  54.5 3.1 %collective-permute-start.19 = (bf16[4,128,128]{1,2,0:T(8,128)(2,1)S(1)}, bf16[4,128,128]{1,2,0:T(8,128)(2,1)S(1)}, u32[]{:S(2)}, u32[]{:S(2)}) collective-permute-start(bf16[4,128,128]{1,2,0:T(8,128)(2,1)S(1)} %pad_maximum_fusion.7), channel_id=1, source_target_pairs={{0,1},{1,0},{2,3},{3,2},{4,5},{5,4},{6,7},{7,6},{8,9},{9,8},{10,11... | collective-permute-start | bytes 393224 | tf_op jit(solution)/shard_map/ppermute | solution.py:32
  54.6 3.1 %collective-permute-start.22 = (bf16[1,128,128]{1,2,0:T(8,128)(2,1)S(1)}, bf16[1,128,128]{1,2,0:T(8,128)(2,1)S(1)}, u32[]{:S(2)}, u32[]{:S(2)}) collective-permute-start(bf16[1,128,128]{1,2,0:T(8,128)(2,1)S(1)} %collective-permute-done.20), channel_id=1, source_target_pairs={{0,1},{1,0},{2,3},{3,2},{4,5},{5,4},{6,7},{7,6},{8,9},{9,8},{10,11... | collective-permute-start | bytes 98312 | tf_op jit(solution)/shard_map/ppermute | solution.py:32
  57.6 1.3 %collective-permute-start.23 = (bf16[3,128,128]{1,2,0:T(8,128)(2,1)S(1)}, bf16[3,128,128]{1,2,0:T(8,128)(2,1)S(1)}, u32[]{:S(2)}, u32[]{:S(2)}) collective-permute-start(bf16[3,128,128]{1,2,0:T(8,128)(2,1)S(1)} %collective-permute-done.21), channel_id=1, source_target_pairs={{0,1},{1,0},{2,3},{3,2},{4,5},{5,4},{6,7},{7,6},{8,9},{9,8},{10,11... | collective-permute-start | bytes 294920 | tf_op jit(solution)/shard_map/ppermute | solution.py:32

commit v11 on v10

--- a/solution.py
+++ b/solution.py
@@ -32,7 +32,7 @@
     return lax.ppermute(x, "wide", [(d, d ^ mask) for d in range(wide)])
 
 
-def slab_stage(parts, wide, inner, early):
+def slab_stage(parts, wide, inner, early, direct=False):
     stack = parts[0] if len(parts) == 1 else jnp.concatenate(parts)
     if inner != 4:
         return [stack] + [swap(stack, wide, m) for m in range(1, inner)]
@@ -40,23 +40,18 @@
         rest = jnp.concatenate(parts[1:])
         across_own = swap(parts[0], wide, 2)
         across_rest = swap(rest, wide, 2)
-        return [
-            stack,
-            swap(stack, wide, 1),
-            across_own,
-            across_rest,
-            swap(across_own, wide, 1),
-            swap(across_rest, wide, 1),
-        ]
+        diagonal_own = swap(parts[0], wide, 3) if direct else swap(across_own, wide, 1)
+        diagonal_rest = swap(rest, wide, 3) if direct else swap(across_rest, wide, 1)
+        return [stack, swap(stack, wide, 1), across_own, across_rest, diagonal_own, diagonal_rest]
     across = swap(stack, wide, 2)
     return [stack, swap(stack, wide, 1), across, swap(across, wide, 1)]
 
 
-def gather_blocks(x, wide, early):
+def gather_blocks(x, wide, early, direct=False):
     inner = inner_size(wide)
     lines = wide // inner
     parts, shifted = line_stage(x, wide, inner)
-    pieces = slab_stage(parts, wide, inner, early)
+    pieces = slab_stage(parts, wide, inner, early, direct)
     me = lax.axis_index("wide")
     line = np.arange(lines, dtype=np.int32)
     source_line = (me // inner - line) % lines if shifted else jnp.asarray(line)
@@ -126,7 +121,7 @@
         current = advance(moment, retarded)
         results[moment] = current
         if moment > 0:
-            pieces, new_blocks = gather_blocks(current.astype(jnp.bfloat16), wide, True)
+            pieces, new_blocks = gather_blocks(current.astype(jnp.bfloat16), wide, True, direct=True)
             newer[moment] = jnp.concatenate(pieces)
             if recent is None:
                 recent = tiles_by_lag(

time: 60.8 us -> 61.7 us (1.015)
  waiting for transfers between devices: 17.1 us -> 18.6 us
  starting transfers between devices: 28.6 us -> 27.8 us
    ppermute x9, waiting for transfers between devices: 1.57 us -> 2.52 us  [line_stage(): parts.append(lax.ppermute(x, 'wide', pairs)[None])]
    ppermute x15, starting transfers between devices: 11.1 us -> 10.3 us  [swap(): return lax.ppermute(x, 'wide', [(d, d ^ mask) for d in range(wide)])]
  transfers between devices with their start and end apart: 24 -> 24, of which waited for: 8 -> 12; matrix products, arithmetic and copies ran while one was open for 18% -> 18% of each run, Pallas kernels for 0% -> 0%
where the time goes in v11:
time: 61.7 us; the launch traced here: 61.3 us
  starting transfers between devices  27.8 us (45%)
  waiting for transfers between devices  18.6 us (30%)
  matrix products  6.94 us (11%)
  local copies, waits for them, and re-layouts  4.43 us (7%)
  other arithmetic  3.15 us (5%)
    ppermute x9, starting transfers between devices, line_stage(): parts.append(lax.ppermute(x, 'wide', pairs)[None])  17.5 us
    ppermute x15, waiting for transfers between devices, swap(): return lax.ppermute(x, 'wide', [(d, d ^ mask) for d in range(wide)])  16 us
    ppermute x15, starting transfers between devices, swap(): return lax.ppermute(x, 'wide', [(d, d ^ mask) for d in range(wide)])  10.3 us
    dot_general x21, matrix products, rowwise(): return jnp.einsum(spec, tiles, currents, preferred_element_type=jnp.float32)  6.09 us
    ppermute x9, waiting for transfers between devices, line_stage(): parts.append(lax.ppermute(x, 'wide', pairs)[None])  2.52 us
    sort x1, other arithmetic, per_device(): column_of_block = jnp.argsort(block_owner)  1.9 us
  transfers between devices with their start and end apart: 24, of which 12 were waited for; matrix products, arithmetic and copies ran while one was open for 18% of the time, Pallas kernels for 0%

profile of v11, /device:TPU:0, one launch (start us, length us, event | category | flops | bytes accessed | tf_op | source)
XLA Modules:
  0.0 61.3 jit_solution(13113796763073756378)
XLA Ops:
  0.0 3.0 %collective-permute-start = (bf16[4,128,128]{2,1,0:T(8,128)(2,1)}, bf16[4,128,128]{2,1,0:T(8,128)(2,1)S(1)}, u32[]{:S(2)}, u32[]{:S(2)}) collective-permute-start(bf16[4,128,128]{2,1,0:T(8,128)(2,1)} %param.19), channel_id=1, source_target_pairs={{0,4},{1,5},{2,6},{3,7},{4,8},{5,9},{6,10},{7,11},{8,12},{9,13},{1... | collective-permute-start | bytes 393224 | tf_op jit(solution)/shard_map/ppermute | solution.py:25
  3.0 2.6 %collective-permute-start.1 = (bf16[4,128,128]{2,1,0:T(8,128)(2,1)}, bf16[4,128,128]{2,1,0:T(8,128)(2,1)S(1)}, u32[]{:S(2)}, u32[]{:S(2)}) collective-permute-start(bf16[4,128,128]{2,1,0:T(8,128)(2,1)} %param.19), channel_id=1, source_target_pairs={{0,8},{1,9},{2,10},{3,11},{4,12},{5,13},{6,14},{7,15},{8,0},{9,1},... | collective-permute-start | bytes 393224 | tf_op jit(solution)/shard_map/ppermute | solution.py:25
  5.6 1.3 %collective-permute-start.2 = (bf16[4,128,128]{2,1,0:T(8,128)(2,1)}, bf16[4,128,128]{2,1,0:T(8,128)(2,1)S(1)}, u32[]{:S(2)}, u32[]{:S(2)}) collective-permute-start(bf16[4,128,128]{2,1,0:T(8,128)(2,1)} %param.19), channel_id=1, source_target_pairs={{0,12},{1,13},{2,14},{3,15},{4,0},{5,1},{6,2},{7,3},{8,4},{9,5},{1... | collective-permute-start | bytes 393224 | tf_op jit(solution)/shard_map/ppermute | solution.py:25
  7.0 1.5 %collective-permute-start.4 = (bf16[1,4,128,128]{3,2,1,0:T(8,128)(2,1)}, bf16[1,4,128,128]{3,2,1,0:T(8,128)(2,1)S(1)}, u32[]{:S(2)}, u32[]{:S(2)}) collective-permute-start(bf16[1,4,128,128]{3,2,1,0:T(8,128)(2,1)} %bitcast.263), channel_id=1, source_target_pairs={{0,2},{1,3},{2,0},{3,1},{4,6},{5,7},{6,4},{7,5},{8,10},{9,11},{10,... | collective-permute-start | bytes 393224 | tf_op jit(solution)/shard_map/ppermute | solution.py:32
  8.7 1.9 %sort.17 = (s32[16]{0:T(128)}, s32[16]{0:T(128)S(1)}) sort(s32[16]{0:T(128)} %param.18, s32[16]{0:T(128)S(1)} %iota.5), dimensions={0}, to_apply=%region_0.0 | sort | flops 64 | bytes 256 | tf_op jit(solution)/shard_map/jit(argsort)/sort | solution.py:92
  10.6 0.7 %gather_fusion = s32[16]{0:T(128)S(1)} fusion(s32[16]{0:T(128)S(1)} %get-tuple-element.8, s32[1024]{0:T(1024)S(1)} %pad_clamp_fusion.1), kind=kCustom, calls=%fused_computation.clone | custom fusion | bytes 192 | tf_op jit(solution)/shard_map/jit(_take)/gather | solution.py:67
  11.3 0.8 %copy.18 = s32[16,2]{1,0:T(8,128)S(1)} copy(s32[16,2]{0,1:T(2,128)} %bitcast.272) | data formatting | bytes 256 | tf_op jit(solution)/shard_map/squeeze | solution.py:69
  12.0 0.7 %gather_fusion.2 = bf16[16,2,128,128]{3,2,1,0:T(8,128)(2,1)S(1)} fusion(bf16[16,2,128,128]{3,2,1,0:T(8,128)(2,1)S(1)} %bitcast.239, s32[1024]{0:T(1024)S(1)} %pad_clamp_fusion), kind=kCustom, calls=%fused_computation.2.clone | custom fusion | bytes 2097216 | tf_op jit(solution)/shard_map/jit(_take)/gather | solution.py:68
  12.8 0.6 gather_fusion.1
  14.5 1.6 %collective-permute-start.5 = (bf16[3,4,128,128]{3,2,1,0:T(8,128)(2,1)S(1)}, bf16[3,4,128,128]{3,2,1,0:T(8,128)(2,1)S(1)}, u32[]{:S(2)}, u32[]{:S(2)}) collective-permute-start(bf16[3,4,128,128]{3,2,1,0:T(8,128)(2,1)S(1)} %pad_maximum_fusion.4), channel_id=1, source_target_pairs={{0,2},{1,3},{2,0},{3,1},{4,6},{5,7},{6,4},{7,5},{8,10},{9,11},{10,... | collective-permute-start | bytes 1179656 | tf_op jit(solution)/shard_map/ppermute | solution.py:32
  16.3 0.3 convolution_bitcast_fusion.7
  16.9 0.6 collective-permute-start.6
  17.4 8.1 %collective-permute-done.5 = bf16[3,4,128,128]{3,2,1,0:T(8,128)(2,1)S(1)} collective-permute-done((bf16[3,4,128,128]{3,2,1,0:T(8,128)(2,1)S(1)}, bf16[3,4,128,128]{3,2,1,0:T(8,128)(2,1)S(1)}, u32[]{:S(2)}, u32[]{:S(2)}) %collective-permute-start.5) | collective-permute-done | bytes 393248 | tf_op jit(solution)/shard_map/ppermute | solution.py:32
  25.8 0.3 convolution_bitcast_fusion.5
  26.1 0.3 convolution_bitcast_fusion.3
  26.4 0.3 convolution_bitcast_fusion
  26.8 0.4 fusion.20
  27.4 0.3 fusion.19
  28.4 0.3 convolution_bitcast_fusion.2
  28.8 0.6 copy-done.2
  29.9 3.4 %collective-permute-start.8 = (bf16[128,128]{0,1:T(8,128)(2,1)S(1)}, bf16[128,128]{0,1:T(8,128)(2,1)S(1)}, u32[]{:S(2)}, u32[]{:S(2)}) collective-permute-start(bf16[128,128]{0,1:T(8,128)(2,1)S(1)} %get-tuple-element.21), channel_id=1, source_target_pairs={{0,4},{1,5},{2,6},{3,7},{4,8},{5,9},{6,10},{7,11},{8,12},{9,13},{1... | collective-permute-start | bytes 98312 | tf_op jit(solution)/shard_map/ppermute | solution.py:25
  33.3 0.6 collective-permute-start.9
  33.9 1.8 %collective-permute-start.10 = (bf16[128,128]{0,1:T(8,128)(2,1)S(1)}, bf16[128,128]{0,1:T(8,128)(2,1)S(1)}, u32[]{:S(2)}, u32[]{:S(2)}) collective-permute-start(bf16[128,128]{0,1:T(8,128)(2,1)S(1)} %get-tuple-element.21), channel_id=1, source_target_pairs={{0,12},{1,13},{2,14},{3,15},{4,0},{5,1},{6,2},{7,3},{8,4},{9,5},{1... | collective-permute-start | bytes 98312 | tf_op jit(solution)/shard_map/ppermute | solution.py:25
  35.8 1.5 %collective-permute-start.12 = (bf16[1,128,128]{1,2,0:T(8,128)(2,1)S(1)}, bf16[1,128,128]{1,2,0:T(8,128)(2,1)S(1)}, u32[]{:S(2)}, u32[]{:S(2)}) collective-permute-start(bf16[1,128,128]{1,2,0:T(8,128)(2,1)S(1)} %bitcast.269), channel_id=1, source_target_pairs={{0,2},{1,3},{2,0},{3,1},{4,6},{5,7},{6,4},{7,5},{8,10},{9,11},{10,... | collective-permute-start | bytes 98312 | tf_op jit(solution)/shard_map/ppermute | solution.py:32
  37.3 0.3 convolution_bitcast_fusion.4
  37.9 0.6 %collective-permute-done.9 = bf16[128,128]{0,1:T(8,128)(2,1)S(1)} collective-permute-done((bf16[128,128]{0,1:T(8,128)(2,1)S(1)}, bf16[128,128]{0,1:T(8,128)(2,1)S(1)}, u32[]{:S(2)}, u32[]{:S(2)}) %collective-permute-start.9) | collective-permute-done | bytes 32800 | tf_op jit(solution)/shard_map/ppermute | solution.py:25
  38.5 1.6 %collective-permute-start.13 = (bf16[3,128,128]{1,2,0:T(8,128)(2,1)S(1)}, bf16[3,128,128]{1,2,0:T(8,128)(2,1)S(1)}, u32[]{:S(2)}, u32[]{:S(2)}) collective-permute-start(bf16[3,128,128]{1,2,0:T(8,128)(2,1)S(1)} %pad_maximum_fusion.8), channel_id=1, source_target_pairs={{0,2},{1,3},{2,0},{3,1},{4,6},{5,7},{6,4},{7,5},{8,10},{9,11},{10,... | collective-permute-start | bytes 294920 | tf_op jit(solution)/shard_map/ppermute | solution.py:32
  40.1 0.6 %collective-permute-start.11 = (bf16[4,128,128]{1,2,0:T(8,128)(2,1)S(1)}, bf16[4,128,128]{1,2,0:T(8,128)(2,1)S(1)}, u32[]{:S(2)}, u32[]{:S(2)}) collective-permute-start(bf16[4,128,128]{1,2,0:T(8,128)(2,1)S(1)} %pad_maximum_fusion.6), channel_id=1, source_target_pairs={{0,1},{1,0},{2,3},{3,2},{4,5},{5,4},{6,7},{7,6},{8,9},{9,8},{10,11... | collective-permute-start | bytes 393224 | tf_op jit(solution)/shard_map/ppermute | solution.py:32
  40.8 1.0 %collective-permute-done.11 = bf16[4,128,128]{1,2,0:T(8,128)(2,1)S(1)} collective-permute-done((bf16[4,128,128]{1,2,0:T(8,128)(2,1)S(1)}, bf16[4,128,128]{1,2,0:T(8,128)(2,1)S(1)}, u32[]{:S(2)}, u32[]{:S(2)}) %collective-permute-start.11) | collective-permute-done | bytes 131104 | tf_op jit(solution)/shard_map/ppermute | solution.py:32
  41.8 1.7 %collective-permute-done.13 = bf16[3,128,128]{1,2,0:T(8,128)(2,1)S(1)} collective-permute-done((bf16[3,128,128]{1,2,0:T(8,128)(2,1)S(1)}, bf16[3,128,128]{1,2,0:T(8,128)(2,1)S(1)}, u32[]{:S(2)}, u32[]{:S(2)}) %collective-permute-start.13) | collective-permute-done | bytes 98336 | tf_op jit(solution)/shard_map/ppermute | solution.py:32
  43.6 1.6 %collective-permute-done.15 = bf16[3,128,128]{1,2,0:T(8,128)(2,1)S(1)} collective-permute-done((bf16[3,128,128]{1,2,0:T(8,128)(2,1)S(1)}, bf16[3,128,128]{1,2,0:T(8,128)(2,1)S(1)}, u32[]{:S(2)}, u32[]{:S(2)}) %collective-permute-start.15) | collective-permute-done | bytes 98336 | tf_op jit(solution)/shard_map/ppermute | solution.py:32
  45.2 0.3 convolution_bitcast_fusion.13
  46.1 1.1 %collective-permute-start.16 = (bf16[128,128]{0,1:T(8,128)(2,1)S(1)}, bf16[128,128]{0,1:T(8,128)(2,1)S(1)}, u32[]{:S(2)}, u32[]{:S(2)}) collective-permute-start(bf16[128,128]{0,1:T(8,128)(2,1)S(1)} %get-tuple-element.19), channel_id=1, source_target_pairs={{0,4},{1,5},{2,6},{3,7},{4,8},{5,9},{6,10},{7,11},{8,12},{9,13},{1... | collective-permute-start | bytes 98312 | tf_op jit(solution)/shard_map/ppermute | solution.py:25
  47.2 2.5 %collective-permute-start.17 = (bf16[128,128]{0,1:T(8,128)(2,1)S(1)}, bf16[128,128]{0,1:T(8,128)(2,1)S(1)}, u32[]{:S(2)}, u32[]{:S(2)}) collective-permute-start(bf16[128,128]{0,1:T(8,128)(2,1)S(1)} %get-tuple-element.19), channel_id=1, source_target_pairs={{0,8},{1,9},{2,10},{3,11},{4,12},{5,13},{6,14},{7,15},{8,0},{9,1},... | collective-permute-start | bytes 98312 | tf_op jit(solution)/shard_map/ppermute | solution.py:25
  49.7 1.0 %collective-permute-start.18 = (bf16[128,128]{0,1:T(8,128)(2,1)S(1)}, bf16[128,128]{0,1:T(8,128)(2,1)S(1)}, u32[]{:S(2)}, u32[]{:S(2)}) collective-permute-start(bf16[128,128]{0,1:T(8,128)(2,1)S(1)} %get-tuple-element.19), channel_id=1, source_target_pairs={{0,12},{1,13},{2,14},{3,15},{4,0},{5,1},{6,2},{7,3},{8,4},{9,5},{1... | collective-permute-start | bytes 98312 | tf_op jit(solution)/shard_map/ppermute | solution.py:25
  50.7 0.6 collective-permute-start.20
  51.4 0.5 convolution_bitcast_fusion.11
  52.0 0.7 %collective-permute-done.17 = bf16[128,128]{0,1:T(8,128)(2,1)S(1)} collective-permute-done((bf16[128,128]{0,1:T(8,128)(2,1)S(1)}, bf16[128,128]{0,1:T(8,128)(2,1)S(1)}, u32[]{:S(2)}, u32[]{:S(2)}) %collective-permute-start.17) | collective-permute-done | bytes 32800 | tf_op jit(solution)/shard_map/ppermute | solution.py:25
  52.7 0.9 %collective-permute-done.18 = bf16[128,128]{0,1:T(8,128)(2,1)S(1)} collective-permute-done((bf16[128,128]{0,1:T(8,128)(2,1)S(1)}, bf16[128,128]{0,1:T(8,128)(2,1)S(1)}, u32[]{:S(2)}, u32[]{:S(2)}) %collective-permute-start.18) | collective-permute-done | bytes 32800 | tf_op jit(solution)/shard_map/ppermute | solution.py:25
  53.6 0.8 %collective-permute-start.21 = (bf16[3,128,128]{1,2,0:T(8,128)(2,1)S(1)}, bf16[3,128,128]{1,2,0:T(8,128)(2,1)S(1)}, u32[]{:S(2)}, u32[]{:S(2)}) collective-permute-start(bf16[3,128,128]{1,2,0:T(8,128)(2,1)S(1)} %pad_maximum_fusion.9), channel_id=1, source_target_pairs={{0,2},{1,3},{2,0},{3,1},{4,6},{5,7},{6,4},{7,5},{8,10},{9,11},{10,... | collective-permute-start | bytes 294920 | tf_op jit(solution)/shard_map/ppermute | solution.py:32
  54.5 0.4 collective-permute-start.23
  54.9 1.0 %collective-permute-start.19 = (bf16[4,128,128]{1,2,0:T(8,128)(2,1)S(1)}, bf16[4,128,128]{1,2,0:T(8,128)(2,1)S(1)}, u32[]{:S(2)}, u32[]{:S(2)}) collective-permute-start(bf16[4,128,128]{1,2,0:T(8,128)(2,1)S(1)} %pad_maximum_fusion.7), channel_id=1, source_target_pairs={{0,1},{1,0},{2,3},{3,2},{4,5},{5,4},{6,7},{7,6},{8,9},{9,8},{10,11... | collective-permute-start | bytes 393224 | tf_op jit(solution)/shard_map/ppermute | solution.py:32
  55.9 1.0 %collective-permute-done.19 = bf16[4,128,128]{1,2,0:T(8,128)(2,1)S(1)} collective-permute-done((bf16[4,128,128]{1,2,0:T(8,128)(2,1)S(1)}, bf16[4,128,128]{1,2,0:T(8,128)(2,1)S(1)}, u32[]{:S(2)}, u32[]{:S(2)}) %collective-permute-start.19) | collective-permute-done | bytes 131104 | tf_op jit(solution)/shard_map/ppermute | solution.py:32
  56.9 2.3 %collective-permute-done.21 = bf16[3,128,128]{1,2,0:T(8,128)(2,1)S(1)} collective-permute-done((bf16[3,128,128]{1,2,0:T(8,128)(2,1)S(1)}, bf16[3,128,128]{1,2,0:T(8,128)(2,1)S(1)}, u32[]{:S(2)}, u32[]{:S(2)}) %collective-permute-start.21) | collective-permute-done | bytes 98336 | tf_op jit(solution)/shard_map/ppermute | solution.py:32
  59.2 0.3 collective-permute-done.23
  59.6 0.3 convolution_bitcast_fusion.12
  60.1 0.3 convolution_bitcast_fusion.10
  60.4 0.8 %copy.24 = f32[3,128,128]{2,1,0:T(8,128)} copy(f32[3,128,128]{1,2,0:T(8,128)S(1)} %pad_maximum_fusion.5) | data formatting | bytes 393216 | tf_op jit(solution)/shard_map/stack | solution.py:134
  (74 shorter events, 5.0 us)
Async XLA Ops:
  0.0 12.0 %copy-start = (bf16[1,16,2,128,128]{4,3,2,1,0:T(8,128)(2,1)S(1)}, bf16[1,16,2,128,128]{4,3,2,1,0:T(8,128)(2,1)}, u32[]{:S(2)}) copy-start(bf16[1,16,2,128,128]{4,3,2,1,0:T(8,128)(2,1)} %param.16) | copy-start | bytes 3145732
  0.0 14.3 %collective-permute-start = (bf16[4,128,128]{2,1,0:T(8,128)(2,1)}, bf16[4,128,128]{2,1,0:T(8,128)(2,1)S(1)}, u32[]{:S(2)}, u32[]{:S(2)}) collective-permute-start(bf16[4,128,128]{2,1,0:T(8,128)(2,1)} %param.19), channel_id=1, source_target_pairs={{0,4},{1,5},{2,6},{3,7},{4,8},{5,9},{6,10},{7,11},{8,12},{9,13},{1... | collective-permute-start | bytes 393224 | tf_op jit(solution)/shard_map/ppermute | solution.py:25
  3.0 11.4 %collective-permute-start.1 = (bf16[4,128,128]{2,1,0:T(8,128)(2,1)}, bf16[4,128,128]{2,1,0:T(8,128)(2,1)S(1)}, u32[]{:S(2)}, u32[]{:S(2)}) collective-permute-start(bf16[4,128,128]{2,1,0:T(8,128)(2,1)} %param.19), channel_id=1, source_target_pairs={{0,8},{1,9},{2,10},{3,11},{4,12},{5,13},{6,14},{7,15},{8,0},{9,1},... | collective-permute-start | bytes 393224 | tf_op jit(solution)/shard_map/ppermute | solution.py:25
  5.6 8.9 %collective-permute-start.2 = (bf16[4,128,128]{2,1,0:T(8,128)(2,1)}, bf16[4,128,128]{2,1,0:T(8,128)(2,1)S(1)}, u32[]{:S(2)}, u32[]{:S(2)}) collective-permute-start(bf16[4,128,128]{2,1,0:T(8,128)(2,1)} %param.19), channel_id=1, source_target_pairs={{0,12},{1,13},{2,14},{3,15},{4,0},{5,1},{6,2},{7,3},{8,4},{9,5},{1... | collective-permute-start | bytes 393224 | tf_op jit(solution)/shard_map/ppermute | solution.py:25
  7.0 9.9 %collective-permute-start.4 = (bf16[1,4,128,128]{3,2,1,0:T(8,128)(2,1)}, bf16[1,4,128,128]{3,2,1,0:T(8,128)(2,1)S(1)}, u32[]{:S(2)}, u32[]{:S(2)}) collective-permute-start(bf16[1,4,128,128]{3,2,1,0:T(8,128)(2,1)} %bitcast.263), channel_id=1, source_target_pairs={{0,2},{1,3},{2,0},{3,1},{4,6},{5,7},{6,4},{7,5},{8,10},{9,11},{10,... | collective-permute-start | bytes 393224 | tf_op jit(solution)/shard_map/ppermute | solution.py:32
  14.1 2.0 %copy-start.3 = (bf16[4,128,128]{2,1,0:T(8,128)(2,1)S(1)}, bf16[4,128,128]{2,1,0:T(8,128)(2,1)}, u32[]{:S(2)}) copy-start(bf16[4,128,128]{2,1,0:T(8,128)(2,1)} %param.19) | copy-start | bytes 393220
  14.5 11.0 %collective-permute-start.5 = (bf16[3,4,128,128]{3,2,1,0:T(8,128)(2,1)S(1)}, bf16[3,4,128,128]{3,2,1,0:T(8,128)(2,1)S(1)}, u32[]{:S(2)}, u32[]{:S(2)}) collective-permute-start(bf16[3,4,128,128]{3,2,1,0:T(8,128)(2,1)S(1)} %pad_maximum_fusion.4), channel_id=1, source_target_pairs={{0,2},{1,3},{2,0},{3,1},{4,6},{5,7},{6,4},{7,5},{8,10},{9,11},{10,... | collective-permute-start | bytes 1179656 | tf_op jit(solution)/shard_map/ppermute | solution.py:32
  16.2 10.2 %collective-permute-start.3 = (bf16[4,4,128,128]{3,2,1,0:T(8,128)(2,1)S(1)}, bf16[4,4,128,128]{3,2,1,0:T(8,128)(2,1)S(1)}, u32[]{:S(2)}, u32[]{:S(2)}) collective-permute-start(bf16[4,4,128,128]{3,2,1,0:T(8,128)(2,1)S(1)} %pad_maximum_fusion.3), channel_id=1, source_target_pairs={{0,1},{1,0},{2,3},{3,2},{4,5},{5,4},{6,7},{7,6},{8,9},{9,8},{10,11... | collective-permute-start | bytes 1572872 | tf_op jit(solution)/shard_map/ppermute | solution.py:32
  16.9 11.9 %collective-permute-start.6 = (bf16[1,4,128,128]{3,2,1,0:T(8,128)(2,1)S(1)}, bf16[1,4,128,128]{3,2,1,0:T(8,128)(2,1)S(1)}, u32[]{:S(2)}, u32[]{:S(2)}) collective-permute-start(bf16[1,4,128,128]{3,2,1,0:T(8,128)(2,1)S(1)} %collective-permute-done.4), channel_id=1, source_target_pairs={{0,1},{1,0},{2,3},{3,2},{4,5},{5,4},{6,7},{7,6},{8,9},{9,8},{10,11... | collective-permute-start | bytes 393224 | tf_op jit(solution)/shard_map/ppermute | solution.py:32
  25.5 2.9 %collective-permute-start.7 = (bf16[3,4,128,128]{3,2,1,0:T(8,128)(2,1)S(1)}, bf16[3,4,128,128]{3,2,1,0:T(8,128)(2,1)S(1)}, u32[]{:S(2)}, u32[]{:S(2)}) collective-permute-start(bf16[3,4,128,128]{3,2,1,0:T(8,128)(2,1)S(1)} %collective-permute-done.5), channel_id=1, source_target_pairs={{0,1},{1,0},{2,3},{3,2},{4,5},{5,4},{6,7},{7,6},{8,9},{9,8},{10,11... | collective-permute-start | bytes 1179656 | tf_op jit(solution)/shard_map/ppermute | solution.py:32
  28.4 0.9 %copy-start.2 = (f32[3,128,128]{2,1,0:T(8,128)S(1)}, f32[3,128,128]{2,1,0:T(8,128)}, u32[]{:S(2)}) copy-start(f32[3,128,128]{2,1,0:T(8,128)} %param.20) | copy-start | bytes 589828
  28.8 0.9 %copy-start.1 = (f32[1,128,128]{2,1,0:T(8,128)S(1)}, f32[1,128,128]{2,1,0:T(8,128)}, u32[]{:S(2)}) copy-start(f32[1,128,128]{2,1,0:T(8,128)} %param.21) | copy-start | bytes 196612
  29.9 7.9 %collective-permute-start.8 = (bf16[128,128]{0,1:T(8,128)(2,1)S(1)}, bf16[128,128]{0,1:T(8,128)(2,1)S(1)}, u32[]{:S(2)}, u32[]{:S(2)}) collective-permute-start(bf16[128,128]{0,1:T(8,128)(2,1)S(1)} %get-tuple-element.21), channel_id=1, source_target_pairs={{0,4},{1,5},{2,6},{3,7},{4,8},{5,9},{6,10},{7,11},{8,12},{9,13},{1... | collective-permute-start | bytes 98312 | tf_op jit(solution)/shard_map/ppermute | solution.py:25
  33.3 5.2 %collective-permute-start.9 = (bf16[128,128]{0,1:T(8,128)(2,1)S(1)}, bf16[128,128]{0,1:T(8,128)(2,1)S(1)}, u32[]{:S(2)}, u32[]{:S(2)}) collective-permute-start(bf16[128,128]{0,1:T(8,128)(2,1)S(1)} %get-tuple-element.21), channel_id=1, source_target_pairs={{0,8},{1,9},{2,10},{3,11},{4,12},{5,13},{6,14},{7,15},{8,0},{9,1},... | collective-permute-start | bytes 98312 | tf_op jit(solution)/shard_map/ppermute | solution.py:25
  33.9 4.6 %collective-permute-start.10 = (bf16[128,128]{0,1:T(8,128)(2,1)S(1)}, bf16[128,128]{0,1:T(8,128)(2,1)S(1)}, u32[]{:S(2)}, u32[]{:S(2)}) collective-permute-start(bf16[128,128]{0,1:T(8,128)(2,1)S(1)} %get-tuple-element.21), channel_id=1, source_target_pairs={{0,12},{1,13},{2,14},{3,15},{4,0},{5,1},{6,2},{7,3},{8,4},{9,5},{1... | collective-permute-start | bytes 98312 | tf_op jit(solution)/shard_map/ppermute | solution.py:25
  35.8 6.0 %collective-permute-start.12 = (bf16[1,128,128]{1,2,0:T(8,128)(2,1)S(1)}, bf16[1,128,128]{1,2,0:T(8,128)(2,1)S(1)}, u32[]{:S(2)}, u32[]{:S(2)}) collective-permute-start(bf16[1,128,128]{1,2,0:T(8,128)(2,1)S(1)} %bitcast.269), channel_id=1, source_target_pairs={{0,2},{1,3},{2,0},{3,1},{4,6},{5,7},{6,4},{7,5},{8,10},{9,11},{10,... | collective-permute-start | bytes 98312 | tf_op jit(solution)/shard_map/ppermute | solution.py:32
  37.3 6.3 %collective-permute-start.14 = (bf16[1,128,128]{1,2,0:T(8,128)(2,1)S(1)}, bf16[1,128,128]{1,2,0:T(8,128)(2,1)S(1)}, u32[]{:S(2)}, u32[]{:S(2)}) collective-permute-start(bf16[1,128,128]{1,2,0:T(8,128)(2,1)S(1)} %bitcast.270), channel_id=1, source_target_pairs={{0,3},{1,2},{2,1},{3,0},{4,7},{5,6},{6,5},{7,4},{8,11},{9,10},{10,... | collective-permute-start | bytes 98312 | tf_op jit(solution)/shard_map/ppermute | solution.py:32
  38.5 5.0 %collective-permute-start.13 = (bf16[3,128,128]{1,2,0:T(8,128)(2,1)S(1)}, bf16[3,128,128]{1,2,0:T(8,128)(2,1)S(1)}, u32[]{:S(2)}, u32[]{:S(2)}) collective-permute-start(bf16[3,128,128]{1,2,0:T(8,128)(2,1)S(1)} %pad_maximum_fusion.8), channel_id=1, source_target_pairs={{0,2},{1,3},{2,0},{3,1},{4,6},{5,7},{6,4},{7,5},{8,10},{9,11},{10,... | collective-permute-start | bytes 294920 | tf_op jit(solution)/shard_map/ppermute | solution.py:32
  40.1 5.1 %collective-permute-start.15 = (bf16[3,128,128]{1,2,0:T(8,128)(2,1)S(1)}, bf16[3,128,128]{1,2,0:T(8,128)(2,1)S(1)}, u32[]{:S(2)}, u32[]{:S(2)}) collective-permute-start(bf16[3,128,128]{1,2,0:T(8,128)(2,1)S(1)} %pad_maximum_fusion.8), channel_id=1, source_target_pairs={{0,3},{1,2},{2,1},{3,0},{4,7},{5,6},{6,5},{7,4},{8,11},{9,10},{10,... | collective-permute-start | bytes 294920 | tf_op jit(solution)/shard_map/ppermute | solution.py:32
  40.1 1.6 %collective-permute-start.11 = (bf16[4,128,128]{1,2,0:T(8,128)(2,1)S(1)}, bf16[4,128,128]{1,2,0:T(8,128)(2,1)S(1)}, u32[]{:S(2)}, u32[]{:S(2)}) collective-permute-start(bf16[4,128,128]{1,2,0:T(8,128)(2,1)S(1)} %pad_maximum_fusion.6), channel_id=1, source_target_pairs={{0,1},{1,0},{2,3},{3,2},{4,5},{5,4},{6,7},{7,6},{8,9},{9,8},{10,11... | collective-permute-start | bytes 393224 | tf_op jit(solution)/shard_map/ppermute | solution.py:32
  46.1 6.0 %collective-permute-start.16 = (bf16[128,128]{0,1:T(8,128)(2,1)S(1)}, bf16[128,128]{0,1:T(8,128)(2,1)S(1)}, u32[]{:S(2)}, u32[]{:S(2)}) collective-permute-start(bf16[128,128]{0,1:T(8,128)(2,1)S(1)} %get-tuple-element.19), channel_id=1, source_target_pairs={{0,4},{1,5},{2,6},{3,7},{4,8},{5,9},{6,10},{7,11},{8,12},{9,13},{1... | collective-permute-start | bytes 98312 | tf_op jit(solution)/shard_map/ppermute | solution.py:25
  47.2 5.6 %collective-permute-start.17 = (bf16[128,128]{0,1:T(8,128)(2,1)S(1)}, bf16[128,128]{0,1:T(8,128)(2,1)S(1)}, u32[]{:S(2)}, u32[]{:S(2)}) collective-permute-start(bf16[128,128]{0,1:T(8,128)(2,1)S(1)} %get-tuple-element.19), channel_id=1, source_target_pairs={{0,8},{1,9},{2,10},{3,11},{4,12},{5,13},{6,14},{7,15},{8,0},{9,1},... | collective-permute-start | bytes 98312 | tf_op jit(solution)/shard_map/ppermute | solution.py:25
  49.7 3.9 %collective-permute-start.18 = (bf16[128,128]{0,1:T(8,128)(2,1)S(1)}, bf16[128,128]{0,1:T(8,128)(2,1)S(1)}, u32[]{:S(2)}, u32[]{:S(2)}) collective-permute-start(bf16[128,128]{0,1:T(8,128)(2,1)S(1)} %get-tuple-element.19), channel_id=1, source_target_pairs={{0,12},{1,13},{2,14},{3,15},{4,0},{5,1},{6,2},{7,3},{8,4},{9,5},{1... | collective-permute-start | bytes 98312 | tf_op jit(solution)/shard_map/ppermute | solution.py:25
  50.7 6.1 %collective-permute-start.20 = (bf16[1,128,128]{1,2,0:T(8,128)(2,1)S(1)}, bf16[1,128,128]{1,2,0:T(8,128)(2,1)S(1)}, u32[]{:S(2)}, u32[]{:S(2)}) collective-permute-start(bf16[1,128,128]{1,2,0:T(8,128)(2,1)S(1)} %bitcast.266), channel_id=1, source_target_pairs={{0,2},{1,3},{2,0},{3,1},{4,6},{5,7},{6,4},{7,5},{8,10},{9,11},{10,... | collective-permute-start | bytes 98312 | tf_op jit(solution)/shard_map/ppermute | solution.py:32
  51.3 7.9 %collective-permute-start.22 = (bf16[1,128,128]{1,2,0:T(8,128)(2,1)S(1)}, bf16[1,128,128]{1,2,0:T(8,128)(2,1)S(1)}, u32[]{:S(2)}, u32[]{:S(2)}) collective-permute-start(bf16[1,128,128]{1,2,0:T(8,128)(2,1)S(1)} %bitcast.267), channel_id=1, source_target_pairs={{0,3},{1,2},{2,1},{3,0},{4,7},{5,6},{6,5},{7,4},{8,11},{9,10},{10,... | collective-permute-start | bytes 98312 | tf_op jit(solution)/shard_map/ppermute | solution.py:32
  53.6 5.5 %collective-permute-start.21 = (bf16[3,128,128]{1,2,0:T(8,128)(2,1)S(1)}, bf16[3,128,128]{1,2,0:T(8,128)(2,1)S(1)}, u32[]{:S(2)}, u32[]{:S(2)}) collective-permute-start(bf16[3,128,128]{1,2,0:T(8,128)(2,1)S(1)} %pad_maximum_fusion.9), channel_id=1, source_target_pairs={{0,2},{1,3},{2,0},{3,1},{4,6},{5,7},{6,4},{7,5},{8,10},{9,11},{10,... | collective-permute-start | bytes 294920 | tf_op jit(solution)/shard_map/ppermute | solution.py:32
  54.5 5.1 %collective-permute-start.23 = (bf16[3,128,128]{1,2,0:T(8,128)(2,1)S(1)}, bf16[3,128,128]{1,2,0:T(8,128)(2,1)S(1)}, u32[]{:S(2)}, u32[]{:S(2)}) collective-permute-start(bf16[3,128,128]{1,2,0:T(8,128)(2,1)S(1)} %pad_maximum_fusion.9), channel_id=1, source_target_pairs={{0,3},{1,2},{2,1},{3,0},{4,7},{5,6},{6,5},{7,4},{8,11},{9,10},{10,... | collective-permute-start | bytes 294920 | tf_op jit(solution)/shard_map/ppermute | solution.py:32
  54.9 2.0 %collective-permute-start.19 = (bf16[4,128,128]{1,2,0:T(8,128)(2,1)S(1)}, bf16[4,128,128]{1,2,0:T(8,128)(2,1)S(1)}, u32[]{:S(2)}, u32[]{:S(2)}) collective-permute-start(bf16[4,128,128]{1,2,0:T(8,128)(2,1)S(1)} %pad_maximum_fusion.7), channel_id=1, source_target_pairs={{0,1},{1,0},{2,3},{3,2},{4,5},{5,4},{6,7},{7,6},{8,9},{9,8},{10,11... | collective-permute-start | bytes 393224 | tf_op jit(solution)/shard_map/ppermute | solution.py:32

commit v12 on v10

--- a/solution.py
+++ b/solution.py
@@ -122,12 +122,16 @@
             )
             retarded = term if retarded is None else retarded + term
         for delay in range(1, first):
-            retarded = retarded + rowwise(recent[:, delay - 1], newer[moment + delay])
+            for low, high, piece in newer[moment + delay]:
+                retarded = retarded + rowwise(recent[low:high, delay - 1], piece)
         current = advance(moment, retarded)
         results[moment] = current
         if moment > 0:
             pieces, new_blocks = gather_blocks(current.astype(jnp.bfloat16), wide, True)
-            newer[moment] = jnp.concatenate(pieces)
+            bounds = np.cumsum([0] + [piece.shape[0] for piece in pieces])
+            newer[moment] = [
+                (bounds[k], bounds[k + 1], piece) for k, piece in enumerate(pieces)
+            ]
             if recent is None:
                 recent = tiles_by_lag(
                     retarded_tiles,

time: 60.8 us -> 61.7 us (1.015)
  starting transfers between devices: 28.6 us -> 24.2 us
  waiting for transfers between devices: 17.1 us -> 20 us
  matrix products: 6.94 us -> 9.4 us
    ppermute x9, waiting for transfers between devices: 1.57 us -> 7.84 us  [line_stage(): parts.append(lax.ppermute(x, 'wide', pairs)[None])]
    ppermute x9, starting transfers between devices: 17.5 us -> 13.1 us  [line_stage(): parts.append(lax.ppermute(x, 'wide', pairs)[None])]
    ppermute x15, waiting for transfers between devices: 15.5 us -> 12.2 us  [swap(): return lax.ppermute(x, 'wide', [(d, d ^ mask) for d in range(wide)])]
    dot_general x21 -> x36, matrix products: 6.09 us -> 8.55 us  [rowwise(): return jnp.einsum(spec, tiles, currents, preferred_element_type=jnp.float32)]
  transfers between devices with their start and end apart: 24 -> 24, of which waited for: 8 -> 9; matrix products, arithmetic and copies ran while one was open for 18% -> 22% of each run, Pallas kernels for 0% -> 0%
where the time goes in v12:
time: 61.7 us; the launch traced here: 61.6 us
  starting transfers between devices  24.2 us (39%)
  waiting for transfers between devices  20 us (32%)
  matrix products  9.4 us (15%)
  local copies, waits for them, and re-layouts  4.25 us (7%)
  other arithmetic  3.19 us (5%)
    ppermute x9, starting transfers between devices, line_stage(): parts.append(lax.ppermute(x, 'wide', pairs)[None])  13.1 us
    ppermute x15, waiting for transfers between devices, swap(): return lax.ppermute(x, 'wide', [(d, d ^ mask) for d in range(wide)])  12.2 us
    ppermute x15, starting transfers between devices, swap(): return lax.ppermute(x, 'wide', [(d, d ^ mask) for d in range(wide)])  11.1 us
    dot_general x36, matrix products, rowwise(): return jnp.einsum(spec, tiles, currents, preferred_element_type=jnp.float32)  8.55 us
    ppermute x9, waiting for transfers between devices, line_stage(): parts.append(lax.ppermute(x, 'wide', pairs)[None])  7.84 us
    sort x1, other arithmetic, per_device(): column_of_block = jnp.argsort(block_owner)  1.9 us
  transfers between devices with their start and end apart: 24, of which 9 were waited for; matrix products, arithmetic and copies ran while one was open for 22% of the time, Pallas kernels for 0%

profile of v12, /device:TPU:0, one launch (start us, length us, event | category | flops | bytes accessed | tf_op | source)
XLA Modules:
  0.0 61.6 jit_solution(14673804221602911724)
XLA Ops:
  0.0 5.0 %collective-permute-start.2 = (bf16[4,128,128]{2,1,0:T(8,128)(2,1)}, bf16[4,128,128]{2,1,0:T(8,128)(2,1)S(1)}, u32[]{:S(2)}, u32[]{:S(2)}) collective-permute-start(bf16[4,128,128]{2,1,0:T(8,128)(2,1)} %param.19), channel_id=1, source_target_pairs={{0,12},{1,13},{2,14},{3,15},{4,0},{5,1},{6,2},{7,3},{8,4},{9,5},{1... | collective-permute-start | bytes 393224 | tf_op jit(solution)/shard_map/ppermute | solution.py:25
  5.1 1.0 %collective-permute-start = (bf16[4,128,128]{2,1,0:T(8,128)(2,1)}, bf16[4,128,128]{2,1,0:T(8,128)(2,1)S(1)}, u32[]{:S(2)}, u32[]{:S(2)}) collective-permute-start(bf16[4,128,128]{2,1,0:T(8,128)(2,1)} %param.19), channel_id=1, source_target_pairs={{0,4},{1,5},{2,6},{3,7},{4,8},{5,9},{6,10},{7,11},{8,12},{9,13},{1... | collective-permute-start | bytes 393224 | tf_op jit(solution)/shard_map/ppermute | solution.py:25
  6.1 1.5 %collective-permute-start.4 = (bf16[1,4,128,128]{3,2,1,0:T(8,128)(2,1)}, bf16[1,4,128,128]{3,2,1,0:T(8,128)(2,1)S(1)}, u32[]{:S(2)}, u32[]{:S(2)}) collective-permute-start(bf16[1,4,128,128]{3,2,1,0:T(8,128)(2,1)} %bitcast.337), channel_id=1, source_target_pairs={{0,2},{1,3},{2,0},{3,1},{4,6},{5,7},{6,4},{7,5},{8,10},{9,11},{10,... | collective-permute-start | bytes 393224 | tf_op jit(solution)/shard_map/ppermute | solution.py:32
  7.6 0.8 %copy.18 = s32[16,2]{1,0:T(8,128)S(1)} copy(s32[16,2]{0,1:T(2,128)} %bitcast.340) | data formatting | bytes 256 | tf_op jit(solution)/shard_map/squeeze | solution.py:74
  8.5 1.9 %sort.17 = (s32[16]{0:T(128)}, s32[16]{0:T(128)S(1)}) sort(s32[16]{0:T(128)} %param.18, s32[16]{0:T(128)S(1)} %iota.5), dimensions={0}, to_apply=%region_0.0 | sort | flops 64 | bytes 256 | tf_op jit(solution)/shard_map/jit(argsort)/sort | solution.py:97
  10.4 0.7 %gather_fusion = s32[16]{0:T(128)S(1)} fusion(s32[16]{0:T(128)S(1)} %get-tuple-element.8, s32[1024]{0:T(1024)S(1)} %pad_clamp_fusion.1), kind=kCustom, calls=%fused_computation.clone | custom fusion | bytes 192 | tf_op jit(solution)/shard_map/jit(_take)/gather | solution.py:72
  11.1 0.6 gather_fusion.1
  11.8 0.3 compare_reduce_fusion.3
  12.0 0.8 %gather_fusion.2 = bf16[16,2,128,128]{3,2,1,0:T(8,128)(2,1)S(1)} fusion(bf16[16,2,128,128]{3,2,1,0:T(8,128)(2,1)S(1)} %bitcast.297, s32[1024]{0:T(1024)S(1)} %pad_clamp_fusion), kind=kCustom, calls=%fused_computation.2.clone | custom fusion | bytes 2097216 | tf_op jit(solution)/shard_map/jit(_take)/gather | solution.py:73
  13.0 0.3 bitcast_select_fusion.2
  13.5 3.0 %collective-permute-done.1 = bf16[4,128,128]{2,1,0:T(8,128)(2,1)S(1)} collective-permute-done((bf16[4,128,128]{2,1,0:T(8,128)(2,1)}, bf16[4,128,128]{2,1,0:T(8,128)(2,1)S(1)}, u32[]{:S(2)}, u32[]{:S(2)}) %collective-permute-start.1) | collective-permute-done | bytes 131104 | tf_op jit(solution)/shard_map/ppermute | solution.py:25
  16.5 1.6 %collective-permute-start.5 = (bf16[3,4,128,128]{3,2,1,0:T(8,128)(2,1)S(1)}, bf16[3,4,128,128]{3,2,1,0:T(8,128)(2,1)S(1)}, u32[]{:S(2)}, u32[]{:S(2)}) collective-permute-start(bf16[3,4,128,128]{3,2,1,0:T(8,128)(2,1)S(1)} %pad_maximum_fusion.4), channel_id=1, source_target_pairs={{0,2},{1,3},{2,0},{3,1},{4,6},{5,7},{6,4},{7,5},{8,10},{9,11},{10,... | collective-permute-start | bytes 1179656 | tf_op jit(solution)/shard_map/ppermute | solution.py:32
  18.3 0.3 convolution_bitcast_fusion.13
  18.6 0.3 convolution_bitcast_fusion.15
  18.9 0.6 collective-permute-start.6
  19.4 7.5 %collective-permute-done.5 = bf16[3,4,128,128]{3,2,1,0:T(8,128)(2,1)S(1)} collective-permute-done((bf16[3,4,128,128]{3,2,1,0:T(8,128)(2,1)S(1)}, bf16[3,4,128,128]{3,2,1,0:T(8,128)(2,1)S(1)}, u32[]{:S(2)}, u32[]{:S(2)}) %collective-permute-start.5) | collective-permute-done | bytes 393248 | tf_op jit(solution)/shard_map/ppermute | solution.py:32
  27.2 0.3 convolution_bitcast_fusion.11
  27.5 0.3 convolution_bitcast_fusion.9
  27.8 0.3 convolution_bitcast_fusion
  28.2 0.4 fusion.32
  28.5 0.3 fusion.31
  28.9 0.3 fusion.30
  29.8 0.3 convolution_bitcast_fusion.8
  30.2 0.6 copy-done.2
  31.0 0.3 bitcast_convert_fusion.1
  31.3 0.7 %collective-permute-start.10 = (bf16[128,128]{0,1:T(8,128)(2,1)S(1)}, bf16[128,128]{0,1:T(8,128)(2,1)S(1)}, u32[]{:S(2)}, u32[]{:S(2)}) collective-permute-start(bf16[128,128]{0,1:T(8,128)(2,1)S(1)} %get-tuple-element.26), channel_id=1, source_target_pairs={{0,12},{1,13},{2,14},{3,15},{4,0},{5,1},{6,2},{7,3},{8,4},{9,5},{1... | collective-permute-start | bytes 98312 | tf_op jit(solution)/shard_map/ppermute | solution.py:25
  32.0 2.0 %collective-permute-start.9 = (bf16[128,128]{0,1:T(8,128)(2,1)S(1)}, bf16[128,128]{0,1:T(8,128)(2,1)S(1)}, u32[]{:S(2)}, u32[]{:S(2)}) collective-permute-start(bf16[128,128]{0,1:T(8,128)(2,1)S(1)} %get-tuple-element.26), channel_id=1, source_target_pairs={{0,8},{1,9},{2,10},{3,11},{4,12},{5,13},{6,14},{7,15},{8,0},{9,1},... | collective-permute-start | bytes 98312 | tf_op jit(solution)/shard_map/ppermute | solution.py:25
  33.9 1.9 %collective-permute-start.8 = (bf16[128,128]{0,1:T(8,128)(2,1)S(1)}, bf16[128,128]{0,1:T(8,128)(2,1)S(1)}, u32[]{:S(2)}, u32[]{:S(2)}) collective-permute-start(bf16[128,128]{0,1:T(8,128)(2,1)S(1)} %get-tuple-element.26), channel_id=1, source_target_pairs={{0,4},{1,5},{2,6},{3,7},{4,8},{5,9},{6,10},{7,11},{8,12},{9,13},{1... | collective-permute-start | bytes 98312 | tf_op jit(solution)/shard_map/ppermute | solution.py:25
  35.9 1.5 %collective-permute-start.12 = (bf16[1,128,128]{1,2,0:T(8,128)(2,1)S(1)}, bf16[1,128,128]{1,2,0:T(8,128)(2,1)S(1)}, u32[]{:S(2)}, u32[]{:S(2)}) collective-permute-start(bf16[1,128,128]{1,2,0:T(8,128)(2,1)S(1)} %bitcast.309), channel_id=1, source_target_pairs={{0,2},{1,3},{2,0},{3,1},{4,6},{5,7},{6,4},{7,5},{8,10},{9,11},{10,... | collective-permute-start | bytes 98312 | tf_op jit(solution)/shard_map/ppermute | solution.py:32
  37.4 0.3 convolution_bitcast_fusion.10
  37.7 0.3 convolution_bitcast_fusion.29
  38.0 1.7 %collective-permute-done.8 = bf16[128,128]{0,1:T(8,128)(2,1)S(1)} collective-permute-done((bf16[128,128]{0,1:T(8,128)(2,1)S(1)}, bf16[128,128]{0,1:T(8,128)(2,1)S(1)}, u32[]{:S(2)}, u32[]{:S(2)}) %collective-permute-start.8) | collective-permute-done | bytes 32800 | tf_op jit(solution)/shard_map/ppermute | solution.py:25
  39.7 1.6 %collective-permute-start.13 = (bf16[3,128,128]{1,2,0:T(8,128)(2,1)S(1)}, bf16[3,128,128]{1,2,0:T(8,128)(2,1)S(1)}, u32[]{:S(2)}, u32[]{:S(2)}) collective-permute-start(bf16[3,128,128]{1,2,0:T(8,128)(2,1)S(1)} %pad_maximum_fusion.8), channel_id=1, source_target_pairs={{0,2},{1,3},{2,0},{3,1},{4,6},{5,7},{6,4},{7,5},{8,10},{9,11},{10,... | collective-permute-start | bytes 294920 | tf_op jit(solution)/shard_map/ppermute | solution.py:32
  41.7 0.6 collective-permute-start.14
  42.7 1.7 %collective-permute-done.13 = bf16[3,128,128]{1,2,0:T(8,128)(2,1)S(1)} collective-permute-done((bf16[3,128,128]{1,2,0:T(8,128)(2,1)S(1)}, bf16[3,128,128]{1,2,0:T(8,128)(2,1)S(1)}, u32[]{:S(2)}, u32[]{:S(2)}) %collective-permute-start.13) | collective-permute-done | bytes 98336 | tf_op jit(solution)/shard_map/ppermute | solution.py:32
  46.1 0.3 bitcast_convert_fusion
  46.4 0.9 %collective-permute-start.18 = (bf16[128,128]{0,1:T(8,128)(2,1)S(1)}, bf16[128,128]{0,1:T(8,128)(2,1)S(1)}, u32[]{:S(2)}, u32[]{:S(2)}) collective-permute-start(bf16[128,128]{0,1:T(8,128)(2,1)S(1)} %get-tuple-element.28), channel_id=1, source_target_pairs={{0,12},{1,13},{2,14},{3,15},{4,0},{5,1},{6,2},{7,3},{8,4},{9,5},{1... | collective-permute-start | bytes 98312 | tf_op jit(solution)/shard_map/ppermute | solution.py:25
  47.3 0.8 %collective-permute-start.17 = (bf16[128,128]{0,1:T(8,128)(2,1)S(1)}, bf16[128,128]{0,1:T(8,128)(2,1)S(1)}, u32[]{:S(2)}, u32[]{:S(2)}) collective-permute-start(bf16[128,128]{0,1:T(8,128)(2,1)S(1)} %get-tuple-element.28), channel_id=1, source_target_pairs={{0,8},{1,9},{2,10},{3,11},{4,12},{5,13},{6,14},{7,15},{8,0},{9,1},... | collective-permute-start | bytes 98312 | tf_op jit(solution)/shard_map/ppermute | solution.py:25
  48.1 0.8 %collective-permute-start.16 = (bf16[128,128]{0,1:T(8,128)(2,1)S(1)}, bf16[128,128]{0,1:T(8,128)(2,1)S(1)}, u32[]{:S(2)}, u32[]{:S(2)}) collective-permute-start(bf16[128,128]{0,1:T(8,128)(2,1)S(1)} %get-tuple-element.28), channel_id=1, source_target_pairs={{0,4},{1,5},{2,6},{3,7},{4,8},{5,9},{6,10},{7,11},{8,12},{9,13},{1... | collective-permute-start | bytes 98312 | tf_op jit(solution)/shard_map/ppermute | solution.py:25
  48.9 1.5 %collective-permute-start.20 = (bf16[1,128,128]{1,2,0:T(8,128)(2,1)S(1)}, bf16[1,128,128]{1,2,0:T(8,128)(2,1)S(1)}, u32[]{:S(2)}, u32[]{:S(2)}) collective-permute-start(bf16[1,128,128]{1,2,0:T(8,128)(2,1)S(1)} %bitcast.313), channel_id=1, source_target_pairs={{0,2},{1,3},{2,0},{3,1},{4,6},{5,7},{6,4},{7,5},{8,10},{9,11},{10,... | collective-permute-start | bytes 98312 | tf_op jit(solution)/shard_map/ppermute | solution.py:32
  50.6 1.6 %collective-permute-done.17 = bf16[128,128]{0,1:T(8,128)(2,1)S(1)} collective-permute-done((bf16[128,128]{0,1:T(8,128)(2,1)S(1)}, bf16[128,128]{0,1:T(8,128)(2,1)S(1)}, u32[]{:S(2)}, u32[]{:S(2)}) %collective-permute-start.17) | collective-permute-done | bytes 32800 | tf_op jit(solution)/shard_map/ppermute | solution.py:25
  52.2 1.6 %collective-permute-done.16 = bf16[128,128]{0,1:T(8,128)(2,1)S(1)} collective-permute-done((bf16[128,128]{0,1:T(8,128)(2,1)S(1)}, bf16[128,128]{0,1:T(8,128)(2,1)S(1)}, u32[]{:S(2)}, u32[]{:S(2)}) %collective-permute-start.16) | collective-permute-done | bytes 32800 | tf_op jit(solution)/shard_map/ppermute | solution.py:25
  53.8 1.6 %collective-permute-start.21 = (bf16[3,128,128]{1,2,0:T(8,128)(2,1)S(1)}, bf16[3,128,128]{1,2,0:T(8,128)(2,1)S(1)}, u32[]{:S(2)}, u32[]{:S(2)}) collective-permute-start(bf16[3,128,128]{1,2,0:T(8,128)(2,1)S(1)} %pad_maximum_fusion.9), channel_id=1, source_target_pairs={{0,2},{1,3},{2,0},{3,1},{4,6},{5,7},{6,4},{7,5},{8,10},{9,11},{10,... | collective-permute-start | bytes 294920 | tf_op jit(solution)/shard_map/ppermute | solution.py:32
  55.8 0.6 collective-permute-start.22
  56.4 2.1 %collective-permute-done.21 = bf16[3,128,128]{1,2,0:T(8,128)(2,1)S(1)} collective-permute-done((bf16[3,128,128]{1,2,0:T(8,128)(2,1)S(1)}, bf16[3,128,128]{1,2,0:T(8,128)(2,1)S(1)}, u32[]{:S(2)}, u32[]{:S(2)}) %collective-permute-start.21) | collective-permute-done | bytes 98336 | tf_op jit(solution)/shard_map/ppermute | solution.py:32
  59.2 0.6 %collective-permute-done.23 = bf16[3,128,128]{1,2,0:T(8,128)(2,1)S(1)} collective-permute-done((bf16[3,128,128]{1,2,0:T(8,128)(2,1)S(1)}, bf16[3,128,128]{1,2,0:T(8,128)(2,1)S(1)}, u32[]{:S(2)}, u32[]{:S(2)}) %collective-permute-start.23) | collective-permute-done | bytes 98336 | tf_op jit(solution)/shard_map/ppermute | solution.py:32
  60.4 0.3 convolution_bitcast_fusion.16
  60.8 0.8 %copy.24 = f32[3,128,128]{2,1,0:T(8,128)} copy(f32[3,128,128]{1,2,0:T(8,128)S(1)} %pad_maximum_fusion.5) | data formatting | bytes 393216 | tf_op jit(solution)/shard_map/stack | solution.py:143
  (73 shorter events, 6.4 us)
Async XLA Ops:
  0.0 12.0 %copy-start = (bf16[1,16,2,128,128]{4,3,2,1,0:T(8,128)(2,1)S(1)}, bf16[1,16,2,128,128]{4,3,2,1,0:T(8,128)(2,1)}, u32[]{:S(2)}) copy-start(bf16[1,16,2,128,128]{4,3,2,1,0:T(8,128)(2,1)} %param.16) | copy-start | bytes 3145732
  0.0 13.5 %collective-permute-start.2 = (bf16[4,128,128]{2,1,0:T(8,128)(2,1)}, bf16[4,128,128]{2,1,0:T(8,128)(2,1)S(1)}, u32[]{:S(2)}, u32[]{:S(2)}) collective-permute-start(bf16[4,128,128]{2,1,0:T(8,128)(2,1)} %param.19), channel_id=1, source_target_pairs={{0,12},{1,13},{2,14},{3,15},{4,0},{5,1},{6,2},{7,3},{8,4},{9,5},{1... | collective-permute-start | bytes 393224 | tf_op jit(solution)/shard_map/ppermute | solution.py:25
  5.1 11.4 %collective-permute-start.1 = (bf16[4,128,128]{2,1,0:T(8,128)(2,1)}, bf16[4,128,128]{2,1,0:T(8,128)(2,1)S(1)}, u32[]{:S(2)}, u32[]{:S(2)}) collective-permute-start(bf16[4,128,128]{2,1,0:T(8,128)(2,1)} %param.19), channel_id=1, source_target_pairs={{0,8},{1,9},{2,10},{3,11},{4,12},{5,13},{6,14},{7,15},{8,0},{9,1},... | collective-permute-start | bytes 393224 | tf_op jit(solution)/shard_map/ppermute | solution.py:25
  5.1 11.4 %collective-permute-start = (bf16[4,128,128]{2,1,0:T(8,128)(2,1)}, bf16[4,128,128]{2,1,0:T(8,128)(2,1)S(1)}, u32[]{:S(2)}, u32[]{:S(2)}) collective-permute-start(bf16[4,128,128]{2,1,0:T(8,128)(2,1)} %param.19), channel_id=1, source_target_pairs={{0,4},{1,5},{2,6},{3,7},{4,8},{5,9},{6,10},{7,11},{8,12},{9,13},{1... | collective-permute-start | bytes 393224 | tf_op jit(solution)/shard_map/ppermute | solution.py:25
  6.1 12.8 %collective-permute-start.4 = (bf16[1,4,128,128]{3,2,1,0:T(8,128)(2,1)}, bf16[1,4,128,128]{3,2,1,0:T(8,128)(2,1)S(1)}, u32[]{:S(2)}, u32[]{:S(2)}) collective-permute-start(bf16[1,4,128,128]{3,2,1,0:T(8,128)(2,1)} %bitcast.337), channel_id=1, source_target_pairs={{0,2},{1,3},{2,0},{3,1},{4,6},{5,7},{6,4},{7,5},{8,10},{9,11},{10,... | collective-permute-start | bytes 393224 | tf_op jit(solution)/shard_map/ppermute | solution.py:32
  13.3 4.9 %copy-start.3 = (bf16[4,128,128]{2,1,0:T(8,128)(2,1)S(1)}, bf16[4,128,128]{2,1,0:T(8,128)(2,1)}, u32[]{:S(2)}) copy-start(bf16[4,128,128]{2,1,0:T(8,128)(2,1)} %param.19) | copy-start | bytes 393220
  16.5 10.4 %collective-permute-start.5 = (bf16[3,4,128,128]{3,2,1,0:T(8,128)(2,1)S(1)}, bf16[3,4,128,128]{3,2,1,0:T(8,128)(2,1)S(1)}, u32[]{:S(2)}, u32[]{:S(2)}) collective-permute-start(bf16[3,4,128,128]{3,2,1,0:T(8,128)(2,1)S(1)} %pad_maximum_fusion.4), channel_id=1, source_target_pairs={{0,2},{1,3},{2,0},{3,1},{4,6},{5,7},{6,4},{7,5},{8,10},{9,11},{10,... | collective-permute-start | bytes 1179656 | tf_op jit(solution)/shard_map/ppermute | solution.py:32
  18.2 9.6 %collective-permute-start.3 = (bf16[4,4,128,128]{3,2,1,0:T(8,128)(2,1)S(1)}, bf16[4,4,128,128]{3,2,1,0:T(8,128)(2,1)S(1)}, u32[]{:S(2)}, u32[]{:S(2)}) collective-permute-start(bf16[4,4,128,128]{3,2,1,0:T(8,128)(2,1)S(1)} %pad_maximum_fusion.3), channel_id=1, source_target_pairs={{0,1},{1,0},{2,3},{3,2},{4,5},{5,4},{6,7},{7,6},{8,9},{9,8},{10,11... | collective-permute-start | bytes 1572872 | tf_op jit(solution)/shard_map/ppermute | solution.py:32
  18.9 11.3 %collective-permute-start.6 = (bf16[1,4,128,128]{3,2,1,0:T(8,128)(2,1)S(1)}, bf16[1,4,128,128]{3,2,1,0:T(8,128)(2,1)S(1)}, u32[]{:S(2)}, u32[]{:S(2)}) collective-permute-start(bf16[1,4,128,128]{3,2,1,0:T(8,128)(2,1)S(1)} %collective-permute-done.4), channel_id=1, source_target_pairs={{0,1},{1,0},{2,3},{3,2},{4,5},{5,4},{6,7},{7,6},{8,9},{9,8},{10,11... | collective-permute-start | bytes 393224 | tf_op jit(solution)/shard_map/ppermute | solution.py:32
  27.0 2.9 %collective-permute-start.7 = (bf16[3,4,128,128]{3,2,1,0:T(8,128)(2,1)S(1)}, bf16[3,4,128,128]{3,2,1,0:T(8,128)(2,1)S(1)}, u32[]{:S(2)}, u32[]{:S(2)}) collective-permute-start(bf16[3,4,128,128]{3,2,1,0:T(8,128)(2,1)S(1)} %collective-permute-done.5), channel_id=1, source_target_pairs={{0,1},{1,0},{2,3},{3,2},{4,5},{5,4},{6,7},{7,6},{8,9},{9,8},{10,11... | collective-permute-start | bytes 1179656 | tf_op jit(solution)/shard_map/ppermute | solution.py:32
  29.8 0.9 %copy-start.2 = (f32[3,128,128]{2,1,0:T(8,128)S(1)}, f32[3,128,128]{2,1,0:T(8,128)}, u32[]{:S(2)}) copy-start(f32[3,128,128]{2,1,0:T(8,128)} %param.20) | copy-start | bytes 589828
  30.2 0.9 %copy-start.1 = (f32[1,128,128]{2,1,0:T(8,128)S(1)}, f32[1,128,128]{2,1,0:T(8,128)}, u32[]{:S(2)}) copy-start(f32[1,128,128]{2,1,0:T(8,128)} %param.21) | copy-start | bytes 196612
  31.3 6.7 %collective-permute-start.10 = (bf16[128,128]{0,1:T(8,128)(2,1)S(1)}, bf16[128,128]{0,1:T(8,128)(2,1)S(1)}, u32[]{:S(2)}, u32[]{:S(2)}) collective-permute-start(bf16[128,128]{0,1:T(8,128)(2,1)S(1)} %get-tuple-element.26), channel_id=1, source_target_pairs={{0,12},{1,13},{2,14},{3,15},{4,0},{5,1},{6,2},{7,3},{8,4},{9,5},{1... | collective-permute-start | bytes 98312 | tf_op jit(solution)/shard_map/ppermute | solution.py:25
  32.0 6.0 %collective-permute-start.9 = (bf16[128,128]{0,1:T(8,128)(2,1)S(1)}, bf16[128,128]{0,1:T(8,128)(2,1)S(1)}, u32[]{:S(2)}, u32[]{:S(2)}) collective-permute-start(bf16[128,128]{0,1:T(8,128)(2,1)S(1)} %get-tuple-element.26), channel_id=1, source_target_pairs={{0,8},{1,9},{2,10},{3,11},{4,12},{5,13},{6,14},{7,15},{8,0},{9,1},... | collective-permute-start | bytes 98312 | tf_op jit(solution)/shard_map/ppermute | solution.py:25
  33.9 5.7 %collective-permute-start.8 = (bf16[128,128]{0,1:T(8,128)(2,1)S(1)}, bf16[128,128]{0,1:T(8,128)(2,1)S(1)}, u32[]{:S(2)}, u32[]{:S(2)}) collective-permute-start(bf16[128,128]{0,1:T(8,128)(2,1)S(1)} %get-tuple-element.26), channel_id=1, source_target_pairs={{0,4},{1,5},{2,6},{3,7},{4,8},{5,9},{6,10},{7,11},{8,12},{9,13},{1... | collective-permute-start | bytes 98312 | tf_op jit(solution)/shard_map/ppermute | solution.py:25
  35.9 5.6 %collective-permute-start.12 = (bf16[1,128,128]{1,2,0:T(8,128)(2,1)S(1)}, bf16[1,128,128]{1,2,0:T(8,128)(2,1)S(1)}, u32[]{:S(2)}, u32[]{:S(2)}) collective-permute-start(bf16[1,128,128]{1,2,0:T(8,128)(2,1)S(1)} %bitcast.309), channel_id=1, source_target_pairs={{0,2},{1,3},{2,0},{3,1},{4,6},{5,7},{6,4},{7,5},{8,10},{9,11},{10,... | collective-permute-start | bytes 98312 | tf_op jit(solution)/shard_map/ppermute | solution.py:32
  39.7 4.7 %collective-permute-start.13 = (bf16[3,128,128]{1,2,0:T(8,128)(2,1)S(1)}, bf16[3,128,128]{1,2,0:T(8,128)(2,1)S(1)}, u32[]{:S(2)}, u32[]{:S(2)}) collective-permute-start(bf16[3,128,128]{1,2,0:T(8,128)(2,1)S(1)} %pad_maximum_fusion.8), channel_id=1, source_target_pairs={{0,2},{1,3},{2,0},{3,1},{4,6},{5,7},{6,4},{7,5},{8,10},{9,11},{10,... | collective-permute-start | bytes 294920 | tf_op jit(solution)/shard_map/ppermute | solution.py:32
  41.3 3.5 %collective-permute-start.11 = (bf16[4,128,128]{1,2,0:T(8,128)(2,1)S(1)}, bf16[4,128,128]{1,2,0:T(8,128)(2,1)S(1)}, u32[]{:S(2)}, u32[]{:S(2)}) collective-permute-start(bf16[4,128,128]{1,2,0:T(8,128)(2,1)S(1)} %pad_maximum_fusion.6), channel_id=1, source_target_pairs={{0,1},{1,0},{2,3},{3,2},{4,5},{5,4},{6,7},{7,6},{8,9},{9,8},{10,11... | collective-permute-start | bytes 393224 | tf_op jit(solution)/shard_map/ppermute | solution.py:32
  41.7 4.2 %collective-permute-start.14 = (bf16[1,128,128]{1,2,0:T(8,128)(2,1)S(1)}, bf16[1,128,128]{1,2,0:T(8,128)(2,1)S(1)}, u32[]{:S(2)}, u32[]{:S(2)}) collective-permute-start(bf16[1,128,128]{1,2,0:T(8,128)(2,1)S(1)} %collective-permute-done.12), channel_id=1, source_target_pairs={{0,1},{1,0},{2,3},{3,2},{4,5},{5,4},{6,7},{7,6},{8,9},{9,8},{10,11... | collective-permute-start | bytes 98312 | tf_op jit(solution)/shard_map/ppermute | solution.py:32
  44.4 1.3 %collective-permute-start.15 = (bf16[3,128,128]{1,2,0:T(8,128)(2,1)S(1)}, bf16[3,128,128]{1,2,0:T(8,128)(2,1)S(1)}, u32[]{:S(2)}, u32[]{:S(2)}) collective-permute-start(bf16[3,128,128]{1,2,0:T(8,128)(2,1)S(1)} %collective-permute-done.13), channel_id=1, source_target_pairs={{0,1},{1,0},{2,3},{3,2},{4,5},{5,4},{6,7},{7,6},{8,9},{9,8},{10,11... | collective-permute-start | bytes 294920 | tf_op jit(solution)/shard_map/ppermute | solution.py:32
  46.4 4.2 %collective-permute-start.18 = (bf16[128,128]{0,1:T(8,128)(2,1)S(1)}, bf16[128,128]{0,1:T(8,128)(2,1)S(1)}, u32[]{:S(2)}, u32[]{:S(2)}) collective-permute-start(bf16[128,128]{0,1:T(8,128)(2,1)S(1)} %get-tuple-element.28), channel_id=1, source_target_pairs={{0,12},{1,13},{2,14},{3,15},{4,0},{5,1},{6,2},{7,3},{8,4},{9,5},{1... | collective-permute-start | bytes 98312 | tf_op jit(solution)/shard_map/ppermute | solution.py:25
  47.3 4.9 %collective-permute-start.17 = (bf16[128,128]{0,1:T(8,128)(2,1)S(1)}, bf16[128,128]{0,1:T(8,128)(2,1)S(1)}, u32[]{:S(2)}, u32[]{:S(2)}) collective-permute-start(bf16[128,128]{0,1:T(8,128)(2,1)S(1)} %get-tuple-element.28), channel_id=1, source_target_pairs={{0,8},{1,9},{2,10},{3,11},{4,12},{5,13},{6,14},{7,15},{8,0},{9,1},... | collective-permute-start | bytes 98312 | tf_op jit(solution)/shard_map/ppermute | solution.py:25
  48.1 5.7 %collective-permute-start.16 = (bf16[128,128]{0,1:T(8,128)(2,1)S(1)}, bf16[128,128]{0,1:T(8,128)(2,1)S(1)}, u32[]{:S(2)}, u32[]{:S(2)}) collective-permute-start(bf16[128,128]{0,1:T(8,128)(2,1)S(1)} %get-tuple-element.28), channel_id=1, source_target_pairs={{0,4},{1,5},{2,6},{3,7},{4,8},{5,9},{6,10},{7,11},{8,12},{9,13},{1... | collective-permute-start | bytes 98312 | tf_op jit(solution)/shard_map/ppermute | solution.py:25
  48.9 6.5 %collective-permute-start.20 = (bf16[1,128,128]{1,2,0:T(8,128)(2,1)S(1)}, bf16[1,128,128]{1,2,0:T(8,128)(2,1)S(1)}, u32[]{:S(2)}, u32[]{:S(2)}) collective-permute-start(bf16[1,128,128]{1,2,0:T(8,128)(2,1)S(1)} %bitcast.313), channel_id=1, source_target_pairs={{0,2},{1,3},{2,0},{3,1},{4,6},{5,7},{6,4},{7,5},{8,10},{9,11},{10,... | collective-permute-start | bytes 98312 | tf_op jit(solution)/shard_map/ppermute | solution.py:32
  53.8 4.7 %collective-permute-start.21 = (bf16[3,128,128]{1,2,0:T(8,128)(2,1)S(1)}, bf16[3,128,128]{1,2,0:T(8,128)(2,1)S(1)}, u32[]{:S(2)}, u32[]{:S(2)}) collective-permute-start(bf16[3,128,128]{1,2,0:T(8,128)(2,1)S(1)} %pad_maximum_fusion.9), channel_id=1, source_target_pairs={{0,2},{1,3},{2,0},{3,1},{4,6},{5,7},{6,4},{7,5},{8,10},{9,11},{10,... | collective-permute-start | bytes 294920 | tf_op jit(solution)/shard_map/ppermute | solution.py:32
  55.4 3.3 %collective-permute-start.19 = (bf16[4,128,128]{1,2,0:T(8,128)(2,1)S(1)}, bf16[4,128,128]{1,2,0:T(8,128)(2,1)S(1)}, u32[]{:S(2)}, u32[]{:S(2)}) collective-permute-start(bf16[4,128,128]{1,2,0:T(8,128)(2,1)S(1)} %pad_maximum_fusion.7), channel_id=1, source_target_pairs={{0,1},{1,0},{2,3},{3,2},{4,5},{5,4},{6,7},{7,6},{8,9},{9,8},{10,11... | collective-permute-start | bytes 393224 | tf_op jit(solution)/shard_map/ppermute | solution.py:32
  55.8 4.2 %collective-permute-start.22 = (bf16[1,128,128]{1,2,0:T(8,128)(2,1)S(1)}, bf16[1,128,128]{1,2,0:T(8,128)(2,1)S(1)}, u32[]{:S(2)}, u32[]{:S(2)}) collective-permute-start(bf16[1,128,128]{1,2,0:T(8,128)(2,1)S(1)} %collective-permute-done.20), channel_id=1, source_target_pairs={{0,1},{1,0},{2,3},{3,2},{4,5},{5,4},{6,7},{7,6},{8,9},{9,8},{10,11... | collective-permute-start | bytes 98312 | tf_op jit(solution)/shard_map/ppermute | solution.py:32
  58.5 1.3 %collective-permute-start.23 = (bf16[3,128,128]{1,2,0:T(8,128)(2,1)S(1)}, bf16[3,128,128]{1,2,0:T(8,128)(2,1)S(1)}, u32[]{:S(2)}, u32[]{:S(2)}) collective-permute-start(bf16[3,128,128]{1,2,0:T(8,128)(2,1)S(1)} %collective-permute-done.21), channel_id=1, source_target_pairs={{0,1},{1,0},{2,3},{3,2},{4,5},{5,4},{6,7},{7,6},{8,9},{9,8},{10,11... | collective-permute-start | bytes 294920 | tf_op jit(solution)/shard_map/ppermute | solution.py:32

commit v13 on v11

--- a/solution.py
+++ b/solution.py
@@ -32,26 +32,27 @@
     return lax.ppermute(x, "wide", [(d, d ^ mask) for d in range(wide)])
 
 
-def slab_stage(parts, wide, inner, early, direct=False):
+def slab_stage(parts, wide, inner, early, split):
     stack = parts[0] if len(parts) == 1 else jnp.concatenate(parts)
     if inner != 4:
         return [stack] + [swap(stack, wide, m) for m in range(1, inner)]
     if early and len(parts) > 1:
-        rest = jnp.concatenate(parts[1:])
-        across_own = swap(parts[0], wide, 2)
-        across_rest = swap(rest, wide, 2)
-        diagonal_own = swap(parts[0], wide, 3) if direct else swap(across_own, wide, 1)
-        diagonal_rest = swap(rest, wide, 3) if direct else swap(across_rest, wide, 1)
-        return [stack, swap(stack, wide, 1), across_own, across_rest, diagonal_own, diagonal_rest]
+        across = [swap(parts[0], wide, 2)]
+        if split and len(parts) > 2:
+            chunks = [parts[1], jnp.concatenate(parts[2:])]
+        else:
+            chunks = [jnp.concatenate(parts[1:])]
+        across += [swap(chunk, wide, 2) for chunk in chunks]
+        return [stack, swap(stack, wide, 1)] + across + [swap(piece, wide, 1) for piece in across]
     across = swap(stack, wide, 2)
     return [stack, swap(stack, wide, 1), across, swap(across, wide, 1)]
 
 
-def gather_blocks(x, wide, early, direct=False):
+def gather_blocks(x, wide, early, split=False):
     inner = inner_size(wide)
     lines = wide // inner
     parts, shifted = line_stage(x, wide, inner)
-    pieces = slab_stage(parts, wide, inner, early, direct)
+    pieces = slab_stage(parts, wide, inner, early, split)
     me = lax.axis_index("wide")
     line = np.arange(lines, dtype=np.int32)
     source_line = (me // inner - line) % lines if shifted else jnp.asarray(line)
@@ -91,7 +92,7 @@
     step_count = excitation.shape[0]
     column_of_block = jnp.argsort(block_owner)
 
-    later, later_blocks = gather_blocks(later_current, wide, True)
+    later, later_blocks = gather_blocks(later_current, wide, True, split=True)
     offsets = np.cumsum([0] + [piece.shape[0] for piece in later])
     by_lag = tiles_by_lag(
         retarded_tiles, tile_lags, column_of_block, later_blocks, range(1, lag_count + 1)
@@ -121,7 +122,7 @@
         current = advance(moment, retarded)
         results[moment] = current
         if moment > 0:
-            pieces, new_blocks = gather_blocks(current.astype(jnp.bfloat16), wide, True, direct=True)
+            pieces, new_blocks = gather_blocks(current.astype(jnp.bfloat16), wide, True)
             newer[moment] = jnp.concatenate(pieces)
             if recent is None:
                 recent = tiles_by_lag(

time: 61.7 us -> 60 us (0.972)
  waiting for transfers between devices: 18.6 us -> 15.1 us
  matrix products: 6.94 us -> 8 us
    ppermute x15 -> x17, waiting for transfers between devices: 16 us -> 14.2 us  [swap(): return lax.ppermute(x, 'wide', [(d, d ^ mask) for d in range(wide)])]
    ppermute x9, waiting for transfers between devices: 2.52 us -> 0.95 us  [line_stage(): parts.append(lax.ppermute(x, 'wide', pairs)[None])]
    dot_general x21 -> x27, matrix products: 6.09 us -> 7.14 us  [rowwise(): return jnp.einsum(spec, tiles, currents, preferred_element_type=jnp.float32)]
    ppermute x15 -> x17, starting transfers between devices: 10.3 us -> 11.1 us  [swap(): return lax.ppermute(x, 'wide', [(d, d ^ mask) for d in range(wide)])]
  transfers between devices with their start and end apart: 24 -> 26, of which waited for: 12 -> 9; matrix products, arithmetic and copies ran while one was open for 18% -> 20% of each run, Pallas kernels for 0% -> 0%
where the time goes in v13:
time: 60 us; the launch traced here: 59.8 us
  starting transfers between devices  28 us (47%)
  waiting for transfers between devices  15.1 us (25%)
  matrix products  8 us (13%)
  local copies, waits for them, and re-layouts  4.99 us (8%)
  other arithmetic  3.13 us (5%)
    ppermute x9, starting transfers between devices, line_stage(): parts.append(lax.ppermute(x, 'wide', pairs)[None])  16.9 us
    ppermute x17, waiting for transfers between devices, swap(): return lax.ppermute(x, 'wide', [(d, d ^ mask) for d in range(wide)])  14.2 us
    ppermute x17, starting transfers between devices, swap(): return lax.ppermute(x, 'wide', [(d, d ^ mask) for d in range(wide)])  11.1 us
    dot_general x27, matrix products, rowwise(): return jnp.einsum(spec, tiles, currents, preferred_element_type=jnp.float32)  7.14 us
    sort x1, other arithmetic, per_device(): column_of_block = jnp.argsort(block_owner)  1.9 us
    unnamed x22, local copies, waits for them, and re-layouts  1.34 us
  transfers between devices with their start and end apart: 26, of which 9 were waited for; matrix products, arithmetic and copies ran while one was open for 20% of the time, Pallas kernels for 0%

profile of v13, /device:TPU:0, one launch (start us, length us, event | category | flops | bytes accessed | tf_op | source)
XLA Modules:
  0.0 59.8 jit_solution(4338773478128158308)
XLA Ops:
  0.0 3.0 %collective-permute-start = (bf16[4,128,128]{2,1,0:T(8,128)(2,1)}, bf16[4,128,128]{2,1,0:T(8,128)(2,1)S(1)}, u32[]{:S(2)}, u32[]{:S(2)}) collective-permute-start(bf16[4,128,128]{2,1,0:T(8,128)(2,1)} %param.19), channel_id=1, source_target_pairs={{0,4},{1,5},{2,6},{3,7},{4,8},{5,9},{6,10},{7,11},{8,12},{9,13},{1... | collective-permute-start | bytes 393224 | tf_op jit(solution)/shard_map/ppermute | solution.py:25
  3.0 2.6 %collective-permute-start.1 = (bf16[4,128,128]{2,1,0:T(8,128)(2,1)}, bf16[4,128,128]{2,1,0:T(8,128)(2,1)S(1)}, u32[]{:S(2)}, u32[]{:S(2)}) collective-permute-start(bf16[4,128,128]{2,1,0:T(8,128)(2,1)} %param.19), channel_id=1, source_target_pairs={{0,8},{1,9},{2,10},{3,11},{4,12},{5,13},{6,14},{7,15},{8,0},{9,1},... | collective-permute-start | bytes 393224 | tf_op jit(solution)/shard_map/ppermute | solution.py:25
  5.6 1.3 %collective-permute-start.2 = (bf16[4,128,128]{2,1,0:T(8,128)(2,1)}, bf16[4,128,128]{2,1,0:T(8,128)(2,1)S(1)}, u32[]{:S(2)}, u32[]{:S(2)}) collective-permute-start(bf16[4,128,128]{2,1,0:T(8,128)(2,1)} %param.19), channel_id=1, source_target_pairs={{0,12},{1,13},{2,14},{3,15},{4,0},{5,1},{6,2},{7,3},{8,4},{9,5},{1... | collective-permute-start | bytes 393224 | tf_op jit(solution)/shard_map/ppermute | solution.py:25
  7.0 1.5 %collective-permute-start.4 = (bf16[1,4,128,128]{3,2,1,0:T(8,128)(2,1)}, bf16[1,4,128,128]{3,2,1,0:T(8,128)(2,1)S(1)}, u32[]{:S(2)}, u32[]{:S(2)}) collective-permute-start(bf16[1,4,128,128]{3,2,1,0:T(8,128)(2,1)} %bitcast.320), channel_id=1, source_target_pairs={{0,2},{1,3},{2,0},{3,1},{4,6},{5,7},{6,4},{7,5},{8,10},{9,11},{10,... | collective-permute-start | bytes 393224 | tf_op jit(solution)/shard_map/ppermute | solution.py:32
  8.7 1.9 %sort.17 = (s32[16]{0:T(128)}, s32[16]{0:T(128)S(1)}) sort(s32[16]{0:T(128)} %param.18, s32[16]{0:T(128)S(1)} %iota.5), dimensions={0}, to_apply=%region_0.0 | sort | flops 64 | bytes 256 | tf_op jit(solution)/shard_map/jit(argsort)/sort | solution.py:93
  10.6 0.7 %gather_fusion = s32[16]{0:T(128)S(1)} fusion(s32[16]{0:T(128)S(1)} %get-tuple-element.8, s32[1024]{0:T(1024)S(1)} %pad_clamp_fusion.1), kind=kCustom, calls=%fused_computation.clone | custom fusion | bytes 192 | tf_op jit(solution)/shard_map/jit(_take)/gather | solution.py:68
  11.3 0.8 %copy.18 = s32[16,2]{1,0:T(8,128)S(1)} copy(s32[16,2]{0,1:T(2,128)} %bitcast.330) | data formatting | bytes 256 | tf_op jit(solution)/shard_map/squeeze | solution.py:70
  12.0 0.7 %gather_fusion.2 = bf16[16,2,128,128]{3,2,1,0:T(8,128)(2,1)S(1)} fusion(bf16[16,2,128,128]{3,2,1,0:T(8,128)(2,1)S(1)} %bitcast.299, s32[1024]{0:T(1024)S(1)} %pad_clamp_fusion), kind=kCustom, calls=%fused_computation.2.clone | custom fusion | bytes 2097216 | tf_op jit(solution)/shard_map/jit(_take)/gather | solution.py:69
  12.8 0.6 gather_fusion.1
  13.9 0.3 bitcast_select_fusion.3
  14.5 0.5 copy-done.3
  15.1 1.1 %collective-permute-start.5 = (bf16[1,4,128,128]{3,2,1,0:T(8,128)(2,1)S(1)}, bf16[1,4,128,128]{3,2,1,0:T(8,128)(2,1)S(1)}, u32[]{:S(2)}, u32[]{:S(2)}) collective-permute-start(bf16[1,4,128,128]{3,2,1,0:T(8,128)(2,1)S(1)} %bitcast.324), channel_id=1, source_target_pairs={{0,2},{1,3},{2,0},{3,1},{4,6},{5,7},{6,4},{7,5},{8,10},{9,11},{10,... | collective-permute-start | bytes 393224 | tf_op jit(solution)/shard_map/ppermute | solution.py:32
  16.2 1.0 %collective-permute-start.6 = (bf16[2,4,128,128]{3,2,1,0:T(8,128)(2,1)S(1)}, bf16[2,4,128,128]{3,2,1,0:T(8,128)(2,1)S(1)}, u32[]{:S(2)}, u32[]{:S(2)}) collective-permute-start(bf16[2,4,128,128]{3,2,1,0:T(8,128)(2,1)S(1)} %pad_maximum_fusion.4), channel_id=1, source_target_pairs={{0,2},{1,3},{2,0},{3,1},{4,6},{5,7},{6,4},{7,5},{8,10},{9,11},{10,... | collective-permute-start | bytes 786440 | tf_op jit(solution)/shard_map/ppermute | solution.py:32
  17.2 0.3 convolution_bitcast_fusion.5
  17.6 0.3 collective-permute-start.7
  18.1 3.0 %collective-permute-done.5 = bf16[1,4,128,128]{3,2,1,0:T(8,128)(2,1)S(1)} collective-permute-done((bf16[1,4,128,128]{3,2,1,0:T(8,128)(2,1)S(1)}, bf16[1,4,128,128]{3,2,1,0:T(8,128)(2,1)S(1)}, u32[]{:S(2)}, u32[]{:S(2)}) %collective-permute-start.5) | collective-permute-done | bytes 131104 | tf_op jit(solution)/shard_map/ppermute | solution.py:32
  21.7 0.7 %collective-permute-done.8 = bf16[1,4,128,128]{3,2,1,0:T(8,128)(2,1)S(1)} collective-permute-done((bf16[1,4,128,128]{3,2,1,0:T(8,128)(2,1)S(1)}, bf16[1,4,128,128]{3,2,1,0:T(8,128)(2,1)S(1)}, u32[]{:S(2)}, u32[]{:S(2)}) %collective-permute-start.8) | collective-permute-done | bytes 131104 | tf_op jit(solution)/shard_map/ppermute | solution.py:32
  22.9 2.9 %collective-permute-done.6 = bf16[2,4,128,128]{3,2,1,0:T(8,128)(2,1)S(1)} collective-permute-done((bf16[2,4,128,128]{3,2,1,0:T(8,128)(2,1)S(1)}, bf16[2,4,128,128]{3,2,1,0:T(8,128)(2,1)S(1)}, u32[]{:S(2)}, u32[]{:S(2)}) %collective-permute-start.6) | collective-permute-done | bytes 262176 | tf_op jit(solution)/shard_map/ppermute | solution.py:32
  26.5 0.3 convolution_bitcast_fusion.3
  26.8 0.3 convolution_bitcast_fusion
  27.1 0.4 fusion.26
  28.1 0.6 %copy-done.2 = f32[3,128,128]{2,1,0:T(8,128)S(1)} copy-done((f32[3,128,128]{2,1,0:T(8,128)S(1)}, f32[3,128,128]{2,1,0:T(8,128)}, u32[]{:S(2)}) %copy-start.2) | copy-done | bytes 196632
  28.9 0.3 constant_dynamic-update-slice_fusion.8
  29.2 3.3 %collective-permute-start.10 = (bf16[128,128]{0,1:T(8,128)(2,1)S(1)}, bf16[128,128]{0,1:T(8,128)(2,1)S(1)}, u32[]{:S(2)}, u32[]{:S(2)}) collective-permute-start(bf16[128,128]{0,1:T(8,128)(2,1)S(1)} %get-tuple-element.21), channel_id=1, source_target_pairs={{0,4},{1,5},{2,6},{3,7},{4,8},{5,9},{6,10},{7,11},{8,12},{9,13},{1... | collective-permute-start | bytes 98312 | tf_op jit(solution)/shard_map/ppermute | solution.py:25
  32.5 1.2 %collective-permute-start.11 = (bf16[128,128]{0,1:T(8,128)(2,1)S(1)}, bf16[128,128]{0,1:T(8,128)(2,1)S(1)}, u32[]{:S(2)}, u32[]{:S(2)}) collective-permute-start(bf16[128,128]{0,1:T(8,128)(2,1)S(1)} %get-tuple-element.21), channel_id=1, source_target_pairs={{0,8},{1,9},{2,10},{3,11},{4,12},{5,13},{6,14},{7,15},{8,0},{9,1},... | collective-permute-start | bytes 98312 | tf_op jit(solution)/shard_map/ppermute | solution.py:25
  33.6 1.3 %collective-permute-start.12 = (bf16[128,128]{0,1:T(8,128)(2,1)S(1)}, bf16[128,128]{0,1:T(8,128)(2,1)S(1)}, u32[]{:S(2)}, u32[]{:S(2)}) collective-permute-start(bf16[128,128]{0,1:T(8,128)(2,1)S(1)} %get-tuple-element.21), channel_id=1, source_target_pairs={{0,12},{1,13},{2,14},{3,15},{4,0},{5,1},{6,2},{7,3},{8,4},{9,5},{1... | collective-permute-start | bytes 98312 | tf_op jit(solution)/shard_map/ppermute | solution.py:25
  34.9 1.5 %collective-permute-start.14 = (bf16[1,128,128]{1,2,0:T(8,128)(2,1)S(1)}, bf16[1,128,128]{1,2,0:T(8,128)(2,1)S(1)}, u32[]{:S(2)}, u32[]{:S(2)}) collective-permute-start(bf16[1,128,128]{1,2,0:T(8,128)(2,1)S(1)} %bitcast.326), channel_id=1, source_target_pairs={{0,2},{1,3},{2,0},{3,1},{4,6},{5,7},{6,4},{7,5},{8,10},{9,11},{10,... | collective-permute-start | bytes 98312 | tf_op jit(solution)/shard_map/ppermute | solution.py:32
  36.7 0.3 fusion.24
  37.0 0.3 fusion.25
  38.0 1.4 %collective-permute-start.15 = (bf16[3,128,128]{1,2,0:T(8,128)(2,1)S(1)}, bf16[3,128,128]{1,2,0:T(8,128)(2,1)S(1)}, u32[]{:S(2)}, u32[]{:S(2)}) collective-permute-start(bf16[3,128,128]{1,2,0:T(8,128)(2,1)S(1)} %pad_maximum_fusion.8), channel_id=1, source_target_pairs={{0,2},{1,3},{2,0},{3,1},{4,6},{5,7},{6,4},{7,5},{8,10},{9,11},{10,... | collective-permute-start | bytes 294920 | tf_op jit(solution)/shard_map/ppermute | solution.py:32
  39.4 0.6 collective-permute-start.16
  40.0 2.7 %collective-permute-done.15 = bf16[3,128,128]{1,2,0:T(8,128)(2,1)S(1)} collective-permute-done((bf16[3,128,128]{1,2,0:T(8,128)(2,1)S(1)}, bf16[3,128,128]{1,2,0:T(8,128)(2,1)S(1)}, u32[]{:S(2)}, u32[]{:S(2)}) %collective-permute-start.15) | collective-permute-done | bytes 98336 | tf_op jit(solution)/shard_map/ppermute | solution.py:32
  42.8 1.2 %collective-permute-done.17 = bf16[3,128,128]{1,2,0:T(8,128)(2,1)S(1)} collective-permute-done((bf16[3,128,128]{1,2,0:T(8,128)(2,1)S(1)}, bf16[3,128,128]{1,2,0:T(8,128)(2,1)S(1)}, u32[]{:S(2)}, u32[]{:S(2)}) %collective-permute-start.17) | collective-permute-done | bytes 98336 | tf_op jit(solution)/shard_map/ppermute | solution.py:32
  44.0 0.3 convolution_bitcast_fusion.11
  44.6 0.3 constant_dynamic-update-slice_fusion.17
  44.9 0.8 %collective-permute-start.18 = (bf16[128,128]{0,1:T(8,128)(2,1)S(1)}, bf16[128,128]{0,1:T(8,128)(2,1)S(1)}, u32[]{:S(2)}, u32[]{:S(2)}) collective-permute-start(bf16[128,128]{0,1:T(8,128)(2,1)S(1)} %get-tuple-element.19), channel_id=1, source_target_pairs={{0,4},{1,5},{2,6},{3,7},{4,8},{5,9},{6,10},{7,11},{8,12},{9,13},{1... | collective-permute-start | bytes 98312 | tf_op jit(solution)/shard_map/ppermute | solution.py:25
  45.7 2.4 %collective-permute-start.19 = (bf16[128,128]{0,1:T(8,128)(2,1)S(1)}, bf16[128,128]{0,1:T(8,128)(2,1)S(1)}, u32[]{:S(2)}, u32[]{:S(2)}) collective-permute-start(bf16[128,128]{0,1:T(8,128)(2,1)S(1)} %get-tuple-element.19), channel_id=1, source_target_pairs={{0,8},{1,9},{2,10},{3,11},{4,12},{5,13},{6,14},{7,15},{8,0},{9,1},... | collective-permute-start | bytes 98312 | tf_op jit(solution)/shard_map/ppermute | solution.py:25
  48.1 1.0 %collective-permute-start.20 = (bf16[128,128]{0,1:T(8,128)(2,1)S(1)}, bf16[128,128]{0,1:T(8,128)(2,1)S(1)}, u32[]{:S(2)}, u32[]{:S(2)}) collective-permute-start(bf16[128,128]{0,1:T(8,128)(2,1)S(1)} %get-tuple-element.19), channel_id=1, source_target_pairs={{0,12},{1,13},{2,14},{3,15},{4,0},{5,1},{6,2},{7,3},{8,4},{9,5},{1... | collective-permute-start | bytes 98312 | tf_op jit(solution)/shard_map/ppermute | solution.py:25
  49.2 0.5 convolution_bitcast_fusion.9
  49.7 1.6 %collective-permute-start.22 = (bf16[1,128,128]{1,2,0:T(8,128)(2,1)S(1)}, bf16[1,128,128]{1,2,0:T(8,128)(2,1)S(1)}, u32[]{:S(2)}, u32[]{:S(2)}) collective-permute-start(bf16[1,128,128]{1,2,0:T(8,128)(2,1)S(1)} %bitcast.328), channel_id=1, source_target_pairs={{0,2},{1,3},{2,0},{3,1},{4,6},{5,7},{6,4},{7,5},{8,10},{9,11},{10,... | collective-permute-start | bytes 98312 | tf_op jit(solution)/shard_map/ppermute | solution.py:32
  51.3 0.8 %collective-permute-done.20 = bf16[128,128]{0,1:T(8,128)(2,1)S(1)} collective-permute-done((bf16[128,128]{0,1:T(8,128)(2,1)S(1)}, bf16[128,128]{0,1:T(8,128)(2,1)S(1)}, u32[]{:S(2)}, u32[]{:S(2)}) %collective-permute-start.20) | collective-permute-done | bytes 32800 | tf_op jit(solution)/shard_map/ppermute | solution.py:25
  52.1 1.6 %collective-permute-start.23 = (bf16[3,128,128]{1,2,0:T(8,128)(2,1)S(1)}, bf16[3,128,128]{1,2,0:T(8,128)(2,1)S(1)}, u32[]{:S(2)}, u32[]{:S(2)}) collective-permute-start(bf16[3,128,128]{1,2,0:T(8,128)(2,1)S(1)} %pad_maximum_fusion.9), channel_id=1, source_target_pairs={{0,2},{1,3},{2,0},{3,1},{4,6},{5,7},{6,4},{7,5},{8,10},{9,11},{10,... | collective-permute-start | bytes 294920 | tf_op jit(solution)/shard_map/ppermute | solution.py:32
  53.7 0.6 collective-permute-start.24
  54.3 2.5 %collective-permute-done.23 = bf16[3,128,128]{1,2,0:T(8,128)(2,1)S(1)} collective-permute-done((bf16[3,128,128]{1,2,0:T(8,128)(2,1)S(1)}, bf16[3,128,128]{1,2,0:T(8,128)(2,1)S(1)}, u32[]{:S(2)}, u32[]{:S(2)}) %collective-permute-start.23) | collective-permute-done | bytes 98336 | tf_op jit(solution)/shard_map/ppermute | solution.py:32
  56.9 1.2 %collective-permute-done.25 = bf16[3,128,128]{1,2,0:T(8,128)(2,1)S(1)} collective-permute-done((bf16[3,128,128]{1,2,0:T(8,128)(2,1)S(1)}, bf16[3,128,128]{1,2,0:T(8,128)(2,1)S(1)}, u32[]{:S(2)}, u32[]{:S(2)}) %collective-permute-start.25) | collective-permute-done | bytes 98336 | tf_op jit(solution)/shard_map/ppermute | solution.py:32
  58.1 0.3 convolution_bitcast_fusion.10
  58.7 0.3 convolution_bitcast_fusion.8
  59.0 0.8 %copy.24 = f32[3,128,128]{2,1,0:T(8,128)} copy(f32[3,128,128]{1,2,0:T(8,128)S(1)} %pad_maximum_fusion.5) | data formatting | bytes 393216 | tf_op jit(solution)/shard_map/stack | solution.py:135
  (84 shorter events, 5.6 us)
Async XLA Ops:
  0.0 12.0 %copy-start = (bf16[1,16,2,128,128]{4,3,2,1,0:T(8,128)(2,1)S(1)}, bf16[1,16,2,128,128]{4,3,2,1,0:T(8,128)(2,1)}, u32[]{:S(2)}) copy-start(bf16[1,16,2,128,128]{4,3,2,1,0:T(8,128)(2,1)} %param.16) | copy-start | bytes 3145732
  0.0 14.5 %collective-permute-start = (bf16[4,128,128]{2,1,0:T(8,128)(2,1)}, bf16[4,128,128]{2,1,0:T(8,128)(2,1)S(1)}, u32[]{:S(2)}, u32[]{:S(2)}) collective-permute-start(bf16[4,128,128]{2,1,0:T(8,128)(2,1)} %param.19), channel_id=1, source_target_pairs={{0,4},{1,5},{2,6},{3,7},{4,8},{5,9},{6,10},{7,11},{8,12},{9,13},{1... | collective-permute-start | bytes 393224 | tf_op jit(solution)/shard_map/ppermute | solution.py:25
  3.0 11.4 %collective-permute-start.1 = (bf16[4,128,128]{2,1,0:T(8,128)(2,1)}, bf16[4,128,128]{2,1,0:T(8,128)(2,1)S(1)}, u32[]{:S(2)}, u32[]{:S(2)}) collective-permute-start(bf16[4,128,128]{2,1,0:T(8,128)(2,1)} %param.19), channel_id=1, source_target_pairs={{0,8},{1,9},{2,10},{3,11},{4,12},{5,13},{6,14},{7,15},{8,0},{9,1},... | collective-permute-start | bytes 393224 | tf_op jit(solution)/shard_map/ppermute | solution.py:25
  5.6 8.9 %collective-permute-start.2 = (bf16[4,128,128]{2,1,0:T(8,128)(2,1)}, bf16[4,128,128]{2,1,0:T(8,128)(2,1)S(1)}, u32[]{:S(2)}, u32[]{:S(2)}) collective-permute-start(bf16[4,128,128]{2,1,0:T(8,128)(2,1)} %param.19), channel_id=1, source_target_pairs={{0,12},{1,13},{2,14},{3,15},{4,0},{5,1},{6,2},{7,3},{8,4},{9,5},{1... | collective-permute-start | bytes 393224 | tf_op jit(solution)/shard_map/ppermute | solution.py:25
  7.0 10.6 %collective-permute-start.4 = (bf16[1,4,128,128]{3,2,1,0:T(8,128)(2,1)}, bf16[1,4,128,128]{3,2,1,0:T(8,128)(2,1)S(1)}, u32[]{:S(2)}, u32[]{:S(2)}) collective-permute-start(bf16[1,4,128,128]{3,2,1,0:T(8,128)(2,1)} %bitcast.320), channel_id=1, source_target_pairs={{0,2},{1,3},{2,0},{3,1},{4,6},{5,7},{6,4},{7,5},{8,10},{9,11},{10,... | collective-permute-start | bytes 393224 | tf_op jit(solution)/shard_map/ppermute | solution.py:32
  14.1 0.9 %copy-start.3 = (bf16[4,128,128]{2,1,0:T(8,128)(2,1)S(1)}, bf16[4,128,128]{2,1,0:T(8,128)(2,1)}, u32[]{:S(2)}) copy-start(bf16[4,128,128]{2,1,0:T(8,128)(2,1)} %param.19) | copy-start | bytes 393220
  15.1 6.0 %collective-permute-start.5 = (bf16[1,4,128,128]{3,2,1,0:T(8,128)(2,1)S(1)}, bf16[1,4,128,128]{3,2,1,0:T(8,128)(2,1)S(1)}, u32[]{:S(2)}, u32[]{:S(2)}) collective-permute-start(bf16[1,4,128,128]{3,2,1,0:T(8,128)(2,1)S(1)} %bitcast.324), channel_id=1, source_target_pairs={{0,2},{1,3},{2,0},{3,1},{4,6},{5,7},{6,4},{7,5},{8,10},{9,11},{10,... | collective-permute-start | bytes 393224 | tf_op jit(solution)/shard_map/ppermute | solution.py:32
  16.2 10.6 %collective-permute-start.3 = (bf16[4,4,128,128]{3,2,1,0:T(8,128)(2,1)S(1)}, bf16[4,4,128,128]{3,2,1,0:T(8,128)(2,1)S(1)}, u32[]{:S(2)}, u32[]{:S(2)}) collective-permute-start(bf16[4,4,128,128]{3,2,1,0:T(8,128)(2,1)S(1)} %pad_maximum_fusion.3), channel_id=1, source_target_pairs={{0,1},{1,0},{2,3},{3,2},{4,5},{5,4},{6,7},{7,6},{8,9},{9,8},{10,11... | collective-permute-start | bytes 1572872 | tf_op jit(solution)/shard_map/ppermute | solution.py:32
  16.2 9.6 %collective-permute-start.6 = (bf16[2,4,128,128]{3,2,1,0:T(8,128)(2,1)S(1)}, bf16[2,4,128,128]{3,2,1,0:T(8,128)(2,1)S(1)}, u32[]{:S(2)}, u32[]{:S(2)}) collective-permute-start(bf16[2,4,128,128]{3,2,1,0:T(8,128)(2,1)S(1)} %pad_maximum_fusion.4), channel_id=1, source_target_pairs={{0,2},{1,3},{2,0},{3,1},{4,6},{5,7},{6,4},{7,5},{8,10},{9,11},{10,... | collective-permute-start | bytes 786440 | tf_op jit(solution)/shard_map/ppermute | solution.py:32
  17.6 10.5 %collective-permute-start.7 = (bf16[1,4,128,128]{3,2,1,0:T(8,128)(2,1)S(1)}, bf16[1,4,128,128]{3,2,1,0:T(8,128)(2,1)S(1)}, u32[]{:S(2)}, u32[]{:S(2)}) collective-permute-start(bf16[1,4,128,128]{3,2,1,0:T(8,128)(2,1)S(1)} %collective-permute-done.4), channel_id=1, source_target_pairs={{0,1},{1,0},{2,3},{3,2},{4,5},{5,4},{6,7},{7,6},{8,9},{9,8},{10,11... | collective-permute-start | bytes 393224 | tf_op jit(solution)/shard_map/ppermute | solution.py:32
  21.1 1.3 %collective-permute-start.8 = (bf16[1,4,128,128]{3,2,1,0:T(8,128)(2,1)S(1)}, bf16[1,4,128,128]{3,2,1,0:T(8,128)(2,1)S(1)}, u32[]{:S(2)}, u32[]{:S(2)}) collective-permute-start(bf16[1,4,128,128]{3,2,1,0:T(8,128)(2,1)S(1)} %collective-permute-done.5), channel_id=1, source_target_pairs={{0,1},{1,0},{2,3},{3,2},{4,5},{5,4},{6,7},{7,6},{8,9},{9,8},{10,11... | collective-permute-start | bytes 393224 | tf_op jit(solution)/shard_map/ppermute | solution.py:32
  25.8 2.0 %collective-permute-start.9 = (bf16[2,4,128,128]{3,2,1,0:T(8,128)(2,1)S(1)}, bf16[2,4,128,128]{3,2,1,0:T(8,128)(2,1)S(1)}, u32[]{:S(2)}, u32[]{:S(2)}) collective-permute-start(bf16[2,4,128,128]{3,2,1,0:T(8,128)(2,1)S(1)} %collective-permute-done.6), channel_id=1, source_target_pairs={{0,1},{1,0},{2,3},{3,2},{4,5},{5,4},{6,7},{7,6},{8,9},{9,8},{10,11... | collective-permute-start | bytes 786440 | tf_op jit(solution)/shard_map/ppermute | solution.py:32
  27.7 0.9 %copy-start.2 = (f32[3,128,128]{2,1,0:T(8,128)S(1)}, f32[3,128,128]{2,1,0:T(8,128)}, u32[]{:S(2)}) copy-start(f32[3,128,128]{2,1,0:T(8,128)} %param.20) | copy-start | bytes 589828
  28.0 0.9 %copy-start.1 = (f32[1,128,128]{2,1,0:T(8,128)S(1)}, f32[1,128,128]{2,1,0:T(8,128)}, u32[]{:S(2)}) copy-start(f32[1,128,128]{2,1,0:T(8,128)} %param.21) | copy-start | bytes 196612
  29.2 8.8 %collective-permute-start.10 = (bf16[128,128]{0,1:T(8,128)(2,1)S(1)}, bf16[128,128]{0,1:T(8,128)(2,1)S(1)}, u32[]{:S(2)}, u32[]{:S(2)}) collective-permute-start(bf16[128,128]{0,1:T(8,128)(2,1)S(1)} %get-tuple-element.21), channel_id=1, source_target_pairs={{0,4},{1,5},{2,6},{3,7},{4,8},{5,9},{6,10},{7,11},{8,12},{9,13},{1... | collective-permute-start | bytes 98312 | tf_op jit(solution)/shard_map/ppermute | solution.py:25
  32.5 5.5 %collective-permute-start.11 = (bf16[128,128]{0,1:T(8,128)(2,1)S(1)}, bf16[128,128]{0,1:T(8,128)(2,1)S(1)}, u32[]{:S(2)}, u32[]{:S(2)}) collective-permute-start(bf16[128,128]{0,1:T(8,128)(2,1)S(1)} %get-tuple-element.21), channel_id=1, source_target_pairs={{0,8},{1,9},{2,10},{3,11},{4,12},{5,13},{6,14},{7,15},{8,0},{9,1},... | collective-permute-start | bytes 98312 | tf_op jit(solution)/shard_map/ppermute | solution.py:25
  33.6 4.3 %collective-permute-start.12 = (bf16[128,128]{0,1:T(8,128)(2,1)S(1)}, bf16[128,128]{0,1:T(8,128)(2,1)S(1)}, u32[]{:S(2)}, u32[]{:S(2)}) collective-permute-start(bf16[128,128]{0,1:T(8,128)(2,1)S(1)} %get-tuple-element.21), channel_id=1, source_target_pairs={{0,12},{1,13},{2,14},{3,15},{4,0},{5,1},{6,2},{7,3},{8,4},{9,5},{1... | collective-permute-start | bytes 98312 | tf_op jit(solution)/shard_map/ppermute | solution.py:25
  34.9 4.5 %collective-permute-start.14 = (bf16[1,128,128]{1,2,0:T(8,128)(2,1)S(1)}, bf16[1,128,128]{1,2,0:T(8,128)(2,1)S(1)}, u32[]{:S(2)}, u32[]{:S(2)}) collective-permute-start(bf16[1,128,128]{1,2,0:T(8,128)(2,1)S(1)} %bitcast.326), channel_id=1, source_target_pairs={{0,2},{1,3},{2,0},{3,1},{4,6},{5,7},{6,4},{7,5},{8,10},{9,11},{10,... | collective-permute-start | bytes 98312 | tf_op jit(solution)/shard_map/ppermute | solution.py:32
  38.0 4.7 %collective-permute-start.15 = (bf16[3,128,128]{1,2,0:T(8,128)(2,1)S(1)}, bf16[3,128,128]{1,2,0:T(8,128)(2,1)S(1)}, u32[]{:S(2)}, u32[]{:S(2)}) collective-permute-start(bf16[3,128,128]{1,2,0:T(8,128)(2,1)S(1)} %pad_maximum_fusion.8), channel_id=1, source_target_pairs={{0,2},{1,3},{2,0},{3,1},{4,6},{5,7},{6,4},{7,5},{8,10},{9,11},{10,... | collective-permute-start | bytes 294920 | tf_op jit(solution)/shard_map/ppermute | solution.py:32
  39.4 3.3 %collective-permute-start.13 = (bf16[4,128,128]{1,2,0:T(8,128)(2,1)S(1)}, bf16[4,128,128]{1,2,0:T(8,128)(2,1)S(1)}, u32[]{:S(2)}, u32[]{:S(2)}) collective-permute-start(bf16[4,128,128]{1,2,0:T(8,128)(2,1)S(1)} %pad_maximum_fusion.6), channel_id=1, source_target_pairs={{0,1},{1,0},{2,3},{3,2},{4,5},{5,4},{6,7},{7,6},{8,9},{9,8},{10,11... | collective-permute-start | bytes 393224 | tf_op jit(solution)/shard_map/ppermute | solution.py:32
  39.4 3.3 %collective-permute-start.16 = (bf16[1,128,128]{1,2,0:T(8,128)(2,1)S(1)}, bf16[1,128,128]{1,2,0:T(8,128)(2,1)S(1)}, u32[]{:S(2)}, u32[]{:S(2)}) collective-permute-start(bf16[1,128,128]{1,2,0:T(8,128)(2,1)S(1)} %collective-permute-done.14), channel_id=1, source_target_pairs={{0,1},{1,0},{2,3},{3,2},{4,5},{5,4},{6,7},{7,6},{8,9},{9,8},{10,11... | collective-permute-start | bytes 98312 | tf_op jit(solution)/shard_map/ppermute | solution.py:32
  42.7 1.3 %collective-permute-start.17 = (bf16[3,128,128]{1,2,0:T(8,128)(2,1)S(1)}, bf16[3,128,128]{1,2,0:T(8,128)(2,1)S(1)}, u32[]{:S(2)}, u32[]{:S(2)}) collective-permute-start(bf16[3,128,128]{1,2,0:T(8,128)(2,1)S(1)} %collective-permute-done.15), channel_id=1, source_target_pairs={{0,1},{1,0},{2,3},{3,2},{4,5},{5,4},{6,7},{7,6},{8,9},{9,8},{10,11... | collective-permute-start | bytes 294920 | tf_op jit(solution)/shard_map/ppermute | solution.py:32
  44.9 6.4 %collective-permute-start.18 = (bf16[128,128]{0,1:T(8,128)(2,1)S(1)}, bf16[128,128]{0,1:T(8,128)(2,1)S(1)}, u32[]{:S(2)}, u32[]{:S(2)}) collective-permute-start(bf16[128,128]{0,1:T(8,128)(2,1)S(1)} %get-tuple-element.19), channel_id=1, source_target_pairs={{0,4},{1,5},{2,6},{3,7},{4,8},{5,9},{6,10},{7,11},{8,12},{9,13},{1... | collective-permute-start | bytes 98312 | tf_op jit(solution)/shard_map/ppermute | solution.py:25
  45.7 5.5 %collective-permute-start.19 = (bf16[128,128]{0,1:T(8,128)(2,1)S(1)}, bf16[128,128]{0,1:T(8,128)(2,1)S(1)}, u32[]{:S(2)}, u32[]{:S(2)}) collective-permute-start(bf16[128,128]{0,1:T(8,128)(2,1)S(1)} %get-tuple-element.19), channel_id=1, source_target_pairs={{0,8},{1,9},{2,10},{3,11},{4,12},{5,13},{6,14},{7,15},{8,0},{9,1},... | collective-permute-start | bytes 98312 | tf_op jit(solution)/shard_map/ppermute | solution.py:25
  48.1 3.9 %collective-permute-start.20 = (bf16[128,128]{0,1:T(8,128)(2,1)S(1)}, bf16[128,128]{0,1:T(8,128)(2,1)S(1)}, u32[]{:S(2)}, u32[]{:S(2)}) collective-permute-start(bf16[128,128]{0,1:T(8,128)(2,1)S(1)} %get-tuple-element.19), channel_id=1, source_target_pairs={{0,12},{1,13},{2,14},{3,15},{4,0},{5,1},{6,2},{7,3},{8,4},{9,5},{1... | collective-permute-start | bytes 98312 | tf_op jit(solution)/shard_map/ppermute | solution.py:25
  49.7 4.0 %collective-permute-start.22 = (bf16[1,128,128]{1,2,0:T(8,128)(2,1)S(1)}, bf16[1,128,128]{1,2,0:T(8,128)(2,1)S(1)}, u32[]{:S(2)}, u32[]{:S(2)}) collective-permute-start(bf16[1,128,128]{1,2,0:T(8,128)(2,1)S(1)} %bitcast.328), channel_id=1, source_target_pairs={{0,2},{1,3},{2,0},{3,1},{4,6},{5,7},{6,4},{7,5},{8,10},{9,11},{10,... | collective-permute-start | bytes 98312 | tf_op jit(solution)/shard_map/ppermute | solution.py:32
  52.1 4.7 %collective-permute-start.23 = (bf16[3,128,128]{1,2,0:T(8,128)(2,1)S(1)}, bf16[3,128,128]{1,2,0:T(8,128)(2,1)S(1)}, u32[]{:S(2)}, u32[]{:S(2)}) collective-permute-start(bf16[3,128,128]{1,2,0:T(8,128)(2,1)S(1)} %pad_maximum_fusion.9), channel_id=1, source_target_pairs={{0,2},{1,3},{2,0},{3,1},{4,6},{5,7},{6,4},{7,5},{8,10},{9,11},{10,... | collective-permute-start | bytes 294920 | tf_op jit(solution)/shard_map/ppermute | solution.py:32
  53.7 3.1 %collective-permute-start.21 = (bf16[4,128,128]{1,2,0:T(8,128)(2,1)S(1)}, bf16[4,128,128]{1,2,0:T(8,128)(2,1)S(1)}, u32[]{:S(2)}, u32[]{:S(2)}) collective-permute-start(bf16[4,128,128]{1,2,0:T(8,128)(2,1)S(1)} %pad_maximum_fusion.7), channel_id=1, source_target_pairs={{0,1},{1,0},{2,3},{3,2},{4,5},{5,4},{6,7},{7,6},{8,9},{9,8},{10,11... | collective-permute-start | bytes 393224 | tf_op jit(solution)/shard_map/ppermute | solution.py:32
  53.7 3.1 %collective-permute-start.24 = (bf16[1,128,128]{1,2,0:T(8,128)(2,1)S(1)}, bf16[1,128,128]{1,2,0:T(8,128)(2,1)S(1)}, u32[]{:S(2)}, u32[]{:S(2)}) collective-permute-start(bf16[1,128,128]{1,2,0:T(8,128)(2,1)S(1)} %collective-permute-done.22), channel_id=1, source_target_pairs={{0,1},{1,0},{2,3},{3,2},{4,5},{5,4},{6,7},{7,6},{8,9},{9,8},{10,11... | collective-permute-start | bytes 98312 | tf_op jit(solution)/shard_map/ppermute | solution.py:32
  56.8 1.3 %collective-permute-start.25 = (bf16[3,128,128]{1,2,0:T(8,128)(2,1)S(1)}, bf16[3,128,128]{1,2,0:T(8,128)(2,1)S(1)}, u32[]{:S(2)}, u32[]{:S(2)}) collective-permute-start(bf16[3,128,128]{1,2,0:T(8,128)(2,1)S(1)} %collective-permute-done.23), channel_id=1, source_target_pairs={{0,1},{1,0},{2,3},{3,2},{4,5},{5,4},{6,7},{7,6},{8,9},{9,8},{10,11... | collective-permute-start | bytes 294920 | tf_op jit(solution)/shard_map/ppermute | solution.py:32

commit v14 on v13

--- a/solution.py
+++ b/solution.py
@@ -4,6 +4,7 @@
 import jax.numpy as jnp
 import numpy as np
 from jax import lax
+from jax.experimental.layout import Layout, with_layout_constraint
 from jax.sharding import PartitionSpec as P
 
 
@@ -101,9 +102,9 @@
 
     def advance(moment, retarded):
         source = excitation[moment] - retarded
-        return jnp.dot(
+        return with_layout_constraint(jnp.dot(
             inverse_t, source, precision=lax.Precision.HIGHEST, preferred_element_type=jnp.float32
-        )
+        ), Layout((0, 1)))
 
     results = [None] * step_count
     newer = {}

time: 60 us -> 59.8 us (level)
  local copies, waits for them, and re-layouts: 4.99 us -> 4.18 us
  other arithmetic: 3.13 us -> 3.8 us
    another operation x1 -> x0, local copies, waits for them, and re-layouts: 0.81 us -> none  [per_device(): return jnp.stack(results)]
    another operation x1, other arithmetic: 0.02 us -> 0.69 us  [per_device(): return jnp.stack(results)]
where the time goes in v14:
time: 59.8 us; the launch traced here: 59.6 us
  starting transfers between devices  28 us (47%)
  waiting for transfers between devices  15.1 us (25%)
  matrix products  8.03 us (13%)
  local copies, waits for them, and re-layouts  4.18 us (7%)
  other arithmetic  3.8 us (6%)
    ppermute x9, starting transfers between devices, line_stage(): parts.append(lax.ppermute(x, 'wide', pairs)[None])  16.9 us
    ppermute x17, waiting for transfers between devices, swap(): return lax.ppermute(x, 'wide', [(d, d ^ mask) for d in range(wide)])  14.2 us
    ppermute x17, starting transfers between devices, swap(): return lax.ppermute(x, 'wide', [(d, d ^ mask) for d in range(wide)])  11.1 us
    dot_general x27, matrix products, rowwise(): return jnp.einsum(spec, tiles, currents, preferred_element_type=jnp.float32)  7.16 us
    sort x1, other arithmetic, per_device(): column_of_block = jnp.argsort(block_owner)  1.9 us
    unnamed x22, local copies, waits for them, and re-layouts  1.34 us
  transfers between devices with their start and end apart: 26, of which 9 were waited for; matrix products, arithmetic and copies ran while one was open for 20% of the time, Pallas kernels for 0%

profile of v14, /device:TPU:0, one launch (start us, length us, event | category | flops | bytes accessed | tf_op | source)
XLA Modules:
  0.0 59.6 jit_solution(3763781957275695458)
XLA Ops:
  0.0 3.0 %collective-permute-start = (bf16[4,128,128]{2,1,0:T(8,128)(2,1)}, bf16[4,128,128]{2,1,0:T(8,128)(2,1)S(1)}, u32[]{:S(2)}, u32[]{:S(2)}) collective-permute-start(bf16[4,128,128]{2,1,0:T(8,128)(2,1)} %param.19), channel_id=1, source_target_pairs={{0,4},{1,5},{2,6},{3,7},{4,8},{5,9},{6,10},{7,11},{8,12},{9,13},{1... | collective-permute-start | bytes 393224 | tf_op jit(solution)/shard_map/ppermute | solution.py:26
  3.0 2.6 %collective-permute-start.1 = (bf16[4,128,128]{2,1,0:T(8,128)(2,1)}, bf16[4,128,128]{2,1,0:T(8,128)(2,1)S(1)}, u32[]{:S(2)}, u32[]{:S(2)}) collective-permute-start(bf16[4,128,128]{2,1,0:T(8,128)(2,1)} %param.19), channel_id=1, source_target_pairs={{0,8},{1,9},{2,10},{3,11},{4,12},{5,13},{6,14},{7,15},{8,0},{9,1},... | collective-permute-start | bytes 393224 | tf_op jit(solution)/shard_map/ppermute | solution.py:26
  5.6 1.3 %collective-permute-start.2 = (bf16[4,128,128]{2,1,0:T(8,128)(2,1)}, bf16[4,128,128]{2,1,0:T(8,128)(2,1)S(1)}, u32[]{:S(2)}, u32[]{:S(2)}) collective-permute-start(bf16[4,128,128]{2,1,0:T(8,128)(2,1)} %param.19), channel_id=1, source_target_pairs={{0,12},{1,13},{2,14},{3,15},{4,0},{5,1},{6,2},{7,3},{8,4},{9,5},{1... | collective-permute-start | bytes 393224 | tf_op jit(solution)/shard_map/ppermute | solution.py:26
  7.0 1.5 %collective-permute-start.4 = (bf16[1,4,128,128]{3,2,1,0:T(8,128)(2,1)}, bf16[1,4,128,128]{3,2,1,0:T(8,128)(2,1)S(1)}, u32[]{:S(2)}, u32[]{:S(2)}) collective-permute-start(bf16[1,4,128,128]{3,2,1,0:T(8,128)(2,1)} %bitcast.320), channel_id=1, source_target_pairs={{0,2},{1,3},{2,0},{3,1},{4,6},{5,7},{6,4},{7,5},{8,10},{9,11},{10,... | collective-permute-start | bytes 393224 | tf_op jit(solution)/shard_map/ppermute | solution.py:33
  8.7 1.9 %sort.17 = (s32[16]{0:T(128)}, s32[16]{0:T(128)S(1)}) sort(s32[16]{0:T(128)} %param.18, s32[16]{0:T(128)S(1)} %iota.5), dimensions={0}, to_apply=%region_0.0 | sort | flops 64 | bytes 256 | tf_op jit(solution)/shard_map/jit(argsort)/sort | solution.py:94
  10.6 0.7 %gather_fusion = s32[16]{0:T(128)S(1)} fusion(s32[16]{0:T(128)S(1)} %get-tuple-element.8, s32[1024]{0:T(1024)S(1)} %pad_clamp_fusion.1), kind=kCustom, calls=%fused_computation.clone | custom fusion | bytes 192 | tf_op jit(solution)/shard_map/jit(_take)/gather | solution.py:69
  11.3 0.8 %copy.17 = s32[16,2]{1,0:T(8,128)S(1)} copy(s32[16,2]{0,1:T(2,128)} %bitcast.330) | data formatting | bytes 256 | tf_op jit(solution)/shard_map/squeeze | solution.py:71
  12.0 0.7 %gather_fusion.2 = bf16[16,2,128,128]{3,2,1,0:T(8,128)(2,1)S(1)} fusion(bf16[16,2,128,128]{3,2,1,0:T(8,128)(2,1)S(1)} %bitcast.299, s32[1024]{0:T(1024)S(1)} %pad_clamp_fusion), kind=kCustom, calls=%fused_computation.2.clone | custom fusion | bytes 2097216 | tf_op jit(solution)/shard_map/jit(_take)/gather | solution.py:70
  12.8 0.6 gather_fusion.1
  13.9 0.3 bitcast_select_fusion.3
  14.5 0.5 copy-done.3
  15.1 1.1 %collective-permute-start.5 = (bf16[1,4,128,128]{3,2,1,0:T(8,128)(2,1)S(1)}, bf16[1,4,128,128]{3,2,1,0:T(8,128)(2,1)S(1)}, u32[]{:S(2)}, u32[]{:S(2)}) collective-permute-start(bf16[1,4,128,128]{3,2,1,0:T(8,128)(2,1)S(1)} %bitcast.324), channel_id=1, source_target_pairs={{0,2},{1,3},{2,0},{3,1},{4,6},{5,7},{6,4},{7,5},{8,10},{9,11},{10,... | collective-permute-start | bytes 393224 | tf_op jit(solution)/shard_map/ppermute | solution.py:33
  16.2 1.0 %collective-permute-start.6 = (bf16[2,4,128,128]{3,2,1,0:T(8,128)(2,1)S(1)}, bf16[2,4,128,128]{3,2,1,0:T(8,128)(2,1)S(1)}, u32[]{:S(2)}, u32[]{:S(2)}) collective-permute-start(bf16[2,4,128,128]{3,2,1,0:T(8,128)(2,1)S(1)} %pad_maximum_fusion.4), channel_id=1, source_target_pairs={{0,2},{1,3},{2,0},{3,1},{4,6},{5,7},{6,4},{7,5},{8,10},{9,11},{10,... | collective-permute-start | bytes 786440 | tf_op jit(solution)/shard_map/ppermute | solution.py:33
  17.2 0.3 convolution_bitcast_fusion.5
  17.6 0.3 collective-permute-start.7
  18.1 3.0 %collective-permute-done.5 = bf16[1,4,128,128]{3,2,1,0:T(8,128)(2,1)S(1)} collective-permute-done((bf16[1,4,128,128]{3,2,1,0:T(8,128)(2,1)S(1)}, bf16[1,4,128,128]{3,2,1,0:T(8,128)(2,1)S(1)}, u32[]{:S(2)}, u32[]{:S(2)}) %collective-permute-start.5) | collective-permute-done | bytes 131104 | tf_op jit(solution)/shard_map/ppermute | solution.py:33
  21.7 0.7 %collective-permute-done.8 = bf16[1,4,128,128]{3,2,1,0:T(8,128)(2,1)S(1)} collective-permute-done((bf16[1,4,128,128]{3,2,1,0:T(8,128)(2,1)S(1)}, bf16[1,4,128,128]{3,2,1,0:T(8,128)(2,1)S(1)}, u32[]{:S(2)}, u32[]{:S(2)}) %collective-permute-start.8) | collective-permute-done | bytes 131104 | tf_op jit(solution)/shard_map/ppermute | solution.py:33
  22.9 2.9 %collective-permute-done.6 = bf16[2,4,128,128]{3,2,1,0:T(8,128)(2,1)S(1)} collective-permute-done((bf16[2,4,128,128]{3,2,1,0:T(8,128)(2,1)S(1)}, bf16[2,4,128,128]{3,2,1,0:T(8,128)(2,1)S(1)}, u32[]{:S(2)}, u32[]{:S(2)}) %collective-permute-start.6) | collective-permute-done | bytes 262176 | tf_op jit(solution)/shard_map/ppermute | solution.py:33
  26.5 0.3 convolution_bitcast_fusion.3
  26.8 0.4 convolution_bitcast_fusion
  27.1 0.4 fusion.26
  28.1 0.6 %copy-done.2 = f32[3,128,128]{2,1,0:T(8,128)S(1)} copy-done((f32[3,128,128]{2,1,0:T(8,128)S(1)}, f32[3,128,128]{2,1,0:T(8,128)}, u32[]{:S(2)}) %copy-start.2) | copy-done | bytes 196632
  28.9 0.3 constant_dynamic-update-slice_fusion.8
  29.2 3.2 %collective-permute-start.10 = (bf16[128,128]{1,0:T(8,128)(2,1)S(1)}, bf16[128,128]{1,0:T(8,128)(2,1)S(1)}, u32[]{:S(2)}, u32[]{:S(2)}) collective-permute-start(bf16[128,128]{1,0:T(8,128)(2,1)S(1)} %get-tuple-element.21), channel_id=1, source_target_pairs={{0,4},{1,5},{2,6},{3,7},{4,8},{5,9},{6,10},{7,11},{8,12},{9,13},{1... | collective-permute-start | bytes 98312 | tf_op jit(solution)/shard_map/ppermute | solution.py:26
  32.5 1.2 %collective-permute-start.11 = (bf16[128,128]{1,0:T(8,128)(2,1)S(1)}, bf16[128,128]{1,0:T(8,128)(2,1)S(1)}, u32[]{:S(2)}, u32[]{:S(2)}) collective-permute-start(bf16[128,128]{1,0:T(8,128)(2,1)S(1)} %get-tuple-element.21), channel_id=1, source_target_pairs={{0,8},{1,9},{2,10},{3,11},{4,12},{5,13},{6,14},{7,15},{8,0},{9,1},... | collective-permute-start | bytes 98312 | tf_op jit(solution)/shard_map/ppermute | solution.py:26
  33.6 1.3 %collective-permute-start.12 = (bf16[128,128]{1,0:T(8,128)(2,1)S(1)}, bf16[128,128]{1,0:T(8,128)(2,1)S(1)}, u32[]{:S(2)}, u32[]{:S(2)}) collective-permute-start(bf16[128,128]{1,0:T(8,128)(2,1)S(1)} %get-tuple-element.21), channel_id=1, source_target_pairs={{0,12},{1,13},{2,14},{3,15},{4,0},{5,1},{6,2},{7,3},{8,4},{9,5},{1... | collective-permute-start | bytes 98312 | tf_op jit(solution)/shard_map/ppermute | solution.py:26
  34.9 1.5 %collective-permute-start.14 = (bf16[1,128,128]{2,1,0:T(8,128)(2,1)S(1)}, bf16[1,128,128]{2,1,0:T(8,128)(2,1)S(1)}, u32[]{:S(2)}, u32[]{:S(2)}) collective-permute-start(bf16[1,128,128]{2,1,0:T(8,128)(2,1)S(1)} %bitcast.326), channel_id=1, source_target_pairs={{0,2},{1,3},{2,0},{3,1},{4,6},{5,7},{6,4},{7,5},{8,10},{9,11},{10,... | collective-permute-start | bytes 98312 | tf_op jit(solution)/shard_map/ppermute | solution.py:33
  36.7 0.3 fusion.24
  37.0 0.3 fusion.25
  38.0 1.4 %collective-permute-start.15 = (bf16[3,128,128]{2,1,0:T(8,128)(2,1)S(1)}, bf16[3,128,128]{2,1,0:T(8,128)(2,1)S(1)}, u32[]{:S(2)}, u32[]{:S(2)}) collective-permute-start(bf16[3,128,128]{2,1,0:T(8,128)(2,1)S(1)} %pad_maximum_fusion.8), channel_id=1, source_target_pairs={{0,2},{1,3},{2,0},{3,1},{4,6},{5,7},{6,4},{7,5},{8,10},{9,11},{10,... | collective-permute-start | bytes 294920 | tf_op jit(solution)/shard_map/ppermute | solution.py:33
  39.4 0.6 collective-permute-start.16
  40.0 2.7 %collective-permute-done.15 = bf16[3,128,128]{2,1,0:T(8,128)(2,1)S(1)} collective-permute-done((bf16[3,128,128]{2,1,0:T(8,128)(2,1)S(1)}, bf16[3,128,128]{2,1,0:T(8,128)(2,1)S(1)}, u32[]{:S(2)}, u32[]{:S(2)}) %collective-permute-start.15) | collective-permute-done | bytes 98336 | tf_op jit(solution)/shard_map/ppermute | solution.py:33
  42.8 1.2 %collective-permute-done.17 = bf16[3,128,128]{2,1,0:T(8,128)(2,1)S(1)} collective-permute-done((bf16[3,128,128]{2,1,0:T(8,128)(2,1)S(1)}, bf16[3,128,128]{2,1,0:T(8,128)(2,1)S(1)}, u32[]{:S(2)}, u32[]{:S(2)}) %collective-permute-start.17) | collective-permute-done | bytes 98336 | tf_op jit(solution)/shard_map/ppermute | solution.py:33
  44.0 0.3 convolution_bitcast_fusion.11
  44.6 0.3 constant_dynamic-update-slice_fusion.17
  44.9 0.8 %collective-permute-start.18 = (bf16[128,128]{1,0:T(8,128)(2,1)S(1)}, bf16[128,128]{1,0:T(8,128)(2,1)S(1)}, u32[]{:S(2)}, u32[]{:S(2)}) collective-permute-start(bf16[128,128]{1,0:T(8,128)(2,1)S(1)} %get-tuple-element.19), channel_id=1, source_target_pairs={{0,4},{1,5},{2,6},{3,7},{4,8},{5,9},{6,10},{7,11},{8,12},{9,13},{1... | collective-permute-start | bytes 98312 | tf_op jit(solution)/shard_map/ppermute | solution.py:26
  45.7 2.4 %collective-permute-start.19 = (bf16[128,128]{1,0:T(8,128)(2,1)S(1)}, bf16[128,128]{1,0:T(8,128)(2,1)S(1)}, u32[]{:S(2)}, u32[]{:S(2)}) collective-permute-start(bf16[128,128]{1,0:T(8,128)(2,1)S(1)} %get-tuple-element.19), channel_id=1, source_target_pairs={{0,8},{1,9},{2,10},{3,11},{4,12},{5,13},{6,14},{7,15},{8,0},{9,1},... | collective-permute-start | bytes 98312 | tf_op jit(solution)/shard_map/ppermute | solution.py:26
  48.1 1.0 %collective-permute-start.20 = (bf16[128,128]{1,0:T(8,128)(2,1)S(1)}, bf16[128,128]{1,0:T(8,128)(2,1)S(1)}, u32[]{:S(2)}, u32[]{:S(2)}) collective-permute-start(bf16[128,128]{1,0:T(8,128)(2,1)S(1)} %get-tuple-element.19), channel_id=1, source_target_pairs={{0,12},{1,13},{2,14},{3,15},{4,0},{5,1},{6,2},{7,3},{8,4},{9,5},{1... | collective-permute-start | bytes 98312 | tf_op jit(solution)/shard_map/ppermute | solution.py:26
  49.2 0.5 convolution_bitcast_fusion.9
  49.7 1.6 %collective-permute-start.22 = (bf16[1,128,128]{2,1,0:T(8,128)(2,1)S(1)}, bf16[1,128,128]{2,1,0:T(8,128)(2,1)S(1)}, u32[]{:S(2)}, u32[]{:S(2)}) collective-permute-start(bf16[1,128,128]{2,1,0:T(8,128)(2,1)S(1)} %bitcast.328), channel_id=1, source_target_pairs={{0,2},{1,3},{2,0},{3,1},{4,6},{5,7},{6,4},{7,5},{8,10},{9,11},{10,... | collective-permute-start | bytes 98312 | tf_op jit(solution)/shard_map/ppermute | solution.py:33
  51.3 0.8 %collective-permute-done.20 = bf16[128,128]{1,0:T(8,128)(2,1)S(1)} collective-permute-done((bf16[128,128]{1,0:T(8,128)(2,1)S(1)}, bf16[128,128]{1,0:T(8,128)(2,1)S(1)}, u32[]{:S(2)}, u32[]{:S(2)}) %collective-permute-start.20) | collective-permute-done | bytes 32800 | tf_op jit(solution)/shard_map/ppermute | solution.py:26
  52.1 1.6 %collective-permute-start.23 = (bf16[3,128,128]{2,1,0:T(8,128)(2,1)S(1)}, bf16[3,128,128]{2,1,0:T(8,128)(2,1)S(1)}, u32[]{:S(2)}, u32[]{:S(2)}) collective-permute-start(bf16[3,128,128]{2,1,0:T(8,128)(2,1)S(1)} %pad_maximum_fusion.9), channel_id=1, source_target_pairs={{0,2},{1,3},{2,0},{3,1},{4,6},{5,7},{6,4},{7,5},{8,10},{9,11},{10,... | collective-permute-start | bytes 294920 | tf_op jit(solution)/shard_map/ppermute | solution.py:33
  53.7 0.6 collective-permute-start.24
  54.3 2.5 %collective-permute-done.23 = bf16[3,128,128]{2,1,0:T(8,128)(2,1)S(1)} collective-permute-done((bf16[3,128,128]{2,1,0:T(8,128)(2,1)S(1)}, bf16[3,128,128]{2,1,0:T(8,128)(2,1)S(1)}, u32[]{:S(2)}, u32[]{:S(2)}) %collective-permute-start.23) | collective-permute-done | bytes 98336 | tf_op jit(solution)/shard_map/ppermute | solution.py:33
  56.9 1.2 %collective-permute-done.25 = bf16[3,128,128]{2,1,0:T(8,128)(2,1)S(1)} collective-permute-done((bf16[3,128,128]{2,1,0:T(8,128)(2,1)S(1)}, bf16[3,128,128]{2,1,0:T(8,128)(2,1)S(1)}, u32[]{:S(2)}, u32[]{:S(2)}) %collective-permute-start.25) | collective-permute-done | bytes 98336 | tf_op jit(solution)/shard_map/ppermute | solution.py:33
  58.1 0.3 convolution_bitcast_fusion.10
  58.7 0.3 convolution_bitcast_fusion.8
  59.0 0.7 %pad_maximum_fusion.5 = f32[3,128,128]{2,1,0:T(8,128)} fusion(f32[1,128,128]{2,1,0:T(8,128)S(1)} %bitcast.318, f32[1,128,128]{2,1,0:T(8,128)S(1)} %bitcast.319, f32[1,128,128]{2,1,0:T(8,128)S(1)} %convolution_bitcast_fusion.8), kind=kLoop, calls=%fused_computation.89 | loop fusion | flops 98304 | bytes 393216 | tf_op jit(solution)/shard_map/stack | solution.py:136
  (83 shorter events, 5.5 us)
Async XLA Ops:
  0.0 12.0 %copy-start = (bf16[1,16,2,128,128]{4,3,2,1,0:T(8,128)(2,1)S(1)}, bf16[1,16,2,128,128]{4,3,2,1,0:T(8,128)(2,1)}, u32[]{:S(2)}) copy-start(bf16[1,16,2,128,128]{4,3,2,1,0:T(8,128)(2,1)} %param.16) | copy-start | bytes 3145732
  0.0 14.5 %collective-permute-start = (bf16[4,128,128]{2,1,0:T(8,128)(2,1)}, bf16[4,128,128]{2,1,0:T(8,128)(2,1)S(1)}, u32[]{:S(2)}, u32[]{:S(2)}) collective-permute-start(bf16[4,128,128]{2,1,0:T(8,128)(2,1)} %param.19), channel_id=1, source_target_pairs={{0,4},{1,5},{2,6},{3,7},{4,8},{5,9},{6,10},{7,11},{8,12},{9,13},{1... | collective-permute-start | bytes 393224 | tf_op jit(solution)/shard_map/ppermute | solution.py:26
  3.0 11.4 %collective-permute-start.1 = (bf16[4,128,128]{2,1,0:T(8,128)(2,1)}, bf16[4,128,128]{2,1,0:T(8,128)(2,1)S(1)}, u32[]{:S(2)}, u32[]{:S(2)}) collective-permute-start(bf16[4,128,128]{2,1,0:T(8,128)(2,1)} %param.19), channel_id=1, source_target_pairs={{0,8},{1,9},{2,10},{3,11},{4,12},{5,13},{6,14},{7,15},{8,0},{9,1},... | collective-permute-start | bytes 393224 | tf_op jit(solution)/shard_map/ppermute | solution.py:26
  5.6 8.9 %collective-permute-start.2 = (bf16[4,128,128]{2,1,0:T(8,128)(2,1)}, bf16[4,128,128]{2,1,0:T(8,128)(2,1)S(1)}, u32[]{:S(2)}, u32[]{:S(2)}) collective-permute-start(bf16[4,128,128]{2,1,0:T(8,128)(2,1)} %param.19), channel_id=1, source_target_pairs={{0,12},{1,13},{2,14},{3,15},{4,0},{5,1},{6,2},{7,3},{8,4},{9,5},{1... | collective-permute-start | bytes 393224 | tf_op jit(solution)/shard_map/ppermute | solution.py:26
  7.0 10.6 %collective-permute-start.4 = (bf16[1,4,128,128]{3,2,1,0:T(8,128)(2,1)}, bf16[1,4,128,128]{3,2,1,0:T(8,128)(2,1)S(1)}, u32[]{:S(2)}, u32[]{:S(2)}) collective-permute-start(bf16[1,4,128,128]{3,2,1,0:T(8,128)(2,1)} %bitcast.320), channel_id=1, source_target_pairs={{0,2},{1,3},{2,0},{3,1},{4,6},{5,7},{6,4},{7,5},{8,10},{9,11},{10,... | collective-permute-start | bytes 393224 | tf_op jit(solution)/shard_map/ppermute | solution.py:33
  14.1 0.9 %copy-start.3 = (bf16[4,128,128]{2,1,0:T(8,128)(2,1)S(1)}, bf16[4,128,128]{2,1,0:T(8,128)(2,1)}, u32[]{:S(2)}) copy-start(bf16[4,128,128]{2,1,0:T(8,128)(2,1)} %param.19) | copy-start | bytes 393220
  15.1 6.0 %collective-permute-start.5 = (bf16[1,4,128,128]{3,2,1,0:T(8,128)(2,1)S(1)}, bf16[1,4,128,128]{3,2,1,0:T(8,128)(2,1)S(1)}, u32[]{:S(2)}, u32[]{:S(2)}) collective-permute-start(bf16[1,4,128,128]{3,2,1,0:T(8,128)(2,1)S(1)} %bitcast.324), channel_id=1, source_target_pairs={{0,2},{1,3},{2,0},{3,1},{4,6},{5,7},{6,4},{7,5},{8,10},{9,11},{10,... | collective-permute-start | bytes 393224 | tf_op jit(solution)/shard_map/ppermute | solution.py:33
  16.2 10.6 %collective-permute-start.3 = (bf16[4,4,128,128]{3,2,1,0:T(8,128)(2,1)S(1)}, bf16[4,4,128,128]{3,2,1,0:T(8,128)(2,1)S(1)}, u32[]{:S(2)}, u32[]{:S(2)}) collective-permute-start(bf16[4,4,128,128]{3,2,1,0:T(8,128)(2,1)S(1)} %pad_maximum_fusion.3), channel_id=1, source_target_pairs={{0,1},{1,0},{2,3},{3,2},{4,5},{5,4},{6,7},{7,6},{8,9},{9,8},{10,11... | collective-permute-start | bytes 1572872 | tf_op jit(solution)/shard_map/ppermute | solution.py:33
  16.2 9.6 %collective-permute-start.6 = (bf16[2,4,128,128]{3,2,1,0:T(8,128)(2,1)S(1)}, bf16[2,4,128,128]{3,2,1,0:T(8,128)(2,1)S(1)}, u32[]{:S(2)}, u32[]{:S(2)}) collective-permute-start(bf16[2,4,128,128]{3,2,1,0:T(8,128)(2,1)S(1)} %pad_maximum_fusion.4), channel_id=1, source_target_pairs={{0,2},{1,3},{2,0},{3,1},{4,6},{5,7},{6,4},{7,5},{8,10},{9,11},{10,... | collective-permute-start | bytes 786440 | tf_op jit(solution)/shard_map/ppermute | solution.py:33
  17.6 10.5 %collective-permute-start.7 = (bf16[1,4,128,128]{3,2,1,0:T(8,128)(2,1)S(1)}, bf16[1,4,128,128]{3,2,1,0:T(8,128)(2,1)S(1)}, u32[]{:S(2)}, u32[]{:S(2)}) collective-permute-start(bf16[1,4,128,128]{3,2,1,0:T(8,128)(2,1)S(1)} %collective-permute-done.4), channel_id=1, source_target_pairs={{0,1},{1,0},{2,3},{3,2},{4,5},{5,4},{6,7},{7,6},{8,9},{9,8},{10,11... | collective-permute-start | bytes 393224 | tf_op jit(solution)/shard_map/ppermute | solution.py:33
  21.1 1.3 %collective-permute-start.8 = (bf16[1,4,128,128]{3,2,1,0:T(8,128)(2,1)S(1)}, bf16[1,4,128,128]{3,2,1,0:T(8,128)(2,1)S(1)}, u32[]{:S(2)}, u32[]{:S(2)}) collective-permute-start(bf16[1,4,128,128]{3,2,1,0:T(8,128)(2,1)S(1)} %collective-permute-done.5), channel_id=1, source_target_pairs={{0,1},{1,0},{2,3},{3,2},{4,5},{5,4},{6,7},{7,6},{8,9},{9,8},{10,11... | collective-permute-start | bytes 393224 | tf_op jit(solution)/shard_map/ppermute | solution.py:33
  25.8 2.0 %collective-permute-start.9 = (bf16[2,4,128,128]{3,2,1,0:T(8,128)(2,1)S(1)}, bf16[2,4,128,128]{3,2,1,0:T(8,128)(2,1)S(1)}, u32[]{:S(2)}, u32[]{:S(2)}) collective-permute-start(bf16[2,4,128,128]{3,2,1,0:T(8,128)(2,1)S(1)} %collective-permute-done.6), channel_id=1, source_target_pairs={{0,1},{1,0},{2,3},{3,2},{4,5},{5,4},{6,7},{7,6},{8,9},{9,8},{10,11... | collective-permute-start | bytes 786440 | tf_op jit(solution)/shard_map/ppermute | solution.py:33
  27.7 0.9 %copy-start.2 = (f32[3,128,128]{2,1,0:T(8,128)S(1)}, f32[3,128,128]{2,1,0:T(8,128)}, u32[]{:S(2)}) copy-start(f32[3,128,128]{2,1,0:T(8,128)} %param.20) | copy-start | bytes 589828
  28.0 0.9 %copy-start.1 = (f32[1,128,128]{2,1,0:T(8,128)S(1)}, f32[1,128,128]{2,1,0:T(8,128)}, u32[]{:S(2)}) copy-start(f32[1,128,128]{2,1,0:T(8,128)} %param.21) | copy-start | bytes 196612
  29.2 8.7 %collective-permute-start.10 = (bf16[128,128]{1,0:T(8,128)(2,1)S(1)}, bf16[128,128]{1,0:T(8,128)(2,1)S(1)}, u32[]{:S(2)}, u32[]{:S(2)}) collective-permute-start(bf16[128,128]{1,0:T(8,128)(2,1)S(1)} %get-tuple-element.21), channel_id=1, source_target_pairs={{0,4},{1,5},{2,6},{3,7},{4,8},{5,9},{6,10},{7,11},{8,12},{9,13},{1... | collective-permute-start | bytes 98312 | tf_op jit(solution)/shard_map/ppermute | solution.py:26
  32.5 5.5 %collective-permute-start.11 = (bf16[128,128]{1,0:T(8,128)(2,1)S(1)}, bf16[128,128]{1,0:T(8,128)(2,1)S(1)}, u32[]{:S(2)}, u32[]{:S(2)}) collective-permute-start(bf16[128,128]{1,0:T(8,128)(2,1)S(1)} %get-tuple-element.21), channel_id=1, source_target_pairs={{0,8},{1,9},{2,10},{3,11},{4,12},{5,13},{6,14},{7,15},{8,0},{9,1},... | collective-permute-start | bytes 98312 | tf_op jit(solution)/shard_map/ppermute | solution.py:26
  33.6 4.3 %collective-permute-start.12 = (bf16[128,128]{1,0:T(8,128)(2,1)S(1)}, bf16[128,128]{1,0:T(8,128)(2,1)S(1)}, u32[]{:S(2)}, u32[]{:S(2)}) collective-permute-start(bf16[128,128]{1,0:T(8,128)(2,1)S(1)} %get-tuple-element.21), channel_id=1, source_target_pairs={{0,12},{1,13},{2,14},{3,15},{4,0},{5,1},{6,2},{7,3},{8,4},{9,5},{1... | collective-permute-start | bytes 98312 | tf_op jit(solution)/shard_map/ppermute | solution.py:26
  34.9 4.5 %collective-permute-start.14 = (bf16[1,128,128]{2,1,0:T(8,128)(2,1)S(1)}, bf16[1,128,128]{2,1,0:T(8,128)(2,1)S(1)}, u32[]{:S(2)}, u32[]{:S(2)}) collective-permute-start(bf16[1,128,128]{2,1,0:T(8,128)(2,1)S(1)} %bitcast.326), channel_id=1, source_target_pairs={{0,2},{1,3},{2,0},{3,1},{4,6},{5,7},{6,4},{7,5},{8,10},{9,11},{10,... | collective-permute-start | bytes 98312 | tf_op jit(solution)/shard_map/ppermute | solution.py:33
  38.0 4.7 %collective-permute-start.15 = (bf16[3,128,128]{2,1,0:T(8,128)(2,1)S(1)}, bf16[3,128,128]{2,1,0:T(8,128)(2,1)S(1)}, u32[]{:S(2)}, u32[]{:S(2)}) collective-permute-start(bf16[3,128,128]{2,1,0:T(8,128)(2,1)S(1)} %pad_maximum_fusion.8), channel_id=1, source_target_pairs={{0,2},{1,3},{2,0},{3,1},{4,6},{5,7},{6,4},{7,5},{8,10},{9,11},{10,... | collective-permute-start | bytes 294920 | tf_op jit(solution)/shard_map/ppermute | solution.py:33
  39.4 3.3 %collective-permute-start.13 = (bf16[4,128,128]{2,1,0:T(8,128)(2,1)S(1)}, bf16[4,128,128]{2,1,0:T(8,128)(2,1)S(1)}, u32[]{:S(2)}, u32[]{:S(2)}) collective-permute-start(bf16[4,128,128]{2,1,0:T(8,128)(2,1)S(1)} %pad_maximum_fusion.6), channel_id=1, source_target_pairs={{0,1},{1,0},{2,3},{3,2},{4,5},{5,4},{6,7},{7,6},{8,9},{9,8},{10,11... | collective-permute-start | bytes 393224 | tf_op jit(solution)/shard_map/ppermute | solution.py:33
  39.4 3.3 %collective-permute-start.16 = (bf16[1,128,128]{2,1,0:T(8,128)(2,1)S(1)}, bf16[1,128,128]{2,1,0:T(8,128)(2,1)S(1)}, u32[]{:S(2)}, u32[]{:S(2)}) collective-permute-start(bf16[1,128,128]{2,1,0:T(8,128)(2,1)S(1)} %collective-permute-done.14), channel_id=1, source_target_pairs={{0,1},{1,0},{2,3},{3,2},{4,5},{5,4},{6,7},{7,6},{8,9},{9,8},{10,11... | collective-permute-start | bytes 98312 | tf_op jit(solution)/shard_map/ppermute | solution.py:33
  42.7 1.3 %collective-permute-start.17 = (bf16[3,128,128]{2,1,0:T(8,128)(2,1)S(1)}, bf16[3,128,128]{2,1,0:T(8,128)(2,1)S(1)}, u32[]{:S(2)}, u32[]{:S(2)}) collective-permute-start(bf16[3,128,128]{2,1,0:T(8,128)(2,1)S(1)} %collective-permute-done.15), channel_id=1, source_target_pairs={{0,1},{1,0},{2,3},{3,2},{4,5},{5,4},{6,7},{7,6},{8,9},{9,8},{10,11... | collective-permute-start | bytes 294920 | tf_op jit(solution)/shard_map/ppermute | solution.py:33
  44.9 6.4 %collective-permute-start.18 = (bf16[128,128]{1,0:T(8,128)(2,1)S(1)}, bf16[128,128]{1,0:T(8,128)(2,1)S(1)}, u32[]{:S(2)}, u32[]{:S(2)}) collective-permute-start(bf16[128,128]{1,0:T(8,128)(2,1)S(1)} %get-tuple-element.19), channel_id=1, source_target_pairs={{0,4},{1,5},{2,6},{3,7},{4,8},{5,9},{6,10},{7,11},{8,12},{9,13},{1... | collective-permute-start | bytes 98312 | tf_op jit(solution)/shard_map/ppermute | solution.py:26
  45.7 5.6 %collective-permute-start.19 = (bf16[128,128]{1,0:T(8,128)(2,1)S(1)}, bf16[128,128]{1,0:T(8,128)(2,1)S(1)}, u32[]{:S(2)}, u32[]{:S(2)}) collective-permute-start(bf16[128,128]{1,0:T(8,128)(2,1)S(1)} %get-tuple-element.19), channel_id=1, source_target_pairs={{0,8},{1,9},{2,10},{3,11},{4,12},{5,13},{6,14},{7,15},{8,0},{9,1},... | collective-permute-start | bytes 98312 | tf_op jit(solution)/shard_map/ppermute | solution.py:26
  48.1 3.9 %collective-permute-start.20 = (bf16[128,128]{1,0:T(8,128)(2,1)S(1)}, bf16[128,128]{1,0:T(8,128)(2,1)S(1)}, u32[]{:S(2)}, u32[]{:S(2)}) collective-permute-start(bf16[128,128]{1,0:T(8,128)(2,1)S(1)} %get-tuple-element.19), channel_id=1, source_target_pairs={{0,12},{1,13},{2,14},{3,15},{4,0},{5,1},{6,2},{7,3},{8,4},{9,5},{1... | collective-permute-start | bytes 98312 | tf_op jit(solution)/shard_map/ppermute | solution.py:26
  49.7 4.0 %collective-permute-start.22 = (bf16[1,128,128]{2,1,0:T(8,128)(2,1)S(1)}, bf16[1,128,128]{2,1,0:T(8,128)(2,1)S(1)}, u32[]{:S(2)}, u32[]{:S(2)}) collective-permute-start(bf16[1,128,128]{2,1,0:T(8,128)(2,1)S(1)} %bitcast.328), channel_id=1, source_target_pairs={{0,2},{1,3},{2,0},{3,1},{4,6},{5,7},{6,4},{7,5},{8,10},{9,11},{10,... | collective-permute-start | bytes 98312 | tf_op jit(solution)/shard_map/ppermute | solution.py:33
  52.1 4.7 %collective-permute-start.23 = (bf16[3,128,128]{2,1,0:T(8,128)(2,1)S(1)}, bf16[3,128,128]{2,1,0:T(8,128)(2,1)S(1)}, u32[]{:S(2)}, u32[]{:S(2)}) collective-permute-start(bf16[3,128,128]{2,1,0:T(8,128)(2,1)S(1)} %pad_maximum_fusion.9), channel_id=1, source_target_pairs={{0,2},{1,3},{2,0},{3,1},{4,6},{5,7},{6,4},{7,5},{8,10},{9,11},{10,... | collective-permute-start | bytes 294920 | tf_op jit(solution)/shard_map/ppermute | solution.py:33
  53.7 3.1 %collective-permute-start.21 = (bf16[4,128,128]{2,1,0:T(8,128)(2,1)S(1)}, bf16[4,128,128]{2,1,0:T(8,128)(2,1)S(1)}, u32[]{:S(2)}, u32[]{:S(2)}) collective-permute-start(bf16[4,128,128]{2,1,0:T(8,128)(2,1)S(1)} %pad_maximum_fusion.7), channel_id=1, source_target_pairs={{0,1},{1,0},{2,3},{3,2},{4,5},{5,4},{6,7},{7,6},{8,9},{9,8},{10,11... | collective-permute-start | bytes 393224 | tf_op jit(solution)/shard_map/ppermute | solution.py:33
  53.7 3.1 %collective-permute-start.24 = (bf16[1,128,128]{2,1,0:T(8,128)(2,1)S(1)}, bf16[1,128,128]{2,1,0:T(8,128)(2,1)S(1)}, u32[]{:S(2)}, u32[]{:S(2)}) collective-permute-start(bf16[1,128,128]{2,1,0:T(8,128)(2,1)S(1)} %collective-permute-done.22), channel_id=1, source_target_pairs={{0,1},{1,0},{2,3},{3,2},{4,5},{5,4},{6,7},{7,6},{8,9},{9,8},{10,11... | collective-permute-start | bytes 98312 | tf_op jit(solution)/shard_map/ppermute | solution.py:33
  56.8 1.3 %collective-permute-start.25 = (bf16[3,128,128]{2,1,0:T(8,128)(2,1)S(1)}, bf16[3,128,128]{2,1,0:T(8,128)(2,1)S(1)}, u32[]{:S(2)}, u32[]{:S(2)}) collective-permute-start(bf16[3,128,128]{2,1,0:T(8,128)(2,1)S(1)} %collective-permute-done.23), channel_id=1, source_target_pairs={{0,1},{1,0},{2,3},{3,2},{4,5},{5,4},{6,7},{7,6},{8,9},{9,8},{10,11... | collective-permute-start | bytes 294920 | tf_op jit(solution)/shard_map/ppermute | solution.py:33

commit v15 on v14

--- a/solution.py
+++ b/solution.py
@@ -106,7 +106,7 @@
             inverse_t, source, precision=lax.Precision.HIGHEST, preferred_element_type=jnp.float32
         ), Layout((0, 1)))
 
-    results = [None] * step_count
+    output = jnp.zeros((step_count,) + excitation.shape[1:], jnp.float32)
     newer = {}
     recent = None
     for moment in range(step_count - 1, -1, -1):
@@ -121,7 +121,7 @@
         for delay in range(1, first):
             retarded = retarded + rowwise(recent[:, delay - 1], newer[moment + delay])
         current = advance(moment, retarded)
-        results[moment] = current
+        output = lax.dynamic_update_slice(output, current[None], (moment, 0, 0))
         if moment > 0:
             pieces, new_blocks = gather_blocks(current.astype(jnp.bfloat16), wide, True)
             newer[moment] = jnp.concatenate(pieces)
@@ -133,7 +133,7 @@
                     new_blocks,
                     range(1, min(lag_count, step_count - 1) + 1),
                 )
-    return jnp.stack(results)
+    return output
 
 
 def solution(mesh):

time: 59.8 us -> 59.9 us (level)
  waiting for transfers between devices: 15.1 us -> 19.4 us
  starting transfers between devices: 28 us -> 24.4 us
  other arithmetic: 3.8 us -> 3.1 us
  matrix products: 8.03 us -> 8.69 us
    ppermute x9, waiting for transfers between devices: 0.94 us -> 4.55 us  [line_stage(): parts.append(lax.ppermute(x, 'wide', pairs)[None])]
    ppermute x9, starting transfers between devices: 16.9 us -> 14.9 us  [line_stage(): parts.append(lax.ppermute(x, 'wide', pairs)[None])]
    ppermute x17, starting transfers between devices: 11.1 us -> 9.44 us  [swap(): return lax.ppermute(x, 'wide', [(d, d ^ mask) for d in range(wide)])]
    another operation x1 -> x0, other arithmetic: 0.69 us -> none  [per_device(): return jnp.stack(results)]
    ppermute x17, waiting for transfers between devices: 14.2 us -> 14.8 us  [swap(): return lax.ppermute(x, 'wide', [(d, d ^ mask) for d in range(wide)])]
    dot_general x3, matrix products: 0.87 us -> 1.5 us  [advance(): jnp.dot(inverse_t, source, precision=lax.Precision.HIGHEST, preferred_ele...]
    unnamed x22 -> x25, local copies, waits for them, and re-layouts: 1.34 us -> 0.81 us
  transfers between devices with their start and end apart: 26 -> 26, of which waited for: 9 -> 11; matrix products, arithmetic and copies ran while one was open for 20% -> 20% of each run, Pallas kernels for 0% -> 0%
where the time goes in v15:
time: 59.9 us; the launch traced here: 59.7 us
  starting transfers between devices  24.4 us (41%)
  waiting for transfers between devices  19.4 us (32%)
  matrix products  8.69 us (15%)
  local copies, waits for them, and re-layouts  3.66 us (6%)
  other arithmetic  3.1 us (5%)
    ppermute x9, starting transfers between devices, line_stage(): parts.append(lax.ppermute(x, 'wide', pairs)[None])  14.9 us
    ppermute x17, waiting for transfers between devices, swap(): return lax.ppermute(x, 'wide', [(d, d ^ mask) for d in range(wide)])  14.8 us
    ppermute x17, starting transfers between devices, swap(): return lax.ppermute(x, 'wide', [(d, d ^ mask) for d in range(wide)])  9.44 us
    dot_general x27, matrix products, rowwise(): return jnp.einsum(spec, tiles, currents, preferred_element_type=jnp.float32)  7.18 us
    ppermute x9, waiting for transfers between devices, line_stage(): parts.append(lax.ppermute(x, 'wide', pairs)[None])  4.55 us
    sort x1, other arithmetic, per_device(): column_of_block = jnp.argsort(block_owner)  1.9 us
    dot_general x3, matrix products, advance(): jnp.dot(inverse_t, source, precision=lax.Precision.HIGHEST, preferred_ele...  1.5 us
  transfers between devices with their start and end apart: 26, of which 11 were waited for; matrix products, arithmetic and copies ran while one was open for 20% of the time, Pallas kernels for 0%

profile of v15, /device:TPU:0, one launch (start us, length us, event | category | flops | bytes accessed | tf_op | source)
XLA Modules:
  0.0 59.7 jit_solution(17901729585848432400)
XLA Ops:
  0.0 5.0 %collective-permute-start.2 = (bf16[4,128,128]{2,1,0:T(8,128)(2,1)}, bf16[4,128,128]{2,1,0:T(8,128)(2,1)S(1)}, u32[]{:S(2)}, u32[]{:S(2)}) collective-permute-start(bf16[4,128,128]{2,1,0:T(8,128)(2,1)} %param.19), channel_id=1, source_target_pairs={{0,12},{1,13},{2,14},{3,15},{4,0},{5,1},{6,2},{7,3},{8,4},{9,5},{1... | collective-permute-start | bytes 393224 | tf_op jit(solution)/shard_map/ppermute | solution.py:26
  5.1 1.0 %collective-permute-start.1 = (bf16[4,128,128]{2,1,0:T(8,128)(2,1)}, bf16[4,128,128]{2,1,0:T(8,128)(2,1)S(1)}, u32[]{:S(2)}, u32[]{:S(2)}) collective-permute-start(bf16[4,128,128]{2,1,0:T(8,128)(2,1)} %param.19), channel_id=1, source_target_pairs={{0,8},{1,9},{2,10},{3,11},{4,12},{5,13},{6,14},{7,15},{8,0},{9,1},... | collective-permute-start | bytes 393224 | tf_op jit(solution)/shard_map/ppermute | solution.py:26
  6.1 1.5 %collective-permute-start.4 = (bf16[1,4,128,128]{3,2,1,0:T(8,128)(2,1)}, bf16[1,4,128,128]{3,2,1,0:T(8,128)(2,1)S(1)}, u32[]{:S(2)}, u32[]{:S(2)}) collective-permute-start(bf16[1,4,128,128]{3,2,1,0:T(8,128)(2,1)} %bitcast.324), channel_id=1, source_target_pairs={{0,2},{1,3},{2,0},{3,1},{4,6},{5,7},{6,4},{7,5},{8,10},{9,11},{10,... | collective-permute-start | bytes 393224 | tf_op jit(solution)/shard_map/ppermute | solution.py:33
  7.8 1.9 %sort.17 = (s32[16]{0:T(128)}, s32[16]{0:T(128)S(1)}) sort(s32[16]{0:T(128)} %param.18, s32[16]{0:T(128)S(1)} %iota.5), dimensions={0}, to_apply=%region_0.0 | sort | flops 64 | bytes 256 | tf_op jit(solution)/shard_map/jit(argsort)/sort | solution.py:94
  9.7 0.7 %gather_fusion = s32[16]{0:T(128)S(1)} fusion(s32[16]{0:T(128)S(1)} %get-tuple-element.8, s32[1024]{0:T(1024)S(1)} %pad_clamp_fusion.1), kind=kCustom, calls=%fused_computation.clone | custom fusion | bytes 192 | tf_op jit(solution)/shard_map/jit(_take)/gather | solution.py:69
  10.4 0.8 %copy.17 = s32[16,2]{1,0:T(8,128)S(1)} copy(s32[16,2]{0,1:T(2,128)} %bitcast.332) | data formatting | bytes 256 | tf_op jit(solution)/shard_map/squeeze | solution.py:71
  11.1 0.7 %gather_fusion.2 = bf16[16,2,128,128]{3,2,1,0:T(8,128)(2,1)S(1)} fusion(bf16[16,2,128,128]{3,2,1,0:T(8,128)(2,1)S(1)} %bitcast.302, s32[1024]{0:T(1024)S(1)} %pad_clamp_fusion), kind=kCustom, calls=%fused_computation.2.clone | custom fusion | bytes 2097216 | tf_op jit(solution)/shard_map/jit(_take)/gather | solution.py:70
  11.9 0.6 gather_fusion.1
  12.9 0.3 bitcast_select_fusion.6
  13.4 3.3 %collective-permute-done.1 = bf16[4,128,128]{2,1,0:T(8,128)(2,1)S(1)} collective-permute-done((bf16[4,128,128]{2,1,0:T(8,128)(2,1)}, bf16[4,128,128]{2,1,0:T(8,128)(2,1)S(1)}, u32[]{:S(2)}, u32[]{:S(2)}) %collective-permute-start.1) | collective-permute-done | bytes 131104 | tf_op jit(solution)/shard_map/ppermute | solution.py:26
  16.9 1.6 %collective-permute-start.5 = (bf16[1,4,128,128]{3,2,1,0:T(8,128)(2,1)S(1)}, bf16[1,4,128,128]{3,2,1,0:T(8,128)(2,1)S(1)}, u32[]{:S(2)}, u32[]{:S(2)}) collective-permute-start(bf16[1,4,128,128]{3,2,1,0:T(8,128)(2,1)S(1)} %bitcast.328), channel_id=1, source_target_pairs={{0,2},{1,3},{2,0},{3,1},{4,6},{5,7},{6,4},{7,5},{8,10},{9,11},{10,... | collective-permute-start | bytes 393224 | tf_op jit(solution)/shard_map/ppermute | solution.py:33
  18.5 0.5 collective-permute-start.6
  19.0 0.3 convolution_bitcast_fusion.5
  19.3 0.3 collective-permute-start.7
  19.6 0.3 convolution_bitcast_fusion.3
  19.9 2.4 %collective-permute-done.5 = bf16[1,4,128,128]{3,2,1,0:T(8,128)(2,1)S(1)} collective-permute-done((bf16[1,4,128,128]{3,2,1,0:T(8,128)(2,1)S(1)}, bf16[1,4,128,128]{3,2,1,0:T(8,128)(2,1)S(1)}, u32[]{:S(2)}, u32[]{:S(2)}) %collective-permute-start.5) | collective-permute-done | bytes 131104 | tf_op jit(solution)/shard_map/ppermute | solution.py:33
  22.9 0.7 %collective-permute-done.8 = bf16[1,4,128,128]{3,2,1,0:T(8,128)(2,1)S(1)} collective-permute-done((bf16[1,4,128,128]{3,2,1,0:T(8,128)(2,1)S(1)}, bf16[1,4,128,128]{3,2,1,0:T(8,128)(2,1)S(1)}, u32[]{:S(2)}, u32[]{:S(2)}) %collective-permute-start.8) | collective-permute-done | bytes 131104 | tf_op jit(solution)/shard_map/ppermute | solution.py:33
  24.1 3.4 %collective-permute-done.6 = bf16[2,4,128,128]{3,2,1,0:T(8,128)(2,1)S(1)} collective-permute-done((bf16[2,4,128,128]{3,2,1,0:T(8,128)(2,1)S(1)}, bf16[2,4,128,128]{3,2,1,0:T(8,128)(2,1)S(1)}, u32[]{:S(2)}, u32[]{:S(2)}) %collective-permute-start.6) | collective-permute-done | bytes 262176 | tf_op jit(solution)/shard_map/ppermute | solution.py:33
  28.2 0.3 convolution_bitcast_fusion.7
  28.5 0.3 convolution_bitcast_fusion
  28.9 0.4 fusion.27
  29.5 0.3 convolution_bitcast_fusion.6
  29.8 0.6 %copy-done.2 = f32[3,128,128]{2,1,0:T(8,128)S(1)} copy-done((f32[3,128,128]{2,1,0:T(8,128)S(1)}, f32[3,128,128]{2,1,0:T(8,128)}, u32[]{:S(2)}) %copy-start.2) | copy-done | bytes 196632
  30.6 0.3 constant_dynamic-update-slice_fusion.8
  30.9 0.8 %collective-permute-start.10 = (bf16[128,128]{1,0:T(8,128)(2,1)S(1)}, bf16[128,128]{1,0:T(8,128)(2,1)S(1)}, u32[]{:S(2)}, u32[]{:S(2)}) collective-permute-start(bf16[128,128]{1,0:T(8,128)(2,1)S(1)} %get-tuple-element.21), channel_id=1, source_target_pairs={{0,4},{1,5},{2,6},{3,7},{4,8},{5,9},{6,10},{7,11},{8,12},{9,13},{1... | collective-permute-start | bytes 98312 | tf_op jit(solution)/shard_map/ppermute | solution.py:26
  31.7 2.1 %collective-permute-start.11 = (bf16[128,128]{1,0:T(8,128)(2,1)S(1)}, bf16[128,128]{1,0:T(8,128)(2,1)S(1)}, u32[]{:S(2)}, u32[]{:S(2)}) collective-permute-start(bf16[128,128]{1,0:T(8,128)(2,1)S(1)} %get-tuple-element.21), channel_id=1, source_target_pairs={{0,8},{1,9},{2,10},{3,11},{4,12},{5,13},{6,14},{7,15},{8,0},{9,1},... | collective-permute-start | bytes 98312 | tf_op jit(solution)/shard_map/ppermute | solution.py:26
  33.8 1.0 %collective-permute-start.12 = (bf16[128,128]{1,0:T(8,128)(2,1)S(1)}, bf16[128,128]{1,0:T(8,128)(2,1)S(1)}, u32[]{:S(2)}, u32[]{:S(2)}) collective-permute-start(bf16[128,128]{1,0:T(8,128)(2,1)S(1)} %get-tuple-element.21), channel_id=1, source_target_pairs={{0,12},{1,13},{2,14},{3,15},{4,0},{5,1},{6,2},{7,3},{8,4},{9,5},{1... | collective-permute-start | bytes 98312 | tf_op jit(solution)/shard_map/ppermute | solution.py:26
  34.8 1.5 %collective-permute-start.14 = (bf16[1,128,128]{2,1,0:T(8,128)(2,1)S(1)}, bf16[1,128,128]{2,1,0:T(8,128)(2,1)S(1)}, u32[]{:S(2)}, u32[]{:S(2)}) collective-permute-start(bf16[1,128,128]{2,1,0:T(8,128)(2,1)S(1)} %bitcast.330), channel_id=1, source_target_pairs={{0,2},{1,3},{2,0},{3,1},{4,6},{5,7},{6,4},{7,5},{8,10},{9,11},{10,... | collective-permute-start | bytes 98312 | tf_op jit(solution)/shard_map/ppermute | solution.py:33
  36.6 0.3 fusion.26
  36.9 0.3 fusion.25
  38.0 1.4 %collective-permute-start.15 = (bf16[3,128,128]{2,1,0:T(8,128)(2,1)S(1)}, bf16[3,128,128]{2,1,0:T(8,128)(2,1)S(1)}, u32[]{:S(2)}, u32[]{:S(2)}) collective-permute-start(bf16[3,128,128]{2,1,0:T(8,128)(2,1)S(1)} %pad_maximum_fusion.7), channel_id=1, source_target_pairs={{0,2},{1,3},{2,0},{3,1},{4,6},{5,7},{6,4},{7,5},{8,10},{9,11},{10,... | collective-permute-start | bytes 294920 | tf_op jit(solution)/shard_map/ppermute | solution.py:33
  39.4 0.6 collective-permute-start.16
  40.0 2.7 %collective-permute-done.15 = bf16[3,128,128]{2,1,0:T(8,128)(2,1)S(1)} collective-permute-done((bf16[3,128,128]{2,1,0:T(8,128)(2,1)S(1)}, bf16[3,128,128]{2,1,0:T(8,128)(2,1)S(1)}, u32[]{:S(2)}, u32[]{:S(2)}) %collective-permute-start.15) | collective-permute-done | bytes 98336 | tf_op jit(solution)/shard_map/ppermute | solution.py:33
  42.8 1.2 %collective-permute-done.17 = bf16[3,128,128]{2,1,0:T(8,128)(2,1)S(1)} collective-permute-done((bf16[3,128,128]{2,1,0:T(8,128)(2,1)S(1)}, bf16[3,128,128]{2,1,0:T(8,128)(2,1)S(1)}, u32[]{:S(2)}, u32[]{:S(2)}) %collective-permute-start.17) | collective-permute-done | bytes 98336 | tf_op jit(solution)/shard_map/ppermute | solution.py:33
  44.0 0.3 convolution_bitcast_fusion.15
  44.6 0.3 bitcast_dynamic-update-slice_fusion
  44.9 1.4 %collective-permute-start.18 = (bf16[128,128]{1,0:T(8,128)(2,1)S(1)}, bf16[128,128]{1,0:T(8,128)(2,1)S(1)}, u32[]{:S(2)}, u32[]{:S(2)}) collective-permute-start(bf16[128,128]{1,0:T(8,128)(2,1)S(1)} %get-tuple-element.19), channel_id=1, source_target_pairs={{0,4},{1,5},{2,6},{3,7},{4,8},{5,9},{6,10},{7,11},{8,12},{9,13},{1... | collective-permute-start | bytes 98312 | tf_op jit(solution)/shard_map/ppermute | solution.py:26
  46.3 1.8 %collective-permute-start.19 = (bf16[128,128]{1,0:T(8,128)(2,1)S(1)}, bf16[128,128]{1,0:T(8,128)(2,1)S(1)}, u32[]{:S(2)}, u32[]{:S(2)}) collective-permute-start(bf16[128,128]{1,0:T(8,128)(2,1)S(1)} %get-tuple-element.19), channel_id=1, source_target_pairs={{0,8},{1,9},{2,10},{3,11},{4,12},{5,13},{6,14},{7,15},{8,0},{9,1},... | collective-permute-start | bytes 98312 | tf_op jit(solution)/shard_map/ppermute | solution.py:26
  48.1 1.7 %collective-permute-start.20 = (bf16[128,128]{1,0:T(8,128)(2,1)S(1)}, bf16[128,128]{1,0:T(8,128)(2,1)S(1)}, u32[]{:S(2)}, u32[]{:S(2)}) collective-permute-start(bf16[128,128]{1,0:T(8,128)(2,1)S(1)} %get-tuple-element.19), channel_id=1, source_target_pairs={{0,12},{1,13},{2,14},{3,15},{4,0},{5,1},{6,2},{7,3},{8,4},{9,5},{1... | collective-permute-start | bytes 98312 | tf_op jit(solution)/shard_map/ppermute | solution.py:26
  49.9 0.5 convolution_bitcast_fusion.9
  50.4 0.6 collective-permute-start.22
  51.0 1.0 %collective-permute-done.19 = bf16[128,128]{1,0:T(8,128)(2,1)S(1)} collective-permute-done((bf16[128,128]{1,0:T(8,128)(2,1)S(1)}, bf16[128,128]{1,0:T(8,128)(2,1)S(1)}, u32[]{:S(2)}, u32[]{:S(2)}) %collective-permute-start.19) | collective-permute-done | bytes 32800 | tf_op jit(solution)/shard_map/ppermute | solution.py:26
  52.2 1.5 %collective-permute-start.23 = (bf16[3,128,128]{2,1,0:T(8,128)(2,1)S(1)}, bf16[3,128,128]{2,1,0:T(8,128)(2,1)S(1)}, u32[]{:S(2)}, u32[]{:S(2)}) collective-permute-start(bf16[3,128,128]{2,1,0:T(8,128)(2,1)S(1)} %pad_maximum_fusion.8), channel_id=1, source_target_pairs={{0,2},{1,3},{2,0},{3,1},{4,6},{5,7},{6,4},{7,5},{8,10},{9,11},{10,... | collective-permute-start | bytes 294920 | tf_op jit(solution)/shard_map/ppermute | solution.py:33
  53.7 1.0 %collective-permute-done.22 = bf16[1,128,128]{2,1,0:T(8,128)(2,1)S(1)} collective-permute-done((bf16[1,128,128]{2,1,0:T(8,128)(2,1)S(1)}, bf16[1,128,128]{2,1,0:T(8,128)(2,1)S(1)}, u32[]{:S(2)}, u32[]{:S(2)}) %collective-permute-start.22) | collective-permute-done | bytes 32800 | tf_op jit(solution)/shard_map/ppermute | solution.py:33
  54.7 2.2 %collective-permute-done.23 = bf16[3,128,128]{2,1,0:T(8,128)(2,1)S(1)} collective-permute-done((bf16[3,128,128]{2,1,0:T(8,128)(2,1)S(1)}, bf16[3,128,128]{2,1,0:T(8,128)(2,1)S(1)}, u32[]{:S(2)}, u32[]{:S(2)}) %collective-permute-start.23) | collective-permute-done | bytes 98336 | tf_op jit(solution)/shard_map/ppermute | solution.py:33
  57.0 1.2 %collective-permute-done.25 = bf16[3,128,128]{2,1,0:T(8,128)(2,1)S(1)} collective-permute-done((bf16[3,128,128]{2,1,0:T(8,128)(2,1)S(1)}, bf16[3,128,128]{2,1,0:T(8,128)(2,1)S(1)}, u32[]{:S(2)}, u32[]{:S(2)}) %collective-permute-start.25) | collective-permute-done | bytes 98336 | tf_op jit(solution)/shard_map/ppermute | solution.py:33
  58.2 0.3 convolution_bitcast_fusion.10
  58.8 0.9 %fusion = f32[3,128,128]{2,1,0:T(8,128)} fusion(f32[3,128,128]{2,1,0:T(8,128)} %copy-done.3, f32[128,128]{1,0:T(8,128)S(1)} %fusion.24, f32[1,128,128]{2,1,0:T(8,128)S(1)} %copy-done.1), kind=kOutput, calls=%fused_computation.14 | convolution fusion | flops 25165824 | bytes 196608 | tf_op jit(solution)/shard_map/dot_general | solution.py:105
  (86 shorter events, 5.1 us)
Async XLA Ops:
  0.0 11.1 %copy-start = (bf16[1,16,2,128,128]{4,3,2,1,0:T(8,128)(2,1)S(1)}, bf16[1,16,2,128,128]{4,3,2,1,0:T(8,128)(2,1)}, u32[]{:S(2)}) copy-start(bf16[1,16,2,128,128]{4,3,2,1,0:T(8,128)(2,1)} %param.16) | copy-start | bytes 3145732
  0.0 13.4 %collective-permute-start.2 = (bf16[4,128,128]{2,1,0:T(8,128)(2,1)}, bf16[4,128,128]{2,1,0:T(8,128)(2,1)S(1)}, u32[]{:S(2)}, u32[]{:S(2)}) collective-permute-start(bf16[4,128,128]{2,1,0:T(8,128)(2,1)} %param.19), channel_id=1, source_target_pairs={{0,12},{1,13},{2,14},{3,15},{4,0},{5,1},{6,2},{7,3},{8,4},{9,5},{1... | collective-permute-start | bytes 393224 | tf_op jit(solution)/shard_map/ppermute | solution.py:26
  5.1 11.7 %collective-permute-start = (bf16[4,128,128]{2,1,0:T(8,128)(2,1)}, bf16[4,128,128]{2,1,0:T(8,128)(2,1)S(1)}, u32[]{:S(2)}, u32[]{:S(2)}) collective-permute-start(bf16[4,128,128]{2,1,0:T(8,128)(2,1)} %param.19), channel_id=1, source_target_pairs={{0,4},{1,5},{2,6},{3,7},{4,8},{5,9},{6,10},{7,11},{8,12},{9,13},{1... | collective-permute-start | bytes 393224 | tf_op jit(solution)/shard_map/ppermute | solution.py:26
  5.1 11.7 %collective-permute-start.1 = (bf16[4,128,128]{2,1,0:T(8,128)(2,1)}, bf16[4,128,128]{2,1,0:T(8,128)(2,1)S(1)}, u32[]{:S(2)}, u32[]{:S(2)}) collective-permute-start(bf16[4,128,128]{2,1,0:T(8,128)(2,1)} %param.19), channel_id=1, source_target_pairs={{0,8},{1,9},{2,10},{3,11},{4,12},{5,13},{6,14},{7,15},{8,0},{9,1},... | collective-permute-start | bytes 393224 | tf_op jit(solution)/shard_map/ppermute | solution.py:26
  6.1 13.2 %collective-permute-start.4 = (bf16[1,4,128,128]{3,2,1,0:T(8,128)(2,1)}, bf16[1,4,128,128]{3,2,1,0:T(8,128)(2,1)S(1)}, u32[]{:S(2)}, u32[]{:S(2)}) collective-permute-start(bf16[1,4,128,128]{3,2,1,0:T(8,128)(2,1)} %bitcast.324), channel_id=1, source_target_pairs={{0,2},{1,3},{2,0},{3,1},{4,6},{5,7},{6,4},{7,5},{8,10},{9,11},{10,... | collective-permute-start | bytes 393224 | tf_op jit(solution)/shard_map/ppermute | solution.py:33
  13.2 3.5 %copy-start.4 = (bf16[4,128,128]{2,1,0:T(8,128)(2,1)S(1)}, bf16[4,128,128]{2,1,0:T(8,128)(2,1)}, u32[]{:S(2)}) copy-start(bf16[4,128,128]{2,1,0:T(8,128)(2,1)} %param.19) | copy-start | bytes 393220
  16.9 5.4 %collective-permute-start.5 = (bf16[1,4,128,128]{3,2,1,0:T(8,128)(2,1)S(1)}, bf16[1,4,128,128]{3,2,1,0:T(8,128)(2,1)S(1)}, u32[]{:S(2)}, u32[]{:S(2)}) collective-permute-start(bf16[1,4,128,128]{3,2,1,0:T(8,128)(2,1)S(1)} %bitcast.328), channel_id=1, source_target_pairs={{0,2},{1,3},{2,0},{3,1},{4,6},{5,7},{6,4},{7,5},{8,10},{9,11},{10,... | collective-permute-start | bytes 393224 | tf_op jit(solution)/shard_map/ppermute | solution.py:33
  18.5 10.1 %collective-permute-start.3 = (bf16[4,4,128,128]{3,2,1,0:T(8,128)(2,1)S(1)}, bf16[4,4,128,128]{3,2,1,0:T(8,128)(2,1)S(1)}, u32[]{:S(2)}, u32[]{:S(2)}) collective-permute-start(bf16[4,4,128,128]{3,2,1,0:T(8,128)(2,1)S(1)} %pad_maximum_fusion.3), channel_id=1, source_target_pairs={{0,1},{1,0},{2,3},{3,2},{4,5},{5,4},{6,7},{7,6},{8,9},{9,8},{10,11... | collective-permute-start | bytes 1572872 | tf_op jit(solution)/shard_map/ppermute | solution.py:33
  18.5 9.1 %collective-permute-start.6 = (bf16[2,4,128,128]{3,2,1,0:T(8,128)(2,1)S(1)}, bf16[2,4,128,128]{3,2,1,0:T(8,128)(2,1)S(1)}, u32[]{:S(2)}, u32[]{:S(2)}) collective-permute-start(bf16[2,4,128,128]{3,2,1,0:T(8,128)(2,1)S(1)} %pad_maximum_fusion.4), channel_id=1, source_target_pairs={{0,2},{1,3},{2,0},{3,1},{4,6},{5,7},{6,4},{7,5},{8,10},{9,11},{10,... | collective-permute-start | bytes 786440 | tf_op jit(solution)/shard_map/ppermute | solution.py:33
  19.3 10.5 %collective-permute-start.7 = (bf16[1,4,128,128]{3,2,1,0:T(8,128)(2,1)S(1)}, bf16[1,4,128,128]{3,2,1,0:T(8,128)(2,1)S(1)}, u32[]{:S(2)}, u32[]{:S(2)}) collective-permute-start(bf16[1,4,128,128]{3,2,1,0:T(8,128)(2,1)S(1)} %collective-permute-done.4), channel_id=1, source_target_pairs={{0,1},{1,0},{2,3},{3,2},{4,5},{5,4},{6,7},{7,6},{8,9},{9,8},{10,11... | collective-permute-start | bytes 393224 | tf_op jit(solution)/shard_map/ppermute | solution.py:33
  22.3 1.3 %collective-permute-start.8 = (bf16[1,4,128,128]{3,2,1,0:T(8,128)(2,1)S(1)}, bf16[1,4,128,128]{3,2,1,0:T(8,128)(2,1)S(1)}, u32[]{:S(2)}, u32[]{:S(2)}) collective-permute-start(bf16[1,4,128,128]{3,2,1,0:T(8,128)(2,1)S(1)} %collective-permute-done.5), channel_id=1, source_target_pairs={{0,1},{1,0},{2,3},{3,2},{4,5},{5,4},{6,7},{7,6},{8,9},{9,8},{10,11... | collective-permute-start | bytes 393224 | tf_op jit(solution)/shard_map/ppermute | solution.py:33
  27.5 2.0 %collective-permute-start.9 = (bf16[2,4,128,128]{3,2,1,0:T(8,128)(2,1)S(1)}, bf16[2,4,128,128]{3,2,1,0:T(8,128)(2,1)S(1)}, u32[]{:S(2)}, u32[]{:S(2)}) collective-permute-start(bf16[2,4,128,128]{3,2,1,0:T(8,128)(2,1)S(1)} %collective-permute-done.6), channel_id=1, source_target_pairs={{0,1},{1,0},{2,3},{3,2},{4,5},{5,4},{6,7},{7,6},{8,9},{9,8},{10,11... | collective-permute-start | bytes 786440 | tf_op jit(solution)/shard_map/ppermute | solution.py:33
  29.5 0.9 %copy-start.2 = (f32[3,128,128]{2,1,0:T(8,128)S(1)}, f32[3,128,128]{2,1,0:T(8,128)}, u32[]{:S(2)}) copy-start(f32[3,128,128]{2,1,0:T(8,128)} %param.20) | copy-start | bytes 589828
  29.8 0.9 %copy-start.1 = (f32[1,128,128]{2,1,0:T(8,128)S(1)}, f32[1,128,128]{2,1,0:T(8,128)}, u32[]{:S(2)}) copy-start(f32[1,128,128]{2,1,0:T(8,128)} %param.21) | copy-start | bytes 196612
  30.9 6.9 %collective-permute-start.10 = (bf16[128,128]{1,0:T(8,128)(2,1)S(1)}, bf16[128,128]{1,0:T(8,128)(2,1)S(1)}, u32[]{:S(2)}, u32[]{:S(2)}) collective-permute-start(bf16[128,128]{1,0:T(8,128)(2,1)S(1)} %get-tuple-element.21), channel_id=1, source_target_pairs={{0,4},{1,5},{2,6},{3,7},{4,8},{5,9},{6,10},{7,11},{8,12},{9,13},{1... | collective-permute-start | bytes 98312 | tf_op jit(solution)/shard_map/ppermute | solution.py:26
  31.7 6.2 %collective-permute-start.11 = (bf16[128,128]{1,0:T(8,128)(2,1)S(1)}, bf16[128,128]{1,0:T(8,128)(2,1)S(1)}, u32[]{:S(2)}, u32[]{:S(2)}) collective-permute-start(bf16[128,128]{1,0:T(8,128)(2,1)S(1)} %get-tuple-element.21), channel_id=1, source_target_pairs={{0,8},{1,9},{2,10},{3,11},{4,12},{5,13},{6,14},{7,15},{8,0},{9,1},... | collective-permute-start | bytes 98312 | tf_op jit(solution)/shard_map/ppermute | solution.py:26
  33.8 4.1 %collective-permute-start.12 = (bf16[128,128]{1,0:T(8,128)(2,1)S(1)}, bf16[128,128]{1,0:T(8,128)(2,1)S(1)}, u32[]{:S(2)}, u32[]{:S(2)}) collective-permute-start(bf16[128,128]{1,0:T(8,128)(2,1)S(1)} %get-tuple-element.21), channel_id=1, source_target_pairs={{0,12},{1,13},{2,14},{3,15},{4,0},{5,1},{6,2},{7,3},{8,4},{9,5},{1... | collective-permute-start | bytes 98312 | tf_op jit(solution)/shard_map/ppermute | solution.py:26
  34.8 4.6 %collective-permute-start.14 = (bf16[1,128,128]{2,1,0:T(8,128)(2,1)S(1)}, bf16[1,128,128]{2,1,0:T(8,128)(2,1)S(1)}, u32[]{:S(2)}, u32[]{:S(2)}) collective-permute-start(bf16[1,128,128]{2,1,0:T(8,128)(2,1)S(1)} %bitcast.330), channel_id=1, source_target_pairs={{0,2},{1,3},{2,0},{3,1},{4,6},{5,7},{6,4},{7,5},{8,10},{9,11},{10,... | collective-permute-start | bytes 98312 | tf_op jit(solution)/shard_map/ppermute | solution.py:33
  38.0 4.7 %collective-permute-start.15 = (bf16[3,128,128]{2,1,0:T(8,128)(2,1)S(1)}, bf16[3,128,128]{2,1,0:T(8,128)(2,1)S(1)}, u32[]{:S(2)}, u32[]{:S(2)}) collective-permute-start(bf16[3,128,128]{2,1,0:T(8,128)(2,1)S(1)} %pad_maximum_fusion.7), channel_id=1, source_target_pairs={{0,2},{1,3},{2,0},{3,1},{4,6},{5,7},{6,4},{7,5},{8,10},{9,11},{10,... | collective-permute-start | bytes 294920 | tf_op jit(solution)/shard_map/ppermute | solution.py:33
  39.4 3.3 %collective-permute-start.13 = (bf16[4,128,128]{2,1,0:T(8,128)(2,1)S(1)}, bf16[4,128,128]{2,1,0:T(8,128)(2,1)S(1)}, u32[]{:S(2)}, u32[]{:S(2)}) collective-permute-start(bf16[4,128,128]{2,1,0:T(8,128)(2,1)S(1)} %pad_maximum_fusion.5), channel_id=1, source_target_pairs={{0,1},{1,0},{2,3},{3,2},{4,5},{5,4},{6,7},{7,6},{8,9},{9,8},{10,11... | collective-permute-start | bytes 393224 | tf_op jit(solution)/shard_map/ppermute | solution.py:33
  39.4 3.3 %collective-permute-start.16 = (bf16[1,128,128]{2,1,0:T(8,128)(2,1)S(1)}, bf16[1,128,128]{2,1,0:T(8,128)(2,1)S(1)}, u32[]{:S(2)}, u32[]{:S(2)}) collective-permute-start(bf16[1,128,128]{2,1,0:T(8,128)(2,1)S(1)} %collective-permute-done.14), channel_id=1, source_target_pairs={{0,1},{1,0},{2,3},{3,2},{4,5},{5,4},{6,7},{7,6},{8,9},{9,8},{10,11... | collective-permute-start | bytes 98312 | tf_op jit(solution)/shard_map/ppermute | solution.py:33
  42.7 1.3 %collective-permute-start.17 = (bf16[3,128,128]{2,1,0:T(8,128)(2,1)S(1)}, bf16[3,128,128]{2,1,0:T(8,128)(2,1)S(1)}, u32[]{:S(2)}, u32[]{:S(2)}) collective-permute-start(bf16[3,128,128]{2,1,0:T(8,128)(2,1)S(1)} %collective-permute-done.15), channel_id=1, source_target_pairs={{0,1},{1,0},{2,3},{3,2},{4,5},{5,4},{6,7},{7,6},{8,9},{9,8},{10,11... | collective-permute-start | bytes 294920 | tf_op jit(solution)/shard_map/ppermute | solution.py:33
  44.9 5.5 %copy-start.3 = (f32[3,128,128]{2,1,0:T(8,128)}, f32[3,128,128]{2,1,0:T(8,128)S(1)}, u32[]{:S(2)}) copy-start(f32[3,128,128]{2,1,0:T(8,128)S(1)} %get-tuple-element.29) | copy-start | bytes 589828
  44.9 6.1 %collective-permute-start.18 = (bf16[128,128]{1,0:T(8,128)(2,1)S(1)}, bf16[128,128]{1,0:T(8,128)(2,1)S(1)}, u32[]{:S(2)}, u32[]{:S(2)}) collective-permute-start(bf16[128,128]{1,0:T(8,128)(2,1)S(1)} %get-tuple-element.19), channel_id=1, source_target_pairs={{0,4},{1,5},{2,6},{3,7},{4,8},{5,9},{6,10},{7,11},{8,12},{9,13},{1... | collective-permute-start | bytes 98312 | tf_op jit(solution)/shard_map/ppermute | solution.py:26
  46.3 5.7 %collective-permute-start.19 = (bf16[128,128]{1,0:T(8,128)(2,1)S(1)}, bf16[128,128]{1,0:T(8,128)(2,1)S(1)}, u32[]{:S(2)}, u32[]{:S(2)}) collective-permute-start(bf16[128,128]{1,0:T(8,128)(2,1)S(1)} %get-tuple-element.19), channel_id=1, source_target_pairs={{0,8},{1,9},{2,10},{3,11},{4,12},{5,13},{6,14},{7,15},{8,0},{9,1},... | collective-permute-start | bytes 98312 | tf_op jit(solution)/shard_map/ppermute | solution.py:26
  48.1 4.1 %collective-permute-start.20 = (bf16[128,128]{1,0:T(8,128)(2,1)S(1)}, bf16[128,128]{1,0:T(8,128)(2,1)S(1)}, u32[]{:S(2)}, u32[]{:S(2)}) collective-permute-start(bf16[128,128]{1,0:T(8,128)(2,1)S(1)} %get-tuple-element.19), channel_id=1, source_target_pairs={{0,12},{1,13},{2,14},{3,15},{4,0},{5,1},{6,2},{7,3},{8,4},{9,5},{1... | collective-permute-start | bytes 98312 | tf_op jit(solution)/shard_map/ppermute | solution.py:26
  50.4 4.3 %collective-permute-start.22 = (bf16[1,128,128]{2,1,0:T(8,128)(2,1)S(1)}, bf16[1,128,128]{2,1,0:T(8,128)(2,1)S(1)}, u32[]{:S(2)}, u32[]{:S(2)}) collective-permute-start(bf16[1,128,128]{2,1,0:T(8,128)(2,1)S(1)} %bitcast.322), channel_id=1, source_target_pairs={{0,2},{1,3},{2,0},{3,1},{4,6},{5,7},{6,4},{7,5},{8,10},{9,11},{10,... | collective-permute-start | bytes 98312 | tf_op jit(solution)/shard_map/ppermute | solution.py:33
  52.2 4.7 %collective-permute-start.23 = (bf16[3,128,128]{2,1,0:T(8,128)(2,1)S(1)}, bf16[3,128,128]{2,1,0:T(8,128)(2,1)S(1)}, u32[]{:S(2)}, u32[]{:S(2)}) collective-permute-start(bf16[3,128,128]{2,1,0:T(8,128)(2,1)S(1)} %pad_maximum_fusion.8), channel_id=1, source_target_pairs={{0,2},{1,3},{2,0},{3,1},{4,6},{5,7},{6,4},{7,5},{8,10},{9,11},{10,... | collective-permute-start | bytes 294920 | tf_op jit(solution)/shard_map/ppermute | solution.py:33
  53.7 3.2 %collective-permute-start.21 = (bf16[4,128,128]{2,1,0:T(8,128)(2,1)S(1)}, bf16[4,128,128]{2,1,0:T(8,128)(2,1)S(1)}, u32[]{:S(2)}, u32[]{:S(2)}) collective-permute-start(bf16[4,128,128]{2,1,0:T(8,128)(2,1)S(1)} %pad_maximum_fusion.6), channel_id=1, source_target_pairs={{0,1},{1,0},{2,3},{3,2},{4,5},{5,4},{6,7},{7,6},{8,9},{9,8},{10,11... | collective-permute-start | bytes 393224 | tf_op jit(solution)/shard_map/ppermute | solution.py:33
  54.7 2.3 %collective-permute-start.24 = (bf16[1,128,128]{2,1,0:T(8,128)(2,1)S(1)}, bf16[1,128,128]{2,1,0:T(8,128)(2,1)S(1)}, u32[]{:S(2)}, u32[]{:S(2)}) collective-permute-start(bf16[1,128,128]{2,1,0:T(8,128)(2,1)S(1)} %collective-permute-done.22), channel_id=1, source_target_pairs={{0,1},{1,0},{2,3},{3,2},{4,5},{5,4},{6,7},{7,6},{8,9},{9,8},{10,11... | collective-permute-start | bytes 98312 | tf_op jit(solution)/shard_map/ppermute | solution.py:33
  56.9 1.3 %collective-permute-start.25 = (bf16[3,128,128]{2,1,0:T(8,128)(2,1)S(1)}, bf16[3,128,128]{2,1,0:T(8,128)(2,1)S(1)}, u32[]{:S(2)}, u32[]{:S(2)}) collective-permute-start(bf16[3,128,128]{2,1,0:T(8,128)(2,1)S(1)} %collective-permute-done.23), channel_id=1, source_target_pairs={{0,1},{1,0},{2,3},{3,2},{4,5},{5,4},{6,7},{7,6},{8,9},{9,8},{10,11... | collective-permute-start | bytes 294920 | tf_op jit(solution)/shard_map/ppermute | solution.py:33

commit v16 on v14

--- a/solution.py
+++ b/solution.py
@@ -40,7 +40,7 @@
     if early and len(parts) > 1:
         across = [swap(parts[0], wide, 2)]
         if split and len(parts) > 2:
-            chunks = [parts[1], jnp.concatenate(parts[2:])]
+            chunks = parts[1:]
         else:
             chunks = [jnp.concatenate(parts[1:])]
         across += [swap(chunk, wide, 2) for chunk in chunks]

time: 59.8 us -> 62.8 us (1.050)
  starting transfers between devices: 28 us -> 31.7 us
  waiting for transfers between devices: 15.1 us -> 13.9 us
  matrix products: 8.03 us -> 9.06 us
    ppermute x9, starting transfers between devices: 16.9 us -> 18.9 us  [line_stage(): parts.append(lax.ppermute(x, 'wide', pairs)[None])]
    ppermute x17 -> x19, starting transfers between devices: 11.1 us -> 12.8 us  [swap(): return lax.ppermute(x, 'wide', [(d, d ^ mask) for d in range(wide)])]
    ppermute x17 -> x19, waiting for transfers between devices: 14.2 us -> 13.1 us  [swap(): return lax.ppermute(x, 'wide', [(d, d ^ mask) for d in range(wide)])]
    dot_general x27 -> x33, matrix products: 7.16 us -> 8.19 us  [rowwise(): return jnp.einsum(spec, tiles, currents, preferred_element_type=jnp.float32)]
  transfers between devices with their start and end apart: 26 -> 28, of which waited for: 9 -> 10; matrix products, arithmetic and copies ran while one was open for 20% -> 21% of each run, Pallas kernels for 0% -> 0%
where the time goes in v16:
time: 62.8 us; the launch traced here: 62.7 us
  starting transfers between devices  31.7 us (50%)
  waiting for transfers between devices  13.9 us (22%)
  matrix products  9.06 us (14%)
  other arithmetic  3.78 us (6%)
  local copies, waits for them, and re-layouts  3.69 us (6%)
    ppermute x9, starting transfers between devices, line_stage(): parts.append(lax.ppermute(x, 'wide', pairs)[None])  18.9 us
    ppermute x19, waiting for transfers between devices, swap(): return lax.ppermute(x, 'wide', [(d, d ^ mask) for d in range(wide)])  13.1 us
    ppermute x19, starting transfers between devices, swap(): return lax.ppermute(x, 'wide', [(d, d ^ mask) for d in range(wide)])  12.8 us
    dot_general x33, matrix products, rowwise(): return jnp.einsum(spec, tiles, currents, preferred_element_type=jnp.float32)  8.19 us
    sort x1, other arithmetic, per_device(): column_of_block = jnp.argsort(block_owner)  1.9 us
  transfers between devices with their start and end apart: 28, of which 10 were waited for; matrix products, arithmetic and copies ran while one was open for 21% of the time, Pallas kernels for 0%

profile of v16, /device:TPU:0, one launch (start us, length us, event | category | flops | bytes accessed | tf_op | source)
XLA Modules:
  0.0 62.7 jit_solution(4954771910959179825)
XLA Ops:
  0.0 3.0 %collective-permute-start = (bf16[4,128,128]{2,1,0:T(8,128)(2,1)}, bf16[4,128,128]{2,1,0:T(8,128)(2,1)S(1)}, u32[]{:S(2)}, u32[]{:S(2)}) collective-permute-start(bf16[4,128,128]{2,1,0:T(8,128)(2,1)} %param.19), channel_id=1, source_target_pairs={{0,4},{1,5},{2,6},{3,7},{4,8},{5,9},{6,10},{7,11},{8,12},{9,13},{1... | collective-permute-start | bytes 393224 | tf_op jit(solution)/shard_map/ppermute | solution.py:26
  3.0 2.6 %collective-permute-start.1 = (bf16[4,128,128]{2,1,0:T(8,128)(2,1)}, bf16[4,128,128]{2,1,0:T(8,128)(2,1)S(1)}, u32[]{:S(2)}, u32[]{:S(2)}) collective-permute-start(bf16[4,128,128]{2,1,0:T(8,128)(2,1)} %param.19), channel_id=1, source_target_pairs={{0,8},{1,9},{2,10},{3,11},{4,12},{5,13},{6,14},{7,15},{8,0},{9,1},... | collective-permute-start | bytes 393224 | tf_op jit(solution)/shard_map/ppermute | solution.py:26
  5.6 1.3 %collective-permute-start.2 = (bf16[4,128,128]{2,1,0:T(8,128)(2,1)}, bf16[4,128,128]{2,1,0:T(8,128)(2,1)S(1)}, u32[]{:S(2)}, u32[]{:S(2)}) collective-permute-start(bf16[4,128,128]{2,1,0:T(8,128)(2,1)} %param.19), channel_id=1, source_target_pairs={{0,12},{1,13},{2,14},{3,15},{4,0},{5,1},{6,2},{7,3},{8,4},{9,5},{1... | collective-permute-start | bytes 393224 | tf_op jit(solution)/shard_map/ppermute | solution.py:26
  7.0 1.5 %collective-permute-start.4 = (bf16[1,4,128,128]{3,2,1,0:T(8,128)(2,1)}, bf16[1,4,128,128]{3,2,1,0:T(8,128)(2,1)S(1)}, u32[]{:S(2)}, u32[]{:S(2)}) collective-permute-start(bf16[1,4,128,128]{3,2,1,0:T(8,128)(2,1)} %bitcast.398), channel_id=1, source_target_pairs={{0,2},{1,3},{2,0},{3,1},{4,6},{5,7},{6,4},{7,5},{8,10},{9,11},{10,... | collective-permute-start | bytes 393224 | tf_op jit(solution)/shard_map/ppermute | solution.py:33
  8.7 1.9 %sort.17 = (s32[16]{0:T(128)}, s32[16]{0:T(128)S(1)}) sort(s32[16]{0:T(128)} %param.18, s32[16]{0:T(128)S(1)} %iota.5), dimensions={0}, to_apply=%region_0.0 | sort | flops 64 | bytes 256 | tf_op jit(solution)/shard_map/jit(argsort)/sort | solution.py:94
  10.6 0.7 %gather_fusion = s32[16]{0:T(128)S(1)} fusion(s32[16]{0:T(128)S(1)} %get-tuple-element.8, s32[1024]{0:T(1024)S(1)} %pad_clamp_fusion.1), kind=kCustom, calls=%fused_computation.clone | custom fusion | bytes 192 | tf_op jit(solution)/shard_map/jit(_take)/gather | solution.py:69
  11.3 0.8 %copy.17 = s32[16,2]{1,0:T(8,128)S(1)} copy(s32[16,2]{0,1:T(2,128)} %bitcast.414) | data formatting | bytes 256 | tf_op jit(solution)/shard_map/squeeze | solution.py:71
  12.0 0.7 %gather_fusion.2 = bf16[16,2,128,128]{3,2,1,0:T(8,128)(2,1)S(1)} fusion(bf16[16,2,128,128]{3,2,1,0:T(8,128)(2,1)S(1)} %bitcast.383, s32[1024]{0:T(1024)S(1)} %pad_clamp_fusion), kind=kCustom, calls=%fused_computation.2.clone | custom fusion | bytes 2097216 | tf_op jit(solution)/shard_map/jit(_take)/gather | solution.py:70
  12.8 0.6 gather_fusion.1
  13.9 0.3 bitcast_select_fusion.3
  14.3 0.6 collective-permute-start.7
  14.9 1.5 %collective-permute-start.6 = (bf16[1,4,128,128]{3,2,1,0:T(8,128)(2,1)S(1)}, bf16[1,4,128,128]{3,2,1,0:T(8,128)(2,1)S(1)}, u32[]{:S(2)}, u32[]{:S(2)}) collective-permute-start(bf16[1,4,128,128]{3,2,1,0:T(8,128)(2,1)S(1)} %bitcast.404), channel_id=1, source_target_pairs={{0,2},{1,3},{2,0},{3,1},{4,6},{5,7},{6,4},{7,5},{8,10},{9,11},{10,... | collective-permute-start | bytes 393224 | tf_op jit(solution)/shard_map/ppermute | solution.py:33
  16.5 0.6 collective-permute-start.5
  17.1 0.3 convolution_bitcast_fusion.3
  17.4 0.6 collective-permute-start.8
  18.3 2.6 %collective-permute-done.7 = bf16[1,4,128,128]{3,2,1,0:T(8,128)(2,1)S(1)} collective-permute-done((bf16[1,4,128,128]{3,2,1,0:T(8,128)(2,1)S(1)}, bf16[1,4,128,128]{3,2,1,0:T(8,128)(2,1)S(1)}, u32[]{:S(2)}, u32[]{:S(2)}) %collective-permute-start.7) | collective-permute-done | bytes 131104 | tf_op jit(solution)/shard_map/ppermute | solution.py:33
  21.3 1.5 %collective-permute-done.6 = bf16[1,4,128,128]{3,2,1,0:T(8,128)(2,1)S(1)} collective-permute-done((bf16[1,4,128,128]{3,2,1,0:T(8,128)(2,1)S(1)}, bf16[1,4,128,128]{3,2,1,0:T(8,128)(2,1)S(1)}, u32[]{:S(2)}, u32[]{:S(2)}) %collective-permute-start.6) | collective-permute-done | bytes 131104 | tf_op jit(solution)/shard_map/ppermute | solution.py:33
  23.1 1.0 %collective-permute-done.5 = bf16[1,4,128,128]{3,2,1,0:T(8,128)(2,1)S(1)} collective-permute-done((bf16[1,4,128,128]{3,2,1,0:T(8,128)(2,1)S(1)}, bf16[1,4,128,128]{3,2,1,0:T(8,128)(2,1)S(1)}, u32[]{:S(2)}, u32[]{:S(2)}) %collective-permute-start.5) | collective-permute-done | bytes 131104 | tf_op jit(solution)/shard_map/ppermute | solution.py:33
  25.1 0.6 collective-permute-start.9
  26.6 0.4 collective-permute-done.10
  28.6 0.3 convolution_bitcast_fusion
  28.9 0.4 fusion.32
  29.5 0.7 %copy-done.2 = f32[3,128,128]{2,1,0:T(8,128)S(1)} copy-done((f32[3,128,128]{2,1,0:T(8,128)S(1)}, f32[3,128,128]{2,1,0:T(8,128)}, u32[]{:S(2)}) %copy-start.2) | copy-done | bytes 196632
  30.5 0.3 constant_dynamic-update-slice_fusion.8
  30.7 4.7 %collective-permute-start.12 = (bf16[128,128]{1,0:T(8,128)(2,1)S(1)}, bf16[128,128]{1,0:T(8,128)(2,1)S(1)}, u32[]{:S(2)}, u32[]{:S(2)}) collective-permute-start(bf16[128,128]{1,0:T(8,128)(2,1)S(1)} %get-tuple-element.21), channel_id=1, source_target_pairs={{0,4},{1,5},{2,6},{3,7},{4,8},{5,9},{6,10},{7,11},{8,12},{9,13},{1... | collective-permute-start | bytes 98312 | tf_op jit(solution)/shard_map/ppermute | solution.py:26
  35.5 2.4 %collective-permute-start.14 = (bf16[128,128]{1,0:T(8,128)(2,1)S(1)}, bf16[128,128]{1,0:T(8,128)(2,1)S(1)}, u32[]{:S(2)}, u32[]{:S(2)}) collective-permute-start(bf16[128,128]{1,0:T(8,128)(2,1)S(1)} %get-tuple-element.21), channel_id=1, source_target_pairs={{0,12},{1,13},{2,14},{3,15},{4,0},{5,1},{6,2},{7,3},{8,4},{9,5},{1... | collective-permute-start | bytes 98312 | tf_op jit(solution)/shard_map/ppermute | solution.py:26
  37.9 1.5 %collective-permute-start.16 = (bf16[1,128,128]{2,1,0:T(8,128)(2,1)S(1)}, bf16[1,128,128]{2,1,0:T(8,128)(2,1)S(1)}, u32[]{:S(2)}, u32[]{:S(2)}) collective-permute-start(bf16[1,128,128]{2,1,0:T(8,128)(2,1)S(1)} %bitcast.410), channel_id=1, source_target_pairs={{0,2},{1,3},{2,0},{3,1},{4,6},{5,7},{6,4},{7,5},{8,10},{9,11},{10,... | collective-permute-start | bytes 98312 | tf_op jit(solution)/shard_map/ppermute | solution.py:33
  39.4 0.3 fusion.30
  39.7 0.3 fusion.31
  40.5 1.5 %collective-permute-start.17 = (bf16[3,128,128]{2,1,0:T(8,128)(2,1)S(1)}, bf16[3,128,128]{2,1,0:T(8,128)(2,1)S(1)}, u32[]{:S(2)}, u32[]{:S(2)}) collective-permute-start(bf16[3,128,128]{2,1,0:T(8,128)(2,1)S(1)} %pad_maximum_fusion.13), channel_id=1, source_target_pairs={{0,2},{1,3},{2,0},{3,1},{4,6},{5,7},{6,4},{7,5},{8,10},{9,11},{10,... | collective-permute-start | bytes 294920 | tf_op jit(solution)/shard_map/ppermute | solution.py:33
  42.1 0.6 collective-permute-start.18
  42.7 2.5 %collective-permute-done.17 = bf16[3,128,128]{2,1,0:T(8,128)(2,1)S(1)} collective-permute-done((bf16[3,128,128]{2,1,0:T(8,128)(2,1)S(1)}, bf16[3,128,128]{2,1,0:T(8,128)(2,1)S(1)}, u32[]{:S(2)}, u32[]{:S(2)}) %collective-permute-start.17) | collective-permute-done | bytes 98336 | tf_op jit(solution)/shard_map/ppermute | solution.py:33
  45.3 1.2 %collective-permute-done.19 = bf16[3,128,128]{2,1,0:T(8,128)(2,1)S(1)} collective-permute-done((bf16[3,128,128]{2,1,0:T(8,128)(2,1)S(1)}, bf16[3,128,128]{2,1,0:T(8,128)(2,1)S(1)}, u32[]{:S(2)}, u32[]{:S(2)}) %collective-permute-start.19) | collective-permute-done | bytes 98336 | tf_op jit(solution)/shard_map/ppermute | solution.py:33
  46.5 0.3 convolution_bitcast_fusion.9
  47.1 0.3 constant_dynamic-update-slice_fusion.17
  47.4 0.9 %collective-permute-start.20 = (bf16[128,128]{1,0:T(8,128)(2,1)S(1)}, bf16[128,128]{1,0:T(8,128)(2,1)S(1)}, u32[]{:S(2)}, u32[]{:S(2)}) collective-permute-start(bf16[128,128]{1,0:T(8,128)(2,1)S(1)} %get-tuple-element.19), channel_id=1, source_target_pairs={{0,4},{1,5},{2,6},{3,7},{4,8},{5,9},{6,10},{7,11},{8,12},{9,13},{1... | collective-permute-start | bytes 98312 | tf_op jit(solution)/shard_map/ppermute | solution.py:26
  48.3 2.9 %collective-permute-start.21 = (bf16[128,128]{1,0:T(8,128)(2,1)S(1)}, bf16[128,128]{1,0:T(8,128)(2,1)S(1)}, u32[]{:S(2)}, u32[]{:S(2)}) collective-permute-start(bf16[128,128]{1,0:T(8,128)(2,1)S(1)} %get-tuple-element.19), channel_id=1, source_target_pairs={{0,8},{1,9},{2,10},{3,11},{4,12},{5,13},{6,14},{7,15},{8,0},{9,1},... | collective-permute-start | bytes 98312 | tf_op jit(solution)/shard_map/ppermute | solution.py:26
  51.2 1.0 %collective-permute-start.22 = (bf16[128,128]{1,0:T(8,128)(2,1)S(1)}, bf16[128,128]{1,0:T(8,128)(2,1)S(1)}, u32[]{:S(2)}, u32[]{:S(2)}) collective-permute-start(bf16[128,128]{1,0:T(8,128)(2,1)S(1)} %get-tuple-element.19), channel_id=1, source_target_pairs={{0,12},{1,13},{2,14},{3,15},{4,0},{5,1},{6,2},{7,3},{8,4},{9,5},{1... | collective-permute-start | bytes 98312 | tf_op jit(solution)/shard_map/ppermute | solution.py:26
  52.2 0.5 convolution_bitcast_fusion.7
  52.7 1.6 %collective-permute-start.24 = (bf16[1,128,128]{2,1,0:T(8,128)(2,1)S(1)}, bf16[1,128,128]{2,1,0:T(8,128)(2,1)S(1)}, u32[]{:S(2)}, u32[]{:S(2)}) collective-permute-start(bf16[1,128,128]{2,1,0:T(8,128)(2,1)S(1)} %bitcast.412), channel_id=1, source_target_pairs={{0,2},{1,3},{2,0},{3,1},{4,6},{5,7},{6,4},{7,5},{8,10},{9,11},{10,... | collective-permute-start | bytes 98312 | tf_op jit(solution)/shard_map/ppermute | solution.py:33
  54.3 0.8 %collective-permute-done.22 = bf16[128,128]{1,0:T(8,128)(2,1)S(1)} collective-permute-done((bf16[128,128]{1,0:T(8,128)(2,1)S(1)}, bf16[128,128]{1,0:T(8,128)(2,1)S(1)}, u32[]{:S(2)}, u32[]{:S(2)}) %collective-permute-start.22) | collective-permute-done | bytes 32800 | tf_op jit(solution)/shard_map/ppermute | solution.py:26
  55.1 1.6 %collective-permute-start.25 = (bf16[3,128,128]{2,1,0:T(8,128)(2,1)S(1)}, bf16[3,128,128]{2,1,0:T(8,128)(2,1)S(1)}, u32[]{:S(2)}, u32[]{:S(2)}) collective-permute-start(bf16[3,128,128]{2,1,0:T(8,128)(2,1)S(1)} %pad_maximum_fusion.14), channel_id=1, source_target_pairs={{0,2},{1,3},{2,0},{3,1},{4,6},{5,7},{6,4},{7,5},{8,10},{9,11},{10,... | collective-permute-start | bytes 294920 | tf_op jit(solution)/shard_map/ppermute | solution.py:33
  56.7 0.6 collective-permute-start.26
  57.3 2.5 %collective-permute-done.25 = bf16[3,128,128]{2,1,0:T(8,128)(2,1)S(1)} collective-permute-done((bf16[3,128,128]{2,1,0:T(8,128)(2,1)S(1)}, bf16[3,128,128]{2,1,0:T(8,128)(2,1)S(1)}, u32[]{:S(2)}, u32[]{:S(2)}) %collective-permute-start.25) | collective-permute-done | bytes 98336 | tf_op jit(solution)/shard_map/ppermute | solution.py:33
  59.9 1.2 %collective-permute-done.27 = bf16[3,128,128]{2,1,0:T(8,128)(2,1)S(1)} collective-permute-done((bf16[3,128,128]{2,1,0:T(8,128)(2,1)S(1)}, bf16[3,128,128]{2,1,0:T(8,128)(2,1)S(1)}, u32[]{:S(2)}, u32[]{:S(2)}) %collective-permute-start.27) | collective-permute-done | bytes 98336 | tf_op jit(solution)/shard_map/ppermute | solution.py:33
  61.1 0.3 convolution_bitcast_fusion.8
  61.7 0.3 convolution_bitcast_fusion.6
  62.0 0.7 %pad_maximum_fusion.10 = f32[3,128,128]{2,1,0:T(8,128)} fusion(f32[1,128,128]{2,1,0:T(8,128)S(1)} %bitcast.396, f32[1,128,128]{2,1,0:T(8,128)S(1)} %bitcast.397, f32[1,128,128]{2,1,0:T(8,128)S(1)} %convolution_bitcast_fusion.6), kind=kLoop, calls=%fused_computation.98 | loop fusion | flops 98304 | bytes 393216 | tf_op jit(solution)/shard_map/stack | solution.py:136
  (92 shorter events, 7.1 us)
Async XLA Ops:
  0.0 12.0 %copy-start = (bf16[1,16,2,128,128]{4,3,2,1,0:T(8,128)(2,1)S(1)}, bf16[1,16,2,128,128]{4,3,2,1,0:T(8,128)(2,1)}, u32[]{:S(2)}) copy-start(bf16[1,16,2,128,128]{4,3,2,1,0:T(8,128)(2,1)} %param.16) | copy-start | bytes 3145732
  0.0 16.4 %collective-permute-start = (bf16[4,128,128]{2,1,0:T(8,128)(2,1)}, bf16[4,128,128]{2,1,0:T(8,128)(2,1)S(1)}, u32[]{:S(2)}, u32[]{:S(2)}) collective-permute-start(bf16[4,128,128]{2,1,0:T(8,128)(2,1)} %param.19), channel_id=1, source_target_pairs={{0,4},{1,5},{2,6},{3,7},{4,8},{5,9},{6,10},{7,11},{8,12},{9,13},{1... | collective-permute-start | bytes 393224 | tf_op jit(solution)/shard_map/ppermute | solution.py:26
  3.0 11.9 %collective-permute-start.1 = (bf16[4,128,128]{2,1,0:T(8,128)(2,1)}, bf16[4,128,128]{2,1,0:T(8,128)(2,1)S(1)}, u32[]{:S(2)}, u32[]{:S(2)}) collective-permute-start(bf16[4,128,128]{2,1,0:T(8,128)(2,1)} %param.19), channel_id=1, source_target_pairs={{0,8},{1,9},{2,10},{3,11},{4,12},{5,13},{6,14},{7,15},{8,0},{9,1},... | collective-permute-start | bytes 393224 | tf_op jit(solution)/shard_map/ppermute | solution.py:26
  5.6 8.7 %collective-permute-start.2 = (bf16[4,128,128]{2,1,0:T(8,128)(2,1)}, bf16[4,128,128]{2,1,0:T(8,128)(2,1)S(1)}, u32[]{:S(2)}, u32[]{:S(2)}) collective-permute-start(bf16[4,128,128]{2,1,0:T(8,128)(2,1)} %param.19), channel_id=1, source_target_pairs={{0,12},{1,13},{2,14},{3,15},{4,0},{5,1},{6,2},{7,3},{8,4},{9,5},{1... | collective-permute-start | bytes 393224 | tf_op jit(solution)/shard_map/ppermute | solution.py:26
  7.0 10.4 %collective-permute-start.4 = (bf16[1,4,128,128]{3,2,1,0:T(8,128)(2,1)}, bf16[1,4,128,128]{3,2,1,0:T(8,128)(2,1)S(1)}, u32[]{:S(2)}, u32[]{:S(2)}) collective-permute-start(bf16[1,4,128,128]{3,2,1,0:T(8,128)(2,1)} %bitcast.398), channel_id=1, source_target_pairs={{0,2},{1,3},{2,0},{3,1},{4,6},{5,7},{6,4},{7,5},{8,10},{9,11},{10,... | collective-permute-start | bytes 393224 | tf_op jit(solution)/shard_map/ppermute | solution.py:33
  14.2 2.3 %copy-start.3 = (bf16[4,128,128]{2,1,0:T(8,128)(2,1)S(1)}, bf16[4,128,128]{2,1,0:T(8,128)(2,1)}, u32[]{:S(2)}) copy-start(bf16[4,128,128]{2,1,0:T(8,128)(2,1)} %param.19) | copy-start | bytes 393220
  14.3 6.5 %collective-permute-start.7 = (bf16[1,4,128,128]{3,2,1,0:T(8,128)(2,1)S(1)}, bf16[1,4,128,128]{3,2,1,0:T(8,128)(2,1)S(1)}, u32[]{:S(2)}, u32[]{:S(2)}) collective-permute-start(bf16[1,4,128,128]{3,2,1,0:T(8,128)(2,1)S(1)} %bitcast.407), channel_id=1, source_target_pairs={{0,2},{1,3},{2,0},{3,1},{4,6},{5,7},{6,4},{7,5},{8,10},{9,11},{10,... | collective-permute-start | bytes 393224 | tf_op jit(solution)/shard_map/ppermute | solution.py:33
  14.9 7.8 %collective-permute-start.6 = (bf16[1,4,128,128]{3,2,1,0:T(8,128)(2,1)S(1)}, bf16[1,4,128,128]{3,2,1,0:T(8,128)(2,1)S(1)}, u32[]{:S(2)}, u32[]{:S(2)}) collective-permute-start(bf16[1,4,128,128]{3,2,1,0:T(8,128)(2,1)S(1)} %bitcast.404), channel_id=1, source_target_pairs={{0,2},{1,3},{2,0},{3,1},{4,6},{5,7},{6,4},{7,5},{8,10},{9,11},{10,... | collective-permute-start | bytes 393224 | tf_op jit(solution)/shard_map/ppermute | solution.py:33
  16.5 7.6 %collective-permute-start.5 = (bf16[1,4,128,128]{3,2,1,0:T(8,128)(2,1)S(1)}, bf16[1,4,128,128]{3,2,1,0:T(8,128)(2,1)S(1)}, u32[]{:S(2)}, u32[]{:S(2)}) collective-permute-start(bf16[1,4,128,128]{3,2,1,0:T(8,128)(2,1)S(1)} %bitcast.402), channel_id=1, source_target_pairs={{0,2},{1,3},{2,0},{3,1},{4,6},{5,7},{6,4},{7,5},{8,10},{9,11},{10,... | collective-permute-start | bytes 393224 | tf_op jit(solution)/shard_map/ppermute | solution.py:33
  17.1 11.5 %collective-permute-start.3 = (bf16[4,4,128,128]{3,2,1,0:T(8,128)(2,1)S(1)}, bf16[4,4,128,128]{3,2,1,0:T(8,128)(2,1)S(1)}, u32[]{:S(2)}, u32[]{:S(2)}) collective-permute-start(bf16[4,4,128,128]{3,2,1,0:T(8,128)(2,1)S(1)} %pad_maximum_fusion.7), channel_id=1, source_target_pairs={{0,1},{1,0},{2,3},{3,2},{4,5},{5,4},{6,7},{7,6},{8,9},{9,8},{10,11... | collective-permute-start | bytes 1572872 | tf_op jit(solution)/shard_map/ppermute | solution.py:33
  17.4 12.1 %collective-permute-start.8 = (bf16[1,4,128,128]{3,2,1,0:T(8,128)(2,1)S(1)}, bf16[1,4,128,128]{3,2,1,0:T(8,128)(2,1)S(1)}, u32[]{:S(2)}, u32[]{:S(2)}) collective-permute-start(bf16[1,4,128,128]{3,2,1,0:T(8,128)(2,1)S(1)} %collective-permute-done.4), channel_id=1, source_target_pairs={{0,1},{1,0},{2,3},{3,2},{4,5},{5,4},{6,7},{7,6},{8,9},{9,8},{10,11... | collective-permute-start | bytes 393224 | tf_op jit(solution)/shard_map/ppermute | solution.py:33
  24.8 1.4 %collective-permute-start.11 = (bf16[1,4,128,128]{3,2,1,0:T(8,128)(2,1)S(1)}, bf16[1,4,128,128]{3,2,1,0:T(8,128)(2,1)S(1)}, u32[]{:S(2)}, u32[]{:S(2)}) collective-permute-start(bf16[1,4,128,128]{3,2,1,0:T(8,128)(2,1)S(1)} %collective-permute-done.7), channel_id=1, source_target_pairs={{0,1},{1,0},{2,3},{3,2},{4,5},{5,4},{6,7},{7,6},{8,9},{9,8},{10,11... | collective-permute-start | bytes 393224 | tf_op jit(solution)/shard_map/ppermute | solution.py:33
  25.1 2.3 %collective-permute-start.9 = (bf16[1,4,128,128]{3,2,1,0:T(8,128)(2,1)S(1)}, bf16[1,4,128,128]{3,2,1,0:T(8,128)(2,1)S(1)}, u32[]{:S(2)}, u32[]{:S(2)}) collective-permute-start(bf16[1,4,128,128]{3,2,1,0:T(8,128)(2,1)S(1)} %collective-permute-done.5), channel_id=1, source_target_pairs={{0,1},{1,0},{2,3},{3,2},{4,5},{5,4},{6,7},{7,6},{8,9},{9,8},{10,11... | collective-permute-start | bytes 393224 | tf_op jit(solution)/shard_map/ppermute | solution.py:33
  25.6 1.3 %collective-permute-start.10 = (bf16[1,4,128,128]{3,2,1,0:T(8,128)(2,1)S(1)}, bf16[1,4,128,128]{3,2,1,0:T(8,128)(2,1)S(1)}, u32[]{:S(2)}, u32[]{:S(2)}) collective-permute-start(bf16[1,4,128,128]{3,2,1,0:T(8,128)(2,1)S(1)} %collective-permute-done.6), channel_id=1, source_target_pairs={{0,1},{1,0},{2,3},{3,2},{4,5},{5,4},{6,7},{7,6},{8,9},{9,8},{10,11... | collective-permute-start | bytes 393224 | tf_op jit(solution)/shard_map/ppermute | solution.py:33
  29.3 0.9 %copy-start.2 = (f32[3,128,128]{2,1,0:T(8,128)S(1)}, f32[3,128,128]{2,1,0:T(8,128)}, u32[]{:S(2)}) copy-start(f32[3,128,128]{2,1,0:T(8,128)} %param.20) | copy-start | bytes 589828
  29.5 0.9 %copy-start.1 = (f32[1,128,128]{2,1,0:T(8,128)S(1)}, f32[1,128,128]{2,1,0:T(8,128)}, u32[]{:S(2)}) copy-start(f32[1,128,128]{2,1,0:T(8,128)} %param.21) | copy-start | bytes 196612
  30.7 9.7 %collective-permute-start.12 = (bf16[128,128]{1,0:T(8,128)(2,1)S(1)}, bf16[128,128]{1,0:T(8,128)(2,1)S(1)}, u32[]{:S(2)}, u32[]{:S(2)}) collective-permute-start(bf16[128,128]{1,0:T(8,128)(2,1)S(1)} %get-tuple-element.21), channel_id=1, source_target_pairs={{0,4},{1,5},{2,6},{3,7},{4,8},{5,9},{6,10},{7,11},{8,12},{9,13},{1... | collective-permute-start | bytes 98312 | tf_op jit(solution)/shard_map/ppermute | solution.py:26
  35.5 5.0 %collective-permute-start.13 = (bf16[128,128]{1,0:T(8,128)(2,1)S(1)}, bf16[128,128]{1,0:T(8,128)(2,1)S(1)}, u32[]{:S(2)}, u32[]{:S(2)}) collective-permute-start(bf16[128,128]{1,0:T(8,128)(2,1)S(1)} %get-tuple-element.21), channel_id=1, source_target_pairs={{0,8},{1,9},{2,10},{3,11},{4,12},{5,13},{6,14},{7,15},{8,0},{9,1},... | collective-permute-start | bytes 98312 | tf_op jit(solution)/shard_map/ppermute | solution.py:26
  35.5 5.0 %collective-permute-start.14 = (bf16[128,128]{1,0:T(8,128)(2,1)S(1)}, bf16[128,128]{1,0:T(8,128)(2,1)S(1)}, u32[]{:S(2)}, u32[]{:S(2)}) collective-permute-start(bf16[128,128]{1,0:T(8,128)(2,1)S(1)} %get-tuple-element.21), channel_id=1, source_target_pairs={{0,12},{1,13},{2,14},{3,15},{4,0},{5,1},{6,2},{7,3},{8,4},{9,5},{1... | collective-permute-start | bytes 98312 | tf_op jit(solution)/shard_map/ppermute | solution.py:26
  37.9 4.2 %collective-permute-start.16 = (bf16[1,128,128]{2,1,0:T(8,128)(2,1)S(1)}, bf16[1,128,128]{2,1,0:T(8,128)(2,1)S(1)}, u32[]{:S(2)}, u32[]{:S(2)}) collective-permute-start(bf16[1,128,128]{2,1,0:T(8,128)(2,1)S(1)} %bitcast.410), channel_id=1, source_target_pairs={{0,2},{1,3},{2,0},{3,1},{4,6},{5,7},{6,4},{7,5},{8,10},{9,11},{10,... | collective-permute-start | bytes 98312 | tf_op jit(solution)/shard_map/ppermute | solution.py:33
  40.5 4.7 %collective-permute-start.17 = (bf16[3,128,128]{2,1,0:T(8,128)(2,1)S(1)}, bf16[3,128,128]{2,1,0:T(8,128)(2,1)S(1)}, u32[]{:S(2)}, u32[]{:S(2)}) collective-permute-start(bf16[3,128,128]{2,1,0:T(8,128)(2,1)S(1)} %pad_maximum_fusion.13), channel_id=1, source_target_pairs={{0,2},{1,3},{2,0},{3,1},{4,6},{5,7},{6,4},{7,5},{8,10},{9,11},{10,... | collective-permute-start | bytes 294920 | tf_op jit(solution)/shard_map/ppermute | solution.py:33
  42.0 3.2 %collective-permute-start.15 = (bf16[4,128,128]{2,1,0:T(8,128)(2,1)S(1)}, bf16[4,128,128]{2,1,0:T(8,128)(2,1)S(1)}, u32[]{:S(2)}, u32[]{:S(2)}) collective-permute-start(bf16[4,128,128]{2,1,0:T(8,128)(2,1)S(1)} %pad_maximum_fusion.11), channel_id=1, source_target_pairs={{0,1},{1,0},{2,3},{3,2},{4,5},{5,4},{6,7},{7,6},{8,9},{9,8},{10,11... | collective-permute-start | bytes 393224 | tf_op jit(solution)/shard_map/ppermute | solution.py:33
  42.1 3.2 %collective-permute-start.18 = (bf16[1,128,128]{2,1,0:T(8,128)(2,1)S(1)}, bf16[1,128,128]{2,1,0:T(8,128)(2,1)S(1)}, u32[]{:S(2)}, u32[]{:S(2)}) collective-permute-start(bf16[1,128,128]{2,1,0:T(8,128)(2,1)S(1)} %collective-permute-done.16), channel_id=1, source_target_pairs={{0,1},{1,0},{2,3},{3,2},{4,5},{5,4},{6,7},{7,6},{8,9},{9,8},{10,11... | collective-permute-start | bytes 98312 | tf_op jit(solution)/shard_map/ppermute | solution.py:33
  45.2 1.3 %collective-permute-start.19 = (bf16[3,128,128]{2,1,0:T(8,128)(2,1)S(1)}, bf16[3,128,128]{2,1,0:T(8,128)(2,1)S(1)}, u32[]{:S(2)}, u32[]{:S(2)}) collective-permute-start(bf16[3,128,128]{2,1,0:T(8,128)(2,1)S(1)} %collective-permute-done.17), channel_id=1, source_target_pairs={{0,1},{1,0},{2,3},{3,2},{4,5},{5,4},{6,7},{7,6},{8,9},{9,8},{10,11... | collective-permute-start | bytes 294920 | tf_op jit(solution)/shard_map/ppermute | solution.py:33
  47.4 6.9 %collective-permute-start.20 = (bf16[128,128]{1,0:T(8,128)(2,1)S(1)}, bf16[128,128]{1,0:T(8,128)(2,1)S(1)}, u32[]{:S(2)}, u32[]{:S(2)}) collective-permute-start(bf16[128,128]{1,0:T(8,128)(2,1)S(1)} %get-tuple-element.19), channel_id=1, source_target_pairs={{0,4},{1,5},{2,6},{3,7},{4,8},{5,9},{6,10},{7,11},{8,12},{9,13},{1... | collective-permute-start | bytes 98312 | tf_op jit(solution)/shard_map/ppermute | solution.py:26
  48.3 6.0 %collective-permute-start.21 = (bf16[128,128]{1,0:T(8,128)(2,1)S(1)}, bf16[128,128]{1,0:T(8,128)(2,1)S(1)}, u32[]{:S(2)}, u32[]{:S(2)}) collective-permute-start(bf16[128,128]{1,0:T(8,128)(2,1)S(1)} %get-tuple-element.19), channel_id=1, source_target_pairs={{0,8},{1,9},{2,10},{3,11},{4,12},{5,13},{6,14},{7,15},{8,0},{9,1},... | collective-permute-start | bytes 98312 | tf_op jit(solution)/shard_map/ppermute | solution.py:26
  51.2 3.9 %collective-permute-start.22 = (bf16[128,128]{1,0:T(8,128)(2,1)S(1)}, bf16[128,128]{1,0:T(8,128)(2,1)S(1)}, u32[]{:S(2)}, u32[]{:S(2)}) collective-permute-start(bf16[128,128]{1,0:T(8,128)(2,1)S(1)} %get-tuple-element.19), channel_id=1, source_target_pairs={{0,12},{1,13},{2,14},{3,15},{4,0},{5,1},{6,2},{7,3},{8,4},{9,5},{1... | collective-permute-start | bytes 98312 | tf_op jit(solution)/shard_map/ppermute | solution.py:26
  52.7 4.0 %collective-permute-start.24 = (bf16[1,128,128]{2,1,0:T(8,128)(2,1)S(1)}, bf16[1,128,128]{2,1,0:T(8,128)(2,1)S(1)}, u32[]{:S(2)}, u32[]{:S(2)}) collective-permute-start(bf16[1,128,128]{2,1,0:T(8,128)(2,1)S(1)} %bitcast.412), channel_id=1, source_target_pairs={{0,2},{1,3},{2,0},{3,1},{4,6},{5,7},{6,4},{7,5},{8,10},{9,11},{10,... | collective-permute-start | bytes 98312 | tf_op jit(solution)/shard_map/ppermute | solution.py:33
  55.1 4.7 %collective-permute-start.25 = (bf16[3,128,128]{2,1,0:T(8,128)(2,1)S(1)}, bf16[3,128,128]{2,1,0:T(8,128)(2,1)S(1)}, u32[]{:S(2)}, u32[]{:S(2)}) collective-permute-start(bf16[3,128,128]{2,1,0:T(8,128)(2,1)S(1)} %pad_maximum_fusion.14), channel_id=1, source_target_pairs={{0,2},{1,3},{2,0},{3,1},{4,6},{5,7},{6,4},{7,5},{8,10},{9,11},{10,... | collective-permute-start | bytes 294920 | tf_op jit(solution)/shard_map/ppermute | solution.py:33
  56.7 3.1 %collective-permute-start.23 = (bf16[4,128,128]{2,1,0:T(8,128)(2,1)S(1)}, bf16[4,128,128]{2,1,0:T(8,128)(2,1)S(1)}, u32[]{:S(2)}, u32[]{:S(2)}) collective-permute-start(bf16[4,128,128]{2,1,0:T(8,128)(2,1)S(1)} %pad_maximum_fusion.12), channel_id=1, source_target_pairs={{0,1},{1,0},{2,3},{3,2},{4,5},{5,4},{6,7},{7,6},{8,9},{9,8},{10,11... | collective-permute-start | bytes 393224 | tf_op jit(solution)/shard_map/ppermute | solution.py:33
  56.7 3.1 %collective-permute-start.26 = (bf16[1,128,128]{2,1,0:T(8,128)(2,1)S(1)}, bf16[1,128,128]{2,1,0:T(8,128)(2,1)S(1)}, u32[]{:S(2)}, u32[]{:S(2)}) collective-permute-start(bf16[1,128,128]{2,1,0:T(8,128)(2,1)S(1)} %collective-permute-done.24), channel_id=1, source_target_pairs={{0,1},{1,0},{2,3},{3,2},{4,5},{5,4},{6,7},{7,6},{8,9},{9,8},{10,11... | collective-permute-start | bytes 98312 | tf_op jit(solution)/shard_map/ppermute | solution.py:33
  59.8 1.3 %collective-permute-start.27 = (bf16[3,128,128]{2,1,0:T(8,128)(2,1)S(1)}, bf16[3,128,128]{2,1,0:T(8,128)(2,1)S(1)}, u32[]{:S(2)}, u32[]{:S(2)}) collective-permute-start(bf16[3,128,128]{2,1,0:T(8,128)(2,1)S(1)} %collective-permute-done.25), channel_id=1, source_target_pairs={{0,1},{1,0},{2,3},{3,2},{4,5},{5,4},{6,7},{7,6},{8,9},{9,8},{10,11... | collective-permute-start | bytes 294920 | tf_op jit(solution)/shard_map/ppermute | solution.py:33

commit v17 on v14

--- a/solution.py
+++ b/solution.py
@@ -44,7 +44,12 @@
         else:
             chunks = [jnp.concatenate(parts[1:])]
         across += [swap(chunk, wide, 2) for chunk in chunks]
-        return [stack, swap(stack, wide, 1)] + across + [swap(piece, wide, 1) for piece in across]
+        beside = [swap(parts[0], wide, 1)]
+        if split:
+            beside.append(swap(jnp.concatenate(parts[1:]), wide, 1))
+        else:
+            beside = [swap(stack, wide, 1)]
+        return [stack] + beside + across + [swap(piece, wide, 1) for piece in across]
     across = swap(stack, wide, 2)
     return [stack, swap(stack, wide, 1), across, swap(across, wide, 1)]
 

time: 59.8 us -> 60.5 us (1.012)
    ppermute x17 -> x18, waiting for transfers between devices: 14.2 us -> 13.1 us  [swap(): return lax.ppermute(x, 'wide', [(d, d ^ mask) for d in range(wide)])]
    ppermute x9, waiting for transfers between devices: 0.94 us -> 1.63 us  [line_stage(): parts.append(lax.ppermute(x, 'wide', pairs)[None])]
    ppermute x17 -> x18, starting transfers between devices: 11.1 us -> 11.7 us  [swap(): return lax.ppermute(x, 'wide', [(d, d ^ mask) for d in range(wide)])]
    dot_general x27 -> x30, matrix products: 7.16 us -> 7.73 us  [rowwise(): return jnp.einsum(spec, tiles, currents, preferred_element_type=jnp.float32)]
  transfers between devices with their start and end apart: 26 -> 27, of which waited for: 9 -> 9; matrix products, arithmetic and copies ran while one was open for 20% -> 21% of each run, Pallas kernels for 0% -> 0%
where the time goes in v17:
time: 60.5 us; the launch traced here: 60.3 us
  starting transfers between devices  28.4 us (47%)
  waiting for transfers between devices  14.8 us (24%)
  matrix products  8.59 us (14%)
  local copies, waits for them, and re-layouts  4.18 us (7%)
  other arithmetic  3.85 us (6%)
    ppermute x9, starting transfers between devices, line_stage(): parts.append(lax.ppermute(x, 'wide', pairs)[None])  16.6 us
    ppermute x18, waiting for transfers between devices, swap(): return lax.ppermute(x, 'wide', [(d, d ^ mask) for d in range(wide)])  13.1 us
    ppermute x18, starting transfers between devices, swap(): return lax.ppermute(x, 'wide', [(d, d ^ mask) for d in range(wide)])  11.7 us
    dot_general x30, matrix products, rowwise(): return jnp.einsum(spec, tiles, currents, preferred_element_type=jnp.float32)  7.73 us
    sort x1, other arithmetic, per_device(): column_of_block = jnp.argsort(block_owner)  1.9 us
    ppermute x9, waiting for transfers between devices, line_stage(): parts.append(lax.ppermute(x, 'wide', pairs)[None])  1.63 us
    unnamed x22, local copies, waits for them, and re-layouts  1.34 us
  transfers between devices with their start and end apart: 27, of which 9 were waited for; matrix products, arithmetic and copies ran while one was open for 21% of the time, Pallas kernels for 0%

profile of v17, /device:TPU:0, one launch (start us, length us, event | category | flops | bytes accessed | tf_op | source)
XLA Modules:
  0.0 60.3 jit_solution(4074949401950338352)
XLA Ops:
  0.0 3.0 %collective-permute-start = (bf16[4,128,128]{2,1,0:T(8,128)(2,1)}, bf16[4,128,128]{2,1,0:T(8,128)(2,1)S(1)}, u32[]{:S(2)}, u32[]{:S(2)}) collective-permute-start(bf16[4,128,128]{2,1,0:T(8,128)(2,1)} %param.19), channel_id=1, source_target_pairs={{0,4},{1,5},{2,6},{3,7},{4,8},{5,9},{6,10},{7,11},{8,12},{9,13},{1... | collective-permute-start | bytes 393224 | tf_op jit(solution)/shard_map/ppermute | solution.py:26
  3.0 2.6 %collective-permute-start.1 = (bf16[4,128,128]{2,1,0:T(8,128)(2,1)}, bf16[4,128,128]{2,1,0:T(8,128)(2,1)S(1)}, u32[]{:S(2)}, u32[]{:S(2)}) collective-permute-start(bf16[4,128,128]{2,1,0:T(8,128)(2,1)} %param.19), channel_id=1, source_target_pairs={{0,8},{1,9},{2,10},{3,11},{4,12},{5,13},{6,14},{7,15},{8,0},{9,1},... | collective-permute-start | bytes 393224 | tf_op jit(solution)/shard_map/ppermute | solution.py:26
  5.6 1.3 %collective-permute-start.2 = (bf16[4,128,128]{2,1,0:T(8,128)(2,1)}, bf16[4,128,128]{2,1,0:T(8,128)(2,1)S(1)}, u32[]{:S(2)}, u32[]{:S(2)}) collective-permute-start(bf16[4,128,128]{2,1,0:T(8,128)(2,1)} %param.19), channel_id=1, source_target_pairs={{0,12},{1,13},{2,14},{3,15},{4,0},{5,1},{6,2},{7,3},{8,4},{9,5},{1... | collective-permute-start | bytes 393224 | tf_op jit(solution)/shard_map/ppermute | solution.py:26
  7.0 1.5 %collective-permute-start.5 = (bf16[1,4,128,128]{3,2,1,0:T(8,128)(2,1)}, bf16[1,4,128,128]{3,2,1,0:T(8,128)(2,1)S(1)}, u32[]{:S(2)}, u32[]{:S(2)}) collective-permute-start(bf16[1,4,128,128]{3,2,1,0:T(8,128)(2,1)} %bitcast.357), channel_id=1, source_target_pairs={{0,2},{1,3},{2,0},{3,1},{4,6},{5,7},{6,4},{7,5},{8,10},{9,11},{10,... | collective-permute-start | bytes 393224 | tf_op jit(solution)/shard_map/ppermute | solution.py:33
  8.7 1.9 %sort.17 = (s32[16]{0:T(128)}, s32[16]{0:T(128)S(1)}) sort(s32[16]{0:T(128)} %param.18, s32[16]{0:T(128)S(1)} %iota.5), dimensions={0}, to_apply=%region_0.0 | sort | flops 64 | bytes 256 | tf_op jit(solution)/shard_map/jit(argsort)/sort | solution.py:99
  10.6 0.7 %gather_fusion = s32[16]{0:T(128)S(1)} fusion(s32[16]{0:T(128)S(1)} %get-tuple-element.8, s32[1024]{0:T(1024)S(1)} %pad_clamp_fusion.1), kind=kCustom, calls=%fused_computation.clone | custom fusion | bytes 192 | tf_op jit(solution)/shard_map/jit(_take)/gather | solution.py:74
  11.3 0.8 %copy.17 = s32[16,2]{1,0:T(8,128)S(1)} copy(s32[16,2]{0,1:T(2,128)} %bitcast.364) | data formatting | bytes 256 | tf_op jit(solution)/shard_map/squeeze | solution.py:76
  12.0 0.7 %gather_fusion.2 = bf16[16,2,128,128]{3,2,1,0:T(8,128)(2,1)S(1)} fusion(bf16[16,2,128,128]{3,2,1,0:T(8,128)(2,1)S(1)} %bitcast.329, s32[1024]{0:T(1024)S(1)} %pad_clamp_fusion), kind=kCustom, calls=%fused_computation.2.clone | custom fusion | bytes 2097216 | tf_op jit(solution)/shard_map/jit(_take)/gather | solution.py:75
  12.8 0.6 gather_fusion.1
  13.9 0.3 bitcast_select_fusion.3
  14.5 0.5 copy-done.3
  15.1 1.1 %collective-permute-start.6 = (bf16[1,4,128,128]{3,2,1,0:T(8,128)(2,1)S(1)}, bf16[1,4,128,128]{3,2,1,0:T(8,128)(2,1)S(1)}, u32[]{:S(2)}, u32[]{:S(2)}) collective-permute-start(bf16[1,4,128,128]{3,2,1,0:T(8,128)(2,1)S(1)} %bitcast.339), channel_id=1, source_target_pairs={{0,2},{1,3},{2,0},{3,1},{4,6},{5,7},{6,4},{7,5},{8,10},{9,11},{10,... | collective-permute-start | bytes 393224 | tf_op jit(solution)/shard_map/ppermute | solution.py:33
  16.2 1.1 %collective-permute-start.7 = (bf16[2,4,128,128]{3,2,1,0:T(8,128)(2,1)S(1)}, bf16[2,4,128,128]{3,2,1,0:T(8,128)(2,1)S(1)}, u32[]{:S(2)}, u32[]{:S(2)}) collective-permute-start(bf16[2,4,128,128]{3,2,1,0:T(8,128)(2,1)S(1)} %pad_maximum_fusion.5), channel_id=1, source_target_pairs={{0,2},{1,3},{2,0},{3,1},{4,6},{5,7},{6,4},{7,5},{8,10},{9,11},{10,... | collective-permute-start | bytes 786440 | tf_op jit(solution)/shard_map/ppermute | solution.py:33
  17.9 0.4 fusion.29
  18.4 0.3 convolution_bitcast_fusion.5
  19.2 0.6 collective-permute-start.8
  20.0 1.5 %collective-permute-done.6 = bf16[1,4,128,128]{3,2,1,0:T(8,128)(2,1)S(1)} collective-permute-done((bf16[1,4,128,128]{3,2,1,0:T(8,128)(2,1)S(1)}, bf16[1,4,128,128]{3,2,1,0:T(8,128)(2,1)S(1)}, u32[]{:S(2)}, u32[]{:S(2)}) %collective-permute-start.6) | collective-permute-done | bytes 131104 | tf_op jit(solution)/shard_map/ppermute | solution.py:33
  22.3 4.2 %collective-permute-done.7 = bf16[2,4,128,128]{3,2,1,0:T(8,128)(2,1)S(1)} collective-permute-done((bf16[2,4,128,128]{3,2,1,0:T(8,128)(2,1)S(1)}, bf16[2,4,128,128]{3,2,1,0:T(8,128)(2,1)S(1)}, u32[]{:S(2)}, u32[]{:S(2)}) %collective-permute-start.7) | collective-permute-done | bytes 262176 | tf_op jit(solution)/shard_map/ppermute | solution.py:33
  27.6 0.3 convolution_bitcast_fusion.2
  27.9 0.3 convolution_bitcast_fusion.4
  28.7 0.3 fusion.28
  29.0 0.3 convolution_bitcast_fusion.1
  29.4 0.6 copy-done.2
  30.2 0.3 constant_dynamic-update-slice_fusion.8
  30.5 2.6 %collective-permute-start.11 = (bf16[128,128]{1,0:T(8,128)(2,1)S(1)}, bf16[128,128]{1,0:T(8,128)(2,1)S(1)}, u32[]{:S(2)}, u32[]{:S(2)}) collective-permute-start(bf16[128,128]{1,0:T(8,128)(2,1)S(1)} %get-tuple-element.21), channel_id=1, source_target_pairs={{0,4},{1,5},{2,6},{3,7},{4,8},{5,9},{6,10},{7,11},{8,12},{9,13},{1... | collective-permute-start | bytes 98312 | tf_op jit(solution)/shard_map/ppermute | solution.py:26
  33.1 0.6 collective-permute-start.12
  33.7 1.9 %collective-permute-start.13 = (bf16[128,128]{1,0:T(8,128)(2,1)S(1)}, bf16[128,128]{1,0:T(8,128)(2,1)S(1)}, u32[]{:S(2)}, u32[]{:S(2)}) collective-permute-start(bf16[128,128]{1,0:T(8,128)(2,1)S(1)} %get-tuple-element.21), channel_id=1, source_target_pairs={{0,12},{1,13},{2,14},{3,15},{4,0},{5,1},{6,2},{7,3},{8,4},{9,5},{1... | collective-permute-start | bytes 98312 | tf_op jit(solution)/shard_map/ppermute | solution.py:26
  35.5 1.5 %collective-permute-start.15 = (bf16[1,128,128]{2,1,0:T(8,128)(2,1)S(1)}, bf16[1,128,128]{2,1,0:T(8,128)(2,1)S(1)}, u32[]{:S(2)}, u32[]{:S(2)}) collective-permute-start(bf16[1,128,128]{2,1,0:T(8,128)(2,1)S(1)} %bitcast.362), channel_id=1, source_target_pairs={{0,2},{1,3},{2,0},{3,1},{4,6},{5,7},{6,4},{7,5},{8,10},{9,11},{10,... | collective-permute-start | bytes 98312 | tf_op jit(solution)/shard_map/ppermute | solution.py:33
  37.5 0.7 %collective-permute-done.12 = bf16[128,128]{1,0:T(8,128)(2,1)S(1)} collective-permute-done((bf16[128,128]{1,0:T(8,128)(2,1)S(1)}, bf16[128,128]{1,0:T(8,128)(2,1)S(1)}, u32[]{:S(2)}, u32[]{:S(2)}) %collective-permute-start.12) | collective-permute-done | bytes 32800 | tf_op jit(solution)/shard_map/ppermute | solution.py:26
  38.3 1.6 %collective-permute-start.16 = (bf16[3,128,128]{2,1,0:T(8,128)(2,1)S(1)}, bf16[3,128,128]{2,1,0:T(8,128)(2,1)S(1)}, u32[]{:S(2)}, u32[]{:S(2)}) collective-permute-start(bf16[3,128,128]{2,1,0:T(8,128)(2,1)S(1)} %pad_maximum_fusion.9), channel_id=1, source_target_pairs={{0,2},{1,3},{2,0},{3,1},{4,6},{5,7},{6,4},{7,5},{8,10},{9,11},{10,... | collective-permute-start | bytes 294920 | tf_op jit(solution)/shard_map/ppermute | solution.py:33
  39.9 0.6 collective-permute-start.17
  40.5 2.5 %collective-permute-done.16 = bf16[3,128,128]{2,1,0:T(8,128)(2,1)S(1)} collective-permute-done((bf16[3,128,128]{2,1,0:T(8,128)(2,1)S(1)}, bf16[3,128,128]{2,1,0:T(8,128)(2,1)S(1)}, u32[]{:S(2)}, u32[]{:S(2)}) %collective-permute-start.16) | collective-permute-done | bytes 98336 | tf_op jit(solution)/shard_map/ppermute | solution.py:33
  43.1 1.2 %collective-permute-done.18 = bf16[3,128,128]{2,1,0:T(8,128)(2,1)S(1)} collective-permute-done((bf16[3,128,128]{2,1,0:T(8,128)(2,1)S(1)}, bf16[3,128,128]{2,1,0:T(8,128)(2,1)S(1)}, u32[]{:S(2)}, u32[]{:S(2)}) %collective-permute-start.18) | collective-permute-done | bytes 98336 | tf_op jit(solution)/shard_map/ppermute | solution.py:33
  44.3 0.3 convolution_bitcast_fusion.10
  44.9 0.3 constant_dynamic-update-slice_fusion.17
  45.2 1.1 %collective-permute-start.19 = (bf16[128,128]{1,0:T(8,128)(2,1)S(1)}, bf16[128,128]{1,0:T(8,128)(2,1)S(1)}, u32[]{:S(2)}, u32[]{:S(2)}) collective-permute-start(bf16[128,128]{1,0:T(8,128)(2,1)S(1)} %get-tuple-element.19), channel_id=1, source_target_pairs={{0,4},{1,5},{2,6},{3,7},{4,8},{5,9},{6,10},{7,11},{8,12},{9,13},{1... | collective-permute-start | bytes 98312 | tf_op jit(solution)/shard_map/ppermute | solution.py:26
  46.2 2.5 %collective-permute-start.20 = (bf16[128,128]{1,0:T(8,128)(2,1)S(1)}, bf16[128,128]{1,0:T(8,128)(2,1)S(1)}, u32[]{:S(2)}, u32[]{:S(2)}) collective-permute-start(bf16[128,128]{1,0:T(8,128)(2,1)S(1)} %get-tuple-element.19), channel_id=1, source_target_pairs={{0,8},{1,9},{2,10},{3,11},{4,12},{5,13},{6,14},{7,15},{8,0},{9,1},... | collective-permute-start | bytes 98312 | tf_op jit(solution)/shard_map/ppermute | solution.py:26
  48.8 1.0 %collective-permute-start.21 = (bf16[128,128]{1,0:T(8,128)(2,1)S(1)}, bf16[128,128]{1,0:T(8,128)(2,1)S(1)}, u32[]{:S(2)}, u32[]{:S(2)}) collective-permute-start(bf16[128,128]{1,0:T(8,128)(2,1)S(1)} %get-tuple-element.19), channel_id=1, source_target_pairs={{0,12},{1,13},{2,14},{3,15},{4,0},{5,1},{6,2},{7,3},{8,4},{9,5},{1... | collective-permute-start | bytes 98312 | tf_op jit(solution)/shard_map/ppermute | solution.py:26
  49.8 0.5 convolution_bitcast_fusion.8
  50.3 1.6 %collective-permute-start.23 = (bf16[1,128,128]{2,1,0:T(8,128)(2,1)S(1)}, bf16[1,128,128]{2,1,0:T(8,128)(2,1)S(1)}, u32[]{:S(2)}, u32[]{:S(2)}) collective-permute-start(bf16[1,128,128]{2,1,0:T(8,128)(2,1)S(1)} %bitcast.360), channel_id=1, source_target_pairs={{0,2},{1,3},{2,0},{3,1},{4,6},{5,7},{6,4},{7,5},{8,10},{9,11},{10,... | collective-permute-start | bytes 98312 | tf_op jit(solution)/shard_map/ppermute | solution.py:33
  51.9 0.8 %collective-permute-done.21 = bf16[128,128]{1,0:T(8,128)(2,1)S(1)} collective-permute-done((bf16[128,128]{1,0:T(8,128)(2,1)S(1)}, bf16[128,128]{1,0:T(8,128)(2,1)S(1)}, u32[]{:S(2)}, u32[]{:S(2)}) %collective-permute-start.21) | collective-permute-done | bytes 32800 | tf_op jit(solution)/shard_map/ppermute | solution.py:26
  52.7 1.6 %collective-permute-start.24 = (bf16[3,128,128]{2,1,0:T(8,128)(2,1)S(1)}, bf16[3,128,128]{2,1,0:T(8,128)(2,1)S(1)}, u32[]{:S(2)}, u32[]{:S(2)}) collective-permute-start(bf16[3,128,128]{2,1,0:T(8,128)(2,1)S(1)} %pad_maximum_fusion.10), channel_id=1, source_target_pairs={{0,2},{1,3},{2,0},{3,1},{4,6},{5,7},{6,4},{7,5},{8,10},{9,11},{10,... | collective-permute-start | bytes 294920 | tf_op jit(solution)/shard_map/ppermute | solution.py:33
  54.4 0.6 collective-permute-start.25
  54.9 2.5 %collective-permute-done.24 = bf16[3,128,128]{2,1,0:T(8,128)(2,1)S(1)} collective-permute-done((bf16[3,128,128]{2,1,0:T(8,128)(2,1)S(1)}, bf16[3,128,128]{2,1,0:T(8,128)(2,1)S(1)}, u32[]{:S(2)}, u32[]{:S(2)}) %collective-permute-start.24) | collective-permute-done | bytes 98336 | tf_op jit(solution)/shard_map/ppermute | solution.py:33
  57.5 1.2 %collective-permute-done.26 = bf16[3,128,128]{2,1,0:T(8,128)(2,1)S(1)} collective-permute-done((bf16[3,128,128]{2,1,0:T(8,128)(2,1)S(1)}, bf16[3,128,128]{2,1,0:T(8,128)(2,1)S(1)}, u32[]{:S(2)}, u32[]{:S(2)}) %collective-permute-start.26) | collective-permute-done | bytes 98336 | tf_op jit(solution)/shard_map/ppermute | solution.py:33
  58.7 0.3 convolution_bitcast_fusion.9
  59.3 0.3 convolution_bitcast_fusion.7
  59.6 0.7 %pad_maximum_fusion.6 = f32[3,128,128]{2,1,0:T(8,128)} fusion(f32[1,128,128]{2,1,0:T(8,128)S(1)} %bitcast.354, f32[1,128,128]{2,1,0:T(8,128)S(1)} %bitcast.355, f32[1,128,128]{2,1,0:T(8,128)S(1)} %convolution_bitcast_fusion.7), kind=kLoop, calls=%fused_computation.95 | loop fusion | flops 98304 | bytes 393216 | tf_op jit(solution)/shard_map/stack | solution.py:141
  (89 shorter events, 6.3 us)
Async XLA Ops:
  0.0 12.0 %copy-start = (bf16[1,16,2,128,128]{4,3,2,1,0:T(8,128)(2,1)S(1)}, bf16[1,16,2,128,128]{4,3,2,1,0:T(8,128)(2,1)}, u32[]{:S(2)}) copy-start(bf16[1,16,2,128,128]{4,3,2,1,0:T(8,128)(2,1)} %param.16) | copy-start | bytes 3145732
  0.0 14.5 %collective-permute-start = (bf16[4,128,128]{2,1,0:T(8,128)(2,1)}, bf16[4,128,128]{2,1,0:T(8,128)(2,1)S(1)}, u32[]{:S(2)}, u32[]{:S(2)}) collective-permute-start(bf16[4,128,128]{2,1,0:T(8,128)(2,1)} %param.19), channel_id=1, source_target_pairs={{0,4},{1,5},{2,6},{3,7},{4,8},{5,9},{6,10},{7,11},{8,12},{9,13},{1... | collective-permute-start | bytes 393224 | tf_op jit(solution)/shard_map/ppermute | solution.py:26
  3.0 11.4 %collective-permute-start.1 = (bf16[4,128,128]{2,1,0:T(8,128)(2,1)}, bf16[4,128,128]{2,1,0:T(8,128)(2,1)S(1)}, u32[]{:S(2)}, u32[]{:S(2)}) collective-permute-start(bf16[4,128,128]{2,1,0:T(8,128)(2,1)} %param.19), channel_id=1, source_target_pairs={{0,8},{1,9},{2,10},{3,11},{4,12},{5,13},{6,14},{7,15},{8,0},{9,1},... | collective-permute-start | bytes 393224 | tf_op jit(solution)/shard_map/ppermute | solution.py:26
  5.6 8.9 %collective-permute-start.2 = (bf16[4,128,128]{2,1,0:T(8,128)(2,1)}, bf16[4,128,128]{2,1,0:T(8,128)(2,1)S(1)}, u32[]{:S(2)}, u32[]{:S(2)}) collective-permute-start(bf16[4,128,128]{2,1,0:T(8,128)(2,1)} %param.19), channel_id=1, source_target_pairs={{0,12},{1,13},{2,14},{3,15},{4,0},{5,1},{6,2},{7,3},{8,4},{9,5},{1... | collective-permute-start | bytes 393224 | tf_op jit(solution)/shard_map/ppermute | solution.py:26
  7.0 10.7 %collective-permute-start.3 = (bf16[1,4,128,128]{3,2,1,0:T(8,128)(2,1)}, bf16[1,4,128,128]{3,2,1,0:T(8,128)(2,1)S(1)}, u32[]{:S(2)}, u32[]{:S(2)}) collective-permute-start(bf16[1,4,128,128]{3,2,1,0:T(8,128)(2,1)} %bitcast.356), channel_id=1, source_target_pairs={{0,1},{1,0},{2,3},{3,2},{4,5},{5,4},{6,7},{7,6},{8,9},{9,8},{10,11... | collective-permute-start | bytes 393224 | tf_op jit(solution)/shard_map/ppermute | solution.py:33
  7.0 11.8 %collective-permute-start.5 = (bf16[1,4,128,128]{3,2,1,0:T(8,128)(2,1)}, bf16[1,4,128,128]{3,2,1,0:T(8,128)(2,1)S(1)}, u32[]{:S(2)}, u32[]{:S(2)}) collective-permute-start(bf16[1,4,128,128]{3,2,1,0:T(8,128)(2,1)} %bitcast.357), channel_id=1, source_target_pairs={{0,2},{1,3},{2,0},{3,1},{4,6},{5,7},{6,4},{7,5},{8,10},{9,11},{10,... | collective-permute-start | bytes 393224 | tf_op jit(solution)/shard_map/ppermute | solution.py:33
  14.2 0.9 %copy-start.3 = (bf16[4,128,128]{2,1,0:T(8,128)(2,1)S(1)}, bf16[4,128,128]{2,1,0:T(8,128)(2,1)}, u32[]{:S(2)}) copy-start(bf16[4,128,128]{2,1,0:T(8,128)(2,1)} %param.19) | copy-start | bytes 393220
  15.1 6.4 %collective-permute-start.6 = (bf16[1,4,128,128]{3,2,1,0:T(8,128)(2,1)S(1)}, bf16[1,4,128,128]{3,2,1,0:T(8,128)(2,1)S(1)}, u32[]{:S(2)}, u32[]{:S(2)}) collective-permute-start(bf16[1,4,128,128]{3,2,1,0:T(8,128)(2,1)S(1)} %bitcast.339), channel_id=1, source_target_pairs={{0,2},{1,3},{2,0},{3,1},{4,6},{5,7},{6,4},{7,5},{8,10},{9,11},{10,... | collective-permute-start | bytes 393224 | tf_op jit(solution)/shard_map/ppermute | solution.py:33
  16.2 10.2 %collective-permute-start.7 = (bf16[2,4,128,128]{3,2,1,0:T(8,128)(2,1)S(1)}, bf16[2,4,128,128]{3,2,1,0:T(8,128)(2,1)S(1)}, u32[]{:S(2)}, u32[]{:S(2)}) collective-permute-start(bf16[2,4,128,128]{3,2,1,0:T(8,128)(2,1)S(1)} %pad_maximum_fusion.5), channel_id=1, source_target_pairs={{0,2},{1,3},{2,0},{3,1},{4,6},{5,7},{6,4},{7,5},{8,10},{9,11},{10,... | collective-permute-start | bytes 786440 | tf_op jit(solution)/shard_map/ppermute | solution.py:33
  17.3 10.6 %collective-permute-start.4 = (bf16[3,4,128,128]{3,2,1,0:T(8,128)(2,1)S(1)}, bf16[3,4,128,128]{3,2,1,0:T(8,128)(2,1)S(1)}, u32[]{:S(2)}, u32[]{:S(2)}) collective-permute-start(bf16[3,4,128,128]{3,2,1,0:T(8,128)(2,1)S(1)} %pad_maximum_fusion.4), channel_id=1, source_target_pairs={{0,1},{1,0},{2,3},{3,2},{4,5},{5,4},{6,7},{7,6},{8,9},{9,8},{10,11... | collective-permute-start | bytes 1179656 | tf_op jit(solution)/shard_map/ppermute | solution.py:33
  19.2 10.2 %collective-permute-start.8 = (bf16[1,4,128,128]{3,2,1,0:T(8,128)(2,1)S(1)}, bf16[1,4,128,128]{3,2,1,0:T(8,128)(2,1)S(1)}, u32[]{:S(2)}, u32[]{:S(2)}) collective-permute-start(bf16[1,4,128,128]{3,2,1,0:T(8,128)(2,1)S(1)} %collective-permute-done.5), channel_id=1, source_target_pairs={{0,1},{1,0},{2,3},{3,2},{4,5},{5,4},{6,7},{7,6},{8,9},{9,8},{10,11... | collective-permute-start | bytes 393224 | tf_op jit(solution)/shard_map/ppermute | solution.py:33
  21.7 5.0 %collective-permute-start.9 = (bf16[1,4,128,128]{3,2,1,0:T(8,128)(2,1)S(1)}, bf16[1,4,128,128]{3,2,1,0:T(8,128)(2,1)S(1)}, u32[]{:S(2)}, u32[]{:S(2)}) collective-permute-start(bf16[1,4,128,128]{3,2,1,0:T(8,128)(2,1)S(1)} %collective-permute-done.6), channel_id=1, source_target_pairs={{0,1},{1,0},{2,3},{3,2},{4,5},{5,4},{6,7},{7,6},{8,9},{9,8},{10,11... | collective-permute-start | bytes 393224 | tf_op jit(solution)/shard_map/ppermute | solution.py:33
  26.4 2.6 %collective-permute-start.10 = (bf16[2,4,128,128]{3,2,1,0:T(8,128)(2,1)S(1)}, bf16[2,4,128,128]{3,2,1,0:T(8,128)(2,1)S(1)}, u32[]{:S(2)}, u32[]{:S(2)}) collective-permute-start(bf16[2,4,128,128]{3,2,1,0:T(8,128)(2,1)S(1)} %collective-permute-done.7), channel_id=1, source_target_pairs={{0,1},{1,0},{2,3},{3,2},{4,5},{5,4},{6,7},{7,6},{8,9},{9,8},{10,11... | collective-permute-start | bytes 786440 | tf_op jit(solution)/shard_map/ppermute | solution.py:33
  29.0 0.9 %copy-start.2 = (f32[3,128,128]{2,1,0:T(8,128)S(1)}, f32[3,128,128]{2,1,0:T(8,128)}, u32[]{:S(2)}) copy-start(f32[3,128,128]{2,1,0:T(8,128)} %param.20) | copy-start | bytes 589828
  29.3 0.9 %copy-start.1 = (f32[1,128,128]{2,1,0:T(8,128)S(1)}, f32[1,128,128]{2,1,0:T(8,128)}, u32[]{:S(2)}) copy-start(f32[1,128,128]{2,1,0:T(8,128)} %param.21) | copy-start | bytes 196612
  30.5 7.0 %collective-permute-start.11 = (bf16[128,128]{1,0:T(8,128)(2,1)S(1)}, bf16[128,128]{1,0:T(8,128)(2,1)S(1)}, u32[]{:S(2)}, u32[]{:S(2)}) collective-permute-start(bf16[128,128]{1,0:T(8,128)(2,1)S(1)} %get-tuple-element.21), channel_id=1, source_target_pairs={{0,4},{1,5},{2,6},{3,7},{4,8},{5,9},{6,10},{7,11},{8,12},{9,13},{1... | collective-permute-start | bytes 98312 | tf_op jit(solution)/shard_map/ppermute | solution.py:26
  33.1 5.2 %collective-permute-start.12 = (bf16[128,128]{1,0:T(8,128)(2,1)S(1)}, bf16[128,128]{1,0:T(8,128)(2,1)S(1)}, u32[]{:S(2)}, u32[]{:S(2)}) collective-permute-start(bf16[128,128]{1,0:T(8,128)(2,1)S(1)} %get-tuple-element.21), channel_id=1, source_target_pairs={{0,8},{1,9},{2,10},{3,11},{4,12},{5,13},{6,14},{7,15},{8,0},{9,1},... | collective-permute-start | bytes 98312 | tf_op jit(solution)/shard_map/ppermute | solution.py:26
  33.7 4.6 %collective-permute-start.13 = (bf16[128,128]{1,0:T(8,128)(2,1)S(1)}, bf16[128,128]{1,0:T(8,128)(2,1)S(1)}, u32[]{:S(2)}, u32[]{:S(2)}) collective-permute-start(bf16[128,128]{1,0:T(8,128)(2,1)S(1)} %get-tuple-element.21), channel_id=1, source_target_pairs={{0,12},{1,13},{2,14},{3,15},{4,0},{5,1},{6,2},{7,3},{8,4},{9,5},{1... | collective-permute-start | bytes 98312 | tf_op jit(solution)/shard_map/ppermute | solution.py:26
  35.5 4.4 %collective-permute-start.15 = (bf16[1,128,128]{2,1,0:T(8,128)(2,1)S(1)}, bf16[1,128,128]{2,1,0:T(8,128)(2,1)S(1)}, u32[]{:S(2)}, u32[]{:S(2)}) collective-permute-start(bf16[1,128,128]{2,1,0:T(8,128)(2,1)S(1)} %bitcast.362), channel_id=1, source_target_pairs={{0,2},{1,3},{2,0},{3,1},{4,6},{5,7},{6,4},{7,5},{8,10},{9,11},{10,... | collective-permute-start | bytes 98312 | tf_op jit(solution)/shard_map/ppermute | solution.py:33
  38.3 4.7 %collective-permute-start.16 = (bf16[3,128,128]{2,1,0:T(8,128)(2,1)S(1)}, bf16[3,128,128]{2,1,0:T(8,128)(2,1)S(1)}, u32[]{:S(2)}, u32[]{:S(2)}) collective-permute-start(bf16[3,128,128]{2,1,0:T(8,128)(2,1)S(1)} %pad_maximum_fusion.9), channel_id=1, source_target_pairs={{0,2},{1,3},{2,0},{3,1},{4,6},{5,7},{6,4},{7,5},{8,10},{9,11},{10,... | collective-permute-start | bytes 294920 | tf_op jit(solution)/shard_map/ppermute | solution.py:33
  39.9 3.1 %collective-permute-start.14 = (bf16[4,128,128]{2,1,0:T(8,128)(2,1)S(1)}, bf16[4,128,128]{2,1,0:T(8,128)(2,1)S(1)}, u32[]{:S(2)}, u32[]{:S(2)}) collective-permute-start(bf16[4,128,128]{2,1,0:T(8,128)(2,1)S(1)} %pad_maximum_fusion.7), channel_id=1, source_target_pairs={{0,1},{1,0},{2,3},{3,2},{4,5},{5,4},{6,7},{7,6},{8,9},{9,8},{10,11... | collective-permute-start | bytes 393224 | tf_op jit(solution)/shard_map/ppermute | solution.py:33
  39.9 3.1 %collective-permute-start.17 = (bf16[1,128,128]{2,1,0:T(8,128)(2,1)S(1)}, bf16[1,128,128]{2,1,0:T(8,128)(2,1)S(1)}, u32[]{:S(2)}, u32[]{:S(2)}) collective-permute-start(bf16[1,128,128]{2,1,0:T(8,128)(2,1)S(1)} %collective-permute-done.15), channel_id=1, source_target_pairs={{0,1},{1,0},{2,3},{3,2},{4,5},{5,4},{6,7},{7,6},{8,9},{9,8},{10,11... | collective-permute-start | bytes 98312 | tf_op jit(solution)/shard_map/ppermute | solution.py:33
  43.0 1.3 %collective-permute-start.18 = (bf16[3,128,128]{2,1,0:T(8,128)(2,1)S(1)}, bf16[3,128,128]{2,1,0:T(8,128)(2,1)S(1)}, u32[]{:S(2)}, u32[]{:S(2)}) collective-permute-start(bf16[3,128,128]{2,1,0:T(8,128)(2,1)S(1)} %collective-permute-done.16), channel_id=1, source_target_pairs={{0,1},{1,0},{2,3},{3,2},{4,5},{5,4},{6,7},{7,6},{8,9},{9,8},{10,11... | collective-permute-start | bytes 294920 | tf_op jit(solution)/shard_map/ppermute | solution.py:33
  45.2 6.7 %collective-permute-start.19 = (bf16[128,128]{1,0:T(8,128)(2,1)S(1)}, bf16[128,128]{1,0:T(8,128)(2,1)S(1)}, u32[]{:S(2)}, u32[]{:S(2)}) collective-permute-start(bf16[128,128]{1,0:T(8,128)(2,1)S(1)} %get-tuple-element.19), channel_id=1, source_target_pairs={{0,4},{1,5},{2,6},{3,7},{4,8},{5,9},{6,10},{7,11},{8,12},{9,13},{1... | collective-permute-start | bytes 98312 | tf_op jit(solution)/shard_map/ppermute | solution.py:26
  46.2 5.7 %collective-permute-start.20 = (bf16[128,128]{1,0:T(8,128)(2,1)S(1)}, bf16[128,128]{1,0:T(8,128)(2,1)S(1)}, u32[]{:S(2)}, u32[]{:S(2)}) collective-permute-start(bf16[128,128]{1,0:T(8,128)(2,1)S(1)} %get-tuple-element.19), channel_id=1, source_target_pairs={{0,8},{1,9},{2,10},{3,11},{4,12},{5,13},{6,14},{7,15},{8,0},{9,1},... | collective-permute-start | bytes 98312 | tf_op jit(solution)/shard_map/ppermute | solution.py:26
  48.8 3.9 %collective-permute-start.21 = (bf16[128,128]{1,0:T(8,128)(2,1)S(1)}, bf16[128,128]{1,0:T(8,128)(2,1)S(1)}, u32[]{:S(2)}, u32[]{:S(2)}) collective-permute-start(bf16[128,128]{1,0:T(8,128)(2,1)S(1)} %get-tuple-element.19), channel_id=1, source_target_pairs={{0,12},{1,13},{2,14},{3,15},{4,0},{5,1},{6,2},{7,3},{8,4},{9,5},{1... | collective-permute-start | bytes 98312 | tf_op jit(solution)/shard_map/ppermute | solution.py:26
  50.3 4.0 %collective-permute-start.23 = (bf16[1,128,128]{2,1,0:T(8,128)(2,1)S(1)}, bf16[1,128,128]{2,1,0:T(8,128)(2,1)S(1)}, u32[]{:S(2)}, u32[]{:S(2)}) collective-permute-start(bf16[1,128,128]{2,1,0:T(8,128)(2,1)S(1)} %bitcast.360), channel_id=1, source_target_pairs={{0,2},{1,3},{2,0},{3,1},{4,6},{5,7},{6,4},{7,5},{8,10},{9,11},{10,... | collective-permute-start | bytes 98312 | tf_op jit(solution)/shard_map/ppermute | solution.py:33
  52.7 4.7 %collective-permute-start.24 = (bf16[3,128,128]{2,1,0:T(8,128)(2,1)S(1)}, bf16[3,128,128]{2,1,0:T(8,128)(2,1)S(1)}, u32[]{:S(2)}, u32[]{:S(2)}) collective-permute-start(bf16[3,128,128]{2,1,0:T(8,128)(2,1)S(1)} %pad_maximum_fusion.10), channel_id=1, source_target_pairs={{0,2},{1,3},{2,0},{3,1},{4,6},{5,7},{6,4},{7,5},{8,10},{9,11},{10,... | collective-permute-start | bytes 294920 | tf_op jit(solution)/shard_map/ppermute | solution.py:33
  54.3 3.1 %collective-permute-start.22 = (bf16[4,128,128]{2,1,0:T(8,128)(2,1)S(1)}, bf16[4,128,128]{2,1,0:T(8,128)(2,1)S(1)}, u32[]{:S(2)}, u32[]{:S(2)}) collective-permute-start(bf16[4,128,128]{2,1,0:T(8,128)(2,1)S(1)} %pad_maximum_fusion.8), channel_id=1, source_target_pairs={{0,1},{1,0},{2,3},{3,2},{4,5},{5,4},{6,7},{7,6},{8,9},{9,8},{10,11... | collective-permute-start | bytes 393224 | tf_op jit(solution)/shard_map/ppermute | solution.py:33
  54.4 3.1 %collective-permute-start.25 = (bf16[1,128,128]{2,1,0:T(8,128)(2,1)S(1)}, bf16[1,128,128]{2,1,0:T(8,128)(2,1)S(1)}, u32[]{:S(2)}, u32[]{:S(2)}) collective-permute-start(bf16[1,128,128]{2,1,0:T(8,128)(2,1)S(1)} %collective-permute-done.23), channel_id=1, source_target_pairs={{0,1},{1,0},{2,3},{3,2},{4,5},{5,4},{6,7},{7,6},{8,9},{9,8},{10,11... | collective-permute-start | bytes 98312 | tf_op jit(solution)/shard_map/ppermute | solution.py:33
  57.4 1.3 %collective-permute-start.26 = (bf16[3,128,128]{2,1,0:T(8,128)(2,1)S(1)}, bf16[3,128,128]{2,1,0:T(8,128)(2,1)S(1)}, u32[]{:S(2)}, u32[]{:S(2)}) collective-permute-start(bf16[3,128,128]{2,1,0:T(8,128)(2,1)S(1)} %collective-permute-done.24), channel_id=1, source_target_pairs={{0,1},{1,0},{2,3},{3,2},{4,5},{5,4},{6,7},{7,6},{8,9},{9,8},{10,11... | collective-permute-start | bytes 294920 | tf_op jit(solution)/shard_map/ppermute | solution.py:33

commit v18 on v14

--- a/solution.py
+++ b/solution.py
@@ -18,15 +18,17 @@
 def line_stage(x, wide, inner):
     lines = wide // inner
     if lines <= 4:
+        paired = (lines & (lines - 1)) == 0
         parts = [x[None]]
         for shift in range(1, lines):
             pairs = [
-                (d, ((d // inner + shift) % lines) * inner + d % inner) for d in range(wide)
+                (d, ((d // inner ^ shift) if paired else (d // inner + shift) % lines) * inner + d % inner)
+                for d in range(wide)
             ]
             parts.append(lax.ppermute(x, "wide", pairs)[None])
-        return parts, True
+        return parts, "paired" if paired else "shifted"
     groups = [[z * inner + k for z in range(lines)] for k in range(inner)]
-    return [lax.all_gather(x, "wide", axis=0, tiled=False, axis_index_groups=groups)], False
+    return [lax.all_gather(x, "wide", axis=0, tiled=False, axis_index_groups=groups)], "ordered"
 
 
 def swap(x, wide, mask):
@@ -56,7 +58,12 @@
     pieces = slab_stage(parts, wide, inner, early, split)
     me = lax.axis_index("wide")
     line = np.arange(lines, dtype=np.int32)
-    source_line = (me // inner - line) % lines if shifted else jnp.asarray(line)
+    if shifted == "paired":
+        source_line = jnp.bitwise_xor(me // inner, jnp.asarray(line))
+    elif shifted == "shifted":
+        source_line = (me // inner - line) % lines
+    else:
+        source_line = jnp.asarray(line)
     masks = np.arange(inner, dtype=np.int32)
     blocks = (
         source_line[None, :] * inner

time: 59.8 us -> 61.8 us (1.033)
  waiting for transfers between devices: 15.1 us -> 19.6 us
  starting transfers between devices: 28 us -> 26.1 us
    ppermute x9, waiting for transfers between devices: 0.94 us -> 5.62 us  [line_stage(): parts.append(lax.ppermute(x, 'wide', pairs)[None])]
    ppermute x9, starting transfers between devices: 16.9 us -> 14.6 us  [line_stage(): parts.append(lax.ppermute(x, 'wide', pairs)[None])]
  transfers between devices with their start and end apart: 26 -> 26, of which waited for: 9 -> 10; matrix products, arithmetic and copies ran while one was open for 20% -> 19% of each run, Pallas kernels for 0% -> 0%
where the time goes in v18:
time: 61.8 us; the launch traced here: 61.6 us
  starting transfers between devices  26.1 us (42%)
  waiting for transfers between devices  19.6 us (32%)
  matrix products  8.02 us (13%)
  other arithmetic  3.8 us (6%)
  local copies, waits for them, and re-layouts  3.64 us (6%)
    ppermute x9, starting transfers between devices, line_stage(): parts.append(lax.ppermute(x, 'wide', pairs)[None])  14.6 us
    ppermute x17, waiting for transfers between devices, swap(): return lax.ppermute(x, 'wide', [(d, d ^ mask) for d in range(wide)])  14 us
    ppermute x17, starting transfers between devices, swap(): return lax.ppermute(x, 'wide', [(d, d ^ mask) for d in range(wide)])  11.5 us
    dot_general x27, matrix products, rowwise(): return jnp.einsum(spec, tiles, currents, preferred_element_type=jnp.float32)  7.16 us
    ppermute x9, waiting for transfers between devices, line_stage(): parts.append(lax.ppermute(x, 'wide', pairs)[None])  5.62 us
    sort x1, other arithmetic, per_device(): column_of_block = jnp.argsort(block_owner)  1.9 us
  transfers between devices with their start and end apart: 26, of which 10 were waited for; matrix products, arithmetic and copies ran while one was open for 19% of the time, Pallas kernels for 0%

profile of v18, /device:TPU:0, one launch (start us, length us, event | category | flops | bytes accessed | tf_op | source)
XLA Modules:
  0.0 61.6 jit_solution(8178240546411066041)
XLA Ops:
  0.0 3.0 %collective-permute-start = (bf16[4,128,128]{2,1,0:T(8,128)(2,1)}, bf16[4,128,128]{2,1,0:T(8,128)(2,1)S(1)}, u32[]{:S(2)}, u32[]{:S(2)}) collective-permute-start(bf16[4,128,128]{2,1,0:T(8,128)(2,1)} %param.19), channel_id=1, source_target_pairs={{0,4},{1,5},{2,6},{3,7},{4,0},{5,1},{6,2},{7,3},{8,12},{9,13},{10,... | collective-permute-start | bytes 393224 | tf_op jit(solution)/shard_map/ppermute | solution.py:28
  3.0 2.6 %collective-permute-start.1 = (bf16[4,128,128]{2,1,0:T(8,128)(2,1)}, bf16[4,128,128]{2,1,0:T(8,128)(2,1)S(1)}, u32[]{:S(2)}, u32[]{:S(2)}) collective-permute-start(bf16[4,128,128]{2,1,0:T(8,128)(2,1)} %param.19), channel_id=1, source_target_pairs={{0,8},{1,9},{2,10},{3,11},{4,12},{5,13},{6,14},{7,15},{8,0},{9,1},... | collective-permute-start | bytes 393224 | tf_op jit(solution)/shard_map/ppermute | solution.py:28
  5.6 1.7 %collective-permute-start.4 = (bf16[1,4,128,128]{3,2,1,0:T(8,128)(2,1)}, bf16[1,4,128,128]{3,2,1,0:T(8,128)(2,1)S(1)}, u32[]{:S(2)}, u32[]{:S(2)}) collective-permute-start(bf16[1,4,128,128]{3,2,1,0:T(8,128)(2,1)} %bitcast.320), channel_id=1, source_target_pairs={{0,2},{1,3},{2,0},{3,1},{4,6},{5,7},{6,4},{7,5},{8,10},{9,11},{10,... | collective-permute-start | bytes 393224 | tf_op jit(solution)/shard_map/ppermute | solution.py:35
  7.5 1.9 %sort.17 = (s32[16]{0:T(128)}, s32[16]{0:T(128)S(1)}) sort(s32[16]{0:T(128)} %param.18, s32[16]{0:T(128)S(1)} %iota.5), dimensions={0}, to_apply=%region_0.0 | sort | flops 64 | bytes 256 | tf_op jit(solution)/shard_map/jit(argsort)/sort | solution.py:101
  9.4 0.7 %gather_fusion = s32[16]{0:T(128)S(1)} fusion(s32[16]{0:T(128)S(1)} %get-tuple-element.8, s32[1024]{0:T(1024)S(1)} %pad_clamp_fusion.1), kind=kCustom, calls=%fused_computation.clone | custom fusion | bytes 192 | tf_op jit(solution)/shard_map/jit(_take)/gather | solution.py:76
  10.1 0.8 %copy.17 = s32[16,2]{1,0:T(8,128)S(1)} copy(s32[16,2]{0,1:T(2,128)} %bitcast.330) | data formatting | bytes 256 | tf_op jit(solution)/shard_map/squeeze | solution.py:78
  10.9 0.7 %gather_fusion.2 = bf16[16,2,128,128]{3,2,1,0:T(8,128)(2,1)S(1)} fusion(bf16[16,2,128,128]{3,2,1,0:T(8,128)(2,1)S(1)} %bitcast.299, s32[1024]{0:T(1024)S(1)} %pad_clamp_fusion), kind=kCustom, calls=%fused_computation.2.clone | custom fusion | bytes 2097216 | tf_op jit(solution)/shard_map/jit(_take)/gather | solution.py:77
  11.7 0.6 gather_fusion.1
  12.7 0.3 bitcast_select_fusion.3
  13.2 3.0 %collective-permute-done.1 = bf16[4,128,128]{2,1,0:T(8,128)(2,1)S(1)} collective-permute-done((bf16[4,128,128]{2,1,0:T(8,128)(2,1)}, bf16[4,128,128]{2,1,0:T(8,128)(2,1)S(1)}, u32[]{:S(2)}, u32[]{:S(2)}) %collective-permute-start.1) | collective-permute-done | bytes 131104 | tf_op jit(solution)/shard_map/ppermute | solution.py:28
  16.3 1.6 %collective-permute-start.5 = (bf16[1,4,128,128]{3,2,1,0:T(8,128)(2,1)S(1)}, bf16[1,4,128,128]{3,2,1,0:T(8,128)(2,1)S(1)}, u32[]{:S(2)}, u32[]{:S(2)}) collective-permute-start(bf16[1,4,128,128]{3,2,1,0:T(8,128)(2,1)S(1)} %bitcast.324), channel_id=1, source_target_pairs={{0,2},{1,3},{2,0},{3,1},{4,6},{5,7},{6,4},{7,5},{8,10},{9,11},{10,... | collective-permute-start | bytes 393224 | tf_op jit(solution)/shard_map/ppermute | solution.py:35
  17.9 0.5 collective-permute-start.6
  18.4 0.3 convolution_bitcast_fusion.5
  18.7 0.3 collective-permute-start.7
  19.3 2.4 %collective-permute-done.5 = bf16[1,4,128,128]{3,2,1,0:T(8,128)(2,1)S(1)} collective-permute-done((bf16[1,4,128,128]{3,2,1,0:T(8,128)(2,1)S(1)}, bf16[1,4,128,128]{3,2,1,0:T(8,128)(2,1)S(1)}, u32[]{:S(2)}, u32[]{:S(2)}) %collective-permute-start.5) | collective-permute-done | bytes 131104 | tf_op jit(solution)/shard_map/ppermute | solution.py:35
  22.4 0.7 %collective-permute-done.8 = bf16[1,4,128,128]{3,2,1,0:T(8,128)(2,1)S(1)} collective-permute-done((bf16[1,4,128,128]{3,2,1,0:T(8,128)(2,1)S(1)}, bf16[1,4,128,128]{3,2,1,0:T(8,128)(2,1)S(1)}, u32[]{:S(2)}, u32[]{:S(2)}) %collective-permute-start.8) | collective-permute-done | bytes 131104 | tf_op jit(solution)/shard_map/ppermute | solution.py:35
  23.5 3.4 %collective-permute-done.6 = bf16[2,4,128,128]{3,2,1,0:T(8,128)(2,1)S(1)} collective-permute-done((bf16[2,4,128,128]{3,2,1,0:T(8,128)(2,1)S(1)}, bf16[2,4,128,128]{3,2,1,0:T(8,128)(2,1)S(1)}, u32[]{:S(2)}, u32[]{:S(2)}) %collective-permute-start.6) | collective-permute-done | bytes 262176 | tf_op jit(solution)/shard_map/ppermute | solution.py:35
  27.7 0.3 convolution_bitcast_fusion.3
  28.0 0.3 convolution_bitcast_fusion
  28.3 0.4 fusion.26
  28.9 0.3 convolution_bitcast_fusion.2
  29.2 0.6 copy-done.2
  30.1 0.3 constant_dynamic-update-slice_fusion.8
  30.4 2.0 %collective-permute-start.10 = (bf16[128,128]{1,0:T(8,128)(2,1)S(1)}, bf16[128,128]{1,0:T(8,128)(2,1)S(1)}, u32[]{:S(2)}, u32[]{:S(2)}) collective-permute-start(bf16[128,128]{1,0:T(8,128)(2,1)S(1)} %get-tuple-element.21), channel_id=1, source_target_pairs={{0,4},{1,5},{2,6},{3,7},{4,0},{5,1},{6,2},{7,3},{8,12},{9,13},{10,... | collective-permute-start | bytes 98312 | tf_op jit(solution)/shard_map/ppermute | solution.py:28
  32.4 1.1 %collective-permute-start.11 = (bf16[128,128]{1,0:T(8,128)(2,1)S(1)}, bf16[128,128]{1,0:T(8,128)(2,1)S(1)}, u32[]{:S(2)}, u32[]{:S(2)}) collective-permute-start(bf16[128,128]{1,0:T(8,128)(2,1)S(1)} %get-tuple-element.21), channel_id=1, source_target_pairs={{0,8},{1,9},{2,10},{3,11},{4,12},{5,13},{6,14},{7,15},{8,0},{9,1},... | collective-permute-start | bytes 98312 | tf_op jit(solution)/shard_map/ppermute | solution.py:28
  33.5 1.4 %collective-permute-start.12 = (bf16[128,128]{1,0:T(8,128)(2,1)S(1)}, bf16[128,128]{1,0:T(8,128)(2,1)S(1)}, u32[]{:S(2)}, u32[]{:S(2)}) collective-permute-start(bf16[128,128]{1,0:T(8,128)(2,1)S(1)} %get-tuple-element.21), channel_id=1, source_target_pairs={{0,12},{1,13},{2,14},{3,15},{4,8},{5,9},{6,10},{7,11},{8,4},{9,5},... | collective-permute-start | bytes 98312 | tf_op jit(solution)/shard_map/ppermute | solution.py:28
  34.9 1.5 %collective-permute-start.14 = (bf16[1,128,128]{2,1,0:T(8,128)(2,1)S(1)}, bf16[1,128,128]{2,1,0:T(8,128)(2,1)S(1)}, u32[]{:S(2)}, u32[]{:S(2)}) collective-permute-start(bf16[1,128,128]{2,1,0:T(8,128)(2,1)S(1)} %bitcast.326), channel_id=1, source_target_pairs={{0,2},{1,3},{2,0},{3,1},{4,6},{5,7},{6,4},{7,5},{8,10},{9,11},{10,... | collective-permute-start | bytes 98312 | tf_op jit(solution)/shard_map/ppermute | solution.py:35
  36.7 0.3 fusion.24
  36.9 0.3 fusion.25
  37.9 1.3 %collective-permute-done.12 = bf16[128,128]{1,0:T(8,128)(2,1)S(1)} collective-permute-done((bf16[128,128]{1,0:T(8,128)(2,1)S(1)}, bf16[128,128]{1,0:T(8,128)(2,1)S(1)}, u32[]{:S(2)}, u32[]{:S(2)}) %collective-permute-start.12) | collective-permute-done | bytes 32800 | tf_op jit(solution)/shard_map/ppermute | solution.py:28
  39.3 1.6 %collective-permute-start.15 = (bf16[3,128,128]{2,1,0:T(8,128)(2,1)S(1)}, bf16[3,128,128]{2,1,0:T(8,128)(2,1)S(1)}, u32[]{:S(2)}, u32[]{:S(2)}) collective-permute-start(bf16[3,128,128]{2,1,0:T(8,128)(2,1)S(1)} %pad_maximum_fusion.8), channel_id=1, source_target_pairs={{0,2},{1,3},{2,0},{3,1},{4,6},{5,7},{6,4},{7,5},{8,10},{9,11},{10,... | collective-permute-start | bytes 294920 | tf_op jit(solution)/shard_map/ppermute | solution.py:35
  40.9 0.6 collective-permute-start.16
  41.4 2.5 %collective-permute-done.15 = bf16[3,128,128]{2,1,0:T(8,128)(2,1)S(1)} collective-permute-done((bf16[3,128,128]{2,1,0:T(8,128)(2,1)S(1)}, bf16[3,128,128]{2,1,0:T(8,128)(2,1)S(1)}, u32[]{:S(2)}, u32[]{:S(2)}) %collective-permute-start.15) | collective-permute-done | bytes 98336 | tf_op jit(solution)/shard_map/ppermute | solution.py:35
  44.0 1.2 %collective-permute-done.17 = bf16[3,128,128]{2,1,0:T(8,128)(2,1)S(1)} collective-permute-done((bf16[3,128,128]{2,1,0:T(8,128)(2,1)S(1)}, bf16[3,128,128]{2,1,0:T(8,128)(2,1)S(1)}, u32[]{:S(2)}, u32[]{:S(2)}) %collective-permute-start.17) | collective-permute-done | bytes 98336 | tf_op jit(solution)/shard_map/ppermute | solution.py:35
  45.3 0.3 convolution_bitcast_fusion.11
  45.8 0.3 constant_dynamic-update-slice_fusion.17
  46.4 1.9 %collective-permute-start.19 = (bf16[128,128]{1,0:T(8,128)(2,1)S(1)}, bf16[128,128]{1,0:T(8,128)(2,1)S(1)}, u32[]{:S(2)}, u32[]{:S(2)}) collective-permute-start(bf16[128,128]{1,0:T(8,128)(2,1)S(1)} %get-tuple-element.19), channel_id=1, source_target_pairs={{0,8},{1,9},{2,10},{3,11},{4,12},{5,13},{6,14},{7,15},{8,0},{9,1},... | collective-permute-start | bytes 98312 | tf_op jit(solution)/shard_map/ppermute | solution.py:28
  48.3 2.3 %collective-permute-start.20 = (bf16[128,128]{1,0:T(8,128)(2,1)S(1)}, bf16[128,128]{1,0:T(8,128)(2,1)S(1)}, u32[]{:S(2)}, u32[]{:S(2)}) collective-permute-start(bf16[128,128]{1,0:T(8,128)(2,1)S(1)} %get-tuple-element.19), channel_id=1, source_target_pairs={{0,12},{1,13},{2,14},{3,15},{4,8},{5,9},{6,10},{7,11},{8,4},{9,5},... | collective-permute-start | bytes 98312 | tf_op jit(solution)/shard_map/ppermute | solution.py:28
  50.6 0.5 convolution_bitcast_fusion.9
  51.1 1.6 %collective-permute-start.22 = (bf16[1,128,128]{2,1,0:T(8,128)(2,1)S(1)}, bf16[1,128,128]{2,1,0:T(8,128)(2,1)S(1)}, u32[]{:S(2)}, u32[]{:S(2)}) collective-permute-start(bf16[1,128,128]{2,1,0:T(8,128)(2,1)S(1)} %bitcast.328), channel_id=1, source_target_pairs={{0,2},{1,3},{2,0},{3,1},{4,6},{5,7},{6,4},{7,5},{8,10},{9,11},{10,... | collective-permute-start | bytes 98312 | tf_op jit(solution)/shard_map/ppermute | solution.py:35
  52.7 1.3 %collective-permute-done.20 = bf16[128,128]{1,0:T(8,128)(2,1)S(1)} collective-permute-done((bf16[128,128]{1,0:T(8,128)(2,1)S(1)}, bf16[128,128]{1,0:T(8,128)(2,1)S(1)}, u32[]{:S(2)}, u32[]{:S(2)}) %collective-permute-start.20) | collective-permute-done | bytes 32800 | tf_op jit(solution)/shard_map/ppermute | solution.py:28
  54.1 1.6 %collective-permute-start.23 = (bf16[3,128,128]{2,1,0:T(8,128)(2,1)S(1)}, bf16[3,128,128]{2,1,0:T(8,128)(2,1)S(1)}, u32[]{:S(2)}, u32[]{:S(2)}) collective-permute-start(bf16[3,128,128]{2,1,0:T(8,128)(2,1)S(1)} %pad_maximum_fusion.9), channel_id=1, source_target_pairs={{0,2},{1,3},{2,0},{3,1},{4,6},{5,7},{6,4},{7,5},{8,10},{9,11},{10,... | collective-permute-start | bytes 294920 | tf_op jit(solution)/shard_map/ppermute | solution.py:35
  55.7 0.6 collective-permute-start.24
  56.2 2.5 %collective-permute-done.23 = bf16[3,128,128]{2,1,0:T(8,128)(2,1)S(1)} collective-permute-done((bf16[3,128,128]{2,1,0:T(8,128)(2,1)S(1)}, bf16[3,128,128]{2,1,0:T(8,128)(2,1)S(1)}, u32[]{:S(2)}, u32[]{:S(2)}) %collective-permute-start.23) | collective-permute-done | bytes 98336 | tf_op jit(solution)/shard_map/ppermute | solution.py:35
  58.8 1.2 %collective-permute-done.25 = bf16[3,128,128]{2,1,0:T(8,128)(2,1)S(1)} collective-permute-done((bf16[3,128,128]{2,1,0:T(8,128)(2,1)S(1)}, bf16[3,128,128]{2,1,0:T(8,128)(2,1)S(1)}, u32[]{:S(2)}, u32[]{:S(2)}) %collective-permute-start.25) | collective-permute-done | bytes 98336 | tf_op jit(solution)/shard_map/ppermute | solution.py:35
  60.1 0.3 convolution_bitcast_fusion.10
  60.6 0.3 convolution_bitcast_fusion.8
  60.9 0.7 %pad_maximum_fusion.5 = f32[3,128,128]{2,1,0:T(8,128)} fusion(f32[1,128,128]{2,1,0:T(8,128)S(1)} %bitcast.318, f32[1,128,128]{2,1,0:T(8,128)S(1)} %bitcast.319, f32[1,128,128]{2,1,0:T(8,128)S(1)} %convolution_bitcast_fusion.8), kind=kLoop, calls=%fused_computation.89 | loop fusion | flops 98304 | bytes 393216 | tf_op jit(solution)/shard_map/stack | solution.py:143
  (83 shorter events, 5.3 us)
Async XLA Ops:
  0.0 10.9 %copy-start = (bf16[1,16,2,128,128]{4,3,2,1,0:T(8,128)(2,1)S(1)}, bf16[1,16,2,128,128]{4,3,2,1,0:T(8,128)(2,1)}, u32[]{:S(2)}) copy-start(bf16[1,16,2,128,128]{4,3,2,1,0:T(8,128)(2,1)} %param.16) | copy-start | bytes 3145732
  0.0 16.2 %collective-permute-start = (bf16[4,128,128]{2,1,0:T(8,128)(2,1)}, bf16[4,128,128]{2,1,0:T(8,128)(2,1)S(1)}, u32[]{:S(2)}, u32[]{:S(2)}) collective-permute-start(bf16[4,128,128]{2,1,0:T(8,128)(2,1)} %param.19), channel_id=1, source_target_pairs={{0,4},{1,5},{2,6},{3,7},{4,0},{5,1},{6,2},{7,3},{8,12},{9,13},{10,... | collective-permute-start | bytes 393224 | tf_op jit(solution)/shard_map/ppermute | solution.py:28
  3.0 13.2 %collective-permute-start.1 = (bf16[4,128,128]{2,1,0:T(8,128)(2,1)}, bf16[4,128,128]{2,1,0:T(8,128)(2,1)S(1)}, u32[]{:S(2)}, u32[]{:S(2)}) collective-permute-start(bf16[4,128,128]{2,1,0:T(8,128)(2,1)} %param.19), channel_id=1, source_target_pairs={{0,8},{1,9},{2,10},{3,11},{4,12},{5,13},{6,14},{7,15},{8,0},{9,1},... | collective-permute-start | bytes 393224 | tf_op jit(solution)/shard_map/ppermute | solution.py:28
  5.6 10.6 %collective-permute-start.2 = (bf16[4,128,128]{2,1,0:T(8,128)(2,1)}, bf16[4,128,128]{2,1,0:T(8,128)(2,1)S(1)}, u32[]{:S(2)}, u32[]{:S(2)}) collective-permute-start(bf16[4,128,128]{2,1,0:T(8,128)(2,1)} %param.19), channel_id=1, source_target_pairs={{0,12},{1,13},{2,14},{3,15},{4,8},{5,9},{6,10},{7,11},{8,4},{9,5},... | collective-permute-start | bytes 393224 | tf_op jit(solution)/shard_map/ppermute | solution.py:28
  5.6 13.1 %collective-permute-start.4 = (bf16[1,4,128,128]{3,2,1,0:T(8,128)(2,1)}, bf16[1,4,128,128]{3,2,1,0:T(8,128)(2,1)S(1)}, u32[]{:S(2)}, u32[]{:S(2)}) collective-permute-start(bf16[1,4,128,128]{3,2,1,0:T(8,128)(2,1)} %bitcast.320), channel_id=1, source_target_pairs={{0,2},{1,3},{2,0},{3,1},{4,6},{5,7},{6,4},{7,5},{8,10},{9,11},{10,... | collective-permute-start | bytes 393224 | tf_op jit(solution)/shard_map/ppermute | solution.py:35
  13.0 3.2 %copy-start.3 = (bf16[4,128,128]{2,1,0:T(8,128)(2,1)S(1)}, bf16[4,128,128]{2,1,0:T(8,128)(2,1)}, u32[]{:S(2)}) copy-start(bf16[4,128,128]{2,1,0:T(8,128)(2,1)} %param.19) | copy-start | bytes 393220
  16.3 5.4 %collective-permute-start.5 = (bf16[1,4,128,128]{3,2,1,0:T(8,128)(2,1)S(1)}, bf16[1,4,128,128]{3,2,1,0:T(8,128)(2,1)S(1)}, u32[]{:S(2)}, u32[]{:S(2)}) collective-permute-start(bf16[1,4,128,128]{3,2,1,0:T(8,128)(2,1)S(1)} %bitcast.324), channel_id=1, source_target_pairs={{0,2},{1,3},{2,0},{3,1},{4,6},{5,7},{6,4},{7,5},{8,10},{9,11},{10,... | collective-permute-start | bytes 393224 | tf_op jit(solution)/shard_map/ppermute | solution.py:35
  17.9 10.1 %collective-permute-start.3 = (bf16[4,4,128,128]{3,2,1,0:T(8,128)(2,1)S(1)}, bf16[4,4,128,128]{3,2,1,0:T(8,128)(2,1)S(1)}, u32[]{:S(2)}, u32[]{:S(2)}) collective-permute-start(bf16[4,4,128,128]{3,2,1,0:T(8,128)(2,1)S(1)} %pad_maximum_fusion.3), channel_id=1, source_target_pairs={{0,1},{1,0},{2,3},{3,2},{4,5},{5,4},{6,7},{7,6},{8,9},{9,8},{10,11... | collective-permute-start | bytes 1572872 | tf_op jit(solution)/shard_map/ppermute | solution.py:35
  17.9 9.1 %collective-permute-start.6 = (bf16[2,4,128,128]{3,2,1,0:T(8,128)(2,1)S(1)}, bf16[2,4,128,128]{3,2,1,0:T(8,128)(2,1)S(1)}, u32[]{:S(2)}, u32[]{:S(2)}) collective-permute-start(bf16[2,4,128,128]{3,2,1,0:T(8,128)(2,1)S(1)} %pad_maximum_fusion.4), channel_id=1, source_target_pairs={{0,2},{1,3},{2,0},{3,1},{4,6},{5,7},{6,4},{7,5},{8,10},{9,11},{10,... | collective-permute-start | bytes 786440 | tf_op jit(solution)/shard_map/ppermute | solution.py:35
  18.7 10.5 %collective-permute-start.7 = (bf16[1,4,128,128]{3,2,1,0:T(8,128)(2,1)S(1)}, bf16[1,4,128,128]{3,2,1,0:T(8,128)(2,1)S(1)}, u32[]{:S(2)}, u32[]{:S(2)}) collective-permute-start(bf16[1,4,128,128]{3,2,1,0:T(8,128)(2,1)S(1)} %collective-permute-done.4), channel_id=1, source_target_pairs={{0,1},{1,0},{2,3},{3,2},{4,5},{5,4},{6,7},{7,6},{8,9},{9,8},{10,11... | collective-permute-start | bytes 393224 | tf_op jit(solution)/shard_map/ppermute | solution.py:35
  21.7 1.3 %collective-permute-start.8 = (bf16[1,4,128,128]{3,2,1,0:T(8,128)(2,1)S(1)}, bf16[1,4,128,128]{3,2,1,0:T(8,128)(2,1)S(1)}, u32[]{:S(2)}, u32[]{:S(2)}) collective-permute-start(bf16[1,4,128,128]{3,2,1,0:T(8,128)(2,1)S(1)} %collective-permute-done.5), channel_id=1, source_target_pairs={{0,1},{1,0},{2,3},{3,2},{4,5},{5,4},{6,7},{7,6},{8,9},{9,8},{10,11... | collective-permute-start | bytes 393224 | tf_op jit(solution)/shard_map/ppermute | solution.py:35
  27.0 2.0 %collective-permute-start.9 = (bf16[2,4,128,128]{3,2,1,0:T(8,128)(2,1)S(1)}, bf16[2,4,128,128]{3,2,1,0:T(8,128)(2,1)S(1)}, u32[]{:S(2)}, u32[]{:S(2)}) collective-permute-start(bf16[2,4,128,128]{3,2,1,0:T(8,128)(2,1)S(1)} %collective-permute-done.6), channel_id=1, source_target_pairs={{0,1},{1,0},{2,3},{3,2},{4,5},{5,4},{6,7},{7,6},{8,9},{9,8},{10,11... | collective-permute-start | bytes 786440 | tf_op jit(solution)/shard_map/ppermute | solution.py:35
  28.9 0.9 %copy-start.2 = (f32[3,128,128]{2,1,0:T(8,128)S(1)}, f32[3,128,128]{2,1,0:T(8,128)}, u32[]{:S(2)}) copy-start(f32[3,128,128]{2,1,0:T(8,128)} %param.20) | copy-start | bytes 589828
  29.2 0.9 %copy-start.1 = (f32[1,128,128]{2,1,0:T(8,128)S(1)}, f32[1,128,128]{2,1,0:T(8,128)}, u32[]{:S(2)}) copy-start(f32[1,128,128]{2,1,0:T(8,128)} %param.21) | copy-start | bytes 196612
  30.4 7.5 %collective-permute-start.10 = (bf16[128,128]{1,0:T(8,128)(2,1)S(1)}, bf16[128,128]{1,0:T(8,128)(2,1)S(1)}, u32[]{:S(2)}, u32[]{:S(2)}) collective-permute-start(bf16[128,128]{1,0:T(8,128)(2,1)S(1)} %get-tuple-element.21), channel_id=1, source_target_pairs={{0,4},{1,5},{2,6},{3,7},{4,0},{5,1},{6,2},{7,3},{8,12},{9,13},{10,... | collective-permute-start | bytes 98312 | tf_op jit(solution)/shard_map/ppermute | solution.py:28
  32.4 5.5 %collective-permute-start.11 = (bf16[128,128]{1,0:T(8,128)(2,1)S(1)}, bf16[128,128]{1,0:T(8,128)(2,1)S(1)}, u32[]{:S(2)}, u32[]{:S(2)}) collective-permute-start(bf16[128,128]{1,0:T(8,128)(2,1)S(1)} %get-tuple-element.21), channel_id=1, source_target_pairs={{0,8},{1,9},{2,10},{3,11},{4,12},{5,13},{6,14},{7,15},{8,0},{9,1},... | collective-permute-start | bytes 98312 | tf_op jit(solution)/shard_map/ppermute | solution.py:28
  33.5 5.7 %collective-permute-start.12 = (bf16[128,128]{1,0:T(8,128)(2,1)S(1)}, bf16[128,128]{1,0:T(8,128)(2,1)S(1)}, u32[]{:S(2)}, u32[]{:S(2)}) collective-permute-start(bf16[128,128]{1,0:T(8,128)(2,1)S(1)} %get-tuple-element.21), channel_id=1, source_target_pairs={{0,12},{1,13},{2,14},{3,15},{4,8},{5,9},{6,10},{7,11},{8,4},{9,5},... | collective-permute-start | bytes 98312 | tf_op jit(solution)/shard_map/ppermute | solution.py:28
  34.9 6.0 %collective-permute-start.14 = (bf16[1,128,128]{2,1,0:T(8,128)(2,1)S(1)}, bf16[1,128,128]{2,1,0:T(8,128)(2,1)S(1)}, u32[]{:S(2)}, u32[]{:S(2)}) collective-permute-start(bf16[1,128,128]{2,1,0:T(8,128)(2,1)S(1)} %bitcast.326), channel_id=1, source_target_pairs={{0,2},{1,3},{2,0},{3,1},{4,6},{5,7},{6,4},{7,5},{8,10},{9,11},{10,... | collective-permute-start | bytes 98312 | tf_op jit(solution)/shard_map/ppermute | solution.py:35
  39.3 4.7 %collective-permute-start.15 = (bf16[3,128,128]{2,1,0:T(8,128)(2,1)S(1)}, bf16[3,128,128]{2,1,0:T(8,128)(2,1)S(1)}, u32[]{:S(2)}, u32[]{:S(2)}) collective-permute-start(bf16[3,128,128]{2,1,0:T(8,128)(2,1)S(1)} %pad_maximum_fusion.8), channel_id=1, source_target_pairs={{0,2},{1,3},{2,0},{3,1},{4,6},{5,7},{6,4},{7,5},{8,10},{9,11},{10,... | collective-permute-start | bytes 294920 | tf_op jit(solution)/shard_map/ppermute | solution.py:35
  40.8 3.1 %collective-permute-start.13 = (bf16[4,128,128]{2,1,0:T(8,128)(2,1)S(1)}, bf16[4,128,128]{2,1,0:T(8,128)(2,1)S(1)}, u32[]{:S(2)}, u32[]{:S(2)}) collective-permute-start(bf16[4,128,128]{2,1,0:T(8,128)(2,1)S(1)} %pad_maximum_fusion.6), channel_id=1, source_target_pairs={{0,1},{1,0},{2,3},{3,2},{4,5},{5,4},{6,7},{7,6},{8,9},{9,8},{10,11... | collective-permute-start | bytes 393224 | tf_op jit(solution)/shard_map/ppermute | solution.py:35
  40.9 3.1 %collective-permute-start.16 = (bf16[1,128,128]{2,1,0:T(8,128)(2,1)S(1)}, bf16[1,128,128]{2,1,0:T(8,128)(2,1)S(1)}, u32[]{:S(2)}, u32[]{:S(2)}) collective-permute-start(bf16[1,128,128]{2,1,0:T(8,128)(2,1)S(1)} %collective-permute-done.14), channel_id=1, source_target_pairs={{0,1},{1,0},{2,3},{3,2},{4,5},{5,4},{6,7},{7,6},{8,9},{9,8},{10,11... | collective-permute-start | bytes 98312 | tf_op jit(solution)/shard_map/ppermute | solution.py:35
  43.9 1.3 %collective-permute-start.17 = (bf16[3,128,128]{2,1,0:T(8,128)(2,1)S(1)}, bf16[3,128,128]{2,1,0:T(8,128)(2,1)S(1)}, u32[]{:S(2)}, u32[]{:S(2)}) collective-permute-start(bf16[3,128,128]{2,1,0:T(8,128)(2,1)S(1)} %collective-permute-done.15), channel_id=1, source_target_pairs={{0,1},{1,0},{2,3},{3,2},{4,5},{5,4},{6,7},{7,6},{8,9},{9,8},{10,11... | collective-permute-start | bytes 294920 | tf_op jit(solution)/shard_map/ppermute | solution.py:35
  46.1 6.5 %collective-permute-start.18 = (bf16[128,128]{1,0:T(8,128)(2,1)S(1)}, bf16[128,128]{1,0:T(8,128)(2,1)S(1)}, u32[]{:S(2)}, u32[]{:S(2)}) collective-permute-start(bf16[128,128]{1,0:T(8,128)(2,1)S(1)} %get-tuple-element.19), channel_id=1, source_target_pairs={{0,4},{1,5},{2,6},{3,7},{4,0},{5,1},{6,2},{7,3},{8,12},{9,13},{10,... | collective-permute-start | bytes 98312 | tf_op jit(solution)/shard_map/ppermute | solution.py:28
  46.4 6.3 %collective-permute-start.19 = (bf16[128,128]{1,0:T(8,128)(2,1)S(1)}, bf16[128,128]{1,0:T(8,128)(2,1)S(1)}, u32[]{:S(2)}, u32[]{:S(2)}) collective-permute-start(bf16[128,128]{1,0:T(8,128)(2,1)S(1)} %get-tuple-element.19), channel_id=1, source_target_pairs={{0,8},{1,9},{2,10},{3,11},{4,12},{5,13},{6,14},{7,15},{8,0},{9,1},... | collective-permute-start | bytes 98312 | tf_op jit(solution)/shard_map/ppermute | solution.py:28
  48.3 5.7 %collective-permute-start.20 = (bf16[128,128]{1,0:T(8,128)(2,1)S(1)}, bf16[128,128]{1,0:T(8,128)(2,1)S(1)}, u32[]{:S(2)}, u32[]{:S(2)}) collective-permute-start(bf16[128,128]{1,0:T(8,128)(2,1)S(1)} %get-tuple-element.19), channel_id=1, source_target_pairs={{0,12},{1,13},{2,14},{3,15},{4,8},{5,9},{6,10},{7,11},{8,4},{9,5},... | collective-permute-start | bytes 98312 | tf_op jit(solution)/shard_map/ppermute | solution.py:28
  51.1 4.6 %collective-permute-start.22 = (bf16[1,128,128]{2,1,0:T(8,128)(2,1)S(1)}, bf16[1,128,128]{2,1,0:T(8,128)(2,1)S(1)}, u32[]{:S(2)}, u32[]{:S(2)}) collective-permute-start(bf16[1,128,128]{2,1,0:T(8,128)(2,1)S(1)} %bitcast.328), channel_id=1, source_target_pairs={{0,2},{1,3},{2,0},{3,1},{4,6},{5,7},{6,4},{7,5},{8,10},{9,11},{10,... | collective-permute-start | bytes 98312 | tf_op jit(solution)/shard_map/ppermute | solution.py:35
  54.1 4.7 %collective-permute-start.23 = (bf16[3,128,128]{2,1,0:T(8,128)(2,1)S(1)}, bf16[3,128,128]{2,1,0:T(8,128)(2,1)S(1)}, u32[]{:S(2)}, u32[]{:S(2)}) collective-permute-start(bf16[3,128,128]{2,1,0:T(8,128)(2,1)S(1)} %pad_maximum_fusion.9), channel_id=1, source_target_pairs={{0,2},{1,3},{2,0},{3,1},{4,6},{5,7},{6,4},{7,5},{8,10},{9,11},{10,... | collective-permute-start | bytes 294920 | tf_op jit(solution)/shard_map/ppermute | solution.py:35
  55.6 3.1 %collective-permute-start.21 = (bf16[4,128,128]{2,1,0:T(8,128)(2,1)S(1)}, bf16[4,128,128]{2,1,0:T(8,128)(2,1)S(1)}, u32[]{:S(2)}, u32[]{:S(2)}) collective-permute-start(bf16[4,128,128]{2,1,0:T(8,128)(2,1)S(1)} %pad_maximum_fusion.7), channel_id=1, source_target_pairs={{0,1},{1,0},{2,3},{3,2},{4,5},{5,4},{6,7},{7,6},{8,9},{9,8},{10,11... | collective-permute-start | bytes 393224 | tf_op jit(solution)/shard_map/ppermute | solution.py:35
  55.7 3.1 %collective-permute-start.24 = (bf16[1,128,128]{2,1,0:T(8,128)(2,1)S(1)}, bf16[1,128,128]{2,1,0:T(8,128)(2,1)S(1)}, u32[]{:S(2)}, u32[]{:S(2)}) collective-permute-start(bf16[1,128,128]{2,1,0:T(8,128)(2,1)S(1)} %collective-permute-done.22), channel_id=1, source_target_pairs={{0,1},{1,0},{2,3},{3,2},{4,5},{5,4},{6,7},{7,6},{8,9},{9,8},{10,11... | collective-permute-start | bytes 98312 | tf_op jit(solution)/shard_map/ppermute | solution.py:35
  58.7 1.3 %collective-permute-start.25 = (bf16[3,128,128]{2,1,0:T(8,128)(2,1)S(1)}, bf16[3,128,128]{2,1,0:T(8,128)(2,1)S(1)}, u32[]{:S(2)}, u32[]{:S(2)}) collective-permute-start(bf16[3,128,128]{2,1,0:T(8,128)(2,1)S(1)} %collective-permute-done.23), channel_id=1, source_target_pairs={{0,1},{1,0},{2,3},{3,2},{4,5},{5,4},{6,7},{7,6},{8,9},{9,8},{10,11... | collective-permute-start | bytes 294920 | tf_op jit(solution)/shard_map/ppermute | solution.py:35

commit v19 on v16

--- a/solution.py
+++ b/solution.py
@@ -40,10 +40,11 @@
     if early and len(parts) > 1:
         across = [swap(parts[0], wide, 2)]
         if split and len(parts) > 2:
-            chunks = parts[1:]
+            across.append(swap(jnp.concatenate(parts[1:-1]), wide, 2))
+            last, _ = lax.optimization_barrier((parts[-1], across[-1]))
+            across.append(swap(last, wide, 2))
         else:
-            chunks = [jnp.concatenate(parts[1:])]
-        across += [swap(chunk, wide, 2) for chunk in chunks]
+            across.append(swap(jnp.concatenate(parts[1:]), wide, 2))
         return [stack, swap(stack, wide, 1)] + across + [swap(piece, wide, 1) for piece in across]
     across = swap(stack, wide, 2)
     return [stack, swap(stack, wide, 1), across, swap(across, wide, 1)]

time: 62.8 us -> 62.8 us (level)
  waiting for transfers between devices: 13.9 us -> 19.3 us
  starting transfers between devices: 31.7 us -> 26.7 us
  matrix products: 9.06 us -> 8.02 us
    ppermute x19 -> x17, waiting for transfers between devices: 13.1 us -> 18.1 us  [swap(): return lax.ppermute(x, 'wide', [(d, d ^ mask) for d in range(wide)])]
    ppermute x9, starting transfers between devices: 18.9 us -> 16 us  [line_stage(): parts.append(lax.ppermute(x, 'wide', pairs)[None])]
    ppermute x19 -> x17, starting transfers between devices: 12.8 us -> 10.7 us  [swap(): return lax.ppermute(x, 'wide', [(d, d ^ mask) for d in range(wide)])]
    dot_general x33 -> x27, matrix products: 8.19 us -> 7.15 us  [rowwise(): return jnp.einsum(spec, tiles, currents, preferred_element_type=jnp.float32)]
  transfers between devices with their start and end apart: 28 -> 26, of which waited for: 10 -> 9; matrix products, arithmetic and copies ran while one was open for 21% -> 19% of each run, Pallas kernels for 0% -> 0%
where the time goes in v19:
time: 62.8 us; the launch traced here: 62.6 us
  starting transfers between devices  26.7 us (43%)
  waiting for transfers between devices  19.3 us (31%)
  matrix products  8.02 us (13%)
  local copies, waits for them, and re-layouts  4.23 us (7%)
  other arithmetic  3.8 us (6%)
    ppermute x17, waiting for transfers between devices, swap(): return lax.ppermute(x, 'wide', [(d, d ^ mask) for d in range(wide)])  18.1 us
    ppermute x9, starting transfers between devices, line_stage(): parts.append(lax.ppermute(x, 'wide', pairs)[None])  16 us
    ppermute x17, starting transfers between devices, swap(): return lax.ppermute(x, 'wide', [(d, d ^ mask) for d in range(wide)])  10.7 us
    dot_general x27, matrix products, rowwise(): return jnp.einsum(spec, tiles, currents, preferred_element_type=jnp.float32)  7.15 us
    sort x1, other arithmetic, per_device(): column_of_block = jnp.argsort(block_owner)  1.9 us
    unnamed x22, local copies, waits for them, and re-layouts  1.39 us
  transfers between devices with their start and end apart: 26, of which 9 were waited for; matrix products, arithmetic and copies ran while one was open for 19% of the time, Pallas kernels for 0%

profile of v19, /device:TPU:0, one launch (start us, length us, event | category | flops | bytes accessed | tf_op | source)
XLA Modules:
  0.0 62.6 jit_solution(2921314491719645)
XLA Ops:
  0.0 3.0 %collective-permute-start = (bf16[4,128,128]{2,1,0:T(8,128)(2,1)}, bf16[4,128,128]{2,1,0:T(8,128)(2,1)S(1)}, u32[]{:S(2)}, u32[]{:S(2)}) collective-permute-start(bf16[4,128,128]{2,1,0:T(8,128)(2,1)} %param.19), channel_id=1, source_target_pairs={{0,4},{1,5},{2,6},{3,7},{4,8},{5,9},{6,10},{7,11},{8,12},{9,13},{1... | collective-permute-start | bytes 393224 | tf_op jit(solution)/shard_map/ppermute | solution.py:26
  3.0 2.6 %collective-permute-start.1 = (bf16[4,128,128]{2,1,0:T(8,128)(2,1)}, bf16[4,128,128]{2,1,0:T(8,128)(2,1)S(1)}, u32[]{:S(2)}, u32[]{:S(2)}) collective-permute-start(bf16[4,128,128]{2,1,0:T(8,128)(2,1)} %param.19), channel_id=1, source_target_pairs={{0,8},{1,9},{2,10},{3,11},{4,12},{5,13},{6,14},{7,15},{8,0},{9,1},... | collective-permute-start | bytes 393224 | tf_op jit(solution)/shard_map/ppermute | solution.py:26
  5.6 1.3 %collective-permute-start.2 = (bf16[4,128,128]{2,1,0:T(8,128)(2,1)}, bf16[4,128,128]{2,1,0:T(8,128)(2,1)S(1)}, u32[]{:S(2)}, u32[]{:S(2)}) collective-permute-start(bf16[4,128,128]{2,1,0:T(8,128)(2,1)} %param.19), channel_id=1, source_target_pairs={{0,12},{1,13},{2,14},{3,15},{4,0},{5,1},{6,2},{7,3},{8,4},{9,5},{1... | collective-permute-start | bytes 393224 | tf_op jit(solution)/shard_map/ppermute | solution.py:26
  7.0 1.5 %collective-permute-start.4 = (bf16[1,4,128,128]{3,2,1,0:T(8,128)(2,1)}, bf16[1,4,128,128]{3,2,1,0:T(8,128)(2,1)S(1)}, u32[]{:S(2)}, u32[]{:S(2)}) collective-permute-start(bf16[1,4,128,128]{3,2,1,0:T(8,128)(2,1)} %bitcast.320), channel_id=1, source_target_pairs={{0,2},{1,3},{2,0},{3,1},{4,6},{5,7},{6,4},{7,5},{8,10},{9,11},{10,... | collective-permute-start | bytes 393224 | tf_op jit(solution)/shard_map/ppermute | solution.py:33
  8.7 1.9 %sort.17 = (s32[16]{0:T(128)}, s32[16]{0:T(128)S(1)}) sort(s32[16]{0:T(128)} %param.18, s32[16]{0:T(128)S(1)} %iota.5), dimensions={0}, to_apply=%region_0.0 | sort | flops 64 | bytes 256 | tf_op jit(solution)/shard_map/jit(argsort)/sort | solution.py:95
  10.6 0.7 %gather_fusion = s32[16]{0:T(128)S(1)} fusion(s32[16]{0:T(128)S(1)} %get-tuple-element.10, s32[1024]{0:T(1024)S(1)} %pad_clamp_fusion.1), kind=kCustom, calls=%fused_computation.clone | custom fusion | bytes 192 | tf_op jit(solution)/shard_map/jit(_take)/gather | solution.py:70
  11.3 0.8 %copy.17 = s32[16,2]{1,0:T(8,128)S(1)} copy(s32[16,2]{0,1:T(2,128)} %bitcast.330) | data formatting | bytes 256 | tf_op jit(solution)/shard_map/squeeze | solution.py:72
  12.0 0.7 %gather_fusion.2 = bf16[16,2,128,128]{3,2,1,0:T(8,128)(2,1)S(1)} fusion(bf16[16,2,128,128]{3,2,1,0:T(8,128)(2,1)S(1)} %bitcast.299, s32[1024]{0:T(1024)S(1)} %pad_clamp_fusion), kind=kCustom, calls=%fused_computation.2.clone | custom fusion | bytes 2097216 | tf_op jit(solution)/shard_map/jit(_take)/gather | solution.py:71
  12.8 0.6 gather_fusion.1
  13.9 0.3 bitcast_select_fusion.3
  14.5 0.5 copy-done.3
  15.2 1.1 %collective-permute-start.5 = (bf16[2,4,128,128]{3,2,1,0:T(8,128)(2,1)S(1)}, bf16[2,4,128,128]{3,2,1,0:T(8,128)(2,1)S(1)}, u32[]{:S(2)}, u32[]{:S(2)}) collective-permute-start(bf16[2,4,128,128]{3,2,1,0:T(8,128)(2,1)S(1)} %pad_maximum_fusion.4), channel_id=1, source_target_pairs={{0,2},{1,3},{2,0},{3,1},{4,6},{5,7},{6,4},{7,5},{8,10},{9,11},{10,... | collective-permute-start | bytes 786440 | tf_op jit(solution)/shard_map/ppermute | solution.py:33
  16.3 0.3 convolution_bitcast_fusion.7
  16.8 0.3 convolution_bitcast_fusion.5
  17.1 6.8 %collective-permute-done.5 = bf16[2,4,128,128]{3,2,1,0:T(8,128)(2,1)S(1)} collective-permute-done((bf16[2,4,128,128]{3,2,1,0:T(8,128)(2,1)S(1)}, bf16[2,4,128,128]{3,2,1,0:T(8,128)(2,1)S(1)}, u32[]{:S(2)}, u32[]{:S(2)}) %collective-permute-start.5) | collective-permute-done | bytes 262176 | tf_op jit(solution)/shard_map/ppermute | solution.py:33
  23.9 1.0 %collective-permute-start.6 = (bf16[1,4,128,128]{3,2,1,0:T(8,128)(2,1)S(1)}, bf16[1,4,128,128]{3,2,1,0:T(8,128)(2,1)S(1)}, u32[]{:S(2)}, u32[]{:S(2)}) collective-permute-start(bf16[1,4,128,128]{3,2,1,0:T(8,128)(2,1)S(1)} %bitcast.324), channel_id=1, source_target_pairs={{0,2},{1,3},{2,0},{3,1},{4,6},{5,7},{6,4},{7,5},{8,10},{9,11},{10,... | collective-permute-start | bytes 393224 | tf_op jit(solution)/shard_map/ppermute | solution.py:33
  24.9 0.3 convolution_bitcast_fusion.3
  25.8 3.2 %collective-permute-done.6 = bf16[1,4,128,128]{3,2,1,0:T(8,128)(2,1)S(1)} collective-permute-done((bf16[1,4,128,128]{3,2,1,0:T(8,128)(2,1)S(1)}, bf16[1,4,128,128]{3,2,1,0:T(8,128)(2,1)S(1)}, u32[]{:S(2)}, u32[]{:S(2)}) %collective-permute-start.6) | collective-permute-done | bytes 131104 | tf_op jit(solution)/shard_map/ppermute | solution.py:33
  29.7 0.3 convolution_bitcast_fusion
  30.0 0.4 fusion.26
  30.6 0.3 convolution_bitcast_fusion.2
  31.2 0.7 %copy-done.2 = f32[3,128,128]{2,1,0:T(8,128)S(1)} copy-done((f32[3,128,128]{2,1,0:T(8,128)S(1)}, f32[3,128,128]{2,1,0:T(8,128)}, u32[]{:S(2)}) %copy-start.2) | copy-done | bytes 196632
  32.1 0.3 constant_dynamic-update-slice_fusion.8
  32.4 2.8 %collective-permute-start.10 = (bf16[128,128]{1,0:T(8,128)(2,1)S(1)}, bf16[128,128]{1,0:T(8,128)(2,1)S(1)}, u32[]{:S(2)}, u32[]{:S(2)}) collective-permute-start(bf16[128,128]{1,0:T(8,128)(2,1)S(1)} %get-tuple-element.23), channel_id=1, source_target_pairs={{0,4},{1,5},{2,6},{3,7},{4,8},{5,9},{6,10},{7,11},{8,12},{9,13},{1... | collective-permute-start | bytes 98312 | tf_op jit(solution)/shard_map/ppermute | solution.py:26
  35.1 1.7 %collective-permute-start.11 = (bf16[128,128]{1,0:T(8,128)(2,1)S(1)}, bf16[128,128]{1,0:T(8,128)(2,1)S(1)}, u32[]{:S(2)}, u32[]{:S(2)}) collective-permute-start(bf16[128,128]{1,0:T(8,128)(2,1)S(1)} %get-tuple-element.23), channel_id=1, source_target_pairs={{0,8},{1,9},{2,10},{3,11},{4,12},{5,13},{6,14},{7,15},{8,0},{9,1},... | collective-permute-start | bytes 98312 | tf_op jit(solution)/shard_map/ppermute | solution.py:26
  36.8 0.8 %collective-permute-start.12 = (bf16[128,128]{1,0:T(8,128)(2,1)S(1)}, bf16[128,128]{1,0:T(8,128)(2,1)S(1)}, u32[]{:S(2)}, u32[]{:S(2)}) collective-permute-start(bf16[128,128]{1,0:T(8,128)(2,1)S(1)} %get-tuple-element.23), channel_id=1, source_target_pairs={{0,12},{1,13},{2,14},{3,15},{4,0},{5,1},{6,2},{7,3},{8,4},{9,5},{1... | collective-permute-start | bytes 98312 | tf_op jit(solution)/shard_map/ppermute | solution.py:26
  37.6 1.5 %collective-permute-start.14 = (bf16[1,128,128]{2,1,0:T(8,128)(2,1)S(1)}, bf16[1,128,128]{2,1,0:T(8,128)(2,1)S(1)}, u32[]{:S(2)}, u32[]{:S(2)}) collective-permute-start(bf16[1,128,128]{2,1,0:T(8,128)(2,1)S(1)} %bitcast.326), channel_id=1, source_target_pairs={{0,2},{1,3},{2,0},{3,1},{4,6},{5,7},{6,4},{7,5},{8,10},{9,11},{10,... | collective-permute-start | bytes 98312 | tf_op jit(solution)/shard_map/ppermute | solution.py:33
  39.8 0.3 fusion.24
  40.1 0.3 fusion.25
  41.1 1.2 %collective-permute-start.15 = (bf16[3,128,128]{2,1,0:T(8,128)(2,1)S(1)}, bf16[3,128,128]{2,1,0:T(8,128)(2,1)S(1)}, u32[]{:S(2)}, u32[]{:S(2)}) collective-permute-start(bf16[3,128,128]{2,1,0:T(8,128)(2,1)S(1)} %pad_maximum_fusion.8), channel_id=1, source_target_pairs={{0,2},{1,3},{2,0},{3,1},{4,6},{5,7},{6,4},{7,5},{8,10},{9,11},{10,... | collective-permute-start | bytes 294920 | tf_op jit(solution)/shard_map/ppermute | solution.py:33
  42.4 0.6 collective-permute-start.16
  43.0 2.8 %collective-permute-done.15 = bf16[3,128,128]{2,1,0:T(8,128)(2,1)S(1)} collective-permute-done((bf16[3,128,128]{2,1,0:T(8,128)(2,1)S(1)}, bf16[3,128,128]{2,1,0:T(8,128)(2,1)S(1)}, u32[]{:S(2)}, u32[]{:S(2)}) %collective-permute-start.15) | collective-permute-done | bytes 98336 | tf_op jit(solution)/shard_map/ppermute | solution.py:33
  45.9 1.2 %collective-permute-done.17 = bf16[3,128,128]{2,1,0:T(8,128)(2,1)S(1)} collective-permute-done((bf16[3,128,128]{2,1,0:T(8,128)(2,1)S(1)}, bf16[3,128,128]{2,1,0:T(8,128)(2,1)S(1)}, u32[]{:S(2)}, u32[]{:S(2)}) %collective-permute-start.17) | collective-permute-done | bytes 98336 | tf_op jit(solution)/shard_map/ppermute | solution.py:33
  47.1 0.3 convolution_bitcast_fusion.11
  47.7 0.3 constant_dynamic-update-slice_fusion.17
  48.0 1.3 %collective-permute-start.18 = (bf16[128,128]{1,0:T(8,128)(2,1)S(1)}, bf16[128,128]{1,0:T(8,128)(2,1)S(1)}, u32[]{:S(2)}, u32[]{:S(2)}) collective-permute-start(bf16[128,128]{1,0:T(8,128)(2,1)S(1)} %get-tuple-element.21), channel_id=1, source_target_pairs={{0,4},{1,5},{2,6},{3,7},{4,8},{5,9},{6,10},{7,11},{8,12},{9,13},{1... | collective-permute-start | bytes 98312 | tf_op jit(solution)/shard_map/ppermute | solution.py:26
  49.3 1.5 %collective-permute-start.19 = (bf16[128,128]{1,0:T(8,128)(2,1)S(1)}, bf16[128,128]{1,0:T(8,128)(2,1)S(1)}, u32[]{:S(2)}, u32[]{:S(2)}) collective-permute-start(bf16[128,128]{1,0:T(8,128)(2,1)S(1)} %get-tuple-element.21), channel_id=1, source_target_pairs={{0,8},{1,9},{2,10},{3,11},{4,12},{5,13},{6,14},{7,15},{8,0},{9,1},... | collective-permute-start | bytes 98312 | tf_op jit(solution)/shard_map/ppermute | solution.py:26
  50.8 1.1 %collective-permute-start.20 = (bf16[128,128]{1,0:T(8,128)(2,1)S(1)}, bf16[128,128]{1,0:T(8,128)(2,1)S(1)}, u32[]{:S(2)}, u32[]{:S(2)}) collective-permute-start(bf16[128,128]{1,0:T(8,128)(2,1)S(1)} %get-tuple-element.21), channel_id=1, source_target_pairs={{0,12},{1,13},{2,14},{3,15},{4,0},{5,1},{6,2},{7,3},{8,4},{9,5},{1... | collective-permute-start | bytes 98312 | tf_op jit(solution)/shard_map/ppermute | solution.py:26
  51.9 0.5 convolution_bitcast_fusion.9
  52.4 1.6 %collective-permute-start.22 = (bf16[1,128,128]{2,1,0:T(8,128)(2,1)S(1)}, bf16[1,128,128]{2,1,0:T(8,128)(2,1)S(1)}, u32[]{:S(2)}, u32[]{:S(2)}) collective-permute-start(bf16[1,128,128]{2,1,0:T(8,128)(2,1)S(1)} %bitcast.328), channel_id=1, source_target_pairs={{0,2},{1,3},{2,0},{3,1},{4,6},{5,7},{6,4},{7,5},{8,10},{9,11},{10,... | collective-permute-start | bytes 98312 | tf_op jit(solution)/shard_map/ppermute | solution.py:33
  53.9 0.8 %collective-permute-done.19 = bf16[128,128]{1,0:T(8,128)(2,1)S(1)} collective-permute-done((bf16[128,128]{1,0:T(8,128)(2,1)S(1)}, bf16[128,128]{1,0:T(8,128)(2,1)S(1)}, u32[]{:S(2)}, u32[]{:S(2)}) %collective-permute-start.19) | collective-permute-done | bytes 32800 | tf_op jit(solution)/shard_map/ppermute | solution.py:26
  55.0 1.3 %collective-permute-start.23 = (bf16[3,128,128]{2,1,0:T(8,128)(2,1)S(1)}, bf16[3,128,128]{2,1,0:T(8,128)(2,1)S(1)}, u32[]{:S(2)}, u32[]{:S(2)}) collective-permute-start(bf16[3,128,128]{2,1,0:T(8,128)(2,1)S(1)} %pad_maximum_fusion.9), channel_id=1, source_target_pairs={{0,2},{1,3},{2,0},{3,1},{4,6},{5,7},{6,4},{7,5},{8,10},{9,11},{10,... | collective-permute-start | bytes 294920 | tf_op jit(solution)/shard_map/ppermute | solution.py:33
  56.4 0.6 collective-permute-start.24
  57.0 2.8 %collective-permute-done.23 = bf16[3,128,128]{2,1,0:T(8,128)(2,1)S(1)} collective-permute-done((bf16[3,128,128]{2,1,0:T(8,128)(2,1)S(1)}, bf16[3,128,128]{2,1,0:T(8,128)(2,1)S(1)}, u32[]{:S(2)}, u32[]{:S(2)}) %collective-permute-start.23) | collective-permute-done | bytes 98336 | tf_op jit(solution)/shard_map/ppermute | solution.py:33
  59.8 1.2 %collective-permute-done.25 = bf16[3,128,128]{2,1,0:T(8,128)(2,1)S(1)} collective-permute-done((bf16[3,128,128]{2,1,0:T(8,128)(2,1)S(1)}, bf16[3,128,128]{2,1,0:T(8,128)(2,1)S(1)}, u32[]{:S(2)}, u32[]{:S(2)}) %collective-permute-start.25) | collective-permute-done | bytes 98336 | tf_op jit(solution)/shard_map/ppermute | solution.py:33
  61.1 0.3 convolution_bitcast_fusion.10
  61.6 0.3 convolution_bitcast_fusion.8
  61.9 0.7 %pad_maximum_fusion.5 = f32[3,128,128]{2,1,0:T(8,128)} fusion(f32[1,128,128]{2,1,0:T(8,128)S(1)} %bitcast.318, f32[1,128,128]{2,1,0:T(8,128)S(1)} %bitcast.319, f32[1,128,128]{2,1,0:T(8,128)S(1)} %convolution_bitcast_fusion.8), kind=kLoop, calls=%fused_computation.89 | loop fusion | flops 98304 | bytes 393216 | tf_op jit(solution)/shard_map/stack | solution.py:137
  (83 shorter events, 5.6 us)
Async XLA Ops:
  0.0 12.0 %copy-start = (bf16[1,16,2,128,128]{4,3,2,1,0:T(8,128)(2,1)S(1)}, bf16[1,16,2,128,128]{4,3,2,1,0:T(8,128)(2,1)}, u32[]{:S(2)}) copy-start(bf16[1,16,2,128,128]{4,3,2,1,0:T(8,128)(2,1)} %param.16) | copy-start | bytes 3145732
  0.0 14.3 %collective-permute-start = (bf16[4,128,128]{2,1,0:T(8,128)(2,1)}, bf16[4,128,128]{2,1,0:T(8,128)(2,1)S(1)}, u32[]{:S(2)}, u32[]{:S(2)}) collective-permute-start(bf16[4,128,128]{2,1,0:T(8,128)(2,1)} %param.19), channel_id=1, source_target_pairs={{0,4},{1,5},{2,6},{3,7},{4,8},{5,9},{6,10},{7,11},{8,12},{9,13},{1... | collective-permute-start | bytes 393224 | tf_op jit(solution)/shard_map/ppermute | solution.py:26
  3.0 11.4 %collective-permute-start.1 = (bf16[4,128,128]{2,1,0:T(8,128)(2,1)}, bf16[4,128,128]{2,1,0:T(8,128)(2,1)S(1)}, u32[]{:S(2)}, u32[]{:S(2)}) collective-permute-start(bf16[4,128,128]{2,1,0:T(8,128)(2,1)} %param.19), channel_id=1, source_target_pairs={{0,8},{1,9},{2,10},{3,11},{4,12},{5,13},{6,14},{7,15},{8,0},{9,1},... | collective-permute-start | bytes 393224 | tf_op jit(solution)/shard_map/ppermute | solution.py:26
  5.6 8.9 %collective-permute-start.2 = (bf16[4,128,128]{2,1,0:T(8,128)(2,1)}, bf16[4,128,128]{2,1,0:T(8,128)(2,1)S(1)}, u32[]{:S(2)}, u32[]{:S(2)}) collective-permute-start(bf16[4,128,128]{2,1,0:T(8,128)(2,1)} %param.19), channel_id=1, source_target_pairs={{0,12},{1,13},{2,14},{3,15},{4,0},{5,1},{6,2},{7,3},{8,4},{9,5},{1... | collective-permute-start | bytes 393224 | tf_op jit(solution)/shard_map/ppermute | solution.py:26
  7.0 9.6 %collective-permute-start.4 = (bf16[1,4,128,128]{3,2,1,0:T(8,128)(2,1)}, bf16[1,4,128,128]{3,2,1,0:T(8,128)(2,1)S(1)}, u32[]{:S(2)}, u32[]{:S(2)}) collective-permute-start(bf16[1,4,128,128]{3,2,1,0:T(8,128)(2,1)} %bitcast.320), channel_id=1, source_target_pairs={{0,2},{1,3},{2,0},{3,1},{4,6},{5,7},{6,4},{7,5},{8,10},{9,11},{10,... | collective-permute-start | bytes 393224 | tf_op jit(solution)/shard_map/ppermute | solution.py:33
  14.1 0.9 %copy-start.3 = (bf16[4,128,128]{2,1,0:T(8,128)(2,1)S(1)}, bf16[4,128,128]{2,1,0:T(8,128)(2,1)}, u32[]{:S(2)}) copy-start(bf16[4,128,128]{2,1,0:T(8,128)(2,1)} %param.19) | copy-start | bytes 393220
  15.1 14.5 %collective-permute-start.3 = (bf16[4,4,128,128]{3,2,1,0:T(8,128)(2,1)S(1)}, bf16[4,4,128,128]{3,2,1,0:T(8,128)(2,1)S(1)}, u32[]{:S(2)}, u32[]{:S(2)}) collective-permute-start(bf16[4,4,128,128]{3,2,1,0:T(8,128)(2,1)S(1)} %pad_maximum_fusion.3), channel_id=1, source_target_pairs={{0,1},{1,0},{2,3},{3,2},{4,5},{5,4},{6,7},{7,6},{8,9},{9,8},{10,11... | collective-permute-start | bytes 1572872 | tf_op jit(solution)/shard_map/ppermute | solution.py:33
  15.2 8.7 %collective-permute-start.5 = (bf16[2,4,128,128]{3,2,1,0:T(8,128)(2,1)S(1)}, bf16[2,4,128,128]{3,2,1,0:T(8,128)(2,1)S(1)}, u32[]{:S(2)}, u32[]{:S(2)}) collective-permute-start(bf16[2,4,128,128]{3,2,1,0:T(8,128)(2,1)S(1)} %pad_maximum_fusion.4), channel_id=1, source_target_pairs={{0,2},{1,3},{2,0},{3,1},{4,6},{5,7},{6,4},{7,5},{8,10},{9,11},{10,... | collective-permute-start | bytes 786440 | tf_op jit(solution)/shard_map/ppermute | solution.py:33
  16.6 14.6 %collective-permute-start.7 = (bf16[1,4,128,128]{3,2,1,0:T(8,128)(2,1)S(1)}, bf16[1,4,128,128]{3,2,1,0:T(8,128)(2,1)S(1)}, u32[]{:S(2)}, u32[]{:S(2)}) collective-permute-start(bf16[1,4,128,128]{3,2,1,0:T(8,128)(2,1)S(1)} %collective-permute-done.4), channel_id=1, source_target_pairs={{0,1},{1,0},{2,3},{3,2},{4,5},{5,4},{6,7},{7,6},{8,9},{9,8},{10,11... | collective-permute-start | bytes 393224 | tf_op jit(solution)/shard_map/ppermute | solution.py:33
  23.9 5.1 %collective-permute-start.6 = (bf16[1,4,128,128]{3,2,1,0:T(8,128)(2,1)S(1)}, bf16[1,4,128,128]{3,2,1,0:T(8,128)(2,1)S(1)}, u32[]{:S(2)}, u32[]{:S(2)}) collective-permute-start(bf16[1,4,128,128]{3,2,1,0:T(8,128)(2,1)S(1)} %bitcast.324), channel_id=1, source_target_pairs={{0,2},{1,3},{2,0},{3,1},{4,6},{5,7},{6,4},{7,5},{8,10},{9,11},{10,... | collective-permute-start | bytes 393224 | tf_op jit(solution)/shard_map/ppermute | solution.py:33
  25.5 5.1 %collective-permute-start.8 = (bf16[2,4,128,128]{3,2,1,0:T(8,128)(2,1)S(1)}, bf16[2,4,128,128]{3,2,1,0:T(8,128)(2,1)S(1)}, u32[]{:S(2)}, u32[]{:S(2)}) collective-permute-start(bf16[2,4,128,128]{3,2,1,0:T(8,128)(2,1)S(1)} %collective-permute-done.5), channel_id=1, source_target_pairs={{0,1},{1,0},{2,3},{3,2},{4,5},{5,4},{6,7},{7,6},{8,9},{9,8},{10,11... | collective-permute-start | bytes 786440 | tf_op jit(solution)/shard_map/ppermute | solution.py:33
  29.0 1.9 %collective-permute-start.9 = (bf16[1,4,128,128]{3,2,1,0:T(8,128)(2,1)S(1)}, bf16[1,4,128,128]{3,2,1,0:T(8,128)(2,1)S(1)}, u32[]{:S(2)}, u32[]{:S(2)}) collective-permute-start(bf16[1,4,128,128]{3,2,1,0:T(8,128)(2,1)S(1)} %collective-permute-done.6), channel_id=1, source_target_pairs={{0,1},{1,0},{2,3},{3,2},{4,5},{5,4},{6,7},{7,6},{8,9},{9,8},{10,11... | collective-permute-start | bytes 393224 | tf_op jit(solution)/shard_map/ppermute | solution.py:33
  30.9 0.9 %copy-start.2 = (f32[3,128,128]{2,1,0:T(8,128)S(1)}, f32[3,128,128]{2,1,0:T(8,128)}, u32[]{:S(2)}) copy-start(f32[3,128,128]{2,1,0:T(8,128)} %param.20) | copy-start | bytes 589828
  31.2 0.9 %copy-start.1 = (f32[1,128,128]{2,1,0:T(8,128)S(1)}, f32[1,128,128]{2,1,0:T(8,128)}, u32[]{:S(2)}) copy-start(f32[1,128,128]{2,1,0:T(8,128)} %param.21) | copy-start | bytes 196612
  32.4 8.6 %collective-permute-start.10 = (bf16[128,128]{1,0:T(8,128)(2,1)S(1)}, bf16[128,128]{1,0:T(8,128)(2,1)S(1)}, u32[]{:S(2)}, u32[]{:S(2)}) collective-permute-start(bf16[128,128]{1,0:T(8,128)(2,1)S(1)} %get-tuple-element.23), channel_id=1, source_target_pairs={{0,4},{1,5},{2,6},{3,7},{4,8},{5,9},{6,10},{7,11},{8,12},{9,13},{1... | collective-permute-start | bytes 98312 | tf_op jit(solution)/shard_map/ppermute | solution.py:26
  35.1 5.9 %collective-permute-start.11 = (bf16[128,128]{1,0:T(8,128)(2,1)S(1)}, bf16[128,128]{1,0:T(8,128)(2,1)S(1)}, u32[]{:S(2)}, u32[]{:S(2)}) collective-permute-start(bf16[128,128]{1,0:T(8,128)(2,1)S(1)} %get-tuple-element.23), channel_id=1, source_target_pairs={{0,8},{1,9},{2,10},{3,11},{4,12},{5,13},{6,14},{7,15},{8,0},{9,1},... | collective-permute-start | bytes 98312 | tf_op jit(solution)/shard_map/ppermute | solution.py:26
  36.8 4.2 %collective-permute-start.12 = (bf16[128,128]{1,0:T(8,128)(2,1)S(1)}, bf16[128,128]{1,0:T(8,128)(2,1)S(1)}, u32[]{:S(2)}, u32[]{:S(2)}) collective-permute-start(bf16[128,128]{1,0:T(8,128)(2,1)S(1)} %get-tuple-element.23), channel_id=1, source_target_pairs={{0,12},{1,13},{2,14},{3,15},{4,0},{5,1},{6,2},{7,3},{8,4},{9,5},{1... | collective-permute-start | bytes 98312 | tf_op jit(solution)/shard_map/ppermute | solution.py:26
  37.6 4.8 %collective-permute-start.14 = (bf16[1,128,128]{2,1,0:T(8,128)(2,1)S(1)}, bf16[1,128,128]{2,1,0:T(8,128)(2,1)S(1)}, u32[]{:S(2)}, u32[]{:S(2)}) collective-permute-start(bf16[1,128,128]{2,1,0:T(8,128)(2,1)S(1)} %bitcast.326), channel_id=1, source_target_pairs={{0,2},{1,3},{2,0},{3,1},{4,6},{5,7},{6,4},{7,5},{8,10},{9,11},{10,... | collective-permute-start | bytes 98312 | tf_op jit(solution)/shard_map/ppermute | solution.py:33
  41.1 4.7 %collective-permute-start.15 = (bf16[3,128,128]{2,1,0:T(8,128)(2,1)S(1)}, bf16[3,128,128]{2,1,0:T(8,128)(2,1)S(1)}, u32[]{:S(2)}, u32[]{:S(2)}) collective-permute-start(bf16[3,128,128]{2,1,0:T(8,128)(2,1)S(1)} %pad_maximum_fusion.8), channel_id=1, source_target_pairs={{0,2},{1,3},{2,0},{3,1},{4,6},{5,7},{6,4},{7,5},{8,10},{9,11},{10,... | collective-permute-start | bytes 294920 | tf_op jit(solution)/shard_map/ppermute | solution.py:33
  42.3 3.4 %collective-permute-start.13 = (bf16[4,128,128]{2,1,0:T(8,128)(2,1)S(1)}, bf16[4,128,128]{2,1,0:T(8,128)(2,1)S(1)}, u32[]{:S(2)}, u32[]{:S(2)}) collective-permute-start(bf16[4,128,128]{2,1,0:T(8,128)(2,1)S(1)} %pad_maximum_fusion.6), channel_id=1, source_target_pairs={{0,1},{1,0},{2,3},{3,2},{4,5},{5,4},{6,7},{7,6},{8,9},{9,8},{10,11... | collective-permute-start | bytes 393224 | tf_op jit(solution)/shard_map/ppermute | solution.py:33
  42.4 3.5 %collective-permute-start.16 = (bf16[1,128,128]{2,1,0:T(8,128)(2,1)S(1)}, bf16[1,128,128]{2,1,0:T(8,128)(2,1)S(1)}, u32[]{:S(2)}, u32[]{:S(2)}) collective-permute-start(bf16[1,128,128]{2,1,0:T(8,128)(2,1)S(1)} %collective-permute-done.14), channel_id=1, source_target_pairs={{0,1},{1,0},{2,3},{3,2},{4,5},{5,4},{6,7},{7,6},{8,9},{9,8},{10,11... | collective-permute-start | bytes 98312 | tf_op jit(solution)/shard_map/ppermute | solution.py:33
  45.8 1.3 %collective-permute-start.17 = (bf16[3,128,128]{2,1,0:T(8,128)(2,1)S(1)}, bf16[3,128,128]{2,1,0:T(8,128)(2,1)S(1)}, u32[]{:S(2)}, u32[]{:S(2)}) collective-permute-start(bf16[3,128,128]{2,1,0:T(8,128)(2,1)S(1)} %collective-permute-done.15), channel_id=1, source_target_pairs={{0,1},{1,0},{2,3},{3,2},{4,5},{5,4},{6,7},{7,6},{8,9},{9,8},{10,11... | collective-permute-start | bytes 294920 | tf_op jit(solution)/shard_map/ppermute | solution.py:33
  48.0 6.0 %collective-permute-start.18 = (bf16[128,128]{1,0:T(8,128)(2,1)S(1)}, bf16[128,128]{1,0:T(8,128)(2,1)S(1)}, u32[]{:S(2)}, u32[]{:S(2)}) collective-permute-start(bf16[128,128]{1,0:T(8,128)(2,1)S(1)} %get-tuple-element.21), channel_id=1, source_target_pairs={{0,4},{1,5},{2,6},{3,7},{4,8},{5,9},{6,10},{7,11},{8,12},{9,13},{1... | collective-permute-start | bytes 98312 | tf_op jit(solution)/shard_map/ppermute | solution.py:26
  49.3 5.5 %collective-permute-start.19 = (bf16[128,128]{1,0:T(8,128)(2,1)S(1)}, bf16[128,128]{1,0:T(8,128)(2,1)S(1)}, u32[]{:S(2)}, u32[]{:S(2)}) collective-permute-start(bf16[128,128]{1,0:T(8,128)(2,1)S(1)} %get-tuple-element.21), channel_id=1, source_target_pairs={{0,8},{1,9},{2,10},{3,11},{4,12},{5,13},{6,14},{7,15},{8,0},{9,1},... | collective-permute-start | bytes 98312 | tf_op jit(solution)/shard_map/ppermute | solution.py:26
  50.8 4.2 %collective-permute-start.20 = (bf16[128,128]{1,0:T(8,128)(2,1)S(1)}, bf16[128,128]{1,0:T(8,128)(2,1)S(1)}, u32[]{:S(2)}, u32[]{:S(2)}) collective-permute-start(bf16[128,128]{1,0:T(8,128)(2,1)S(1)} %get-tuple-element.21), channel_id=1, source_target_pairs={{0,12},{1,13},{2,14},{3,15},{4,0},{5,1},{6,2},{7,3},{8,4},{9,5},{1... | collective-permute-start | bytes 98312 | tf_op jit(solution)/shard_map/ppermute | solution.py:26
  52.4 4.0 %collective-permute-start.22 = (bf16[1,128,128]{2,1,0:T(8,128)(2,1)S(1)}, bf16[1,128,128]{2,1,0:T(8,128)(2,1)S(1)}, u32[]{:S(2)}, u32[]{:S(2)}) collective-permute-start(bf16[1,128,128]{2,1,0:T(8,128)(2,1)S(1)} %bitcast.328), channel_id=1, source_target_pairs={{0,2},{1,3},{2,0},{3,1},{4,6},{5,7},{6,4},{7,5},{8,10},{9,11},{10,... | collective-permute-start | bytes 98312 | tf_op jit(solution)/shard_map/ppermute | solution.py:33
  55.0 4.7 %collective-permute-start.23 = (bf16[3,128,128]{2,1,0:T(8,128)(2,1)S(1)}, bf16[3,128,128]{2,1,0:T(8,128)(2,1)S(1)}, u32[]{:S(2)}, u32[]{:S(2)}) collective-permute-start(bf16[3,128,128]{2,1,0:T(8,128)(2,1)S(1)} %pad_maximum_fusion.9), channel_id=1, source_target_pairs={{0,2},{1,3},{2,0},{3,1},{4,6},{5,7},{6,4},{7,5},{8,10},{9,11},{10,... | collective-permute-start | bytes 294920 | tf_op jit(solution)/shard_map/ppermute | solution.py:33
  56.3 3.4 %collective-permute-start.21 = (bf16[4,128,128]{2,1,0:T(8,128)(2,1)S(1)}, bf16[4,128,128]{2,1,0:T(8,128)(2,1)S(1)}, u32[]{:S(2)}, u32[]{:S(2)}) collective-permute-start(bf16[4,128,128]{2,1,0:T(8,128)(2,1)S(1)} %pad_maximum_fusion.7), channel_id=1, source_target_pairs={{0,1},{1,0},{2,3},{3,2},{4,5},{5,4},{6,7},{7,6},{8,9},{9,8},{10,11... | collective-permute-start | bytes 393224 | tf_op jit(solution)/shard_map/ppermute | solution.py:33
  56.4 3.4 %collective-permute-start.24 = (bf16[1,128,128]{2,1,0:T(8,128)(2,1)S(1)}, bf16[1,128,128]{2,1,0:T(8,128)(2,1)S(1)}, u32[]{:S(2)}, u32[]{:S(2)}) collective-permute-start(bf16[1,128,128]{2,1,0:T(8,128)(2,1)S(1)} %collective-permute-done.22), channel_id=1, source_target_pairs={{0,1},{1,0},{2,3},{3,2},{4,5},{5,4},{6,7},{7,6},{8,9},{9,8},{10,11... | collective-permute-start | bytes 98312 | tf_op jit(solution)/shard_map/ppermute | solution.py:33
  59.7 1.3 %collective-permute-start.25 = (bf16[3,128,128]{2,1,0:T(8,128)(2,1)S(1)}, bf16[3,128,128]{2,1,0:T(8,128)(2,1)S(1)}, u32[]{:S(2)}, u32[]{:S(2)}) collective-permute-start(bf16[3,128,128]{2,1,0:T(8,128)(2,1)S(1)} %collective-permute-done.23), channel_id=1, source_target_pairs={{0,1},{1,0},{2,3},{3,2},{4,5},{5,4},{6,7},{7,6},{8,9},{9,8},{10,11... | collective-permute-start | bytes 294920 | tf_op jit(solution)/shard_map/ppermute | solution.py:33

commit v20 on v14

--- a/solution.py
+++ b/solution.py
@@ -103,7 +103,7 @@
     def advance(moment, retarded):
         source = excitation[moment] - retarded
         return with_layout_constraint(jnp.dot(
-            inverse_t, source, precision=lax.Precision.HIGHEST, preferred_element_type=jnp.float32
+            inverse_t, source, precision=lax.Precision.HIGH, preferred_element_type=jnp.float32
         ), Layout((0, 1)))
 
     results = [None] * step_count

time: 59.8 us -> 59.7 us (level)
  no operation moved by 1% of the time
where the time goes in v20:
time: 59.7 us; the launch traced here: 59.5 us
  starting transfers between devices  28 us (47%)
  waiting for transfers between devices  15.1 us (25%)
  matrix products  7.92 us (13%)
  local copies, waits for them, and re-layouts  4.18 us (7%)
  other arithmetic  3.81 us (6%)
    ppermute x9, starting transfers between devices, line_stage(): parts.append(lax.ppermute(x, 'wide', pairs)[None])  16.9 us
    ppermute x17, waiting for transfers between devices, swap(): return lax.ppermute(x, 'wide', [(d, d ^ mask) for d in range(wide)])  14.2 us
    ppermute x17, starting transfers between devices, swap(): return lax.ppermute(x, 'wide', [(d, d ^ mask) for d in range(wide)])  11.1 us
    dot_general x27, matrix products, rowwise(): return jnp.einsum(spec, tiles, currents, preferred_element_type=jnp.float32)  7.17 us
    sort x1, other arithmetic, per_device(): column_of_block = jnp.argsort(block_owner)  1.9 us
    unnamed x22, local copies, waits for them, and re-layouts  1.34 us
  transfers between devices with their start and end apart: 26, of which 9 were waited for; matrix products, arithmetic and copies ran while one was open for 20% of the time, Pallas kernels for 0%

profile of v20, /device:TPU:0, one launch (start us, length us, event | category | flops | bytes accessed | tf_op | source)
XLA Modules:
  0.0 59.5 jit_solution(7693835913577827082)
XLA Ops:
  0.0 3.0 %collective-permute-start = (bf16[4,128,128]{2,1,0:T(8,128)(2,1)}, bf16[4,128,128]{2,1,0:T(8,128)(2,1)S(1)}, u32[]{:S(2)}, u32[]{:S(2)}) collective-permute-start(bf16[4,128,128]{2,1,0:T(8,128)(2,1)} %param.19), channel_id=1, source_target_pairs={{0,4},{1,5},{2,6},{3,7},{4,8},{5,9},{6,10},{7,11},{8,12},{9,13},{1... | collective-permute-start | bytes 393224 | tf_op jit(solution)/shard_map/ppermute | solution.py:26
  3.0 2.6 %collective-permute-start.1 = (bf16[4,128,128]{2,1,0:T(8,128)(2,1)}, bf16[4,128,128]{2,1,0:T(8,128)(2,1)S(1)}, u32[]{:S(2)}, u32[]{:S(2)}) collective-permute-start(bf16[4,128,128]{2,1,0:T(8,128)(2,1)} %param.19), channel_id=1, source_target_pairs={{0,8},{1,9},{2,10},{3,11},{4,12},{5,13},{6,14},{7,15},{8,0},{9,1},... | collective-permute-start | bytes 393224 | tf_op jit(solution)/shard_map/ppermute | solution.py:26
  5.6 1.3 %collective-permute-start.2 = (bf16[4,128,128]{2,1,0:T(8,128)(2,1)}, bf16[4,128,128]{2,1,0:T(8,128)(2,1)S(1)}, u32[]{:S(2)}, u32[]{:S(2)}) collective-permute-start(bf16[4,128,128]{2,1,0:T(8,128)(2,1)} %param.19), channel_id=1, source_target_pairs={{0,12},{1,13},{2,14},{3,15},{4,0},{5,1},{6,2},{7,3},{8,4},{9,5},{1... | collective-permute-start | bytes 393224 | tf_op jit(solution)/shard_map/ppermute | solution.py:26
  7.0 1.5 %collective-permute-start.4 = (bf16[1,4,128,128]{3,2,1,0:T(8,128)(2,1)}, bf16[1,4,128,128]{3,2,1,0:T(8,128)(2,1)S(1)}, u32[]{:S(2)}, u32[]{:S(2)}) collective-permute-start(bf16[1,4,128,128]{3,2,1,0:T(8,128)(2,1)} %bitcast.320), channel_id=1, source_target_pairs={{0,2},{1,3},{2,0},{3,1},{4,6},{5,7},{6,4},{7,5},{8,10},{9,11},{10,... | collective-permute-start | bytes 393224 | tf_op jit(solution)/shard_map/ppermute | solution.py:33
  8.7 1.9 %sort.17 = (s32[16]{0:T(128)}, s32[16]{0:T(128)S(1)}) sort(s32[16]{0:T(128)} %param.18, s32[16]{0:T(128)S(1)} %iota.5), dimensions={0}, to_apply=%region_0.0 | sort | flops 64 | bytes 256 | tf_op jit(solution)/shard_map/jit(argsort)/sort | solution.py:94
  10.6 0.7 %gather_fusion = s32[16]{0:T(128)S(1)} fusion(s32[16]{0:T(128)S(1)} %get-tuple-element.8, s32[1024]{0:T(1024)S(1)} %pad_clamp_fusion.1), kind=kCustom, calls=%fused_computation.clone | custom fusion | bytes 192 | tf_op jit(solution)/shard_map/jit(_take)/gather | solution.py:69
  11.3 0.8 %copy.17 = s32[16,2]{1,0:T(8,128)S(1)} copy(s32[16,2]{0,1:T(2,128)} %bitcast.330) | data formatting | bytes 256 | tf_op jit(solution)/shard_map/squeeze | solution.py:71
  12.0 0.7 %gather_fusion.2 = bf16[16,2,128,128]{3,2,1,0:T(8,128)(2,1)S(1)} fusion(bf16[16,2,128,128]{3,2,1,0:T(8,128)(2,1)S(1)} %bitcast.299, s32[1024]{0:T(1024)S(1)} %pad_clamp_fusion), kind=kCustom, calls=%fused_computation.2.clone | custom fusion | bytes 2097216 | tf_op jit(solution)/shard_map/jit(_take)/gather | solution.py:70
  12.8 0.6 gather_fusion.1
  13.6 0.3 compare_reduce_fusion.3
  13.9 0.3 bitcast_select_fusion.3
  14.5 0.5 copy-done.3
  15.1 1.1 %collective-permute-start.5 = (bf16[1,4,128,128]{3,2,1,0:T(8,128)(2,1)S(1)}, bf16[1,4,128,128]{3,2,1,0:T(8,128)(2,1)S(1)}, u32[]{:S(2)}, u32[]{:S(2)}) collective-permute-start(bf16[1,4,128,128]{3,2,1,0:T(8,128)(2,1)S(1)} %bitcast.324), channel_id=1, source_target_pairs={{0,2},{1,3},{2,0},{3,1},{4,6},{5,7},{6,4},{7,5},{8,10},{9,11},{10,... | collective-permute-start | bytes 393224 | tf_op jit(solution)/shard_map/ppermute | solution.py:33
  16.2 1.0 %collective-permute-start.6 = (bf16[2,4,128,128]{3,2,1,0:T(8,128)(2,1)S(1)}, bf16[2,4,128,128]{3,2,1,0:T(8,128)(2,1)S(1)}, u32[]{:S(2)}, u32[]{:S(2)}) collective-permute-start(bf16[2,4,128,128]{3,2,1,0:T(8,128)(2,1)S(1)} %pad_maximum_fusion.4), channel_id=1, source_target_pairs={{0,2},{1,3},{2,0},{3,1},{4,6},{5,7},{6,4},{7,5},{8,10},{9,11},{10,... | collective-permute-start | bytes 786440 | tf_op jit(solution)/shard_map/ppermute | solution.py:33
  17.2 0.3 convolution_bitcast_fusion.5
  17.6 0.3 collective-permute-start.7
  17.8 0.3 convolution_bitcast_fusion.7
  18.1 3.0 %collective-permute-done.5 = bf16[1,4,128,128]{3,2,1,0:T(8,128)(2,1)S(1)} collective-permute-done((bf16[1,4,128,128]{3,2,1,0:T(8,128)(2,1)S(1)}, bf16[1,4,128,128]{3,2,1,0:T(8,128)(2,1)S(1)}, u32[]{:S(2)}, u32[]{:S(2)}) %collective-permute-start.5) | collective-permute-done | bytes 131104 | tf_op jit(solution)/shard_map/ppermute | solution.py:33
  21.7 0.7 %collective-permute-done.8 = bf16[1,4,128,128]{3,2,1,0:T(8,128)(2,1)S(1)} collective-permute-done((bf16[1,4,128,128]{3,2,1,0:T(8,128)(2,1)S(1)}, bf16[1,4,128,128]{3,2,1,0:T(8,128)(2,1)S(1)}, u32[]{:S(2)}, u32[]{:S(2)}) %collective-permute-start.8) | collective-permute-done | bytes 131104 | tf_op jit(solution)/shard_map/ppermute | solution.py:33
  22.9 2.9 %collective-permute-done.6 = bf16[2,4,128,128]{3,2,1,0:T(8,128)(2,1)S(1)} collective-permute-done((bf16[2,4,128,128]{3,2,1,0:T(8,128)(2,1)S(1)}, bf16[2,4,128,128]{3,2,1,0:T(8,128)(2,1)S(1)}, u32[]{:S(2)}, u32[]{:S(2)}) %collective-permute-start.6) | collective-permute-done | bytes 262176 | tf_op jit(solution)/shard_map/ppermute | solution.py:33
  26.5 0.3 convolution_bitcast_fusion.3
  26.8 0.4 convolution_bitcast_fusion
  27.1 0.4 fusion.26
  27.8 0.3 convolution_bitcast_fusion.2
  28.1 0.6 %copy-done.2 = f32[3,128,128]{2,1,0:T(8,128)S(1)} copy-done((f32[3,128,128]{2,1,0:T(8,128)S(1)}, f32[3,128,128]{2,1,0:T(8,128)}, u32[]{:S(2)}) %copy-start.2) | copy-done | bytes 196632
  29.2 3.2 %collective-permute-start.10 = (bf16[128,128]{1,0:T(8,128)(2,1)S(1)}, bf16[128,128]{1,0:T(8,128)(2,1)S(1)}, u32[]{:S(2)}, u32[]{:S(2)}) collective-permute-start(bf16[128,128]{1,0:T(8,128)(2,1)S(1)} %get-tuple-element.21), channel_id=1, source_target_pairs={{0,4},{1,5},{2,6},{3,7},{4,8},{5,9},{6,10},{7,11},{8,12},{9,13},{1... | collective-permute-start | bytes 98312 | tf_op jit(solution)/shard_map/ppermute | solution.py:26
  32.4 1.2 %collective-permute-start.11 = (bf16[128,128]{1,0:T(8,128)(2,1)S(1)}, bf16[128,128]{1,0:T(8,128)(2,1)S(1)}, u32[]{:S(2)}, u32[]{:S(2)}) collective-permute-start(bf16[128,128]{1,0:T(8,128)(2,1)S(1)} %get-tuple-element.21), channel_id=1, source_target_pairs={{0,8},{1,9},{2,10},{3,11},{4,12},{5,13},{6,14},{7,15},{8,0},{9,1},... | collective-permute-start | bytes 98312 | tf_op jit(solution)/shard_map/ppermute | solution.py:26
  33.6 1.3 %collective-permute-start.12 = (bf16[128,128]{1,0:T(8,128)(2,1)S(1)}, bf16[128,128]{1,0:T(8,128)(2,1)S(1)}, u32[]{:S(2)}, u32[]{:S(2)}) collective-permute-start(bf16[128,128]{1,0:T(8,128)(2,1)S(1)} %get-tuple-element.21), channel_id=1, source_target_pairs={{0,12},{1,13},{2,14},{3,15},{4,0},{5,1},{6,2},{7,3},{8,4},{9,5},{1... | collective-permute-start | bytes 98312 | tf_op jit(solution)/shard_map/ppermute | solution.py:26
  34.9 1.5 %collective-permute-start.14 = (bf16[1,128,128]{2,1,0:T(8,128)(2,1)S(1)}, bf16[1,128,128]{2,1,0:T(8,128)(2,1)S(1)}, u32[]{:S(2)}, u32[]{:S(2)}) collective-permute-start(bf16[1,128,128]{2,1,0:T(8,128)(2,1)S(1)} %bitcast.326), channel_id=1, source_target_pairs={{0,2},{1,3},{2,0},{3,1},{4,6},{5,7},{6,4},{7,5},{8,10},{9,11},{10,... | collective-permute-start | bytes 98312 | tf_op jit(solution)/shard_map/ppermute | solution.py:33
  36.6 0.3 fusion.24
  36.9 0.3 fusion.25
  38.0 1.4 %collective-permute-start.15 = (bf16[3,128,128]{2,1,0:T(8,128)(2,1)S(1)}, bf16[3,128,128]{2,1,0:T(8,128)(2,1)S(1)}, u32[]{:S(2)}, u32[]{:S(2)}) collective-permute-start(bf16[3,128,128]{2,1,0:T(8,128)(2,1)S(1)} %pad_maximum_fusion.8), channel_id=1, source_target_pairs={{0,2},{1,3},{2,0},{3,1},{4,6},{5,7},{6,4},{7,5},{8,10},{9,11},{10,... | collective-permute-start | bytes 294920 | tf_op jit(solution)/shard_map/ppermute | solution.py:33
  39.4 0.6 collective-permute-start.16
  40.0 2.7 %collective-permute-done.15 = bf16[3,128,128]{2,1,0:T(8,128)(2,1)S(1)} collective-permute-done((bf16[3,128,128]{2,1,0:T(8,128)(2,1)S(1)}, bf16[3,128,128]{2,1,0:T(8,128)(2,1)S(1)}, u32[]{:S(2)}, u32[]{:S(2)}) %collective-permute-start.15) | collective-permute-done | bytes 98336 | tf_op jit(solution)/shard_map/ppermute | solution.py:33
  42.8 1.2 %collective-permute-done.17 = bf16[3,128,128]{2,1,0:T(8,128)(2,1)S(1)} collective-permute-done((bf16[3,128,128]{2,1,0:T(8,128)(2,1)S(1)}, bf16[3,128,128]{2,1,0:T(8,128)(2,1)S(1)}, u32[]{:S(2)}, u32[]{:S(2)}) %collective-permute-start.17) | collective-permute-done | bytes 98336 | tf_op jit(solution)/shard_map/ppermute | solution.py:33
  44.0 0.3 convolution_bitcast_fusion.11
  44.8 0.8 %collective-permute-start.18 = (bf16[128,128]{1,0:T(8,128)(2,1)S(1)}, bf16[128,128]{1,0:T(8,128)(2,1)S(1)}, u32[]{:S(2)}, u32[]{:S(2)}) collective-permute-start(bf16[128,128]{1,0:T(8,128)(2,1)S(1)} %get-tuple-element.19), channel_id=1, source_target_pairs={{0,4},{1,5},{2,6},{3,7},{4,8},{5,9},{6,10},{7,11},{8,12},{9,13},{1... | collective-permute-start | bytes 98312 | tf_op jit(solution)/shard_map/ppermute | solution.py:26
  45.6 2.4 %collective-permute-start.19 = (bf16[128,128]{1,0:T(8,128)(2,1)S(1)}, bf16[128,128]{1,0:T(8,128)(2,1)S(1)}, u32[]{:S(2)}, u32[]{:S(2)}) collective-permute-start(bf16[128,128]{1,0:T(8,128)(2,1)S(1)} %get-tuple-element.19), channel_id=1, source_target_pairs={{0,8},{1,9},{2,10},{3,11},{4,12},{5,13},{6,14},{7,15},{8,0},{9,1},... | collective-permute-start | bytes 98312 | tf_op jit(solution)/shard_map/ppermute | solution.py:26
  48.1 1.1 %collective-permute-start.20 = (bf16[128,128]{1,0:T(8,128)(2,1)S(1)}, bf16[128,128]{1,0:T(8,128)(2,1)S(1)}, u32[]{:S(2)}, u32[]{:S(2)}) collective-permute-start(bf16[128,128]{1,0:T(8,128)(2,1)S(1)} %get-tuple-element.19), channel_id=1, source_target_pairs={{0,12},{1,13},{2,14},{3,15},{4,0},{5,1},{6,2},{7,3},{8,4},{9,5},{1... | collective-permute-start | bytes 98312 | tf_op jit(solution)/shard_map/ppermute | solution.py:26
  49.1 0.5 convolution_bitcast_fusion.9
  49.6 1.6 %collective-permute-start.22 = (bf16[1,128,128]{2,1,0:T(8,128)(2,1)S(1)}, bf16[1,128,128]{2,1,0:T(8,128)(2,1)S(1)}, u32[]{:S(2)}, u32[]{:S(2)}) collective-permute-start(bf16[1,128,128]{2,1,0:T(8,128)(2,1)S(1)} %bitcast.328), channel_id=1, source_target_pairs={{0,2},{1,3},{2,0},{3,1},{4,6},{5,7},{6,4},{7,5},{8,10},{9,11},{10,... | collective-permute-start | bytes 98312 | tf_op jit(solution)/shard_map/ppermute | solution.py:33
  51.2 0.8 %collective-permute-done.20 = bf16[128,128]{1,0:T(8,128)(2,1)S(1)} collective-permute-done((bf16[128,128]{1,0:T(8,128)(2,1)S(1)}, bf16[128,128]{1,0:T(8,128)(2,1)S(1)}, u32[]{:S(2)}, u32[]{:S(2)}) %collective-permute-start.20) | collective-permute-done | bytes 32800 | tf_op jit(solution)/shard_map/ppermute | solution.py:26
  52.0 1.6 %collective-permute-start.23 = (bf16[3,128,128]{2,1,0:T(8,128)(2,1)S(1)}, bf16[3,128,128]{2,1,0:T(8,128)(2,1)S(1)}, u32[]{:S(2)}, u32[]{:S(2)}) collective-permute-start(bf16[3,128,128]{2,1,0:T(8,128)(2,1)S(1)} %pad_maximum_fusion.9), channel_id=1, source_target_pairs={{0,2},{1,3},{2,0},{3,1},{4,6},{5,7},{6,4},{7,5},{8,10},{9,11},{10,... | collective-permute-start | bytes 294920 | tf_op jit(solution)/shard_map/ppermute | solution.py:33
  53.7 0.6 collective-permute-start.24
  54.2 2.5 %collective-permute-done.23 = bf16[3,128,128]{2,1,0:T(8,128)(2,1)S(1)} collective-permute-done((bf16[3,128,128]{2,1,0:T(8,128)(2,1)S(1)}, bf16[3,128,128]{2,1,0:T(8,128)(2,1)S(1)}, u32[]{:S(2)}, u32[]{:S(2)}) %collective-permute-start.23) | collective-permute-done | bytes 98336 | tf_op jit(solution)/shard_map/ppermute | solution.py:33
  56.8 1.2 %collective-permute-done.25 = bf16[3,128,128]{2,1,0:T(8,128)(2,1)S(1)} collective-permute-done((bf16[3,128,128]{2,1,0:T(8,128)(2,1)S(1)}, bf16[3,128,128]{2,1,0:T(8,128)(2,1)S(1)}, u32[]{:S(2)}, u32[]{:S(2)}) %collective-permute-start.25) | collective-permute-done | bytes 98336 | tf_op jit(solution)/shard_map/ppermute | solution.py:33
  58.0 0.3 convolution_bitcast_fusion.10
  58.8 0.7 %pad_maximum_fusion.5 = f32[3,128,128]{2,1,0:T(8,128)} fusion(f32[1,128,128]{2,1,0:T(8,128)S(1)} %bitcast.318, f32[1,128,128]{2,1,0:T(8,128)S(1)} %bitcast.319, f32[1,128,128]{2,1,0:T(8,128)S(1)} %convolution_bitcast_fusion.8), kind=kLoop, calls=%fused_computation.89 | loop fusion | flops 98304 | bytes 393216 | tf_op jit(solution)/shard_map/stack | solution.py:136
  (83 shorter events, 5.5 us)
Async XLA Ops:
  0.0 12.0 %copy-start = (bf16[1,16,2,128,128]{4,3,2,1,0:T(8,128)(2,1)S(1)}, bf16[1,16,2,128,128]{4,3,2,1,0:T(8,128)(2,1)}, u32[]{:S(2)}) copy-start(bf16[1,16,2,128,128]{4,3,2,1,0:T(8,128)(2,1)} %param.16) | copy-start | bytes 3145732
  0.0 14.5 %collective-permute-start = (bf16[4,128,128]{2,1,0:T(8,128)(2,1)}, bf16[4,128,128]{2,1,0:T(8,128)(2,1)S(1)}, u32[]{:S(2)}, u32[]{:S(2)}) collective-permute-start(bf16[4,128,128]{2,1,0:T(8,128)(2,1)} %param.19), channel_id=1, source_target_pairs={{0,4},{1,5},{2,6},{3,7},{4,8},{5,9},{6,10},{7,11},{8,12},{9,13},{1... | collective-permute-start | bytes 393224 | tf_op jit(solution)/shard_map/ppermute | solution.py:26
  3.0 11.4 %collective-permute-start.1 = (bf16[4,128,128]{2,1,0:T(8,128)(2,1)}, bf16[4,128,128]{2,1,0:T(8,128)(2,1)S(1)}, u32[]{:S(2)}, u32[]{:S(2)}) collective-permute-start(bf16[4,128,128]{2,1,0:T(8,128)(2,1)} %param.19), channel_id=1, source_target_pairs={{0,8},{1,9},{2,10},{3,11},{4,12},{5,13},{6,14},{7,15},{8,0},{9,1},... | collective-permute-start | bytes 393224 | tf_op jit(solution)/shard_map/ppermute | solution.py:26
  5.6 8.9 %collective-permute-start.2 = (bf16[4,128,128]{2,1,0:T(8,128)(2,1)}, bf16[4,128,128]{2,1,0:T(8,128)(2,1)S(1)}, u32[]{:S(2)}, u32[]{:S(2)}) collective-permute-start(bf16[4,128,128]{2,1,0:T(8,128)(2,1)} %param.19), channel_id=1, source_target_pairs={{0,12},{1,13},{2,14},{3,15},{4,0},{5,1},{6,2},{7,3},{8,4},{9,5},{1... | collective-permute-start | bytes 393224 | tf_op jit(solution)/shard_map/ppermute | solution.py:26
  7.0 10.6 %collective-permute-start.4 = (bf16[1,4,128,128]{3,2,1,0:T(8,128)(2,1)}, bf16[1,4,128,128]{3,2,1,0:T(8,128)(2,1)S(1)}, u32[]{:S(2)}, u32[]{:S(2)}) collective-permute-start(bf16[1,4,128,128]{3,2,1,0:T(8,128)(2,1)} %bitcast.320), channel_id=1, source_target_pairs={{0,2},{1,3},{2,0},{3,1},{4,6},{5,7},{6,4},{7,5},{8,10},{9,11},{10,... | collective-permute-start | bytes 393224 | tf_op jit(solution)/shard_map/ppermute | solution.py:33
  14.1 0.9 %copy-start.3 = (bf16[4,128,128]{2,1,0:T(8,128)(2,1)S(1)}, bf16[4,128,128]{2,1,0:T(8,128)(2,1)}, u32[]{:S(2)}) copy-start(bf16[4,128,128]{2,1,0:T(8,128)(2,1)} %param.19) | copy-start | bytes 393220
  15.1 6.0 %collective-permute-start.5 = (bf16[1,4,128,128]{3,2,1,0:T(8,128)(2,1)S(1)}, bf16[1,4,128,128]{3,2,1,0:T(8,128)(2,1)S(1)}, u32[]{:S(2)}, u32[]{:S(2)}) collective-permute-start(bf16[1,4,128,128]{3,2,1,0:T(8,128)(2,1)S(1)} %bitcast.324), channel_id=1, source_target_pairs={{0,2},{1,3},{2,0},{3,1},{4,6},{5,7},{6,4},{7,5},{8,10},{9,11},{10,... | collective-permute-start | bytes 393224 | tf_op jit(solution)/shard_map/ppermute | solution.py:33
  16.2 10.6 %collective-permute-start.3 = (bf16[4,4,128,128]{3,2,1,0:T(8,128)(2,1)S(1)}, bf16[4,4,128,128]{3,2,1,0:T(8,128)(2,1)S(1)}, u32[]{:S(2)}, u32[]{:S(2)}) collective-permute-start(bf16[4,4,128,128]{3,2,1,0:T(8,128)(2,1)S(1)} %pad_maximum_fusion.3), channel_id=1, source_target_pairs={{0,1},{1,0},{2,3},{3,2},{4,5},{5,4},{6,7},{7,6},{8,9},{9,8},{10,11... | collective-permute-start | bytes 1572872 | tf_op jit(solution)/shard_map/ppermute | solution.py:33
  16.2 9.6 %collective-permute-start.6 = (bf16[2,4,128,128]{3,2,1,0:T(8,128)(2,1)S(1)}, bf16[2,4,128,128]{3,2,1,0:T(8,128)(2,1)S(1)}, u32[]{:S(2)}, u32[]{:S(2)}) collective-permute-start(bf16[2,4,128,128]{3,2,1,0:T(8,128)(2,1)S(1)} %pad_maximum_fusion.4), channel_id=1, source_target_pairs={{0,2},{1,3},{2,0},{3,1},{4,6},{5,7},{6,4},{7,5},{8,10},{9,11},{10,... | collective-permute-start | bytes 786440 | tf_op jit(solution)/shard_map/ppermute | solution.py:33
  17.6 10.5 %collective-permute-start.7 = (bf16[1,4,128,128]{3,2,1,0:T(8,128)(2,1)S(1)}, bf16[1,4,128,128]{3,2,1,0:T(8,128)(2,1)S(1)}, u32[]{:S(2)}, u32[]{:S(2)}) collective-permute-start(bf16[1,4,128,128]{3,2,1,0:T(8,128)(2,1)S(1)} %collective-permute-done.4), channel_id=1, source_target_pairs={{0,1},{1,0},{2,3},{3,2},{4,5},{5,4},{6,7},{7,6},{8,9},{9,8},{10,11... | collective-permute-start | bytes 393224 | tf_op jit(solution)/shard_map/ppermute | solution.py:33
  21.1 1.3 %collective-permute-start.8 = (bf16[1,4,128,128]{3,2,1,0:T(8,128)(2,1)S(1)}, bf16[1,4,128,128]{3,2,1,0:T(8,128)(2,1)S(1)}, u32[]{:S(2)}, u32[]{:S(2)}) collective-permute-start(bf16[1,4,128,128]{3,2,1,0:T(8,128)(2,1)S(1)} %collective-permute-done.5), channel_id=1, source_target_pairs={{0,1},{1,0},{2,3},{3,2},{4,5},{5,4},{6,7},{7,6},{8,9},{9,8},{10,11... | collective-permute-start | bytes 393224 | tf_op jit(solution)/shard_map/ppermute | solution.py:33
  25.8 2.0 %collective-permute-start.9 = (bf16[2,4,128,128]{3,2,1,0:T(8,128)(2,1)S(1)}, bf16[2,4,128,128]{3,2,1,0:T(8,128)(2,1)S(1)}, u32[]{:S(2)}, u32[]{:S(2)}) collective-permute-start(bf16[2,4,128,128]{3,2,1,0:T(8,128)(2,1)S(1)} %collective-permute-done.6), channel_id=1, source_target_pairs={{0,1},{1,0},{2,3},{3,2},{4,5},{5,4},{6,7},{7,6},{8,9},{9,8},{10,11... | collective-permute-start | bytes 786440 | tf_op jit(solution)/shard_map/ppermute | solution.py:33
  27.7 0.9 %copy-start.2 = (f32[3,128,128]{2,1,0:T(8,128)S(1)}, f32[3,128,128]{2,1,0:T(8,128)}, u32[]{:S(2)}) copy-start(f32[3,128,128]{2,1,0:T(8,128)} %param.20) | copy-start | bytes 589828
  28.0 0.9 %copy-start.1 = (f32[1,128,128]{2,1,0:T(8,128)S(1)}, f32[1,128,128]{2,1,0:T(8,128)}, u32[]{:S(2)}) copy-start(f32[1,128,128]{2,1,0:T(8,128)} %param.21) | copy-start | bytes 196612
  29.2 8.7 %collective-permute-start.10 = (bf16[128,128]{1,0:T(8,128)(2,1)S(1)}, bf16[128,128]{1,0:T(8,128)(2,1)S(1)}, u32[]{:S(2)}, u32[]{:S(2)}) collective-permute-start(bf16[128,128]{1,0:T(8,128)(2,1)S(1)} %get-tuple-element.21), channel_id=1, source_target_pairs={{0,4},{1,5},{2,6},{3,7},{4,8},{5,9},{6,10},{7,11},{8,12},{9,13},{1... | collective-permute-start | bytes 98312 | tf_op jit(solution)/shard_map/ppermute | solution.py:26
  32.4 5.5 %collective-permute-start.11 = (bf16[128,128]{1,0:T(8,128)(2,1)S(1)}, bf16[128,128]{1,0:T(8,128)(2,1)S(1)}, u32[]{:S(2)}, u32[]{:S(2)}) collective-permute-start(bf16[128,128]{1,0:T(8,128)(2,1)S(1)} %get-tuple-element.21), channel_id=1, source_target_pairs={{0,8},{1,9},{2,10},{3,11},{4,12},{5,13},{6,14},{7,15},{8,0},{9,1},... | collective-permute-start | bytes 98312 | tf_op jit(solution)/shard_map/ppermute | solution.py:26
  33.6 4.3 %collective-permute-start.12 = (bf16[128,128]{1,0:T(8,128)(2,1)S(1)}, bf16[128,128]{1,0:T(8,128)(2,1)S(1)}, u32[]{:S(2)}, u32[]{:S(2)}) collective-permute-start(bf16[128,128]{1,0:T(8,128)(2,1)S(1)} %get-tuple-element.21), channel_id=1, source_target_pairs={{0,12},{1,13},{2,14},{3,15},{4,0},{5,1},{6,2},{7,3},{8,4},{9,5},{1... | collective-permute-start | bytes 98312 | tf_op jit(solution)/shard_map/ppermute | solution.py:26
  34.9 4.5 %collective-permute-start.14 = (bf16[1,128,128]{2,1,0:T(8,128)(2,1)S(1)}, bf16[1,128,128]{2,1,0:T(8,128)(2,1)S(1)}, u32[]{:S(2)}, u32[]{:S(2)}) collective-permute-start(bf16[1,128,128]{2,1,0:T(8,128)(2,1)S(1)} %bitcast.326), channel_id=1, source_target_pairs={{0,2},{1,3},{2,0},{3,1},{4,6},{5,7},{6,4},{7,5},{8,10},{9,11},{10,... | collective-permute-start | bytes 98312 | tf_op jit(solution)/shard_map/ppermute | solution.py:33
  38.0 4.7 %collective-permute-start.15 = (bf16[3,128,128]{2,1,0:T(8,128)(2,1)S(1)}, bf16[3,128,128]{2,1,0:T(8,128)(2,1)S(1)}, u32[]{:S(2)}, u32[]{:S(2)}) collective-permute-start(bf16[3,128,128]{2,1,0:T(8,128)(2,1)S(1)} %pad_maximum_fusion.8), channel_id=1, source_target_pairs={{0,2},{1,3},{2,0},{3,1},{4,6},{5,7},{6,4},{7,5},{8,10},{9,11},{10,... | collective-permute-start | bytes 294920 | tf_op jit(solution)/shard_map/ppermute | solution.py:33
  39.4 3.3 %collective-permute-start.13 = (bf16[4,128,128]{2,1,0:T(8,128)(2,1)S(1)}, bf16[4,128,128]{2,1,0:T(8,128)(2,1)S(1)}, u32[]{:S(2)}, u32[]{:S(2)}) collective-permute-start(bf16[4,128,128]{2,1,0:T(8,128)(2,1)S(1)} %pad_maximum_fusion.6), channel_id=1, source_target_pairs={{0,1},{1,0},{2,3},{3,2},{4,5},{5,4},{6,7},{7,6},{8,9},{9,8},{10,11... | collective-permute-start | bytes 393224 | tf_op jit(solution)/shard_map/ppermute | solution.py:33
  39.4 3.3 %collective-permute-start.16 = (bf16[1,128,128]{2,1,0:T(8,128)(2,1)S(1)}, bf16[1,128,128]{2,1,0:T(8,128)(2,1)S(1)}, u32[]{:S(2)}, u32[]{:S(2)}) collective-permute-start(bf16[1,128,128]{2,1,0:T(8,128)(2,1)S(1)} %collective-permute-done.14), channel_id=1, source_target_pairs={{0,1},{1,0},{2,3},{3,2},{4,5},{5,4},{6,7},{7,6},{8,9},{9,8},{10,11... | collective-permute-start | bytes 98312 | tf_op jit(solution)/shard_map/ppermute | solution.py:33
  42.7 1.3 %collective-permute-start.17 = (bf16[3,128,128]{2,1,0:T(8,128)(2,1)S(1)}, bf16[3,128,128]{2,1,0:T(8,128)(2,1)S(1)}, u32[]{:S(2)}, u32[]{:S(2)}) collective-permute-start(bf16[3,128,128]{2,1,0:T(8,128)(2,1)S(1)} %collective-permute-done.15), channel_id=1, source_target_pairs={{0,1},{1,0},{2,3},{3,2},{4,5},{5,4},{6,7},{7,6},{8,9},{9,8},{10,11... | collective-permute-start | bytes 294920 | tf_op jit(solution)/shard_map/ppermute | solution.py:33
  44.8 6.4 %collective-permute-start.18 = (bf16[128,128]{1,0:T(8,128)(2,1)S(1)}, bf16[128,128]{1,0:T(8,128)(2,1)S(1)}, u32[]{:S(2)}, u32[]{:S(2)}) collective-permute-start(bf16[128,128]{1,0:T(8,128)(2,1)S(1)} %get-tuple-element.19), channel_id=1, source_target_pairs={{0,4},{1,5},{2,6},{3,7},{4,8},{5,9},{6,10},{7,11},{8,12},{9,13},{1... | collective-permute-start | bytes 98312 | tf_op jit(solution)/shard_map/ppermute | solution.py:26
  45.6 5.6 %collective-permute-start.19 = (bf16[128,128]{1,0:T(8,128)(2,1)S(1)}, bf16[128,128]{1,0:T(8,128)(2,1)S(1)}, u32[]{:S(2)}, u32[]{:S(2)}) collective-permute-start(bf16[128,128]{1,0:T(8,128)(2,1)S(1)} %get-tuple-element.19), channel_id=1, source_target_pairs={{0,8},{1,9},{2,10},{3,11},{4,12},{5,13},{6,14},{7,15},{8,0},{9,1},... | collective-permute-start | bytes 98312 | tf_op jit(solution)/shard_map/ppermute | solution.py:26
  48.1 3.9 %collective-permute-start.20 = (bf16[128,128]{1,0:T(8,128)(2,1)S(1)}, bf16[128,128]{1,0:T(8,128)(2,1)S(1)}, u32[]{:S(2)}, u32[]{:S(2)}) collective-permute-start(bf16[128,128]{1,0:T(8,128)(2,1)S(1)} %get-tuple-element.19), channel_id=1, source_target_pairs={{0,12},{1,13},{2,14},{3,15},{4,0},{5,1},{6,2},{7,3},{8,4},{9,5},{1... | collective-permute-start | bytes 98312 | tf_op jit(solution)/shard_map/ppermute | solution.py:26
  49.6 4.0 %collective-permute-start.22 = (bf16[1,128,128]{2,1,0:T(8,128)(2,1)S(1)}, bf16[1,128,128]{2,1,0:T(8,128)(2,1)S(1)}, u32[]{:S(2)}, u32[]{:S(2)}) collective-permute-start(bf16[1,128,128]{2,1,0:T(8,128)(2,1)S(1)} %bitcast.328), channel_id=1, source_target_pairs={{0,2},{1,3},{2,0},{3,1},{4,6},{5,7},{6,4},{7,5},{8,10},{9,11},{10,... | collective-permute-start | bytes 98312 | tf_op jit(solution)/shard_map/ppermute | solution.py:33
  52.0 4.7 %collective-permute-start.23 = (bf16[3,128,128]{2,1,0:T(8,128)(2,1)S(1)}, bf16[3,128,128]{2,1,0:T(8,128)(2,1)S(1)}, u32[]{:S(2)}, u32[]{:S(2)}) collective-permute-start(bf16[3,128,128]{2,1,0:T(8,128)(2,1)S(1)} %pad_maximum_fusion.9), channel_id=1, source_target_pairs={{0,2},{1,3},{2,0},{3,1},{4,6},{5,7},{6,4},{7,5},{8,10},{9,11},{10,... | collective-permute-start | bytes 294920 | tf_op jit(solution)/shard_map/ppermute | solution.py:33
  53.6 3.1 %collective-permute-start.21 = (bf16[4,128,128]{2,1,0:T(8,128)(2,1)S(1)}, bf16[4,128,128]{2,1,0:T(8,128)(2,1)S(1)}, u32[]{:S(2)}, u32[]{:S(2)}) collective-permute-start(bf16[4,128,128]{2,1,0:T(8,128)(2,1)S(1)} %pad_maximum_fusion.7), channel_id=1, source_target_pairs={{0,1},{1,0},{2,3},{3,2},{4,5},{5,4},{6,7},{7,6},{8,9},{9,8},{10,11... | collective-permute-start | bytes 393224 | tf_op jit(solution)/shard_map/ppermute | solution.py:33
  53.7 3.1 %collective-permute-start.24 = (bf16[1,128,128]{2,1,0:T(8,128)(2,1)S(1)}, bf16[1,128,128]{2,1,0:T(8,128)(2,1)S(1)}, u32[]{:S(2)}, u32[]{:S(2)}) collective-permute-start(bf16[1,128,128]{2,1,0:T(8,128)(2,1)S(1)} %collective-permute-done.22), channel_id=1, source_target_pairs={{0,1},{1,0},{2,3},{3,2},{4,5},{5,4},{6,7},{7,6},{8,9},{9,8},{10,11... | collective-permute-start | bytes 98312 | tf_op jit(solution)/shard_map/ppermute | solution.py:33
  56.7 1.3 %collective-permute-start.25 = (bf16[3,128,128]{2,1,0:T(8,128)(2,1)S(1)}, bf16[3,128,128]{2,1,0:T(8,128)(2,1)S(1)}, u32[]{:S(2)}, u32[]{:S(2)}) collective-permute-start(bf16[3,128,128]{2,1,0:T(8,128)(2,1)S(1)} %collective-permute-done.23), channel_id=1, source_target_pairs={{0,1},{1,0},{2,3},{3,2},{4,5},{5,4},{6,7},{7,6},{8,9},{9,8},{10,11... | collective-permute-start | bytes 294920 | tf_op jit(solution)/shard_map/ppermute | solution.py:33

commit v21 on v14

--- a/solution.py
+++ b/solution.py
@@ -123,7 +123,7 @@
         current = advance(moment, retarded)
         results[moment] = current
         if moment > 0:
-            pieces, new_blocks = gather_blocks(current.astype(jnp.bfloat16), wide, True)
+            pieces, new_blocks = gather_blocks(current.astype(jnp.bfloat16), wide, True, split=True)
             newer[moment] = jnp.concatenate(pieces)
             if recent is None:
                 recent = tiles_by_lag(

time: 59.8 us -> 63.5 us (1.062)
  waiting for transfers between devices: 15.1 us -> 20.7 us
  starting transfers between devices: 28 us -> 26.1 us
    ppermute x9, waiting for transfers between devices: 0.94 us -> 6.23 us  [line_stage(): parts.append(lax.ppermute(x, 'wide', pairs)[None])]
    ppermute x9, starting transfers between devices: 16.9 us -> 14.7 us  [line_stage(): parts.append(lax.ppermute(x, 'wide', pairs)[None])]
    ppermute x17 -> x21, waiting for transfers between devices: 14.2 us -> 14.5 us  [swap(): return lax.ppermute(x, 'wide', [(d, d ^ mask) for d in range(wide)])]
    ppermute x17 -> x21, starting transfers between devices: 11.1 us -> 11.3 us  [swap(): return lax.ppermute(x, 'wide', [(d, d ^ mask) for d in range(wide)])]
    unnamed x22 -> x26, local copies, waits for them, and re-layouts: 1.34 us -> 1.38 us
  transfers between devices with their start and end apart: 26 -> 30, of which waited for: 9 -> 13; matrix products, arithmetic and copies ran while one was open for 20% -> 19% of each run, Pallas kernels for 0% -> 0%
where the time goes in v21:
time: 63.5 us; the launch traced here: 63.3 us
  starting transfers between devices  26.1 us (41%)
  waiting for transfers between devices  20.7 us (33%)
  matrix products  8.03 us (13%)
  local copies, waits for them, and re-layouts  4.22 us (7%)
  other arithmetic  3.79 us (6%)
    ppermute x9, starting transfers between devices, line_stage(): parts.append(lax.ppermute(x, 'wide', pairs)[None])  14.7 us
    ppermute x21, waiting for transfers between devices, swap(): return lax.ppermute(x, 'wide', [(d, d ^ mask) for d in range(wide)])  14.5 us
    ppermute x21, starting transfers between devices, swap(): return lax.ppermute(x, 'wide', [(d, d ^ mask) for d in range(wide)])  11.3 us
    dot_general x27, matrix products, rowwise(): return jnp.einsum(spec, tiles, currents, preferred_element_type=jnp.float32)  7.17 us
    ppermute x9, waiting for transfers between devices, line_stage(): parts.append(lax.ppermute(x, 'wide', pairs)[None])  6.23 us
    sort x1, other arithmetic, per_device(): column_of_block = jnp.argsort(block_owner)  1.9 us
    unnamed x26, local copies, waits for them, and re-layouts  1.38 us
  transfers between devices with their start and end apart: 30, of which 13 were waited for; matrix products, arithmetic and copies ran while one was open for 19% of the time, Pallas kernels for 0%

profile of v21, /device:TPU:0, one launch (start us, length us, event | category | flops | bytes accessed | tf_op | source)
XLA Modules:
  0.0 63.3 jit_solution(3752616993740191150)
XLA Ops:
  0.0 3.0 %collective-permute-start = (bf16[4,128,128]{2,1,0:T(8,128)(2,1)}, bf16[4,128,128]{2,1,0:T(8,128)(2,1)S(1)}, u32[]{:S(2)}, u32[]{:S(2)}) collective-permute-start(bf16[4,128,128]{2,1,0:T(8,128)(2,1)} %param.19), channel_id=1, source_target_pairs={{0,4},{1,5},{2,6},{3,7},{4,8},{5,9},{6,10},{7,11},{8,12},{9,13},{1... | collective-permute-start | bytes 393224 | tf_op jit(solution)/shard_map/ppermute | solution.py:26
  3.0 2.6 %collective-permute-start.1 = (bf16[4,128,128]{2,1,0:T(8,128)(2,1)}, bf16[4,128,128]{2,1,0:T(8,128)(2,1)S(1)}, u32[]{:S(2)}, u32[]{:S(2)}) collective-permute-start(bf16[4,128,128]{2,1,0:T(8,128)(2,1)} %param.19), channel_id=1, source_target_pairs={{0,8},{1,9},{2,10},{3,11},{4,12},{5,13},{6,14},{7,15},{8,0},{9,1},... | collective-permute-start | bytes 393224 | tf_op jit(solution)/shard_map/ppermute | solution.py:26
  5.6 1.3 %collective-permute-start.2 = (bf16[4,128,128]{2,1,0:T(8,128)(2,1)}, bf16[4,128,128]{2,1,0:T(8,128)(2,1)S(1)}, u32[]{:S(2)}, u32[]{:S(2)}) collective-permute-start(bf16[4,128,128]{2,1,0:T(8,128)(2,1)} %param.19), channel_id=1, source_target_pairs={{0,12},{1,13},{2,14},{3,15},{4,0},{5,1},{6,2},{7,3},{8,4},{9,5},{1... | collective-permute-start | bytes 393224 | tf_op jit(solution)/shard_map/ppermute | solution.py:26
  7.0 1.5 %collective-permute-start.4 = (bf16[1,4,128,128]{3,2,1,0:T(8,128)(2,1)}, bf16[1,4,128,128]{3,2,1,0:T(8,128)(2,1)S(1)}, u32[]{:S(2)}, u32[]{:S(2)}) collective-permute-start(bf16[1,4,128,128]{3,2,1,0:T(8,128)(2,1)} %bitcast.320), channel_id=1, source_target_pairs={{0,2},{1,3},{2,0},{3,1},{4,6},{5,7},{6,4},{7,5},{8,10},{9,11},{10,... | collective-permute-start | bytes 393224 | tf_op jit(solution)/shard_map/ppermute | solution.py:33
  8.7 1.9 %sort.17 = (s32[16]{0:T(128)}, s32[16]{0:T(128)S(1)}) sort(s32[16]{0:T(128)} %param.18, s32[16]{0:T(128)S(1)} %iota.5), dimensions={0}, to_apply=%region_0.0 | sort | flops 64 | bytes 256 | tf_op jit(solution)/shard_map/jit(argsort)/sort | solution.py:94
  10.6 0.7 %gather_fusion = s32[16]{0:T(128)S(1)} fusion(s32[16]{0:T(128)S(1)} %get-tuple-element.8, s32[1024]{0:T(1024)S(1)} %pad_clamp_fusion.1), kind=kCustom, calls=%fused_computation.clone | custom fusion | bytes 192 | tf_op jit(solution)/shard_map/jit(_take)/gather | solution.py:69
  11.3 0.8 %copy.17 = s32[16,2]{1,0:T(8,128)S(1)} copy(s32[16,2]{0,1:T(2,128)} %bitcast.330) | data formatting | bytes 256 | tf_op jit(solution)/shard_map/squeeze | solution.py:71
  12.0 0.7 %gather_fusion.2 = bf16[16,2,128,128]{3,2,1,0:T(8,128)(2,1)S(1)} fusion(bf16[16,2,128,128]{3,2,1,0:T(8,128)(2,1)S(1)} %bitcast.299, s32[1024]{0:T(1024)S(1)} %pad_clamp_fusion), kind=kCustom, calls=%fused_computation.2.clone | custom fusion | bytes 2097216 | tf_op jit(solution)/shard_map/jit(_take)/gather | solution.py:70
  12.8 0.6 gather_fusion.1
  14.5 0.5 copy-done.3
  15.1 1.1 %collective-permute-start.5 = (bf16[1,4,128,128]{3,2,1,0:T(8,128)(2,1)S(1)}, bf16[1,4,128,128]{3,2,1,0:T(8,128)(2,1)S(1)}, u32[]{:S(2)}, u32[]{:S(2)}) collective-permute-start(bf16[1,4,128,128]{3,2,1,0:T(8,128)(2,1)S(1)} %bitcast.324), channel_id=1, source_target_pairs={{0,2},{1,3},{2,0},{3,1},{4,6},{5,7},{6,4},{7,5},{8,10},{9,11},{10,... | collective-permute-start | bytes 393224 | tf_op jit(solution)/shard_map/ppermute | solution.py:33
  16.2 1.0 %collective-permute-start.6 = (bf16[2,4,128,128]{3,2,1,0:T(8,128)(2,1)S(1)}, bf16[2,4,128,128]{3,2,1,0:T(8,128)(2,1)S(1)}, u32[]{:S(2)}, u32[]{:S(2)}) collective-permute-start(bf16[2,4,128,128]{3,2,1,0:T(8,128)(2,1)S(1)} %pad_maximum_fusion.4), channel_id=1, source_target_pairs={{0,2},{1,3},{2,0},{3,1},{4,6},{5,7},{6,4},{7,5},{8,10},{9,11},{10,... | collective-permute-start | bytes 786440 | tf_op jit(solution)/shard_map/ppermute | solution.py:33
  17.2 0.3 convolution_bitcast_fusion.5
  17.6 0.3 collective-permute-start.7
  18.1 3.0 %collective-permute-done.5 = bf16[1,4,128,128]{3,2,1,0:T(8,128)(2,1)S(1)} collective-permute-done((bf16[1,4,128,128]{3,2,1,0:T(8,128)(2,1)S(1)}, bf16[1,4,128,128]{3,2,1,0:T(8,128)(2,1)S(1)}, u32[]{:S(2)}, u32[]{:S(2)}) %collective-permute-start.5) | collective-permute-done | bytes 131104 | tf_op jit(solution)/shard_map/ppermute | solution.py:33
  21.7 0.7 %collective-permute-done.8 = bf16[1,4,128,128]{3,2,1,0:T(8,128)(2,1)S(1)} collective-permute-done((bf16[1,4,128,128]{3,2,1,0:T(8,128)(2,1)S(1)}, bf16[1,4,128,128]{3,2,1,0:T(8,128)(2,1)S(1)}, u32[]{:S(2)}, u32[]{:S(2)}) %collective-permute-start.8) | collective-permute-done | bytes 131104 | tf_op jit(solution)/shard_map/ppermute | solution.py:33
  22.9 2.9 %collective-permute-done.6 = bf16[2,4,128,128]{3,2,1,0:T(8,128)(2,1)S(1)} collective-permute-done((bf16[2,4,128,128]{3,2,1,0:T(8,128)(2,1)S(1)}, bf16[2,4,128,128]{3,2,1,0:T(8,128)(2,1)S(1)}, u32[]{:S(2)}, u32[]{:S(2)}) %collective-permute-start.6) | collective-permute-done | bytes 262176 | tf_op jit(solution)/shard_map/ppermute | solution.py:33
  26.8 0.4 convolution_bitcast_fusion
  27.1 0.4 fusion.26
  28.1 0.6 copy-done.2
  28.9 0.3 constant_dynamic-update-slice_fusion.10
  29.2 2.3 %collective-permute-start.11 = (bf16[128,128]{1,0:T(8,128)(2,1)S(1)}, bf16[128,128]{1,0:T(8,128)(2,1)S(1)}, u32[]{:S(2)}, u32[]{:S(2)}) collective-permute-start(bf16[128,128]{1,0:T(8,128)(2,1)S(1)} %get-tuple-element.21), channel_id=1, source_target_pairs={{0,8},{1,9},{2,10},{3,11},{4,12},{5,13},{6,14},{7,15},{8,0},{9,1},... | collective-permute-start | bytes 98312 | tf_op jit(solution)/shard_map/ppermute | solution.py:26
  31.5 3.3 %collective-permute-start.12 = (bf16[128,128]{1,0:T(8,128)(2,1)S(1)}, bf16[128,128]{1,0:T(8,128)(2,1)S(1)}, u32[]{:S(2)}, u32[]{:S(2)}) collective-permute-start(bf16[128,128]{1,0:T(8,128)(2,1)S(1)} %get-tuple-element.21), channel_id=1, source_target_pairs={{0,12},{1,13},{2,14},{3,15},{4,0},{5,1},{6,2},{7,3},{8,4},{9,5},{1... | collective-permute-start | bytes 98312 | tf_op jit(solution)/shard_map/ppermute | solution.py:26
  34.8 1.5 %collective-permute-start.14 = (bf16[1,128,128]{2,1,0:T(8,128)(2,1)S(1)}, bf16[1,128,128]{2,1,0:T(8,128)(2,1)S(1)}, u32[]{:S(2)}, u32[]{:S(2)}) collective-permute-start(bf16[1,128,128]{2,1,0:T(8,128)(2,1)S(1)} %bitcast.326), channel_id=1, source_target_pairs={{0,2},{1,3},{2,0},{3,1},{4,6},{5,7},{6,4},{7,5},{8,10},{9,11},{10,... | collective-permute-start | bytes 98312 | tf_op jit(solution)/shard_map/ppermute | solution.py:33
  36.9 0.3 fusion.25
  37.9 2.6 %collective-permute-done.10 = bf16[128,128]{1,0:T(8,128)(2,1)S(1)} collective-permute-done((bf16[128,128]{1,0:T(8,128)(2,1)S(1)}, bf16[128,128]{1,0:T(8,128)(2,1)S(1)}, u32[]{:S(2)}, u32[]{:S(2)}) %collective-permute-start.10) | collective-permute-done | bytes 32800 | tf_op jit(solution)/shard_map/ppermute | solution.py:26
  40.6 1.6 %collective-permute-start.15 = (bf16[1,128,128]{2,1,0:T(8,128)(2,1)S(1)}, bf16[1,128,128]{2,1,0:T(8,128)(2,1)S(1)}, u32[]{:S(2)}, u32[]{:S(2)}) collective-permute-start(bf16[1,128,128]{2,1,0:T(8,128)(2,1)S(1)} %bitcast.317), channel_id=1, source_target_pairs={{0,2},{1,3},{2,0},{3,1},{4,6},{5,7},{6,4},{7,5},{8,10},{9,11},{10,... | collective-permute-start | bytes 98312 | tf_op jit(solution)/shard_map/ppermute | solution.py:33
  42.1 0.5 collective-permute-start.16
  42.7 0.6 collective-permute-start.17
  43.3 1.3 %collective-permute-done.15 = bf16[1,128,128]{2,1,0:T(8,128)(2,1)S(1)} collective-permute-done((bf16[1,128,128]{2,1,0:T(8,128)(2,1)S(1)}, bf16[1,128,128]{2,1,0:T(8,128)(2,1)S(1)}, u32[]{:S(2)}, u32[]{:S(2)}) %collective-permute-start.15) | collective-permute-done | bytes 32800 | tf_op jit(solution)/shard_map/ppermute | solution.py:33
  44.5 1.9 %collective-permute-done.16 = bf16[2,128,128]{2,1,0:T(8,128)(2,1)S(1)} collective-permute-done((bf16[2,128,128]{2,1,0:T(8,128)(2,1)S(1)}, bf16[2,128,128]{2,1,0:T(8,128)(2,1)S(1)}, u32[]{:S(2)}, u32[]{:S(2)}) %collective-permute-start.16) | collective-permute-done | bytes 65568 | tf_op jit(solution)/shard_map/ppermute | solution.py:33
  46.5 1.1 %collective-permute-done.19 = bf16[2,128,128]{2,1,0:T(8,128)(2,1)S(1)} collective-permute-done((bf16[2,128,128]{2,1,0:T(8,128)(2,1)S(1)}, bf16[2,128,128]{2,1,0:T(8,128)(2,1)S(1)}, u32[]{:S(2)}, u32[]{:S(2)}) %collective-permute-start.19) | collective-permute-done | bytes 65568 | tf_op jit(solution)/shard_map/ppermute | solution.py:33
  47.7 0.3 convolution_bitcast_fusion.11
  48.3 0.3 constant_dynamic-update-slice_fusion.21
  48.6 0.9 %collective-permute-start.22 = (bf16[128,128]{1,0:T(8,128)(2,1)S(1)}, bf16[128,128]{1,0:T(8,128)(2,1)S(1)}, u32[]{:S(2)}, u32[]{:S(2)}) collective-permute-start(bf16[128,128]{1,0:T(8,128)(2,1)S(1)} %get-tuple-element.19), channel_id=1, source_target_pairs={{0,12},{1,13},{2,14},{3,15},{4,0},{5,1},{6,2},{7,3},{8,4},{9,5},{1... | collective-permute-start | bytes 98312 | tf_op jit(solution)/shard_map/ppermute | solution.py:26
  49.5 1.2 %collective-permute-start.20 = (bf16[128,128]{1,0:T(8,128)(2,1)S(1)}, bf16[128,128]{1,0:T(8,128)(2,1)S(1)}, u32[]{:S(2)}, u32[]{:S(2)}) collective-permute-start(bf16[128,128]{1,0:T(8,128)(2,1)S(1)} %get-tuple-element.19), channel_id=1, source_target_pairs={{0,4},{1,5},{2,6},{3,7},{4,8},{5,9},{6,10},{7,11},{8,12},{9,13},{1... | collective-permute-start | bytes 98312 | tf_op jit(solution)/shard_map/ppermute | solution.py:26
  50.7 0.5 convolution_bitcast_fusion.9
  51.2 0.6 collective-permute-start.24
  51.8 1.6 %collective-permute-done.21 = bf16[128,128]{1,0:T(8,128)(2,1)S(1)} collective-permute-done((bf16[128,128]{1,0:T(8,128)(2,1)S(1)}, bf16[128,128]{1,0:T(8,128)(2,1)S(1)}, u32[]{:S(2)}, u32[]{:S(2)}) %collective-permute-start.21) | collective-permute-done | bytes 32800 | tf_op jit(solution)/shard_map/ppermute | solution.py:26
  53.4 1.8 %collective-permute-done.20 = bf16[128,128]{1,0:T(8,128)(2,1)S(1)} collective-permute-done((bf16[128,128]{1,0:T(8,128)(2,1)S(1)}, bf16[128,128]{1,0:T(8,128)(2,1)S(1)}, u32[]{:S(2)}, u32[]{:S(2)}) %collective-permute-start.20) | collective-permute-done | bytes 32800 | tf_op jit(solution)/shard_map/ppermute | solution.py:26
  55.3 0.9 %collective-permute-start.25 = (bf16[1,128,128]{2,1,0:T(8,128)(2,1)S(1)}, bf16[1,128,128]{2,1,0:T(8,128)(2,1)S(1)}, u32[]{:S(2)}, u32[]{:S(2)}) collective-permute-start(bf16[1,128,128]{2,1,0:T(8,128)(2,1)S(1)} %bitcast.319), channel_id=1, source_target_pairs={{0,2},{1,3},{2,0},{3,1},{4,6},{5,7},{6,4},{7,5},{8,10},{9,11},{10,... | collective-permute-start | bytes 98312 | tf_op jit(solution)/shard_map/ppermute | solution.py:33
  56.2 1.2 %collective-permute-start.26 = (bf16[2,128,128]{2,1,0:T(8,128)(2,1)S(1)}, bf16[2,128,128]{2,1,0:T(8,128)(2,1)S(1)}, u32[]{:S(2)}, u32[]{:S(2)}) collective-permute-start(bf16[2,128,128]{2,1,0:T(8,128)(2,1)S(1)} %pad_maximum_fusion.9), channel_id=1, source_target_pairs={{0,2},{1,3},{2,0},{3,1},{4,6},{5,7},{6,4},{7,5},{8,10},{9,11},{10,... | collective-permute-start | bytes 196616 | tf_op jit(solution)/shard_map/ppermute | solution.py:33
  57.4 0.6 collective-permute-start.27
  58.0 1.3 %collective-permute-done.25 = bf16[1,128,128]{2,1,0:T(8,128)(2,1)S(1)} collective-permute-done((bf16[1,128,128]{2,1,0:T(8,128)(2,1)S(1)}, bf16[1,128,128]{2,1,0:T(8,128)(2,1)S(1)}, u32[]{:S(2)}, u32[]{:S(2)}) %collective-permute-start.25) | collective-permute-done | bytes 32800 | tf_op jit(solution)/shard_map/ppermute | solution.py:33
  59.3 1.2 %collective-permute-done.26 = bf16[2,128,128]{2,1,0:T(8,128)(2,1)S(1)} collective-permute-done((bf16[2,128,128]{2,1,0:T(8,128)(2,1)S(1)}, bf16[2,128,128]{2,1,0:T(8,128)(2,1)S(1)}, u32[]{:S(2)}, u32[]{:S(2)}) %collective-permute-start.26) | collective-permute-done | bytes 65568 | tf_op jit(solution)/shard_map/ppermute | solution.py:33
  60.6 1.1 %collective-permute-done.29 = bf16[2,128,128]{2,1,0:T(8,128)(2,1)S(1)} collective-permute-done((bf16[2,128,128]{2,1,0:T(8,128)(2,1)S(1)}, bf16[2,128,128]{2,1,0:T(8,128)(2,1)S(1)}, u32[]{:S(2)}, u32[]{:S(2)}) %collective-permute-start.29) | collective-permute-done | bytes 65568 | tf_op jit(solution)/shard_map/ppermute | solution.py:33
  61.7 0.3 convolution_bitcast_fusion.10
  62.6 0.7 %pad_maximum_fusion.5 = f32[3,128,128]{2,1,0:T(8,128)} fusion(f32[1,128,128]{2,1,0:T(8,128)S(1)} %bitcast.314, f32[1,128,128]{2,1,0:T(8,128)S(1)} %bitcast.315, f32[1,128,128]{2,1,0:T(8,128)S(1)} %convolution_bitcast_fusion.8), kind=kLoop, calls=%fused_computation.89 | loop fusion | flops 98304 | bytes 393216 | tf_op jit(solution)/shard_map/stack | solution.py:136
  (95 shorter events, 6.8 us)
Async XLA Ops:
  0.0 12.0 %copy-start = (bf16[1,16,2,128,128]{4,3,2,1,0:T(8,128)(2,1)S(1)}, bf16[1,16,2,128,128]{4,3,2,1,0:T(8,128)(2,1)}, u32[]{:S(2)}) copy-start(bf16[1,16,2,128,128]{4,3,2,1,0:T(8,128)(2,1)} %param.16) | copy-start | bytes 3145732
  0.0 14.5 %collective-permute-start = (bf16[4,128,128]{2,1,0:T(8,128)(2,1)}, bf16[4,128,128]{2,1,0:T(8,128)(2,1)S(1)}, u32[]{:S(2)}, u32[]{:S(2)}) collective-permute-start(bf16[4,128,128]{2,1,0:T(8,128)(2,1)} %param.19), channel_id=1, source_target_pairs={{0,4},{1,5},{2,6},{3,7},{4,8},{5,9},{6,10},{7,11},{8,12},{9,13},{1... | collective-permute-start | bytes 393224 | tf_op jit(solution)/shard_map/ppermute | solution.py:26
  3.0 11.4 %collective-permute-start.1 = (bf16[4,128,128]{2,1,0:T(8,128)(2,1)}, bf16[4,128,128]{2,1,0:T(8,128)(2,1)S(1)}, u32[]{:S(2)}, u32[]{:S(2)}) collective-permute-start(bf16[4,128,128]{2,1,0:T(8,128)(2,1)} %param.19), channel_id=1, source_target_pairs={{0,8},{1,9},{2,10},{3,11},{4,12},{5,13},{6,14},{7,15},{8,0},{9,1},... | collective-permute-start | bytes 393224 | tf_op jit(solution)/shard_map/ppermute | solution.py:26
  5.6 8.9 %collective-permute-start.2 = (bf16[4,128,128]{2,1,0:T(8,128)(2,1)}, bf16[4,128,128]{2,1,0:T(8,128)(2,1)S(1)}, u32[]{:S(2)}, u32[]{:S(2)}) collective-permute-start(bf16[4,128,128]{2,1,0:T(8,128)(2,1)} %param.19), channel_id=1, source_target_pairs={{0,12},{1,13},{2,14},{3,15},{4,0},{5,1},{6,2},{7,3},{8,4},{9,5},{1... | collective-permute-start | bytes 393224 | tf_op jit(solution)/shard_map/ppermute | solution.py:26
  7.0 10.6 %collective-permute-start.4 = (bf16[1,4,128,128]{3,2,1,0:T(8,128)(2,1)}, bf16[1,4,128,128]{3,2,1,0:T(8,128)(2,1)S(1)}, u32[]{:S(2)}, u32[]{:S(2)}) collective-permute-start(bf16[1,4,128,128]{3,2,1,0:T(8,128)(2,1)} %bitcast.320), channel_id=1, source_target_pairs={{0,2},{1,3},{2,0},{3,1},{4,6},{5,7},{6,4},{7,5},{8,10},{9,11},{10,... | collective-permute-start | bytes 393224 | tf_op jit(solution)/shard_map/ppermute | solution.py:33
  14.1 0.9 %copy-start.3 = (bf16[4,128,128]{2,1,0:T(8,128)(2,1)S(1)}, bf16[4,128,128]{2,1,0:T(8,128)(2,1)}, u32[]{:S(2)}) copy-start(bf16[4,128,128]{2,1,0:T(8,128)(2,1)} %param.19) | copy-start | bytes 393220
  15.1 6.0 %collective-permute-start.5 = (bf16[1,4,128,128]{3,2,1,0:T(8,128)(2,1)S(1)}, bf16[1,4,128,128]{3,2,1,0:T(8,128)(2,1)S(1)}, u32[]{:S(2)}, u32[]{:S(2)}) collective-permute-start(bf16[1,4,128,128]{3,2,1,0:T(8,128)(2,1)S(1)} %bitcast.324), channel_id=1, source_target_pairs={{0,2},{1,3},{2,0},{3,1},{4,6},{5,7},{6,4},{7,5},{8,10},{9,11},{10,... | collective-permute-start | bytes 393224 | tf_op jit(solution)/shard_map/ppermute | solution.py:33
  16.2 10.6 %collective-permute-start.3 = (bf16[4,4,128,128]{3,2,1,0:T(8,128)(2,1)S(1)}, bf16[4,4,128,128]{3,2,1,0:T(8,128)(2,1)S(1)}, u32[]{:S(2)}, u32[]{:S(2)}) collective-permute-start(bf16[4,4,128,128]{3,2,1,0:T(8,128)(2,1)S(1)} %pad_maximum_fusion.3), channel_id=1, source_target_pairs={{0,1},{1,0},{2,3},{3,2},{4,5},{5,4},{6,7},{7,6},{8,9},{9,8},{10,11... | collective-permute-start | bytes 1572872 | tf_op jit(solution)/shard_map/ppermute | solution.py:33
  16.2 9.6 %collective-permute-start.6 = (bf16[2,4,128,128]{3,2,1,0:T(8,128)(2,1)S(1)}, bf16[2,4,128,128]{3,2,1,0:T(8,128)(2,1)S(1)}, u32[]{:S(2)}, u32[]{:S(2)}) collective-permute-start(bf16[2,4,128,128]{3,2,1,0:T(8,128)(2,1)S(1)} %pad_maximum_fusion.4), channel_id=1, source_target_pairs={{0,2},{1,3},{2,0},{3,1},{4,6},{5,7},{6,4},{7,5},{8,10},{9,11},{10,... | collective-permute-start | bytes 786440 | tf_op jit(solution)/shard_map/ppermute | solution.py:33
  17.6 10.5 %collective-permute-start.7 = (bf16[1,4,128,128]{3,2,1,0:T(8,128)(2,1)S(1)}, bf16[1,4,128,128]{3,2,1,0:T(8,128)(2,1)S(1)}, u32[]{:S(2)}, u32[]{:S(2)}) collective-permute-start(bf16[1,4,128,128]{3,2,1,0:T(8,128)(2,1)S(1)} %collective-permute-done.4), channel_id=1, source_target_pairs={{0,1},{1,0},{2,3},{3,2},{4,5},{5,4},{6,7},{7,6},{8,9},{9,8},{10,11... | collective-permute-start | bytes 393224 | tf_op jit(solution)/shard_map/ppermute | solution.py:33
  21.1 1.3 %collective-permute-start.8 = (bf16[1,4,128,128]{3,2,1,0:T(8,128)(2,1)S(1)}, bf16[1,4,128,128]{3,2,1,0:T(8,128)(2,1)S(1)}, u32[]{:S(2)}, u32[]{:S(2)}) collective-permute-start(bf16[1,4,128,128]{3,2,1,0:T(8,128)(2,1)S(1)} %collective-permute-done.5), channel_id=1, source_target_pairs={{0,1},{1,0},{2,3},{3,2},{4,5},{5,4},{6,7},{7,6},{8,9},{9,8},{10,11... | collective-permute-start | bytes 393224 | tf_op jit(solution)/shard_map/ppermute | solution.py:33
  25.8 2.0 %collective-permute-start.9 = (bf16[2,4,128,128]{3,2,1,0:T(8,128)(2,1)S(1)}, bf16[2,4,128,128]{3,2,1,0:T(8,128)(2,1)S(1)}, u32[]{:S(2)}, u32[]{:S(2)}) collective-permute-start(bf16[2,4,128,128]{3,2,1,0:T(8,128)(2,1)S(1)} %collective-permute-done.6), channel_id=1, source_target_pairs={{0,1},{1,0},{2,3},{3,2},{4,5},{5,4},{6,7},{7,6},{8,9},{9,8},{10,11... | collective-permute-start | bytes 786440 | tf_op jit(solution)/shard_map/ppermute | solution.py:33
  27.7 0.9 %copy-start.2 = (f32[3,128,128]{2,1,0:T(8,128)S(1)}, f32[3,128,128]{2,1,0:T(8,128)}, u32[]{:S(2)}) copy-start(f32[3,128,128]{2,1,0:T(8,128)} %param.20) | copy-start | bytes 589828
  28.0 0.9 %copy-start.1 = (f32[1,128,128]{2,1,0:T(8,128)S(1)}, f32[1,128,128]{2,1,0:T(8,128)}, u32[]{:S(2)}) copy-start(f32[1,128,128]{2,1,0:T(8,128)} %param.21) | copy-start | bytes 196612
  29.2 8.7 %collective-permute-start.11 = (bf16[128,128]{1,0:T(8,128)(2,1)S(1)}, bf16[128,128]{1,0:T(8,128)(2,1)S(1)}, u32[]{:S(2)}, u32[]{:S(2)}) collective-permute-start(bf16[128,128]{1,0:T(8,128)(2,1)S(1)} %get-tuple-element.21), channel_id=1, source_target_pairs={{0,8},{1,9},{2,10},{3,11},{4,12},{5,13},{6,14},{7,15},{8,0},{9,1},... | collective-permute-start | bytes 98312 | tf_op jit(solution)/shard_map/ppermute | solution.py:26
  31.5 6.4 %collective-permute-start.12 = (bf16[128,128]{1,0:T(8,128)(2,1)S(1)}, bf16[128,128]{1,0:T(8,128)(2,1)S(1)}, u32[]{:S(2)}, u32[]{:S(2)}) collective-permute-start(bf16[128,128]{1,0:T(8,128)(2,1)S(1)} %get-tuple-element.21), channel_id=1, source_target_pairs={{0,12},{1,13},{2,14},{3,15},{4,0},{5,1},{6,2},{7,3},{8,4},{9,5},{1... | collective-permute-start | bytes 98312 | tf_op jit(solution)/shard_map/ppermute | solution.py:26
  34.8 5.7 %collective-permute-start.10 = (bf16[128,128]{1,0:T(8,128)(2,1)S(1)}, bf16[128,128]{1,0:T(8,128)(2,1)S(1)}, u32[]{:S(2)}, u32[]{:S(2)}) collective-permute-start(bf16[128,128]{1,0:T(8,128)(2,1)S(1)} %get-tuple-element.21), channel_id=1, source_target_pairs={{0,4},{1,5},{2,6},{3,7},{4,8},{5,9},{6,10},{7,11},{8,12},{9,13},{1... | collective-permute-start | bytes 98312 | tf_op jit(solution)/shard_map/ppermute | solution.py:26
  34.8 7.9 %collective-permute-start.14 = (bf16[1,128,128]{2,1,0:T(8,128)(2,1)S(1)}, bf16[1,128,128]{2,1,0:T(8,128)(2,1)S(1)}, u32[]{:S(2)}, u32[]{:S(2)}) collective-permute-start(bf16[1,128,128]{2,1,0:T(8,128)(2,1)S(1)} %bitcast.326), channel_id=1, source_target_pairs={{0,2},{1,3},{2,0},{3,1},{4,6},{5,7},{6,4},{7,5},{8,10},{9,11},{10,... | collective-permute-start | bytes 98312 | tf_op jit(solution)/shard_map/ppermute | solution.py:33
  40.6 4.0 %collective-permute-start.15 = (bf16[1,128,128]{2,1,0:T(8,128)(2,1)S(1)}, bf16[1,128,128]{2,1,0:T(8,128)(2,1)S(1)}, u32[]{:S(2)}, u32[]{:S(2)}) collective-permute-start(bf16[1,128,128]{2,1,0:T(8,128)(2,1)S(1)} %bitcast.317), channel_id=1, source_target_pairs={{0,2},{1,3},{2,0},{3,1},{4,6},{5,7},{6,4},{7,5},{8,10},{9,11},{10,... | collective-permute-start | bytes 98312 | tf_op jit(solution)/shard_map/ppermute | solution.py:33
  42.1 4.3 %collective-permute-start.16 = (bf16[2,128,128]{2,1,0:T(8,128)(2,1)S(1)}, bf16[2,128,128]{2,1,0:T(8,128)(2,1)S(1)}, u32[]{:S(2)}, u32[]{:S(2)}) collective-permute-start(bf16[2,128,128]{2,1,0:T(8,128)(2,1)S(1)} %pad_maximum_fusion.8), channel_id=1, source_target_pairs={{0,2},{1,3},{2,0},{3,1},{4,6},{5,7},{6,4},{7,5},{8,10},{9,11},{10,... | collective-permute-start | bytes 196616 | tf_op jit(solution)/shard_map/ppermute | solution.py:33
  42.7 3.8 %collective-permute-start.13 = (bf16[4,128,128]{2,1,0:T(8,128)(2,1)S(1)}, bf16[4,128,128]{2,1,0:T(8,128)(2,1)S(1)}, u32[]{:S(2)}, u32[]{:S(2)}) collective-permute-start(bf16[4,128,128]{2,1,0:T(8,128)(2,1)S(1)} %pad_maximum_fusion.6), channel_id=1, source_target_pairs={{0,1},{1,0},{2,3},{3,2},{4,5},{5,4},{6,7},{7,6},{8,9},{9,8},{10,11... | collective-permute-start | bytes 393224 | tf_op jit(solution)/shard_map/ppermute | solution.py:33
  42.7 3.8 %collective-permute-start.17 = (bf16[1,128,128]{2,1,0:T(8,128)(2,1)S(1)}, bf16[1,128,128]{2,1,0:T(8,128)(2,1)S(1)}, u32[]{:S(2)}, u32[]{:S(2)}) collective-permute-start(bf16[1,128,128]{2,1,0:T(8,128)(2,1)S(1)} %collective-permute-done.14), channel_id=1, source_target_pairs={{0,1},{1,0},{2,3},{3,2},{4,5},{5,4},{6,7},{7,6},{8,9},{9,8},{10,11... | collective-permute-start | bytes 98312 | tf_op jit(solution)/shard_map/ppermute | solution.py:33
  44.5 2.0 %collective-permute-start.18 = (bf16[1,128,128]{2,1,0:T(8,128)(2,1)S(1)}, bf16[1,128,128]{2,1,0:T(8,128)(2,1)S(1)}, u32[]{:S(2)}, u32[]{:S(2)}) collective-permute-start(bf16[1,128,128]{2,1,0:T(8,128)(2,1)S(1)} %collective-permute-done.15), channel_id=1, source_target_pairs={{0,1},{1,0},{2,3},{3,2},{4,5},{5,4},{6,7},{7,6},{8,9},{9,8},{10,11... | collective-permute-start | bytes 98312 | tf_op jit(solution)/shard_map/ppermute | solution.py:33
  46.4 1.3 %collective-permute-start.19 = (bf16[2,128,128]{2,1,0:T(8,128)(2,1)S(1)}, bf16[2,128,128]{2,1,0:T(8,128)(2,1)S(1)}, u32[]{:S(2)}, u32[]{:S(2)}) collective-permute-start(bf16[2,128,128]{2,1,0:T(8,128)(2,1)S(1)} %collective-permute-done.16), channel_id=1, source_target_pairs={{0,1},{1,0},{2,3},{3,2},{4,5},{5,4},{6,7},{7,6},{8,9},{9,8},{10,11... | collective-permute-start | bytes 196616 | tf_op jit(solution)/shard_map/ppermute | solution.py:33
  48.6 4.9 %collective-permute-start.21 = (bf16[128,128]{1,0:T(8,128)(2,1)S(1)}, bf16[128,128]{1,0:T(8,128)(2,1)S(1)}, u32[]{:S(2)}, u32[]{:S(2)}) collective-permute-start(bf16[128,128]{1,0:T(8,128)(2,1)S(1)} %get-tuple-element.19), channel_id=1, source_target_pairs={{0,8},{1,9},{2,10},{3,11},{4,12},{5,13},{6,14},{7,15},{8,0},{9,1},... | collective-permute-start | bytes 98312 | tf_op jit(solution)/shard_map/ppermute | solution.py:26
  48.6 4.8 %collective-permute-start.22 = (bf16[128,128]{1,0:T(8,128)(2,1)S(1)}, bf16[128,128]{1,0:T(8,128)(2,1)S(1)}, u32[]{:S(2)}, u32[]{:S(2)}) collective-permute-start(bf16[128,128]{1,0:T(8,128)(2,1)S(1)} %get-tuple-element.19), channel_id=1, source_target_pairs={{0,12},{1,13},{2,14},{3,15},{4,0},{5,1},{6,2},{7,3},{8,4},{9,5},{1... | collective-permute-start | bytes 98312 | tf_op jit(solution)/shard_map/ppermute | solution.py:26
  49.5 5.7 %collective-permute-start.20 = (bf16[128,128]{1,0:T(8,128)(2,1)S(1)}, bf16[128,128]{1,0:T(8,128)(2,1)S(1)}, u32[]{:S(2)}, u32[]{:S(2)}) collective-permute-start(bf16[128,128]{1,0:T(8,128)(2,1)S(1)} %get-tuple-element.19), channel_id=1, source_target_pairs={{0,4},{1,5},{2,6},{3,7},{4,8},{5,9},{6,10},{7,11},{8,12},{9,13},{1... | collective-permute-start | bytes 98312 | tf_op jit(solution)/shard_map/ppermute | solution.py:26
  51.2 6.2 %collective-permute-start.24 = (bf16[1,128,128]{2,1,0:T(8,128)(2,1)S(1)}, bf16[1,128,128]{2,1,0:T(8,128)(2,1)S(1)}, u32[]{:S(2)}, u32[]{:S(2)}) collective-permute-start(bf16[1,128,128]{2,1,0:T(8,128)(2,1)S(1)} %bitcast.328), channel_id=1, source_target_pairs={{0,2},{1,3},{2,0},{3,1},{4,6},{5,7},{6,4},{7,5},{8,10},{9,11},{10,... | collective-permute-start | bytes 98312 | tf_op jit(solution)/shard_map/ppermute | solution.py:33
  55.3 4.0 %collective-permute-start.25 = (bf16[1,128,128]{2,1,0:T(8,128)(2,1)S(1)}, bf16[1,128,128]{2,1,0:T(8,128)(2,1)S(1)}, u32[]{:S(2)}, u32[]{:S(2)}) collective-permute-start(bf16[1,128,128]{2,1,0:T(8,128)(2,1)S(1)} %bitcast.319), channel_id=1, source_target_pairs={{0,2},{1,3},{2,0},{3,1},{4,6},{5,7},{6,4},{7,5},{8,10},{9,11},{10,... | collective-permute-start | bytes 98312 | tf_op jit(solution)/shard_map/ppermute | solution.py:33
  56.2 4.3 %collective-permute-start.26 = (bf16[2,128,128]{2,1,0:T(8,128)(2,1)S(1)}, bf16[2,128,128]{2,1,0:T(8,128)(2,1)S(1)}, u32[]{:S(2)}, u32[]{:S(2)}) collective-permute-start(bf16[2,128,128]{2,1,0:T(8,128)(2,1)S(1)} %pad_maximum_fusion.9), channel_id=1, source_target_pairs={{0,2},{1,3},{2,0},{3,1},{4,6},{5,7},{6,4},{7,5},{8,10},{9,11},{10,... | collective-permute-start | bytes 196616 | tf_op jit(solution)/shard_map/ppermute | solution.py:33
  57.4 3.1 %collective-permute-start.23 = (bf16[4,128,128]{2,1,0:T(8,128)(2,1)S(1)}, bf16[4,128,128]{2,1,0:T(8,128)(2,1)S(1)}, u32[]{:S(2)}, u32[]{:S(2)}) collective-permute-start(bf16[4,128,128]{2,1,0:T(8,128)(2,1)S(1)} %pad_maximum_fusion.7), channel_id=1, source_target_pairs={{0,1},{1,0},{2,3},{3,2},{4,5},{5,4},{6,7},{7,6},{8,9},{9,8},{10,11... | collective-permute-start | bytes 393224 | tf_op jit(solution)/shard_map/ppermute | solution.py:33
  57.4 3.1 %collective-permute-start.27 = (bf16[1,128,128]{2,1,0:T(8,128)(2,1)S(1)}, bf16[1,128,128]{2,1,0:T(8,128)(2,1)S(1)}, u32[]{:S(2)}, u32[]{:S(2)}) collective-permute-start(bf16[1,128,128]{2,1,0:T(8,128)(2,1)S(1)} %collective-permute-done.24), channel_id=1, source_target_pairs={{0,1},{1,0},{2,3},{3,2},{4,5},{5,4},{6,7},{7,6},{8,9},{9,8},{10,11... | collective-permute-start | bytes 98312 | tf_op jit(solution)/shard_map/ppermute | solution.py:33
  59.2 1.3 %collective-permute-start.28 = (bf16[1,128,128]{2,1,0:T(8,128)(2,1)S(1)}, bf16[1,128,128]{2,1,0:T(8,128)(2,1)S(1)}, u32[]{:S(2)}, u32[]{:S(2)}) collective-permute-start(bf16[1,128,128]{2,1,0:T(8,128)(2,1)S(1)} %collective-permute-done.25), channel_id=1, source_target_pairs={{0,1},{1,0},{2,3},{3,2},{4,5},{5,4},{6,7},{7,6},{8,9},{9,8},{10,11... | collective-permute-start | bytes 98312 | tf_op jit(solution)/shard_map/ppermute | solution.py:33
  60.5 1.3 %collective-permute-start.29 = (bf16[2,128,128]{2,1,0:T(8,128)(2,1)S(1)}, bf16[2,128,128]{2,1,0:T(8,128)(2,1)S(1)}, u32[]{:S(2)}, u32[]{:S(2)}) collective-permute-start(bf16[2,128,128]{2,1,0:T(8,128)(2,1)S(1)} %collective-permute-done.26), channel_id=1, source_target_pairs={{0,1},{1,0},{2,3},{3,2},{4,5},{5,4},{6,7},{7,6},{8,9},{9,8},{10,11... | collective-permute-start | bytes 196616 | tf_op jit(solution)/shard_map/ppermute | solution.py:33

commit v22 on v17

--- a/solution.py
+++ b/solution.py
@@ -44,11 +44,10 @@
         else:
             chunks = [jnp.concatenate(parts[1:])]
         across += [swap(chunk, wide, 2) for chunk in chunks]
-        beside = [swap(parts[0], wide, 1)]
         if split:
-            beside.append(swap(jnp.concatenate(parts[1:]), wide, 1))
+            beside = [swap(stack, wide, 1)]
         else:
-            beside = [swap(stack, wide, 1)]
+            beside = [swap(parts[0], wide, 1), swap(chunks[0], wide, 1)]
         return [stack] + beside + across + [swap(piece, wide, 1) for piece in across]
     across = swap(stack, wide, 2)
     return [stack, swap(stack, wide, 1), across, swap(across, wide, 1)]

time: 60.5 us -> 61 us (level)
  waiting for transfers between devices: 14.8 us -> 16.9 us
  starting transfers between devices: 28.4 us -> 27.5 us
    ppermute x18 -> x19, waiting for transfers between devices: 13.1 us -> 15.9 us  [swap(): return lax.ppermute(x, 'wide', [(d, d ^ mask) for d in range(wide)])]
    ppermute x18 -> x19, starting transfers between devices: 11.7 us -> 10.5 us  [swap(): return lax.ppermute(x, 'wide', [(d, d ^ mask) for d in range(wide)])]
    ppermute x9, waiting for transfers between devices: 1.63 us -> 0.99 us  [line_stage(): parts.append(lax.ppermute(x, 'wide', pairs)[None])]
    dot_general x30 -> x27, matrix products: 7.73 us -> 7.16 us  [rowwise(): return jnp.einsum(spec, tiles, currents, preferred_element_type=jnp.float32)]
    unnamed x22 -> x24, local copies, waits for them, and re-layouts: 1.34 us -> 1.34 us
  transfers between devices with their start and end apart: 27 -> 28, of which waited for: 9 -> 9; matrix products, arithmetic and copies ran while one was open for 21% -> 20% of each run, Pallas kernels for 0% -> 0%
where the time goes in v22:
time: 61 us; the launch traced here: 60.8 us
  starting transfers between devices  27.5 us (45%)
  waiting for transfers between devices  16.9 us (28%)
  matrix products  8.03 us (13%)
  local copies, waits for them, and re-layouts  4.18 us (7%)
  other arithmetic  3.76 us (6%)
    ppermute x9, starting transfers between devices, line_stage(): parts.append(lax.ppermute(x, 'wide', pairs)[None])  17 us
    ppermute x19, waiting for transfers between devices, swap(): return lax.ppermute(x, 'wide', [(d, d ^ mask) for d in range(wide)])  15.9 us
    ppermute x19, starting transfers between devices, swap(): return lax.ppermute(x, 'wide', [(d, d ^ mask) for d in range(wide)])  10.5 us
    dot_general x27, matrix products, rowwise(): return jnp.einsum(spec, tiles, currents, preferred_element_type=jnp.float32)  7.16 us
    sort x1, other arithmetic, per_device(): column_of_block = jnp.argsort(block_owner)  1.9 us
    unnamed x24, local copies, waits for them, and re-layouts  1.34 us
  transfers between devices with their start and end apart: 28, of which 9 were waited for; matrix products, arithmetic and copies ran while one was open for 20% of the time, Pallas kernels for 0%

profile of v22, /device:TPU:0, one launch (start us, length us, event | category | flops | bytes accessed | tf_op | source)
XLA Modules:
  0.0 60.8 jit_solution(14013197715990270062)
XLA Ops:
  0.0 3.0 %collective-permute-start = (bf16[4,128,128]{2,1,0:T(8,128)(2,1)}, bf16[4,128,128]{2,1,0:T(8,128)(2,1)S(1)}, u32[]{:S(2)}, u32[]{:S(2)}) collective-permute-start(bf16[4,128,128]{2,1,0:T(8,128)(2,1)} %param.19), channel_id=1, source_target_pairs={{0,4},{1,5},{2,6},{3,7},{4,8},{5,9},{6,10},{7,11},{8,12},{9,13},{1... | collective-permute-start | bytes 393224 | tf_op jit(solution)/shard_map/ppermute | solution.py:26
  3.0 2.6 %collective-permute-start.1 = (bf16[4,128,128]{2,1,0:T(8,128)(2,1)}, bf16[4,128,128]{2,1,0:T(8,128)(2,1)S(1)}, u32[]{:S(2)}, u32[]{:S(2)}) collective-permute-start(bf16[4,128,128]{2,1,0:T(8,128)(2,1)} %param.19), channel_id=1, source_target_pairs={{0,8},{1,9},{2,10},{3,11},{4,12},{5,13},{6,14},{7,15},{8,0},{9,1},... | collective-permute-start | bytes 393224 | tf_op jit(solution)/shard_map/ppermute | solution.py:26
  5.6 1.3 %collective-permute-start.2 = (bf16[4,128,128]{2,1,0:T(8,128)(2,1)}, bf16[4,128,128]{2,1,0:T(8,128)(2,1)S(1)}, u32[]{:S(2)}, u32[]{:S(2)}) collective-permute-start(bf16[4,128,128]{2,1,0:T(8,128)(2,1)} %param.19), channel_id=1, source_target_pairs={{0,12},{1,13},{2,14},{3,15},{4,0},{5,1},{6,2},{7,3},{8,4},{9,5},{1... | collective-permute-start | bytes 393224 | tf_op jit(solution)/shard_map/ppermute | solution.py:26
  7.0 1.5 %collective-permute-start.4 = (bf16[1,4,128,128]{3,2,1,0:T(8,128)(2,1)}, bf16[1,4,128,128]{3,2,1,0:T(8,128)(2,1)S(1)}, u32[]{:S(2)}, u32[]{:S(2)}) collective-permute-start(bf16[1,4,128,128]{3,2,1,0:T(8,128)(2,1)} %bitcast.314), channel_id=1, source_target_pairs={{0,2},{1,3},{2,0},{3,1},{4,6},{5,7},{6,4},{7,5},{8,10},{9,11},{10,... | collective-permute-start | bytes 393224 | tf_op jit(solution)/shard_map/ppermute | solution.py:33
  8.7 1.9 %sort.17 = (s32[16]{0:T(128)}, s32[16]{0:T(128)S(1)}) sort(s32[16]{0:T(128)} %param.18, s32[16]{0:T(128)S(1)} %iota.5), dimensions={0}, to_apply=%region_0.0 | sort | flops 64 | bytes 256 | tf_op jit(solution)/shard_map/jit(argsort)/sort | solution.py:98
  10.6 0.7 %gather_fusion = s32[16]{0:T(128)S(1)} fusion(s32[16]{0:T(128)S(1)} %get-tuple-element.8, s32[1024]{0:T(1024)S(1)} %pad_clamp_fusion.1), kind=kCustom, calls=%fused_computation.clone | custom fusion | bytes 192 | tf_op jit(solution)/shard_map/jit(_take)/gather | solution.py:73
  11.3 0.8 %copy.17 = s32[16,2]{1,0:T(8,128)S(1)} copy(s32[16,2]{0,1:T(2,128)} %bitcast.324) | data formatting | bytes 256 | tf_op jit(solution)/shard_map/squeeze | solution.py:75
  12.0 0.7 %gather_fusion.2 = bf16[16,2,128,128]{3,2,1,0:T(8,128)(2,1)S(1)} fusion(bf16[16,2,128,128]{3,2,1,0:T(8,128)(2,1)S(1)} %bitcast.299, s32[1024]{0:T(1024)S(1)} %pad_clamp_fusion), kind=kCustom, calls=%fused_computation.2.clone | custom fusion | bytes 2097216 | tf_op jit(solution)/shard_map/jit(_take)/gather | solution.py:74
  12.8 0.6 gather_fusion.1
  13.9 0.3 bitcast_select_fusion.3
  14.5 0.5 copy-done.3
  15.1 1.1 %collective-permute-start.5 = (bf16[1,4,128,128]{3,2,1,0:T(8,128)(2,1)S(1)}, bf16[1,4,128,128]{3,2,1,0:T(8,128)(2,1)S(1)}, u32[]{:S(2)}, u32[]{:S(2)}) collective-permute-start(bf16[1,4,128,128]{3,2,1,0:T(8,128)(2,1)S(1)} %bitcast.318), channel_id=1, source_target_pairs={{0,2},{1,3},{2,0},{3,1},{4,6},{5,7},{6,4},{7,5},{8,10},{9,11},{10,... | collective-permute-start | bytes 393224 | tf_op jit(solution)/shard_map/ppermute | solution.py:33
  16.2 1.0 %collective-permute-start.6 = (bf16[2,4,128,128]{3,2,1,0:T(8,128)(2,1)S(1)}, bf16[2,4,128,128]{3,2,1,0:T(8,128)(2,1)S(1)}, u32[]{:S(2)}, u32[]{:S(2)}) collective-permute-start(bf16[2,4,128,128]{3,2,1,0:T(8,128)(2,1)S(1)} %pad_maximum_fusion.4), channel_id=1, source_target_pairs={{0,2},{1,3},{2,0},{3,1},{4,6},{5,7},{6,4},{7,5},{8,10},{9,11},{10,... | collective-permute-start | bytes 786440 | tf_op jit(solution)/shard_map/ppermute | solution.py:33
  17.2 0.3 convolution_bitcast_fusion.5
  17.6 0.3 collective-permute-start.7
  18.1 3.0 %collective-permute-done.5 = bf16[1,4,128,128]{3,2,1,0:T(8,128)(2,1)S(1)} collective-permute-done((bf16[1,4,128,128]{3,2,1,0:T(8,128)(2,1)S(1)}, bf16[1,4,128,128]{3,2,1,0:T(8,128)(2,1)S(1)}, u32[]{:S(2)}, u32[]{:S(2)}) %collective-permute-start.5) | collective-permute-done | bytes 131104 | tf_op jit(solution)/shard_map/ppermute | solution.py:33
  21.7 0.7 %collective-permute-done.8 = bf16[1,4,128,128]{3,2,1,0:T(8,128)(2,1)S(1)} collective-permute-done((bf16[1,4,128,128]{3,2,1,0:T(8,128)(2,1)S(1)}, bf16[1,4,128,128]{3,2,1,0:T(8,128)(2,1)S(1)}, u32[]{:S(2)}, u32[]{:S(2)}) %collective-permute-start.8) | collective-permute-done | bytes 131104 | tf_op jit(solution)/shard_map/ppermute | solution.py:33
  22.9 2.9 %collective-permute-done.6 = bf16[2,4,128,128]{3,2,1,0:T(8,128)(2,1)S(1)} collective-permute-done((bf16[2,4,128,128]{3,2,1,0:T(8,128)(2,1)S(1)}, bf16[2,4,128,128]{3,2,1,0:T(8,128)(2,1)S(1)}, u32[]{:S(2)}, u32[]{:S(2)}) %collective-permute-start.6) | collective-permute-done | bytes 262176 | tf_op jit(solution)/shard_map/ppermute | solution.py:33
  26.5 0.3 convolution_bitcast_fusion.3
  26.8 0.4 convolution_bitcast_fusion
  27.1 0.4 fusion.26
  27.8 0.3 convolution_bitcast_fusion.2
  28.1 0.6 copy-done.2
  28.9 0.3 constant_dynamic-update-slice_fusion.9
  29.2 3.2 %collective-permute-start.10 = (bf16[128,128]{1,0:T(8,128)(2,1)S(1)}, bf16[128,128]{1,0:T(8,128)(2,1)S(1)}, u32[]{:S(2)}, u32[]{:S(2)}) collective-permute-start(bf16[128,128]{1,0:T(8,128)(2,1)S(1)} %get-tuple-element.21), channel_id=1, source_target_pairs={{0,4},{1,5},{2,6},{3,7},{4,8},{5,9},{6,10},{7,11},{8,12},{9,13},{1... | collective-permute-start | bytes 98312 | tf_op jit(solution)/shard_map/ppermute | solution.py:26
  32.5 1.2 %collective-permute-start.11 = (bf16[128,128]{1,0:T(8,128)(2,1)S(1)}, bf16[128,128]{1,0:T(8,128)(2,1)S(1)}, u32[]{:S(2)}, u32[]{:S(2)}) collective-permute-start(bf16[128,128]{1,0:T(8,128)(2,1)S(1)} %get-tuple-element.21), channel_id=1, source_target_pairs={{0,8},{1,9},{2,10},{3,11},{4,12},{5,13},{6,14},{7,15},{8,0},{9,1},... | collective-permute-start | bytes 98312 | tf_op jit(solution)/shard_map/ppermute | solution.py:26
  33.6 1.3 %collective-permute-start.12 = (bf16[128,128]{1,0:T(8,128)(2,1)S(1)}, bf16[128,128]{1,0:T(8,128)(2,1)S(1)}, u32[]{:S(2)}, u32[]{:S(2)}) collective-permute-start(bf16[128,128]{1,0:T(8,128)(2,1)S(1)} %get-tuple-element.21), channel_id=1, source_target_pairs={{0,12},{1,13},{2,14},{3,15},{4,0},{5,1},{6,2},{7,3},{8,4},{9,5},{1... | collective-permute-start | bytes 98312 | tf_op jit(solution)/shard_map/ppermute | solution.py:26
  34.9 1.5 %collective-permute-start.15 = (bf16[1,128,128]{2,1,0:T(8,128)(2,1)S(1)}, bf16[1,128,128]{2,1,0:T(8,128)(2,1)S(1)}, u32[]{:S(2)}, u32[]{:S(2)}) collective-permute-start(bf16[1,128,128]{2,1,0:T(8,128)(2,1)S(1)} %bitcast.321), channel_id=1, source_target_pairs={{0,2},{1,3},{2,0},{3,1},{4,6},{5,7},{6,4},{7,5},{8,10},{9,11},{10,... | collective-permute-start | bytes 98312 | tf_op jit(solution)/shard_map/ppermute | solution.py:33
  36.7 0.3 fusion.24
  37.0 0.3 fusion.25
  38.0 0.3 collective-permute-start.14
  38.3 1.2 %collective-permute-start.16 = (bf16[3,128,128]{2,1,0:T(8,128)(2,1)S(1)}, bf16[3,128,128]{2,1,0:T(8,128)(2,1)S(1)}, u32[]{:S(2)}, u32[]{:S(2)}) collective-permute-start(bf16[3,128,128]{2,1,0:T(8,128)(2,1)S(1)} %pad_maximum_fusion.6), channel_id=1, source_target_pairs={{0,2},{1,3},{2,0},{3,1},{4,6},{5,7},{6,4},{7,5},{8,10},{9,11},{10,... | collective-permute-start | bytes 294920 | tf_op jit(solution)/shard_map/ppermute | solution.py:33
  39.8 3.5 %collective-permute-done.16 = bf16[3,128,128]{2,1,0:T(8,128)(2,1)S(1)} collective-permute-done((bf16[3,128,128]{2,1,0:T(8,128)(2,1)S(1)}, bf16[3,128,128]{2,1,0:T(8,128)(2,1)S(1)}, u32[]{:S(2)}, u32[]{:S(2)}) %collective-permute-start.16) | collective-permute-done | bytes 98336 | tf_op jit(solution)/shard_map/ppermute | solution.py:33
  43.3 1.3 %collective-permute-done.18 = bf16[3,128,128]{2,1,0:T(8,128)(2,1)S(1)} collective-permute-done((bf16[3,128,128]{2,1,0:T(8,128)(2,1)S(1)}, bf16[3,128,128]{2,1,0:T(8,128)(2,1)S(1)}, u32[]{:S(2)}, u32[]{:S(2)}) %collective-permute-start.18) | collective-permute-done | bytes 98336 | tf_op jit(solution)/shard_map/ppermute | solution.py:33
  44.6 0.3 convolution_bitcast_fusion.11
  45.2 0.3 constant_dynamic-update-slice_fusion.19
  45.5 0.8 %collective-permute-start.19 = (bf16[128,128]{1,0:T(8,128)(2,1)S(1)}, bf16[128,128]{1,0:T(8,128)(2,1)S(1)}, u32[]{:S(2)}, u32[]{:S(2)}) collective-permute-start(bf16[128,128]{1,0:T(8,128)(2,1)S(1)} %get-tuple-element.19), channel_id=1, source_target_pairs={{0,4},{1,5},{2,6},{3,7},{4,8},{5,9},{6,10},{7,11},{8,12},{9,13},{1... | collective-permute-start | bytes 98312 | tf_op jit(solution)/shard_map/ppermute | solution.py:26
  46.3 2.4 %collective-permute-start.20 = (bf16[128,128]{1,0:T(8,128)(2,1)S(1)}, bf16[128,128]{1,0:T(8,128)(2,1)S(1)}, u32[]{:S(2)}, u32[]{:S(2)}) collective-permute-start(bf16[128,128]{1,0:T(8,128)(2,1)S(1)} %get-tuple-element.19), channel_id=1, source_target_pairs={{0,8},{1,9},{2,10},{3,11},{4,12},{5,13},{6,14},{7,15},{8,0},{9,1},... | collective-permute-start | bytes 98312 | tf_op jit(solution)/shard_map/ppermute | solution.py:26
  48.7 1.0 %collective-permute-start.21 = (bf16[128,128]{1,0:T(8,128)(2,1)S(1)}, bf16[128,128]{1,0:T(8,128)(2,1)S(1)}, u32[]{:S(2)}, u32[]{:S(2)}) collective-permute-start(bf16[128,128]{1,0:T(8,128)(2,1)S(1)} %get-tuple-element.19), channel_id=1, source_target_pairs={{0,12},{1,13},{2,14},{3,15},{4,0},{5,1},{6,2},{7,3},{8,4},{9,5},{1... | collective-permute-start | bytes 98312 | tf_op jit(solution)/shard_map/ppermute | solution.py:26
  49.8 1.5 %collective-permute-start.24 = (bf16[1,128,128]{2,1,0:T(8,128)(2,1)S(1)}, bf16[1,128,128]{2,1,0:T(8,128)(2,1)S(1)}, u32[]{:S(2)}, u32[]{:S(2)}) collective-permute-start(bf16[1,128,128]{2,1,0:T(8,128)(2,1)S(1)} %bitcast.323), channel_id=1, source_target_pairs={{0,2},{1,3},{2,0},{3,1},{4,6},{5,7},{6,4},{7,5},{8,10},{9,11},{10,... | collective-permute-start | bytes 98312 | tf_op jit(solution)/shard_map/ppermute | solution.py:33
  51.3 0.5 convolution_bitcast_fusion.9
  51.8 0.8 %collective-permute-done.21 = bf16[128,128]{1,0:T(8,128)(2,1)S(1)} collective-permute-done((bf16[128,128]{1,0:T(8,128)(2,1)S(1)}, bf16[128,128]{1,0:T(8,128)(2,1)S(1)}, u32[]{:S(2)}, u32[]{:S(2)}) %collective-permute-start.21) | collective-permute-done | bytes 32800 | tf_op jit(solution)/shard_map/ppermute | solution.py:26
  52.7 1.6 %collective-permute-start.25 = (bf16[3,128,128]{2,1,0:T(8,128)(2,1)S(1)}, bf16[3,128,128]{2,1,0:T(8,128)(2,1)S(1)}, u32[]{:S(2)}, u32[]{:S(2)}) collective-permute-start(bf16[3,128,128]{2,1,0:T(8,128)(2,1)S(1)} %pad_maximum_fusion.7), channel_id=1, source_target_pairs={{0,2},{1,3},{2,0},{3,1},{4,6},{5,7},{6,4},{7,5},{8,10},{9,11},{10,... | collective-permute-start | bytes 294920 | tf_op jit(solution)/shard_map/ppermute | solution.py:33
  54.7 3.3 %collective-permute-done.25 = bf16[3,128,128]{2,1,0:T(8,128)(2,1)S(1)} collective-permute-done((bf16[3,128,128]{2,1,0:T(8,128)(2,1)S(1)}, bf16[3,128,128]{2,1,0:T(8,128)(2,1)S(1)}, u32[]{:S(2)}, u32[]{:S(2)}) %collective-permute-start.25) | collective-permute-done | bytes 98336 | tf_op jit(solution)/shard_map/ppermute | solution.py:33
  58.0 1.3 %collective-permute-done.27 = bf16[3,128,128]{2,1,0:T(8,128)(2,1)S(1)} collective-permute-done((bf16[3,128,128]{2,1,0:T(8,128)(2,1)S(1)}, bf16[3,128,128]{2,1,0:T(8,128)(2,1)S(1)}, u32[]{:S(2)}, u32[]{:S(2)}) %collective-permute-start.27) | collective-permute-done | bytes 98336 | tf_op jit(solution)/shard_map/ppermute | solution.py:33
  59.3 0.3 convolution_bitcast_fusion.10
  59.8 0.3 convolution_bitcast_fusion.8
  60.1 0.7 %pad_maximum_fusion.5 = f32[3,128,128]{2,1,0:T(8,128)} fusion(f32[1,128,128]{2,1,0:T(8,128)S(1)} %bitcast.306, f32[1,128,128]{2,1,0:T(8,128)S(1)} %bitcast.307, f32[1,128,128]{2,1,0:T(8,128)S(1)} %convolution_bitcast_fusion.8), kind=kLoop, calls=%fused_computation.89 | loop fusion | flops 98304 | bytes 393216 | tf_op jit(solution)/shard_map/stack | solution.py:140
  (87 shorter events, 5.8 us)
Async XLA Ops:
  0.0 12.0 %copy-start = (bf16[1,16,2,128,128]{4,3,2,1,0:T(8,128)(2,1)S(1)}, bf16[1,16,2,128,128]{4,3,2,1,0:T(8,128)(2,1)}, u32[]{:S(2)}) copy-start(bf16[1,16,2,128,128]{4,3,2,1,0:T(8,128)(2,1)} %param.16) | copy-start | bytes 3145732
  0.0 14.5 %collective-permute-start = (bf16[4,128,128]{2,1,0:T(8,128)(2,1)}, bf16[4,128,128]{2,1,0:T(8,128)(2,1)S(1)}, u32[]{:S(2)}, u32[]{:S(2)}) collective-permute-start(bf16[4,128,128]{2,1,0:T(8,128)(2,1)} %param.19), channel_id=1, source_target_pairs={{0,4},{1,5},{2,6},{3,7},{4,8},{5,9},{6,10},{7,11},{8,12},{9,13},{1... | collective-permute-start | bytes 393224 | tf_op jit(solution)/shard_map/ppermute | solution.py:26
  3.0 11.4 %collective-permute-start.1 = (bf16[4,128,128]{2,1,0:T(8,128)(2,1)}, bf16[4,128,128]{2,1,0:T(8,128)(2,1)S(1)}, u32[]{:S(2)}, u32[]{:S(2)}) collective-permute-start(bf16[4,128,128]{2,1,0:T(8,128)(2,1)} %param.19), channel_id=1, source_target_pairs={{0,8},{1,9},{2,10},{3,11},{4,12},{5,13},{6,14},{7,15},{8,0},{9,1},... | collective-permute-start | bytes 393224 | tf_op jit(solution)/shard_map/ppermute | solution.py:26
  5.6 8.9 %collective-permute-start.2 = (bf16[4,128,128]{2,1,0:T(8,128)(2,1)}, bf16[4,128,128]{2,1,0:T(8,128)(2,1)S(1)}, u32[]{:S(2)}, u32[]{:S(2)}) collective-permute-start(bf16[4,128,128]{2,1,0:T(8,128)(2,1)} %param.19), channel_id=1, source_target_pairs={{0,12},{1,13},{2,14},{3,15},{4,0},{5,1},{6,2},{7,3},{8,4},{9,5},{1... | collective-permute-start | bytes 393224 | tf_op jit(solution)/shard_map/ppermute | solution.py:26
  7.0 10.6 %collective-permute-start.4 = (bf16[1,4,128,128]{3,2,1,0:T(8,128)(2,1)}, bf16[1,4,128,128]{3,2,1,0:T(8,128)(2,1)S(1)}, u32[]{:S(2)}, u32[]{:S(2)}) collective-permute-start(bf16[1,4,128,128]{3,2,1,0:T(8,128)(2,1)} %bitcast.314), channel_id=1, source_target_pairs={{0,2},{1,3},{2,0},{3,1},{4,6},{5,7},{6,4},{7,5},{8,10},{9,11},{10,... | collective-permute-start | bytes 393224 | tf_op jit(solution)/shard_map/ppermute | solution.py:33
  14.1 0.9 %copy-start.3 = (bf16[4,128,128]{2,1,0:T(8,128)(2,1)S(1)}, bf16[4,128,128]{2,1,0:T(8,128)(2,1)}, u32[]{:S(2)}) copy-start(bf16[4,128,128]{2,1,0:T(8,128)(2,1)} %param.19) | copy-start | bytes 393220
  15.1 6.0 %collective-permute-start.5 = (bf16[1,4,128,128]{3,2,1,0:T(8,128)(2,1)S(1)}, bf16[1,4,128,128]{3,2,1,0:T(8,128)(2,1)S(1)}, u32[]{:S(2)}, u32[]{:S(2)}) collective-permute-start(bf16[1,4,128,128]{3,2,1,0:T(8,128)(2,1)S(1)} %bitcast.318), channel_id=1, source_target_pairs={{0,2},{1,3},{2,0},{3,1},{4,6},{5,7},{6,4},{7,5},{8,10},{9,11},{10,... | collective-permute-start | bytes 393224 | tf_op jit(solution)/shard_map/ppermute | solution.py:33
  16.2 10.6 %collective-permute-start.3 = (bf16[4,4,128,128]{3,2,1,0:T(8,128)(2,1)S(1)}, bf16[4,4,128,128]{3,2,1,0:T(8,128)(2,1)S(1)}, u32[]{:S(2)}, u32[]{:S(2)}) collective-permute-start(bf16[4,4,128,128]{3,2,1,0:T(8,128)(2,1)S(1)} %pad_maximum_fusion.3), channel_id=1, source_target_pairs={{0,1},{1,0},{2,3},{3,2},{4,5},{5,4},{6,7},{7,6},{8,9},{9,8},{10,11... | collective-permute-start | bytes 1572872 | tf_op jit(solution)/shard_map/ppermute | solution.py:33
  16.2 9.6 %collective-permute-start.6 = (bf16[2,4,128,128]{3,2,1,0:T(8,128)(2,1)S(1)}, bf16[2,4,128,128]{3,2,1,0:T(8,128)(2,1)S(1)}, u32[]{:S(2)}, u32[]{:S(2)}) collective-permute-start(bf16[2,4,128,128]{3,2,1,0:T(8,128)(2,1)S(1)} %pad_maximum_fusion.4), channel_id=1, source_target_pairs={{0,2},{1,3},{2,0},{3,1},{4,6},{5,7},{6,4},{7,5},{8,10},{9,11},{10,... | collective-permute-start | bytes 786440 | tf_op jit(solution)/shard_map/ppermute | solution.py:33
  17.6 10.5 %collective-permute-start.7 = (bf16[1,4,128,128]{3,2,1,0:T(8,128)(2,1)S(1)}, bf16[1,4,128,128]{3,2,1,0:T(8,128)(2,1)S(1)}, u32[]{:S(2)}, u32[]{:S(2)}) collective-permute-start(bf16[1,4,128,128]{3,2,1,0:T(8,128)(2,1)S(1)} %collective-permute-done.4), channel_id=1, source_target_pairs={{0,1},{1,0},{2,3},{3,2},{4,5},{5,4},{6,7},{7,6},{8,9},{9,8},{10,11... | collective-permute-start | bytes 393224 | tf_op jit(solution)/shard_map/ppermute | solution.py:33
  21.1 1.3 %collective-permute-start.8 = (bf16[1,4,128,128]{3,2,1,0:T(8,128)(2,1)S(1)}, bf16[1,4,128,128]{3,2,1,0:T(8,128)(2,1)S(1)}, u32[]{:S(2)}, u32[]{:S(2)}) collective-permute-start(bf16[1,4,128,128]{3,2,1,0:T(8,128)(2,1)S(1)} %collective-permute-done.5), channel_id=1, source_target_pairs={{0,1},{1,0},{2,3},{3,2},{4,5},{5,4},{6,7},{7,6},{8,9},{9,8},{10,11... | collective-permute-start | bytes 393224 | tf_op jit(solution)/shard_map/ppermute | solution.py:33
  25.8 2.0 %collective-permute-start.9 = (bf16[2,4,128,128]{3,2,1,0:T(8,128)(2,1)S(1)}, bf16[2,4,128,128]{3,2,1,0:T(8,128)(2,1)S(1)}, u32[]{:S(2)}, u32[]{:S(2)}) collective-permute-start(bf16[2,4,128,128]{3,2,1,0:T(8,128)(2,1)S(1)} %collective-permute-done.6), channel_id=1, source_target_pairs={{0,1},{1,0},{2,3},{3,2},{4,5},{5,4},{6,7},{7,6},{8,9},{9,8},{10,11... | collective-permute-start | bytes 786440 | tf_op jit(solution)/shard_map/ppermute | solution.py:33
  27.7 0.9 %copy-start.2 = (f32[3,128,128]{2,1,0:T(8,128)S(1)}, f32[3,128,128]{2,1,0:T(8,128)}, u32[]{:S(2)}) copy-start(f32[3,128,128]{2,1,0:T(8,128)} %param.20) | copy-start | bytes 589828
  28.0 0.9 %copy-start.1 = (f32[1,128,128]{2,1,0:T(8,128)S(1)}, f32[1,128,128]{2,1,0:T(8,128)}, u32[]{:S(2)}) copy-start(f32[1,128,128]{2,1,0:T(8,128)} %param.21) | copy-start | bytes 196612
  29.2 8.7 %collective-permute-start.10 = (bf16[128,128]{1,0:T(8,128)(2,1)S(1)}, bf16[128,128]{1,0:T(8,128)(2,1)S(1)}, u32[]{:S(2)}, u32[]{:S(2)}) collective-permute-start(bf16[128,128]{1,0:T(8,128)(2,1)S(1)} %get-tuple-element.21), channel_id=1, source_target_pairs={{0,4},{1,5},{2,6},{3,7},{4,8},{5,9},{6,10},{7,11},{8,12},{9,13},{1... | collective-permute-start | bytes 98312 | tf_op jit(solution)/shard_map/ppermute | solution.py:26
  32.5 5.5 %collective-permute-start.11 = (bf16[128,128]{1,0:T(8,128)(2,1)S(1)}, bf16[128,128]{1,0:T(8,128)(2,1)S(1)}, u32[]{:S(2)}, u32[]{:S(2)}) collective-permute-start(bf16[128,128]{1,0:T(8,128)(2,1)S(1)} %get-tuple-element.21), channel_id=1, source_target_pairs={{0,8},{1,9},{2,10},{3,11},{4,12},{5,13},{6,14},{7,15},{8,0},{9,1},... | collective-permute-start | bytes 98312 | tf_op jit(solution)/shard_map/ppermute | solution.py:26
  33.6 4.3 %collective-permute-start.12 = (bf16[128,128]{1,0:T(8,128)(2,1)S(1)}, bf16[128,128]{1,0:T(8,128)(2,1)S(1)}, u32[]{:S(2)}, u32[]{:S(2)}) collective-permute-start(bf16[128,128]{1,0:T(8,128)(2,1)S(1)} %get-tuple-element.21), channel_id=1, source_target_pairs={{0,12},{1,13},{2,14},{3,15},{4,0},{5,1},{6,2},{7,3},{8,4},{9,5},{1... | collective-permute-start | bytes 98312 | tf_op jit(solution)/shard_map/ppermute | solution.py:26
  34.9 4.8 %collective-permute-start.13 = (bf16[1,128,128]{2,1,0:T(8,128)(2,1)S(1)}, bf16[1,128,128]{2,1,0:T(8,128)(2,1)S(1)}, u32[]{:S(2)}, u32[]{:S(2)}) collective-permute-start(bf16[1,128,128]{2,1,0:T(8,128)(2,1)S(1)} %bitcast.320), channel_id=1, source_target_pairs={{0,1},{1,0},{2,3},{3,2},{4,5},{5,4},{6,7},{7,6},{8,9},{9,8},{10,11... | collective-permute-start | bytes 98312 | tf_op jit(solution)/shard_map/ppermute | solution.py:33
  34.9 4.6 %collective-permute-start.15 = (bf16[1,128,128]{2,1,0:T(8,128)(2,1)S(1)}, bf16[1,128,128]{2,1,0:T(8,128)(2,1)S(1)}, u32[]{:S(2)}, u32[]{:S(2)}) collective-permute-start(bf16[1,128,128]{2,1,0:T(8,128)(2,1)S(1)} %bitcast.321), channel_id=1, source_target_pairs={{0,2},{1,3},{2,0},{3,1},{4,6},{5,7},{6,4},{7,5},{8,10},{9,11},{10,... | collective-permute-start | bytes 98312 | tf_op jit(solution)/shard_map/ppermute | solution.py:33
  38.0 1.7 %collective-permute-start.14 = (bf16[3,128,128]{2,1,0:T(8,128)(2,1)S(1)}, bf16[3,128,128]{2,1,0:T(8,128)(2,1)S(1)}, u32[]{:S(2)}, u32[]{:S(2)}) collective-permute-start(bf16[3,128,128]{2,1,0:T(8,128)(2,1)S(1)} %pad_maximum_fusion.6), channel_id=1, source_target_pairs={{0,1},{1,0},{2,3},{3,2},{4,5},{5,4},{6,7},{7,6},{8,9},{9,8},{10,11... | collective-permute-start | bytes 294920 | tf_op jit(solution)/shard_map/ppermute | solution.py:33
  38.3 5.0 %collective-permute-start.16 = (bf16[3,128,128]{2,1,0:T(8,128)(2,1)S(1)}, bf16[3,128,128]{2,1,0:T(8,128)(2,1)S(1)}, u32[]{:S(2)}, u32[]{:S(2)}) collective-permute-start(bf16[3,128,128]{2,1,0:T(8,128)(2,1)S(1)} %pad_maximum_fusion.6), channel_id=1, source_target_pairs={{0,2},{1,3},{2,0},{3,1},{4,6},{5,7},{6,4},{7,5},{8,10},{9,11},{10,... | collective-permute-start | bytes 294920 | tf_op jit(solution)/shard_map/ppermute | solution.py:33
  39.5 3.8 %collective-permute-start.17 = (bf16[1,128,128]{2,1,0:T(8,128)(2,1)S(1)}, bf16[1,128,128]{2,1,0:T(8,128)(2,1)S(1)}, u32[]{:S(2)}, u32[]{:S(2)}) collective-permute-start(bf16[1,128,128]{2,1,0:T(8,128)(2,1)S(1)} %collective-permute-done.15), channel_id=1, source_target_pairs={{0,1},{1,0},{2,3},{3,2},{4,5},{5,4},{6,7},{7,6},{8,9},{9,8},{10,11... | collective-permute-start | bytes 98312 | tf_op jit(solution)/shard_map/ppermute | solution.py:33
  43.3 1.3 %collective-permute-start.18 = (bf16[3,128,128]{2,1,0:T(8,128)(2,1)S(1)}, bf16[3,128,128]{2,1,0:T(8,128)(2,1)S(1)}, u32[]{:S(2)}, u32[]{:S(2)}) collective-permute-start(bf16[3,128,128]{2,1,0:T(8,128)(2,1)S(1)} %collective-permute-done.16), channel_id=1, source_target_pairs={{0,1},{1,0},{2,3},{3,2},{4,5},{5,4},{6,7},{7,6},{8,9},{9,8},{10,11... | collective-permute-start | bytes 294920 | tf_op jit(solution)/shard_map/ppermute | solution.py:33
  45.5 6.3 %collective-permute-start.19 = (bf16[128,128]{1,0:T(8,128)(2,1)S(1)}, bf16[128,128]{1,0:T(8,128)(2,1)S(1)}, u32[]{:S(2)}, u32[]{:S(2)}) collective-permute-start(bf16[128,128]{1,0:T(8,128)(2,1)S(1)} %get-tuple-element.19), channel_id=1, source_target_pairs={{0,4},{1,5},{2,6},{3,7},{4,8},{5,9},{6,10},{7,11},{8,12},{9,13},{1... | collective-permute-start | bytes 98312 | tf_op jit(solution)/shard_map/ppermute | solution.py:26
  46.3 5.5 %collective-permute-start.20 = (bf16[128,128]{1,0:T(8,128)(2,1)S(1)}, bf16[128,128]{1,0:T(8,128)(2,1)S(1)}, u32[]{:S(2)}, u32[]{:S(2)}) collective-permute-start(bf16[128,128]{1,0:T(8,128)(2,1)S(1)} %get-tuple-element.19), channel_id=1, source_target_pairs={{0,8},{1,9},{2,10},{3,11},{4,12},{5,13},{6,14},{7,15},{8,0},{9,1},... | collective-permute-start | bytes 98312 | tf_op jit(solution)/shard_map/ppermute | solution.py:26
  48.7 3.9 %collective-permute-start.21 = (bf16[128,128]{1,0:T(8,128)(2,1)S(1)}, bf16[128,128]{1,0:T(8,128)(2,1)S(1)}, u32[]{:S(2)}, u32[]{:S(2)}) collective-permute-start(bf16[128,128]{1,0:T(8,128)(2,1)S(1)} %get-tuple-element.19), channel_id=1, source_target_pairs={{0,12},{1,13},{2,14},{3,15},{4,0},{5,1},{6,2},{7,3},{8,4},{9,5},{1... | collective-permute-start | bytes 98312 | tf_op jit(solution)/shard_map/ppermute | solution.py:26
  49.8 4.8 %collective-permute-start.22 = (bf16[1,128,128]{2,1,0:T(8,128)(2,1)S(1)}, bf16[1,128,128]{2,1,0:T(8,128)(2,1)S(1)}, u32[]{:S(2)}, u32[]{:S(2)}) collective-permute-start(bf16[1,128,128]{2,1,0:T(8,128)(2,1)S(1)} %bitcast.322), channel_id=1, source_target_pairs={{0,1},{1,0},{2,3},{3,2},{4,5},{5,4},{6,7},{7,6},{8,9},{9,8},{10,11... | collective-permute-start | bytes 98312 | tf_op jit(solution)/shard_map/ppermute | solution.py:33
  49.8 4.6 %collective-permute-start.24 = (bf16[1,128,128]{2,1,0:T(8,128)(2,1)S(1)}, bf16[1,128,128]{2,1,0:T(8,128)(2,1)S(1)}, u32[]{:S(2)}, u32[]{:S(2)}) collective-permute-start(bf16[1,128,128]{2,1,0:T(8,128)(2,1)S(1)} %bitcast.323), channel_id=1, source_target_pairs={{0,2},{1,3},{2,0},{3,1},{4,6},{5,7},{6,4},{7,5},{8,10},{9,11},{10,... | collective-permute-start | bytes 98312 | tf_op jit(solution)/shard_map/ppermute | solution.py:33
  52.7 2.0 %collective-permute-start.23 = (bf16[3,128,128]{2,1,0:T(8,128)(2,1)S(1)}, bf16[3,128,128]{2,1,0:T(8,128)(2,1)S(1)}, u32[]{:S(2)}, u32[]{:S(2)}) collective-permute-start(bf16[3,128,128]{2,1,0:T(8,128)(2,1)S(1)} %pad_maximum_fusion.7), channel_id=1, source_target_pairs={{0,1},{1,0},{2,3},{3,2},{4,5},{5,4},{6,7},{7,6},{8,9},{9,8},{10,11... | collective-permute-start | bytes 294920 | tf_op jit(solution)/shard_map/ppermute | solution.py:33
  52.7 5.2 %collective-permute-start.25 = (bf16[3,128,128]{2,1,0:T(8,128)(2,1)S(1)}, bf16[3,128,128]{2,1,0:T(8,128)(2,1)S(1)}, u32[]{:S(2)}, u32[]{:S(2)}) collective-permute-start(bf16[3,128,128]{2,1,0:T(8,128)(2,1)S(1)} %pad_maximum_fusion.7), channel_id=1, source_target_pairs={{0,2},{1,3},{2,0},{3,1},{4,6},{5,7},{6,4},{7,5},{8,10},{9,11},{10,... | collective-permute-start | bytes 294920 | tf_op jit(solution)/shard_map/ppermute | solution.py:33
  54.4 3.6 %collective-permute-start.26 = (bf16[1,128,128]{2,1,0:T(8,128)(2,1)S(1)}, bf16[1,128,128]{2,1,0:T(8,128)(2,1)S(1)}, u32[]{:S(2)}, u32[]{:S(2)}) collective-permute-start(bf16[1,128,128]{2,1,0:T(8,128)(2,1)S(1)} %collective-permute-done.24), channel_id=1, source_target_pairs={{0,1},{1,0},{2,3},{3,2},{4,5},{5,4},{6,7},{7,6},{8,9},{9,8},{10,11... | collective-permute-start | bytes 98312 | tf_op jit(solution)/shard_map/ppermute | solution.py:33
  57.9 1.3 %collective-permute-start.27 = (bf16[3,128,128]{2,1,0:T(8,128)(2,1)S(1)}, bf16[3,128,128]{2,1,0:T(8,128)(2,1)S(1)}, u32[]{:S(2)}, u32[]{:S(2)}) collective-permute-start(bf16[3,128,128]{2,1,0:T(8,128)(2,1)S(1)} %collective-permute-done.25), channel_id=1, source_target_pairs={{0,1},{1,0},{2,3},{3,2},{4,5},{5,4},{6,7},{7,6},{8,9},{9,8},{10,11... | collective-permute-start | bytes 294920 | tf_op jit(solution)/shard_map/ppermute | solution.py:33
